TPU v7x, 32 devices: a whole 2x2x4 slice. The times are simulated.
32 devices in a mesh: section: 2 (over x), seq: 8 (over z, y), head: 2 (over core).
Axes of the slice: x: 2, y: 2, z: 4, core: 2. Of those that a mesh axis runs over, the one named last changes fastest.
Arguments:
- bwd_input: bfloat16 [2, 1024, 3584], P('section', 'seq', 'head'), may hold values from -6 to 6
- bwd_docs: int32 [2, 1024], P('section', 'seq'), may hold values from 0 to 3, as said below
- bwd_grad: bfloat16 [2, 1024, 3584], P('section', 'seq', 'head'), may hold values from -6 to 6
- proj_weight: bfloat16 [2, 256, 3584], P('section', 'seq', 'head'), may hold values from -0.09375 to 0.09375
- step_weight: float32 [2, 3584], P('section', 'head'), may hold values from -0.75 to 0.75
- step_bias: float32 [2, 56], P('section', 'head'), may hold values from -5 to -2
- rate_log: float32 [2, 56], P('section', 'head'), may hold values from -4 to 0.5
- skip_gain: float32 [2, 56], P('section', 'head'), may hold values from 0.5 to 1.5
Outputs:
- prev_grad: bfloat16 [2, 1024, 3584], P('section', 'seq', 'head')
- grad_proj: float32 [2, 256, 3584], P('section', 'seq', 'head')
- grad_step_weight: float32 [2, 3584], P('section', 'head')
- grad_step_bias: float32 [2, 56], P('section', 'head')
- grad_rate_log: float32 [2, 56], P('section', 'head')
- grad_skip: float32 [2, 56], P('section', 'head')
Inputs may be any that keep to these rules, and one draw needn't show every extreme that they name: `bwd_docs`: document ids of each row never fall, start at 0, every id occurs, and one document of each row holds 512 tokens.
All inputs are finite; a program needn't handle non-finite values.
Results may differ from a plain program's by a relative error of at most 0.023.
Values may be sent and summed in bfloat16 or wider, within the bound.
No kernel may reach another device: no remote copies, remote signals or barrier semaphores. Data moves between devices by JAX's collectives and lax.ppermute only.
A program may use at most 64 MiB of HBM per device.

v0:
```python
import jax
import jax.numpy as jnp
from jax import lax
from jax.sharding import PartitionSpec as P

EXACT = lax.Precision.HIGHEST


def shifted(block, axis, distance):
    devices = range(lax.axis_size(axis))
    route = [(i - distance, i) for i in devices if i - distance in devices]
    return lax.ppermute(block, axis, route)


def entering(value, axis, combine, identity):
    size, mine = (lax.axis_size(axis), lax.axis_index(axis))
    everything = jax.tree.map(
        lambda part, kind: lax.all_gather(part.astype(kind), axis),
        value,
        (jnp.bfloat16, jnp.bfloat16),
    )
    start = jax.tree.map(
        lambda part, zero: jnp.broadcast_to(jnp.asarray(zero, part.dtype), part.shape),
        value,
        identity,
    )

    def lap(k, before):
        reached = k < mine
        new = combine(
            before, jax.tree.map(lambda part, own: part[k].astype(own.dtype), everything, value)
        )
        return jax.tree.map(lambda a, b: jnp.where(reached, a, b), new, before)

    return lax.fori_loop(0, size, lap, start)


def entering_2(value, axis, combine, identity):
    size, mine = (lax.axis_size(axis), lax.axis_index(axis))
    everything = jax.tree.map(
        lambda part, kind: lax.all_gather(part.astype(kind), axis),
        value,
        jax.tree.map(lambda a: jnp.bfloat16 if a.dtype == jnp.float32 else a.dtype, value),
    )
    start = jax.tree.map(
        lambda part, zero: jnp.broadcast_to(jnp.asarray(zero, part.dtype), part.shape),
        value,
        identity,
    )

    def lap(k, before):
        at = size - 1 - k
        reached = at > mine
        new = combine(
            before, jax.tree.map(lambda part, own: part[at].astype(own.dtype), everything, value)
        )
        return jax.tree.map(lambda a, b: jnp.where(reached, a, b), new, before)

    return lax.fori_loop(0, size, lap, start)


def contract(spec, left, right):
    return jnp.einsum(spec, left, right, preferred_element_type=jnp.float32)


def local_setup(values, step_weight, step_bias, rate_log):
    tokens = values.shape[0]
    raw_step = (
        jnp.einsum("thp,hp->th", values.astype(jnp.float32), step_weight, precision=EXACT)
        + step_bias[None, :]
    )
    step_size = jax.nn.softplus(raw_step)
    decay_log = -jnp.exp(rate_log)[None, :] * step_size
    row_ids = lax.broadcasted_iota(jnp.int32, (tokens, tokens), 0)
    col_ids = lax.broadcasted_iota(jnp.int32, (tokens, tokens), 1)
    triangle = (row_ids >= col_ids).astype(jnp.float32)
    cumulative = jnp.dot(triangle, decay_log, precision=EXACT)
    return (step_size, cumulative, row_ids, col_ids)


def span_summary(values, mixer, step_weight, step_bias, rate_log, docs, doc_before):
    step_size, cumulative, row_ids, col_ids = local_setup(values, step_weight, step_bias, rate_log)
    final_log = cumulative[-1]
    tail_mask = (docs == docs[-1]).astype(jnp.float32)[:, None]
    tail_weight = (
        jnp.exp(jnp.where(tail_mask > 0, final_log[None, :] - cumulative, 0.0))
        * tail_mask
        * step_size
    )
    unbroken = (docs[-1] == doc_before).astype(jnp.float32)
    carry_decay = jnp.exp(final_log) * unbroken
    half_width = mixer.shape[1] // 2
    writers = mixer[:, :half_width]
    weighted = (tail_weight[:, :, None] * writers.astype(jnp.float32)[:, None, :]).astype(
        jnp.bfloat16
    )
    span_state = contract("thn,thp->hnp", weighted, values)
    return (carry_decay, span_state)


def span_output(
    values, mixer, step_weight, step_bias, rate_log, skip_gain, docs, doc_before, incoming
):
    step_size, cumulative, row_ids, col_ids = local_setup(values, step_weight, step_bias, rate_log)
    half_width = mixer.shape[1] // 2
    writers = mixer[:, :half_width]
    readers = mixer[:, half_width:]
    affinity = jnp.dot(readers, writers.T, preferred_element_type=jnp.float32)
    same_doc = ((docs[:, None] == docs[None, :]) & (row_ids >= col_ids)).astype(jnp.float32)
    heads_first = cumulative.T
    log_gap = heads_first[:, :, None] - heads_first[:, None, :]
    mixing = (
        jnp.exp(jnp.where(same_doc[None] > 0, log_gap, 0.0))
        * same_doc[None]
        * affinity[None]
        * step_size.T[:, None, :]
    )
    mixing = mixing.astype(jnp.bfloat16)
    local_part = contract("hts,shp->thp", mixing, values)
    unbroken = (docs == doc_before).astype(jnp.float32)
    carry_scale = jnp.exp(cumulative) * unbroken[:, None]
    carried = jnp.einsum("tn,hnp->thp", readers.astype(jnp.float32), incoming, precision=EXACT)
    combined = (
        values.astype(jnp.float32) * (1.0 + skip_gain)[None, :, None]
        + local_part
        + carry_scale[:, :, None] * carried
    )
    return combined.astype(jnp.bfloat16)


def carry_join(earlier, later):
    return (earlier[0] * later[0], later[0][:, None] * earlier[1] + later[1])


def back_join(earlier, later):
    return (earlier[0] * later[0], later[1] + later[0][:, None] * earlier[1])


def shards(bwd_input, bwd_docs, bwd_grad, proj_weight, step_weight, step_bias, rate_log, skip_gain):
    tokens = bwd_input.shape[1]
    channels_here = bwd_input.shape[2]
    heads_here = step_bias.shape[1]
    head_width = channels_here // heads_here
    bwd_flat = bwd_input[0]
    bwd_values = bwd_flat.reshape(tokens, heads_here, head_width)
    weight_heads = step_weight[0].reshape(heads_here, head_width)
    bias_heads = step_bias[0]
    rate_heads = rate_log[0]
    skip_heads = skip_gain[0]
    docs_bwd = bwd_docs[0]
    doc_before = shifted(docs_bwd[-1:], "seq", 1)[0]
    full_weight = lax.all_gather(proj_weight[0], "seq", axis=0, tiled=True)
    partial_value = jnp.dot(bwd_flat, full_weight.T, preferred_element_type=jnp.float32)
    mixer_bwd = lax.psum_scatter(
        partial_value.astype(jnp.bfloat16), "head", scatter_dimension=1, tiled=True
    )

    def summary_bwd(values_in, mixer_in, weight_in, bias_in, rate_in):
        return span_summary(values_in, mixer_in, weight_in, bias_in, rate_in, docs_bwd, doc_before)

    summary_out, summary_pull = jax.vjp(
        summary_bwd, bwd_values, mixer_bwd, weight_heads, bias_heads, rate_heads
    )
    decay_bwd, state_bwd = summary_out
    state_shape = state_bwd.shape
    state_flat = state_bwd.reshape(heads_here, -1)
    seeds = (jnp.ones_like(decay_bwd), jnp.zeros_like(state_flat))
    incoming_flat = entering((decay_bwd, state_flat), "seq", carry_join, seeds)[1]
    incoming_bwd = incoming_flat.reshape(state_shape)

    def output_bwd(values_in, mixer_in, weight_in, bias_in, rate_in, skip_in, state_in):
        return span_output(
            values_in,
            mixer_in,
            weight_in,
            bias_in,
            rate_in,
            skip_in,
            docs_bwd,
            doc_before,
            state_in,
        )

    unused, output_pull = jax.vjp(
        output_bwd,
        bwd_values,
        mixer_bwd,
        weight_heads,
        bias_heads,
        rate_heads,
        skip_heads,
        incoming_bwd,
    )
    cotangent = bwd_grad[0].reshape(tokens, heads_here, head_width)
    out_grads = output_pull(cotangent)
    state_grad = out_grads[6].reshape(heads_here, -1)
    back_seeds = (jnp.ones_like(decay_bwd), jnp.zeros_like(state_grad))
    adjoint_flat = entering_2((decay_bwd, state_grad), "seq", back_join, back_seeds)[1]
    decay_grad = jnp.sum(adjoint_flat * incoming_flat, axis=1)
    sum_grads = summary_pull((decay_grad, adjoint_flat.reshape(state_shape)))
    mixer_grad = (out_grads[1].astype(jnp.float32) + sum_grads[1].astype(jnp.float32)).astype(
        jnp.bfloat16
    )
    mixer_full = lax.all_gather(mixer_grad, "head", axis=1, tiled=True)
    back_proj = jnp.dot(mixer_full, full_weight, preferred_element_type=jnp.float32)
    value_grad = (out_grads[0].astype(jnp.float32) + sum_grads[0].astype(jnp.float32)).reshape(
        tokens, channels_here
    ) + back_proj
    value_grad = value_grad.astype(jnp.bfloat16)
    prev_part = shifted(value_grad.reshape(1, tokens, channels_here), "section", -1)
    grad_rows = lax.psum_scatter(
        lax.dot_general(
            mixer_full, bwd_flat, (((0,), (0,)), ((), ())), preferred_element_type=jnp.float32
        ).astype(jnp.bfloat16),
        "seq",
        scatter_dimension=0,
        tiled=True,
    ).astype(jnp.float32)
    totals = lax.psum(
        (
            (out_grads[2] + sum_grads[2]).reshape(channels_here),
            out_grads[3] + sum_grads[3],
            out_grads[4] + sum_grads[4],
            out_grads[5],
        ),
        "seq",
    )
    return (
        prev_part,
        grad_rows[None],
        totals[0][None],
        totals[1][None],
        totals[2][None],
        totals[3][None],
    )


def solution(mesh):
    in_specs = (
        P("section", "seq", "head"),
        P("section", "seq"),
        P("section", "seq", "head"),
        P("section", "seq", "head"),
        P("section", "head"),
        P("section", "head"),
        P("section", "head"),
        P("section", "head"),
    )
    out_specs = (
        P("section", "seq", "head"),
        P("section", "seq", "head"),
        P("section", "head"),
        P("section", "head"),
        P("section", "head"),
        P("section", "head"),
    )
    return jax.shard_map(shards, mesh=mesh, in_specs=in_specs, out_specs=out_specs, check_vma=False)
```

profile of v0, /device:TPU:4, one launch (start us, length us, event | category | flops | bytes accessed | tf_op | source)
XLA Modules:
  0.0 256.7 jit_solution(6643911628214129203)
XLA Ops:
  7.2 1.3 slice.21
  8.5 3.4 %collective-permute-start = (s32[1]{0:T(128)}, s32[1]{0:T(128)}, u32[]{:S(2)}, u32[]{:S(2)}) collective-permute-start(s32[1]{0:T(128)} %bitcast.17), channel_id=1, source_target_pairs={{0,2},{2,4},{4,6},{6,8},{8,10},{10,12},{12,14},{1,3},{3,5},{5,7},{... | collective-permute-start | bytes 20 | tf_op jit(solution)/shard_map/ppermute | solution.py:12
  11.9 31.0 %all-gather = bf16[1,256,1792]{2,1,0:T(8,128)(2,1)S(1)} all-gather(bf16[1,32,1792]{2,1,0:T(8,128)(2,1)} %param.16), channel_id=2, replica_groups=mesh['section'=2,'seq'=8,'head'=2] {'seq'}, dimensions={1}, use_global_device_ids=true | all-gather | bytes 1032192 | tf_op jit(solution)/shard_map/all_gather | solution.py:152
  42.9 1.5 convolution_convert_fusion.7
  47.5 1.2 broadcast_compare_fusion.1
  48.8 0.9 exponential_multiply_fusion
  50.4 3.5 %reduce-scatter.7.cloned.1.call-done = bf16[128,128]{1,0:T(8,128)(2,1)} async-done(((bf16[256,128]{1,0:T(8,128)(2,1)}), bf16[128,128]{1,0:T(8,128)(2,1)}) %reduce-scatter.7.cloned.1.call-update) | async-done | bytes 32784
  55.0 1.1 convert_element_type.239
  57.1 1.3 add_bitcast_fusion.1
  58.4 1.4 broadcast_compare_fusion
  59.9 16.9 %all-gather.1 = bf16[8,1,28]{2,1,0:T(2,128)(2,1)S(1)} all-gather(bf16[1,1,28]{2,1,0:T(2,128)(2,1)} %get-tuple-element.322), channel_id=1, replica_groups=mesh['section'=2,'seq'=8,'head'=2] {'seq'}, dimensions={0}, use_global_device_ids=true | all-gather | bytes 504 | tf_op jit(solution)/shard_map/all_gather | solution.py:18
  77.3 1.9 fusion.28
  80.7 1.1 convert_element_type.246
  82.7 22.8 %all-gather.5.cloned.1.call-done = bf16[8,28,4096]{2,1,0:T(8,128)(2,1)} async-done(((bf16[1,28,4096]{2,1,0:T(8,128)(2,1)}), bf16[8,28,4096]{2,1,0:T(8,128)(2,1)}) %all-gather.5.cloned.1.call-update) | async-done | bytes 1835024 | tf_op jit(solution)/shard_map/all_gather | solution.py:18
  105.5 14.4 %while.30 = (s32[]{:T(128)}, f32[28,4096]{1,0:T(8,128)S(1)}, s32[]{:T(128)}, bf16[8,28]{1,0:T(8,128)(2,1)}, bf16[8,28,4096]{2,1,0:T(8,128)(2,1)}, /*index=5*/s32[]{:T(128)}, s32[]{:T(128)}) while((s32[]{:T(128)}, f32[28,4096]{1,0:T(8,128)S(1)}, s32[]{:T(128)}, bf16[8,28]{1,0:T(8,128)(2,1)}, bf16[8,28,4096]{2,1,0:T(8,128)(2,1)}, ...), condition=%wide.region_3.5_spmd.clone, body=%wide.region_2.4_spmd.clone.sunk | while | flops 573472 | bytes 1147273 | solution.py:35
  106.2 1.1 fusion.116
  108.0 1.1 fusion.116
  109.8 1.1 fusion.116
  111.6 1.1 fusion.116
  113.4 1.1 fusion.116
  115.3 1.1 fusion.116
  117.1 1.1 fusion.116
  118.9 1.1 fusion.116
  120.0 36.1 %all-gather.7.cloned.1.call-done = bf16[8,28,4096]{2,1,0:T(8,128)(2,1)} async-done(((bf16[1,28,4096]{2,1,0:T(8,128)(2,1)}), bf16[8,28,4096]{2,1,0:T(8,128)(2,1)}) %all-gather.7.cloned.1.call-update) | async-done | bytes 1835024 | tf_op jit(solution)/shard_map/all_gather | solution.py:41
  156.1 14.4 %while.31 = (s32[]{:T(128)}, f32[28,4096]{1,0:T(8,128)S(1)}, s32[]{:T(128)}, bf16[8,28,4096]{2,1,0:T(8,128)(2,1)}, bf16[8,28]{1,0:T(8,128)(2,1)}, /*index=5*/s32[]{:T(128)}, s32[]{:T(128)}, s32[]{:T(128)}, s32[]{:T(128)}) while((s32[]{:T(128)}, f32[28,4096]{1,0:T(8,128)S(1)}, s32[]{:T(128)}, bf16[8,28,4096]{2,1,0:T(8,128)(2,1)}, ...), condition=%wide.region_8.10_spmd.clone, body=%wide.region_7.9_spmd.clone.sunk | while | flops 573476 | bytes 1147335 | solution.py:59
  156.7 1.1 fusion.117
  158.6 1.1 fusion.117
  160.4 1.1 fusion.117
  162.2 1.1 fusion.117
  164.0 1.1 fusion.117
  165.8 1.1 fusion.117
  167.6 1.1 fusion.117
  169.4 1.1 fusion.117
  170.5 1.2 reshape.241
  172.8 1.5 multiply_reduce_fusion
  175.3 1.9 fusion.14
  177.5 1.2 copy.90
  178.7 2.3 fusion.26
  182.0 2.0 all_gather.24
  184.0 1.3 convolution_convert_fusion
  186.3 0.9 fusion.24
  187.8 1.3 copy.100
  189.1 1.5 fusion.3
  190.6 1.3 collective-permute-start.1
  192.7 0.8 fusion.93
  193.7 19.7 %all-reduce.4 = (f32[1,1792]{1,0:T(1,128)}, f32[1,28]{1,0:T(1,128)}, f32[1,28]{1,0:T(1,128)}, f32[1,28]{1,0:T(1,128)}) all-reduce(f32[1,1792]{1,0:T(1,128)S(1)} %broadcast_in_dim.73, f32[1,28]{1,0:T(1,128)S(1)} %get-tuple-element.329, f32[1,28]{1,0:T(1,128)S(1)} %get-tuple-element.328, ...), channel_id=1, replica_groups=mesh['section'=2,'seq'=8,'head'=2] {'seq'}, use_global_device_ids=true, to_apply=%region_15.17 | all-reduce | flops 1876 | bytes 15008 | tf_op jit(solution)/shard_map/psum | solution.py:219
  213.3 34.4 %reduce-scatter.5.cloned.1.call-done = bf16[32,1792]{1,0:T(8,128)(2,1)} async-done(((bf16[256,1792]{1,0:T(8,128)(2,1)}), bf16[32,1792]{1,0:T(8,128)(2,1)}) %reduce-scatter.5.cloned.1.call-update) | async-done | bytes 114704 | tf_op jit(solution)/shard_map/reduce_scatter | solution.py:211
  247.8 1.6 bitcast_convert_fusion.2
  (141 shorter events, 25.1 us)
Async XLA Ops:
  7.2 38.1 %copy-start = (bf16[1,128,1792]{2,1,0:T(8,128)(2,1)S(1)}, bf16[1,128,1792]{2,1,0:T(8,128)(2,1)}, u32[]{:S(2)}) copy-start(bf16[1,128,1792]{2,1,0:T(8,128)(2,1)} %param.13) | copy-start | bytes 1376260
  7.2 38.3 %copy-start.27 = (f32[1,28]{1,0:T(1,128)S(1)}, f32[1,28]{1,0:T(1,128)}, u32[]{:S(2)}) copy-start(f32[1,28]{1,0:T(1,128)} %param.19) | copy-start | bytes 340
  7.2 38.4 %copy-start.15 = (f32[1,1792]{1,0:T(1,128)S(1)}, f32[1,1792]{1,0:T(1,128)}, u32[]{:S(2)}) copy-start(f32[1,1792]{1,0:T(1,128)} %param.17) | copy-start | bytes 21508
  7.2 46.7 %reduce-scatter.7.cloned.1.call-start = ((), (), s32[]{:S(2)}) async-start(), calls=%async_computation.5 | async-start | bytes 98304
  8.5 37.7 %collective-permute-start = (s32[1]{0:T(128)}, s32[1]{0:T(128)}, u32[]{:S(2)}, u32[]{:S(2)}) collective-permute-start(s32[1]{0:T(128)} %bitcast.17), channel_id=1, source_target_pairs={{0,2},{2,4},{4,6},{6,8},{8,10},{10,12},{12,14},{1,3},{3,5},{5,7},{... | collective-permute-start | bytes 20 | tf_op jit(solution)/shard_map/ppermute | solution.py:12
  42.9 4.6 %copy-start.22 = (s32[1,128]{1,0:T(1,128)S(1)}, s32[1,128]{1,0:T(1,128)}, u32[]{:S(2)}) copy-start(s32[1,128]{1,0:T(1,128)} %param.14) | copy-start | bytes 1540
  42.9 5.8 %copy-start.23 = (f32[1,28]{1,0:T(1,128)S(1)}, f32[1,28]{1,0:T(1,128)}, u32[]{:S(2)}) copy-start(f32[1,28]{1,0:T(1,128)} %param.18) | copy-start | bytes 340
  45.2 60.4 %all-gather.5.cloned.1.call-start = ((), (), s32[]{:S(2)}) async-start(), calls=%async_computation.2 | async-start | bytes 2359296 | tf_op jit(solution)/shard_map/all_gather | solution.py:18
  45.5 31.8 %copy-start.2 = (bf16[1,128,1792]{1,2,0:T(8,128)(2,1)}, bf16[1,128,1792]{1,2,0:T(8,128)(2,1)S(1)}, u32[]{:S(2)}) copy-start(bf16[1,128,1792]{1,2,0:T(8,128)(2,1)S(1)} %copy.82) | copy-start | bytes 1376260
  45.5 11.4 %copy-start.6 = (bf16[1,128,1792]{2,1,0:T(8,128)(2,1)S(1)}, bf16[1,128,1792]{2,1,0:T(8,128)(2,1)}, u32[]{:S(2)}) copy-start(bf16[1,128,1792]{2,1,0:T(8,128)(2,1)} %param.15) | copy-start | bytes 1376260
  45.5 4.1 %copy-start.31 = (f32[28]{0:T(128)}, f32[28]{0:T(128)S(1)}, u32[]{:S(2)}) copy-start(f32[28]{0:T(128)S(1)} %negate_bitcast_fusion) | copy-start | bytes 340
  48.7 0.9 copy-start.29
  48.7 5.2 %copy-start.16 = (pred[128]{0:T(512)(128)(4,1)}, pred[128]{0:T(512)(128)(4,1)S(1)}, u32[]{:S(2)}) copy-start(pred[128]{0:T(512)(128)(4,1)S(1)} %get-tuple-element.312) | copy-start | bytes 388
  48.7 5.2 %copy-start.18 = (f32[128]{0:T(128)}, f32[128]{0:T(128)S(1)}, u32[]{:S(2)}) copy-start(f32[128]{0:T(128)S(1)} %get-tuple-element.313) | copy-start | bytes 1540
  49.6 0.6 copy-start.12
  50.3 3.7 %copy-start.20 = (f32[28]{0:T(128)}, f32[28]{0:T(128)S(1)}, u32[]{:S(2)}) copy-start(f32[28]{0:T(128)S(1)} %get-tuple-element.321) | copy-start | bytes 340
  55.0 24.9 %copy-start.7 = (bf16[128,128]{1,0:T(8,128)(2,1)S(1)}, bf16[128,128]{1,0:T(8,128)(2,1)}, u32[]{:S(2)}) copy-start(bf16[128,128]{1,0:T(8,128)(2,1)} %reduce-scatter.7.cloned.1.call-done) | copy-start | bytes 98308
  56.2 99.9 %all-gather.7.cloned.1.call-start = ((), (), s32[]{:S(2)}) async-start(), calls=%async_computation.3 | async-start | bytes 2359296 | tf_op jit(solution)/shard_map/all_gather | solution.py:41
  57.1 22.8 %copy-start.9 = (f32[128,28]{0,1:T(8,128)S(1)}, f32[128,28]{0,1:T(8,128)}, u32[]{:S(2)}) copy-start(f32[128,28]{0,1:T(8,128)} %get-tuple-element.326) | copy-start | bytes 43012
  82.7 165.1 %reduce-scatter.5.cloned.1.call-start = ((), (), s32[]{:S(2)}) async-start(), calls=%async_computation.4 | async-start | bytes 1032192 | tf_op jit(solution)/shard_map/reduce_scatter | solution.py:211
  172.4 2.9 %copy-start.3 = (bf16[1,128,1792]{1,2,0:T(8,128)(2,1)S(1)}, bf16[1,128,1792]{1,2,0:T(8,128)(2,1)}, u32[]{:S(2)}) copy-start(bf16[1,128,1792]{1,2,0:T(8,128)(2,1)} %copy-done.2) | copy-start | bytes 1376260
  172.8 2.5 copy-start.10
  172.8 2.5 copy-start.11
  172.8 2.5 copy-start.13
  172.8 2.5 copy-start.14
  178.7 2.4 copy-start.4
  181.0 3.0 %copy-start.1 = (bf16[1,128,1792]{2,1,0:T(8,128)(2,1)S(1)}, bf16[1,128,1792]{2,1,0:T(8,128)(2,1)}, u32[]{:S(2)}) copy-start(bf16[1,128,1792]{2,1,0:T(8,128)(2,1)} %param.13) | copy-start | bytes 1376260
  181.7 3.6 %copy-start.25 = (f32[28]{0:T(128)S(1)}, f32[28]{0:T(128)}, u32[]{:S(2)}) copy-start(f32[28]{0:T(128)} %multiply_reduce_fusion.2) | copy-start | bytes 340
  181.7 3.9 %copy-start.17 = (pred[128]{0:T(512)(128)(4,1)S(1)}, pred[128]{0:T(512)(128)(4,1)}, u32[]{:S(2)}) copy-start(pred[128]{0:T(512)(128)(4,1)} %copy-done.16) | copy-start | bytes 388
  181.7 3.9 %copy-start.19 = (f32[128]{0:T(128)S(1)}, f32[128]{0:T(128)}, u32[]{:S(2)}) copy-start(f32[128]{0:T(128)} %copy-done.18) | copy-start | bytes 1540
  181.7 3.9 %copy-start.21 = (f32[28]{0:T(128)S(1)}, f32[28]{0:T(128)}, u32[]{:S(2)}) copy-start(f32[28]{0:T(128)} %copy-done.20) | copy-start | bytes 340
  181.8 3.9 %copy-start.24 = (f32[1,28]{1,0:T(1,128)S(1)}, f32[1,28]{1,0:T(1,128)}, u32[]{:S(2)}) copy-start(f32[1,28]{1,0:T(1,128)} %param.18) | copy-start | bytes 340
  181.8 3.9 %copy-start.30 = (f32[128]{0:T(128)S(1)}, f32[128]{0:T(128)}, u32[]{:S(2)}) copy-start(f32[128]{0:T(128)} %copy-done.29) | copy-start | bytes 1540
  181.8 3.9 %copy-start.32 = (f32[28]{0:T(128)S(1)}, f32[28]{0:T(128)}, u32[]{:S(2)}) copy-start(f32[28]{0:T(128)} %copy-done.31) | copy-start | bytes 340
  181.9 4.4 %copy-start.8 = (f32[28,64]{1,0:T(8,128)S(1)}, f32[28,64]{1,0:T(8,128)}, u32[]{:S(2)}) copy-start(f32[28,64]{1,0:T(8,128)} %reshape_squeeze.10) | copy-start | bytes 21508
  181.9 4.4 %copy-start.33 = (f32[28]{0:T(128)S(1)}, f32[28]{0:T(128)}, u32[]{:S(2)}) copy-start(f32[28]{0:T(128)} %add_bitcast_fusion.1) | copy-start | bytes 340
  186.3 1.0 copy-start.5
  189.1 4.5 %copy-start.28 = (f32[1,28]{1,0:T(1,128)S(1)}, f32[1,28]{1,0:T(1,128)}, u32[]{:S(2)}) copy-start(f32[1,28]{1,0:T(1,128)} %param.19) | copy-start | bytes 340
  189.1 4.6 %copy-start.26 = (f32[28]{0:T(128)S(1)}, f32[28]{0:T(128)}, u32[]{:S(2)}) copy-start(f32[28]{0:T(128)} %reduce_sum.161) | copy-start | bytes 340
  190.6 22.7 %collective-permute-start.1 = (bf16[1,128,1792]{2,1,0:T(8,128)(2,1)S(1)}, bf16[1,128,1792]{2,1,0:T(8,128)(2,1)S(1)}, u32[]{:S(2)}, u32[]{:S(2)}) collective-permute-start(bf16[1,128,1792]{2,1,0:T(8,128)(2,1)S(1)} %fusion.3), channel_id=1, source_target_pairs={{16,0},{17,1},{18,2},{19,3},{20,4},{21,5},{22,6},{23,7},{24,8},{25... | collective-permute-start | bytes 1376264 | tf_op jit(solution)/shard_map/ppermute | solution.py:12
Sparse Core Ops, SparseCore 0:
  45.3 8.5 reduce-scatter.6
  56.3 49.2 all-gather.4
  108.2 47.7 all-gather.6
  185.5 62.2 reduce-scatter.4
where the time goes:
time: 260 us; the launch traced here: 257 us
  waiting for transfers between devices  96.9 us (37%)
  blocking collectives  69.5 us (27%)
  other arithmetic  39.6 us (15%)
  matrix products  17.4 us (7%)
  between operations  15.6 us (6%)
  local copies, waits for them, and re-layouts  12.4 us (5%)
  starting transfers between devices  4.87 us (2%)
    all_gather x1, waiting for transfers between devices, entering_2(): lax.all_gather(part.astype(kind), axis)  36.1 us
    reduce_scatter x1, waiting for transfers between devices, shards(): lax.psum_scatter(lax.dot_general(mixer_full, bwd_flat, (((0,), (0,)), (()...  34.4 us
    all_gather x1, blocking collectives, shards(): full_weight = lax.all_gather(proj_weight[0], 'seq', axis=0, tiled=True)  31 us
    all_gather x1, waiting for transfers between devices, entering(): lax.all_gather(part.astype(kind), axis)  22.8 us
    psum x1, blocking collectives, shards(): lax.psum(((out_grads[2] + sum_grads[2]).reshape(channels_here), out_grads...  19.7 us
    select_n x16, other arithmetic, lap(): return jax.tree.map(lambda a, b: jnp.where(reached, a, b), new, before)  17.4 us
    all_gather x1, blocking collectives, entering(): lax.all_gather(part.astype(kind), axis)  16.9 us
    convert_element_type x8, other arithmetic, lap(): part[k].astype(own.dtype)  5.53 us
  transfers between devices with their start and end apart: 6, of which 4 were waited for; matrix products, arithmetic and copies ran while one was open for 14% of the time, Pallas kernels for 0%

commit v1 on v0

--- a/solution.py
+++ b/solution.py
@@ -10,53 +10,6 @@
     devices = range(lax.axis_size(axis))
     route = [(i - distance, i) for i in devices if i - distance in devices]
     return lax.ppermute(block, axis, route)
-
-
-def entering(value, axis, combine, identity):
-    size, mine = (lax.axis_size(axis), lax.axis_index(axis))
-    everything = jax.tree.map(
-        lambda part, kind: lax.all_gather(part.astype(kind), axis),
-        value,
-        (jnp.bfloat16, jnp.bfloat16),
-    )
-    start = jax.tree.map(
-        lambda part, zero: jnp.broadcast_to(jnp.asarray(zero, part.dtype), part.shape),
-        value,
-        identity,
-    )
-
-    def lap(k, before):
-        reached = k < mine
-        new = combine(
-            before, jax.tree.map(lambda part, own: part[k].astype(own.dtype), everything, value)
-        )
-        return jax.tree.map(lambda a, b: jnp.where(reached, a, b), new, before)
-
-    return lax.fori_loop(0, size, lap, start)
-
-
-def entering_2(value, axis, combine, identity):
-    size, mine = (lax.axis_size(axis), lax.axis_index(axis))
-    everything = jax.tree.map(
-        lambda part, kind: lax.all_gather(part.astype(kind), axis),
-        value,
-        jax.tree.map(lambda a: jnp.bfloat16 if a.dtype == jnp.float32 else a.dtype, value),
-    )
-    start = jax.tree.map(
-        lambda part, zero: jnp.broadcast_to(jnp.asarray(zero, part.dtype), part.shape),
-        value,
-        identity,
-    )
-
-    def lap(k, before):
-        at = size - 1 - k
-        reached = at > mine
-        new = combine(
-            before, jax.tree.map(lambda part, own: part[at].astype(own.dtype), everything, value)
-        )
-        return jax.tree.map(lambda a, b: jnp.where(reached, a, b), new, before)
-
-    return lax.fori_loop(0, size, lap, start)
 
 
 def contract(spec, left, right):
@@ -128,12 +81,24 @@
     return combined.astype(jnp.bfloat16)
 
 
-def carry_join(earlier, later):
-    return (earlier[0] * later[0], later[0][:, None] * earlier[1] + later[1])
-
-
-def back_join(earlier, later):
-    return (earlier[0] * later[0], later[1] + later[0][:, None] * earlier[1])
+def scan_rounds(decay, state, axis, forward):
+    size, mine = (lax.axis_size(axis), lax.axis_index(axis))
+    far_decay, far_state = (decay, state)
+    near_decay = jnp.ones_like(decay)
+    near_state = jnp.zeros_like(state)
+    distance = 1
+    while distance < size:
+        got_decay, got_state = shifted(
+            (far_decay, far_state.astype(jnp.bfloat16)), axis, distance if forward else -distance
+        )
+        got_state = got_state.astype(jnp.float32)
+        near_state = near_state + near_decay[:, None] * got_state
+        near_decay = near_decay * got_decay
+        if distance * 2 < size:
+            far_state = far_state + far_decay[:, None] * got_state
+            far_decay = far_decay * got_decay
+        distance *= 2
+    return near_state
 
 
 def shards(bwd_input, bwd_docs, bwd_grad, proj_weight, step_weight, step_bias, rate_log, skip_gain):
@@ -154,6 +119,7 @@
     mixer_bwd = lax.psum_scatter(
         partial_value.astype(jnp.bfloat16), "head", scatter_dimension=1, tiled=True
     )
+    cotangent = bwd_grad[0].reshape(tokens, heads_here, head_width)
 
     def summary_bwd(values_in, mixer_in, weight_in, bias_in, rate_in):
         return span_summary(values_in, mixer_in, weight_in, bias_in, rate_in, docs_bwd, doc_before)
@@ -164,9 +130,6 @@
     decay_bwd, state_bwd = summary_out
     state_shape = state_bwd.shape
     state_flat = state_bwd.reshape(heads_here, -1)
-    seeds = (jnp.ones_like(decay_bwd), jnp.zeros_like(state_flat))
-    incoming_flat = entering((decay_bwd, state_flat), "seq", carry_join, seeds)[1]
-    incoming_bwd = incoming_flat.reshape(state_shape)
 
     def output_bwd(values_in, mixer_in, weight_in, bias_in, rate_in, skip_in, state_in):
         return span_output(
@@ -181,6 +144,17 @@
             state_in,
         )
 
+    def carried_only(state_in):
+        return output_bwd(
+            bwd_values, mixer_bwd, weight_heads, bias_heads, rate_heads, skip_heads, state_in
+        )
+
+    state_grad = jax.vjp(carried_only, jnp.zeros(state_shape, jnp.float32))[1](cotangent)[0]
+    state_grad = state_grad.reshape(heads_here, -1)
+    incoming_flat = scan_rounds(decay_bwd, state_flat, "seq", True)
+    adjoint_flat = scan_rounds(decay_bwd, state_grad, "seq", False)
+    incoming_bwd = incoming_flat.reshape(state_shape)
+
     unused, output_pull = jax.vjp(
         output_bwd,
         bwd_values,
@@ -191,11 +165,7 @@
         skip_heads,
         incoming_bwd,
     )
-    cotangent = bwd_grad[0].reshape(tokens, heads_here, head_width)
     out_grads = output_pull(cotangent)
-    state_grad = out_grads[6].reshape(heads_here, -1)
-    back_seeds = (jnp.ones_like(decay_bwd), jnp.zeros_like(state_grad))
-    adjoint_flat = entering_2((decay_bwd, state_grad), "seq", back_join, back_seeds)[1]
     decay_grad = jnp.sum(adjoint_flat * incoming_flat, axis=1)
     sum_grads = summary_pull((decay_grad, adjoint_flat.reshape(state_shape)))
     mixer_grad = (out_grads[1].astype(jnp.float32) + sum_grads[1].astype(jnp.float32)).astype(

time: 260 us -> 212 us (0.82)
  waiting for transfers between devices: 96.9 us -> 51.4 us
  starting transfers between devices: 4.87 us -> 33.7 us
  other arithmetic: 39.6 us -> 20.5 us
  blocking collectives: 69.5 us -> 50.6 us
  local copies, waits for them, and re-layouts: 12.4 us -> 18.9 us
    all_gather x2 -> x0, waiting for transfers between devices: 58.9 us -> none  [the longest x1 36.1 us: entering_2(): lax.all_gather(part.astype(kind), axis)]
    ppermute x2 -> x12, starting transfers between devices: 4.71 us -> 33.7 us  [shifted(): return lax.ppermute(block, axis, route)]
    select_n x16 -> x0, other arithmetic: 17.4 us -> none  [lap(): return jax.tree.map(lambda a, b: jnp.where(reached, a, b), new, before)]
    all_gather x1 -> x0, blocking collectives: 16.9 us -> none  [entering(): lax.all_gather(part.astype(kind), axis)]
    ppermute x2 -> x12, waiting for transfers between devices: 0.01 us -> 9.55 us  [shifted(): return lax.ppermute(block, axis, route)]
    convert_element_type x16 -> x5, other arithmetic: 11 us -> 4.74 us  [scan_rounds(): far_state.astype(jnp.bfloat16)]
    reduce_scatter x1, waiting for transfers between devices: 34.4 us -> 38.7 us  [shards(): lax.psum_scatter(lax.dot_general(mixer_full, bwd_flat, (((0,), (0,)), (()...]
    reshape x0 -> x2, local copies, waits for them, and re-layouts: none -> 3.02 us  [the longest x1 1.52 us: shards(): state_flat = state_bwd.reshape(heads_here, -1)]
  transfers between devices with their start and end apart: 6 -> 14, of which waited for: 4 -> 5; matrix products, arithmetic and copies ran while one was open for 14% -> 13% of each run, Pallas kernels for 0% -> 0%
where the time goes in v1:
time: 212 us; the launch traced here: 209 us
  waiting for transfers between devices  51.4 us (24%)
  blocking collectives  50.6 us (24%)
  starting transfers between devices  33.7 us (16%)
  other arithmetic  20.5 us (10%)
  local copies, waits for them, and re-layouts  18.9 us (9%)
  matrix products  17.6 us (8%)
  between operations  16.4 us (8%)
    reduce_scatter x1, waiting for transfers between devices, shards(): lax.psum_scatter(lax.dot_general(mixer_full, bwd_flat, (((0,), (0,)), (()...  38.7 us
    ppermute x12, starting transfers between devices, shifted(): return lax.ppermute(block, axis, route)  33.7 us
    all_gather x1, blocking collectives, shards(): full_weight = lax.all_gather(proj_weight[0], 'seq', axis=0, tiled=True)  31 us
    psum x1, blocking collectives, shards(): lax.psum(((out_grads[2] + sum_grads[2]).reshape(channels_here), out_grads...  17.6 us
    ppermute x12, waiting for transfers between devices, shifted(): return lax.ppermute(block, axis, route)  9.55 us
    dot_general x5, matrix products, contract(): return jnp.einsum(spec, left, right, preferred_element_type=jnp.float32)  5.53 us
    convert_element_type x5, other arithmetic, scan_rounds(): far_state.astype(jnp.bfloat16)  4.74 us
    unnamed x132, local copies, waits for them, and re-layouts  4.3 us
  transfers between devices with their start and end apart: 14, of which 5 were waited for; matrix products, arithmetic and copies ran while one was open for 13% of the time, Pallas kernels for 0%

profile of v1, /device:TPU:4, one launch (start us, length us, event | category | flops | bytes accessed | tf_op | source)
XLA Modules:
  0.0 209.1 jit_solution(10798965876663877636)
XLA Ops:
  7.2 1.3 slice.21
  8.5 3.4 %collective-permute-start.1 = (s32[1]{0:T(128)}, s32[1]{0:T(128)}, u32[]{:S(2)}, u32[]{:S(2)}) collective-permute-start(s32[1]{0:T(128)} %bitcast.18), channel_id=1, source_target_pairs={{0,2},{2,4},{4,6},{6,8},{8,10},{10,12},{12,14},{1,3},{3,5},{5,7},{... | collective-permute-start | bytes 20 | tf_op jit(solution)/shard_map/ppermute | solution.py:12
  11.9 31.0 %all-gather = bf16[1,256,1792]{2,1,0:T(8,128)(2,1)S(1)} all-gather(bf16[1,32,1792]{2,1,0:T(8,128)(2,1)} %param.12), channel_id=2, replica_groups=mesh['section'=2,'seq'=8,'head'=2] {'seq'}, dimensions={1}, use_global_device_ids=true | all-gather | bytes 1032192 | tf_op jit(solution)/shard_map/all_gather | solution.py:117
  45.5 1.3 broadcast_compare_fusion.1
  49.7 3.1 %reduce-scatter.7.cloned.1.call-done = bf16[128,128]{1,0:T(8,128)(2,1)} async-done(((bf16[256,128]{1,0:T(8,128)(2,1)}), bf16[128,128]{1,0:T(8,128)(2,1)}) %reduce-scatter.7.cloned.1.call-update) | async-done | bytes 32784
  53.6 1.4 fusion.37
  55.0 1.5 reshape.210
  57.2 3.4 %collective-permute-start = (bf16[28,4096]{1,0:T(8,128)(2,1)}, bf16[28,4096]{1,0:T(8,128)(2,1)}, u32[]{:S(2)}, u32[]{:S(2)}) collective-permute-start(bf16[28,4096]{1,0:T(8,128)(2,1)} %convert_element_type.189), channel_id=1, source_target_pairs={{0,2},{2,4},{4,6},{6,8},{8,10},{10,12},{12,14},{1,3},{3,5},{5,7},{... | collective-permute-start | bytes 688136 | tf_op jit(solution)/shard_map/ppermute | solution.py:12
  60.6 1.6 convolution_bitcast_fusion
  62.2 2.4 %copy.93 = f32[28,64,64]{2,1,0:T(8,128)} copy(f32[28,64,64]{1,2,0:T(8,128)} %convolution_bitcast_fusion) | data formatting | bytes 917504 | tf_op jit(solution)/shard_map/transpose(jvp(tn,hnp->thp))/transpose | solution.py:75
  64.6 1.5 reshape.212
  66.2 3.1 %collective-permute-start.6 = (bf16[28,4096]{1,0:T(8,128)(2,1)S(1)}, bf16[28,4096]{1,0:T(8,128)(2,1)S(1)}, u32[]{:S(2)}, u32[]{:S(2)}) collective-permute-start(bf16[28,4096]{1,0:T(8,128)(2,1)S(1)} %convert_element_type.200), channel_id=1, source_target_pairs={{2,0},{4,2},{6,4},{8,6},{10,8},{12,10},{14,12},{3,1},{5,3},{7,5},{... | collective-permute-start | bytes 688136 | tf_op jit(solution)/shard_map/ppermute | solution.py:12
  69.3 1.1 fusion.56
  70.4 2.7 %collective-permute-start.3 = (bf16[28,4096]{1,0:T(8,128)(2,1)S(1)}, bf16[28,4096]{1,0:T(8,128)(2,1)S(1)}, u32[]{:S(2)}, u32[]{:S(2)}) collective-permute-start(bf16[28,4096]{1,0:T(8,128)(2,1)S(1)} %fusion.56), channel_id=1, source_target_pairs={{0,4},{2,6},{4,8},{6,10},{8,12},{10,14},{1,5},{3,7},{5,9},{7,11},{... | collective-permute-start | bytes 688136 | tf_op jit(solution)/shard_map/ppermute | solution.py:12
  73.2 4.3 %collective-permute-start.2 = (f32[28]{0:T(128)S(1)}, f32[28]{0:T(128)S(1)}, u32[]{:S(2)}, u32[]{:S(2)}) collective-permute-start(f32[28]{0:T(128)S(1)} %copy-done.36), channel_id=1, source_target_pairs={{0,2},{2,4},{4,6},{6,8},{8,10},{10,12},{12,14},{1,3},{3,5},{5,7},{... | collective-permute-start | bytes 344 | tf_op jit(solution)/shard_map/ppermute | solution.py:12
  77.4 1.9 collective-permute-start.7
  79.4 4.4 %collective-permute-done.7 = f32[28]{0:T(128)S(1)} collective-permute-done((f32[28]{0:T(128)S(1)}, f32[28]{0:T(128)S(1)}, u32[]{:S(2)}, u32[]{:S(2)}) %collective-permute-start.7) | collective-permute-done | bytes 144 | tf_op jit(solution)/shard_map/ppermute | solution.py:12
  84.3 2.0 fusion.41
  86.3 1.4 collective-permute-start.8
  88.5 5.5 %collective-permute-start.5 = (bf16[28,4096]{1,0:T(8,128)(2,1)}, bf16[28,4096]{1,0:T(8,128)(2,1)S(1)}, u32[]{:S(2)}, u32[]{:S(2)}) collective-permute-start(bf16[28,4096]{1,0:T(8,128)(2,1)} %get-tuple-element.40), channel_id=1, source_target_pairs={{0,8},{2,10},{4,12},{6,14},{1,9},{3,11},{5,13},{7,15},{16,24},{18,... | collective-permute-start | bytes 688136 | tf_op jit(solution)/shard_map/ppermute | solution.py:12
  93.9 0.8 collective-permute-done.8
  94.7 0.9 fusion.45
  95.6 1.3 collective-permute-start.10
  97.5 1.4 reshape_squeeze.10
  98.8 2.6 %fusion.25 = (f32[1792]{0:T(1024)}, f32[1,128,1792]{1,2,0:T(8,128)}) fusion(bf16[1,128,1792]{1,2,0:T(8,128)(2,1)S(1)} %copy.81, bf16[1,128,1792]{1,2,0:T(8,128)(2,1)S(1)} %copy.82, f32[128,28]{0,1:T(8,128)} %copy-done.12), kind=kLoop, calls=%fused_computation.45 | loop fusion | flops 1145088 | bytes 1856512 | tf_op jit(solution)/shard_map/transpose(jvp())/reduce_sum | solution.py:77
  101.4 1.4 reduce_sum.160
  102.8 3.9 %collective-permute-start.4 = (f32[28]{0:T(128)}, f32[28]{0:T(128)}, u32[]{:S(2)}, u32[]{:S(2)}) collective-permute-start(f32[28]{0:T(128)} %copy-done.49), channel_id=1, source_target_pairs={{0,4},{2,6},{4,8},{6,10},{8,12},{10,14},{1,5},{3,7},{5,9},{7,11},{... | collective-permute-start | bytes 344 | tf_op jit(solution)/shard_map/ppermute | solution.py:12
  106.7 1.4 reduce_sum.161
  108.1 1.3 collective-permute-start.9
  110.1 4.4 %collective-permute-done.9 = f32[28]{0:T(128)S(1)} collective-permute-done((f32[28]{0:T(128)}, f32[28]{0:T(128)S(1)}, u32[]{:S(2)}, u32[]{:S(2)}) %collective-permute-start.9) | collective-permute-done | bytes 144 | tf_op jit(solution)/shard_map/ppermute | solution.py:12
  115.1 0.8 fusion.83
  116.6 2.9 %multiply_reduce_fusion.2 = (f32[28]{0:T(128)}, bf16[28,4096]{1,0:T(8,128)(2,1)S(1)}, f32[28,4096]{1,0:T(8,128)}) fusion(bf16[28,4096]{1,0:T(8,128)(2,1)} %collective-permute-done.10, f32[28]{0:T(128)S(1)} %mul.365, bf16[28,4096]{1,0:T(8,128)(2,1)S(1)} %collective-permute-done.8, f32[28]{0:T(128)} %copy-done.46, bf16[28,4096]{1,0:T(8,128)(2,1)S(1)} %copy-done.2, ...), kind=kLoop, calls=%fused_computation.79 | loop fusion | flops 1949668 | bytes 2064944 | tf_op jit(solution)/shard_map/reduce_sum | solution.py:169
  120.8 1.2 fusion.100
  122.2 2.5 %fusion.12 = (f32[28,128]{1,0:T(8,128)}, f32[28,128]{1,0:T(8,128)}, f32[28,128]{1,0:T(8,128)S(1)}, bf16[128,128]{1,0:T(8,128)(2,1)S(1)}) fusion(f32[28,128]{1,0:T(8,128)S(1)} %copy.85, f32[128,128]{1,0:T(8,128)S(1)} %copy-done.15, f32[128,128]{1,0:T(8,128)S(1)} %copy-done.17, f32[28,128]{1,0:T(8,128)S(1)} %bitcast.243, pred[128,128]{1,0:T(8,128)(4,1)S(1)} %copy-done.25, ...), kind=kOutput, calls=%fused_computation.19 | convolution fusion | flops 66491904 | bytes 1169408 | tf_op jit(solution)/shard_map/transpose(jvp(hts,shp->thp))/dot_general | solution.py:16
  125.0 1.4 reshape.211
  126.4 1.2 copy.90
  127.6 1.7 fusion.87
  130.8 2.2 %fusion.24 = bf16[128,64]{0,1:T(8,128)(2,1)S(1)} fusion(bf16[128,64]{0,1:T(8,128)(2,1)S(1)} %convolution_convert_fusion.7, f32[128,28,64]{0,2,1:T(8,128)} %bitcast.228, f32[28,64,64]{2,1,0:T(8,128)S(1)} %reshape.211), kind=kOutput, calls=%fused_computation.44 | convolution fusion | flops 176177152 | bytes 1409024 | tf_op jit(solution)/shard_map/transpose(jvp(tn,hnp->thp))/dot_general | solution.py:75
  133.0 2.0 all_gather.7
  135.2 1.4 convolution_convert_fusion
  137.0 0.8 multiply_reduce_fusion.4
  138.2 0.9 fusion.22
  140.4 1.4 collective-permute-start.11
  141.8 0.8 fusion.103
  142.6 0.8 fusion.104
  143.6 17.6 %all-reduce.4 = (f32[1,1792]{1,0:T(1,128)}, f32[1,28]{1,0:T(1,128)}, f32[1,28]{1,0:T(1,128)}, f32[1,28]{1,0:T(1,128)}) all-reduce(f32[1,1792]{1,0:T(1,128)S(1)} %broadcast_in_dim.47, f32[1,28]{1,0:T(1,128)S(1)} %get-tuple-element.50, f32[1,28]{1,0:T(1,128)S(1)} %get-tuple-element.49, ...), channel_id=1, replica_groups=mesh['section'=2,'seq'=8,'head'=2] {'seq'}, use_global_device_ids=true, to_apply=%region_11.13 | all-reduce | flops 1876 | bytes 15008 | tf_op jit(solution)/shard_map/psum | solution.py:189
  161.2 38.7 %reduce-scatter.5.cloned.1.call-done = bf16[32,1792]{1,0:T(8,128)(2,1)} async-done(((bf16[256,1792]{1,0:T(8,128)(2,1)}), bf16[32,1792]{1,0:T(8,128)(2,1)}) %reduce-scatter.5.cloned.1.call-update) | async-done | bytes 114704 | tf_op jit(solution)/shard_map/reduce_scatter | solution.py:181
  199.8 1.6 bitcast_convert_fusion
  (186 shorter events, 15.2 us)
Async XLA Ops:
  7.2 35.8 %copy-start = (bf16[1,128,1792]{2,1,0:T(8,128)(2,1)S(1)}, bf16[1,128,1792]{2,1,0:T(8,128)(2,1)}, u32[]{:S(2)}) copy-start(bf16[1,128,1792]{2,1,0:T(8,128)(2,1)} %param.9) | copy-start | bytes 1376260
  7.2 45.7 %reduce-scatter.7.cloned.1.call-start = ((), (), s32[]{:S(2)}) async-start(), calls=%async_computation.3 | async-start | bytes 98304
  8.5 37.0 %collective-permute-start.1 = (s32[1]{0:T(128)}, s32[1]{0:T(128)}, u32[]{:S(2)}, u32[]{:S(2)}) collective-permute-start(s32[1]{0:T(128)} %bitcast.18), channel_id=1, source_target_pairs={{0,2},{2,4},{4,6},{6,8},{8,10},{10,12},{12,14},{1,3},{3,5},{5,7},{... | collective-permute-start | bytes 20 | tf_op jit(solution)/shard_map/ppermute | solution.py:12
  44.2 155.7 %reduce-scatter.5.cloned.1.call-start = ((), (), s32[]{:S(2)}) async-start(), calls=%async_computation.2 | async-start | bytes 1032192 | tf_op jit(solution)/shard_map/reduce_scatter | solution.py:181
  44.5 3.6 %copy-start.37 = (f32[1,28]{1,0:T(1,128)S(1)}, f32[1,28]{1,0:T(1,128)}, u32[]{:S(2)}) copy-start(f32[1,28]{1,0:T(1,128)} %param.14) | copy-start | bytes 340
  45.3 9.7 %copy-start.59 = (f32[28]{0:T(128)}, f32[28]{0:T(128)S(1)}, u32[]{:S(2)}) copy-start(f32[28]{0:T(128)S(1)} %negate_bitcast_fusion) | copy-start | bytes 340
  46.9 8.1 %copy-start.28 = (pred[128]{0:T(512)(128)(4,1)}, pred[128]{0:T(512)(128)(4,1)S(1)}, u32[]{:S(2)}) copy-start(pred[128]{0:T(512)(128)(4,1)S(1)} %get-tuple-element.31) | copy-start | bytes 388
  46.9 8.1 %copy-start.31 = (f32[128]{0:T(128)}, f32[128]{0:T(128)S(1)}, u32[]{:S(2)}) copy-start(f32[128]{0:T(128)S(1)} %get-tuple-element.32) | copy-start | bytes 1540
  48.4 12.2 %copy-start.12 = (f32[128,28]{0,1:T(8,128)}, f32[128,28]{0,1:T(8,128)S(1)}, u32[]{:S(2)}) copy-start(f32[128,28]{0,1:T(8,128)S(1)} %get-tuple-element.47) | copy-start | bytes 43012
  48.6 7.9 %copy-start.40 = (f32[28]{0:T(128)}, f32[28]{0:T(128)S(1)}, u32[]{:S(2)}) copy-start(f32[28]{0:T(128)S(1)} %slice_bitcast_fusion) | copy-start | bytes 340
  55.0 5.7 %copy-start.8 = (bf16[128,128]{1,0:T(8,128)(2,1)S(1)}, bf16[128,128]{1,0:T(8,128)(2,1)}, u32[]{:S(2)}) copy-start(bf16[128,128]{1,0:T(8,128)(2,1)} %reduce-scatter.7.cloned.1.call-done) | copy-start | bytes 98308
  57.2 12.1 %collective-permute-start = (bf16[28,4096]{1,0:T(8,128)(2,1)}, bf16[28,4096]{1,0:T(8,128)(2,1)}, u32[]{:S(2)}, u32[]{:S(2)}) collective-permute-start(bf16[28,4096]{1,0:T(8,128)(2,1)} %convert_element_type.189), channel_id=1, source_target_pairs={{0,2},{2,4},{4,6},{6,8},{8,10},{10,12},{12,14},{1,3},{3,5},{5,7},{... | collective-permute-start | bytes 688136 | tf_op jit(solution)/shard_map/ppermute | solution.py:12
  66.1 7.0 %copy-start.36 = (f32[28]{0:T(128)S(1)}, f32[28]{0:T(128)}, u32[]{:S(2)}) copy-start(f32[28]{0:T(128)} %exponential_multiply_fusion.1) | copy-start | bytes 340
  66.2 17.6 %collective-permute-start.6 = (bf16[28,4096]{1,0:T(8,128)(2,1)S(1)}, bf16[28,4096]{1,0:T(8,128)(2,1)S(1)}, u32[]{:S(2)}, u32[]{:S(2)}) collective-permute-start(bf16[28,4096]{1,0:T(8,128)(2,1)S(1)} %convert_element_type.200), channel_id=1, source_target_pairs={{2,0},{4,2},{6,4},{8,6},{10,8},{12,10},{14,12},{3,1},{5,3},{7,5},{... | collective-permute-start | bytes 688136 | tf_op jit(solution)/shard_map/ppermute | solution.py:12
  70.4 13.4 %collective-permute-start.3 = (bf16[28,4096]{1,0:T(8,128)(2,1)S(1)}, bf16[28,4096]{1,0:T(8,128)(2,1)S(1)}, u32[]{:S(2)}, u32[]{:S(2)}) collective-permute-start(bf16[28,4096]{1,0:T(8,128)(2,1)S(1)} %fusion.56), channel_id=1, source_target_pairs={{0,4},{2,6},{4,8},{6,10},{8,12},{10,14},{1,5},{3,7},{5,9},{7,11},{... | collective-permute-start | bytes 688136 | tf_op jit(solution)/shard_map/ppermute | solution.py:12
  73.2 6.2 %collective-permute-start.2 = (f32[28]{0:T(128)S(1)}, f32[28]{0:T(128)S(1)}, u32[]{:S(2)}, u32[]{:S(2)}) collective-permute-start(f32[28]{0:T(128)S(1)} %copy-done.36), channel_id=1, source_target_pairs={{0,2},{2,4},{4,6},{6,8},{8,10},{10,12},{12,14},{1,3},{3,5},{5,7},{... | collective-permute-start | bytes 344 | tf_op jit(solution)/shard_map/ppermute | solution.py:12
  77.4 6.3 %collective-permute-start.7 = (f32[28]{0:T(128)S(1)}, f32[28]{0:T(128)S(1)}, u32[]{:S(2)}, u32[]{:S(2)}) collective-permute-start(f32[28]{0:T(128)S(1)} %copy-done.36), channel_id=1, source_target_pairs={{2,0},{4,2},{6,4},{8,6},{10,8},{12,10},{14,12},{3,1},{5,3},{7,5},{... | collective-permute-start | bytes 344 | tf_op jit(solution)/shard_map/ppermute | solution.py:12
  79.4 4.5 %copy-start.45 = (f32[28]{0:T(128)}, f32[28]{0:T(128)S(1)}, u32[]{:S(2)}) copy-start(f32[28]{0:T(128)S(1)} %collective-permute-done.2) | copy-start | bytes 340
  83.8 2.5 %copy-start.49 = (f32[28]{0:T(128)}, f32[28]{0:T(128)S(1)}, u32[]{:S(2)}) copy-start(f32[28]{0:T(128)S(1)} %get-tuple-element.42) | copy-start | bytes 340
  83.8 10.9 %copy-start.47 = (f32[28]{0:T(128)}, f32[28]{0:T(128)S(1)}, u32[]{:S(2)}) copy-start(f32[28]{0:T(128)S(1)} %get-tuple-element.43) | copy-start | bytes 340
  83.8 10.9 %copy-start.1 = (bf16[28,4096]{1,0:T(8,128)(2,1)}, bf16[28,4096]{1,0:T(8,128)(2,1)S(1)}, u32[]{:S(2)}) copy-start(bf16[28,4096]{1,0:T(8,128)(2,1)S(1)} %collective-permute-done.6) | copy-start | bytes 688132
  84.3 2.0 copy-start.5
  84.3 3.4 %copy-start.35 = (s32[1,128]{1,0:T(1,128)S(1)}, s32[1,128]{1,0:T(1,128)}, u32[]{:S(2)}) copy-start(s32[1,128]{1,0:T(1,128)} %param.10) | copy-start | bytes 1540
  86.3 10.6 %copy-start.58 = (f32[1,28]{1,0:T(1,128)S(1)}, f32[1,28]{1,0:T(1,128)}, u32[]{:S(2)}) copy-start(f32[1,28]{1,0:T(1,128)} %param.16) | copy-start | bytes 340
  86.3 8.4 %collective-permute-start.8 = (bf16[28,4096]{1,0:T(8,128)(2,1)S(1)}, bf16[28,4096]{1,0:T(8,128)(2,1)S(1)}, u32[]{:S(2)}, u32[]{:S(2)}) collective-permute-start(bf16[28,4096]{1,0:T(8,128)(2,1)S(1)} %get-tuple-element.41), channel_id=1, source_target_pairs={{4,0},{6,2},{8,4},{10,6},{12,8},{14,10},{5,1},{7,3},{9,5},{11,7},{... | collective-permute-start | bytes 688136 | tf_op jit(solution)/shard_map/ppermute | solution.py:12
  88.5 27.4 %collective-permute-start.5 = (bf16[28,4096]{1,0:T(8,128)(2,1)}, bf16[28,4096]{1,0:T(8,128)(2,1)S(1)}, u32[]{:S(2)}, u32[]{:S(2)}) collective-permute-start(bf16[28,4096]{1,0:T(8,128)(2,1)} %get-tuple-element.40), channel_id=1, source_target_pairs={{0,8},{2,10},{4,12},{6,14},{1,9},{3,11},{5,13},{7,15},{16,24},{18,... | collective-permute-start | bytes 688136 | tf_op jit(solution)/shard_map/ppermute | solution.py:12
  95.6 21.0 %collective-permute-start.10 = (bf16[28,4096]{1,0:T(8,128)(2,1)}, bf16[28,4096]{1,0:T(8,128)(2,1)}, u32[]{:S(2)}, u32[]{:S(2)}) collective-permute-start(bf16[28,4096]{1,0:T(8,128)(2,1)} %fusion.45), channel_id=1, source_target_pairs={{8,0},{10,2},{12,4},{14,6},{9,1},{11,3},{13,5},{15,7},{24,16},{26,... | collective-permute-start | bytes 688136 | tf_op jit(solution)/shard_map/ppermute | solution.py:12
  98.8 17.8 %copy-start.2 = (bf16[28,4096]{1,0:T(8,128)(2,1)S(1)}, bf16[28,4096]{1,0:T(8,128)(2,1)}, u32[]{:S(2)}) copy-start(bf16[28,4096]{1,0:T(8,128)(2,1)} %copy-done.1) | copy-start | bytes 688132
  98.8 17.8 %copy-start.6 = (bf16[28,4096]{1,0:T(8,128)(2,1)S(1)}, bf16[28,4096]{1,0:T(8,128)(2,1)}, u32[]{:S(2)}) copy-start(bf16[28,4096]{1,0:T(8,128)(2,1)} %copy-done.5) | copy-start | bytes 688132
  102.8 6.6 %collective-permute-start.4 = (f32[28]{0:T(128)}, f32[28]{0:T(128)}, u32[]{:S(2)}, u32[]{:S(2)}) collective-permute-start(f32[28]{0:T(128)} %copy-done.49), channel_id=1, source_target_pairs={{0,4},{2,6},{4,8},{6,10},{8,12},{10,14},{1,5},{3,7},{5,9},{7,11},{... | collective-permute-start | bytes 344 | tf_op jit(solution)/shard_map/ppermute | solution.py:12
  108.1 6.3 %collective-permute-start.9 = (f32[28]{0:T(128)}, f32[28]{0:T(128)S(1)}, u32[]{:S(2)}, u32[]{:S(2)}) collective-permute-start(f32[28]{0:T(128)} %copy-done.47), channel_id=1, source_target_pairs={{4,0},{6,2},{8,4},{10,6},{12,8},{14,10},{5,1},{7,3},{9,5},{11,7},{... | collective-permute-start | bytes 344 | tf_op jit(solution)/shard_map/ppermute | solution.py:12
  120.0 2.1 copy-start.3
  120.1 2.1 %copy-start.15 = (f32[128,128]{1,0:T(8,128)S(1)}, f32[128,128]{1,0:T(8,128)}, u32[]{:S(2)}) copy-start(f32[128,128]{1,0:T(8,128)} %fusion.83) | copy-start | bytes 196612
  120.1 2.1 %copy-start.17 = (f32[128,128]{1,0:T(8,128)S(1)}, f32[128,128]{1,0:T(8,128)}, u32[]{:S(2)}) copy-start(f32[128,128]{1,0:T(8,128)} %get-tuple-element.46) | copy-start | bytes 196612
  120.1 2.1 %copy-start.21 = (f32[128,28]{0,1:T(8,128)S(1)}, f32[128,28]{0,1:T(8,128)}, u32[]{:S(2)}) copy-start(f32[128,28]{0,1:T(8,128)} %copy-done.20) | copy-start | bytes 43012
  120.1 2.1 %copy-start.25 = (pred[128,128]{1,0:T(8,128)(4,1)S(1)}, pred[128,128]{1,0:T(8,128)(4,1)}, u32[]{:S(2)}) copy-start(pred[128,128]{1,0:T(8,128)(4,1)} %get-tuple-element.45) | copy-start | bytes 49156
  122.1 2.5 %copy-start.23 = (f32[28,128]{1,0:T(8,128)}, f32[28,128]{1,0:T(8,128)S(1)}, u32[]{:S(2)}) copy-start(f32[28,128]{1,0:T(8,128)S(1)} %copy.85) | copy-start | bytes 43012
  135.1 1.9 copy-start.19
  135.1 1.9 copy-start.22
  135.1 1.9 copy-start.30
  135.1 1.9 copy-start.33
  140.3 3.2 %copy-start.51 = (f32[1,28]{1,0:T(1,128)S(1)}, f32[1,28]{1,0:T(1,128)}, u32[]{:S(2)}) copy-start(f32[1,28]{1,0:T(1,128)} %param.15) | copy-start | bytes 340
  140.3 3.2 %copy-start.52 = (f32[28]{0:T(128)S(1)}, f32[28]{0:T(128)}, u32[]{:S(2)}) copy-start(f32[28]{0:T(128)} %get-tuple-element.16) | copy-start | bytes 340
  140.4 3.2 %copy-start.53 = (f32[28]{0:T(128)S(1)}, f32[28]{0:T(128)}, u32[]{:S(2)}) copy-start(f32[28]{0:T(128)} %get-tuple-element.17) | copy-start | bytes 340
  140.4 3.2 %copy-start.54 = (f32[28]{0:T(128)S(1)}, f32[28]{0:T(128)}, u32[]{:S(2)}) copy-start(f32[28]{0:T(128)} %get-tuple-element.35) | copy-start | bytes 340
  140.4 3.2 %copy-start.55 = (f32[28]{0:T(128)S(1)}, f32[28]{0:T(128)}, u32[]{:S(2)}) copy-start(f32[28]{0:T(128)} %get-tuple-element.37) | copy-start | bytes 340
  140.4 3.2 %copy-start.48 = (f32[28]{0:T(128)S(1)}, f32[28]{0:T(128)}, u32[]{:S(2)}) copy-start(f32[28]{0:T(128)} %reduce_sum.161) | copy-start | bytes 340
  140.4 20.8 %collective-permute-start.11 = (bf16[1,128,1792]{2,1,0:T(8,128)(2,1)S(1)}, bf16[1,128,1792]{2,1,0:T(8,128)(2,1)S(1)}, u32[]{:S(2)}, u32[]{:S(2)}) collective-permute-start(bf16[1,128,1792]{2,1,0:T(8,128)(2,1)S(1)} %fusion.1), channel_id=1, source_target_pairs={{16,0},{17,1},{18,2},{19,3},{20,4},{21,5},{22,6},{23,7},{24,8},{25... | collective-permute-start | bytes 1376264 | tf_op jit(solution)/shard_map/ppermute | solution.py:12
  (30 other events, 41.2 us)
Sparse Core Ops, SparseCore 0:
  44.3 8.5 reduce-scatter.6
  136.7 63.0 reduce-scatter.4

commit v2 on v1

--- a/solution.py
+++ b/solution.py
@@ -10,6 +10,34 @@
     devices = range(lax.axis_size(axis))
     route = [(i - distance, i) for i in devices if i - distance in devices]
     return lax.ppermute(block, axis, route)
+
+
+def rotated(block, axis, distance):
+    size = lax.axis_size(axis)
+    route = [(i, (i + distance) % size) for i in range(size)]
+    return lax.ppermute(block, axis, route)
+
+
+def roll_blocks(value, shift, parts, dim):
+    doubled = jnp.concatenate([value, value], axis=dim)
+    width = value.shape[dim] // parts
+    start = ((parts - shift) % parts) * width
+    return lax.dynamic_slice_in_dim(doubled, start, value.shape[dim], axis=dim)
+
+
+def swap_heads(block):
+    return lax.ppermute(block, "head", [(0, 1), (1, 0)])
+
+
+def seq_total(value):
+    size = lax.axis_size("seq")
+    if size & (size - 1):
+        return lax.psum(value, "seq")
+    distance = 1
+    while distance < size:
+        value = value + lax.ppermute(value, "seq", [(i, i ^ distance) for i in range(size)])
+        distance *= 2
+    return value
 
 
 def contract(spec, left, right):
@@ -114,11 +142,23 @@
     skip_heads = skip_gain[0]
     docs_bwd = bwd_docs[0]
     doc_before = shifted(docs_bwd[-1:], "seq", 1)[0]
-    full_weight = lax.all_gather(proj_weight[0], "seq", axis=0, tiled=True)
-    partial_value = jnp.dot(bwd_flat, full_weight.T, preferred_element_type=jnp.float32)
-    mixer_bwd = lax.psum_scatter(
-        partial_value.astype(jnp.bfloat16), "head", scatter_dimension=1, tiled=True
-    )
+    size, mine = (lax.axis_size("seq"), lax.axis_index("seq"))
+    group = lax.axis_index("head")
+    own_rows = proj_weight[0]
+    slot_weight = jnp.concatenate(
+        [own_rows] + [rotated(own_rows, "seq", k) for k in range(1, size)], axis=0
+    )
+    slot_value = jnp.dot(bwd_flat, slot_weight.T, preferred_element_type=jnp.float32)
+    slot_value = slot_value.reshape(tokens, size, -1)[:, ::-1].reshape(tokens, -1)
+    partial_value = roll_blocks(slot_value, mine + 1, size, 1)
+    group_width = partial_value.shape[1] // 2
+    mine_part = lax.dynamic_slice_in_dim(partial_value, group * group_width, group_width, axis=1)
+    other_part = lax.dynamic_slice_in_dim(
+        partial_value, (1 - group) * group_width, group_width, axis=1
+    )
+    mixer_bwd = (
+        mine_part + swap_heads(other_part.astype(jnp.bfloat16)).astype(jnp.float32)
+    ).astype(jnp.bfloat16)
     cotangent = bwd_grad[0].reshape(tokens, heads_here, head_width)
 
     def summary_bwd(values_in, mixer_in, weight_in, bias_in, rate_in):
@@ -171,29 +211,43 @@
     mixer_grad = (out_grads[1].astype(jnp.float32) + sum_grads[1].astype(jnp.float32)).astype(
         jnp.bfloat16
     )
-    mixer_full = lax.all_gather(mixer_grad, "head", axis=1, tiled=True)
-    back_proj = jnp.dot(mixer_full, full_weight, preferred_element_type=jnp.float32)
+    other_grad = swap_heads(mixer_grad)
+    mixer_full = jnp.where(
+        group == 0,
+        jnp.concatenate([mixer_grad, other_grad], axis=1),
+        jnp.concatenate([other_grad, mixer_grad], axis=1),
+    )
+    mixer_slots = roll_blocks(mixer_full, size - 1 - mine, size, 1)
+    mixer_slots = mixer_slots.reshape(tokens, size, -1)[:, ::-1].reshape(tokens, -1)
+    back_proj = jnp.dot(mixer_slots, slot_weight, preferred_element_type=jnp.float32)
     value_grad = (out_grads[0].astype(jnp.float32) + sum_grads[0].astype(jnp.float32)).reshape(
         tokens, channels_here
     ) + back_proj
     value_grad = value_grad.astype(jnp.bfloat16)
     prev_part = shifted(value_grad.reshape(1, tokens, channels_here), "section", -1)
-    grad_rows = lax.psum_scatter(
-        lax.dot_general(
-            mixer_full, bwd_flat, (((0,), (0,)), ((), ())), preferred_element_type=jnp.float32
-        ).astype(jnp.bfloat16),
-        "seq",
-        scatter_dimension=0,
-        tiled=True,
-    ).astype(jnp.float32)
-    totals = lax.psum(
-        (
+    dest_grad = roll_blocks(mixer_full, size - mine, size, 1)
+    row_parts = lax.dot_general(
+        dest_grad, bwd_flat, (((0,), (0,)), ((), ())), preferred_element_type=jnp.float32
+    ).reshape(size, -1, channels_here)
+    grad_rows = row_parts[0]
+    for k in range(1, size):
+        grad_rows = grad_rows + rotated(row_parts[k].astype(jnp.bfloat16), "seq", k).astype(
+            jnp.float32
+        )
+    small = jnp.concatenate(
+        [
             (out_grads[2] + sum_grads[2]).reshape(channels_here),
             out_grads[3] + sum_grads[3],
             out_grads[4] + sum_grads[4],
             out_grads[5],
-        ),
-        "seq",
+        ]
+    )
+    small = seq_total(small)
+    totals = (
+        small[:channels_here],
+        small[channels_here : channels_here + heads_here],
+        small[channels_here + heads_here : channels_here + 2 * heads_here],
+        small[channels_here + 2 * heads_here :],
     )
     return (
         prev_part,

time: 212 us -> 171 us (0.81)
  the two profiles are of different devices: /device:TPU:4 before, /device:TPU:8 now
where the time goes in v2:
time: 171 us; the launch traced here: 170 us
  starting transfers between devices  58.2 us (34%)
  waiting for transfers between devices  37.7 us (22%)
  matrix products  24.3 us (14%)
  other arithmetic  23.6 us (14%)
  local copies, waits for them, and re-layouts  23.4 us (14%)
  between operations  2.82 us (2%)
    ppermute x12, starting transfers between devices, shifted(): return lax.ppermute(block, axis, route)  35.2 us
    ppermute x14, waiting for transfers between devices, rotated(): return lax.ppermute(block, axis, route)  22.9 us
    ppermute x14, starting transfers between devices, rotated(): return lax.ppermute(block, axis, route)  20 us
    ppermute x12, waiting for transfers between devices, shifted(): return lax.ppermute(block, axis, route)  13.2 us
    dot_general x5, matrix products, contract(): return jnp.einsum(spec, left, right, preferred_element_type=jnp.float32)  9.29 us
    unnamed x108, local copies, waits for them, and re-layouts  6.14 us
    convert_element_type x5, other arithmetic, scan_rounds(): far_state.astype(jnp.bfloat16)  4.73 us
    reduce_sum x2, other arithmetic, span_output(): values.astype(jnp.float32) * (1.0 + skip_gain)[None, :, None] + local_part  3.83 us
  transfers between devices with their start and end apart: 31, of which 13 were waited for; matrix products, arithmetic and copies ran while one was open for 23% of the time, Pallas kernels for 0%

profile of v2, /device:TPU:8, one launch (start us, length us, event | category | flops | bytes accessed | tf_op | source)
XLA Modules:
  0.0 170.0 jit_solution(197640638795322859)
XLA Ops:
  0.7 1.5 collective-permute-start.6
  2.1 3.6 %collective-permute-start.5 = (bf16[32,1792]{1,0:T(8,128)(2,1)}, bf16[32,1792]{1,0:T(8,128)(2,1)S(1)}, u32[]{:S(2)}, u32[]{:S(2)}) collective-permute-start(bf16[32,1792]{1,0:T(8,128)(2,1)} %bitcast.245), channel_id=1, source_target_pairs={{0,12},{2,14},{4,0},{6,2},{8,4},{10,6},{12,8},{14,10},{1,13},{3,15... | collective-permute-start | bytes 344072 | tf_op jit(solution)/shard_map/ppermute | solution.py:18
  7.0 3.8 %collective-permute-start.9 = (s32[1]{0:T(128)}, s32[1]{0:T(128)}, u32[]{:S(2)}, u32[]{:S(2)}) collective-permute-start(s32[1]{0:T(128)} %bitcast.21), channel_id=1, source_target_pairs={{0,2},{2,4},{4,6},{6,8},{8,10},{10,12},{12,14},{1,3},{3,5},{5,7},{... | collective-permute-start | bytes 20 | tf_op jit(solution)/shard_map/ppermute | solution.py:12
  16.4 1.6 collective-permute-start
  22.2 1.9 %collective-permute-start.1 = (bf16[32,1792]{1,0:T(8,128)(2,1)S(1)}, bf16[32,1792]{1,0:T(8,128)(2,1)S(1)}, u32[]{:S(2)}, u32[]{:S(2)}) collective-permute-start(bf16[32,1792]{1,0:T(8,128)(2,1)S(1)} %bitcast.249), channel_id=1, source_target_pairs={{0,4},{2,6},{4,8},{6,10},{8,12},{10,14},{12,0},{14,2},{1,5},{3,7},... | collective-permute-start | bytes 344072 | tf_op jit(solution)/shard_map/ppermute | solution.py:18
  24.1 6.1 %collective-permute-done.1 = bf16[32,1792]{1,0:T(8,128)(2,1)S(1)} collective-permute-done((bf16[32,1792]{1,0:T(8,128)(2,1)S(1)}, bf16[32,1792]{1,0:T(8,128)(2,1)S(1)}, u32[]{:S(2)}, u32[]{:S(2)}) %collective-permute-start.1) | collective-permute-done | bytes 114720 | tf_op jit(solution)/shard_map/ppermute | solution.py:18
  30.2 6.6 %collective-permute-done.2 = bf16[32,1792]{1,0:T(8,128)(2,1)S(1)} collective-permute-done((bf16[32,1792]{1,0:T(8,128)(2,1)S(1)}, bf16[32,1792]{1,0:T(8,128)(2,1)S(1)}, u32[]{:S(2)}, u32[]{:S(2)}) %collective-permute-start.2) | collective-permute-done | bytes 114720 | tf_op jit(solution)/shard_map/ppermute | solution.py:18
  38.8 1.3 fusion.35
  40.2 1.5 reshape.241
  42.4 4.3 %collective-permute-start.8 = (bf16[28,4096]{1,0:T(8,128)(2,1)}, bf16[28,4096]{1,0:T(8,128)(2,1)}, u32[]{:S(2)}, u32[]{:S(2)}) collective-permute-start(bf16[28,4096]{1,0:T(8,128)(2,1)} %convert_element_type.221), channel_id=1, source_target_pairs={{0,2},{2,4},{4,6},{6,8},{8,10},{10,12},{12,14},{1,3},{3,5},{5,7},{... | collective-permute-start | bytes 688136 | tf_op jit(solution)/shard_map/ppermute | solution.py:12
  46.7 1.6 convolution_bitcast_fusion
  48.3 2.4 %copy.71 = f32[28,64,64]{2,1,0:T(8,128)} copy(f32[28,64,64]{1,2,0:T(8,128)} %convolution_bitcast_fusion) | data formatting | bytes 917504 | tf_op jit(solution)/shard_map/transpose(jvp(tn,hnp->thp))/transpose | solution.py:103
  50.7 1.5 reshape.243
  52.3 2.4 %collective-permute-start.14 = (bf16[28,4096]{1,0:T(8,128)(2,1)S(1)}, bf16[28,4096]{1,0:T(8,128)(2,1)S(1)}, u32[]{:S(2)}, u32[]{:S(2)}) collective-permute-start(bf16[28,4096]{1,0:T(8,128)(2,1)S(1)} %convert_element_type.232), channel_id=1, source_target_pairs={{2,0},{4,2},{6,4},{8,6},{10,8},{12,10},{14,12},{3,1},{5,3},{7,5},{... | collective-permute-start | bytes 688136 | tf_op jit(solution)/shard_map/ppermute | solution.py:12
  55.8 2.9 %collective-permute-start.11 = (bf16[28,4096]{1,0:T(8,128)(2,1)S(1)}, bf16[28,4096]{1,0:T(8,128)(2,1)S(1)}, u32[]{:S(2)}, u32[]{:S(2)}) collective-permute-start(bf16[28,4096]{1,0:T(8,128)(2,1)S(1)} %fusion.56), channel_id=1, source_target_pairs={{0,4},{2,6},{4,8},{6,10},{8,12},{10,14},{1,5},{3,7},{5,9},{7,11},{... | collective-permute-start | bytes 688136 | tf_op jit(solution)/shard_map/ppermute | solution.py:12
  58.7 3.9 %collective-permute-start.15 = (f32[28]{0:T(128)S(1)}, f32[28]{0:T(128)S(1)}, u32[]{:S(2)}, u32[]{:S(2)}) collective-permute-start(f32[28]{0:T(128)S(1)} %copy-done.31), channel_id=1, source_target_pairs={{2,0},{4,2},{6,4},{8,6},{10,8},{12,10},{14,12},{3,1},{5,3},{7,5},{... | collective-permute-start | bytes 344 | tf_op jit(solution)/shard_map/ppermute | solution.py:12
  62.6 1.9 %collective-permute-start.10 = (f32[28]{0:T(128)S(1)}, f32[28]{0:T(128)S(1)}, u32[]{:S(2)}, u32[]{:S(2)}) collective-permute-start(f32[28]{0:T(128)S(1)} %copy-done.31), channel_id=1, source_target_pairs={{0,2},{2,4},{4,6},{6,8},{8,10},{10,12},{12,14},{1,3},{3,5},{5,7},{... | collective-permute-start | bytes 344 | tf_op jit(solution)/shard_map/ppermute | solution.py:12
  64.6 4.4 %collective-permute-done.10 = f32[28]{0:T(128)S(1)} collective-permute-done((f32[28]{0:T(128)S(1)}, f32[28]{0:T(128)S(1)}, u32[]{:S(2)}, u32[]{:S(2)}) %collective-permute-start.10) | collective-permute-done | bytes 144 | tf_op jit(solution)/shard_map/ppermute | solution.py:12
  69.6 2.0 %fusion.39 = (bf16[28,4096]{1,0:T(8,128)(2,1)}, bf16[28,4096]{1,0:T(8,128)(2,1)S(1)}) fusion(bf16[28,4096]{1,0:T(8,128)(2,1)S(1)} %collective-permute-done.11, f32[28,4096]{1,0:T(8,128)S(1)} %reshape.241, bf16[28,4096]{1,0:T(8,128)(2,1)} %collective-permute-done.8, f32[28]{0:T(128)S(1)} %get-tuple-element.48, f32[28]{0:T(128)S(1)} %copy-done.31, ...), kind=kLoop, calls=%fused_computation.70 | loop fusion | flops 1261568 | bytes 2064608 | tf_op jit(solution)/shard_map/convert_element_type | solution.py:120
  71.6 1.9 %collective-permute-start.16 = (bf16[28,4096]{1,0:T(8,128)(2,1)S(1)}, bf16[28,4096]{1,0:T(8,128)(2,1)S(1)}, u32[]{:S(2)}, u32[]{:S(2)}) collective-permute-start(bf16[28,4096]{1,0:T(8,128)(2,1)S(1)} %get-tuple-element.47), channel_id=1, source_target_pairs={{4,0},{6,2},{8,4},{10,6},{12,8},{14,10},{5,1},{7,3},{9,5},{11,7},{... | collective-permute-start | bytes 688136 | tf_op jit(solution)/shard_map/ppermute | solution.py:12
  74.2 4.4 %collective-permute-start.13 = (bf16[28,4096]{1,0:T(8,128)(2,1)}, bf16[28,4096]{1,0:T(8,128)(2,1)S(1)}, u32[]{:S(2)}, u32[]{:S(2)}) collective-permute-start(bf16[28,4096]{1,0:T(8,128)(2,1)} %get-tuple-element.46), channel_id=1, source_target_pairs={{0,8},{2,10},{4,12},{6,14},{1,9},{3,11},{5,13},{7,15},{16,24},{18,... | collective-permute-start | bytes 688136 | tf_op jit(solution)/shard_map/ppermute | solution.py:12
  82.7 1.4 reshape_squeeze.10
  84.0 2.5 %fusion.25 = (f32[1792]{0:T(1024)}, f32[1,128,1792]{1,2,0:T(8,128)}) fusion(bf16[1,128,1792]{1,2,0:T(8,128)(2,1)S(1)} %copy.61, bf16[1,128,1792]{1,2,0:T(8,128)(2,1)S(1)} %copy.62, f32[128,28]{0,1:T(8,128)} %get-tuple-element.53), kind=kLoop, calls=%fused_computation.43 | loop fusion | flops 1145088 | bytes 1856512 | tf_op jit(solution)/shard_map/transpose(jvp())/reduce_sum | solution.py:105
  86.5 1.4 reduce_sum.160
  87.9 4.9 %collective-permute-start.12 = (f32[28]{0:T(128)}, f32[28]{0:T(128)}, u32[]{:S(2)}, u32[]{:S(2)}) collective-permute-start(f32[28]{0:T(128)} %copy-done.41), channel_id=1, source_target_pairs={{0,4},{2,6},{4,8},{6,10},{8,12},{10,14},{1,5},{3,7},{5,9},{7,11},{... | collective-permute-start | bytes 344 | tf_op jit(solution)/shard_map/ppermute | solution.py:12
  92.8 1.3 reduce_sum.161
  94.2 2.1 %collective-permute-start.17 = (f32[28]{0:T(128)}, f32[28]{0:T(128)S(1)}, u32[]{:S(2)}, u32[]{:S(2)}) collective-permute-start(f32[28]{0:T(128)} %copy-done.40), channel_id=1, source_target_pairs={{4,0},{6,2},{8,4},{10,6},{12,8},{14,10},{5,1},{7,3},{9,5},{11,7},{... | collective-permute-start | bytes 344 | tf_op jit(solution)/shard_map/ppermute | solution.py:12
  97.0 2.8 %collective-permute-done.17 = f32[28]{0:T(128)S(1)} collective-permute-done((f32[28]{0:T(128)}, f32[28]{0:T(128)S(1)}, u32[]{:S(2)}, u32[]{:S(2)}) %collective-permute-start.17) | collective-permute-done | bytes 144 | tf_op jit(solution)/shard_map/ppermute | solution.py:12
  101.9 2.9 %multiply_reduce_fusion.2 = (f32[28]{0:T(128)}, bf16[28,4096]{1,0:T(8,128)(2,1)S(1)}, f32[28,4096]{1,0:T(8,128)}) fusion(bf16[28,4096]{1,0:T(8,128)(2,1)} %collective-permute-done.18, f32[28]{0:T(128)S(1)} %mul.383, bf16[28,4096]{1,0:T(8,128)(2,1)S(1)} %collective-permute-done.16, f32[28]{0:T(128)} %copy-done.38, bf16[28,4096]{1,0:T(8,128)(2,1)S(1)} %copy-done.2, ...), kind=kLoop, calls=%fused_computation.75 | loop fusion | flops 1949668 | bytes 2064944 | tf_op jit(solution)/shard_map/reduce_sum | solution.py:209
  106.3 2.0 %fusion.116 = (f32[28]{0:T(128)}, f32[128,28]{1,0:T(8,128)}, f32[28,128]{0,1:T(8,128)S(1)}) fusion(f32[128,28]{1,0:T(8,128)S(1)} %copy.65, f32[28]{0:T(128)} %copy-done.34, f32[128]{0:T(128)} %copy-done.27, f32[128,28]{1,0:T(8,128)S(1)} %copy.73, f32[28]{0:T(128)} %bitcast.255, f32[28,1,128]{0,2,1:T(8,128)S(1)} %copy.83, pred[128]{0:T(512)(128)(4,1)} %copy-done.25), kind=kLoop, calls=%fused_computation.194 | loop fusion | flops 50148 | bytes 72656 | tf_op jit(solution)/shard_map/transpose(jvp())/reduce_sum | solution.py:67
  108.4 2.5 %fusion.12 = (f32[28,128]{1,0:T(8,128)}, f32[28,128]{1,0:T(8,128)}, f32[28,128]{1,0:T(8,128)S(1)}, bf16[128,128]{1,0:T(8,128)(2,1)S(1)}) fusion(f32[28,128]{1,0:T(8,128)S(1)} %copy.63, f32[128,128]{1,0:T(8,128)S(1)} %copy-done.16, f32[128,128]{1,0:T(8,128)S(1)} %copy-done.18, f32[28,128]{1,0:T(8,128)S(1)} %bitcast.253, pred[128,128]{1,0:T(8,128)(4,1)S(1)} %copy-done.24, ...), kind=kOutput, calls=%fused_computation.18 | convolution fusion | flops 66491904 | bytes 1169408 | tf_op jit(solution)/shard_map/transpose(jvp(hts,shp->thp))/dot_general | solution.py:44
  113.1 1.4 reshape.242
  115.9 1.8 %fusion.102 = f32[128,1792]{0,1:S(1)} fusion(f32[64,1792]{0,1:T(8,128)} %bitcast.233, bf16[128,128]{0,1:T(8,128)(2,1)S(1)} %fusion.73), kind=kOutput, calls=%fused_computation.170 | convolution fusion | flops 176160768 | bytes 1392640
  118.2 1.4 multiply_reduce_fusion.4
  124.8 2.2 %fusion.24 = bf16[128,64]{0,1:T(8,128)(2,1)S(1)} fusion(bf16[128,64]{0,1:T(8,128)(2,1)S(1)} %copy-done.14, f32[128,28,64]{0,2,1:T(8,128)} %bitcast.231, f32[28,64,64]{2,1,0:T(8,128)S(1)} %reshape.242), kind=kOutput, calls=%fused_computation.42 | convolution fusion | flops 176177152 | bytes 1409024 | tf_op jit(solution)/shard_map/transpose(jvp(tn,hnp->thp))/dot_general | solution.py:103
  128.2 2.9 %fusion.22 = f32[128,28,64]{0,2,1:T(8,128)} fusion(bf16[28,64,128]{2,1,0:T(8,128)(2,1)S(1)} %bitcast.223, f32[28,128]{1,0:T(8,128)} %copy-done.23, f32[128,128]{1,0:T(8,128)S(1)} %copy-done.17, f32[128,128]{1,0:T(8,128)} %get-tuple-element.52, f32[28,128]{1,0:T(8,128)} %bitcast.252, pred[128,128]{1,0:T(8,128)(4,1)} %get-tuple-element.51, ...), kind=kOutput, calls=%fused_computation.35 | convolution fusion | flops 63537152 | bytes 2032752 | tf_op jit(solution)/shard_map/transpose(jvp(hts,shp->thp))/dot_general | solution.py:44
  131.8 2.5 %collective-permute-start.30 = (f32[1876]{0:T(1024)S(1)}, f32[1876]{0:T(1024)S(1)}, u32[]{:S(2)}, u32[]{:S(2)}) collective-permute-start(f32[1876]{0:T(1024)S(1)} %add.192), channel_id=1, source_target_pairs={{0,8},{2,10},{4,12},{6,14},{8,0},{10,2},{12,4},{14,6},{1,9},{3,11}... | collective-permute-start | bytes 22520 | tf_op jit(solution)/shard_map/ppermute | solution.py:38
  134.3 1.7 fusion.18
  136.4 1.8 %fusion.119 = (bf16[256,1792]{1,0:T(8,128)(2,1)S(1)}, f32[256,1792]{1,0:T(8,128)}) fusion(bf16[1,128,1792]{2,1,0:T(8,128)(2,1)S(1)} %copy-done, s32[]{:T(128)S(6)} %select_n.90, bf16[128,256]{0,1:T(8,128)(2,1)S(1)} %maximum_select_fusion), kind=kOutput, calls=%fused_computation.197 | convolution fusion | flops 118030336 | bytes 3276804 | tf_op jit(solution)/shard_map/dot_general | solution.py:229
  138.3 1.5 collective-permute-start.21
  139.8 1.4 collective-permute-start.27
  142.7 3.2 %collective-permute-start.26 = (bf16[32,1792]{1,0:T(8,128)(2,1)S(1)}, bf16[32,1792]{1,0:T(8,128)(2,1)S(1)}, u32[]{:S(2)}, u32[]{:S(2)}) collective-permute-start(bf16[32,1792]{1,0:T(8,128)(2,1)S(1)} %get-tuple-element.31), channel_id=1, source_target_pairs={{0,12},{2,14},{4,0},{6,2},{8,4},{10,6},{12,8},{14,10},{1,13},{3,15... | collective-permute-start | bytes 344072 | tf_op jit(solution)/shard_map/ppermute | solution.py:18
  147.1 2.7 %collective-permute-start.23 = (bf16[32,1792]{1,0:T(8,128)(2,1)S(1)}, bf16[32,1792]{1,0:T(8,128)(2,1)S(1)}, u32[]{:S(2)}, u32[]{:S(2)}) collective-permute-start(bf16[32,1792]{1,0:T(8,128)(2,1)S(1)} %get-tuple-element.34), channel_id=1, source_target_pairs={{0,6},{2,8},{4,10},{6,12},{8,14},{10,0},{12,2},{14,4},{1,7},{3,9},... | collective-permute-start | bytes 344072 | tf_op jit(solution)/shard_map/ppermute | solution.py:18
  149.8 1.4 collective-permute-start.22
  151.5 7.4 %collective-permute-done.26 = bf16[32,1792]{1,0:T(8,128)(2,1)S(1)} collective-permute-done((bf16[32,1792]{1,0:T(8,128)(2,1)S(1)}, bf16[32,1792]{1,0:T(8,128)(2,1)S(1)}, u32[]{:S(2)}, u32[]{:S(2)}) %collective-permute-start.26) | collective-permute-done | bytes 114720 | tf_op jit(solution)/shard_map/ppermute | solution.py:18
  160.4 2.4 %collective-permute-done.22 = bf16[32,1792]{1,0:T(8,128)(2,1)S(1)} collective-permute-done((bf16[32,1792]{1,0:T(8,128)(2,1)S(1)}, bf16[32,1792]{1,0:T(8,128)(2,1)S(1)}, u32[]{:S(2)}, u32[]{:S(2)}) %collective-permute-start.22) | collective-permute-done | bytes 114720 | tf_op jit(solution)/shard_map/ppermute | solution.py:18
  162.7 1.7 %fusion.63 = f32[1,32,1792]{2,1,0:T(8,128)} fusion(f32[256,1792]{1,0:T(8,128)} %get-tuple-element.56, bf16[32,1792]{1,0:T(8,128)(2,1)S(1)} %collective-permute-done.27, bf16[32,1792]{1,0:T(8,128)(2,1)S(1)} %collective-permute-done.26, bf16[32,1792]{1,0:T(8,128)(2,1)S(1)} %collective-permute-done.25, bf16[32,1792]{1,0:T(8,128)(2,1)S(1)} %collective-permute-done.24, ...), kind=kLoop, calls=%fused_computation.100 | loop fusion | flops 802816 | bytes 1261568 | tf_op jit(solution)/shard_map/broadcast_in_dim | solution.py:254
  164.5 4.8 %collective-permute-done.20 = bf16[1,128,1792]{2,1,0:T(8,128)(2,1)S(1)} collective-permute-done((bf16[1,128,1792]{2,1,0:T(8,128)(2,1)S(1)}, bf16[1,128,1792]{2,1,0:T(8,128)(2,1)S(1)}, u32[]{:S(2)}, u32[]{:S(2)}) %collective-permute-start.20) | collective-permute-done | bytes 458784 | tf_op jit(solution)/shard_map/ppermute | solution.py:12
  (206 shorter events, 39.7 us)
Async XLA Ops:
  0.6 15.8 %copy-start.10 = (bf16[1,32,1792]{2,1,0:T(8,128)(2,1)S(1)}, bf16[1,32,1792]{2,1,0:T(8,128)(2,1)}, u32[]{:S(2)}) copy-start(bf16[1,32,1792]{2,1,0:T(8,128)(2,1)} %param.12) | copy-start | bytes 344068
  0.6 18.6 %copy-start.29 = (s32[1,128]{1,0:T(1,128)S(1)}, s32[1,128]{1,0:T(1,128)}, u32[]{:S(2)}) copy-start(s32[1,128]{1,0:T(1,128)} %param.10) | copy-start | bytes 1540
  0.7 19.8 %copy-start.32 = (f32[1,28]{1,0:T(1,128)S(1)}, f32[1,28]{1,0:T(1,128)}, u32[]{:S(2)}) copy-start(f32[1,28]{1,0:T(1,128)} %param.14) | copy-start | bytes 340
  0.7 36.2 %collective-permute-start.6 = (bf16[32,1792]{1,0:T(8,128)(2,1)}, bf16[32,1792]{1,0:T(8,128)(2,1)S(1)}, u32[]{:S(2)}, u32[]{:S(2)}) collective-permute-start(bf16[32,1792]{1,0:T(8,128)(2,1)} %bitcast.244), channel_id=1, source_target_pairs={{0,14},{2,0},{4,2},{6,4},{8,6},{10,8},{12,10},{14,12},{1,15},{3,1}... | collective-permute-start | bytes 344072 | tf_op jit(solution)/shard_map/ppermute | solution.py:18
  2.1 34.8 %collective-permute-start.5 = (bf16[32,1792]{1,0:T(8,128)(2,1)}, bf16[32,1792]{1,0:T(8,128)(2,1)S(1)}, u32[]{:S(2)}, u32[]{:S(2)}) collective-permute-start(bf16[32,1792]{1,0:T(8,128)(2,1)} %bitcast.245), channel_id=1, source_target_pairs={{0,12},{2,14},{4,0},{6,2},{8,4},{10,6},{12,8},{14,10},{1,13},{3,15... | collective-permute-start | bytes 344072 | tf_op jit(solution)/shard_map/ppermute | solution.py:18
  5.7 31.1 %collective-permute-start.4 = (bf16[32,1792]{1,0:T(8,128)(2,1)}, bf16[32,1792]{1,0:T(8,128)(2,1)S(1)}, u32[]{:S(2)}, u32[]{:S(2)}) collective-permute-start(bf16[32,1792]{1,0:T(8,128)(2,1)} %bitcast.246), channel_id=1, source_target_pairs={{0,10},{2,12},{4,14},{6,0},{8,2},{10,4},{12,6},{14,8},{1,11},{3,13... | collective-permute-start | bytes 344072 | tf_op jit(solution)/shard_map/ppermute | solution.py:18
  5.7 31.1 %collective-permute-start.3 = (bf16[32,1792]{1,0:T(8,128)(2,1)}, bf16[32,1792]{1,0:T(8,128)(2,1)S(1)}, u32[]{:S(2)}, u32[]{:S(2)}) collective-permute-start(bf16[32,1792]{1,0:T(8,128)(2,1)} %bitcast.247), channel_id=1, source_target_pairs={{0,8},{2,10},{4,12},{6,14},{8,0},{10,2},{12,4},{14,6},{1,9},{3,11}... | collective-permute-start | bytes 344072 | tf_op jit(solution)/shard_map/ppermute | solution.py:18
  7.0 9.4 %collective-permute-start.9 = (s32[1]{0:T(128)}, s32[1]{0:T(128)}, u32[]{:S(2)}, u32[]{:S(2)}) collective-permute-start(s32[1]{0:T(128)} %bitcast.21), channel_id=1, source_target_pairs={{0,2},{2,4},{4,6},{6,8},{8,10},{10,12},{12,14},{1,3},{3,5},{5,7},{... | collective-permute-start | bytes 20 | tf_op jit(solution)/shard_map/ppermute | solution.py:12
  12.4 9.1 %copy-start.45 = (f32[28]{0:T(128)}, f32[28]{0:T(128)S(1)}, u32[]{:S(2)}) copy-start(f32[28]{0:T(128)S(1)} %negate_bitcast_fusion) | copy-start | bytes 340
  13.1 23.7 %copy-start.11 = (f32[1792]{0:T(1024)}, f32[1792]{0:T(1024)S(1)}, u32[]{:S(2)}) copy-start(f32[1792]{0:T(1024)S(1)} %reduce.2) | copy-start | bytes 21508
  14.5 22.5 %copy-start = (bf16[1,128,1792]{2,1,0:T(8,128)(2,1)S(1)}, bf16[1,128,1792]{2,1,0:T(8,128)(2,1)}, u32[]{:S(2)}) copy-start(bf16[1,128,1792]{2,1,0:T(8,128)(2,1)} %param.9) | copy-start | bytes 1376260
  16.4 5.7 %collective-permute-start = (bf16[32,1792]{1,0:T(8,128)(2,1)S(1)}, bf16[32,1792]{1,0:T(8,128)(2,1)S(1)}, u32[]{:S(2)}, u32[]{:S(2)}) collective-permute-start(bf16[32,1792]{1,0:T(8,128)(2,1)S(1)} %bitcast.248), channel_id=1, source_target_pairs={{0,2},{2,4},{4,6},{6,8},{8,10},{10,12},{12,14},{14,0},{1,3},{3,5},... | collective-permute-start | bytes 344072 | tf_op jit(solution)/shard_map/ppermute | solution.py:18
  20.4 16.5 %copy-start.25 = (pred[128]{0:T(512)(128)(4,1)}, pred[128]{0:T(512)(128)(4,1)S(1)}, u32[]{:S(2)}) copy-start(pred[128]{0:T(512)(128)(4,1)S(1)} %get-tuple-element.27) | copy-start | bytes 388
  20.4 16.5 %copy-start.27 = (f32[128]{0:T(128)}, f32[128]{0:T(128)S(1)}, u32[]{:S(2)}) copy-start(f32[128]{0:T(128)S(1)} %get-tuple-element.28) | copy-start | bytes 1540
  21.3 15.6 %copy-start.20 = (f32[128,28]{0,1:T(8,128)}, f32[128,28]{0,1:T(8,128)S(1)}, u32[]{:S(2)}) copy-start(f32[128,28]{0,1:T(8,128)S(1)} %get-tuple-element.54) | copy-start | bytes 43012
  22.2 8.1 %collective-permute-start.1 = (bf16[32,1792]{1,0:T(8,128)(2,1)S(1)}, bf16[32,1792]{1,0:T(8,128)(2,1)S(1)}, u32[]{:S(2)}, u32[]{:S(2)}) collective-permute-start(bf16[32,1792]{1,0:T(8,128)(2,1)S(1)} %bitcast.249), channel_id=1, source_target_pairs={{0,4},{2,6},{4,8},{6,10},{8,12},{10,14},{12,0},{14,2},{1,5},{3,7},... | collective-permute-start | bytes 344072 | tf_op jit(solution)/shard_map/ppermute | solution.py:18
  30.2 6.6 %collective-permute-start.2 = (bf16[32,1792]{1,0:T(8,128)(2,1)S(1)}, bf16[32,1792]{1,0:T(8,128)(2,1)S(1)}, u32[]{:S(2)}, u32[]{:S(2)}) collective-permute-start(bf16[32,1792]{1,0:T(8,128)(2,1)S(1)} %bitcast.250), channel_id=1, source_target_pairs={{0,6},{2,8},{4,10},{6,12},{8,14},{10,0},{12,2},{14,4},{1,7},{3,9},... | collective-permute-start | bytes 344072 | tf_op jit(solution)/shard_map/ppermute | solution.py:18
  37.5 1.3 collective-permute-start.7
  42.4 12.3 %collective-permute-start.8 = (bf16[28,4096]{1,0:T(8,128)(2,1)}, bf16[28,4096]{1,0:T(8,128)(2,1)}, u32[]{:S(2)}, u32[]{:S(2)}) collective-permute-start(bf16[28,4096]{1,0:T(8,128)(2,1)} %convert_element_type.221), channel_id=1, source_target_pairs={{0,2},{2,4},{4,6},{6,8},{8,10},{10,12},{12,14},{1,3},{3,5},{5,7},{... | collective-permute-start | bytes 688136 | tf_op jit(solution)/shard_map/ppermute | solution.py:12
  52.3 21.2 %copy-start.30 = (s32[1,128]{1,0:T(1,128)S(1)}, s32[1,128]{1,0:T(1,128)}, u32[]{:S(2)}) copy-start(s32[1,128]{1,0:T(1,128)} %param.10) | copy-start | bytes 1540
  52.3 16.7 %collective-permute-start.14 = (bf16[28,4096]{1,0:T(8,128)(2,1)S(1)}, bf16[28,4096]{1,0:T(8,128)(2,1)S(1)}, u32[]{:S(2)}, u32[]{:S(2)}) collective-permute-start(bf16[28,4096]{1,0:T(8,128)(2,1)S(1)} %convert_element_type.232), channel_id=1, source_target_pairs={{2,0},{4,2},{6,4},{8,6},{10,8},{12,10},{14,12},{3,1},{5,3},{7,5},{... | collective-permute-start | bytes 688136 | tf_op jit(solution)/shard_map/ppermute | solution.py:12
  55.8 13.2 %collective-permute-start.11 = (bf16[28,4096]{1,0:T(8,128)(2,1)S(1)}, bf16[28,4096]{1,0:T(8,128)(2,1)S(1)}, u32[]{:S(2)}, u32[]{:S(2)}) collective-permute-start(bf16[28,4096]{1,0:T(8,128)(2,1)S(1)} %fusion.56), channel_id=1, source_target_pairs={{0,4},{2,6},{4,8},{6,10},{8,12},{10,14},{1,5},{3,7},{5,9},{7,11},{... | collective-permute-start | bytes 688136 | tf_op jit(solution)/shard_map/ppermute | solution.py:12
  58.7 5.9 %collective-permute-start.15 = (f32[28]{0:T(128)S(1)}, f32[28]{0:T(128)S(1)}, u32[]{:S(2)}, u32[]{:S(2)}) collective-permute-start(f32[28]{0:T(128)S(1)} %copy-done.31), channel_id=1, source_target_pairs={{2,0},{4,2},{6,4},{8,6},{10,8},{12,10},{14,12},{3,1},{5,3},{7,5},{... | collective-permute-start | bytes 344 | tf_op jit(solution)/shard_map/ppermute | solution.py:12
  62.6 6.3 %collective-permute-start.10 = (f32[28]{0:T(128)S(1)}, f32[28]{0:T(128)S(1)}, u32[]{:S(2)}, u32[]{:S(2)}) collective-permute-start(f32[28]{0:T(128)S(1)} %copy-done.31), channel_id=1, source_target_pairs={{0,2},{2,4},{4,6},{6,8},{8,10},{10,12},{12,14},{1,3},{3,5},{5,7},{... | collective-permute-start | bytes 344 | tf_op jit(solution)/shard_map/ppermute | solution.py:12
  69.0 11.8 %copy-start.40 = (f32[28]{0:T(128)}, f32[28]{0:T(128)S(1)}, u32[]{:S(2)}) copy-start(f32[28]{0:T(128)S(1)} %get-tuple-element.49) | copy-start | bytes 340
  69.0 11.8 %copy-start.41 = (f32[28]{0:T(128)}, f32[28]{0:T(128)S(1)}, u32[]{:S(2)}) copy-start(f32[28]{0:T(128)S(1)} %get-tuple-element.48) | copy-start | bytes 340
  69.0 11.8 %copy-start.1 = (bf16[28,4096]{1,0:T(8,128)(2,1)}, bf16[28,4096]{1,0:T(8,128)(2,1)S(1)}, u32[]{:S(2)}) copy-start(bf16[28,4096]{1,0:T(8,128)(2,1)S(1)} %collective-permute-done.14) | copy-start | bytes 688132
  69.6 11.2 %copy-start.5 = (bf16[28,4096]{1,0:T(8,128)(2,1)}, bf16[28,4096]{1,0:T(8,128)(2,1)S(1)}, u32[]{:S(2)}) copy-start(bf16[28,4096]{1,0:T(8,128)(2,1)S(1)} %collective-permute-done.11) | copy-start | bytes 688132
  69.6 12.5 %copy-start.44 = (f32[1,28]{1,0:T(1,128)S(1)}, f32[1,28]{1,0:T(1,128)}, u32[]{:S(2)}) copy-start(f32[1,28]{1,0:T(1,128)} %param.16) | copy-start | bytes 340
  71.6 8.3 %collective-permute-start.16 = (bf16[28,4096]{1,0:T(8,128)(2,1)S(1)}, bf16[28,4096]{1,0:T(8,128)(2,1)S(1)}, u32[]{:S(2)}, u32[]{:S(2)}) collective-permute-start(bf16[28,4096]{1,0:T(8,128)(2,1)S(1)} %get-tuple-element.47), channel_id=1, source_target_pairs={{4,0},{6,2},{8,4},{10,6},{12,8},{14,10},{5,1},{7,3},{9,5},{11,7},{... | collective-permute-start | bytes 688136 | tf_op jit(solution)/shard_map/ppermute | solution.py:12
  74.2 27.0 %collective-permute-start.13 = (bf16[28,4096]{1,0:T(8,128)(2,1)}, bf16[28,4096]{1,0:T(8,128)(2,1)S(1)}, u32[]{:S(2)}, u32[]{:S(2)}) collective-permute-start(bf16[28,4096]{1,0:T(8,128)(2,1)} %get-tuple-element.46), channel_id=1, source_target_pairs={{0,8},{2,10},{4,12},{6,14},{1,9},{3,11},{5,13},{7,15},{16,24},{18,... | collective-permute-start | bytes 688136 | tf_op jit(solution)/shard_map/ppermute | solution.py:12
  80.8 21.1 %collective-permute-start.18 = (bf16[28,4096]{1,0:T(8,128)(2,1)}, bf16[28,4096]{1,0:T(8,128)(2,1)}, u32[]{:S(2)}, u32[]{:S(2)}) collective-permute-start(bf16[28,4096]{1,0:T(8,128)(2,1)} %fusion.43), channel_id=1, source_target_pairs={{8,0},{10,2},{12,4},{14,6},{9,1},{11,3},{13,5},{15,7},{24,16},{26,... | collective-permute-start | bytes 688136 | tf_op jit(solution)/shard_map/ppermute | solution.py:12
  82.1 19.8 %copy-start.2 = (bf16[28,4096]{1,0:T(8,128)(2,1)S(1)}, bf16[28,4096]{1,0:T(8,128)(2,1)}, u32[]{:S(2)}) copy-start(bf16[28,4096]{1,0:T(8,128)(2,1)} %copy-done.1) | copy-start | bytes 688132
  82.1 19.8 %copy-start.6 = (bf16[28,4096]{1,0:T(8,128)(2,1)S(1)}, bf16[28,4096]{1,0:T(8,128)(2,1)}, u32[]{:S(2)}) copy-start(bf16[28,4096]{1,0:T(8,128)(2,1)} %copy-done.5) | copy-start | bytes 688132
  87.9 8.4 %collective-permute-start.12 = (f32[28]{0:T(128)}, f32[28]{0:T(128)}, u32[]{:S(2)}, u32[]{:S(2)}) collective-permute-start(f32[28]{0:T(128)} %copy-done.41), channel_id=1, source_target_pairs={{0,4},{2,6},{4,8},{6,10},{8,12},{10,14},{1,5},{3,7},{5,9},{7,11},{... | collective-permute-start | bytes 344 | tf_op jit(solution)/shard_map/ppermute | solution.py:12
  94.2 5.6 %collective-permute-start.17 = (f32[28]{0:T(128)}, f32[28]{0:T(128)S(1)}, u32[]{:S(2)}, u32[]{:S(2)}) collective-permute-start(f32[28]{0:T(128)} %copy-done.40), channel_id=1, source_target_pairs={{4,0},{6,2},{8,4},{10,6},{12,8},{14,10},{5,1},{7,3},{9,5},{11,7},{... | collective-permute-start | bytes 344 | tf_op jit(solution)/shard_map/ppermute | solution.py:12
  124.5 3.7 %collective-permute-start.28 = (f32[1876]{0:T(1024)S(1)}, f32[1876]{0:T(1024)S(1)}, u32[]{:S(2)}, u32[]{:S(2)}) collective-permute-start(f32[1876]{0:T(1024)S(1)} %concatenate.24), channel_id=1, source_target_pairs={{0,2},{2,0},{4,6},{6,4},{8,10},{10,8},{12,14},{14,12},{1,3},{3,1},... | collective-permute-start | bytes 22520 | tf_op jit(solution)/shard_map/ppermute | solution.py:38
  127.8 8.5 %collective-permute-start.19 = (bf16[128,128]{0,1:T(8,128)(2,1)S(1)}, bf16[128,128]{0,1:T(8,128)(2,1)S(1)}, u32[]{:S(2)}, u32[]{:S(2)}) collective-permute-start(bf16[128,128]{0,1:T(8,128)(2,1)S(1)} %add_convert_fusion), channel_id=1, source_target_pairs={{0,1},{1,0},{2,3},{3,2},{4,5},{5,4},{6,7},{7,6},{8,9},{9,8},{10,11... | collective-permute-start | bytes 98312 | tf_op jit(solution)/shard_map/ppermute | solution.py:29
  128.2 3.7 %collective-permute-start.29 = (f32[1876]{0:T(1024)S(1)}, f32[1876]{0:T(1024)S(1)}, u32[]{:S(2)}, u32[]{:S(2)}) collective-permute-start(f32[1876]{0:T(1024)S(1)} %add.191), channel_id=1, source_target_pairs={{0,4},{2,6},{4,0},{6,2},{8,12},{10,14},{12,8},{14,10},{1,5},{3,7},... | collective-permute-start | bytes 22520 | tf_op jit(solution)/shard_map/ppermute | solution.py:38
  131.8 4.5 %collective-permute-start.30 = (f32[1876]{0:T(1024)S(1)}, f32[1876]{0:T(1024)S(1)}, u32[]{:S(2)}, u32[]{:S(2)}) collective-permute-start(f32[1876]{0:T(1024)S(1)} %add.192), channel_id=1, source_target_pairs={{0,8},{2,10},{4,12},{6,14},{8,0},{10,2},{12,4},{14,6},{1,9},{3,11}... | collective-permute-start | bytes 22520 | tf_op jit(solution)/shard_map/ppermute | solution.py:38
  138.3 8.8 %collective-permute-start.21 = (bf16[32,1792]{1,0:T(8,128)(2,1)S(1)}, bf16[32,1792]{1,0:T(8,128)(2,1)S(1)}, u32[]{:S(2)}, u32[]{:S(2)}) collective-permute-start(bf16[32,1792]{1,0:T(8,128)(2,1)S(1)} %get-tuple-element.29), channel_id=1, source_target_pairs={{0,2},{2,4},{4,6},{6,8},{8,10},{10,12},{12,14},{14,0},{1,3},{3,5},... | collective-permute-start | bytes 344072 | tf_op jit(solution)/shard_map/ppermute | solution.py:18
  139.8 9.9 %collective-permute-start.27 = (bf16[32,1792]{1,0:T(8,128)(2,1)S(1)}, bf16[32,1792]{1,0:T(8,128)(2,1)S(1)}, u32[]{:S(2)}, u32[]{:S(2)}) collective-permute-start(bf16[32,1792]{1,0:T(8,128)(2,1)S(1)} %get-tuple-element.30), channel_id=1, source_target_pairs={{0,14},{2,0},{4,2},{6,4},{8,6},{10,8},{12,10},{14,12},{1,15},{3,1}... | collective-permute-start | bytes 344072 | tf_op jit(solution)/shard_map/ppermute | solution.py:18
  142.7 16.2 %collective-permute-start.26 = (bf16[32,1792]{1,0:T(8,128)(2,1)S(1)}, bf16[32,1792]{1,0:T(8,128)(2,1)S(1)}, u32[]{:S(2)}, u32[]{:S(2)}) collective-permute-start(bf16[32,1792]{1,0:T(8,128)(2,1)S(1)} %get-tuple-element.31), channel_id=1, source_target_pairs={{0,12},{2,14},{4,0},{6,2},{8,4},{10,6},{12,8},{14,10},{1,13},{3,15... | collective-permute-start | bytes 344072 | tf_op jit(solution)/shard_map/ppermute | solution.py:18
  145.9 14.2 %collective-permute-start.25 = (bf16[32,1792]{1,0:T(8,128)(2,1)S(1)}, bf16[32,1792]{1,0:T(8,128)(2,1)S(1)}, u32[]{:S(2)}, u32[]{:S(2)}) collective-permute-start(bf16[32,1792]{1,0:T(8,128)(2,1)S(1)} %get-tuple-element.32), channel_id=1, source_target_pairs={{0,10},{2,12},{4,14},{6,0},{8,2},{10,4},{12,6},{14,8},{1,11},{3,13... | collective-permute-start | bytes 344072 | tf_op jit(solution)/shard_map/ppermute | solution.py:18
  146.0 14.2 %collective-permute-start.24 = (bf16[32,1792]{1,0:T(8,128)(2,1)S(1)}, bf16[32,1792]{1,0:T(8,128)(2,1)S(1)}, u32[]{:S(2)}, u32[]{:S(2)}) collective-permute-start(bf16[32,1792]{1,0:T(8,128)(2,1)S(1)} %get-tuple-element.33), channel_id=1, source_target_pairs={{0,8},{2,10},{4,12},{6,14},{8,0},{10,2},{12,4},{14,6},{1,9},{3,11}... | collective-permute-start | bytes 344072 | tf_op jit(solution)/shard_map/ppermute | solution.py:18
  147.1 13.3 %collective-permute-start.23 = (bf16[32,1792]{1,0:T(8,128)(2,1)S(1)}, bf16[32,1792]{1,0:T(8,128)(2,1)S(1)}, u32[]{:S(2)}, u32[]{:S(2)}) collective-permute-start(bf16[32,1792]{1,0:T(8,128)(2,1)S(1)} %get-tuple-element.34), channel_id=1, source_target_pairs={{0,6},{2,8},{4,10},{6,12},{8,14},{10,0},{12,2},{14,4},{1,7},{3,9},... | collective-permute-start | bytes 344072 | tf_op jit(solution)/shard_map/ppermute | solution.py:18
  149.8 13.0 %collective-permute-start.22 = (bf16[32,1792]{1,0:T(8,128)(2,1)S(1)}, bf16[32,1792]{1,0:T(8,128)(2,1)S(1)}, u32[]{:S(2)}, u32[]{:S(2)}) collective-permute-start(bf16[32,1792]{1,0:T(8,128)(2,1)S(1)} %get-tuple-element.35), channel_id=1, source_target_pairs={{0,4},{2,6},{4,8},{6,10},{8,12},{10,14},{12,0},{14,2},{1,5},{3,7},... | collective-permute-start | bytes 344072 | tf_op jit(solution)/shard_map/ppermute | solution.py:18
  158.9 10.4 %collective-permute-start.20 = (bf16[1,128,1792]{2,1,0:T(8,128)(2,1)S(1)}, bf16[1,128,1792]{2,1,0:T(8,128)(2,1)S(1)}, u32[]{:S(2)}, u32[]{:S(2)}) collective-permute-start(bf16[1,128,1792]{2,1,0:T(8,128)(2,1)S(1)} %fusion.1), channel_id=1, source_target_pairs={{16,0},{17,1},{18,2},{19,3},{20,4},{21,5},{22,6},{23,7},{24,8},{25... | collective-permute-start | bytes 1376264 | tf_op jit(solution)/shard_map/ppermute | solution.py:12
  (32 other events, 120.0 us)

commit v3 on v2

--- a/solution.py
+++ b/solution.py
@@ -127,6 +127,54 @@
             far_decay = far_decay * got_decay
         distance *= 2
     return near_state
+
+
+def both_scans(decay, state, state_grad, axis):
+    size, mine = (lax.axis_size(axis), lax.axis_index(axis))
+    if size & (size - 1):
+        return (
+            scan_rounds(decay, state, axis, True),
+            scan_rounds(decay, state_grad, axis, False),
+        )
+    width = state.shape[1]
+    total_decay = decay
+    total_fwd, total_bwd = (state, state_grad)
+    before = jnp.zeros_like(state)
+    before_decay = jnp.ones_like(decay)
+    after = jnp.zeros_like(state_grad)
+    after_decay = jnp.ones_like(decay)
+    distance = 1
+    while distance < size:
+        high = lax.convert_element_type(total_decay.astype(jnp.bfloat16), jnp.float32)
+        low = total_decay - high
+        pad = jnp.zeros((decay.shape[0], 126), jnp.float32)
+        payload = jnp.concatenate(
+            [total_fwd, total_bwd, high[:, None], low[:, None], pad], axis=1
+        ).astype(jnp.bfloat16)
+        got = lax.ppermute(payload, axis, [(i, i ^ distance) for i in range(size)])
+        got = got.astype(jnp.float32)
+        got_fwd = got[:, :width]
+        got_bwd = got[:, width : 2 * width]
+        got_decay = got[:, 2 * width] + got[:, 2 * width + 1]
+        upper = (mine // distance) % 2 == 1
+        before = jnp.where(upper, before + before_decay[:, None] * got_fwd, before)
+        before_decay = jnp.where(upper, before_decay * got_decay, before_decay)
+        after = jnp.where(upper, after, after + after_decay[:, None] * got_bwd)
+        after_decay = jnp.where(upper, after_decay, after_decay * got_decay)
+        if distance * 2 < size:
+            total_fwd = jnp.where(
+                upper,
+                total_fwd + total_decay[:, None] * got_fwd,
+                got_fwd + got_decay[:, None] * total_fwd,
+            )
+            total_bwd = jnp.where(
+                upper,
+                got_bwd + got_decay[:, None] * total_bwd,
+                total_bwd + total_decay[:, None] * got_bwd,
+            )
+            total_decay = total_decay * got_decay
+        distance *= 2
+    return (before, after)
 
 
 def shards(bwd_input, bwd_docs, bwd_grad, proj_weight, step_weight, step_bias, rate_log, skip_gain):
@@ -191,8 +239,7 @@
 
     state_grad = jax.vjp(carried_only, jnp.zeros(state_shape, jnp.float32))[1](cotangent)[0]
     state_grad = state_grad.reshape(heads_here, -1)
-    incoming_flat = scan_rounds(decay_bwd, state_flat, "seq", True)
-    adjoint_flat = scan_rounds(decay_bwd, state_grad, "seq", False)
+    incoming_flat, adjoint_flat = both_scans(decay_bwd, state_flat, state_grad, "seq")
     incoming_bwd = incoming_flat.reshape(state_shape)
 
     unused, output_pull = jax.vjp(

time: 171 us -> 175 us (1.023)
  the two profiles are of different devices: /device:TPU:8 before, /device:TPU:0 now
where the time goes in v3:
time: 175 us; the launch traced here: 174 us
  waiting for transfers between devices  66.5 us (38%)
  starting transfers between devices  39.1 us (22%)
  matrix products  23 us (13%)
  other arithmetic  22.1 us (13%)
  local copies, waits for them, and re-layouts  20.7 us (12%)
  between operations  2.68 us (2%)
    ppermute x3, waiting for transfers between devices, both_scans(): got = lax.ppermute(payload, axis, [(i, i ^ distance) for i in range(size)])  45.8 us
    ppermute x14, starting transfers between devices, rotated(): return lax.ppermute(block, axis, route)  28.4 us
    ppermute x2, waiting for transfers between devices, shifted(): return lax.ppermute(block, axis, route)  10.8 us
    dot_general x5, matrix products, contract(): return jnp.einsum(spec, left, right, preferred_element_type=jnp.float32)  10.1 us
    ppermute x14, waiting for transfers between devices, rotated(): return lax.ppermute(block, axis, route)  6.73 us
    ppermute x2, starting transfers between devices, shifted(): return lax.ppermute(block, axis, route)  4.32 us
    ppermute x3, starting transfers between devices, both_scans(): got = lax.ppermute(payload, axis, [(i, i ^ distance) for i in range(size)])  3.59 us
    unnamed x90, local copies, waits for them, and re-layouts  3.5 us
  transfers between devices with their start and end apart: 24, of which 13 were waited for; matrix products, arithmetic and copies ran while one was open for 13% of the time, Pallas kernels for 0%

profile of v3, /device:TPU:0, one launch (start us, length us, event | category | flops | bytes accessed | tf_op | source)
XLA Modules:
  0.0 174.3 jit_solution(2030299610763062981)
XLA Ops:
  0.7 3.0 %collective-permute-start = (bf16[32,1792]{1,0:T(8,128)(2,1)}, bf16[32,1792]{1,0:T(8,128)(2,1)S(1)}, u32[]{:S(2)}, u32[]{:S(2)}) collective-permute-start(bf16[32,1792]{1,0:T(8,128)(2,1)} %bitcast.243), channel_id=1, source_target_pairs={{0,2},{2,4},{4,6},{6,8},{8,10},{10,12},{12,14},{14,0},{1,3},{3,5},... | collective-permute-start | bytes 344072 | tf_op jit(solution)/shard_map/ppermute | solution.py:18
  3.7 1.6 collective-permute-start.1
  5.3 2.5 %collective-permute-start.2 = (bf16[32,1792]{1,0:T(8,128)(2,1)}, bf16[32,1792]{1,0:T(8,128)(2,1)S(1)}, u32[]{:S(2)}, u32[]{:S(2)}) collective-permute-start(bf16[32,1792]{1,0:T(8,128)(2,1)} %bitcast.245), channel_id=1, source_target_pairs={{0,6},{2,8},{4,10},{6,12},{8,14},{10,0},{12,2},{14,4},{1,7},{3,9},... | collective-permute-start | bytes 344072 | tf_op jit(solution)/shard_map/ppermute | solution.py:18
  7.8 1.2 collective-permute-start.3
  9.0 1.2 slice.102
  10.3 3.0 %collective-permute-start.8 = (s32[1]{0:T(128)}, s32[1]{0:T(128)}, u32[]{:S(2)}, u32[]{:S(2)}) collective-permute-start(s32[1]{0:T(128)} %bitcast.21), channel_id=1, source_target_pairs={{0,2},{2,4},{4,6},{6,8},{8,10},{10,12},{12,14},{1,3},{3,5},{5,7},{... | collective-permute-start | bytes 20 | tf_op jit(solution)/shard_map/ppermute | solution.py:12
  14.2 1.3 copy.89
  18.0 1.7 collective-permute-start.4
  19.6 1.3 broadcast_compare_fusion.1
  22.8 5.3 %collective-permute-start.5 = (bf16[32,1792]{1,0:T(8,128)(2,1)S(1)}, bf16[32,1792]{1,0:T(8,128)(2,1)S(1)}, u32[]{:S(2)}, u32[]{:S(2)}) collective-permute-start(bf16[32,1792]{1,0:T(8,128)(2,1)S(1)} %bitcast.248), channel_id=1, source_target_pairs={{0,12},{2,14},{4,0},{6,2},{8,4},{10,6},{12,8},{14,10},{1,13},{3,15... | collective-permute-start | bytes 344072 | tf_op jit(solution)/shard_map/ppermute | solution.py:18
  28.1 1.9 %collective-permute-start.6 = (bf16[32,1792]{1,0:T(8,128)(2,1)S(1)}, bf16[32,1792]{1,0:T(8,128)(2,1)S(1)}, u32[]{:S(2)}, u32[]{:S(2)}) collective-permute-start(bf16[32,1792]{1,0:T(8,128)(2,1)S(1)} %bitcast.249), channel_id=1, source_target_pairs={{0,14},{2,0},{4,2},{6,4},{8,6},{10,8},{12,10},{14,12},{1,15},{3,1}... | collective-permute-start | bytes 344072 | tf_op jit(solution)/shard_map/ppermute | solution.py:18
  30.5 2.9 %collective-permute-done.6 = bf16[32,1792]{1,0:T(8,128)(2,1)S(1)} collective-permute-done((bf16[32,1792]{1,0:T(8,128)(2,1)S(1)}, bf16[32,1792]{1,0:T(8,128)(2,1)S(1)}, u32[]{:S(2)}, u32[]{:S(2)}) %collective-permute-start.6) | collective-permute-done | bytes 114720 | tf_op jit(solution)/shard_map/ppermute | solution.py:18
  35.3 1.3 fusion.35
  36.6 1.5 reshape.268
  38.1 1.5 convolution_bitcast_fusion
  39.6 1.5 copy.95
  41.9 3.0 %collective-permute-start.9 = (bf16[28,8320]{1,0:T(8,128)(2,1)S(1)}, bf16[28,8320]{1,0:T(8,128)(2,1)S(1)}, u32[]{:S(2)}, u32[]{:S(2)}) collective-permute-start(bf16[28,8320]{1,0:T(8,128)(2,1)S(1)} %concatenate.33), channel_id=1, source_target_pairs={{0,2},{2,0},{4,6},{6,4},{8,10},{10,8},{12,14},{14,12},{1,3},{3,1},... | collective-permute-start | bytes 1397768 | tf_op jit(solution)/shard_map/ppermute | solution.py:154
  45.0 12.3 %collective-permute-done.9 = bf16[28,8320]{1,0:T(8,128)(2,1)S(1)} collective-permute-done((bf16[28,8320]{1,0:T(8,128)(2,1)S(1)}, bf16[28,8320]{1,0:T(8,128)(2,1)S(1)}, u32[]{:S(2)}, u32[]{:S(2)}) %collective-permute-start.9) | collective-permute-done | bytes 465952 | tf_op jit(solution)/shard_map/ppermute | solution.py:154
  58.8 13.7 %collective-permute-done.10 = bf16[28,8320]{1,0:T(8,128)(2,1)} collective-permute-done((bf16[28,8320]{1,0:T(8,128)(2,1)S(1)}, bf16[28,8320]{1,0:T(8,128)(2,1)}, u32[]{:S(2)}, u32[]{:S(2)}) %collective-permute-start.10) | collective-permute-done | bytes 465952 | tf_op jit(solution)/shard_map/ppermute | solution.py:154
  72.6 1.1 convert_element_type.252
  74.5 1.9 %select_convert_fusion = (bf16[28,4096]{1,0:T(8,128)(2,1)S(1)}, bf16[28,4096]{1,0:T(8,128)(2,1)}) fusion(f32[28,8320]{1,0:T(8,128)S(1)} %convert_element_type.252, f32[28]{0:T(128)S(1)} %get-tuple-element.21, f32[28]{0:T(128)} %get-tuple-element.34, pred[]{:T(512)S(6)} %eq.80, f32[28,4096]{1,0:T(8,128)S(1)} %reshape.269, f32[28]{0:T(128)} %copy-done.36, ...), kind=kLoop, calls=%fused_computation.66 | loop fusion | flops 2523136 | bytes 3211714 | tf_op jit(solution)/shard_map/convert.9
  76.4 1.8 %concatenate.35 = bf16[28,8320]{1,0:T(8,128)(2,1)} concatenate(bf16[28,4096]{1,0:T(8,128)(2,1)} %get-tuple-element.44, bf16[28,4096]{1,0:T(8,128)(2,1)S(1)} %get-tuple-element.43, bf16[28,1]{1,0:T(8,128)(2,1)S(1)} %get-tuple-element.61, bf16[28,1]{1,0:T(8,128)(2,1)S(1)} %get-tuple-element.32, bf16[28,126]{1,0:T(8,128)(2,1)S(1)} %broadcast.161), dimensions={1} | concatenate | bytes 931840 | tf_op jit(solution)/shard_map/concatenate | solution.py:151
  80.8 1.5 fusion.25
  83.8 19.8 %collective-permute-done.11 = bf16[28,8320]{1,0:T(8,128)(2,1)} collective-permute-done((bf16[28,8320]{1,0:T(8,128)(2,1)}, bf16[28,8320]{1,0:T(8,128)(2,1)}, u32[]{:S(2)}, u32[]{:S(2)}) %collective-permute-start.11) | collective-permute-done | bytes 465952 | tf_op jit(solution)/shard_map/ppermute | solution.py:154
  103.5 1.1 convert_element_type.255
  104.7 1.9 %multiply_reduce_fusion.2 = (f32[28]{0:T(128)}, bf16[28,4096]{1,0:T(8,128)(2,1)}, f32[28,4096]{1,0:T(8,128)}) fusion(f32[28,8320]{1,0:T(8,128)S(1)} %convert_element_type.255, f32[28]{0:T(128)S(1)} %copy-done.32, f32[28,8320]{1,0:T(8,128)S(1)} %convert_element_type.252, f32[28]{0:T(128)S(1)} %copy-done.34, f32[28,8320]{1,0:T(8,128)S(1)} %convert_element_type.249, ...), kind=kLoop, calls=%fused_computation.65 | loop fusion | flops 1949668 | bytes 3441203 | tf_op jit(solution)/shard_map/reduce_sum | solution.py:256
  106.5 1.4 reshape.270
  108.0 1.2 copy.99
  109.2 1.8 %fusion.93 = f32[128,1792]{0,1:S(1)} fusion(f32[64,1792]{0,1:T(8,128)} %bitcast.232, bf16[128,128]{0,1:T(8,128)(2,1)S(1)} %fusion.63), kind=kOutput, calls=%fused_computation.171 | convolution fusion | flops 176160768 | bytes 1392640
  113.3 2.2 %fusion.108 = (f32[28]{0:T(128)}, f32[128,28]{1,0:T(8,128)}, f32[28,128]{0,1:T(8,128)S(1)}) fusion(f32[128,28]{1,0:T(8,128)} %copy-done.9, f32[28]{0:T(128)} %copy-done.31, f32[128]{0:T(128)} %copy-done.26, f32[128,28]{1,0:T(8,128)S(1)} %copy.103, f32[28]{0:T(128)} %bitcast.254, f32[28,1,128]{0,2,1:T(8,128)} %copy-done.11, pred[128]{0:T(512)(128)(4,1)} %copy-done.25), kind=kLoop, calls=%fused_computation.202 | loop fusion | flops 50148 | bytes 72656 | tf_op jit(solution)/shard_map/transpose(jvp())/reduce_sum | solution.py:67
  116.1 3.5 %fusion.12 = (f32[28,128]{1,0:T(8,128)}, f32[28,128]{1,0:T(8,128)}, f32[28,128]{1,0:T(8,128)}, bf16[128,128]{1,0:T(8,128)(2,1)S(1)}) fusion(f32[28,128]{1,0:T(8,128)} %copy.90, f32[128,128]{1,0:T(8,128)} %fusion.90, f32[128,128]{1,0:T(8,128)} %get-tuple-element.67, f32[28,128]{1,0:T(8,128)} %bitcast.251, pred[128,128]{1,0:T(8,128)(4,1)} %get-tuple-element.66, ...), kind=kOutput, calls=%fused_computation.18 | convolution fusion | flops 66491904 | bytes 1169408 | tf_op jit(solution)/shard_map/transpose(jvp(hts,shp->thp))/dot_general | solution.py:44
  119.6 1.4 copy.91
  122.0 2.4 %multiply_reduce_fusion.4 = (f32[28]{0:T(128)}, f32[28]{0:T(128)}, f32[28]{0:T(128)}, f32[128,28]{1,0:T(8,128)S(1)}, f32[28]{0:T(128)}, /*index=5*/f32[128,28]{1,0:T(8,128)}) fusion(f32[28]{0:T(128)} %bitcast.255, f32[28,1,128]{0,2,1:T(8,128)S(1)} %copy-done.12, f32[128,28]{1,0:T(8,128)S(1)} %fusion.69, f32[28]{0:T(128)} %copy-done.39, ...), kind=kOutput, calls=%fused_computation.120 | convolution fusion | flops 5655952 | bytes 159632 | tf_op jit(solution)/shard_map/transpose(jvp())/dot_general | solution.py:58
  129.3 1.1 collective-permute-start.21
  133.1 2.7 %fusion.22 = f32[128,28,64]{0,2,1:T(8,128)} fusion(bf16[28,64,128]{2,1,0:T(8,128)(2,1)S(1)} %bitcast.222, f32[28,128]{1,0:T(8,128)} %copy.90, f32[128,128]{1,0:T(8,128)S(1)} %copy-done.22, f32[128,128]{1,0:T(8,128)S(1)} %copy-done.23, f32[28,128]{1,0:T(8,128)} %bitcast.252, pred[128,128]{1,0:T(8,128)(4,1)} %get-tuple-element.66, ...), kind=kOutput, calls=%fused_computation.35 | convolution fusion | flops 63537152 | bytes 2032752 | tf_op jit(solution)/shard_map/transpose(jvp(hts,shp->thp))/dot_general | solution.py:44
  136.7 1.6 collective-permute-start.23
  138.3 1.7 fusion.18
  141.3 1.8 %fusion.111 = (bf16[256,1792]{1,0:T(8,128)(2,1)S(1)}, f32[256,1792]{1,0:T(8,128)}) fusion(bf16[1,128,1792]{2,1,0:T(8,128)(2,1)S(1)} %copy-done.7, s32[]{:T(128)S(6)} %select_n.210, bf16[128,256]{0,1:T(8,128)(2,1)S(1)} %maximum_select_fusion), kind=kOutput, calls=%fused_computation.205 | convolution fusion | flops 118030336 | bytes 3276804 | tf_op jit(solution)/shard_map/dot_general | solution.py:276
  143.2 1.1 collective-permute-start.14
  144.3 1.2 collective-permute-start.15
  146.8 1.5 collective-permute-start.16
  148.3 2.7 %collective-permute-start.17 = (bf16[32,1792]{1,0:T(8,128)(2,1)S(1)}, bf16[32,1792]{1,0:T(8,128)(2,1)S(1)}, u32[]{:S(2)}, u32[]{:S(2)}) collective-permute-start(bf16[32,1792]{1,0:T(8,128)(2,1)S(1)} %get-tuple-element.51), channel_id=1, source_target_pairs={{0,8},{2,10},{4,12},{6,14},{8,0},{10,2},{12,4},{14,6},{1,9},{3,11}... | collective-permute-start | bytes 344072 | tf_op jit(solution)/shard_map/ppermute | solution.py:18
  152.2 2.0 %collective-permute-start.19 = (bf16[32,1792]{1,0:T(8,128)(2,1)S(1)}, bf16[32,1792]{1,0:T(8,128)(2,1)S(1)}, u32[]{:S(2)}, u32[]{:S(2)}) collective-permute-start(bf16[32,1792]{1,0:T(8,128)(2,1)S(1)} %get-tuple-element.49), channel_id=1, source_target_pairs={{0,12},{2,14},{4,0},{6,2},{8,4},{10,6},{12,8},{14,10},{1,13},{3,15... | collective-permute-start | bytes 344072 | tf_op jit(solution)/shard_map/ppermute | solution.py:18
  154.2 1.8 %collective-permute-start.20 = (bf16[32,1792]{1,0:T(8,128)(2,1)S(1)}, bf16[32,1792]{1,0:T(8,128)(2,1)S(1)}, u32[]{:S(2)}, u32[]{:S(2)}) collective-permute-start(bf16[32,1792]{1,0:T(8,128)(2,1)S(1)} %get-tuple-element.48), channel_id=1, source_target_pairs={{0,14},{2,0},{4,2},{6,4},{8,6},{10,8},{12,10},{14,12},{1,15},{3,1}... | collective-permute-start | bytes 344072 | tf_op jit(solution)/shard_map/ppermute | solution.py:18
  156.3 3.1 %collective-permute-done.16 = bf16[32,1792]{1,0:T(8,128)(2,1)S(1)} collective-permute-done((bf16[32,1792]{1,0:T(8,128)(2,1)S(1)}, bf16[32,1792]{1,0:T(8,128)(2,1)S(1)}, u32[]{:S(2)}, u32[]{:S(2)}) %collective-permute-start.16) | collective-permute-done | bytes 114720 | tf_op jit(solution)/shard_map/ppermute | solution.py:18
  159.5 1.3 collective-permute-start.13
  161.0 1.7 fusion.53
  162.7 10.8 %collective-permute-done.13 = bf16[1,128,1792]{2,1,0:T(8,128)(2,1)S(1)} collective-permute-done((bf16[1,128,1792]{2,1,0:T(8,128)(2,1)S(1)}, bf16[1,128,1792]{2,1,0:T(8,128)(2,1)S(1)}, u32[]{:S(2)}, u32[]{:S(2)}) %collective-permute-start.13) | collective-permute-done | bytes 458784 | tf_op jit(solution)/shard_map/ppermute | solution.py:12
  (187 shorter events, 30.7 us)
Async XLA Ops:
  0.6 17.3 %copy-start.19 = (bf16[1,32,1792]{2,1,0:T(8,128)(2,1)S(1)}, bf16[1,32,1792]{2,1,0:T(8,128)(2,1)}, u32[]{:S(2)}) copy-start(bf16[1,32,1792]{2,1,0:T(8,128)(2,1)} %param.12) | copy-start | bytes 344068
  0.6 19.0 %copy-start.27 = (s32[1,128]{1,0:T(1,128)S(1)}, s32[1,128]{1,0:T(1,128)}, u32[]{:S(2)}) copy-start(s32[1,128]{1,0:T(1,128)} %param.10) | copy-start | bytes 1540
  0.7 17.0 %copy-start.13 = (bf16[1,128,1792]{2,1,0:T(8,128)(2,1)S(1)}, bf16[1,128,1792]{2,1,0:T(8,128)(2,1)}, u32[]{:S(2)}) copy-start(bf16[1,128,1792]{2,1,0:T(8,128)(2,1)} %param.11) | copy-start | bytes 1376260
  0.7 21.5 %copy-start.30 = (f32[1,28]{1,0:T(1,128)S(1)}, f32[1,28]{1,0:T(1,128)}, u32[]{:S(2)}) copy-start(f32[1,28]{1,0:T(1,128)} %param.14) | copy-start | bytes 340
  0.7 22.1 %collective-permute-start = (bf16[32,1792]{1,0:T(8,128)(2,1)}, bf16[32,1792]{1,0:T(8,128)(2,1)S(1)}, u32[]{:S(2)}, u32[]{:S(2)}) collective-permute-start(bf16[32,1792]{1,0:T(8,128)(2,1)} %bitcast.243), channel_id=1, source_target_pairs={{0,2},{2,4},{4,6},{6,8},{8,10},{10,12},{12,14},{14,0},{1,3},{3,5},... | collective-permute-start | bytes 344072 | tf_op jit(solution)/shard_map/ppermute | solution.py:18
  3.7 24.4 %collective-permute-start.1 = (bf16[32,1792]{1,0:T(8,128)(2,1)}, bf16[32,1792]{1,0:T(8,128)(2,1)S(1)}, u32[]{:S(2)}, u32[]{:S(2)}) collective-permute-start(bf16[32,1792]{1,0:T(8,128)(2,1)} %bitcast.244), channel_id=1, source_target_pairs={{0,4},{2,6},{4,8},{6,10},{8,12},{10,14},{12,0},{14,2},{1,5},{3,7},... | collective-permute-start | bytes 344072 | tf_op jit(solution)/shard_map/ppermute | solution.py:18
  5.3 24.8 %collective-permute-start.2 = (bf16[32,1792]{1,0:T(8,128)(2,1)}, bf16[32,1792]{1,0:T(8,128)(2,1)S(1)}, u32[]{:S(2)}, u32[]{:S(2)}) collective-permute-start(bf16[32,1792]{1,0:T(8,128)(2,1)} %bitcast.245), channel_id=1, source_target_pairs={{0,6},{2,8},{4,10},{6,12},{8,14},{10,0},{12,2},{14,4},{1,7},{3,9},... | collective-permute-start | bytes 344072 | tf_op jit(solution)/shard_map/ppermute | solution.py:18
  7.8 22.3 %collective-permute-start.3 = (bf16[32,1792]{1,0:T(8,128)(2,1)}, bf16[32,1792]{1,0:T(8,128)(2,1)S(1)}, u32[]{:S(2)}, u32[]{:S(2)}) collective-permute-start(bf16[32,1792]{1,0:T(8,128)(2,1)} %bitcast.246), channel_id=1, source_target_pairs={{0,8},{2,10},{4,12},{6,14},{8,0},{10,2},{12,4},{14,6},{1,9},{3,11}... | collective-permute-start | bytes 344072 | tf_op jit(solution)/shard_map/ppermute | solution.py:18
  10.3 7.7 %collective-permute-start.8 = (s32[1]{0:T(128)}, s32[1]{0:T(128)}, u32[]{:S(2)}, u32[]{:S(2)}) collective-permute-start(s32[1]{0:T(128)} %bitcast.21), channel_id=1, source_target_pairs={{0,2},{2,4},{4,6},{6,8},{8,10},{10,12},{12,14},{1,3},{3,5},{5,7},{... | collective-permute-start | bytes 20 | tf_op jit(solution)/shard_map/ppermute | solution.py:12
  15.5 19.8 %copy-start.4 = (bf16[1,128,1792]{1,2,0:T(8,128)(2,1)}, bf16[1,128,1792]{1,2,0:T(8,128)(2,1)S(1)}, u32[]{:S(2)}) copy-start(bf16[1,128,1792]{1,2,0:T(8,128)(2,1)S(1)} %copy.89) | copy-start | bytes 1376260
  15.5 17.9 %copy-start.6 = (bf16[1,128,1792]{2,1,0:T(8,128)(2,1)S(1)}, bf16[1,128,1792]{2,1,0:T(8,128)(2,1)}, u32[]{:S(2)}) copy-start(bf16[1,128,1792]{2,1,0:T(8,128)(2,1)} %param.9) | copy-start | bytes 1376260
  17.0 16.8 %copy-start.11 = (f32[28,1,128]{0,2,1:T(8,128)}, f32[28,1,128]{0,2,1:T(8,128)S(1)}, u32[]{:S(2)}) copy-start(f32[28,1,128]{0,2,1:T(8,128)S(1)} %copy.113) | copy-start | bytes 43012
  17.9 20.2 %copy-start = (bf16[1,128,1792]{1,2,0:T(8,128)(2,1)}, bf16[1,128,1792]{1,2,0:T(8,128)(2,1)S(1)}, u32[]{:S(2)}) copy-start(bf16[1,128,1792]{1,2,0:T(8,128)(2,1)S(1)} %copy.88) | copy-start | bytes 1376260
  18.0 12.1 %collective-permute-start.4 = (bf16[32,1792]{1,0:T(8,128)(2,1)S(1)}, bf16[32,1792]{1,0:T(8,128)(2,1)S(1)}, u32[]{:S(2)}, u32[]{:S(2)}) collective-permute-start(bf16[32,1792]{1,0:T(8,128)(2,1)S(1)} %bitcast.247), channel_id=1, source_target_pairs={{0,10},{2,12},{4,14},{6,0},{8,2},{10,4},{12,6},{14,8},{1,11},{3,13... | collective-permute-start | bytes 344072 | tf_op jit(solution)/shard_map/ppermute | solution.py:18
  20.9 12.4 %copy-start.25 = (pred[128]{0:T(512)(128)(4,1)}, pred[128]{0:T(512)(128)(4,1)S(1)}, u32[]{:S(2)}) copy-start(pred[128]{0:T(512)(128)(4,1)S(1)} %get-tuple-element.41) | copy-start | bytes 388
  20.9 12.4 %copy-start.26 = (f32[128]{0:T(128)}, f32[128]{0:T(128)S(1)}, u32[]{:S(2)}) copy-start(f32[128]{0:T(128)S(1)} %get-tuple-element.42) | copy-start | bytes 1540
  22.5 11.4 %copy-start.24 = (f32[128,28]{0,1:T(8,128)}, f32[128,28]{0,1:T(8,128)S(1)}, u32[]{:S(2)}) copy-start(f32[128,28]{0,1:T(8,128)S(1)} %get-tuple-element.69) | copy-start | bytes 43012
  22.6 22.4 %copy-start.9 = (f32[128,28]{1,0:T(8,128)}, f32[128,28]{1,0:T(8,128)S(1)}, u32[]{:S(2)}) copy-start(f32[128,28]{1,0:T(8,128)S(1)} %copy.92) | copy-start | bytes 43012
  22.6 10.7 %copy-start.31 = (f32[28]{0:T(128)}, f32[28]{0:T(128)S(1)}, u32[]{:S(2)}) copy-start(f32[28]{0:T(128)S(1)} %slice_bitcast_fusion.3) | copy-start | bytes 340
  22.8 7.7 %collective-permute-start.5 = (bf16[32,1792]{1,0:T(8,128)(2,1)S(1)}, bf16[32,1792]{1,0:T(8,128)(2,1)S(1)}, u32[]{:S(2)}, u32[]{:S(2)}) collective-permute-start(bf16[32,1792]{1,0:T(8,128)(2,1)S(1)} %bitcast.248), channel_id=1, source_target_pairs={{0,12},{2,14},{4,0},{6,2},{8,4},{10,6},{12,8},{14,10},{1,13},{3,15... | collective-permute-start | bytes 344072 | tf_op jit(solution)/shard_map/ppermute | solution.py:18
  28.1 5.3 %collective-permute-start.6 = (bf16[32,1792]{1,0:T(8,128)(2,1)S(1)}, bf16[32,1792]{1,0:T(8,128)(2,1)S(1)}, u32[]{:S(2)}, u32[]{:S(2)}) collective-permute-start(bf16[32,1792]{1,0:T(8,128)(2,1)S(1)} %bitcast.249), channel_id=1, source_target_pairs={{0,14},{2,0},{4,2},{6,4},{8,6},{10,8},{12,10},{14,12},{1,15},{3,1}... | collective-permute-start | bytes 344072 | tf_op jit(solution)/shard_map/ppermute | solution.py:18
  33.9 1.3 collective-permute-start.7
  41.9 15.4 %collective-permute-start.9 = (bf16[28,8320]{1,0:T(8,128)(2,1)S(1)}, bf16[28,8320]{1,0:T(8,128)(2,1)S(1)}, u32[]{:S(2)}, u32[]{:S(2)}) collective-permute-start(bf16[28,8320]{1,0:T(8,128)(2,1)S(1)} %concatenate.33), channel_id=1, source_target_pairs={{0,2},{2,0},{4,6},{6,4},{8,10},{10,8},{12,14},{14,12},{1,3},{3,1},... | collective-permute-start | bytes 1397768 | tf_op jit(solution)/shard_map/ppermute | solution.py:154
  45.0 13.5 %copy-start.36 = (f32[28]{0:T(128)}, f32[28]{0:T(128)S(1)}, u32[]{:S(2)}) copy-start(f32[28]{0:T(128)S(1)} %exponential_multiply_fusion.1) | copy-start | bytes 340
  58.8 13.8 %collective-permute-start.10 = (bf16[28,8320]{1,0:T(8,128)(2,1)S(1)}, bf16[28,8320]{1,0:T(8,128)(2,1)}, u32[]{:S(2)}, u32[]{:S(2)}) collective-permute-start(bf16[28,8320]{1,0:T(8,128)(2,1)S(1)} %concatenate.34), channel_id=1, source_target_pairs={{0,4},{2,6},{4,0},{6,2},{8,12},{10,14},{12,8},{14,10},{1,5},{3,7},... | collective-permute-start | bytes 1397768 | tf_op jit(solution)/shard_map/ppermute | solution.py:154
  78.1 25.4 %collective-permute-start.11 = (bf16[28,8320]{1,0:T(8,128)(2,1)}, bf16[28,8320]{1,0:T(8,128)(2,1)}, u32[]{:S(2)}, u32[]{:S(2)}) collective-permute-start(bf16[28,8320]{1,0:T(8,128)(2,1)} %concatenate.35), channel_id=1, source_target_pairs={{0,8},{2,10},{4,12},{6,14},{8,0},{10,2},{12,4},{14,6},{1,9},{3,11}... | collective-permute-start | bytes 1397768 | tf_op jit(solution)/shard_map/ppermute | solution.py:154
  80.0 24.6 %copy-start.32 = (f32[28]{0:T(128)S(1)}, f32[28]{0:T(128)}, u32[]{:S(2)}) copy-start(f32[28]{0:T(128)} %get-tuple-element.18) | copy-start | bytes 340
  80.0 24.6 %copy-start.33 = (f32[28]{0:T(128)S(1)}, f32[28]{0:T(128)}, u32[]{:S(2)}) copy-start(f32[28]{0:T(128)} %get-tuple-element.19) | copy-start | bytes 340
  80.0 24.6 %copy-start.34 = (f32[28]{0:T(128)S(1)}, f32[28]{0:T(128)}, u32[]{:S(2)}) copy-start(f32[28]{0:T(128)} %get-tuple-element.20) | copy-start | bytes 340
  80.0 24.6 %copy-start.35 = (f32[28]{0:T(128)S(1)}, f32[28]{0:T(128)}, u32[]{:S(2)}) copy-start(f32[28]{0:T(128)} %get-tuple-element.22) | copy-start | bytes 340
  116.1 5.9 %copy-start.12 = (f32[28,1,128]{0,2,1:T(8,128)S(1)}, f32[28,1,128]{0,2,1:T(8,128)}, u32[]{:S(2)}) copy-start(f32[28,1,128]{0,2,1:T(8,128)} %copy-done.11) | copy-start | bytes 43012
  124.5 8.0 %copy-start.17 = (f32[128,28]{1,0:T(8,128)S(1)}, f32[128,28]{1,0:T(8,128)}, u32[]{:S(2)}) copy-start(f32[128,28]{1,0:T(8,128)} %get-tuple-element.59) | copy-start | bytes 43012
  124.5 8.6 %copy-start.20 = (f32[28,64]{1,0:T(8,128)S(1)}, f32[28,64]{1,0:T(8,128)}, u32[]{:S(2)}) copy-start(f32[28,64]{1,0:T(8,128)} %reshape_squeeze.10) | copy-start | bytes 21508
  124.5 8.6 %copy-start.22 = (f32[128,128]{1,0:T(8,128)S(1)}, f32[128,128]{1,0:T(8,128)}, u32[]{:S(2)}) copy-start(f32[128,128]{1,0:T(8,128)} %fusion.90) | copy-start | bytes 196612
  127.2 5.9 %copy-start.23 = (f32[128,128]{1,0:T(8,128)S(1)}, f32[128,128]{1,0:T(8,128)}, u32[]{:S(2)}) copy-start(f32[128,128]{1,0:T(8,128)} %get-tuple-element.67) | copy-start | bytes 196612
  129.3 3.7 %collective-permute-start.21 = (f32[1876]{0:T(1024)S(1)}, f32[1876]{0:T(1024)S(1)}, u32[]{:S(2)}, u32[]{:S(2)}) collective-permute-start(f32[1876]{0:T(1024)S(1)} %concatenate.39), channel_id=1, source_target_pairs={{0,2},{2,0},{4,6},{6,4},{8,10},{10,8},{12,14},{14,12},{1,3},{3,1},... | collective-permute-start | bytes 22520 | tf_op jit(solution)/shard_map/ppermute | solution.py:38
  132.4 8.9 %collective-permute-start.12 = (bf16[128,128]{0,1:T(8,128)(2,1)S(1)}, bf16[128,128]{0,1:T(8,128)(2,1)S(1)}, u32[]{:S(2)}, u32[]{:S(2)}) collective-permute-start(bf16[128,128]{0,1:T(8,128)(2,1)S(1)} %add_convert_fusion), channel_id=1, source_target_pairs={{0,1},{1,0},{2,3},{3,2},{4,5},{5,4},{6,7},{7,6},{8,9},{9,8},{10,11... | collective-permute-start | bytes 98312 | tf_op jit(solution)/shard_map/ppermute | solution.py:29
  133.0 3.7 %collective-permute-start.22 = (f32[1876]{0:T(1024)S(1)}, f32[1876]{0:T(1024)S(1)}, u32[]{:S(2)}, u32[]{:S(2)}) collective-permute-start(f32[1876]{0:T(1024)S(1)} %add.245), channel_id=1, source_target_pairs={{0,4},{2,6},{4,0},{6,2},{8,12},{10,14},{12,8},{14,10},{1,5},{3,7},... | collective-permute-start | bytes 22520 | tf_op jit(solution)/shard_map/ppermute | solution.py:38
  136.7 4.5 %collective-permute-start.23 = (f32[1876]{0:T(1024)S(1)}, f32[1876]{0:T(1024)S(1)}, u32[]{:S(2)}, u32[]{:S(2)}) collective-permute-start(f32[1876]{0:T(1024)S(1)} %add.246), channel_id=1, source_target_pairs={{0,8},{2,10},{4,12},{6,14},{8,0},{10,2},{12,4},{14,6},{1,9},{3,11}... | collective-permute-start | bytes 22520 | tf_op jit(solution)/shard_map/ppermute | solution.py:38
  141.3 14.7 %copy-start.3 = (bf16[256,1792]{1,0:T(8,128)(2,1)S(1)}, bf16[256,1792]{1,0:T(8,128)(2,1)}, u32[]{:S(2)}) copy-start(bf16[256,1792]{1,0:T(8,128)(2,1)} %copy-done.2) | copy-start | bytes 2752516
  143.2 8.9 %collective-permute-start.14 = (bf16[32,1792]{1,0:T(8,128)(2,1)S(1)}, bf16[32,1792]{1,0:T(8,128)(2,1)S(1)}, u32[]{:S(2)}, u32[]{:S(2)}) collective-permute-start(bf16[32,1792]{1,0:T(8,128)(2,1)S(1)} %get-tuple-element.47), channel_id=1, source_target_pairs={{0,2},{2,4},{4,6},{6,8},{8,10},{10,12},{12,14},{14,0},{1,3},{3,5},... | collective-permute-start | bytes 344072 | tf_op jit(solution)/shard_map/ppermute | solution.py:18
  144.3 9.8 %collective-permute-start.15 = (bf16[32,1792]{1,0:T(8,128)(2,1)S(1)}, bf16[32,1792]{1,0:T(8,128)(2,1)S(1)}, u32[]{:S(2)}, u32[]{:S(2)}) collective-permute-start(bf16[32,1792]{1,0:T(8,128)(2,1)S(1)} %get-tuple-element.53), channel_id=1, source_target_pairs={{0,4},{2,6},{4,8},{6,10},{8,12},{10,14},{12,0},{14,2},{1,5},{3,7},... | collective-permute-start | bytes 344072 | tf_op jit(solution)/shard_map/ppermute | solution.py:18
  146.8 12.7 %collective-permute-start.16 = (bf16[32,1792]{1,0:T(8,128)(2,1)S(1)}, bf16[32,1792]{1,0:T(8,128)(2,1)S(1)}, u32[]{:S(2)}, u32[]{:S(2)}) collective-permute-start(bf16[32,1792]{1,0:T(8,128)(2,1)S(1)} %get-tuple-element.52), channel_id=1, source_target_pairs={{0,6},{2,8},{4,10},{6,12},{8,14},{10,0},{12,2},{14,4},{1,7},{3,9},... | collective-permute-start | bytes 344072 | tf_op jit(solution)/shard_map/ppermute | solution.py:18
  148.3 12.7 %collective-permute-start.17 = (bf16[32,1792]{1,0:T(8,128)(2,1)S(1)}, bf16[32,1792]{1,0:T(8,128)(2,1)S(1)}, u32[]{:S(2)}, u32[]{:S(2)}) collective-permute-start(bf16[32,1792]{1,0:T(8,128)(2,1)S(1)} %get-tuple-element.51), channel_id=1, source_target_pairs={{0,8},{2,10},{4,12},{6,14},{8,0},{10,2},{12,4},{14,6},{1,9},{3,11}... | collective-permute-start | bytes 344072 | tf_op jit(solution)/shard_map/ppermute | solution.py:18
  151.0 10.0 %collective-permute-start.18 = (bf16[32,1792]{1,0:T(8,128)(2,1)S(1)}, bf16[32,1792]{1,0:T(8,128)(2,1)S(1)}, u32[]{:S(2)}, u32[]{:S(2)}) collective-permute-start(bf16[32,1792]{1,0:T(8,128)(2,1)S(1)} %get-tuple-element.50), channel_id=1, source_target_pairs={{0,10},{2,12},{4,14},{6,0},{8,2},{10,4},{12,6},{14,8},{1,11},{3,13... | collective-permute-start | bytes 344072 | tf_op jit(solution)/shard_map/ppermute | solution.py:18
  152.2 8.8 %collective-permute-start.19 = (bf16[32,1792]{1,0:T(8,128)(2,1)S(1)}, bf16[32,1792]{1,0:T(8,128)(2,1)S(1)}, u32[]{:S(2)}, u32[]{:S(2)}) collective-permute-start(bf16[32,1792]{1,0:T(8,128)(2,1)S(1)} %get-tuple-element.49), channel_id=1, source_target_pairs={{0,12},{2,14},{4,0},{6,2},{8,4},{10,6},{12,8},{14,10},{1,13},{3,15... | collective-permute-start | bytes 344072 | tf_op jit(solution)/shard_map/ppermute | solution.py:18
  154.2 6.8 %collective-permute-start.20 = (bf16[32,1792]{1,0:T(8,128)(2,1)S(1)}, bf16[32,1792]{1,0:T(8,128)(2,1)S(1)}, u32[]{:S(2)}, u32[]{:S(2)}) collective-permute-start(bf16[32,1792]{1,0:T(8,128)(2,1)S(1)} %get-tuple-element.48), channel_id=1, source_target_pairs={{0,14},{2,0},{4,2},{6,4},{8,6},{10,8},{12,10},{14,12},{1,15},{3,1}... | collective-permute-start | bytes 344072 | tf_op jit(solution)/shard_map/ppermute | solution.py:18
  159.5 14.0 %collective-permute-start.13 = (bf16[1,128,1792]{2,1,0:T(8,128)(2,1)S(1)}, bf16[1,128,1792]{2,1,0:T(8,128)(2,1)S(1)}, u32[]{:S(2)}, u32[]{:S(2)}) collective-permute-start(bf16[1,128,1792]{2,1,0:T(8,128)(2,1)S(1)} %fusion.1), channel_id=1, source_target_pairs={{16,0},{17,1},{18,2},{19,3},{20,4},{21,5},{22,6},{23,7},{24,8},{25... | collective-permute-start | bytes 1376264 | tf_op jit(solution)/shard_map/ppermute | solution.py:12
  (16 other events, 61.9 us)

commit v4 on v3

--- a/solution.py
+++ b/solution.py
@@ -79,9 +79,7 @@
     return (carry_decay, span_state)
 
 
-def span_output(
-    values, mixer, step_weight, step_bias, rate_log, skip_gain, docs, doc_before, incoming
-):
+def span_local(values, mixer, step_weight, step_bias, rate_log, skip_gain, docs):
     step_size, cumulative, row_ids, col_ids = local_setup(values, step_weight, step_bias, rate_log)
     half_width = mixer.shape[1] // 2
     writers = mixer[:, :half_width]
@@ -98,15 +96,17 @@
     )
     mixing = mixing.astype(jnp.bfloat16)
     local_part = contract("hts,shp->thp", mixing, values)
+    return values.astype(jnp.float32) * (1.0 + skip_gain)[None, :, None] + local_part
+
+
+def span_carry(values, mixer, step_weight, step_bias, rate_log, docs, doc_before, incoming):
+    step_size, cumulative, row_ids, col_ids = local_setup(values, step_weight, step_bias, rate_log)
+    half_width = mixer.shape[1] // 2
+    readers = mixer[:, half_width:]
     unbroken = (docs == doc_before).astype(jnp.float32)
     carry_scale = jnp.exp(cumulative) * unbroken[:, None]
     carried = jnp.einsum("tn,hnp->thp", readers.astype(jnp.float32), incoming, precision=EXACT)
-    combined = (
-        values.astype(jnp.float32) * (1.0 + skip_gain)[None, :, None]
-        + local_part
-        + carry_scale[:, :, None] * carried
-    )
-    return combined.astype(jnp.bfloat16)
+    return carry_scale[:, :, None] * carried
 
 
 def scan_rounds(decay, state, axis, forward):
@@ -151,12 +151,21 @@
         payload = jnp.concatenate(
             [total_fwd, total_bwd, high[:, None], low[:, None], pad], axis=1
         ).astype(jnp.bfloat16)
-        got = lax.ppermute(payload, axis, [(i, i ^ distance) for i in range(size)])
-        got = got.astype(jnp.float32)
-        got_fwd = got[:, :width]
-        got_bwd = got[:, width : 2 * width]
+        upper = (mine // distance) % 2 == 1
+        if distance * 2 < size:
+            got = lax.ppermute(payload, axis, [(i, i ^ distance) for i in range(size)])
+            got = got.astype(jnp.float32)
+            got_fwd = got[:, :width]
+            got_bwd = got[:, width : 2 * width]
+        else:
+            last = jnp.where(upper, total_bwd, total_fwd).astype(jnp.bfloat16)
+            last = jnp.concatenate([last, payload[:, 2 * width :]], axis=1)
+            got = lax.ppermute(last, axis, [(i, i ^ distance) for i in range(size)])
+            got = got.astype(jnp.float32)
+            got_fwd = got[:, :width]
+            got_bwd = got_fwd
+            got = jnp.concatenate([got[:, :width], got], axis=1)
         got_decay = got[:, 2 * width] + got[:, 2 * width + 1]
-        upper = (mine // distance) % 2 == 1
         before = jnp.where(upper, before + before_decay[:, None] * got_fwd, before)
         before_decay = jnp.where(upper, before_decay * got_decay, before_decay)
         after = jnp.where(upper, after, after + after_decay[:, None] * got_bwd)
@@ -219,40 +228,38 @@
     state_shape = state_bwd.shape
     state_flat = state_bwd.reshape(heads_here, -1)
 
-    def output_bwd(values_in, mixer_in, weight_in, bias_in, rate_in, skip_in, state_in):
-        return span_output(
-            values_in,
-            mixer_in,
-            weight_in,
-            bias_in,
-            rate_in,
-            skip_in,
-            docs_bwd,
-            doc_before,
-            state_in,
+    out_ct = cotangent.astype(jnp.float32)
+
+    def local_bwd(values_in, mixer_in, weight_in, bias_in, rate_in, skip_in):
+        return span_local(values_in, mixer_in, weight_in, bias_in, rate_in, skip_in, docs_bwd)
+
+    local_grads = jax.vjp(
+        local_bwd, bwd_values, mixer_bwd, weight_heads, bias_heads, rate_heads, skip_heads
+    )[1](out_ct)
+
+    def carry_bwd(values_in, mixer_in, weight_in, bias_in, rate_in, state_in):
+        return span_carry(
+            values_in, mixer_in, weight_in, bias_in, rate_in, docs_bwd, doc_before, state_in
         )
 
     def carried_only(state_in):
-        return output_bwd(
-            bwd_values, mixer_bwd, weight_heads, bias_heads, rate_heads, skip_heads, state_in
-        )
-
-    state_grad = jax.vjp(carried_only, jnp.zeros(state_shape, jnp.float32))[1](cotangent)[0]
+        return carry_bwd(bwd_values, mixer_bwd, weight_heads, bias_heads, rate_heads, state_in)
+
+    state_grad = jax.vjp(carried_only, jnp.zeros(state_shape, jnp.float32))[1](out_ct)[0]
     state_grad = state_grad.reshape(heads_here, -1)
     incoming_flat, adjoint_flat = both_scans(decay_bwd, state_flat, state_grad, "seq")
     incoming_bwd = incoming_flat.reshape(state_shape)
-
-    unused, output_pull = jax.vjp(
-        output_bwd,
-        bwd_values,
-        mixer_bwd,
-        weight_heads,
-        bias_heads,
-        rate_heads,
-        skip_heads,
-        incoming_bwd,
-    )
-    out_grads = output_pull(cotangent)
+    carry_grads = jax.vjp(
+        carry_bwd, bwd_values, mixer_bwd, weight_heads, bias_heads, rate_heads, incoming_bwd
+    )[1](out_ct)
+    out_grads = (
+        (local_grads[0].astype(jnp.float32) + carry_grads[0].astype(jnp.float32)),
+        (local_grads[1].astype(jnp.float32) + carry_grads[1].astype(jnp.float32)),
+        local_grads[2] + carry_grads[2],
+        local_grads[3] + carry_grads[3],
+        local_grads[4] + carry_grads[4],
+        local_grads[5],
+    )
     decay_grad = jnp.sum(adjoint_flat * incoming_flat, axis=1)
     sum_grads = summary_pull((decay_grad, adjoint_flat.reshape(state_shape)))
     mixer_grad = (out_grads[1].astype(jnp.float32) + sum_grads[1].astype(jnp.float32)).astype(

time: 175 us -> 150 us (0.86)
  the two profiles are of different devices: /device:TPU:0 before, /device:TPU:4 now
where the time goes in v4:
time: 150 us
  waiting for transfers between devices  57.4 us (38%)
  starting transfers between devices  36.5 us (24%)
  matrix products  18.4 us (12%)
  other arithmetic  18.3 us (12%)
  local copies, waits for them, and re-layouts  16 us (11%)
  between operations  3.19 us (2%)
    ppermute x14, starting transfers between devices, rotated(): return lax.ppermute(block, axis, route)  28.6 us
    ppermute x2, waiting for transfers between devices, both_scans(): got = lax.ppermute(payload, axis, [(i, i ^ distance) for i in range(size)])  26.7 us
    ppermute x3, waiting for transfers between devices, seq_total(): lax.ppermute(value, 'seq', [(i, i ^ distance) for i in range(size)])  8.44 us
    ppermute x2, waiting for transfers between devices, shifted(): return lax.ppermute(block, axis, route)  7.81 us
    ppermute x1, waiting for transfers between devices, both_scans(): got = lax.ppermute(last, axis, [(i, i ^ distance) for i in range(size)])  7.11 us
    ppermute x14, waiting for transfers between devices, rotated(): return lax.ppermute(block, axis, route)  6.48 us
    ppermute x2, starting transfers between devices, shifted(): return lax.ppermute(block, axis, route)  5.6 us
    dot_general x5, matrix products, contract(): return jnp.einsum(spec, left, right, preferred_element_type=jnp.float32)  5.17 us
  transfers between devices with their start and end apart: 24, of which 13 were waited for; matrix products, arithmetic and copies ran while one was open for 14% of the time, Pallas kernels for 0%

profile of v4, /device:TPU:4, one launch (start us, length us, event | category | flops | bytes accessed | tf_op | source)
XLA Modules:
  0.0 149.8 jit_solution(12691181124742430356)
XLA Ops:
  0.7 1.6 %collective-permute-start = (bf16[32,1792]{1,0:T(8,128)(2,1)}, bf16[32,1792]{1,0:T(8,128)(2,1)S(1)}, u32[]{:S(2)}, u32[]{:S(2)}) collective-permute-start(bf16[32,1792]{1,0:T(8,128)(2,1)} %bitcast.260), channel_id=1, source_target_pairs={{0,2},{2,4},{4,6},{6,8},{8,10},{10,12},{12,14},{14,0},{1,3},{3,5},... | collective-permute-start | bytes 344072 | tf_op jit(solution)/shard_map/ppermute | solution.py:18
  2.2 1.6 %collective-permute-start.1 = (bf16[32,1792]{1,0:T(8,128)(2,1)}, bf16[32,1792]{1,0:T(8,128)(2,1)S(1)}, u32[]{:S(2)}, u32[]{:S(2)}) collective-permute-start(bf16[32,1792]{1,0:T(8,128)(2,1)} %bitcast.261), channel_id=1, source_target_pairs={{0,4},{2,6},{4,8},{6,10},{8,12},{10,14},{12,0},{14,2},{1,5},{3,7},... | collective-permute-start | bytes 344072 | tf_op jit(solution)/shard_map/ppermute | solution.py:18
  3.8 2.5 %collective-permute-start.2 = (bf16[32,1792]{1,0:T(8,128)(2,1)}, bf16[32,1792]{1,0:T(8,128)(2,1)S(1)}, u32[]{:S(2)}, u32[]{:S(2)}) collective-permute-start(bf16[32,1792]{1,0:T(8,128)(2,1)} %bitcast.262), channel_id=1, source_target_pairs={{0,6},{2,8},{4,10},{6,12},{8,14},{10,0},{12,2},{14,4},{1,7},{3,9},... | collective-permute-start | bytes 344072 | tf_op jit(solution)/shard_map/ppermute | solution.py:18
  6.7 1.2 slice.105
  7.9 4.3 %collective-permute-start.8 = (s32[1]{0:T(128)}, s32[1]{0:T(128)}, u32[]{:S(2)}, u32[]{:S(2)}) collective-permute-start(s32[1]{0:T(128)} %bitcast.23), channel_id=1, source_target_pairs={{0,2},{2,4},{4,6},{6,8},{8,10},{10,12},{12,14},{1,3},{3,5},{5,7},{... | collective-permute-start | bytes 20 | tf_op jit(solution)/shard_map/ppermute | solution.py:12
  12.3 0.9 constant_dynamic-update-slice_fusion.7
  13.2 1.3 copy.91
  16.0 1.3 copy.92
  18.0 1.3 collective-permute-start.4
  19.3 1.2 broadcast_compare_fusion.1
  22.3 3.8 %collective-permute-start.5 = (bf16[32,1792]{1,0:T(8,128)(2,1)S(1)}, bf16[32,1792]{1,0:T(8,128)(2,1)S(1)}, u32[]{:S(2)}, u32[]{:S(2)}) collective-permute-start(bf16[32,1792]{1,0:T(8,128)(2,1)S(1)} %bitcast.265), channel_id=1, source_target_pairs={{0,12},{2,14},{4,0},{6,2},{8,4},{10,6},{12,8},{14,10},{1,13},{3,15... | collective-permute-start | bytes 344072 | tf_op jit(solution)/shard_map/ppermute | solution.py:18
  26.9 1.6 %collective-permute-done.5 = bf16[32,1792]{1,0:T(8,128)(2,1)S(1)} collective-permute-done((bf16[32,1792]{1,0:T(8,128)(2,1)S(1)}, bf16[32,1792]{1,0:T(8,128)(2,1)S(1)}, u32[]{:S(2)}, u32[]{:S(2)}) %collective-permute-start.5) | collective-permute-done | bytes 114720 | tf_op jit(solution)/shard_map/ppermute | solution.py:18
  28.5 3.4 %collective-permute-done.6 = bf16[32,1792]{1,0:T(8,128)(2,1)S(1)} collective-permute-done((bf16[32,1792]{1,0:T(8,128)(2,1)S(1)}, bf16[32,1792]{1,0:T(8,128)(2,1)S(1)}, u32[]{:S(2)}, u32[]{:S(2)}) %collective-permute-start.6) | collective-permute-done | bytes 114720 | tf_op jit(solution)/shard_map/ppermute | solution.py:18
  32.9 0.9 collective-permute-done.7
  33.8 1.5 %convolution_bitcast_fusion = f32[28,64,64]{1,2,0:T(8,128)} fusion(bf16[128,28,64]{0,2,1:T(8,128)(2,1)S(1)} %bitcast.233, f32[128,28]{0,1:T(8,128)S(1)} %get-tuple-element.71, bf16[128,128]{0,1:T(8,128)(2,1)S(1)} %fusion.63), kind=kOutput, calls=%fused_computation.22 | convolution fusion | flops 176619520 | bytes 950272 | tf_op jit(solution)/shard_map/transpose(jvp(tn,hnp->thp))/dot_general | solution.py:108
  35.4 1.5 copy.100
  38.6 14.0 %collective-permute-done.9 = bf16[28,8320]{1,0:T(8,128)(2,1)S(1)} collective-permute-done((bf16[28,8320]{1,0:T(8,128)(2,1)S(1)}, bf16[28,8320]{1,0:T(8,128)(2,1)S(1)}, u32[]{:S(2)}, u32[]{:S(2)}) %collective-permute-start.9) | collective-permute-done | bytes 465952 | tf_op jit(solution)/shard_map/ppermute | solution.py:156
  54.9 12.7 %collective-permute-done.10 = bf16[28,8320]{1,0:T(8,128)(2,1)} collective-permute-done((bf16[28,8320]{1,0:T(8,128)(2,1)S(1)}, bf16[28,8320]{1,0:T(8,128)(2,1)}, u32[]{:S(2)}, u32[]{:S(2)}) %collective-permute-start.10) | collective-permute-done | bytes 465952 | tf_op jit(solution)/shard_map/ppermute | solution.py:156
  67.5 1.1 convert_element_type.270
  69.3 1.3 fusion.84
  70.6 1.1 select_convert_fusion
  73.3 1.2 add_bitcast_fusion
  74.5 1.4 reshape_squeeze.10
  75.9 2.3 %fusion.25 = (f32[1792]{0:T(1024)S(1)}, f32[1,128,1792]{1,2,0:T(8,128)}) fusion(bf16[1,128,1792]{1,2,0:T(8,128)(2,1)} %copy-done, bf16[1,128,1792]{1,2,0:T(8,128)(2,1)} %copy-done.4, f32[128,28]{0,1:T(8,128)} %copy-done.21), kind=kLoop, calls=%fused_computation.43 | loop fusion | flops 1145088 | bytes 1856512 | tf_op jit(solution)/shard_map/transpose(jvp())/reduce_sum | solution.py:99
  79.0 7.1 %collective-permute-done.11 = bf16[28,4224]{1,0:T(8,128)(2,1)S(1)} collective-permute-done((bf16[28,4224]{1,0:T(8,128)(2,1)S(1)}, bf16[28,4224]{1,0:T(8,128)(2,1)S(1)}, u32[]{:S(2)}, u32[]{:S(2)}) %collective-permute-start.11) | collective-permute-done | bytes 236576 | tf_op jit(solution)/shard_map/ppermute | solution.py:163
  86.2 1.8 %multiply_reduce_fusion.2 = (f32[28]{0:T(128)}, bf16[28,4096]{1,0:T(8,128)(2,1)S(1)}, f32[28,4096]{1,0:T(8,128)}) fusion(bf16[28,4224]{1,0:T(8,128)(2,1)S(1)} %collective-permute-done.11, f32[28]{0:T(128)S(1)} %copy-done.52, f32[28,8320]{1,0:T(8,128)S(1)} %convert_element_type.270, f32[28]{0:T(128)S(1)} %copy-done.54, ...), kind=kLoop, calls=%fused_computation.66 | loop fusion | flops 2064356 | bytes 2753075 | tf_op jit(solution)/shard_map/reduce_sum | solution.py:263
  88.6 0.9 multiply_reduce_fusion
  89.6 1.2 fusion.111
  91.0 2.5 %fusion.12 = (f32[28,128]{1,0:T(8,128)}, f32[28,128]{1,0:T(8,128)}, f32[28,128]{1,0:T(8,128)}, bf16[128,128]{1,0:T(8,128)(2,1)S(1)}) fusion(f32[28,128]{1,0:T(8,128)S(1)} %copy.93, f32[128,128]{1,0:T(8,128)S(1)} %fusion.92, f32[128,128]{1,0:T(8,128)S(1)} %copy-done.26, f32[28,128]{1,0:T(8,128)S(1)} %bitcast.267, pred[128,128]{1,0:T(8,128)(4,1)S(1)} %copy-done.37, ...), kind=kOutput, calls=%fused_computation.18 | convolution fusion | flops 66491904 | bytes 1169408 | tf_op jit(solution)/shard_map/transpose(jvp(hts,shp->thp))/dot_general | solution.py:44
  95.4 1.2 copy.104
  96.6 1.8 %fusion.95 = f32[128,1792]{0,1:S(1)} fusion(f32[64,1792]{0,1:T(8,128)} %bitcast.247, bf16[128,128]{0,1:T(8,128)(2,1)S(1)} %fusion.63), kind=kOutput, calls=%fused_computation.174 | convolution fusion | flops 176160768 | bytes 1392640
  99.0 1.0 fusion.24
  100.5 1.0 multiply_reduce_fusion.5
  104.4 0.9 collective-permute-start.21
  105.7 2.4 %collective-permute-done.21 = f32[1876]{0:T(1024)S(1)} collective-permute-done((f32[1876]{0:T(1024)S(1)}, f32[1876]{0:T(1024)S(1)}, u32[]{:S(2)}, u32[]{:S(2)}) %collective-permute-start.21) | collective-permute-done | bytes 7536 | tf_op jit(solution)/shard_map/ppermute | solution.py:38
  108.1 0.9 fusion.23
  109.1 2.7 %collective-permute-done.22 = f32[1876]{0:T(1024)S(1)} collective-permute-done((f32[1876]{0:T(1024)S(1)}, f32[1876]{0:T(1024)S(1)}, u32[]{:S(2)}, u32[]{:S(2)}) %collective-permute-start.22) | collective-permute-done | bytes 7536 | tf_op jit(solution)/shard_map/ppermute | solution.py:38
  112.9 3.4 %collective-permute-done.23 = f32[1876]{0:T(1024)S(1)} collective-permute-done((f32[1876]{0:T(1024)S(1)}, f32[1876]{0:T(1024)S(1)}, u32[]{:S(2)}, u32[]{:S(2)}) %collective-permute-start.23) | collective-permute-done | bytes 7536 | tf_op jit(solution)/shard_map/ppermute | solution.py:38
  116.3 1.8 %fusion.114 = (bf16[256,1792]{1,0:T(8,128)(2,1)S(1)}, f32[256,1792]{1,0:T(8,128)}) fusion(bf16[1,128,1792]{2,1,0:T(8,128)(2,1)S(1)} %copy-done.7, s32[]{:T(128)S(6)} %select_n.215, bf16[128,256]{0,1:T(8,128)(2,1)S(1)} %maximum_select_fusion), kind=kOutput, calls=%fused_computation.210 | convolution fusion | flops 118030336 | bytes 3276804 | tf_op jit(solution)/shard_map/dot_general | solution.py:283
  118.2 1.0 collective-permute-start.20
  119.2 1.8 %collective-permute-start.19 = (bf16[32,1792]{1,0:T(8,128)(2,1)S(1)}, bf16[32,1792]{1,0:T(8,128)(2,1)S(1)}, u32[]{:S(2)}, u32[]{:S(2)}) collective-permute-start(bf16[32,1792]{1,0:T(8,128)(2,1)S(1)} %get-tuple-element.50), channel_id=1, source_target_pairs={{0,12},{2,14},{4,0},{6,2},{8,4},{10,6},{12,8},{14,10},{1,13},{3,15... | collective-permute-start | bytes 344072 | tf_op jit(solution)/shard_map/ppermute | solution.py:18
  122.5 1.1 collective-permute-start.18
  123.6 2.4 %collective-permute-start.17 = (bf16[32,1792]{1,0:T(8,128)(2,1)S(1)}, bf16[32,1792]{1,0:T(8,128)(2,1)S(1)}, u32[]{:S(2)}, u32[]{:S(2)}) collective-permute-start(bf16[32,1792]{1,0:T(8,128)(2,1)S(1)} %get-tuple-element.52), channel_id=1, source_target_pairs={{0,8},{2,10},{4,12},{6,14},{8,0},{10,2},{12,4},{14,6},{1,9},{3,11}... | collective-permute-start | bytes 344072 | tf_op jit(solution)/shard_map/ppermute | solution.py:18
  126.3 1.2 collective-permute-start.15
  127.5 9.5 %collective-permute-start.14 = (bf16[32,1792]{1,0:T(8,128)(2,1)S(1)}, bf16[32,1792]{1,0:T(8,128)(2,1)S(1)}, u32[]{:S(2)}, u32[]{:S(2)}) collective-permute-start(bf16[32,1792]{1,0:T(8,128)(2,1)S(1)} %get-tuple-element.48), channel_id=1, source_target_pairs={{0,2},{2,4},{4,6},{6,8},{8,10},{10,12},{12,14},{14,0},{1,3},{3,5},... | collective-permute-start | bytes 344072 | tf_op jit(solution)/shard_map/ppermute | solution.py:18
  138.1 1.3 collective-permute-start.13
  139.5 1.7 %fusion.53 = f32[1,32,1792]{2,1,0:T(8,128)} fusion(f32[256,1792]{1,0:T(8,128)} %get-tuple-element.74, bf16[32,1792]{1,0:T(8,128)(2,1)S(1)} %collective-permute-done.20, bf16[32,1792]{1,0:T(8,128)(2,1)S(1)} %collective-permute-done.19, bf16[32,1792]{1,0:T(8,128)(2,1)S(1)} %collective-permute-done.18, bf16[32,1792]{1,0:T(8,128)(2,1)S(1)} %collective-permute-done.17, ...), kind=kLoop, calls=%fused_computation.92 | loop fusion | flops 802816 | bytes 1261568 | tf_op jit(solution)/shard_map/broadcast_in_dim | solution.py:308
  141.2 7.8 %collective-permute-done.13 = bf16[1,128,1792]{2,1,0:T(8,128)(2,1)S(1)} collective-permute-done((bf16[1,128,1792]{2,1,0:T(8,128)(2,1)S(1)}, bf16[1,128,1792]{2,1,0:T(8,128)(2,1)S(1)}, u32[]{:S(2)}, u32[]{:S(2)}) %collective-permute-start.13) | collective-permute-done | bytes 458784 | tf_op jit(solution)/shard_map/ppermute | solution.py:12
  (239 shorter events, 23.1 us)
Async XLA Ops:
  0.6 17.3 %copy-start.19 = (bf16[1,32,1792]{2,1,0:T(8,128)(2,1)S(1)}, bf16[1,32,1792]{2,1,0:T(8,128)(2,1)}, u32[]{:S(2)}) copy-start(bf16[1,32,1792]{2,1,0:T(8,128)(2,1)} %param.12) | copy-start | bytes 344068
  0.6 18.7 %copy-start.46 = (s32[1,128]{1,0:T(1,128)S(1)}, s32[1,128]{1,0:T(1,128)}, u32[]{:S(2)}) copy-start(s32[1,128]{1,0:T(1,128)} %param.10) | copy-start | bytes 1540
  0.7 21.1 %copy-start.48 = (f32[1,28]{1,0:T(1,128)S(1)}, f32[1,28]{1,0:T(1,128)}, u32[]{:S(2)}) copy-start(f32[1,28]{1,0:T(1,128)} %param.14) | copy-start | bytes 340
  0.7 21.6 %collective-permute-start = (bf16[32,1792]{1,0:T(8,128)(2,1)}, bf16[32,1792]{1,0:T(8,128)(2,1)S(1)}, u32[]{:S(2)}, u32[]{:S(2)}) collective-permute-start(bf16[32,1792]{1,0:T(8,128)(2,1)} %bitcast.260), channel_id=1, source_target_pairs={{0,2},{2,4},{4,6},{6,8},{8,10},{10,12},{12,14},{14,0},{1,3},{3,5},... | collective-permute-start | bytes 344072 | tf_op jit(solution)/shard_map/ppermute | solution.py:18
  2.2 23.9 %collective-permute-start.1 = (bf16[32,1792]{1,0:T(8,128)(2,1)}, bf16[32,1792]{1,0:T(8,128)(2,1)S(1)}, u32[]{:S(2)}, u32[]{:S(2)}) collective-permute-start(bf16[32,1792]{1,0:T(8,128)(2,1)} %bitcast.261), channel_id=1, source_target_pairs={{0,4},{2,6},{4,8},{6,10},{8,12},{10,14},{12,0},{14,2},{1,5},{3,7},... | collective-permute-start | bytes 344072 | tf_op jit(solution)/shard_map/ppermute | solution.py:18
  3.8 22.4 %collective-permute-start.2 = (bf16[32,1792]{1,0:T(8,128)(2,1)}, bf16[32,1792]{1,0:T(8,128)(2,1)S(1)}, u32[]{:S(2)}, u32[]{:S(2)}) collective-permute-start(bf16[32,1792]{1,0:T(8,128)(2,1)} %bitcast.262), channel_id=1, source_target_pairs={{0,6},{2,8},{4,10},{6,12},{8,14},{10,0},{12,2},{14,4},{1,7},{3,9},... | collective-permute-start | bytes 344072 | tf_op jit(solution)/shard_map/ppermute | solution.py:18
  6.3 19.9 %collective-permute-start.3 = (bf16[32,1792]{1,0:T(8,128)(2,1)}, bf16[32,1792]{1,0:T(8,128)(2,1)S(1)}, u32[]{:S(2)}, u32[]{:S(2)}) collective-permute-start(bf16[32,1792]{1,0:T(8,128)(2,1)} %bitcast.263), channel_id=1, source_target_pairs={{0,8},{2,10},{4,12},{6,14},{8,0},{10,2},{12,4},{14,6},{1,9},{3,11}... | collective-permute-start | bytes 344072 | tf_op jit(solution)/shard_map/ppermute | solution.py:18
  7.9 10.0 %collective-permute-start.8 = (s32[1]{0:T(128)}, s32[1]{0:T(128)}, u32[]{:S(2)}, u32[]{:S(2)}) collective-permute-start(s32[1]{0:T(128)} %bitcast.23), channel_id=1, source_target_pairs={{0,2},{2,4},{4,6},{6,8},{8,10},{10,12},{12,14},{1,3},{3,5},{5,7},{... | collective-permute-start | bytes 20 | tf_op jit(solution)/shard_map/ppermute | solution.py:12
  14.4 19.4 %copy-start = (bf16[1,128,1792]{1,2,0:T(8,128)(2,1)}, bf16[1,128,1792]{1,2,0:T(8,128)(2,1)S(1)}, u32[]{:S(2)}) copy-start(bf16[1,128,1792]{1,2,0:T(8,128)(2,1)S(1)} %copy.91) | copy-start | bytes 1376260
  14.5 17.4 %copy-start.6 = (bf16[1,128,1792]{2,1,0:T(8,128)(2,1)S(1)}, bf16[1,128,1792]{2,1,0:T(8,128)(2,1)}, u32[]{:S(2)}) copy-start(bf16[1,128,1792]{2,1,0:T(8,128)(2,1)} %param.9) | copy-start | bytes 1376260
  15.2 17.1 %copy-start.63 = (f32[28]{0:T(128)}, f32[28]{0:T(128)S(1)}, u32[]{:S(2)}) copy-start(f32[28]{0:T(128)S(1)} %negate_bitcast_fusion) | copy-start | bytes 340
  17.3 19.9 %copy-start.4 = (bf16[1,128,1792]{1,2,0:T(8,128)(2,1)}, bf16[1,128,1792]{1,2,0:T(8,128)(2,1)S(1)}, u32[]{:S(2)}) copy-start(bf16[1,128,1792]{1,2,0:T(8,128)(2,1)S(1)} %copy.92) | copy-start | bytes 1376260
  17.9 14.4 %copy-start.12 = (f32[28,1,128]{0,2,1:T(8,128)}, f32[28,1,128]{0,2,1:T(8,128)S(1)}, u32[]{:S(2)}) copy-start(f32[28,1,128]{0,2,1:T(8,128)S(1)} %copy.119) | copy-start | bytes 43012
  18.0 8.9 %collective-permute-start.4 = (bf16[32,1792]{1,0:T(8,128)(2,1)S(1)}, bf16[32,1792]{1,0:T(8,128)(2,1)S(1)}, u32[]{:S(2)}, u32[]{:S(2)}) collective-permute-start(bf16[32,1792]{1,0:T(8,128)(2,1)S(1)} %bitcast.264), channel_id=1, source_target_pairs={{0,10},{2,12},{4,14},{6,0},{8,2},{10,4},{12,6},{14,8},{1,11},{3,13... | collective-permute-start | bytes 344072 | tf_op jit(solution)/shard_map/ppermute | solution.py:18
  20.5 11.8 %copy-start.42 = (pred[128]{0:T(512)(128)(4,1)}, pred[128]{0:T(512)(128)(4,1)S(1)}, u32[]{:S(2)}) copy-start(pred[128]{0:T(512)(128)(4,1)S(1)} %get-tuple-element.44) | copy-start | bytes 388
  20.5 11.8 %copy-start.44 = (f32[128]{0:T(128)}, f32[128]{0:T(128)S(1)}, u32[]{:S(2)}) copy-start(f32[128]{0:T(128)S(1)} %get-tuple-element.45) | copy-start | bytes 1540
  22.0 10.4 %copy-start.28 = (f32[128,28]{0,1:T(8,128)}, f32[128,28]{0,1:T(8,128)S(1)}, u32[]{:S(2)}) copy-start(f32[128,28]{0,1:T(8,128)S(1)} %get-tuple-element.72) | copy-start | bytes 43012
  22.0 11.8 %copy-start.21 = (f32[128,28]{0,1:T(8,128)}, f32[128,28]{0,1:T(8,128)S(1)}, u32[]{:S(2)}) copy-start(f32[128,28]{0,1:T(8,128)S(1)} %get-tuple-element.71) | copy-start | bytes 43012
  22.1 10.2 %copy-start.50 = (f32[28]{0:T(128)}, f32[28]{0:T(128)S(1)}, u32[]{:S(2)}) copy-start(f32[28]{0:T(128)S(1)} %slice_bitcast_fusion.3) | copy-start | bytes 340
  22.3 6.2 %collective-permute-start.5 = (bf16[32,1792]{1,0:T(8,128)(2,1)S(1)}, bf16[32,1792]{1,0:T(8,128)(2,1)S(1)}, u32[]{:S(2)}, u32[]{:S(2)}) collective-permute-start(bf16[32,1792]{1,0:T(8,128)(2,1)S(1)} %bitcast.265), channel_id=1, source_target_pairs={{0,12},{2,14},{4,0},{6,2},{8,4},{10,6},{12,8},{14,10},{1,13},{3,15... | collective-permute-start | bytes 344072 | tf_op jit(solution)/shard_map/ppermute | solution.py:18
  26.1 5.7 %collective-permute-start.6 = (bf16[32,1792]{1,0:T(8,128)(2,1)S(1)}, bf16[32,1792]{1,0:T(8,128)(2,1)S(1)}, u32[]{:S(2)}, u32[]{:S(2)}) collective-permute-start(bf16[32,1792]{1,0:T(8,128)(2,1)S(1)} %bitcast.266), channel_id=1, source_target_pairs={{0,14},{2,0},{4,2},{6,4},{8,6},{10,8},{12,10},{14,12},{1,15},{3,1}... | collective-permute-start | bytes 344072 | tf_op jit(solution)/shard_map/ppermute | solution.py:18
  32.5 1.3 collective-permute-start.7
  38.0 15.8 %copy-start.18 = (bf16[28,126]{1,0:T(8,128)(2,1)}, bf16[28,126]{1,0:T(8,128)(2,1)S(1)}, u32[]{:S(2)}) copy-start(bf16[28,126]{1,0:T(8,128)(2,1)S(1)} %broadcast.165) | copy-start | bytes 21172
  38.4 14.2 %collective-permute-start.9 = (bf16[28,8320]{1,0:T(8,128)(2,1)S(1)}, bf16[28,8320]{1,0:T(8,128)(2,1)S(1)}, u32[]{:S(2)}, u32[]{:S(2)}) collective-permute-start(bf16[28,8320]{1,0:T(8,128)(2,1)S(1)} %concatenate.36), channel_id=1, source_target_pairs={{0,2},{2,0},{4,6},{6,4},{8,10},{10,8},{12,14},{14,12},{1,3},{3,1},... | collective-permute-start | bytes 1397768 | tf_op jit(solution)/shard_map/ppermute | solution.py:156
  38.6 15.2 %copy-start.61 = (f32[28]{0:T(128)}, f32[28]{0:T(128)S(1)}, u32[]{:S(2)}) copy-start(f32[28]{0:T(128)S(1)} %exponential_multiply_fusion.1) | copy-start | bytes 340
  54.0 13.5 %collective-permute-start.10 = (bf16[28,8320]{1,0:T(8,128)(2,1)S(1)}, bf16[28,8320]{1,0:T(8,128)(2,1)}, u32[]{:S(2)}, u32[]{:S(2)}) collective-permute-start(bf16[28,8320]{1,0:T(8,128)(2,1)S(1)} %concatenate.37), channel_id=1, source_target_pairs={{0,4},{2,6},{4,0},{6,2},{8,12},{10,14},{12,8},{14,10},{1,5},{3,7},... | collective-permute-start | bytes 1397768 | tf_op jit(solution)/shard_map/ppermute | solution.py:156
  71.7 14.4 %copy-start.52 = (f32[28]{0:T(128)S(1)}, f32[28]{0:T(128)}, u32[]{:S(2)}) copy-start(f32[28]{0:T(128)} %get-tuple-element.19) | copy-start | bytes 340
  71.8 14.4 %copy-start.53 = (f32[28]{0:T(128)S(1)}, f32[28]{0:T(128)}, u32[]{:S(2)}) copy-start(f32[28]{0:T(128)} %get-tuple-element.20) | copy-start | bytes 340
  71.8 14.4 %copy-start.54 = (f32[28]{0:T(128)S(1)}, f32[28]{0:T(128)}, u32[]{:S(2)}) copy-start(f32[28]{0:T(128)} %get-tuple-element.21) | copy-start | bytes 340
  71.8 14.4 %copy-start.55 = (f32[28]{0:T(128)S(1)}, f32[28]{0:T(128)}, u32[]{:S(2)}) copy-start(f32[28]{0:T(128)} %get-tuple-element.23) | copy-start | bytes 340
  72.6 13.6 %collective-permute-start.11 = (bf16[28,4224]{1,0:T(8,128)(2,1)S(1)}, bf16[28,4224]{1,0:T(8,128)(2,1)S(1)}, u32[]{:S(2)}, u32[]{:S(2)}) collective-permute-start(bf16[28,4224]{1,0:T(8,128)(2,1)S(1)} %concatenate.38), channel_id=1, source_target_pairs={{0,8},{2,10},{4,12},{6,14},{8,0},{10,2},{12,4},{14,6},{1,9},{3,11}... | collective-permute-start | bytes 709640 | tf_op jit(solution)/shard_map/ppermute | solution.py:163
  79.0 11.9 %copy-start.24 = (f32[128,128]{1,0:T(8,128)}, f32[128,128]{1,0:T(8,128)S(1)}, u32[]{:S(2)}) copy-start(f32[128,128]{1,0:T(8,128)S(1)} %fusion.92) | copy-start | bytes 196612
  100.1 8.0 %copy-start.22 = (f32[28,64]{1,0:T(8,128)S(1)}, f32[28,64]{1,0:T(8,128)}, u32[]{:S(2)}) copy-start(f32[28,64]{1,0:T(8,128)} %reshape_squeeze.10) | copy-start | bytes 21508
  100.1 8.0 %copy-start.25 = (f32[128,128]{1,0:T(8,128)S(1)}, f32[128,128]{1,0:T(8,128)}, u32[]{:S(2)}) copy-start(f32[128,128]{1,0:T(8,128)} %copy-done.24) | copy-start | bytes 196612
  100.1 8.0 %copy-start.27 = (f32[128,128]{1,0:T(8,128)S(1)}, f32[128,128]{1,0:T(8,128)}, u32[]{:S(2)}) copy-start(f32[128,128]{1,0:T(8,128)} %get-tuple-element.70) | copy-start | bytes 196612
  104.4 3.7 %collective-permute-start.21 = (f32[1876]{0:T(1024)S(1)}, f32[1876]{0:T(1024)S(1)}, u32[]{:S(2)}, u32[]{:S(2)}) collective-permute-start(f32[1876]{0:T(1024)S(1)} %concatenate.42), channel_id=1, source_target_pairs={{0,2},{2,0},{4,6},{6,4},{8,10},{10,8},{12,14},{14,12},{1,3},{3,1},... | collective-permute-start | bytes 22520 | tf_op jit(solution)/shard_map/ppermute | solution.py:38
  105.6 10.7 %collective-permute-start.12 = (bf16[128,128]{0,1:T(8,128)(2,1)S(1)}, bf16[128,128]{0,1:T(8,128)(2,1)S(1)}, u32[]{:S(2)}, u32[]{:S(2)}) collective-permute-start(bf16[128,128]{0,1:T(8,128)(2,1)S(1)} %add_convert_fusion), channel_id=1, source_target_pairs={{0,1},{1,0},{2,3},{3,2},{4,5},{5,4},{6,7},{7,6},{8,9},{9,8},{10,11... | collective-permute-start | bytes 98312 | tf_op jit(solution)/shard_map/ppermute | solution.py:29
  108.1 3.7 %collective-permute-start.22 = (f32[1876]{0:T(1024)S(1)}, f32[1876]{0:T(1024)S(1)}, u32[]{:S(2)}, u32[]{:S(2)}) collective-permute-start(f32[1876]{0:T(1024)S(1)} %add.271), channel_id=1, source_target_pairs={{0,4},{2,6},{4,0},{6,2},{8,12},{10,14},{12,8},{14,10},{1,5},{3,7},... | collective-permute-start | bytes 22520 | tf_op jit(solution)/shard_map/ppermute | solution.py:38
  111.7 4.5 %collective-permute-start.23 = (f32[1876]{0:T(1024)S(1)}, f32[1876]{0:T(1024)S(1)}, u32[]{:S(2)}, u32[]{:S(2)}) collective-permute-start(f32[1876]{0:T(1024)S(1)} %add.272), channel_id=1, source_target_pairs={{0,8},{2,10},{4,12},{6,14},{8,0},{10,2},{12,4},{14,6},{1,9},{3,11}... | collective-permute-start | bytes 22520 | tf_op jit(solution)/shard_map/ppermute | solution.py:38
  116.3 20.7 %copy-start.3 = (bf16[256,1792]{1,0:T(8,128)(2,1)S(1)}, bf16[256,1792]{1,0:T(8,128)(2,1)}, u32[]{:S(2)}) copy-start(bf16[256,1792]{1,0:T(8,128)(2,1)} %copy-done.2) | copy-start | bytes 2752516
  118.2 8.1 %collective-permute-start.20 = (bf16[32,1792]{1,0:T(8,128)(2,1)S(1)}, bf16[32,1792]{1,0:T(8,128)(2,1)S(1)}, u32[]{:S(2)}, u32[]{:S(2)}) collective-permute-start(bf16[32,1792]{1,0:T(8,128)(2,1)S(1)} %get-tuple-element.49), channel_id=1, source_target_pairs={{0,14},{2,0},{4,2},{6,4},{8,6},{10,8},{12,10},{14,12},{1,15},{3,1}... | collective-permute-start | bytes 344072 | tf_op jit(solution)/shard_map/ppermute | solution.py:18
  119.2 8.3 %collective-permute-start.19 = (bf16[32,1792]{1,0:T(8,128)(2,1)S(1)}, bf16[32,1792]{1,0:T(8,128)(2,1)S(1)}, u32[]{:S(2)}, u32[]{:S(2)}) collective-permute-start(bf16[32,1792]{1,0:T(8,128)(2,1)S(1)} %get-tuple-element.50), channel_id=1, source_target_pairs={{0,12},{2,14},{4,0},{6,2},{8,4},{10,6},{12,8},{14,10},{1,13},{3,15... | collective-permute-start | bytes 344072 | tf_op jit(solution)/shard_map/ppermute | solution.py:18
  122.5 15.7 %collective-permute-start.18 = (bf16[32,1792]{1,0:T(8,128)(2,1)S(1)}, bf16[32,1792]{1,0:T(8,128)(2,1)S(1)}, u32[]{:S(2)}, u32[]{:S(2)}) collective-permute-start(bf16[32,1792]{1,0:T(8,128)(2,1)S(1)} %get-tuple-element.51), channel_id=1, source_target_pairs={{0,10},{2,12},{4,14},{6,0},{8,2},{10,4},{12,6},{14,8},{1,11},{3,13... | collective-permute-start | bytes 344072 | tf_op jit(solution)/shard_map/ppermute | solution.py:18
  123.6 15.9 %collective-permute-start.17 = (bf16[32,1792]{1,0:T(8,128)(2,1)S(1)}, bf16[32,1792]{1,0:T(8,128)(2,1)S(1)}, u32[]{:S(2)}, u32[]{:S(2)}) collective-permute-start(bf16[32,1792]{1,0:T(8,128)(2,1)S(1)} %get-tuple-element.52), channel_id=1, source_target_pairs={{0,8},{2,10},{4,12},{6,14},{8,0},{10,2},{12,4},{14,6},{1,9},{3,11}... | collective-permute-start | bytes 344072 | tf_op jit(solution)/shard_map/ppermute | solution.py:18
  126.0 13.5 %collective-permute-start.16 = (bf16[32,1792]{1,0:T(8,128)(2,1)S(1)}, bf16[32,1792]{1,0:T(8,128)(2,1)S(1)}, u32[]{:S(2)}, u32[]{:S(2)}) collective-permute-start(bf16[32,1792]{1,0:T(8,128)(2,1)S(1)} %get-tuple-element.53), channel_id=1, source_target_pairs={{0,6},{2,8},{4,10},{6,12},{8,14},{10,0},{12,2},{14,4},{1,7},{3,9},... | collective-permute-start | bytes 344072 | tf_op jit(solution)/shard_map/ppermute | solution.py:18
  126.3 13.1 %collective-permute-start.15 = (bf16[32,1792]{1,0:T(8,128)(2,1)S(1)}, bf16[32,1792]{1,0:T(8,128)(2,1)S(1)}, u32[]{:S(2)}, u32[]{:S(2)}) collective-permute-start(bf16[32,1792]{1,0:T(8,128)(2,1)S(1)} %get-tuple-element.54), channel_id=1, source_target_pairs={{0,4},{2,6},{4,8},{6,10},{8,12},{10,14},{12,0},{14,2},{1,5},{3,7},... | collective-permute-start | bytes 344072 | tf_op jit(solution)/shard_map/ppermute | solution.py:18
  127.5 12.0 %collective-permute-start.14 = (bf16[32,1792]{1,0:T(8,128)(2,1)S(1)}, bf16[32,1792]{1,0:T(8,128)(2,1)S(1)}, u32[]{:S(2)}, u32[]{:S(2)}) collective-permute-start(bf16[32,1792]{1,0:T(8,128)(2,1)S(1)} %get-tuple-element.48), channel_id=1, source_target_pairs={{0,2},{2,4},{4,6},{6,8},{8,10},{10,12},{12,14},{14,0},{1,3},{3,5},... | collective-permute-start | bytes 344072 | tf_op jit(solution)/shard_map/ppermute | solution.py:18
  138.1 10.9 %collective-permute-start.13 = (bf16[1,128,1792]{2,1,0:T(8,128)(2,1)S(1)}, bf16[1,128,1792]{2,1,0:T(8,128)(2,1)S(1)}, u32[]{:S(2)}, u32[]{:S(2)}) collective-permute-start(bf16[1,128,1792]{2,1,0:T(8,128)(2,1)S(1)} %fusion.1), channel_id=1, source_target_pairs={{16,0},{17,1},{18,2},{19,3},{20,4},{21,5},{22,6},{23,7},{24,8},{25... | collective-permute-start | bytes 1376264 | tf_op jit(solution)/shard_map/ppermute | solution.py:12
  (41 other events, 130.0 us)

commit v5 on v4

--- a/solution.py
+++ b/solution.py
@@ -27,17 +27,6 @@
 
 def swap_heads(block):
     return lax.ppermute(block, "head", [(0, 1), (1, 0)])
-
-
-def seq_total(value):
-    size = lax.axis_size("seq")
-    if size & (size - 1):
-        return lax.psum(value, "seq")
-    distance = 1
-    while distance < size:
-        value = value + lax.ppermute(value, "seq", [(i, i ^ distance) for i in range(size)])
-        distance *= 2
-    return value
 
 
 def contract(spec, left, right):
@@ -129,12 +118,13 @@
     return near_state
 
 
-def both_scans(decay, state, state_grad, axis):
+def both_scans(decay, state, state_grad, axis, filler_fn, filler_args):
     size, mine = (lax.axis_size(axis), lax.axis_index(axis))
     if size & (size - 1):
         return (
             scan_rounds(decay, state, axis, True),
             scan_rounds(decay, state_grad, axis, False),
+            filler_fn(*filler_args),
         )
     width = state.shape[1]
     total_decay = decay
@@ -152,6 +142,8 @@
             [total_fwd, total_bwd, high[:, None], low[:, None], pad], axis=1
         ).astype(jnp.bfloat16)
         upper = (mine // distance) % 2 == 1
+        if distance == 1:
+            payload, filler_args = lax.optimization_barrier((payload, filler_args))
         if distance * 2 < size:
             got = lax.ppermute(payload, axis, [(i, i ^ distance) for i in range(size)])
             got = got.astype(jnp.float32)
@@ -165,6 +157,8 @@
             got_fwd = got[:, :width]
             got_bwd = got_fwd
             got = jnp.concatenate([got[:, :width], got], axis=1)
+        if distance == 1:
+            got, filler = lax.optimization_barrier((got, filler_fn(*filler_args)))
         got_decay = got[:, 2 * width] + got[:, 2 * width + 1]
         before = jnp.where(upper, before + before_decay[:, None] * got_fwd, before)
         before_decay = jnp.where(upper, before_decay * got_decay, before_decay)
@@ -183,7 +177,7 @@
             )
             total_decay = total_decay * got_decay
         distance *= 2
-    return (before, after)
+    return (before, after, filler)
 
 
 def shards(bwd_input, bwd_docs, bwd_grad, proj_weight, step_weight, step_bias, rate_log, skip_gain):
@@ -233,9 +227,9 @@
     def local_bwd(values_in, mixer_in, weight_in, bias_in, rate_in, skip_in):
         return span_local(values_in, mixer_in, weight_in, bias_in, rate_in, skip_in, docs_bwd)
 
-    local_grads = jax.vjp(
-        local_bwd, bwd_values, mixer_bwd, weight_heads, bias_heads, rate_heads, skip_heads
-    )[1](out_ct)
+    def local_pull(*primals):
+        return jax.vjp(local_bwd, *primals[:-1])[1](primals[-1])
+
 
     def carry_bwd(values_in, mixer_in, weight_in, bias_in, rate_in, state_in):
         return span_carry(
@@ -247,7 +241,14 @@
 
     state_grad = jax.vjp(carried_only, jnp.zeros(state_shape, jnp.float32))[1](out_ct)[0]
     state_grad = state_grad.reshape(heads_here, -1)
-    incoming_flat, adjoint_flat = both_scans(decay_bwd, state_flat, state_grad, "seq")
+    incoming_flat, adjoint_flat, local_grads = both_scans(
+        decay_bwd,
+        state_flat,
+        state_grad,
+        "seq",
+        local_pull,
+        (bwd_values, mixer_bwd, weight_heads, bias_heads, rate_heads, skip_heads, out_ct),
+    )
     incoming_bwd = incoming_flat.reshape(state_shape)
     carry_grads = jax.vjp(
         carry_bwd, bwd_values, mixer_bwd, weight_heads, bias_heads, rate_heads, incoming_bwd
@@ -283,11 +284,6 @@
     row_parts = lax.dot_general(
         dest_grad, bwd_flat, (((0,), (0,)), ((), ())), preferred_element_type=jnp.float32
     ).reshape(size, -1, channels_here)
-    grad_rows = row_parts[0]
-    for k in range(1, size):
-        grad_rows = grad_rows + rotated(row_parts[k].astype(jnp.bfloat16), "seq", k).astype(
-            jnp.float32
-        )
     small = jnp.concatenate(
         [
             (out_grads[2] + sum_grads[2]).reshape(channels_here),
@@ -296,12 +292,32 @@
             out_grads[5],
         ]
     )
-    small = seq_total(small)
+    small_rows = -(-small.shape[0] // channels_here)
+    small = jnp.pad(small, (0, small_rows * channels_here - small.shape[0]))
+    small = small.reshape(small_rows, channels_here)
+    small_high = small.astype(jnp.bfloat16)
+    small_low = (small - small_high.astype(jnp.float32)).astype(jnp.bfloat16)
+    small_coded = jnp.concatenate([small_high, small_low], axis=0)
+    block_rows = row_parts.shape[1]
+    grad_rows = row_parts[0]
+    small_slots = [small_coded]
+    for k in range(1, size):
+        message = jnp.concatenate([row_parts[k].astype(jnp.bfloat16), small_coded], axis=0)
+        got = rotated(message, "seq", k)
+        grad_rows = grad_rows + got[:block_rows].astype(jnp.float32)
+        small_slots.append(got[block_rows:])
+    small_slots = jnp.stack(small_slots[::-1])
+    small_slots = roll_blocks(small_slots, mine + 1, size, 0).astype(jnp.float32)
+    small_parts = small_slots[:, :small_rows] + small_slots[:, small_rows:]
+    small_total = small_parts[0]
+    for j in range(1, size):
+        small_total = small_total + small_parts[j]
+    small = small_total.reshape(-1)
     totals = (
         small[:channels_here],
         small[channels_here : channels_here + heads_here],
         small[channels_here + heads_here : channels_here + 2 * heads_here],
-        small[channels_here + 2 * heads_here :],
+        small[channels_here + 2 * heads_here : channels_here + 3 * heads_here],
     )
     return (
         prev_part,

time: 150 us -> 145 us (0.967)
  other arithmetic: 18.3 us -> 14 us
  matrix products: 18.4 us -> 16.6 us
    ppermute x3 -> x0, waiting for transfers between devices: 8.44 us -> none  [seq_total(): lax.ppermute(value, 'seq', [(i, i ^ distance) for i in range(size)])]
    ppermute x14, waiting for transfers between devices: 6.48 us -> 11.7 us  [rotated(): return lax.ppermute(block, axis, route)]
    ppermute x1, waiting for transfers between devices: 7.11 us -> 12.3 us  [both_scans(): got = lax.ppermute(last, axis, [(i, i ^ distance) for i in range(size)])]
    reduce_sum x2 -> x1, other arithmetic: 2.91 us -> 0.3 us  [span_local(): values.astype(jnp.float32) * (1.0 + skip_gain)[None, :, None] + local_part]
    dot_general x5, matrix products: 5.17 us -> 6.82 us  [contract(): return jnp.einsum(spec, left, right, preferred_element_type=jnp.float32)]
    concatenate x0 -> x2, other arithmetic: none -> 1.6 us  [shards(): jnp.concatenate([row_parts[k].astype(jnp.bfloat16), small_coded], axis=0)]
    dot_general x4 -> x5, matrix products: 2.98 us -> 3.41 us  [local_setup(): jnp.einsum('thp,hp->th', values.astype(jnp.float32), step_weight, precisi...]
    unnamed x140 -> x144, local copies, waits for them, and re-layouts: 4.57 us -> 4.32 us
  transfers between devices with their start and end apart: 24 -> 21, of which waited for: 13 -> 11; matrix products, arithmetic and copies ran while one was open for 14% -> 15% of each run, Pallas kernels for 0% -> 0%
where the time goes in v5:
time: 145 us; the launch traced here: 144 us
  waiting for transfers between devices  57.4 us (40%)
  starting transfers between devices  36.1 us (25%)
  local copies, waits for them, and re-layouts  16.6 us (11%)
  matrix products  16.6 us (11%)
  other arithmetic  14 us (10%)
  between operations  3.31 us (2%)
    ppermute x14, starting transfers between devices, rotated(): return lax.ppermute(block, axis, route)  29.5 us
    ppermute x2, waiting for transfers between devices, both_scans(): got = lax.ppermute(payload, axis, [(i, i ^ distance) for i in range(size)])  26.4 us
    ppermute x1, waiting for transfers between devices, both_scans(): got = lax.ppermute(last, axis, [(i, i ^ distance) for i in range(size)])  12.3 us
    ppermute x14, waiting for transfers between devices, rotated(): return lax.ppermute(block, axis, route)  11.7 us
    ppermute x2, waiting for transfers between devices, shifted(): return lax.ppermute(block, axis, route)  7 us
    dot_general x5, matrix products, contract(): return jnp.einsum(spec, left, right, preferred_element_type=jnp.float32)  6.82 us
    ppermute x2, starting transfers between devices, shifted(): return lax.ppermute(block, axis, route)  5.6 us
    unnamed x144, local copies, waits for them, and re-layouts  4.32 us
  transfers between devices with their start and end apart: 21, of which 11 were waited for; matrix products, arithmetic and copies ran while one was open for 15% of the time, Pallas kernels for 0%

profile of v5, /device:TPU:4, one launch (start us, length us, event | category | flops | bytes accessed | tf_op | source)
XLA Modules:
  0.0 144.0 jit_solution(4404183748659384933)
XLA Ops:
  0.7 1.6 %collective-permute-start = (bf16[32,1792]{1,0:T(8,128)(2,1)}, bf16[32,1792]{1,0:T(8,128)(2,1)S(1)}, u32[]{:S(2)}, u32[]{:S(2)}) collective-permute-start(bf16[32,1792]{1,0:T(8,128)(2,1)} %bitcast.349), channel_id=1, source_target_pairs={{0,2},{2,4},{4,6},{6,8},{8,10},{10,12},{12,14},{14,0},{1,3},{3,5},... | collective-permute-start | bytes 344072 | tf_op jit(solution)/shard_map/ppermute | solution.py:18
  2.2 1.6 %collective-permute-start.1 = (bf16[32,1792]{1,0:T(8,128)(2,1)}, bf16[32,1792]{1,0:T(8,128)(2,1)S(1)}, u32[]{:S(2)}, u32[]{:S(2)}) collective-permute-start(bf16[32,1792]{1,0:T(8,128)(2,1)} %bitcast.350), channel_id=1, source_target_pairs={{0,4},{2,6},{4,8},{6,10},{8,12},{10,14},{12,0},{14,2},{1,5},{3,7},... | collective-permute-start | bytes 344072 | tf_op jit(solution)/shard_map/ppermute | solution.py:18
  3.8 2.5 %collective-permute-start.2 = (bf16[32,1792]{1,0:T(8,128)(2,1)}, bf16[32,1792]{1,0:T(8,128)(2,1)S(1)}, u32[]{:S(2)}, u32[]{:S(2)}) collective-permute-start(bf16[32,1792]{1,0:T(8,128)(2,1)} %bitcast.351), channel_id=1, source_target_pairs={{0,6},{2,8},{4,10},{6,12},{8,14},{10,0},{12,2},{14,4},{1,7},{3,9},... | collective-permute-start | bytes 344072 | tf_op jit(solution)/shard_map/ppermute | solution.py:18
  6.7 1.2 slice.180
  7.9 4.3 %collective-permute-start.8 = (s32[1]{0:T(128)}, s32[1]{0:T(128)}, u32[]{:S(2)}, u32[]{:S(2)}) collective-permute-start(s32[1]{0:T(128)} %bitcast.13), channel_id=1, source_target_pairs={{0,2},{2,4},{4,6},{6,8},{8,10},{10,12},{12,14},{1,3},{3,5},{5,7},{... | collective-permute-start | bytes 20 | tf_op jit(solution)/shard_map/ppermute | solution.py:12
  12.2 0.9 constant_dynamic-update-slice_fusion.7
  13.2 0.7 reduce
  14.6 1.3 copy.66
  16.9 1.1 convert.61
  17.9 0.7 broadcast_compare_fusion
  18.6 1.3 collective-permute-start.4
  19.9 1.3 broadcast_compare_fusion.1
  23.5 3.1 %collective-permute-start.5 = (bf16[32,1792]{1,0:T(8,128)(2,1)S(1)}, bf16[32,1792]{1,0:T(8,128)(2,1)S(1)}, u32[]{:S(2)}, u32[]{:S(2)}) collective-permute-start(bf16[32,1792]{1,0:T(8,128)(2,1)S(1)} %bitcast.354), channel_id=1, source_target_pairs={{0,12},{2,14},{4,0},{6,2},{8,4},{10,6},{12,8},{14,10},{1,13},{3,15... | collective-permute-start | bytes 344072 | tf_op jit(solution)/shard_map/ppermute | solution.py:18
  27.5 1.5 %collective-permute-done.5 = bf16[32,1792]{1,0:T(8,128)(2,1)S(1)} collective-permute-done((bf16[32,1792]{1,0:T(8,128)(2,1)S(1)}, bf16[32,1792]{1,0:T(8,128)(2,1)S(1)}, u32[]{:S(2)}, u32[]{:S(2)}) %collective-permute-start.5) | collective-permute-done | bytes 114720 | tf_op jit(solution)/shard_map/ppermute | solution.py:18
  29.0 3.4 %collective-permute-done.6 = bf16[32,1792]{1,0:T(8,128)(2,1)S(1)} collective-permute-done((bf16[32,1792]{1,0:T(8,128)(2,1)S(1)}, bf16[32,1792]{1,0:T(8,128)(2,1)S(1)}, u32[]{:S(2)}, u32[]{:S(2)}) %collective-permute-start.6) | collective-permute-done | bytes 114720 | tf_op jit(solution)/shard_map/ppermute | solution.py:18
  33.5 0.7 copy.74
  34.3 0.7 copy.72
  35.0 0.7 copy.73
  37.2 1.2 copy.71
  38.4 1.6 %reshape.295 = f32[28,4096]{1,0:T(8,128)S(1)} reshape(f32[28,64,64]{2,1,0:T(8,128)} %copy.71) | data formatting | bytes 917504 | tf_op jit(solution)/shard_map/reshape | solution.py:243
  40.1 1.1 concatenate.71
  42.6 2.8 %fusion.12 = (f32[28,128]{1,0:T(8,128)S(1)}, f32[28,128]{1,0:T(8,128)S(1)}, f32[28,128]{1,0:T(8,128)S(1)}, bf16[128,128]{1,0:T(8,128)(2,1)S(1)}) fusion(f32[28,128]{1,0:T(8,128)S(1)} %fusion.114, f32[128,128]{1,0:T(8,128)S(1)} %fusion.100, f32[128,128]{1,0:T(8,128)} %get-tuple-element.106, f32[28,128]{1,0:T(8,128)S(1)} %fusion.74, ...), kind=kOutput, calls=%fused_computation.18 | convolution fusion | flops 66033152 | bytes 1628160 | tf_op jit(solution)/shard_map/transpose(jvp(hts,shp->thp))/dot_general | solution.py:33
  46.0 0.8 fusion.104
  47.0 1.8 %fusion.17 = bf16[128,28,64]{0,2,1:T(8,128)(2,1)} fusion(f32[128,28,64]{0,2,1:T(8,128)S(1)} %copy-done.8, f32[28,128]{1,0:T(8,128)S(1)} %fusion.114, f32[128,128]{1,0:T(8,128)S(1)} %fusion.100, f32[128,128]{1,0:T(8,128)S(1)} %copy-done.33, f32[28,128]{1,0:T(8,128)S(1)} %fusion.74, pred[128,128]{1,0:T(8,128)(4,1)S(1)} %copy-done.40, ...), kind=kOutput, calls=%fused_computation.27 | convolution fusion | flops 63078400 | bytes 1574000 | tf_op jit(solution)/shard_map/transpose(jvp(hts,shp->thp))/dot_general | solution.py:33
  48.8 12.6 %collective-permute-done.9 = bf16[28,8320]{1,0:T(8,128)(2,1)S(1)} collective-permute-done((bf16[28,8320]{1,0:T(8,128)(2,1)S(1)}, bf16[28,8320]{1,0:T(8,128)(2,1)S(1)}, u32[]{:S(2)}, u32[]{:S(2)}) %collective-permute-start.9) | collective-permute-done | bytes 465952 | tf_op jit(solution)/shard_map/ppermute | solution.py:148
  62.5 13.7 %collective-permute-done.10 = bf16[28,8320]{1,0:T(8,128)(2,1)} collective-permute-done((bf16[28,8320]{1,0:T(8,128)(2,1)S(1)}, bf16[28,8320]{1,0:T(8,128)(2,1)}, u32[]{:S(2)}, u32[]{:S(2)}) %collective-permute-start.10) | collective-permute-done | bytes 465952 | tf_op jit(solution)/shard_map/ppermute | solution.py:148
  76.2 1.1 convert_element_type.289
  78.2 0.7 collective-permute-start.11
  78.9 1.0 bitcast_multiply_fusion
  79.9 12.3 %collective-permute-done.11 = bf16[28,4224]{1,0:T(8,128)(2,1)} collective-permute-done((bf16[28,4224]{1,0:T(8,128)(2,1)S(1)}, bf16[28,4224]{1,0:T(8,128)(2,1)}, u32[]{:S(2)}, u32[]{:S(2)}) %collective-permute-start.11) | collective-permute-done | bytes 236576 | tf_op jit(solution)/shard_map/ppermute | solution.py:155
  92.2 1.4 multiply_reduce_fusion.4
  97.0 0.8 fusion.131
  97.9 0.8 fusion.132
  99.0 1.0 fusion.22
  100.3 1.6 %fusion.21 = f32[128,28,64]{0,2,1:T(8,128)S(1)} fusion(bf16[28,64,64]{2,1,0:T(8,128)(2,1)S(1)} %copy-done.20, bf16[128,28,64]{0,2,1:T(8,128)(2,1)} %fusion.17, f32[28,128]{1,0:T(8,128)S(1)} %copy.82, f32[28,64]{1,0:T(8,128)S(1)} %copy-done.39, f32[28,128]{1,0:T(8,128)S(1)} %copy.77, f32[128,64]{0,1:T(8,128)S(1)} %copy-done.26, f32[128,28]{0,1:T(8,128)S(1)} %copy-done.31), kind=kOutput, calls=%fused_computation.31 | convolution fusion | flops 32112640 | bytes 1688576 | tf_op jit(solution)/shard_map/transpose(jvp(thn,thp->hnp))/dot_general | solution.py:33
  102.2 1.8 %fusion.126 = (bf16[256,1792]{1,0:T(8,128)(2,1)S(1)}, f32[256,1792]{1,0:T(8,128)}) fusion(bf16[1,128,1792]{2,1,0:T(8,128)(2,1)S(1)} %copy-done.7, s32[]{:T(128)S(6)} %select_n.220, bf16[128,256]{0,1:T(8,128)(2,1)S(1)} %maximum_select_fusion), kind=kOutput, calls=%fused_computation.281 | convolution fusion | flops 118030336 | bytes 3276804 | tf_op jit(solution)/shard_map/dot_general | solution.py:284
  104.1 0.9 pad_maximum_fusion.6
  105.0 1.8 %collective-permute-start.19 = (bf16[36,1792]{1,0:T(8,128)(2,1)}, bf16[36,1792]{1,0:T(8,128)(2,1)S(1)}, u32[]{:S(2)}, u32[]{:S(2)}) collective-permute-start(bf16[36,1792]{1,0:T(8,128)(2,1)} %get-tuple-element.102), channel_id=1, source_target_pairs={{0,12},{2,14},{4,0},{6,2},{8,4},{10,6},{12,8},{14,10},{1,13},{3,15... | collective-permute-start | bytes 387080 | tf_op jit(solution)/shard_map/ppermute | solution.py:18
  107.5 0.7 collective-permute-start.20
  108.4 3.5 %collective-permute-start.17 = (bf16[36,1792]{1,0:T(8,128)(2,1)}, bf16[36,1792]{1,0:T(8,128)(2,1)S(1)}, u32[]{:S(2)}, u32[]{:S(2)}) collective-permute-start(bf16[36,1792]{1,0:T(8,128)(2,1)} %get-tuple-element.100), channel_id=1, source_target_pairs={{0,8},{2,10},{4,12},{6,14},{8,0},{10,2},{12,4},{14,6},{1,9},{3,11}... | collective-permute-start | bytes 387080 | tf_op jit(solution)/shard_map/ppermute | solution.py:18
  112.7 2.6 %collective-permute-done.20 = bf16[36,1792]{1,0:T(8,128)(2,1)S(1)} collective-permute-done((bf16[36,1792]{1,0:T(8,128)(2,1)}, bf16[36,1792]{1,0:T(8,128)(2,1)S(1)}, u32[]{:S(2)}, u32[]{:S(2)}) %collective-permute-start.20) | collective-permute-done | bytes 129056 | tf_op jit(solution)/shard_map/ppermute | solution.py:18
  115.3 12.4 %collective-permute-start.15 = (bf16[36,1792]{1,0:T(8,128)(2,1)S(1)}, bf16[36,1792]{1,0:T(8,128)(2,1)S(1)}, u32[]{:S(2)}, u32[]{:S(2)}) collective-permute-start(bf16[36,1792]{1,0:T(8,128)(2,1)S(1)} %copy-done.22), channel_id=1, source_target_pairs={{0,4},{2,6},{4,8},{6,10},{8,12},{10,14},{12,0},{14,2},{1,5},{3,7},... | collective-permute-start | bytes 387080 | tf_op jit(solution)/shard_map/ppermute | solution.py:18
  127.8 2.4 %collective-permute-done.18 = bf16[36,1792]{1,0:T(8,128)(2,1)S(1)} collective-permute-done((bf16[36,1792]{1,0:T(8,128)(2,1)}, bf16[36,1792]{1,0:T(8,128)(2,1)S(1)}, u32[]{:S(2)}, u32[]{:S(2)}) %collective-permute-start.18) | collective-permute-done | bytes 129056 | tf_op jit(solution)/shard_map/ppermute | solution.py:18
  130.2 1.3 collective-permute-start.13
  132.2 0.7 collective-permute-done.14
  133.3 1.8 %fusion.51 = f32[1,32,1792]{2,1,0:T(8,128)} fusion(f32[256,1792]{1,0:T(8,128)} %get-tuple-element.111, bf16[36,1792]{1,0:T(8,128)(2,1)S(1)} %collective-permute-done.20, bf16[36,1792]{1,0:T(8,128)(2,1)S(1)} %collective-permute-done.19, bf16[36,1792]{1,0:T(8,128)(2,1)S(1)} %collective-permute-done.18, bf16[36,1792]{1,0:T(8,128)(2,1)S(1)} %collective-permute-done.17, ...), kind=kLoop, calls=%fused_computation.104 | loop fusion | flops 802816 | bytes 1261568 | tf_op jit(solution)/shard_map/broadcast_in_dim | solution.py:324
  136.2 7.0 %collective-permute-done.13 = bf16[1,128,1792]{2,1,0:T(8,128)(2,1)S(1)} collective-permute-done((bf16[1,128,1792]{2,1,0:T(8,128)(2,1)S(1)}, bf16[1,128,1792]{2,1,0:T(8,128)(2,1)S(1)}, u32[]{:S(2)}, u32[]{:S(2)}) %collective-permute-start.13) | collective-permute-done | bytes 458784 | tf_op jit(solution)/shard_map/ppermute | solution.py:12
  143.2 0.8 copy.145
  (248 shorter events, 17.9 us)
Async XLA Ops:
  0.6 15.9 %copy-start.51 = (f32[1,28]{1,0:T(1,128)S(1)}, f32[1,28]{1,0:T(1,128)}, u32[]{:S(2)}) copy-start(f32[1,28]{1,0:T(1,128)} %param.15) | copy-start | bytes 340
  0.6 15.9 %copy-start.18 = (bf16[1,128,1792]{2,1,0:T(8,128)(2,1)S(1)}, bf16[1,128,1792]{2,1,0:T(8,128)(2,1)}, u32[]{:S(2)}) copy-start(bf16[1,128,1792]{2,1,0:T(8,128)(2,1)} %param.11) | copy-start | bytes 1376260
  0.7 22.9 %collective-permute-start = (bf16[32,1792]{1,0:T(8,128)(2,1)}, bf16[32,1792]{1,0:T(8,128)(2,1)S(1)}, u32[]{:S(2)}, u32[]{:S(2)}) collective-permute-start(bf16[32,1792]{1,0:T(8,128)(2,1)} %bitcast.349), channel_id=1, source_target_pairs={{0,2},{2,4},{4,6},{6,8},{8,10},{10,12},{12,14},{14,0},{1,3},{3,5},... | collective-permute-start | bytes 344072 | tf_op jit(solution)/shard_map/ppermute | solution.py:18
  2.2 24.4 %collective-permute-start.1 = (bf16[32,1792]{1,0:T(8,128)(2,1)}, bf16[32,1792]{1,0:T(8,128)(2,1)S(1)}, u32[]{:S(2)}, u32[]{:S(2)}) collective-permute-start(bf16[32,1792]{1,0:T(8,128)(2,1)} %bitcast.350), channel_id=1, source_target_pairs={{0,4},{2,6},{4,8},{6,10},{8,12},{10,14},{12,0},{14,2},{1,5},{3,7},... | collective-permute-start | bytes 344072 | tf_op jit(solution)/shard_map/ppermute | solution.py:18
  3.8 23.1 %collective-permute-start.2 = (bf16[32,1792]{1,0:T(8,128)(2,1)}, bf16[32,1792]{1,0:T(8,128)(2,1)S(1)}, u32[]{:S(2)}, u32[]{:S(2)}) collective-permute-start(bf16[32,1792]{1,0:T(8,128)(2,1)} %bitcast.351), channel_id=1, source_target_pairs={{0,6},{2,8},{4,10},{6,12},{8,14},{10,0},{12,2},{14,4},{1,7},{3,9},... | collective-permute-start | bytes 344072 | tf_op jit(solution)/shard_map/ppermute | solution.py:18
  6.3 20.6 %collective-permute-start.3 = (bf16[32,1792]{1,0:T(8,128)(2,1)}, bf16[32,1792]{1,0:T(8,128)(2,1)S(1)}, u32[]{:S(2)}, u32[]{:S(2)}) collective-permute-start(bf16[32,1792]{1,0:T(8,128)(2,1)} %bitcast.352), channel_id=1, source_target_pairs={{0,8},{2,10},{4,12},{6,14},{8,0},{10,2},{12,4},{14,6},{1,9},{3,11}... | collective-permute-start | bytes 344072 | tf_op jit(solution)/shard_map/ppermute | solution.py:18
  7.9 10.7 %collective-permute-start.8 = (s32[1]{0:T(128)}, s32[1]{0:T(128)}, u32[]{:S(2)}, u32[]{:S(2)}) collective-permute-start(s32[1]{0:T(128)} %bitcast.13), channel_id=1, source_target_pairs={{0,2},{2,4},{4,6},{6,8},{8,10},{10,12},{12,14},{1,3},{3,5},{5,7},{... | collective-permute-start | bytes 20 | tf_op jit(solution)/shard_map/ppermute | solution.py:12
  14.6 4.0 %copy-start.27 = (bf16[1,32,1792]{2,1,0:T(8,128)(2,1)S(1)}, bf16[1,32,1792]{2,1,0:T(8,128)(2,1)}, u32[]{:S(2)}) copy-start(bf16[1,32,1792]{2,1,0:T(8,128)(2,1)} %param.12) | copy-start | bytes 344068
  14.6 7.9 %copy-start.41 = (f32[1,28]{1,0:T(1,128)S(1)}, f32[1,28]{1,0:T(1,128)}, u32[]{:S(2)}) copy-start(f32[1,28]{1,0:T(1,128)} %param.14) | copy-start | bytes 340
  15.9 30.1 %copy-start.4 = (bf16[1,128,1792]{1,2,0:T(8,128)(2,1)}, bf16[1,128,1792]{1,2,0:T(8,128)(2,1)S(1)}, u32[]{:S(2)}) copy-start(bf16[1,128,1792]{1,2,0:T(8,128)(2,1)S(1)} %copy.66) | copy-start | bytes 1376260
  16.5 10.4 %copy-start.15 = (f32[28,1,128]{0,2,1:T(8,128)}, f32[28,1,128]{0,2,1:T(8,128)S(1)}, u32[]{:S(2)}) copy-start(f32[28,1,128]{0,2,1:T(8,128)S(1)} %copy.87) | copy-start | bytes 43012
  16.6 6.2 %copy-start.58 = (f32[28]{0:T(128)}, f32[28]{0:T(128)S(1)}, u32[]{:S(2)}) copy-start(f32[28]{0:T(128)S(1)} %negate_bitcast_fusion) | copy-start | bytes 340
  16.8 15.6 %copy-start.6 = (bf16[1,128,1792]{2,1,0:T(8,128)(2,1)S(1)}, bf16[1,128,1792]{2,1,0:T(8,128)(2,1)}, u32[]{:S(2)}) copy-start(bf16[1,128,1792]{2,1,0:T(8,128)(2,1)} %param.9) | copy-start | bytes 1376260
  18.6 8.8 %collective-permute-start.4 = (bf16[32,1792]{1,0:T(8,128)(2,1)S(1)}, bf16[32,1792]{1,0:T(8,128)(2,1)S(1)}, u32[]{:S(2)}, u32[]{:S(2)}) collective-permute-start(bf16[32,1792]{1,0:T(8,128)(2,1)S(1)} %bitcast.353), channel_id=1, source_target_pairs={{0,10},{2,12},{4,14},{6,0},{8,2},{10,4},{12,6},{14,8},{1,11},{3,13... | collective-permute-start | bytes 344072 | tf_op jit(solution)/shard_map/ppermute | solution.py:18
  21.2 11.2 %copy-start.44 = (pred[128]{0:T(512)(128)(4,1)}, pred[128]{0:T(512)(128)(4,1)S(1)}, u32[]{:S(2)}) copy-start(pred[128]{0:T(512)(128)(4,1)S(1)} %get-tuple-element.77) | copy-start | bytes 388
  21.2 11.1 %copy-start.46 = (f32[128]{0:T(128)}, f32[128]{0:T(128)S(1)}, u32[]{:S(2)}) copy-start(f32[128]{0:T(128)S(1)} %get-tuple-element.78) | copy-start | bytes 1540
  22.8 13.7 %copy-start.28 = (f32[128,28]{0,1:T(8,128)}, f32[128,28]{0,1:T(8,128)S(1)}, u32[]{:S(2)}) copy-start(f32[128,28]{0,1:T(8,128)S(1)} %get-tuple-element.108) | copy-start | bytes 43012
  22.9 10.1 %copy-start.13 = (f32[128,28]{1,0:T(8,128)}, f32[128,28]{1,0:T(8,128)S(1)}, u32[]{:S(2)}) copy-start(f32[128,28]{1,0:T(8,128)S(1)} %copy.67) | copy-start | bytes 43012
  23.0 9.4 %copy-start.49 = (f32[28]{0:T(128)}, f32[28]{0:T(128)S(1)}, u32[]{:S(2)}) copy-start(f32[28]{0:T(128)S(1)} %slice_bitcast_fusion.11) | copy-start | bytes 340
  23.5 5.4 %collective-permute-start.5 = (bf16[32,1792]{1,0:T(8,128)(2,1)S(1)}, bf16[32,1792]{1,0:T(8,128)(2,1)S(1)}, u32[]{:S(2)}, u32[]{:S(2)}) collective-permute-start(bf16[32,1792]{1,0:T(8,128)(2,1)S(1)} %bitcast.354), channel_id=1, source_target_pairs={{0,12},{2,14},{4,0},{6,2},{8,4},{10,6},{12,8},{14,10},{1,13},{3,15... | collective-permute-start | bytes 344072 | tf_op jit(solution)/shard_map/ppermute | solution.py:18
  26.6 5.7 %collective-permute-start.6 = (bf16[32,1792]{1,0:T(8,128)(2,1)S(1)}, bf16[32,1792]{1,0:T(8,128)(2,1)S(1)}, u32[]{:S(2)}, u32[]{:S(2)}) collective-permute-start(bf16[32,1792]{1,0:T(8,128)(2,1)S(1)} %bitcast.355), channel_id=1, source_target_pairs={{0,14},{2,0},{4,2},{6,4},{8,6},{10,8},{12,10},{14,12},{1,15},{3,1}... | collective-permute-start | bytes 344072 | tf_op jit(solution)/shard_map/ppermute | solution.py:18
  32.9 2.8 %collective-permute-start.7 = (bf16[128,128]{0,1:T(8,128)(2,1)S(1)}, bf16[128,128]{0,1:T(8,128)(2,1)S(1)}, u32[]{:S(2)}, u32[]{:S(2)}) collective-permute-start(bf16[128,128]{0,1:T(8,128)(2,1)S(1)} %fusion.58), channel_id=1, source_target_pairs={{0,1},{1,0},{2,3},{3,2},{4,5},{5,4},{6,7},{7,6},{8,9},{9,8},{10,11... | collective-permute-start | bytes 98312 | tf_op jit(solution)/shard_map/ppermute | solution.py:29
  40.0 21.8 %copy-start = (f32[28,4096]{1,0:T(8,128)}, f32[28,4096]{1,0:T(8,128)S(1)}, u32[]{:S(2)}) copy-start(f32[28,4096]{1,0:T(8,128)S(1)} %reshape.295) | copy-start | bytes 1376260
  40.1 5.3 %copy-start.23 = (bf16[28,126]{1,0:T(8,128)(2,1)}, bf16[28,126]{1,0:T(8,128)(2,1)S(1)}, u32[]{:S(2)}) copy-start(bf16[28,126]{1,0:T(8,128)(2,1)S(1)} %broadcast.164) | copy-start | bytes 21172
  42.6 4.3 %copy-start.17 = (bf16[28,8320]{1,0:T(8,128)(2,1)S(1)}, bf16[28,8320]{1,0:T(8,128)(2,1)}, u32[]{:S(2)}) copy-start(bf16[28,8320]{1,0:T(8,128)(2,1)} %concatenate.71) | copy-start | bytes 1397764
  42.6 4.4 %copy-start.55 = (f32[1,28]{1,0:T(1,128)S(1)}, f32[1,28]{1,0:T(1,128)}, u32[]{:S(2)}) copy-start(f32[1,28]{1,0:T(1,128)} %param.16) | copy-start | bytes 340
  42.6 4.4 %copy-start.33 = (f32[128,128]{1,0:T(8,128)S(1)}, f32[128,128]{1,0:T(8,128)}, u32[]{:S(2)}) copy-start(f32[128,128]{1,0:T(8,128)} %get-tuple-element.106) | copy-start | bytes 196612
  42.6 4.4 %copy-start.39 = (f32[28,64]{1,0:T(8,128)S(1)}, f32[28,64]{1,0:T(8,128)}, u32[]{:S(2)}) copy-start(f32[28,64]{1,0:T(8,128)} %reshape_squeeze.7) | copy-start | bytes 21508
  42.6 4.4 %copy-start.40 = (pred[128,128]{1,0:T(8,128)(4,1)S(1)}, pred[128,128]{1,0:T(8,128)(4,1)}, u32[]{:S(2)}) copy-start(pred[128,128]{1,0:T(8,128)(4,1)} %get-tuple-element.105) | copy-start | bytes 49156
  46.9 14.6 %collective-permute-start.9 = (bf16[28,8320]{1,0:T(8,128)(2,1)S(1)}, bf16[28,8320]{1,0:T(8,128)(2,1)S(1)}, u32[]{:S(2)}, u32[]{:S(2)}) collective-permute-start(bf16[28,8320]{1,0:T(8,128)(2,1)S(1)} %copy-done.17), channel_id=1, source_target_pairs={{0,2},{2,0},{4,6},{6,4},{8,10},{10,8},{12,14},{14,12},{1,3},{3,1},... | collective-permute-start | bytes 1397768 | tf_op jit(solution)/shard_map/ppermute | solution.py:148
  47.0 14.5 %copy-start.32 = (f32[28,1]{1,0:T(8,128)S(1)}, f32[28,1]{1,0:T(8,128)}, u32[]{:S(2)}) copy-start(f32[28,1]{1,0:T(8,128)} %copy.74) | copy-start | bytes 340
  47.0 14.8 %copy-start.54 = (f32[28]{0:T(128)S(1)}, f32[28]{0:T(128)}, u32[]{:S(2)}) copy-start(f32[28]{0:T(128)} %exponential_multiply_fusion.1) | copy-start | bytes 340
  48.8 13.3 %copy-start.24 = (bf16[28,126]{1,0:T(8,128)(2,1)S(1)}, bf16[28,126]{1,0:T(8,128)(2,1)}, u32[]{:S(2)}) copy-start(bf16[28,126]{1,0:T(8,128)(2,1)} %copy-done.23) | copy-start | bytes 21172
  62.3 13.9 %collective-permute-start.10 = (bf16[28,8320]{1,0:T(8,128)(2,1)S(1)}, bf16[28,8320]{1,0:T(8,128)(2,1)}, u32[]{:S(2)}, u32[]{:S(2)}) collective-permute-start(bf16[28,8320]{1,0:T(8,128)(2,1)S(1)} %concatenate.72), channel_id=1, source_target_pairs={{0,4},{2,6},{4,0},{6,2},{8,12},{10,14},{12,8},{14,10},{1,5},{3,7},... | collective-permute-start | bytes 1397768 | tf_op jit(solution)/shard_map/ppermute | solution.py:148
  62.5 15.1 %copy-start.1 = (f32[28,4096]{1,0:T(8,128)S(1)}, f32[28,4096]{1,0:T(8,128)}, u32[]{:S(2)}) copy-start(f32[28,4096]{1,0:T(8,128)} %copy-done) | copy-start | bytes 1376260
  78.2 14.1 %collective-permute-start.11 = (bf16[28,4224]{1,0:T(8,128)(2,1)S(1)}, bf16[28,4224]{1,0:T(8,128)(2,1)}, u32[]{:S(2)}, u32[]{:S(2)}) collective-permute-start(bf16[28,4224]{1,0:T(8,128)(2,1)S(1)} %concatenate.73), channel_id=1, source_target_pairs={{0,8},{2,10},{4,12},{6,14},{8,0},{10,2},{12,4},{14,6},{1,9},{3,11}... | collective-permute-start | bytes 709640 | tf_op jit(solution)/shard_map/ppermute | solution.py:155
  100.0 2.1 %collective-permute-start.12 = (bf16[128,128]{0,1:T(8,128)(2,1)S(1)}, bf16[128,128]{0,1:T(8,128)(2,1)S(1)}, u32[]{:S(2)}, u32[]{:S(2)}) collective-permute-start(bf16[128,128]{0,1:T(8,128)(2,1)S(1)} %add_convert_fusion), channel_id=1, source_target_pairs={{0,1},{1,0},{2,3},{3,2},{4,5},{5,4},{6,7},{7,6},{8,9},{9,8},{10,11... | collective-permute-start | bytes 98312 | tf_op jit(solution)/shard_map/ppermute | solution.py:29
  104.0 8.3 %copy-start.3 = (bf16[256,1792]{1,0:T(8,128)(2,1)S(1)}, bf16[256,1792]{1,0:T(8,128)(2,1)}, u32[]{:S(2)}) copy-start(bf16[256,1792]{1,0:T(8,128)(2,1)} %copy-done.2) | copy-start | bytes 2752516
  105.0 10.3 %copy-start.22 = (bf16[36,1792]{1,0:T(8,128)(2,1)S(1)}, bf16[36,1792]{1,0:T(8,128)(2,1)}, u32[]{:S(2)}) copy-start(bf16[36,1792]{1,0:T(8,128)(2,1)} %get-tuple-element.98) | copy-start | bytes 387076
  105.0 22.7 %copy-start.21 = (bf16[36,1792]{1,0:T(8,128)(2,1)S(1)}, bf16[36,1792]{1,0:T(8,128)(2,1)}, u32[]{:S(2)}) copy-start(bf16[36,1792]{1,0:T(8,128)(2,1)} %get-tuple-element.97) | copy-start | bytes 387076
  105.0 22.7 %collective-permute-start.19 = (bf16[36,1792]{1,0:T(8,128)(2,1)}, bf16[36,1792]{1,0:T(8,128)(2,1)S(1)}, u32[]{:S(2)}, u32[]{:S(2)}) collective-permute-start(bf16[36,1792]{1,0:T(8,128)(2,1)} %get-tuple-element.102), channel_id=1, source_target_pairs={{0,12},{2,14},{4,0},{6,2},{8,4},{10,6},{12,8},{14,10},{1,13},{3,15... | collective-permute-start | bytes 387080 | tf_op jit(solution)/shard_map/ppermute | solution.py:18
  107.5 7.8 %collective-permute-start.20 = (bf16[36,1792]{1,0:T(8,128)(2,1)}, bf16[36,1792]{1,0:T(8,128)(2,1)S(1)}, u32[]{:S(2)}, u32[]{:S(2)}) collective-permute-start(bf16[36,1792]{1,0:T(8,128)(2,1)} %pad_maximum_fusion), channel_id=1, source_target_pairs={{0,14},{2,0},{4,2},{6,4},{8,6},{10,8},{12,10},{14,12},{1,15},{3,1}... | collective-permute-start | bytes 387080 | tf_op jit(solution)/shard_map/ppermute | solution.py:18
  108.3 22.0 %collective-permute-start.18 = (bf16[36,1792]{1,0:T(8,128)(2,1)}, bf16[36,1792]{1,0:T(8,128)(2,1)S(1)}, u32[]{:S(2)}, u32[]{:S(2)}) collective-permute-start(bf16[36,1792]{1,0:T(8,128)(2,1)} %get-tuple-element.101), channel_id=1, source_target_pairs={{0,10},{2,12},{4,14},{6,0},{8,2},{10,4},{12,6},{14,8},{1,11},{3,13... | collective-permute-start | bytes 387080 | tf_op jit(solution)/shard_map/ppermute | solution.py:18
  108.4 23.7 %collective-permute-start.17 = (bf16[36,1792]{1,0:T(8,128)(2,1)}, bf16[36,1792]{1,0:T(8,128)(2,1)S(1)}, u32[]{:S(2)}, u32[]{:S(2)}) collective-permute-start(bf16[36,1792]{1,0:T(8,128)(2,1)} %get-tuple-element.100), channel_id=1, source_target_pairs={{0,8},{2,10},{4,12},{6,14},{8,0},{10,2},{12,4},{14,6},{1,9},{3,11}... | collective-permute-start | bytes 387080 | tf_op jit(solution)/shard_map/ppermute | solution.py:18
  111.9 20.2 %collective-permute-start.16 = (bf16[36,1792]{1,0:T(8,128)(2,1)}, bf16[36,1792]{1,0:T(8,128)(2,1)S(1)}, u32[]{:S(2)}, u32[]{:S(2)}) collective-permute-start(bf16[36,1792]{1,0:T(8,128)(2,1)} %get-tuple-element.99), channel_id=1, source_target_pairs={{0,6},{2,8},{4,10},{6,12},{8,14},{10,0},{12,2},{14,4},{1,7},{3,9},... | collective-permute-start | bytes 387080 | tf_op jit(solution)/shard_map/ppermute | solution.py:18
  115.3 16.9 %collective-permute-start.15 = (bf16[36,1792]{1,0:T(8,128)(2,1)S(1)}, bf16[36,1792]{1,0:T(8,128)(2,1)S(1)}, u32[]{:S(2)}, u32[]{:S(2)}) collective-permute-start(bf16[36,1792]{1,0:T(8,128)(2,1)S(1)} %copy-done.22), channel_id=1, source_target_pairs={{0,4},{2,6},{4,8},{6,10},{8,12},{10,14},{12,0},{14,2},{1,5},{3,7},... | collective-permute-start | bytes 387080 | tf_op jit(solution)/shard_map/ppermute | solution.py:18
  127.7 5.2 %collective-permute-start.14 = (bf16[36,1792]{1,0:T(8,128)(2,1)S(1)}, bf16[36,1792]{1,0:T(8,128)(2,1)S(1)}, u32[]{:S(2)}, u32[]{:S(2)}) collective-permute-start(bf16[36,1792]{1,0:T(8,128)(2,1)S(1)} %copy-done.21), channel_id=1, source_target_pairs={{0,2},{2,4},{4,6},{6,8},{8,10},{10,12},{12,14},{14,0},{1,3},{3,5},... | collective-permute-start | bytes 387080 | tf_op jit(solution)/shard_map/ppermute | solution.py:18
  130.2 13.0 %collective-permute-start.13 = (bf16[1,128,1792]{2,1,0:T(8,128)(2,1)S(1)}, bf16[1,128,1792]{2,1,0:T(8,128)(2,1)S(1)}, u32[]{:S(2)}, u32[]{:S(2)}) collective-permute-start(bf16[1,128,1792]{2,1,0:T(8,128)(2,1)S(1)} %fusion.1), channel_id=1, source_target_pairs={{16,0},{17,1},{18,2},{19,3},{20,4},{21,5},{22,6},{23,7},{24,8},{25... | collective-permute-start | bytes 1376264 | tf_op jit(solution)/shard_map/ppermute | solution.py:12
  (33 other events, 61.0 us)

commit v6 on v5

--- a/solution.py
+++ b/solution.py
@@ -196,12 +196,19 @@
     size, mine = (lax.axis_size("seq"), lax.axis_index("seq"))
     group = lax.axis_index("head")
     own_rows = proj_weight[0]
+    pairs, pair, parity = (size // 2, mine // 2, mine % 2)
+    partner_rows = lax.ppermute(own_rows, "seq", [(i, i ^ 1) for i in range(size)])
+    pair_rows = jnp.where(
+        parity == 0,
+        jnp.concatenate([own_rows, partner_rows], axis=0),
+        jnp.concatenate([partner_rows, own_rows], axis=0),
+    )
     slot_weight = jnp.concatenate(
-        [own_rows] + [rotated(own_rows, "seq", k) for k in range(1, size)], axis=0
+        [pair_rows] + [rotated(pair_rows, "seq", 2 * k) for k in range(1, pairs)], axis=0
     )
     slot_value = jnp.dot(bwd_flat, slot_weight.T, preferred_element_type=jnp.float32)
-    slot_value = slot_value.reshape(tokens, size, -1)[:, ::-1].reshape(tokens, -1)
-    partial_value = roll_blocks(slot_value, mine + 1, size, 1)
+    slot_value = slot_value.reshape(tokens, pairs, -1)[:, ::-1].reshape(tokens, -1)
+    partial_value = roll_blocks(slot_value, pair + 1, pairs, 1)
     group_width = partial_value.shape[1] // 2
     mine_part = lax.dynamic_slice_in_dim(partial_value, group * group_width, group_width, axis=1)
     other_part = lax.dynamic_slice_in_dim(
@@ -272,18 +279,18 @@
         jnp.concatenate([mixer_grad, other_grad], axis=1),
         jnp.concatenate([other_grad, mixer_grad], axis=1),
     )
-    mixer_slots = roll_blocks(mixer_full, size - 1 - mine, size, 1)
-    mixer_slots = mixer_slots.reshape(tokens, size, -1)[:, ::-1].reshape(tokens, -1)
+    mixer_slots = roll_blocks(mixer_full, pairs - 1 - pair, pairs, 1)
+    mixer_slots = mixer_slots.reshape(tokens, pairs, -1)[:, ::-1].reshape(tokens, -1)
     back_proj = jnp.dot(mixer_slots, slot_weight, preferred_element_type=jnp.float32)
     value_grad = (out_grads[0].astype(jnp.float32) + sum_grads[0].astype(jnp.float32)).reshape(
         tokens, channels_here
     ) + back_proj
     value_grad = value_grad.astype(jnp.bfloat16)
     prev_part = shifted(value_grad.reshape(1, tokens, channels_here), "section", -1)
-    dest_grad = roll_blocks(mixer_full, size - mine, size, 1)
+    dest_grad = roll_blocks(mixer_full, pairs - pair, pairs, 1)
     row_parts = lax.dot_general(
         dest_grad, bwd_flat, (((0,), (0,)), ((), ())), preferred_element_type=jnp.float32
-    ).reshape(size, -1, channels_here)
+    ).reshape(pairs, -1, channels_here)
     small = jnp.concatenate(
         [
             (out_grads[2] + sum_grads[2]).reshape(channels_here),
@@ -299,19 +306,31 @@
     small_low = (small - small_high.astype(jnp.float32)).astype(jnp.bfloat16)
     small_coded = jnp.concatenate([small_high, small_low], axis=0)
     block_rows = row_parts.shape[1]
-    grad_rows = row_parts[0]
+    pair_sum = row_parts[0]
     small_slots = [small_coded]
-    for k in range(1, size):
+    for k in range(1, pairs):
         message = jnp.concatenate([row_parts[k].astype(jnp.bfloat16), small_coded], axis=0)
-        got = rotated(message, "seq", k)
-        grad_rows = grad_rows + got[:block_rows].astype(jnp.float32)
+        got = rotated(message, "seq", 2 * k)
+        pair_sum = pair_sum + got[:block_rows].astype(jnp.float32)
         small_slots.append(got[block_rows:])
     small_slots = jnp.stack(small_slots[::-1])
-    small_slots = roll_blocks(small_slots, mine + 1, size, 0).astype(jnp.float32)
+    small_slots = roll_blocks(small_slots, pair + 1, pairs, 0).astype(jnp.float32)
     small_parts = small_slots[:, :small_rows] + small_slots[:, small_rows:]
-    small_total = small_parts[0]
-    for j in range(1, size):
-        small_total = small_total + small_parts[j]
+    side_total = small_parts[0]
+    for j in range(1, pairs):
+        side_total = side_total + small_parts[j]
+    side_high = side_total.astype(jnp.bfloat16)
+    side_low = (side_total - side_high.astype(jnp.float32)).astype(jnp.bfloat16)
+    half_rows = block_rows // 2
+    mine_rows = lax.dynamic_slice_in_dim(pair_sum, parity * half_rows, half_rows, axis=0)
+    other_rows = lax.dynamic_slice_in_dim(pair_sum, (1 - parity) * half_rows, half_rows, axis=0)
+    message = jnp.concatenate([other_rows.astype(jnp.bfloat16), side_high, side_low], axis=0)
+    got = lax.ppermute(message, "seq", [(i, i ^ 1) for i in range(size)])
+    grad_rows = mine_rows + got[:half_rows].astype(jnp.float32)
+    own_side = side_high.astype(jnp.float32) + side_low.astype(jnp.float32)
+    got_side = got[half_rows:].astype(jnp.float32)
+    got_side = got_side[:small_rows] + got_side[small_rows:]
+    small_total = jnp.where(parity == 0, own_side + got_side, got_side + own_side)
     small = small_total.reshape(-1)
     totals = (
         small[:channels_here],

time: 145 us -> 156 us (1.076)
  waiting for transfers between devices: 57.4 us -> 78.5 us
  starting transfers between devices: 36.1 us -> 20.1 us
  other arithmetic: 14 us -> 16.5 us
  local copies, waits for them, and re-layouts: 16.6 us -> 19.1 us
    ppermute x14 -> x6, waiting for transfers between devices: 11.7 us -> 36.6 us  [rotated(): return lax.ppermute(block, axis, route)]
    ppermute x14 -> x6, starting transfers between devices: 29.5 us -> 7.98 us  [rotated(): return lax.ppermute(block, axis, route)]
    ppermute x2, waiting for transfers between devices: 26.4 us -> 20.8 us  [both_scans(): got = lax.ppermute(payload, axis, [(i, i ^ distance) for i in range(size)])]
    ppermute x0 -> x2, waiting for transfers between devices: none -> 3.01 us  [the longest x1 3.01 us: shards(): got = lax.ppermute(message, 'seq', [(i, i ^ 1) for i in range(size)])]
    ppermute x2, starting transfers between devices: 0.13 us -> 2.37 us  [both_scans(): got = lax.ppermute(payload, axis, [(i, i ^ distance) for i in range(size)])]
    ppermute x0 -> x2, starting transfers between devices: none -> 2.12 us  [the longest x1 1.12 us: shards(): got = lax.ppermute(message, 'seq', [(i, i ^ 1) for i in range(size)])]
    ppermute x1, starting transfers between devices: 0.73 us -> 2.79 us  [both_scans(): got = lax.ppermute(last, axis, [(i, i ^ distance) for i in range(size)])]
    ppermute x1, waiting for transfers between devices: 12.3 us -> 10.3 us  [both_scans(): got = lax.ppermute(last, axis, [(i, i ^ distance) for i in range(size)])]
  transfers between devices with their start and end apart: 21 -> 15, of which waited for: 11 -> 9; matrix products, arithmetic and copies ran while one was open for 15% -> 15% of each run, Pallas kernels for 0% -> 0%
where the time goes in v6:
time: 156 us; the launch traced here: 154 us
  waiting for transfers between devices  78.5 us (50%)
  starting transfers between devices  20.1 us (13%)
  local copies, waits for them, and re-layouts  19.1 us (12%)
  matrix products  16.6 us (11%)
  other arithmetic  16.5 us (11%)
  between operations  3.1 us (2%)
    ppermute x6, waiting for transfers between devices, rotated(): return lax.ppermute(block, axis, route)  36.6 us
    ppermute x2, waiting for transfers between devices, both_scans(): got = lax.ppermute(payload, axis, [(i, i ^ distance) for i in range(size)])  20.8 us
    ppermute x1, waiting for transfers between devices, both_scans(): got = lax.ppermute(last, axis, [(i, i ^ distance) for i in range(size)])  10.3 us
    ppermute x6, starting transfers between devices, rotated(): return lax.ppermute(block, axis, route)  7.98 us
    ppermute x2, waiting for transfers between devices, shifted(): return lax.ppermute(block, axis, route)  7.82 us
    dot_general x5, matrix products, contract(): return jnp.einsum(spec, left, right, preferred_element_type=jnp.float32)  7.61 us
    ppermute x2, starting transfers between devices, shifted(): return lax.ppermute(block, axis, route)  4.71 us
    unnamed x153, local copies, waits for them, and re-layouts  4.33 us
  transfers between devices with their start and end apart: 15, of which 9 were waited for; matrix products, arithmetic and copies ran while one was open for 15% of the time, Pallas kernels for 0%

profile of v6, /device:TPU:4, one launch (start us, length us, event | category | flops | bytes accessed | tf_op | source)
XLA Modules:
  0.0 153.8 jit_solution(2944865080099960690)
XLA Ops:
  0.6 1.3 slice.136
  1.9 3.4 %collective-permute-start.5 = (s32[1]{0:T(128)}, s32[1]{0:T(128)}, u32[]{:S(2)}, u32[]{:S(2)}) collective-permute-start(s32[1]{0:T(128)} %bitcast.13), channel_id=1, source_target_pairs={{0,2},{2,4},{4,6},{6,8},{8,10},{10,12},{12,14},{1,3},{3,5},{5,7},{... | collective-permute-start | bytes 20 | tf_op jit(solution)/shard_map/ppermute | solution.py:12
  5.4 1.0 collective-permute-start
  6.4 0.7 reduce
  7.9 1.3 copy.66
  10.2 0.7 broadcast_compare_fusion
  10.9 1.2 broadcast_compare_fusion.1
  13.9 3.2 %collective-permute-start.3 = (bf16[64,1792]{1,0:T(8,128)(2,1)S(1)}, bf16[64,1792]{1,0:T(8,128)(2,1)S(1)}, u32[]{:S(2)}, u32[]{:S(2)}) collective-permute-start(bf16[64,1792]{1,0:T(8,128)(2,1)S(1)} %maximum_select_fusion), channel_id=1, source_target_pairs={{0,12},{2,14},{4,0},{6,2},{8,4},{10,6},{12,8},{14,10},{1,13},{3,15... | collective-permute-start | bytes 688136 | tf_op jit(solution)/shard_map/ppermute | solution.py:18
  17.1 1.0 collective-permute-start.1
  18.3 5.0 %collective-permute-done.3 = bf16[64,1792]{1,0:T(8,128)(2,1)S(1)} collective-permute-done((bf16[64,1792]{1,0:T(8,128)(2,1)S(1)}, bf16[64,1792]{1,0:T(8,128)(2,1)S(1)}, u32[]{:S(2)}, u32[]{:S(2)}) %collective-permute-start.3) | collective-permute-done | bytes 229408 | tf_op jit(solution)/shard_map/ppermute | solution.py:18
  23.2 12.8 %collective-permute-done.2 = bf16[64,1792]{1,0:T(8,128)(2,1)S(1)} collective-permute-done((bf16[64,1792]{1,0:T(8,128)(2,1)S(1)}, bf16[64,1792]{1,0:T(8,128)(2,1)S(1)}, u32[]{:S(2)}, u32[]{:S(2)}) %collective-permute-start.2) | collective-permute-done | bytes 229408 | tf_op jit(solution)/shard_map/ppermute | solution.py:18
  39.2 1.2 copy.71
  40.5 1.5 reshape.276
  42.0 1.3 fusion.33
  43.3 1.5 reshape.275
  45.0 1.1 concatenate.66
  47.1 2.8 %fusion.12 = (f32[28,128]{1,0:T(8,128)S(1)}, f32[28,128]{1,0:T(8,128)S(1)}, f32[28,128]{1,0:T(8,128)S(1)}, bf16[128,128]{1,0:T(8,128)(2,1)S(1)}) fusion(f32[28,128]{1,0:T(8,128)S(1)} %fusion.114, f32[128,128]{1,0:T(8,128)S(1)} %fusion.95, f32[128,128]{1,0:T(8,128)} %get-tuple-element.101, f32[28,128]{1,0:T(8,128)S(1)} %fusion.69, ...), kind=kOutput, calls=%fused_computation.18 | convolution fusion | flops 66033152 | bytes 1628160 | tf_op jit(solution)/shard_map/transpose(jvp(hts,shp->thp))/dot_general | solution.py:33
  50.2 0.9 multiply_reduce_fusion.3
  51.2 1.5 collective-permute-start.6
  52.7 0.8 fusion.124
  53.5 0.8 fusion.102
  56.0 1.8 %fusion.17 = bf16[128,28,64]{0,2,1:T(8,128)(2,1)} fusion(f32[128,28,64]{0,2,1:T(8,128)S(1)} %convert.57, f32[28,128]{1,0:T(8,128)S(1)} %fusion.114, f32[128,128]{1,0:T(8,128)S(1)} %fusion.95, f32[128,128]{1,0:T(8,128)S(1)} %copy-done.33, f32[28,128]{1,0:T(8,128)S(1)} %fusion.69, pred[128,128]{1,0:T(8,128)(4,1)S(1)} %copy-done.40, ...), kind=kOutput, calls=%fused_computation.27 | convolution fusion | flops 63078400 | bytes 1574000 | tf_op jit(solution)/shard_map/transpose(jvp(hts,shp->thp))/dot_general | solution.py:33
  57.8 7.8 %collective-permute-done.6 = bf16[28,8320]{1,0:T(8,128)(2,1)S(1)} collective-permute-done((bf16[28,8320]{1,0:T(8,128)(2,1)S(1)}, bf16[28,8320]{1,0:T(8,128)(2,1)S(1)}, u32[]{:S(2)}, u32[]{:S(2)}) %collective-permute-start.6) | collective-permute-done | bytes 465952 | tf_op jit(solution)/shard_map/ppermute | solution.py:148
  67.2 0.9 fusion.116
  68.1 0.9 concatenate.67
  69.0 0.9 collective-permute-start.7
  69.9 13.0 %collective-permute-done.7 = bf16[28,8320]{1,0:T(8,128)(2,1)} collective-permute-done((bf16[28,8320]{1,0:T(8,128)(2,1)S(1)}, bf16[28,8320]{1,0:T(8,128)(2,1)}, u32[]{:S(2)}, u32[]{:S(2)}) %collective-permute-start.7) | collective-permute-done | bytes 465952 | tf_op jit(solution)/shard_map/ppermute | solution.py:148
  82.9 1.1 convert_element_type.295
  84.9 2.8 %collective-permute-start.8 = (bf16[28,4224]{1,0:T(8,128)(2,1)S(1)}, bf16[28,4224]{1,0:T(8,128)(2,1)S(1)}, u32[]{:S(2)}, u32[]{:S(2)}) collective-permute-start(bf16[28,4224]{1,0:T(8,128)(2,1)S(1)} %concatenate.68), channel_id=1, source_target_pairs={{0,8},{2,10},{4,12},{6,14},{8,0},{10,2},{12,4},{14,6},{1,9},{3,11}... | collective-permute-start | bytes 709640 | tf_op jit(solution)/shard_map/ppermute | solution.py:155
  87.7 1.0 bitcast_multiply_fusion
  88.7 10.3 %collective-permute-done.8 = bf16[28,4224]{1,0:T(8,128)(2,1)S(1)} collective-permute-done((bf16[28,4224]{1,0:T(8,128)(2,1)S(1)}, bf16[28,4224]{1,0:T(8,128)(2,1)S(1)}, u32[]{:S(2)}, u32[]{:S(2)}) %collective-permute-start.8) | collective-permute-done | bytes 236576 | tf_op jit(solution)/shard_map/ppermute | solution.py:155
  98.9 0.7 copy-done.17
  99.7 2.3 %multiply_reduce_fusion.4 = (f32[28]{0:T(128)S(1)}, f32[28,4096]{1,0:T(8,128)}, bf16[28,4096]{1,0:T(8,128)(2,1)S(1)}) fusion(bf16[28,4224]{1,0:T(8,128)(2,1)} %copy-done.17, f32[28]{0:T(128)S(1)} %get-tuple-element.52, f32[28,8320]{1,0:T(8,128)S(1)} %convert_element_type.295, f32[28]{0:T(128)S(1)} %get-tuple-element.54, ...), kind=kLoop, calls=%fused_computation.65 | loop fusion | flops 2064356 | bytes 2753075 | tf_op jit(solution)/shard_map/reduce_sum | solution.py:271
  105.2 1.0 fusion.22
  106.9 0.8 fusion.134
  107.8 0.8 fusion.133
  109.8 0.9 pad_maximum_fusion.3
  110.7 2.7 %collective-permute-start.13 = (bf16[68,1792]{1,0:T(8,128)(2,1)}, bf16[68,1792]{1,0:T(8,128)(2,1)S(1)}, u32[]{:S(2)}, u32[]{:S(2)}) collective-permute-start(bf16[68,1792]{1,0:T(8,128)(2,1)} %get-tuple-element.97), channel_id=1, source_target_pairs={{0,12},{2,14},{4,0},{6,2},{8,4},{10,6},{12,8},{14,10},{1,13},{3,15... | collective-permute-start | bytes 731144 | tf_op jit(solution)/shard_map/ppermute | solution.py:18
  113.4 1.4 fusion.21
  114.8 1.5 copy.83
  117.3 1.0 collective-permute-start.11
  118.3 2.0 %collective-permute-done.13 = bf16[68,1792]{1,0:T(8,128)(2,1)S(1)} collective-permute-done((bf16[68,1792]{1,0:T(8,128)(2,1)}, bf16[68,1792]{1,0:T(8,128)(2,1)S(1)}, u32[]{:S(2)}, u32[]{:S(2)}) %collective-permute-start.13) | collective-permute-done | bytes 243744 | tf_op jit(solution)/shard_map/ppermute | solution.py:18
  120.3 16.8 %collective-permute-done.12 = bf16[68,1792]{1,0:T(8,128)(2,1)S(1)} collective-permute-done((bf16[68,1792]{1,0:T(8,128)(2,1)}, bf16[68,1792]{1,0:T(8,128)(2,1)S(1)}, u32[]{:S(2)}, u32[]{:S(2)}) %collective-permute-start.12) | collective-permute-done | bytes 243744 | tf_op jit(solution)/shard_map/ppermute | solution.py:18
  137.5 1.1 collective-permute-start.14
  139.0 1.3 collective-permute-start.10
  140.3 3.0 %collective-permute-done.14 = bf16[36,1792]{1,0:T(8,128)(2,1)S(1)} collective-permute-done((bf16[36,1792]{1,0:T(8,128)(2,1)S(1)}, bf16[36,1792]{1,0:T(8,128)(2,1)S(1)}, u32[]{:S(2)}, u32[]{:S(2)}) %collective-permute-start.14) | collective-permute-done | bytes 129056 | tf_op jit(solution)/shard_map/ppermute | solution.py:328
  145.2 7.8 %collective-permute-done.10 = bf16[1,128,1792]{2,1,0:T(8,128)(2,1)S(1)} collective-permute-done((bf16[1,128,1792]{2,1,0:T(8,128)(2,1)S(1)}, bf16[1,128,1792]{2,1,0:T(8,128)(2,1)S(1)}, u32[]{:S(2)}, u32[]{:S(2)}) %collective-permute-start.10) | collective-permute-done | bytes 458784 | tf_op jit(solution)/shard_map/ppermute | solution.py:12
  153.1 0.8 copy.130
  (250 shorter events, 19.2 us)
Async XLA Ops:
  0.6 9.2 %copy-start.13 = (bf16[1,128,1792]{2,1,0:T(8,128)(2,1)S(1)}, bf16[1,128,1792]{2,1,0:T(8,128)(2,1)}, u32[]{:S(2)}) copy-start(bf16[1,128,1792]{2,1,0:T(8,128)(2,1)} %param.11) | copy-start | bytes 1376260
  1.9 9.0 %collective-permute-start.5 = (s32[1]{0:T(128)}, s32[1]{0:T(128)}, u32[]{:S(2)}, u32[]{:S(2)}) collective-permute-start(s32[1]{0:T(128)} %bitcast.13), channel_id=1, source_target_pairs={{0,2},{2,4},{4,6},{6,8},{8,10},{10,12},{12,14},{1,3},{3,5},{5,7},{... | collective-permute-start | bytes 20 | tf_op jit(solution)/shard_map/ppermute | solution.py:12
  5.4 8.5 %collective-permute-start = (bf16[32,1792]{1,0:T(8,128)(2,1)}, bf16[32,1792]{1,0:T(8,128)(2,1)S(1)}, u32[]{:S(2)}, u32[]{:S(2)}) collective-permute-start(bf16[32,1792]{1,0:T(8,128)(2,1)} %bitcast.322), channel_id=1, source_target_pairs={{0,2},{2,0},{4,6},{6,4},{8,10},{10,8},{12,14},{14,12},{1,3},{3,1},... | collective-permute-start | bytes 344072 | tf_op jit(solution)/shard_map/ppermute | solution.py:200
  7.2 48.8 %copy-start.38 = (f32[28,64]{1,0:T(8,128)}, f32[28,64]{1,0:T(8,128)S(1)}, u32[]{:S(2)}) copy-start(f32[28,64]{1,0:T(8,128)S(1)} %reshape_squeeze.7) | copy-start | bytes 21508
  7.9 5.5 %copy-start.69 = (f32[28]{0:T(128)}, f32[28]{0:T(128)S(1)}, u32[]{:S(2)}) copy-start(f32[28]{0:T(128)S(1)} %negate_bitcast_fusion) | copy-start | bytes 340
  7.9 5.5 %copy-start.41 = (f32[1,28]{1,0:T(1,128)S(1)}, f32[1,28]{1,0:T(1,128)}, u32[]{:S(2)}) copy-start(f32[1,28]{1,0:T(1,128)} %param.14) | copy-start | bytes 340
  9.2 44.2 %copy-start.2 = (bf16[1,128,1792]{1,2,0:T(8,128)(2,1)}, bf16[1,128,1792]{1,2,0:T(8,128)(2,1)S(1)}, u32[]{:S(2)}) copy-start(bf16[1,128,1792]{1,2,0:T(8,128)(2,1)S(1)} %copy.66) | copy-start | bytes 1376260
  9.2 4.6 %copy-start.26 = (bf16[1,32,1792]{2,1,0:T(8,128)(2,1)S(1)}, bf16[1,32,1792]{2,1,0:T(8,128)(2,1)}, u32[]{:S(2)}) copy-start(bf16[1,32,1792]{2,1,0:T(8,128)(2,1)} %param.12) | copy-start | bytes 344068
  9.7 26.4 %copy-start.6 = (bf16[1,128,1792]{2,1,0:T(8,128)(2,1)S(1)}, bf16[1,128,1792]{2,1,0:T(8,128)(2,1)}, u32[]{:S(2)}) copy-start(bf16[1,128,1792]{2,1,0:T(8,128)(2,1)} %param.9) | copy-start | bytes 1376260
  9.8 26.7 %copy-start.10 = (f32[28,1,128]{0,2,1:T(8,128)}, f32[28,1,128]{0,2,1:T(8,128)S(1)}, u32[]{:S(2)}) copy-start(f32[28,1,128]{0,2,1:T(8,128)S(1)} %copy.87) | copy-start | bytes 43012
  12.2 24.3 %copy-start.44 = (pred[128]{0:T(512)(128)(4,1)}, pred[128]{0:T(512)(128)(4,1)S(1)}, u32[]{:S(2)}) copy-start(pred[128]{0:T(512)(128)(4,1)S(1)} %get-tuple-element.79) | copy-start | bytes 388
  12.2 24.3 %copy-start.46 = (f32[128]{0:T(128)}, f32[128]{0:T(128)S(1)}, u32[]{:S(2)}) copy-start(f32[128]{0:T(128)S(1)} %get-tuple-element.80) | copy-start | bytes 1540
  13.7 22.8 %copy-start.36 = (f32[128,28]{0,1:T(8,128)}, f32[128,28]{0,1:T(8,128)S(1)}, u32[]{:S(2)}) copy-start(f32[128,28]{0,1:T(8,128)S(1)} %get-tuple-element.104) | copy-start | bytes 43012
  13.7 24.9 %copy-start.27 = (f32[128,28]{0,1:T(8,128)}, f32[128,28]{0,1:T(8,128)S(1)}, u32[]{:S(2)}) copy-start(f32[128,28]{0,1:T(8,128)S(1)} %get-tuple-element.103) | copy-start | bytes 43012
  13.8 23.2 %copy-start.8 = (f32[128,28]{1,0:T(8,128)}, f32[128,28]{1,0:T(8,128)S(1)}, u32[]{:S(2)}) copy-start(f32[128,28]{1,0:T(8,128)S(1)} %copy.67) | copy-start | bytes 43012
  13.9 22.6 %copy-start.18 = (bf16[64,1792]{1,0:T(8,128)(2,1)}, bf16[64,1792]{1,0:T(8,128)(2,1)S(1)}, u32[]{:S(2)}) copy-start(bf16[64,1792]{1,0:T(8,128)(2,1)S(1)} %maximum_select_fusion) | copy-start | bytes 688132
  13.9 9.3 %collective-permute-start.3 = (bf16[64,1792]{1,0:T(8,128)(2,1)S(1)}, bf16[64,1792]{1,0:T(8,128)(2,1)S(1)}, u32[]{:S(2)}, u32[]{:S(2)}) collective-permute-start(bf16[64,1792]{1,0:T(8,128)(2,1)S(1)} %maximum_select_fusion), channel_id=1, source_target_pairs={{0,12},{2,14},{4,0},{6,2},{8,4},{10,6},{12,8},{14,10},{1,13},{3,15... | collective-permute-start | bytes 688136 | tf_op jit(solution)/shard_map/ppermute | solution.py:18
  17.1 18.9 %collective-permute-start.2 = (bf16[64,1792]{1,0:T(8,128)(2,1)S(1)}, bf16[64,1792]{1,0:T(8,128)(2,1)S(1)}, u32[]{:S(2)}, u32[]{:S(2)}) collective-permute-start(bf16[64,1792]{1,0:T(8,128)(2,1)S(1)} %maximum_select_fusion), channel_id=1, source_target_pairs={{0,8},{2,10},{4,12},{6,14},{8,0},{10,2},{12,4},{14,6},{1,9},{3,11}... | collective-permute-start | bytes 688136 | tf_op jit(solution)/shard_map/ppermute | solution.py:18
  17.1 18.9 %collective-permute-start.1 = (bf16[64,1792]{1,0:T(8,128)(2,1)S(1)}, bf16[64,1792]{1,0:T(8,128)(2,1)S(1)}, u32[]{:S(2)}, u32[]{:S(2)}) collective-permute-start(bf16[64,1792]{1,0:T(8,128)(2,1)S(1)} %maximum_select_fusion), channel_id=1, source_target_pairs={{0,4},{2,6},{4,8},{6,10},{8,12},{10,14},{12,0},{14,2},{1,5},{3,7},... | collective-permute-start | bytes 688136 | tf_op jit(solution)/shard_map/ppermute | solution.py:18
  18.2 18.4 %copy-start.52 = (f32[28]{0:T(128)}, f32[28]{0:T(128)S(1)}, u32[]{:S(2)}) copy-start(f32[28]{0:T(128)S(1)} %slice_bitcast_fusion.6) | copy-start | bytes 340
  23.2 13.3 %copy-start.63 = (bf16[64,1792]{1,0:T(8,128)(2,1)}, bf16[64,1792]{1,0:T(8,128)(2,1)S(1)}, u32[]{:S(2)}) copy-start(bf16[64,1792]{1,0:T(8,128)(2,1)S(1)} %collective-permute-done.3) | copy-start | bytes 688132
  36.9 1.6 %collective-permute-start.4 = (bf16[128,128]{0,1:T(8,128)(2,1)S(1)}, bf16[128,128]{0,1:T(8,128)(2,1)S(1)}, u32[]{:S(2)}, u32[]{:S(2)}) collective-permute-start(bf16[128,128]{0,1:T(8,128)(2,1)S(1)} %fusion.53), channel_id=1, source_target_pairs={{0,1},{1,0},{2,3},{3,2},{4,5},{5,4},{6,7},{7,6},{8,9},{9,8},{10,11... | collective-permute-start | bytes 98312 | tf_op jit(solution)/shard_map/ppermute | solution.py:29
  44.8 22.3 %copy-start = (f32[28,4096]{1,0:T(8,128)}, f32[28,4096]{1,0:T(8,128)S(1)}, u32[]{:S(2)}) copy-start(f32[28,4096]{1,0:T(8,128)S(1)} %reshape.275) | copy-start | bytes 1376260
  47.1 4.0 %copy-start.12 = (bf16[28,8320]{1,0:T(8,128)(2,1)S(1)}, bf16[28,8320]{1,0:T(8,128)(2,1)}, u32[]{:S(2)}) copy-start(bf16[28,8320]{1,0:T(8,128)(2,1)} %concatenate.66) | copy-start | bytes 1397764
  50.0 5.5 %copy-start.59 = (f32[1,28]{1,0:T(1,128)S(1)}, f32[1,28]{1,0:T(1,128)}, u32[]{:S(2)}) copy-start(f32[1,28]{1,0:T(1,128)} %param.16) | copy-start | bytes 340
  50.0 6.1 %copy-start.33 = (f32[128,128]{1,0:T(8,128)S(1)}, f32[128,128]{1,0:T(8,128)}, u32[]{:S(2)}) copy-start(f32[128,128]{1,0:T(8,128)} %get-tuple-element.101) | copy-start | bytes 196612
  51.2 14.5 %collective-permute-start.6 = (bf16[28,8320]{1,0:T(8,128)(2,1)S(1)}, bf16[28,8320]{1,0:T(8,128)(2,1)S(1)}, u32[]{:S(2)}, u32[]{:S(2)}) collective-permute-start(bf16[28,8320]{1,0:T(8,128)(2,1)S(1)} %copy-done.12), channel_id=1, source_target_pairs={{0,2},{2,0},{4,6},{6,4},{8,10},{10,8},{12,14},{14,12},{1,3},{3,1},... | collective-permute-start | bytes 1397768 | tf_op jit(solution)/shard_map/ppermute | solution.py:148
  56.0 9.7 %copy-start.32 = (f32[28,1]{1,0:T(8,128)S(1)}, f32[28,1]{1,0:T(8,128)}, u32[]{:S(2)}) copy-start(f32[28,1]{1,0:T(8,128)} %copy.74) | copy-start | bytes 340
  68.1 16.2 %copy-start.54 = (f32[28]{0:T(128)S(1)}, f32[28]{0:T(128)}, u32[]{:S(2)}) copy-start(f32[28]{0:T(128)} %get-tuple-element.70) | copy-start | bytes 340
  68.1 16.2 %copy-start.58 = (f32[28]{0:T(128)S(1)}, f32[28]{0:T(128)}, u32[]{:S(2)}) copy-start(f32[28]{0:T(128)} %exponential_multiply_fusion.1) | copy-start | bytes 340
  68.1 16.2 %copy-start.50 = (f32[28]{0:T(128)S(1)}, f32[28]{0:T(128)}, u32[]{:S(2)}) copy-start(f32[28]{0:T(128)} %copy-done.49) | copy-start | bytes 340
  69.0 13.9 %collective-permute-start.7 = (bf16[28,8320]{1,0:T(8,128)(2,1)S(1)}, bf16[28,8320]{1,0:T(8,128)(2,1)}, u32[]{:S(2)}, u32[]{:S(2)}) collective-permute-start(bf16[28,8320]{1,0:T(8,128)(2,1)S(1)} %concatenate.67), channel_id=1, source_target_pairs={{0,4},{2,6},{4,0},{6,2},{8,12},{10,14},{12,8},{14,10},{1,5},{3,7},... | collective-permute-start | bytes 1397768 | tf_op jit(solution)/shard_map/ppermute | solution.py:148
  69.9 14.4 %copy-start.1 = (f32[28,4096]{1,0:T(8,128)S(1)}, f32[28,4096]{1,0:T(8,128)}, u32[]{:S(2)}) copy-start(f32[28,4096]{1,0:T(8,128)} %copy-done) | copy-start | bytes 1376260
  84.9 14.1 %collective-permute-start.8 = (bf16[28,4224]{1,0:T(8,128)(2,1)S(1)}, bf16[28,4224]{1,0:T(8,128)(2,1)S(1)}, u32[]{:S(2)}, u32[]{:S(2)}) collective-permute-start(bf16[28,4224]{1,0:T(8,128)(2,1)S(1)} %concatenate.68), channel_id=1, source_target_pairs={{0,8},{2,10},{4,12},{6,14},{8,0},{10,2},{12,4},{14,6},{1,9},{3,11}... | collective-permute-start | bytes 709640 | tf_op jit(solution)/shard_map/ppermute | solution.py:155
  105.2 4.0 %copy-start.7 = (bf16[1,128,1792]{2,1,0:T(8,128)(2,1)S(1)}, bf16[1,128,1792]{2,1,0:T(8,128)(2,1)}, u32[]{:S(2)}) copy-start(bf16[1,128,1792]{2,1,0:T(8,128)(2,1)} %param.9) | copy-start | bytes 1376260
  106.2 2.9 %collective-permute-start.9 = (bf16[128,128]{0,1:T(8,128)(2,1)S(1)}, bf16[128,128]{0,1:T(8,128)(2,1)S(1)}, u32[]{:S(2)}, u32[]{:S(2)}) collective-permute-start(bf16[128,128]{0,1:T(8,128)(2,1)S(1)} %add_convert_fusion), channel_id=1, source_target_pairs={{0,1},{1,0},{2,3},{3,2},{4,5},{5,4},{6,7},{7,6},{8,9},{9,8},{10,11... | collective-permute-start | bytes 98312 | tf_op jit(solution)/shard_map/ppermute | solution.py:29
  109.7 3.7 %copy-start.15 = (bf16[28,64,64]{2,1,0:T(8,128)(2,1)S(1)}, bf16[28,64,64]{2,1,0:T(8,128)(2,1)}, u32[]{:S(2)}) copy-start(bf16[28,64,64]{2,1,0:T(8,128)(2,1)} %copy-done.14) | copy-start | bytes 688132
  110.7 6.6 %copy-start.16 = (bf16[68,1792]{1,0:T(8,128)(2,1)S(1)}, bf16[68,1792]{1,0:T(8,128)(2,1)}, u32[]{:S(2)}) copy-start(bf16[68,1792]{1,0:T(8,128)(2,1)} %get-tuple-element.95) | copy-start | bytes 731140
  110.7 9.6 %collective-permute-start.13 = (bf16[68,1792]{1,0:T(8,128)(2,1)}, bf16[68,1792]{1,0:T(8,128)(2,1)S(1)}, u32[]{:S(2)}, u32[]{:S(2)}) collective-permute-start(bf16[68,1792]{1,0:T(8,128)(2,1)} %get-tuple-element.97), channel_id=1, source_target_pairs={{0,12},{2,14},{4,0},{6,2},{8,4},{10,6},{12,8},{14,10},{1,13},{3,15... | collective-permute-start | bytes 731144 | tf_op jit(solution)/shard_map/ppermute | solution.py:18
  117.2 21.4 %copy-start.19 = (bf16[64,1792]{1,0:T(8,128)(2,1)S(1)}, bf16[64,1792]{1,0:T(8,128)(2,1)}, u32[]{:S(2)}) copy-start(bf16[64,1792]{1,0:T(8,128)(2,1)} %copy-done.18) | copy-start | bytes 688132
  117.2 21.4 %copy-start.34 = (bf16[128,4,64]{0,2,1:T(8,128)(2,1)S(1)}, bf16[128,4,64]{0,2,1:T(8,128)(2,1)}, u32[]{:S(2)}) copy-start(bf16[128,4,64]{0,2,1:T(8,128)(2,1)} %rev.7) | copy-start | bytes 196612
  117.2 21.4 %copy-start.64 = (bf16[64,1792]{1,0:T(8,128)(2,1)S(1)}, bf16[64,1792]{1,0:T(8,128)(2,1)}, u32[]{:S(2)}) copy-start(bf16[64,1792]{1,0:T(8,128)(2,1)} %copy-done.63) | copy-start | bytes 688132
  117.2 21.4 %copy-start.66 = (bf16[64,1792]{1,0:T(8,128)(2,1)S(1)}, bf16[64,1792]{1,0:T(8,128)(2,1)}, u32[]{:S(2)}) copy-start(bf16[64,1792]{1,0:T(8,128)(2,1)} %copy-done.65) | copy-start | bytes 688132
  117.2 21.4 %copy-start.68 = (bf16[64,1792]{1,0:T(8,128)(2,1)S(1)}, bf16[64,1792]{1,0:T(8,128)(2,1)}, u32[]{:S(2)}) copy-start(bf16[64,1792]{1,0:T(8,128)(2,1)} %copy-done.67) | copy-start | bytes 688132
  117.2 19.8 %collective-permute-start.12 = (bf16[68,1792]{1,0:T(8,128)(2,1)}, bf16[68,1792]{1,0:T(8,128)(2,1)S(1)}, u32[]{:S(2)}, u32[]{:S(2)}) collective-permute-start(bf16[68,1792]{1,0:T(8,128)(2,1)} %get-tuple-element.96), channel_id=1, source_target_pairs={{0,8},{2,10},{4,12},{6,14},{8,0},{10,2},{12,4},{14,6},{1,9},{3,11}... | collective-permute-start | bytes 731144 | tf_op jit(solution)/shard_map/ppermute | solution.py:18
  117.3 19.8 %collective-permute-start.11 = (bf16[68,1792]{1,0:T(8,128)(2,1)S(1)}, bf16[68,1792]{1,0:T(8,128)(2,1)S(1)}, u32[]{:S(2)}, u32[]{:S(2)}) collective-permute-start(bf16[68,1792]{1,0:T(8,128)(2,1)S(1)} %copy-done.16), channel_id=1, source_target_pairs={{0,4},{2,6},{4,8},{6,10},{8,12},{10,14},{12,0},{14,2},{1,5},{3,7},... | collective-permute-start | bytes 731144 | tf_op jit(solution)/shard_map/ppermute | solution.py:18
  137.5 5.8 %collective-permute-start.14 = (bf16[36,1792]{1,0:T(8,128)(2,1)S(1)}, bf16[36,1792]{1,0:T(8,128)(2,1)S(1)}, u32[]{:S(2)}, u32[]{:S(2)}) collective-permute-start(bf16[36,1792]{1,0:T(8,128)(2,1)S(1)} %pad_maximum_fusion.9), channel_id=1, source_target_pairs={{0,2},{2,0},{4,6},{6,4},{8,10},{10,8},{12,14},{14,12},{1,3},{3,1},... | collective-permute-start | bytes 387080 | tf_op jit(solution)/shard_map/ppermute | solution.py:328
  139.0 14.1 %collective-permute-start.10 = (bf16[1,128,1792]{2,1,0:T(8,128)(2,1)S(1)}, bf16[1,128,1792]{2,1,0:T(8,128)(2,1)S(1)}, u32[]{:S(2)}, u32[]{:S(2)}) collective-permute-start(bf16[1,128,1792]{2,1,0:T(8,128)(2,1)S(1)} %fusion.1), channel_id=1, source_target_pairs={{16,0},{17,1},{18,2},{19,3},{20,4},{21,5},{22,6},{23,7},{24,8},{25... | collective-permute-start | bytes 1376264 | tf_op jit(solution)/shard_map/ppermute | solution.py:12
  (39 other events, 86.2 us)

commit v7 on v5

--- a/solution.py
+++ b/solution.py
@@ -118,7 +118,51 @@
     return near_state
 
 
-def both_scans(decay, state, state_grad, axis, filler_fn, filler_args):
+def scan_message(part, distance, size, upper):
+    width = part["fwd"].shape[1]
+    high = lax.convert_element_type(part["decay"].astype(jnp.bfloat16), jnp.float32)
+    low = part["decay"] - high
+    pad = jnp.zeros((high.shape[0], 126), jnp.float32)
+    tail = jnp.concatenate([high[:, None], low[:, None], pad], axis=1)
+    if distance * 2 < size:
+        body = [part["fwd"], part["bwd"]]
+    else:
+        body = [jnp.where(upper, part["bwd"], part["fwd"])]
+    return jnp.concatenate(body + [tail], axis=1).astype(jnp.bfloat16)
+
+
+def scan_absorb(part, got, distance, size, upper):
+    width = part["fwd"].shape[1]
+    got = got.astype(jnp.float32)
+    got_fwd = got[:, :width]
+    if distance * 2 < size:
+        got_bwd = got[:, width : 2 * width]
+        at = 2 * width
+    else:
+        got_bwd = got_fwd
+        at = width
+    got_decay = got[:, at] + got[:, at + 1]
+    new = dict(part)
+    new["before"] = jnp.where(upper, part["before"] + part["before_decay"][:, None] * got_fwd, part["before"])
+    new["before_decay"] = jnp.where(upper, part["before_decay"] * got_decay, part["before_decay"])
+    new["after"] = jnp.where(upper, part["after"], part["after"] + part["after_decay"][:, None] * got_bwd)
+    new["after_decay"] = jnp.where(upper, part["after_decay"], part["after_decay"] * got_decay)
+    if distance * 2 < size:
+        new["fwd"] = jnp.where(
+            upper,
+            part["fwd"] + part["decay"][:, None] * got_fwd,
+            got_fwd + got_decay[:, None] * part["fwd"],
+        )
+        new["bwd"] = jnp.where(
+            upper,
+            got_bwd + got_decay[:, None] * part["bwd"],
+            part["bwd"] + part["decay"][:, None] * got_bwd,
+        )
+        new["decay"] = part["decay"] * got_decay
+    return new
+
+
+def both_scans(decay, state, state_grad, axis, filler_fn, filler_args, chunks=2):
     size, mine = (lax.axis_size(axis), lax.axis_index(axis))
     if size & (size - 1):
         return (
@@ -126,57 +170,49 @@
             scan_rounds(decay, state_grad, axis, False),
             filler_fn(*filler_args),
         )
-    width = state.shape[1]
-    total_decay = decay
-    total_fwd, total_bwd = (state, state_grad)
-    before = jnp.zeros_like(state)
-    before_decay = jnp.ones_like(decay)
-    after = jnp.zeros_like(state_grad)
-    after_decay = jnp.ones_like(decay)
-    distance = 1
-    while distance < size:
-        high = lax.convert_element_type(total_decay.astype(jnp.bfloat16), jnp.float32)
-        low = total_decay - high
-        pad = jnp.zeros((decay.shape[0], 126), jnp.float32)
-        payload = jnp.concatenate(
-            [total_fwd, total_bwd, high[:, None], low[:, None], pad], axis=1
-        ).astype(jnp.bfloat16)
-        upper = (mine // distance) % 2 == 1
-        if distance == 1:
-            payload, filler_args = lax.optimization_barrier((payload, filler_args))
-        if distance * 2 < size:
-            got = lax.ppermute(payload, axis, [(i, i ^ distance) for i in range(size)])
-            got = got.astype(jnp.float32)
-            got_fwd = got[:, :width]
-            got_bwd = got[:, width : 2 * width]
-        else:
-            last = jnp.where(upper, total_bwd, total_fwd).astype(jnp.bfloat16)
-            last = jnp.concatenate([last, payload[:, 2 * width :]], axis=1)
-            got = lax.ppermute(last, axis, [(i, i ^ distance) for i in range(size)])
-            got = got.astype(jnp.float32)
-            got_fwd = got[:, :width]
-            got_bwd = got_fwd
-            got = jnp.concatenate([got[:, :width], got], axis=1)
-        if distance == 1:
-            got, filler = lax.optimization_barrier((got, filler_fn(*filler_args)))
-        got_decay = got[:, 2 * width] + got[:, 2 * width + 1]
-        before = jnp.where(upper, before + before_decay[:, None] * got_fwd, before)
-        before_decay = jnp.where(upper, before_decay * got_decay, before_decay)
-        after = jnp.where(upper, after, after + after_decay[:, None] * got_bwd)
-        after_decay = jnp.where(upper, after_decay, after_decay * got_decay)
-        if distance * 2 < size:
-            total_fwd = jnp.where(
-                upper,
-                total_fwd + total_decay[:, None] * got_fwd,
-                got_fwd + got_decay[:, None] * total_fwd,
-            )
-            total_bwd = jnp.where(
-                upper,
-                got_bwd + got_decay[:, None] * total_bwd,
-                total_bwd + total_decay[:, None] * got_bwd,
-            )
-            total_decay = total_decay * got_decay
-        distance *= 2
+    heads = decay.shape[0]
+    if heads % chunks:
+        chunks = 1
+    step_heads = heads // chunks
+    parts = []
+    for c in range(chunks):
+        cut = slice(c * step_heads, (c + 1) * step_heads)
+        parts.append(
+            {
+                "decay": decay[cut],
+                "fwd": state[cut],
+                "bwd": state_grad[cut],
+                "before": jnp.zeros_like(state[cut]),
+                "before_decay": jnp.ones_like(decay[cut]),
+                "after": jnp.zeros_like(state_grad[cut]),
+                "after_decay": jnp.ones_like(decay[cut]),
+            }
+        )
+    rounds = size.bit_length() - 1
+    filler = None
+    for step in range(rounds + chunks - 1):
+        active = [c for c in range(chunks) if 0 <= step - c < rounds]
+        messages = []
+        for c in active:
+            distance = 2 ** (step - c)
+            upper = (mine // distance) % 2 == 1
+            messages.append(scan_message(parts[c], distance, size, upper))
+        if step == 0:
+            messages, filler_args = lax.optimization_barrier((messages, filler_args))
+        gots = []
+        for c, message in zip(active, messages):
+            distance = 2 ** (step - c)
+            gots.append(lax.ppermute(message, axis, [(i, i ^ distance) for i in range(size)]))
+        if step == 0:
+            gots, filler = lax.optimization_barrier((gots, filler_fn(*filler_args)))
+        elif len(gots) > 1:
+            gots = lax.optimization_barrier(gots)
+        for c, got in zip(active, gots):
+            distance = 2 ** (step - c)
+            upper = (mine // distance) % 2 == 1
+            parts[c] = scan_absorb(parts[c], got, distance, size, upper)
+    before = jnp.concatenate([p["before"] for p in parts], axis=0)
+    after = jnp.concatenate([p["after"] for p in parts], axis=0)
     return (before, after, filler)
 
 

time: 145 us -> 149 us (1.028)
  waiting for transfers between devices: 57.4 us -> 40.6 us
  local copies, waits for them, and re-layouts: 16.6 us -> 26.6 us
  starting transfers between devices: 36.1 us -> 41.7 us
  other arithmetic: 14 us -> 17.3 us
  matrix products: 16.6 us -> 18.4 us
    ppermute x3 -> x6, waiting for transfers between devices: 38.7 us -> 23.7 us  [both_scans(): lax.ppermute(message, axis, [(i, i ^ distance) for i in range(size)])]
    unnamed x144 -> x158, local copies, waits for them, and re-layouts: 4.32 us -> 10.1 us
    ppermute x3 -> x6, starting transfers between devices: 0.86 us -> 6.56 us  [both_scans(): lax.ppermute(message, axis, [(i, i ^ distance) for i in range(size)])]
    slice x0 -> x8, local copies, waits for them, and re-layouts: none -> 3.94 us  [the longest x3 2.44 us: both_scans(): state[cut]]
    broadcast_in_dim x0 -> x13, local copies, waits for them, and re-layouts: none -> 3.62 us  [scan_message(): tail = jnp.concatenate([high[:, None], low[:, None], pad], axis=1)]
    ppermute x14, waiting for transfers between devices: 11.7 us -> 9.47 us  [rotated(): return lax.ppermute(block, axis, route)]
    concatenate x3 -> x6, local copies, waits for them, and re-layouts: 1.46 us -> 3.45 us  [scan_message(): return jnp.concatenate(body + [tail], axis=1).astype(jnp.bfloat16)]
    reshape x2 -> x0, local copies, waits for them, and re-layouts: 1.92 us -> none  [the longest x1 1.59 us: shards(): state_grad = state_grad.reshape(heads_here, -1)]
  transfers between devices with their start and end apart: 21 -> 24, of which waited for: 11 -> 11; matrix products, arithmetic and copies ran while one was open for 15% -> 22% of each run, Pallas kernels for 0% -> 0%
where the time goes in v7:
time: 149 us; the launch traced here: 148 us
  starting transfers between devices  41.7 us (28%)
  waiting for transfers between devices  40.6 us (27%)
  local copies, waits for them, and re-layouts  26.6 us (18%)
  matrix products  18.4 us (12%)
  other arithmetic  17.3 us (12%)
  between operations  3.41 us (2%)
    ppermute x14, starting transfers between devices, rotated(): return lax.ppermute(block, axis, route)  29.4 us
    ppermute x6, waiting for transfers between devices, both_scans(): lax.ppermute(message, axis, [(i, i ^ distance) for i in range(size)])  23.7 us
    unnamed x158, local copies, waits for them, and re-layouts  10.1 us
    ppermute x14, waiting for transfers between devices, rotated(): return lax.ppermute(block, axis, route)  9.47 us
    dot_general x5, matrix products, contract(): return jnp.einsum(spec, left, right, preferred_element_type=jnp.float32)  7.51 us
    ppermute x2, waiting for transfers between devices, shifted(): return lax.ppermute(block, axis, route)  7.34 us
    ppermute x6, starting transfers between devices, both_scans(): lax.ppermute(message, axis, [(i, i ^ distance) for i in range(size)])  6.56 us
    ppermute x2, starting transfers between devices, shifted(): return lax.ppermute(block, axis, route)  5.6 us
  transfers between devices with their start and end apart: 24, of which 11 were waited for; matrix products, arithmetic and copies ran while one was open for 22% of the time, Pallas kernels for 0%

profile of v7, /device:TPU:4, one launch (start us, length us, event | category | flops | bytes accessed | tf_op | source)
XLA Modules:
  0.0 148.1 jit_solution(6314184455865043979)
XLA Ops:
  0.7 1.6 %collective-permute-start = (bf16[32,1792]{1,0:T(8,128)(2,1)}, bf16[32,1792]{1,0:T(8,128)(2,1)}, u32[]{:S(2)}, u32[]{:S(2)}) collective-permute-start(bf16[32,1792]{1,0:T(8,128)(2,1)} %bitcast.8), channel_id=1, source_target_pairs={{0,2},{2,4},{4,6},{6,8},{8,10},{10,12},{12,14},{14,0},{1,3},{3,5},... | collective-permute-start | bytes 344072 | tf_op jit(solution)/shard_map/ppermute | solution.py:18
  2.2 1.6 %collective-permute-start.1 = (bf16[32,1792]{1,0:T(8,128)(2,1)}, bf16[32,1792]{1,0:T(8,128)(2,1)}, u32[]{:S(2)}, u32[]{:S(2)}) collective-permute-start(bf16[32,1792]{1,0:T(8,128)(2,1)} %bitcast.8), channel_id=1, source_target_pairs={{0,4},{2,6},{4,8},{6,10},{8,12},{10,14},{12,0},{14,2},{1,5},{3,7},... | collective-permute-start | bytes 344072 | tf_op jit(solution)/shard_map/ppermute | solution.py:18
  3.8 2.5 %collective-permute-start.2 = (bf16[32,1792]{1,0:T(8,128)(2,1)}, bf16[32,1792]{1,0:T(8,128)(2,1)}, u32[]{:S(2)}, u32[]{:S(2)}) collective-permute-start(bf16[32,1792]{1,0:T(8,128)(2,1)} %bitcast.8), channel_id=1, source_target_pairs={{0,6},{2,8},{4,10},{6,12},{8,14},{10,0},{12,2},{14,4},{1,7},{3,9},... | collective-permute-start | bytes 344072 | tf_op jit(solution)/shard_map/ppermute | solution.py:18
  6.7 1.2 slice.238
  7.9 4.3 %collective-permute-start.8 = (s32[1]{0:T(128)}, s32[1]{0:T(128)}, u32[]{:S(2)}, u32[]{:S(2)}) collective-permute-start(s32[1]{0:T(128)} %bitcast.13), channel_id=1, source_target_pairs={{0,2},{2,4},{4,6},{6,8},{8,10},{10,12},{12,14},{1,3},{3,5},{5,7},{... | collective-permute-start | bytes 20 | tf_op jit(solution)/shard_map/ppermute | solution.py:12
  12.2 0.9 constant_dynamic-update-slice_fusion.7
  14.6 1.3 copy.119
  17.7 1.3 collective-permute-start.4
  19.0 1.3 broadcast_compare_fusion.1
  22.6 4.1 %collective-permute-start.5 = (bf16[32,1792]{1,0:T(8,128)(2,1)}, bf16[32,1792]{1,0:T(8,128)(2,1)S(1)}, u32[]{:S(2)}, u32[]{:S(2)}) collective-permute-start(bf16[32,1792]{1,0:T(8,128)(2,1)} %bitcast.8), channel_id=1, source_target_pairs={{0,12},{2,14},{4,0},{6,2},{8,4},{10,6},{12,8},{14,10},{1,13},{3,15... | collective-permute-start | bytes 344072 | tf_op jit(solution)/shard_map/ppermute | solution.py:18
  26.8 0.9 constant_dynamic-update-slice_fusion.6
  27.7 0.9 constant_dynamic-update-slice_fusion.5
  28.7 0.9 constant_dynamic-update-slice_fusion.4
  29.6 0.9 constant_dynamic-update-slice_fusion.3
  30.5 0.9 constant_dynamic-update-slice_fusion.2
  31.4 2.2 %collective-permute-done.6 = bf16[32,1792]{1,0:T(8,128)(2,1)S(1)} collective-permute-done((bf16[32,1792]{1,0:T(8,128)(2,1)}, bf16[32,1792]{1,0:T(8,128)(2,1)S(1)}, u32[]{:S(2)}, u32[]{:S(2)}) %collective-permute-start.6) | collective-permute-done | bytes 114720 | tf_op jit(solution)/shard_map/ppermute | solution.py:18
  37.9 0.8 fusion.132
  39.1 1.0 fusion.133
  41.4 1.5 %concatenate.86 = bf16[14,8320]{1,0:T(8,128)(2,1)} concatenate(bf16[14,4096]{1,0:T(8,128)(2,1)S(1)} %convert.92, bf16[14,4096]{1,0:T(8,128)(2,1)S(1)} %convert.93, bf16[14,1]{1,0:T(8,128)(2,1)} %copy.125, bf16[14,1]{1,0:T(8,128)(2,1)} %copy.126, bf16[14,126]{1,0:T(8,128)(2,1)S(1)} %broadcast.162), dimensions={1} | concatenate | bytes 465920 | tf_op jit(solution)/shard_map/concatenate | solution.py:131
  42.8 0.9 multiply_reduce_fusion.3
  45.3 2.7 %fusion.12 = (f32[28,128]{1,0:T(8,128)}, f32[28,128]{1,0:T(8,128)}, f32[28,128]{1,0:T(8,128)}, bf16[128,128]{1,0:T(8,128)(2,1)S(1)}) fusion(f32[28,128]{1,0:T(8,128)S(1)} %fusion.118, f32[128,128]{1,0:T(8,128)S(1)} %fusion.98, f32[128,128]{1,0:T(8,128)S(1)} %copy-done.24, f32[28,128]{1,0:T(8,128)S(1)} %fusion.74, pred[128,128]{1,0:T(8,128)(4,1)S(1)} %copy-done.33, ...), kind=kOutput, calls=%fused_computation.18 | convolution fusion | flops 66033152 | bytes 1628160 | tf_op jit(solution)/shard_map/transpose(jvp(hts,shp->thp))/dot_general | solution.py:33
  49.3 1.3 slice.255
  53.1 2.1 %collective-permute-start.9 = (bf16[14,8320]{1,0:T(8,128)(2,1)}, bf16[14,8320]{1,0:T(8,128)(2,1)S(1)}, u32[]{:S(2)}, u32[]{:S(2)}) collective-permute-start(bf16[14,8320]{1,0:T(8,128)(2,1)} %concatenate.86), channel_id=1, source_target_pairs={{0,2},{2,0},{4,6},{6,4},{8,10},{10,8},{12,14},{14,12},{1,3},{3,1},... | collective-permute-start | bytes 698888 | tf_op jit(solution)/shard_map/ppermute | solution.py:205
  56.4 2.6 %fusion.17 = bf16[128,28,64]{0,2,1:T(8,128)(2,1)} fusion(f32[128,28,64]{0,2,1:T(8,128)S(1)} %copy-done.7, f32[28,128]{1,0:T(8,128)} %copy-done.32, f32[128,128]{1,0:T(8,128)S(1)} %fusion.98, f32[128,128]{1,0:T(8,128)S(1)} %copy-done.25, f32[28,128]{1,0:T(8,128)} %copy-done.66, pred[128,128]{1,0:T(8,128)(4,1)} %get-tuple-element.135, ...), kind=kOutput, calls=%fused_computation.27 | convolution fusion | flops 63078400 | bytes 1574000 | tf_op jit(solution)/shard_map/transpose(jvp(hts,shp->thp))/dot_general | solution.py:33
  59.0 7.2 %collective-permute-done.9 = bf16[14,8320]{1,0:T(8,128)(2,1)S(1)} collective-permute-done((bf16[14,8320]{1,0:T(8,128)(2,1)}, bf16[14,8320]{1,0:T(8,128)(2,1)S(1)}, u32[]{:S(2)}, u32[]{:S(2)}) %collective-permute-start.9) | collective-permute-done | bytes 232992 | tf_op jit(solution)/shard_map/ppermute | solution.py:205
  67.0 7.9 %collective-permute-done.10 = bf16[14,8320]{1,0:T(8,128)(2,1)S(1)} collective-permute-done((bf16[14,8320]{1,0:T(8,128)(2,1)S(1)}, bf16[14,8320]{1,0:T(8,128)(2,1)S(1)}, u32[]{:S(2)}, u32[]{:S(2)}) %collective-permute-start.10) | collective-permute-done | bytes 232992 | tf_op jit(solution)/shard_map/ppermute | solution.py:205
  75.0 1.1 convert_element_type.289
  77.8 1.0 convert_element_type.286
  79.6 2.1 %collective-permute-start.12 = (bf16[14,4224]{1,0:T(8,128)(2,1)S(1)}, bf16[14,4224]{1,0:T(8,128)(2,1)S(1)}, u32[]{:S(2)}, u32[]{:S(2)}) collective-permute-start(bf16[14,4224]{1,0:T(8,128)(2,1)S(1)} %concatenate.89), channel_id=1, source_target_pairs={{0,8},{2,10},{4,12},{6,14},{8,0},{10,2},{12,4},{14,6},{1,9},{3,11}... | collective-permute-start | bytes 354824 | tf_op jit(solution)/shard_map/ppermute | solution.py:205
  81.7 1.0 bitcast_multiply_fusion
  82.7 4.0 %collective-permute-done.12 = bf16[14,4224]{1,0:T(8,128)(2,1)S(1)} collective-permute-done((bf16[14,4224]{1,0:T(8,128)(2,1)S(1)}, bf16[14,4224]{1,0:T(8,128)(2,1)S(1)}, u32[]{:S(2)}, u32[]{:S(2)}) %collective-permute-start.12) | collective-permute-done | bytes 118304 | tf_op jit(solution)/shard_map/ppermute | solution.py:205
  87.9 1.0 convert_element_type.292
  89.7 2.1 %collective-permute-start.14 = (bf16[14,4224]{1,0:T(8,128)(2,1)S(1)}, bf16[14,4224]{1,0:T(8,128)(2,1)S(1)}, u32[]{:S(2)}, u32[]{:S(2)}) collective-permute-start(bf16[14,4224]{1,0:T(8,128)(2,1)S(1)} %concatenate.91), channel_id=1, source_target_pairs={{0,8},{2,10},{4,12},{6,14},{8,0},{10,2},{12,4},{14,6},{1,9},{3,11}... | collective-permute-start | bytes 354824 | tf_op jit(solution)/shard_map/ppermute | solution.py:205
  91.7 1.1 add_select_fusion.6
  92.8 4.2 %collective-permute-done.14 = bf16[14,4224]{1,0:T(8,128)(2,1)S(1)} collective-permute-done((bf16[14,4224]{1,0:T(8,128)(2,1)S(1)}, bf16[14,4224]{1,0:T(8,128)(2,1)S(1)}, u32[]{:S(2)}, u32[]{:S(2)}) %collective-permute-start.14) | collective-permute-done | bytes 118304 | tf_op jit(solution)/shard_map/ppermute | solution.py:205
  101.8 0.8 fusion.141
  102.9 1.0 fusion.21
  104.2 1.6 %fusion.22 = f32[128,28,64]{0,2,1:T(8,128)S(1)} fusion(bf16[128,28,64]{0,2,1:T(8,128)(2,1)} %fusion.17, f32[28,64]{1,0:T(8,128)S(1)} %copy-done.31, f32[28,128]{1,0:T(8,128)S(1)} %copy.140, f32[28,128]{1,0:T(8,128)S(1)} %copy.145, bf16[28,64,64]{2,1,0:T(8,128)(2,1)S(1)} %copy-done.17, f32[128,64]{0,1:T(8,128)S(1)} %copy-done.20, f32[128,28]{0,1:T(8,128)S(1)} %copy-done.23), kind=kOutput, calls=%fused_computation.37 | convolution fusion | flops 32112640 | bytes 1688576 | tf_op jit(solution)/shard_map/transpose(jvp(thn,thp->hnp))/dot_general | solution.py:33
  106.1 1.8 %fusion.135 = (bf16[256,1792]{1,0:T(8,128)(2,1)S(1)}, f32[256,1792]{1,0:T(8,128)}) fusion(bf16[1,128,1792]{2,1,0:T(8,128)(2,1)S(1)} %copy-done.5, s32[]{:T(128)S(6)} %select_n.316, bf16[128,256]{0,1:T(8,128)(2,1)S(1)} %maximum_select_fusion), kind=kOutput, calls=%fused_computation.315 | convolution fusion | flops 118030336 | bytes 3276804 | tf_op jit(solution)/shard_map/dot_general | solution.py:320
  108.8 1.8 %collective-permute-start.22 = (bf16[36,1792]{1,0:T(8,128)(2,1)}, bf16[36,1792]{1,0:T(8,128)(2,1)S(1)}, u32[]{:S(2)}, u32[]{:S(2)}) collective-permute-start(bf16[36,1792]{1,0:T(8,128)(2,1)} %get-tuple-element.122), channel_id=1, source_target_pairs={{0,12},{2,14},{4,0},{6,2},{8,4},{10,6},{12,8},{14,10},{1,13},{3,15... | collective-permute-start | bytes 387080 | tf_op jit(solution)/shard_map/ppermute | solution.py:18
  112.0 1.5 collective-permute-start.21
  113.5 2.2 %collective-permute-start.20 = (bf16[36,1792]{1,0:T(8,128)(2,1)}, bf16[36,1792]{1,0:T(8,128)(2,1)S(1)}, u32[]{:S(2)}, u32[]{:S(2)}) collective-permute-start(bf16[36,1792]{1,0:T(8,128)(2,1)} %get-tuple-element.120), channel_id=1, source_target_pairs={{0,8},{2,10},{4,12},{6,14},{8,0},{10,2},{12,4},{14,6},{1,9},{3,11}... | collective-permute-start | bytes 387080 | tf_op jit(solution)/shard_map/ppermute | solution.py:18
  116.4 3.6 %collective-permute-done.23 = bf16[36,1792]{1,0:T(8,128)(2,1)S(1)} collective-permute-done((bf16[36,1792]{1,0:T(8,128)(2,1)}, bf16[36,1792]{1,0:T(8,128)(2,1)S(1)}, u32[]{:S(2)}, u32[]{:S(2)}) %collective-permute-start.23) | collective-permute-done | bytes 129056 | tf_op jit(solution)/shard_map/ppermute | solution.py:18
  120.0 11.5 %collective-permute-start.18 = (bf16[36,1792]{1,0:T(8,128)(2,1)S(1)}, bf16[36,1792]{1,0:T(8,128)(2,1)S(1)}, u32[]{:S(2)}, u32[]{:S(2)}) collective-permute-start(bf16[36,1792]{1,0:T(8,128)(2,1)S(1)} %get-tuple-element.118), channel_id=1, source_target_pairs={{0,4},{2,6},{4,8},{6,10},{8,12},{10,14},{12,0},{14,2},{1,5},{3,7},... | collective-permute-start | bytes 387080 | tf_op jit(solution)/shard_map/ppermute | solution.py:18
  131.6 2.4 %collective-permute-done.21 = bf16[36,1792]{1,0:T(8,128)(2,1)S(1)} collective-permute-done((bf16[36,1792]{1,0:T(8,128)(2,1)}, bf16[36,1792]{1,0:T(8,128)(2,1)S(1)}, u32[]{:S(2)}, u32[]{:S(2)}) %collective-permute-start.21) | collective-permute-done | bytes 129056 | tf_op jit(solution)/shard_map/ppermute | solution.py:18
  134.0 1.3 collective-permute-start.16
  137.0 1.8 %fusion.51 = f32[1,32,1792]{2,1,0:T(8,128)} fusion(f32[256,1792]{1,0:T(8,128)} %get-tuple-element.141, bf16[36,1792]{1,0:T(8,128)(2,1)S(1)} %collective-permute-done.23, bf16[36,1792]{1,0:T(8,128)(2,1)S(1)} %collective-permute-done.22, bf16[36,1792]{1,0:T(8,128)(2,1)S(1)} %collective-permute-done.21, bf16[36,1792]{1,0:T(8,128)(2,1)S(1)} %collective-permute-done.20, ...), kind=kLoop, calls=%fused_computation.115 | loop fusion | flops 802816 | bytes 1261568 | tf_op jit(solution)/shard_map/broadcast_in_dim | solution.py:360
  140.0 7.3 %collective-permute-done.16 = bf16[1,128,1792]{2,1,0:T(8,128)(2,1)S(1)} collective-permute-done((bf16[1,128,1792]{2,1,0:T(8,128)(2,1)S(1)}, bf16[1,128,1792]{2,1,0:T(8,128)(2,1)S(1)}, u32[]{:S(2)}, u32[]{:S(2)}) %collective-permute-start.16) | collective-permute-done | bytes 458784 | tf_op jit(solution)/shard_map/ppermute | solution.py:12
  (299 shorter events, 33.8 us)
Async XLA Ops:
  0.6 15.9 %copy-start.50 = (f32[1,28]{1,0:T(1,128)S(1)}, f32[1,28]{1,0:T(1,128)}, u32[]{:S(2)}) copy-start(f32[1,28]{1,0:T(1,128)} %param.15) | copy-start | bytes 340
  0.6 15.9 %copy-start.15 = (bf16[1,128,1792]{2,1,0:T(8,128)(2,1)S(1)}, bf16[1,128,1792]{2,1,0:T(8,128)(2,1)}, u32[]{:S(2)}) copy-start(bf16[1,128,1792]{2,1,0:T(8,128)(2,1)} %param.11) | copy-start | bytes 1376260
  0.7 22.0 %collective-permute-start = (bf16[32,1792]{1,0:T(8,128)(2,1)}, bf16[32,1792]{1,0:T(8,128)(2,1)}, u32[]{:S(2)}, u32[]{:S(2)}) collective-permute-start(bf16[32,1792]{1,0:T(8,128)(2,1)} %bitcast.8), channel_id=1, source_target_pairs={{0,2},{2,4},{4,6},{6,8},{8,10},{10,12},{12,14},{14,0},{1,3},{3,5},... | collective-permute-start | bytes 344072 | tf_op jit(solution)/shard_map/ppermute | solution.py:18
  2.2 25.4 %collective-permute-start.1 = (bf16[32,1792]{1,0:T(8,128)(2,1)}, bf16[32,1792]{1,0:T(8,128)(2,1)}, u32[]{:S(2)}, u32[]{:S(2)}) collective-permute-start(bf16[32,1792]{1,0:T(8,128)(2,1)} %bitcast.8), channel_id=1, source_target_pairs={{0,4},{2,6},{4,8},{6,10},{8,12},{10,14},{12,0},{14,2},{1,5},{3,7},... | collective-permute-start | bytes 344072 | tf_op jit(solution)/shard_map/ppermute | solution.py:18
  3.8 24.9 %collective-permute-start.2 = (bf16[32,1792]{1,0:T(8,128)(2,1)}, bf16[32,1792]{1,0:T(8,128)(2,1)}, u32[]{:S(2)}, u32[]{:S(2)}) collective-permute-start(bf16[32,1792]{1,0:T(8,128)(2,1)} %bitcast.8), channel_id=1, source_target_pairs={{0,6},{2,8},{4,10},{6,12},{8,14},{10,0},{12,2},{14,4},{1,7},{3,9},... | collective-permute-start | bytes 344072 | tf_op jit(solution)/shard_map/ppermute | solution.py:18
  6.3 23.2 %collective-permute-start.3 = (bf16[32,1792]{1,0:T(8,128)(2,1)}, bf16[32,1792]{1,0:T(8,128)(2,1)}, u32[]{:S(2)}, u32[]{:S(2)}) collective-permute-start(bf16[32,1792]{1,0:T(8,128)(2,1)} %bitcast.8), channel_id=1, source_target_pairs={{0,8},{2,10},{4,12},{6,14},{8,0},{10,2},{12,4},{14,6},{1,9},{3,11}... | collective-permute-start | bytes 344072 | tf_op jit(solution)/shard_map/ppermute | solution.py:18
  7.9 9.8 %collective-permute-start.8 = (s32[1]{0:T(128)}, s32[1]{0:T(128)}, u32[]{:S(2)}, u32[]{:S(2)}) collective-permute-start(s32[1]{0:T(128)} %bitcast.13), channel_id=1, source_target_pairs={{0,2},{2,4},{4,6},{6,8},{8,10},{10,12},{12,14},{1,3},{3,5},{5,7},{... | collective-permute-start | bytes 20 | tf_op jit(solution)/shard_map/ppermute | solution.py:12
  14.6 6.9 %copy-start.36 = (f32[1,28]{1,0:T(1,128)S(1)}, f32[1,28]{1,0:T(1,128)}, u32[]{:S(2)}) copy-start(f32[1,28]{1,0:T(1,128)} %param.14) | copy-start | bytes 340
  15.9 36.4 %copy-start.2 = (bf16[1,128,1792]{1,2,0:T(8,128)(2,1)}, bf16[1,128,1792]{1,2,0:T(8,128)(2,1)S(1)}, u32[]{:S(2)}) copy-start(bf16[1,128,1792]{1,2,0:T(8,128)(2,1)S(1)} %copy.119) | copy-start | bytes 1376260
  16.5 14.0 %copy-start.13 = (f32[28,1,128]{0,2,1:T(8,128)}, f32[28,1,128]{0,2,1:T(8,128)S(1)}, u32[]{:S(2)}) copy-start(f32[28,1,128]{0,2,1:T(8,128)S(1)} %copy.150) | copy-start | bytes 43012
  16.6 5.4 %copy-start.59 = (f32[28]{0:T(128)}, f32[28]{0:T(128)S(1)}, u32[]{:S(2)}) copy-start(f32[28]{0:T(128)S(1)} %negate_bitcast_fusion) | copy-start | bytes 340
  16.8 16.8 %copy-start.4 = (bf16[1,128,1792]{2,1,0:T(8,128)(2,1)S(1)}, bf16[1,128,1792]{2,1,0:T(8,128)(2,1)}, u32[]{:S(2)}) copy-start(bf16[1,128,1792]{2,1,0:T(8,128)(2,1)} %param.9) | copy-start | bytes 1376260
  16.9 28.3 %copy-start.6 = (f32[128,28,64]{0,2,1:T(8,128)}, f32[128,28,64]{0,2,1:T(8,128)S(1)}, u32[]{:S(2)}) copy-start(f32[128,28,64]{0,2,1:T(8,128)S(1)} %convert.124) | copy-start | bytes 2752516
  17.7 12.8 %collective-permute-start.4 = (bf16[32,1792]{1,0:T(8,128)(2,1)}, bf16[32,1792]{1,0:T(8,128)(2,1)}, u32[]{:S(2)}, u32[]{:S(2)}) collective-permute-start(bf16[32,1792]{1,0:T(8,128)(2,1)} %bitcast.8), channel_id=1, source_target_pairs={{0,10},{2,12},{4,14},{6,0},{8,2},{10,4},{12,6},{14,8},{1,11},{3,13... | collective-permute-start | bytes 344072 | tf_op jit(solution)/shard_map/ppermute | solution.py:18
  20.3 13.8 %copy-start.42 = (pred[128]{0:T(512)(128)(4,1)}, pred[128]{0:T(512)(128)(4,1)S(1)}, u32[]{:S(2)}) copy-start(pred[128]{0:T(512)(128)(4,1)S(1)} %get-tuple-element.86) | copy-start | bytes 388
  20.3 13.8 %copy-start.44 = (f32[128]{0:T(128)}, f32[128]{0:T(128)S(1)}, u32[]{:S(2)}) copy-start(f32[128]{0:T(128)S(1)} %get-tuple-element.87) | copy-start | bytes 1540
  21.8 12.3 %copy-start.28 = (f32[128,28]{0,1:T(8,128)}, f32[128,28]{0,1:T(8,128)S(1)}, u32[]{:S(2)}) copy-start(f32[128,28]{0,1:T(8,128)S(1)} %get-tuple-element.139) | copy-start | bytes 43012
  22.0 12.2 %copy-start.11 = (f32[128,28]{1,0:T(8,128)}, f32[128,28]{1,0:T(8,128)S(1)}, u32[]{:S(2)}) copy-start(f32[128,28]{1,0:T(8,128)S(1)} %copy.120) | copy-start | bytes 43012
  22.0 12.1 %copy-start.48 = (f32[28]{0:T(128)}, f32[28]{0:T(128)S(1)}, u32[]{:S(2)}) copy-start(f32[28]{0:T(128)S(1)} %slice_bitcast_fusion.11) | copy-start | bytes 340
  22.6 8.8 %collective-permute-start.5 = (bf16[32,1792]{1,0:T(8,128)(2,1)}, bf16[32,1792]{1,0:T(8,128)(2,1)S(1)}, u32[]{:S(2)}, u32[]{:S(2)}) collective-permute-start(bf16[32,1792]{1,0:T(8,128)(2,1)} %bitcast.8), channel_id=1, source_target_pairs={{0,12},{2,14},{4,0},{6,2},{8,4},{10,6},{12,8},{14,10},{1,13},{3,15... | collective-permute-start | bytes 344072 | tf_op jit(solution)/shard_map/ppermute | solution.py:18
  27.7 6.0 %collective-permute-start.6 = (bf16[32,1792]{1,0:T(8,128)(2,1)}, bf16[32,1792]{1,0:T(8,128)(2,1)S(1)}, u32[]{:S(2)}, u32[]{:S(2)}) collective-permute-start(bf16[32,1792]{1,0:T(8,128)(2,1)} %bitcast.8), channel_id=1, source_target_pairs={{0,14},{2,0},{4,2},{6,4},{8,6},{10,8},{12,10},{14,12},{1,15},{3,1}... | collective-permute-start | bytes 344072 | tf_op jit(solution)/shard_map/ppermute | solution.py:18
  33.6 4.2 %copy-start = (bf16[256,1792]{1,0:T(8,128)(2,1)}, bf16[256,1792]{1,0:T(8,128)(2,1)S(1)}, u32[]{:S(2)}) copy-start(bf16[256,1792]{1,0:T(8,128)(2,1)S(1)} %constant_dynamic-update-slice_fusion) | copy-start | bytes 2752516
  34.2 3.0 %collective-permute-start.7 = (bf16[128,128]{0,1:T(8,128)(2,1)S(1)}, bf16[128,128]{0,1:T(8,128)(2,1)S(1)}, u32[]{:S(2)}, u32[]{:S(2)}) collective-permute-start(bf16[128,128]{0,1:T(8,128)(2,1)S(1)} %fusion.58), channel_id=1, source_target_pairs={{0,1},{1,0},{2,3},{3,2},{4,5},{5,4},{6,7},{7,6},{8,9},{9,8},{10,11... | collective-permute-start | bytes 98312 | tf_op jit(solution)/shard_map/ppermute | solution.py:29
  34.4 4.7 %copy-start.22 = (f32[128,28]{0,1:T(8,128)}, f32[128,28]{0,1:T(8,128)S(1)}, u32[]{:S(2)}) copy-start(f32[128,28]{0,1:T(8,128)S(1)} %copy.122) | copy-start | bytes 43012
  41.2 4.1 %copy-start.24 = (f32[128,128]{1,0:T(8,128)S(1)}, f32[128,128]{1,0:T(8,128)}, u32[]{:S(2)}) copy-start(f32[128,128]{1,0:T(8,128)} %get-tuple-element.136) | copy-start | bytes 196612
  41.2 4.1 %copy-start.33 = (pred[128,128]{1,0:T(8,128)(4,1)S(1)}, pred[128,128]{1,0:T(8,128)(4,1)}, u32[]{:S(2)}) copy-start(pred[128,128]{1,0:T(8,128)(4,1)} %get-tuple-element.135) | copy-start | bytes 49156
  49.1 6.8 %copy-start.52 = (f32[1,28]{1,0:T(1,128)S(1)}, f32[1,28]{1,0:T(1,128)}, u32[]{:S(2)}) copy-start(f32[1,28]{1,0:T(1,128)} %param.15) | copy-start | bytes 340
  49.1 6.8 %copy-start.55 = (f32[1,28]{1,0:T(1,128)S(1)}, f32[1,28]{1,0:T(1,128)}, u32[]{:S(2)}) copy-start(f32[1,28]{1,0:T(1,128)} %param.16) | copy-start | bytes 340
  49.1 7.3 %copy-start.7 = (f32[128,28,64]{0,2,1:T(8,128)S(1)}, f32[128,28,64]{0,2,1:T(8,128)}, u32[]{:S(2)}) copy-start(f32[128,28,64]{0,2,1:T(8,128)} %copy-done.6) | copy-start | bytes 2752516
  49.1 7.3 %copy-start.25 = (f32[128,128]{1,0:T(8,128)S(1)}, f32[128,128]{1,0:T(8,128)}, u32[]{:S(2)}) copy-start(f32[128,128]{1,0:T(8,128)} %get-tuple-element.136) | copy-start | bytes 196612
  51.5 15.6 %collective-permute-start.11 = (bf16[14,8320]{1,0:T(8,128)(2,1)}, bf16[14,8320]{1,0:T(8,128)(2,1)}, u32[]{:S(2)}, u32[]{:S(2)}) collective-permute-start(bf16[14,8320]{1,0:T(8,128)(2,1)} %concatenate.88), channel_id=1, source_target_pairs={{0,2},{2,0},{4,6},{6,4},{8,10},{10,8},{12,14},{14,12},{1,3},{3,1},... | collective-permute-start | bytes 698888 | tf_op jit(solution)/shard_map/ppermute | solution.py:205
  53.1 13.1 %collective-permute-start.9 = (bf16[14,8320]{1,0:T(8,128)(2,1)}, bf16[14,8320]{1,0:T(8,128)(2,1)S(1)}, u32[]{:S(2)}, u32[]{:S(2)}) collective-permute-start(bf16[14,8320]{1,0:T(8,128)(2,1)} %concatenate.86), channel_id=1, source_target_pairs={{0,2},{2,0},{4,6},{6,4},{8,10},{10,8},{12,14},{14,12},{1,3},{3,1},... | collective-permute-start | bytes 698888 | tf_op jit(solution)/shard_map/ppermute | solution.py:205
  56.4 10.2 %copy-start.40 = (f32[14]{0:T(128)S(1)}, f32[14]{0:T(128)}, u32[]{:S(2)}) copy-start(f32[14]{0:T(128)} %get-tuple-element.132) | copy-start | bytes 172
  66.9 12.2 %copy-start.41 = (f32[14]{0:T(128)S(1)}, f32[14]{0:T(128)}, u32[]{:S(2)}) copy-start(f32[14]{0:T(128)} %get-tuple-element.132) | copy-start | bytes 172
  66.9 8.1 %collective-permute-start.10 = (bf16[14,8320]{1,0:T(8,128)(2,1)S(1)}, bf16[14,8320]{1,0:T(8,128)(2,1)S(1)}, u32[]{:S(2)}, u32[]{:S(2)}) collective-permute-start(bf16[14,8320]{1,0:T(8,128)(2,1)S(1)} %concatenate.87), channel_id=1, source_target_pairs={{0,4},{2,6},{4,0},{6,2},{8,12},{10,14},{12,8},{14,10},{1,5},{3,7},... | collective-permute-start | bytes 698888 | tf_op jit(solution)/shard_map/ppermute | solution.py:205
  77.5 10.3 %collective-permute-start.13 = (bf16[14,8320]{1,0:T(8,128)(2,1)}, bf16[14,8320]{1,0:T(8,128)(2,1)}, u32[]{:S(2)}, u32[]{:S(2)}) collective-permute-start(bf16[14,8320]{1,0:T(8,128)(2,1)} %concatenate.90), channel_id=1, source_target_pairs={{0,4},{2,6},{4,0},{6,2},{8,12},{10,14},{12,8},{14,10},{1,5},{3,7},... | collective-permute-start | bytes 698888 | tf_op jit(solution)/shard_map/ppermute | solution.py:205
  79.6 7.1 %collective-permute-start.12 = (bf16[14,4224]{1,0:T(8,128)(2,1)S(1)}, bf16[14,4224]{1,0:T(8,128)(2,1)S(1)}, u32[]{:S(2)}, u32[]{:S(2)}) collective-permute-start(bf16[14,4224]{1,0:T(8,128)(2,1)S(1)} %concatenate.89), channel_id=1, source_target_pairs={{0,8},{2,10},{4,12},{6,14},{8,0},{10,2},{12,4},{14,6},{1,9},{3,11}... | collective-permute-start | bytes 354824 | tf_op jit(solution)/shard_map/ppermute | solution.py:205
  89.7 7.4 %collective-permute-start.14 = (bf16[14,4224]{1,0:T(8,128)(2,1)S(1)}, bf16[14,4224]{1,0:T(8,128)(2,1)S(1)}, u32[]{:S(2)}, u32[]{:S(2)}) collective-permute-start(bf16[14,4224]{1,0:T(8,128)(2,1)S(1)} %concatenate.91), channel_id=1, source_target_pairs={{0,8},{2,10},{4,12},{6,14},{8,0},{10,2},{12,4},{14,6},{1,9},{3,11}... | collective-permute-start | bytes 354824 | tf_op jit(solution)/shard_map/ppermute | solution.py:205
  103.9 2.1 %collective-permute-start.15 = (bf16[128,128]{0,1:T(8,128)(2,1)S(1)}, bf16[128,128]{0,1:T(8,128)(2,1)S(1)}, u32[]{:S(2)}, u32[]{:S(2)}) collective-permute-start(bf16[128,128]{0,1:T(8,128)(2,1)S(1)} %add_convert_fusion), channel_id=1, source_target_pairs={{0,1},{1,0},{2,3},{3,2},{4,5},{5,4},{6,7},{7,6},{8,9},{9,8},{10,11... | collective-permute-start | bytes 98312 | tf_op jit(solution)/shard_map/ppermute | solution.py:29
  107.9 8.2 %copy-start.1 = (bf16[256,1792]{1,0:T(8,128)(2,1)S(1)}, bf16[256,1792]{1,0:T(8,128)(2,1)}, u32[]{:S(2)}) copy-start(bf16[256,1792]{1,0:T(8,128)(2,1)} %copy-done) | copy-start | bytes 2752516
  108.8 22.7 %collective-permute-start.22 = (bf16[36,1792]{1,0:T(8,128)(2,1)}, bf16[36,1792]{1,0:T(8,128)(2,1)S(1)}, u32[]{:S(2)}, u32[]{:S(2)}) collective-permute-start(bf16[36,1792]{1,0:T(8,128)(2,1)} %get-tuple-element.122), channel_id=1, source_target_pairs={{0,12},{2,14},{4,0},{6,2},{8,4},{10,6},{12,8},{14,10},{1,13},{3,15... | collective-permute-start | bytes 387080 | tf_op jit(solution)/shard_map/ppermute | solution.py:18
  111.3 8.7 %collective-permute-start.23 = (bf16[36,1792]{1,0:T(8,128)(2,1)}, bf16[36,1792]{1,0:T(8,128)(2,1)S(1)}, u32[]{:S(2)}, u32[]{:S(2)}) collective-permute-start(bf16[36,1792]{1,0:T(8,128)(2,1)} %pad_maximum_fusion.2), channel_id=1, source_target_pairs={{0,14},{2,0},{4,2},{6,4},{8,6},{10,8},{12,10},{14,12},{1,15},{3,1}... | collective-permute-start | bytes 387080 | tf_op jit(solution)/shard_map/ppermute | solution.py:18
  112.0 22.0 %collective-permute-start.21 = (bf16[36,1792]{1,0:T(8,128)(2,1)}, bf16[36,1792]{1,0:T(8,128)(2,1)S(1)}, u32[]{:S(2)}, u32[]{:S(2)}) collective-permute-start(bf16[36,1792]{1,0:T(8,128)(2,1)} %get-tuple-element.121), channel_id=1, source_target_pairs={{0,10},{2,12},{4,14},{6,0},{8,2},{10,4},{12,6},{14,8},{1,11},{3,13... | collective-permute-start | bytes 387080 | tf_op jit(solution)/shard_map/ppermute | solution.py:18
  113.5 22.4 %collective-permute-start.20 = (bf16[36,1792]{1,0:T(8,128)(2,1)}, bf16[36,1792]{1,0:T(8,128)(2,1)S(1)}, u32[]{:S(2)}, u32[]{:S(2)}) collective-permute-start(bf16[36,1792]{1,0:T(8,128)(2,1)} %get-tuple-element.120), channel_id=1, source_target_pairs={{0,8},{2,10},{4,12},{6,14},{8,0},{10,2},{12,4},{14,6},{1,9},{3,11}... | collective-permute-start | bytes 387080 | tf_op jit(solution)/shard_map/ppermute | solution.py:18
  115.7 20.2 %collective-permute-start.19 = (bf16[36,1792]{1,0:T(8,128)(2,1)}, bf16[36,1792]{1,0:T(8,128)(2,1)S(1)}, u32[]{:S(2)}, u32[]{:S(2)}) collective-permute-start(bf16[36,1792]{1,0:T(8,128)(2,1)} %get-tuple-element.119), channel_id=1, source_target_pairs={{0,6},{2,8},{4,10},{6,12},{8,14},{10,0},{12,2},{14,4},{1,7},{3,9},... | collective-permute-start | bytes 387080 | tf_op jit(solution)/shard_map/ppermute | solution.py:18
  120.0 15.9 %collective-permute-start.18 = (bf16[36,1792]{1,0:T(8,128)(2,1)S(1)}, bf16[36,1792]{1,0:T(8,128)(2,1)S(1)}, u32[]{:S(2)}, u32[]{:S(2)}) collective-permute-start(bf16[36,1792]{1,0:T(8,128)(2,1)S(1)} %get-tuple-element.118), channel_id=1, source_target_pairs={{0,4},{2,6},{4,8},{6,10},{8,12},{10,14},{12,0},{14,2},{1,5},{3,7},... | collective-permute-start | bytes 387080 | tf_op jit(solution)/shard_map/ppermute | solution.py:18
  131.5 5.2 %collective-permute-start.17 = (bf16[36,1792]{1,0:T(8,128)(2,1)S(1)}, bf16[36,1792]{1,0:T(8,128)(2,1)S(1)}, u32[]{:S(2)}, u32[]{:S(2)}) collective-permute-start(bf16[36,1792]{1,0:T(8,128)(2,1)S(1)} %get-tuple-element.117), channel_id=1, source_target_pairs={{0,2},{2,4},{4,6},{6,8},{8,10},{10,12},{12,14},{14,0},{1,3},{3,5},... | collective-permute-start | bytes 387080 | tf_op jit(solution)/shard_map/ppermute | solution.py:18
  134.0 13.3 %collective-permute-start.16 = (bf16[1,128,1792]{2,1,0:T(8,128)(2,1)S(1)}, bf16[1,128,1792]{2,1,0:T(8,128)(2,1)S(1)}, u32[]{:S(2)}, u32[]{:S(2)}) collective-permute-start(bf16[1,128,1792]{2,1,0:T(8,128)(2,1)S(1)} %fusion.1), channel_id=1, source_target_pairs={{16,0},{17,1},{18,2},{19,3},{20,4},{21,5},{22,6},{23,7},{24,8},{25... | collective-permute-start | bytes 1376264 | tf_op jit(solution)/shard_map/ppermute | solution.py:12
  (43 other events, 92.9 us)

commit v8 on v5

--- a/solution.py
+++ b/solution.py
@@ -192,12 +192,20 @@
     rate_heads = rate_log[0]
     skip_heads = skip_gain[0]
     docs_bwd = bwd_docs[0]
-    doc_before = shifted(docs_bwd[-1:], "seq", 1)[0]
     size, mine = (lax.axis_size("seq"), lax.axis_index("seq"))
     group = lax.axis_index("head")
     own_rows = proj_weight[0]
+    last_doc = docs_bwd[-1]
+    doc_digits = jnp.stack([last_doc // 256, last_doc % 256]).astype(jnp.bfloat16)
+    doc_column = jnp.zeros((own_rows.shape[0], 128), jnp.bfloat16)
+    doc_column = doc_column.at[:2, 0].set(doc_digits)
+    first = rotated(jnp.concatenate([own_rows, doc_column], axis=1), "seq", 1)
+    got_digits = first[:2, own_rows.shape[1]].astype(jnp.int32)
+    doc_before = jnp.where(mine == 0, 0, got_digits[0] * 256 + got_digits[1])
     slot_weight = jnp.concatenate(
-        [own_rows] + [rotated(own_rows, "seq", k) for k in range(1, size)], axis=0
+        [own_rows, first[:, : own_rows.shape[1]]]
+        + [rotated(own_rows, "seq", k) for k in range(2, size)],
+        axis=0,
     )
     slot_value = jnp.dot(bwd_flat, slot_weight.T, preferred_element_type=jnp.float32)
     slot_value = slot_value.reshape(tokens, size, -1)[:, ::-1].reshape(tokens, -1)

time: 145 us -> 155 us (1.069)
  other arithmetic: 14 us -> 21.2 us
  local copies, waits for them, and re-layouts: 16.6 us -> 22.4 us
  waiting for transfers between devices: 57.4 us -> 53.4 us
  between operations: 3.31 us -> 6.36 us
  starting transfers between devices: 36.1 us -> 34.1 us
    ppermute x2 -> x1, starting transfers between devices: 5.6 us -> 1.28 us  [shifted(): return lax.ppermute(block, axis, route)]
    unnamed x144 -> x132, local copies, waits for them, and re-layouts: 4.32 us -> 6.84 us
    ppermute x14, waiting for transfers between devices: 11.7 us -> 9.83 us  [rotated(): return lax.ppermute(block, axis, route)]
    ppermute x14, starting transfers between devices: 29.5 us -> 31.3 us  [rotated(): return lax.ppermute(block, axis, route)]
    ppermute x2 -> x1, waiting for transfers between devices: 7 us -> 7.02 us  [shifted(): return lax.ppermute(block, axis, route)]
  transfers between devices with their start and end apart: 21 -> 20, of which waited for: 11 -> 10; matrix products, arithmetic and copies ran while one was open for 15% -> 16% of each run, Pallas kernels for 0% -> 0%
where the time goes in v8:
time: 155 us
  waiting for transfers between devices  53.4 us (34%)
  starting transfers between devices  34.1 us (22%)
  local copies, waits for them, and re-layouts  22.4 us (14%)
  other arithmetic  21.2 us (14%)
  matrix products  17.2 us (11%)
  between operations  6.36 us (4%)
    ppermute x14, starting transfers between devices, rotated(): return lax.ppermute(block, axis, route)  31.3 us
    ppermute x2, waiting for transfers between devices, both_scans(): got = lax.ppermute(payload, axis, [(i, i ^ distance) for i in range(size)])  25 us
    ppermute x1, waiting for transfers between devices, both_scans(): got = lax.ppermute(last, axis, [(i, i ^ distance) for i in range(size)])  11.5 us
    ppermute x14, waiting for transfers between devices, rotated(): return lax.ppermute(block, axis, route)  9.83 us
    ppermute x1, waiting for transfers between devices, shifted(): return lax.ppermute(block, axis, route)  7.02 us
    dot_general x5, matrix products, contract(): return jnp.einsum(spec, left, right, preferred_element_type=jnp.float32)  6.89 us
    unnamed x132, local copies, waits for them, and re-layouts  6.84 us
    dot_general x5, matrix products, local_setup(): jnp.einsum('thp,hp->th', values.astype(jnp.float32), step_weight, precisi...  3.41 us
  transfers between devices with their start and end apart: 20, of which 10 were waited for; matrix products, arithmetic and copies ran while one was open for 16% of the time, Pallas kernels for 0%

profile of v8, /device:TPU:4, one launch (start us, length us, event | category | flops | bytes accessed | tf_op | source)
XLA Modules:
  0.0 154.6 jit_solution(7967292296707327489)
XLA Ops:
  0.6 1.6 %collective-permute-start.1 = (bf16[32,1792]{1,0:T(8,128)(2,1)}, bf16[32,1792]{1,0:T(8,128)(2,1)}, u32[]{:S(2)}, u32[]{:S(2)}) collective-permute-start(bf16[32,1792]{1,0:T(8,128)(2,1)} %bitcast.344), channel_id=1, source_target_pairs={{0,4},{2,6},{4,8},{6,10},{8,12},{10,14},{12,0},{14,2},{1,5},{3,7},... | collective-permute-start | bytes 344072 | tf_op jit(solution)/shard_map/ppermute | solution.py:18
  2.3 2.5 %collective-permute-start.2 = (bf16[32,1792]{1,0:T(8,128)(2,1)}, bf16[32,1792]{1,0:T(8,128)(2,1)S(1)}, u32[]{:S(2)}, u32[]{:S(2)}) collective-permute-start(bf16[32,1792]{1,0:T(8,128)(2,1)} %bitcast.345), channel_id=1, source_target_pairs={{0,6},{2,8},{4,10},{6,12},{8,14},{10,0},{12,2},{14,4},{1,7},{3,9},... | collective-permute-start | bytes 344072 | tf_op jit(solution)/shard_map/ppermute | solution.py:18
  5.1 3.5 %collective-permute-start.4 = (bf16[32,1792]{1,0:T(8,128)(2,1)}, bf16[32,1792]{1,0:T(8,128)(2,1)S(1)}, u32[]{:S(2)}, u32[]{:S(2)}) collective-permute-start(bf16[32,1792]{1,0:T(8,128)(2,1)} %bitcast.347), channel_id=1, source_target_pairs={{0,10},{2,12},{4,14},{6,0},{8,2},{10,4},{12,6},{14,8},{1,11},{3,13... | collective-permute-start | bytes 344072 | tf_op jit(solution)/shard_map/ppermute | solution.py:18
  8.7 1.2 slice.208
  12.6 0.9 pad_maximum_fusion.14
  13.6 0.9 constant_dynamic-update-slice_fusion.6
  15.9 1.3 copy.66
  18.1 1.0 convert.71
  19.9 1.1 collective-permute-done
  21.0 2.7 %collective-permute-start.5 = (bf16[32,1792]{1,0:T(8,128)(2,1)S(1)}, bf16[32,1792]{1,0:T(8,128)(2,1)S(1)}, u32[]{:S(2)}, u32[]{:S(2)}) collective-permute-start(bf16[32,1792]{1,0:T(8,128)(2,1)S(1)} %bitcast.349), channel_id=1, source_target_pairs={{0,12},{2,14},{4,0},{6,2},{8,4},{10,6},{12,8},{14,10},{1,13},{3,15... | collective-permute-start | bytes 344072 | tf_op jit(solution)/shard_map/ppermute | solution.py:18
  23.7 0.9 slice_dynamic-update-slice_fusion
  27.8 1.5 collective-permute-start.6
  29.3 0.9 constant_dynamic-update-slice_fusion.5
  31.0 2.5 %collective-permute-done.6 = bf16[32,1792]{1,0:T(8,128)(2,1)S(1)} collective-permute-done((bf16[32,1792]{1,0:T(8,128)(2,1)S(1)}, bf16[32,1792]{1,0:T(8,128)(2,1)S(1)}, u32[]{:S(2)}, u32[]{:S(2)}) %collective-permute-start.6) | collective-permute-done | bytes 114720 | tf_op jit(solution)/shard_map/ppermute | solution.py:18
  36.7 1.3 fusion.33
  38.1 1.5 reshape.356
  40.2 1.3 copy.71
  41.5 1.6 %reshape.357 = f32[28,4096]{1,0:T(8,128)S(1)} reshape(f32[28,64,64]{2,1,0:T(8,128)} %copy.71) | data formatting | bytes 917504 | tf_op jit(solution)/shard_map/reshape | solution.py:251
  43.9 1.8 %concatenate.83 = bf16[28,8320]{1,0:T(8,128)(2,1)} concatenate(bf16[28,4096]{1,0:T(8,128)(2,1)S(1)} %convert.55, bf16[28,4096]{1,0:T(8,128)(2,1)} %convert.56, bf16[28,1]{1,0:T(8,128)(2,1)S(1)} %copy.72, bf16[28,1]{1,0:T(8,128)(2,1)S(1)} %copy.73, bf16[28,126]{1,0:T(8,128)(2,1)S(1)} %broadcast.193), dimensions={1} | concatenate | bytes 931840 | tf_op jit(solution)/shard_map/concatenate | solution.py:141
  45.7 0.9 multiply_reduce_fusion.3
  47.6 1.9 %fusion.12 = (f32[28,128]{1,0:T(8,128)S(1)}, f32[28,128]{1,0:T(8,128)S(1)}, f32[28,128]{1,0:T(8,128)S(1)}, bf16[128,128]{1,0:T(8,128)(2,1)S(1)}) fusion(f32[28,128]{1,0:T(8,128)S(1)} %fusion.120, f32[128,128]{1,0:T(8,128)S(1)} %fusion.103, f32[128,128]{1,0:T(8,128)S(1)} %copy-done.24, f32[28,128]{1,0:T(8,128)S(1)} %fusion.74, ...), kind=kOutput, calls=%fused_computation.18 | convolution fusion | flops 66033152 | bytes 1628160 | tf_op jit(solution)/shard_map/transpose(jvp(hts,shp->thp))/dot_general | solution.py:33
  49.8 0.8 fusion.128
  50.6 0.8 fusion.107
  53.8 1.8 %fusion.17 = bf16[128,28,64]{0,2,1:T(8,128)(2,1)} fusion(f32[128,28,64]{0,2,1:T(8,128)S(1)} %copy-done.8, f32[28,128]{1,0:T(8,128)S(1)} %fusion.120, f32[128,128]{1,0:T(8,128)S(1)} %fusion.103, f32[128,128]{1,0:T(8,128)S(1)} %copy-done.24, f32[28,128]{1,0:T(8,128)S(1)} %fusion.74, pred[128,128]{1,0:T(8,128)(4,1)S(1)} %copy-done.32, ...), kind=kOutput, calls=%fused_computation.27 | convolution fusion | flops 63078400 | bytes 1574000 | tf_op jit(solution)/shard_map/transpose(jvp(hts,shp->thp))/dot_general | solution.py:33
  55.6 11.0 %collective-permute-done.8 = bf16[28,8320]{1,0:T(8,128)(2,1)S(1)} collective-permute-done((bf16[28,8320]{1,0:T(8,128)(2,1)S(1)}, bf16[28,8320]{1,0:T(8,128)(2,1)S(1)}, u32[]{:S(2)}, u32[]{:S(2)}) %collective-permute-start.8) | collective-permute-done | bytes 465952 | tf_op jit(solution)/shard_map/ppermute | solution.py:148
  67.7 1.0 concatenate.84
  68.7 14.0 %collective-permute-done.9 = bf16[28,8320]{1,0:T(8,128)(2,1)} collective-permute-done((bf16[28,8320]{1,0:T(8,128)(2,1)}, bf16[28,8320]{1,0:T(8,128)(2,1)}, u32[]{:S(2)}, u32[]{:S(2)}) %collective-permute-start.9) | collective-permute-done | bytes 465952 | tf_op jit(solution)/shard_map/ppermute | solution.py:148
  82.7 1.1 convert_element_type.300
  83.9 1.3 fusion.80
  85.3 1.1 select_convert_fusion
  86.4 0.8 concatenate.85
  87.9 1.7 %bitcast_multiply_fusion = f32[1,128,1792]{1,2,0:T(8,128)} fusion(f32[128,28]{0,1:T(8,128)} %copy-done.20, bf16[1,128,1792]{1,2,0:T(8,128)(2,1)S(1)} %copy.70), kind=kLoop, calls=%fused_computation.36 | loop fusion | flops 458752 | bytes 1390592 | tf_op jit(solution)/shard_map/transpose(jvp())/mul | solution.py:98
  89.6 11.5 %collective-permute-done.10 = bf16[28,4224]{1,0:T(8,128)(2,1)S(1)} collective-permute-done((bf16[28,4224]{1,0:T(8,128)(2,1)S(1)}, bf16[28,4224]{1,0:T(8,128)(2,1)S(1)}, u32[]{:S(2)}, u32[]{:S(2)}) %collective-permute-start.10) | collective-permute-done | bytes 236576 | tf_op jit(solution)/shard_map/ppermute | solution.py:155
  101.9 2.3 %multiply_reduce_fusion.4 = (f32[28]{0:T(128)S(1)}, f32[28,4096]{1,0:T(8,128)}, bf16[28,4096]{1,0:T(8,128)(2,1)S(1)}) fusion(bf16[28,4224]{1,0:T(8,128)(2,1)} %copy-done.16, f32[28]{0:T(128)} %get-tuple-element.64, f32[28,8320]{1,0:T(8,128)S(1)} %convert_element_type.300, f32[28]{0:T(128)} %get-tuple-element.66, f32[28,8320]{1,0:T(8,128)S(1)} %convert_element_type.284, ...), kind=kLoop, calls=%fused_computation.64 | loop fusion | flops 2064356 | bytes 2753075 | tf_op jit(solution)/shard_map/reduce_sum | solution.py:272
  107.7 0.8 fusion.138
  108.6 0.8 fusion.139
  109.7 1.0 fusion.22
  111.0 1.6 %fusion.21 = f32[128,28,64]{0,2,1:T(8,128)S(1)} fusion(bf16[28,64,64]{2,1,0:T(8,128)(2,1)S(1)} %copy-done.15, bf16[128,28,64]{0,2,1:T(8,128)(2,1)} %fusion.17, f32[28,128]{1,0:T(8,128)S(1)} %copy.82, f32[28,64]{1,0:T(8,128)S(1)} %copy-done.30, f32[28,128]{1,0:T(8,128)S(1)} %copy.77, f32[128,64]{0,1:T(8,128)S(1)} %copy-done.18, f32[128,28]{0,1:T(8,128)S(1)} %copy-done.22), kind=kOutput, calls=%fused_computation.31 | convolution fusion | flops 32112640 | bytes 1688576 | tf_op jit(solution)/shard_map/transpose(jvp(thn,thp->hnp))/dot_general | solution.py:33
  112.9 1.8 %fusion.133 = (bf16[256,1792]{1,0:T(8,128)(2,1)S(1)}, f32[256,1792]{1,0:T(8,128)}) fusion(bf16[1,128,1792]{2,1,0:T(8,128)(2,1)S(1)} %copy-done.7, s32[]{:T(128)S(6)} %select_n.234, bf16[128,256]{0,1:T(8,128)(2,1)S(1)} %maximum_select_fusion), kind=kOutput, calls=%fused_computation.292 | convolution fusion | flops 118030336 | bytes 3276804 | tf_op jit(solution)/shard_map/dot_general | solution.py:292
  114.8 0.9 pad_maximum_fusion.6
  115.6 1.8 %collective-permute-start.18 = (bf16[36,1792]{1,0:T(8,128)(2,1)}, bf16[36,1792]{1,0:T(8,128)(2,1)S(1)}, u32[]{:S(2)}, u32[]{:S(2)}) collective-permute-start(bf16[36,1792]{1,0:T(8,128)(2,1)} %get-tuple-element.114), channel_id=1, source_target_pairs={{0,12},{2,14},{4,0},{6,2},{8,4},{10,6},{12,8},{14,10},{1,13},{3,15... | collective-permute-start | bytes 387080 | tf_op jit(solution)/shard_map/ppermute | solution.py:18
  119.2 3.4 %collective-permute-start.16 = (bf16[36,1792]{1,0:T(8,128)(2,1)}, bf16[36,1792]{1,0:T(8,128)(2,1)S(1)}, u32[]{:S(2)}, u32[]{:S(2)}) collective-permute-start(bf16[36,1792]{1,0:T(8,128)(2,1)} %get-tuple-element.112), channel_id=1, source_target_pairs={{0,8},{2,10},{4,12},{6,14},{8,0},{10,2},{12,4},{14,6},{1,9},{3,11}... | collective-permute-start | bytes 387080 | tf_op jit(solution)/shard_map/ppermute | solution.py:18
  123.3 2.6 %collective-permute-done.19 = bf16[36,1792]{1,0:T(8,128)(2,1)S(1)} collective-permute-done((bf16[36,1792]{1,0:T(8,128)(2,1)}, bf16[36,1792]{1,0:T(8,128)(2,1)S(1)}, u32[]{:S(2)}, u32[]{:S(2)}) %collective-permute-start.19) | collective-permute-done | bytes 129056 | tf_op jit(solution)/shard_map/ppermute | solution.py:18
  125.8 12.5 %collective-permute-start.14 = (bf16[36,1792]{1,0:T(8,128)(2,1)S(1)}, bf16[36,1792]{1,0:T(8,128)(2,1)S(1)}, u32[]{:S(2)}, u32[]{:S(2)}) collective-permute-start(bf16[36,1792]{1,0:T(8,128)(2,1)S(1)} %get-tuple-element.110), channel_id=1, source_target_pairs={{0,4},{2,6},{4,8},{6,10},{8,12},{10,14},{12,0},{14,2},{1,5},{3,7},... | collective-permute-start | bytes 387080 | tf_op jit(solution)/shard_map/ppermute | solution.py:18
  138.4 2.4 %collective-permute-done.17 = bf16[36,1792]{1,0:T(8,128)(2,1)S(1)} collective-permute-done((bf16[36,1792]{1,0:T(8,128)(2,1)}, bf16[36,1792]{1,0:T(8,128)(2,1)S(1)}, u32[]{:S(2)}, u32[]{:S(2)}) %collective-permute-start.17) | collective-permute-done | bytes 129056 | tf_op jit(solution)/shard_map/ppermute | solution.py:18
  140.9 1.3 collective-permute-start.12
  143.9 1.7 %fusion.51 = f32[1,32,1792]{2,1,0:T(8,128)} fusion(f32[256,1792]{1,0:T(8,128)} %get-tuple-element.125, bf16[36,1792]{1,0:T(8,128)(2,1)S(1)} %collective-permute-done.19, bf16[36,1792]{1,0:T(8,128)(2,1)S(1)} %collective-permute-done.18, bf16[36,1792]{1,0:T(8,128)(2,1)S(1)} %collective-permute-done.17, bf16[36,1792]{1,0:T(8,128)(2,1)S(1)} %collective-permute-done.16, ...), kind=kLoop, calls=%fused_computation.104 | loop fusion | flops 802816 | bytes 1261568 | tf_op jit(solution)/shard_map/broadcast_in_dim | solution.py:332
  146.8 7.0 %collective-permute-done.12 = bf16[1,128,1792]{2,1,0:T(8,128)(2,1)S(1)} collective-permute-done((bf16[1,128,1792]{2,1,0:T(8,128)(2,1)S(1)}, bf16[1,128,1792]{2,1,0:T(8,128)(2,1)S(1)}, u32[]{:S(2)}, u32[]{:S(2)}) %collective-permute-start.12) | collective-permute-done | bytes 458784 | tf_op jit(solution)/shard_map/ppermute | solution.py:12
  (238 shorter events, 26.3 us)
Async XLA Ops:
  0.6 17.2 %copy-start.12 = (bf16[1,128,1792]{2,1,0:T(8,128)(2,1)S(1)}, bf16[1,128,1792]{2,1,0:T(8,128)(2,1)}, u32[]{:S(2)}) copy-start(bf16[1,128,1792]{2,1,0:T(8,128)(2,1)} %param.13) | copy-start | bytes 1376260
  0.6 27.1 %collective-permute-start.1 = (bf16[32,1792]{1,0:T(8,128)(2,1)}, bf16[32,1792]{1,0:T(8,128)(2,1)}, u32[]{:S(2)}, u32[]{:S(2)}) collective-permute-start(bf16[32,1792]{1,0:T(8,128)(2,1)} %bitcast.344), channel_id=1, source_target_pairs={{0,4},{2,6},{4,8},{6,10},{8,12},{10,14},{12,0},{14,2},{1,5},{3,7},... | collective-permute-start | bytes 344072 | tf_op jit(solution)/shard_map/ppermute | solution.py:18
  2.3 27.9 %collective-permute-start.2 = (bf16[32,1792]{1,0:T(8,128)(2,1)}, bf16[32,1792]{1,0:T(8,128)(2,1)S(1)}, u32[]{:S(2)}, u32[]{:S(2)}) collective-permute-start(bf16[32,1792]{1,0:T(8,128)(2,1)} %bitcast.345), channel_id=1, source_target_pairs={{0,6},{2,8},{4,10},{6,12},{8,14},{10,0},{12,2},{14,4},{1,7},{3,9},... | collective-permute-start | bytes 344072 | tf_op jit(solution)/shard_map/ppermute | solution.py:18
  4.8 25.4 %collective-permute-start.3 = (bf16[32,1792]{1,0:T(8,128)(2,1)}, bf16[32,1792]{1,0:T(8,128)(2,1)S(1)}, u32[]{:S(2)}, u32[]{:S(2)}) collective-permute-start(bf16[32,1792]{1,0:T(8,128)(2,1)} %bitcast.346), channel_id=1, source_target_pairs={{0,8},{2,10},{4,12},{6,14},{8,0},{10,2},{12,4},{14,6},{1,9},{3,11}... | collective-permute-start | bytes 344072 | tf_op jit(solution)/shard_map/ppermute | solution.py:18
  5.1 25.1 %collective-permute-start.4 = (bf16[32,1792]{1,0:T(8,128)(2,1)}, bf16[32,1792]{1,0:T(8,128)(2,1)S(1)}, u32[]{:S(2)}, u32[]{:S(2)}) collective-permute-start(bf16[32,1792]{1,0:T(8,128)(2,1)} %bitcast.347), channel_id=1, source_target_pairs={{0,10},{2,12},{4,14},{6,0},{8,2},{10,4},{12,6},{14,8},{1,11},{3,13... | collective-permute-start | bytes 344072 | tf_op jit(solution)/shard_map/ppermute | solution.py:18
  13.5 7.5 %collective-permute-start = (bf16[32,1920]{1,0:T(8,128)(2,1)S(1)}, bf16[32,1920]{1,0:T(8,128)(2,1)}, u32[]{:S(2)}, u32[]{:S(2)}) collective-permute-start(bf16[32,1920]{1,0:T(8,128)(2,1)S(1)} %pad_maximum_fusion.14), channel_id=1, source_target_pairs={{0,2},{2,4},{4,6},{6,8},{8,10},{10,12},{12,14},{14,0},{1,3},{3,5},... | collective-permute-start | bytes 368648 | tf_op jit(solution)/shard_map/ppermute | solution.py:18
  15.9 3.9 %copy-start.46 = (f32[1,28]{1,0:T(1,128)S(1)}, f32[1,28]{1,0:T(1,128)}, u32[]{:S(2)}) copy-start(f32[1,28]{1,0:T(1,128)} %param.17) | copy-start | bytes 340
  15.9 5.0 %copy-start.13 = (bf16[1,32,1792]{2,1,0:T(8,128)(2,1)S(1)}, bf16[1,32,1792]{2,1,0:T(8,128)(2,1)}, u32[]{:S(2)}) copy-start(bf16[1,32,1792]{2,1,0:T(8,128)(2,1)} %param.14) | copy-start | bytes 344068
  17.2 33.4 %copy-start.4 = (bf16[1,128,1792]{1,2,0:T(8,128)(2,1)}, bf16[1,128,1792]{1,2,0:T(8,128)(2,1)S(1)}, u32[]{:S(2)}) copy-start(bf16[1,128,1792]{1,2,0:T(8,128)(2,1)S(1)} %copy.66) | copy-start | bytes 1376260
  17.8 15.7 %copy-start.6 = (bf16[1,128,1792]{2,1,0:T(8,128)(2,1)S(1)}, bf16[1,128,1792]{2,1,0:T(8,128)(2,1)}, u32[]{:S(2)}) copy-start(bf16[1,128,1792]{2,1,0:T(8,128)(2,1)} %param.11) | copy-start | bytes 1376260
  19.2 15.0 %copy-start.33 = (f32[1,28]{1,0:T(1,128)S(1)}, f32[1,28]{1,0:T(1,128)}, u32[]{:S(2)}) copy-start(f32[1,28]{1,0:T(1,128)} %param.16) | copy-start | bytes 340
  19.9 14.5 %copy-start.52 = (f32[28]{0:T(128)}, f32[28]{0:T(128)S(1)}, u32[]{:S(2)}) copy-start(f32[28]{0:T(128)S(1)} %negate_bitcast_fusion) | copy-start | bytes 340
  21.0 9.3 %collective-permute-start.5 = (bf16[32,1792]{1,0:T(8,128)(2,1)S(1)}, bf16[32,1792]{1,0:T(8,128)(2,1)S(1)}, u32[]{:S(2)}, u32[]{:S(2)}) collective-permute-start(bf16[32,1792]{1,0:T(8,128)(2,1)S(1)} %bitcast.349), channel_id=1, source_target_pairs={{0,12},{2,14},{4,0},{6,2},{8,4},{10,6},{12,8},{14,10},{1,13},{3,15... | collective-permute-start | bytes 344072 | tf_op jit(solution)/shard_map/ppermute | solution.py:18
  27.8 5.7 %collective-permute-start.6 = (bf16[32,1792]{1,0:T(8,128)(2,1)S(1)}, bf16[32,1792]{1,0:T(8,128)(2,1)S(1)}, u32[]{:S(2)}, u32[]{:S(2)}) collective-permute-start(bf16[32,1792]{1,0:T(8,128)(2,1)S(1)} %bitcast.350), channel_id=1, source_target_pairs={{0,14},{2,0},{4,2},{6,4},{8,6},{10,8},{12,10},{14,12},{1,15},{3,1}... | collective-permute-start | bytes 344072 | tf_op jit(solution)/shard_map/ppermute | solution.py:18
  31.0 7.1 %copy-start.35 = (pred[128]{0:T(512)(128)(4,1)}, pred[128]{0:T(512)(128)(4,1)S(1)}, u32[]{:S(2)}) copy-start(pred[128]{0:T(512)(128)(4,1)S(1)} %get-tuple-element.89) | copy-start | bytes 388
  31.0 7.1 %copy-start.37 = (f32[128]{0:T(128)}, f32[128]{0:T(128)S(1)}, u32[]{:S(2)}) copy-start(f32[128]{0:T(128)S(1)} %get-tuple-element.90) | copy-start | bytes 1540
  31.0 7.1 %copy-start.44 = (f32[128]{0:T(128)}, f32[128]{0:T(128)S(1)}, u32[]{:S(2)}) copy-start(f32[128]{0:T(128)S(1)} %get-tuple-element.121) | copy-start | bytes 1540
  33.5 4.5 %copy-start.2 = (bf16[256,1792]{1,0:T(8,128)(2,1)}, bf16[256,1792]{1,0:T(8,128)(2,1)S(1)}, u32[]{:S(2)}) copy-start(bf16[256,1792]{1,0:T(8,128)(2,1)S(1)} %constant_dynamic-update-slice_fusion) | copy-start | bytes 2752516
  34.0 2.6 %collective-permute-start.7 = (bf16[128,128]{0,1:T(8,128)(2,1)S(1)}, bf16[128,128]{0,1:T(8,128)(2,1)S(1)}, u32[]{:S(2)}, u32[]{:S(2)}) collective-permute-start(bf16[128,128]{0,1:T(8,128)(2,1)S(1)} %fusion.58), channel_id=1, source_target_pairs={{0,1},{1,0},{2,3},{3,2},{4,5},{5,4},{6,7},{7,6},{8,9},{9,8},{10,11... | collective-permute-start | bytes 98312 | tf_op jit(solution)/shard_map/ppermute | solution.py:29
  34.4 5.2 %copy-start.20 = (f32[128,28]{0,1:T(8,128)}, f32[128,28]{0,1:T(8,128)S(1)}, u32[]{:S(2)}) copy-start(f32[128,28]{0,1:T(8,128)S(1)} %get-tuple-element.122) | copy-start | bytes 43012
  36.7 3.5 %copy-start.17 = (f32[128,64]{0,1:T(8,128)}, f32[128,64]{0,1:T(8,128)S(1)}, u32[]{:S(2)}) copy-start(f32[128,64]{0,1:T(8,128)S(1)} %slice_convert_fusion) | copy-start | bytes 98308
  41.5 4.2 %copy-start.8 = (f32[128,28,64]{0,2,1:T(8,128)S(1)}, f32[128,28,64]{0,2,1:T(8,128)}, u32[]{:S(2)}) copy-start(f32[128,28,64]{0,2,1:T(8,128)} %convert.71) | copy-start | bytes 2752516
  43.1 24.4 %copy-start = (f32[28,4096]{1,0:T(8,128)}, f32[28,4096]{1,0:T(8,128)S(1)}, u32[]{:S(2)}) copy-start(f32[28,4096]{1,0:T(8,128)S(1)} %reshape.357) | copy-start | bytes 1376260
  43.1 3.5 %copy-start.28 = (f32[28,64]{1,0:T(8,128)S(1)}, f32[28,64]{1,0:T(8,128)}, u32[]{:S(2)}) copy-start(f32[28,64]{1,0:T(8,128)} %reshape_squeeze.7) | copy-start | bytes 21508
  43.1 4.5 %copy-start.24 = (f32[128,128]{1,0:T(8,128)S(1)}, f32[128,128]{1,0:T(8,128)}, u32[]{:S(2)}) copy-start(f32[128,128]{1,0:T(8,128)} %get-tuple-element.120) | copy-start | bytes 196612
  43.1 4.4 %copy-start.31 = (pred[128,128]{1,0:T(8,128)(4,1)S(1)}, pred[128,128]{1,0:T(8,128)(4,1)}, u32[]{:S(2)}) copy-start(pred[128,128]{1,0:T(8,128)(4,1)} %get-tuple-element.119) | copy-start | bytes 49156
  47.6 4.5 %copy-start.11 = (bf16[28,8320]{1,0:T(8,128)(2,1)S(1)}, bf16[28,8320]{1,0:T(8,128)(2,1)}, u32[]{:S(2)}) copy-start(bf16[28,8320]{1,0:T(8,128)(2,1)} %concatenate.83) | copy-start | bytes 1397764
  47.6 5.7 %copy-start.50 = (f32[1,28]{1,0:T(1,128)S(1)}, f32[1,28]{1,0:T(1,128)}, u32[]{:S(2)}) copy-start(f32[1,28]{1,0:T(1,128)} %param.18) | copy-start | bytes 340
  47.6 6.2 %copy-start.29 = (f32[28,64]{1,0:T(8,128)S(1)}, f32[28,64]{1,0:T(8,128)}, u32[]{:S(2)}) copy-start(f32[28,64]{1,0:T(8,128)} %reshape_squeeze.7) | copy-start | bytes 21508
  47.6 6.2 %copy-start.32 = (pred[128,128]{1,0:T(8,128)(4,1)S(1)}, pred[128,128]{1,0:T(8,128)(4,1)}, u32[]{:S(2)}) copy-start(pred[128,128]{1,0:T(8,128)(4,1)} %get-tuple-element.119) | copy-start | bytes 49156
  52.1 14.5 %collective-permute-start.8 = (bf16[28,8320]{1,0:T(8,128)(2,1)S(1)}, bf16[28,8320]{1,0:T(8,128)(2,1)S(1)}, u32[]{:S(2)}, u32[]{:S(2)}) collective-permute-start(bf16[28,8320]{1,0:T(8,128)(2,1)S(1)} %copy-done.11), channel_id=1, source_target_pairs={{0,2},{2,0},{4,6},{6,4},{8,10},{10,8},{12,14},{14,12},{1,3},{3,1},... | collective-permute-start | bytes 1397768 | tf_op jit(solution)/shard_map/ppermute | solution.py:148
  53.8 12.8 %copy-start.23 = (f32[28,1]{1,0:T(8,128)S(1)}, f32[28,1]{1,0:T(8,128)}, u32[]{:S(2)}) copy-start(f32[28,1]{1,0:T(8,128)} %copy.74) | copy-start | bytes 340
  53.8 13.7 %copy-start.49 = (f32[28]{0:T(128)S(1)}, f32[28]{0:T(128)}, u32[]{:S(2)}) copy-start(f32[28]{0:T(128)} %exponential_multiply_fusion.1) | copy-start | bytes 340
  68.7 14.0 %collective-permute-start.9 = (bf16[28,8320]{1,0:T(8,128)(2,1)}, bf16[28,8320]{1,0:T(8,128)(2,1)}, u32[]{:S(2)}, u32[]{:S(2)}) collective-permute-start(bf16[28,8320]{1,0:T(8,128)(2,1)} %concatenate.84), channel_id=1, source_target_pairs={{0,4},{2,6},{4,0},{6,2},{8,12},{10,14},{12,8},{14,10},{1,5},{3,7},... | collective-permute-start | bytes 1397768 | tf_op jit(solution)/shard_map/ppermute | solution.py:148
  68.7 16.6 %copy-start.1 = (f32[28,4096]{1,0:T(8,128)S(1)}, f32[28,4096]{1,0:T(8,128)}, u32[]{:S(2)}) copy-start(f32[28,4096]{1,0:T(8,128)} %copy-done) | copy-start | bytes 1376260
  87.2 14.0 %collective-permute-start.10 = (bf16[28,4224]{1,0:T(8,128)(2,1)S(1)}, bf16[28,4224]{1,0:T(8,128)(2,1)S(1)}, u32[]{:S(2)}, u32[]{:S(2)}) collective-permute-start(bf16[28,4224]{1,0:T(8,128)(2,1)S(1)} %concatenate.85), channel_id=1, source_target_pairs={{0,8},{2,10},{4,12},{6,14},{8,0},{10,2},{12,4},{14,6},{1,9},{3,11}... | collective-permute-start | bytes 709640 | tf_op jit(solution)/shard_map/ppermute | solution.py:155
  107.3 3.4 %copy-start.19 = (bf16[128,128]{0,1:T(8,128)(2,1)S(1)}, bf16[128,128]{0,1:T(8,128)(2,1)}, u32[]{:S(2)}) copy-start(bf16[128,128]{0,1:T(8,128)(2,1)} %pad_add_fusion) | copy-start | bytes 98308
  107.6 3.4 %copy-start.30 = (f32[28,64]{1,0:T(8,128)S(1)}, f32[28,64]{1,0:T(8,128)}, u32[]{:S(2)}) copy-start(f32[28,64]{1,0:T(8,128)} %reshape_squeeze.7) | copy-start | bytes 21508
  110.7 2.1 %collective-permute-start.11 = (bf16[128,128]{0,1:T(8,128)(2,1)S(1)}, bf16[128,128]{0,1:T(8,128)(2,1)S(1)}, u32[]{:S(2)}, u32[]{:S(2)}) collective-permute-start(bf16[128,128]{0,1:T(8,128)(2,1)S(1)} %add_convert_fusion), channel_id=1, source_target_pairs={{0,1},{1,0},{2,3},{3,2},{4,5},{5,4},{6,7},{7,6},{8,9},{9,8},{10,11... | collective-permute-start | bytes 98312 | tf_op jit(solution)/shard_map/ppermute | solution.py:29
  114.7 8.2 %copy-start.3 = (bf16[256,1792]{1,0:T(8,128)(2,1)S(1)}, bf16[256,1792]{1,0:T(8,128)(2,1)}, u32[]{:S(2)}) copy-start(bf16[256,1792]{1,0:T(8,128)(2,1)} %copy-done.2) | copy-start | bytes 2752516
  115.6 22.7 %collective-permute-start.18 = (bf16[36,1792]{1,0:T(8,128)(2,1)}, bf16[36,1792]{1,0:T(8,128)(2,1)S(1)}, u32[]{:S(2)}, u32[]{:S(2)}) collective-permute-start(bf16[36,1792]{1,0:T(8,128)(2,1)} %get-tuple-element.114), channel_id=1, source_target_pairs={{0,12},{2,14},{4,0},{6,2},{8,4},{10,6},{12,8},{14,10},{1,13},{3,15... | collective-permute-start | bytes 387080 | tf_op jit(solution)/shard_map/ppermute | solution.py:18
  118.2 7.7 %collective-permute-start.19 = (bf16[36,1792]{1,0:T(8,128)(2,1)}, bf16[36,1792]{1,0:T(8,128)(2,1)S(1)}, u32[]{:S(2)}, u32[]{:S(2)}) collective-permute-start(bf16[36,1792]{1,0:T(8,128)(2,1)} %pad_maximum_fusion), channel_id=1, source_target_pairs={{0,14},{2,0},{4,2},{6,4},{8,6},{10,8},{12,10},{14,12},{1,15},{3,1}... | collective-permute-start | bytes 387080 | tf_op jit(solution)/shard_map/ppermute | solution.py:18
  118.9 22.0 %collective-permute-start.17 = (bf16[36,1792]{1,0:T(8,128)(2,1)}, bf16[36,1792]{1,0:T(8,128)(2,1)S(1)}, u32[]{:S(2)}, u32[]{:S(2)}) collective-permute-start(bf16[36,1792]{1,0:T(8,128)(2,1)} %get-tuple-element.113), channel_id=1, source_target_pairs={{0,10},{2,12},{4,14},{6,0},{8,2},{10,4},{12,6},{14,8},{1,11},{3,13... | collective-permute-start | bytes 387080 | tf_op jit(solution)/shard_map/ppermute | solution.py:18
  119.2 23.6 %collective-permute-start.16 = (bf16[36,1792]{1,0:T(8,128)(2,1)}, bf16[36,1792]{1,0:T(8,128)(2,1)S(1)}, u32[]{:S(2)}, u32[]{:S(2)}) collective-permute-start(bf16[36,1792]{1,0:T(8,128)(2,1)} %get-tuple-element.112), channel_id=1, source_target_pairs={{0,8},{2,10},{4,12},{6,14},{8,0},{10,2},{12,4},{14,6},{1,9},{3,11}... | collective-permute-start | bytes 387080 | tf_op jit(solution)/shard_map/ppermute | solution.py:18
  122.5 20.2 %collective-permute-start.15 = (bf16[36,1792]{1,0:T(8,128)(2,1)}, bf16[36,1792]{1,0:T(8,128)(2,1)S(1)}, u32[]{:S(2)}, u32[]{:S(2)}) collective-permute-start(bf16[36,1792]{1,0:T(8,128)(2,1)} %get-tuple-element.111), channel_id=1, source_target_pairs={{0,6},{2,8},{4,10},{6,12},{8,14},{10,0},{12,2},{14,4},{1,7},{3,9},... | collective-permute-start | bytes 387080 | tf_op jit(solution)/shard_map/ppermute | solution.py:18
  125.8 16.9 %collective-permute-start.14 = (bf16[36,1792]{1,0:T(8,128)(2,1)S(1)}, bf16[36,1792]{1,0:T(8,128)(2,1)S(1)}, u32[]{:S(2)}, u32[]{:S(2)}) collective-permute-start(bf16[36,1792]{1,0:T(8,128)(2,1)S(1)} %get-tuple-element.110), channel_id=1, source_target_pairs={{0,4},{2,6},{4,8},{6,10},{8,12},{10,14},{12,0},{14,2},{1,5},{3,7},... | collective-permute-start | bytes 387080 | tf_op jit(solution)/shard_map/ppermute | solution.py:18
  138.4 5.2 %collective-permute-start.13 = (bf16[36,1792]{1,0:T(8,128)(2,1)S(1)}, bf16[36,1792]{1,0:T(8,128)(2,1)S(1)}, u32[]{:S(2)}, u32[]{:S(2)}) collective-permute-start(bf16[36,1792]{1,0:T(8,128)(2,1)S(1)} %get-tuple-element.109), channel_id=1, source_target_pairs={{0,2},{2,4},{4,6},{6,8},{8,10},{10,12},{12,14},{14,0},{1,3},{3,5},... | collective-permute-start | bytes 387080 | tf_op jit(solution)/shard_map/ppermute | solution.py:18
  140.9 13.0 %collective-permute-start.12 = (bf16[1,128,1792]{2,1,0:T(8,128)(2,1)S(1)}, bf16[1,128,1792]{2,1,0:T(8,128)(2,1)S(1)}, u32[]{:S(2)}, u32[]{:S(2)}) collective-permute-start(bf16[1,128,1792]{2,1,0:T(8,128)(2,1)S(1)} %fusion.1), channel_id=1, source_target_pairs={{16,0},{17,1},{18,2},{19,3},{20,4},{21,5},{22,6},{23,7},{24,8},{25... | collective-permute-start | bytes 1376264 | tf_op jit(solution)/shard_map/ppermute | solution.py:12
  (26 other events, 49.0 us)

commit v9 on v5

--- a/solution.py
+++ b/solution.py
@@ -280,9 +280,8 @@
     ) + back_proj
     value_grad = value_grad.astype(jnp.bfloat16)
     prev_part = shifted(value_grad.reshape(1, tokens, channels_here), "section", -1)
-    dest_grad = roll_blocks(mixer_full, size - mine, size, 1)
     row_parts = lax.dot_general(
-        dest_grad, bwd_flat, (((0,), (0,)), ((), ())), preferred_element_type=jnp.float32
+        mixer_full, bwd_flat, (((0,), (0,)), ((), ())), preferred_element_type=jnp.float32
     ).reshape(size, -1, channels_here)
     small = jnp.concatenate(
         [
@@ -299,16 +298,18 @@
     small_low = (small - small_high.astype(jnp.float32)).astype(jnp.bfloat16)
     small_coded = jnp.concatenate([small_high, small_low], axis=0)
     block_rows = row_parts.shape[1]
-    grad_rows = row_parts[0]
-    small_slots = [small_coded]
-    for k in range(1, size):
-        message = jnp.concatenate([row_parts[k].astype(jnp.bfloat16), small_coded], axis=0)
-        got = rotated(message, "seq", k)
-        grad_rows = grad_rows + got[:block_rows].astype(jnp.float32)
-        small_slots.append(got[block_rows:])
-    small_slots = jnp.stack(small_slots[::-1])
-    small_slots = roll_blocks(small_slots, mine + 1, size, 0).astype(jnp.float32)
-    small_parts = small_slots[:, :small_rows] + small_slots[:, small_rows:]
+    messages = jnp.concatenate(
+        [
+            row_parts.astype(jnp.bfloat16),
+            jnp.broadcast_to(small_coded[None], (size,) + small_coded.shape),
+        ],
+        axis=1,
+    )
+    got = lax.all_to_all(messages, "seq", 0, 0, tiled=False).astype(jnp.float32)
+    grad_rows = got[0, :block_rows]
+    for j in range(1, size):
+        grad_rows = grad_rows + got[j, :block_rows]
+    small_parts = got[:, block_rows : block_rows + small_rows] + got[:, block_rows + small_rows :]
     small_total = small_parts[0]
     for j in range(1, size):
         small_total = small_total + small_parts[j]

time: 145 us -> 146 us (level)
  starting transfers between devices: 36.1 us -> 21.6 us
  waiting for transfers between devices: 57.4 us -> 65.9 us
  other arithmetic: 14 us -> 17.4 us
  local copies, waits for them, and re-layouts: 16.6 us -> 19 us
    ppermute x14 -> x7, starting transfers between devices: 29.5 us -> 10.6 us  [rotated(): return lax.ppermute(block, axis, route)]
    all_to_all x0 -> x1, waiting for transfers between devices: none -> 8.89 us  [shards(): got = lax.all_to_all(messages, 'seq', 0, 0, tiled=False).astype(jnp.float32)]
    ppermute x14 -> x7, waiting for transfers between devices: 11.7 us -> 5.58 us  [rotated(): return lax.ppermute(block, axis, route)]
    ppermute x2, waiting for transfers between devices: 7 us -> 12.6 us  [shifted(): return lax.ppermute(block, axis, route)]
    all_to_all x0 -> x1, starting transfers between devices: none -> 4.54 us  [shards(): got = lax.all_to_all(messages, 'seq', 0, 0, tiled=False).astype(jnp.float32)]
    broadcast_in_dim x1 -> x0, other arithmetic: 1.75 us -> none  [shards(): grad_rows[None]]
    unnamed x144 -> x118, local copies, waits for them, and re-layouts: 4.32 us -> 3.85 us
  transfers between devices with their start and end apart: 21 -> 15, of which waited for: 11 -> 9; matrix products, arithmetic and copies ran while one was open for 15% -> 14% of each run, Pallas kernels for 0% -> 0%
where the time goes in v9:
time: 146 us; the launch traced here: 144 us
  waiting for transfers between devices  65.9 us (45%)
  starting transfers between devices  21.6 us (15%)
  local copies, waits for them, and re-layouts  19 us (13%)
  other arithmetic  17.4 us (12%)
  matrix products  17.2 us (12%)
  between operations  3.05 us (2%)
    ppermute x2, waiting for transfers between devices, both_scans(): got = lax.ppermute(payload, axis, [(i, i ^ distance) for i in range(size)])  25.3 us
    ppermute x2, waiting for transfers between devices, shifted(): return lax.ppermute(block, axis, route)  12.6 us
    ppermute x1, waiting for transfers between devices, both_scans(): got = lax.ppermute(last, axis, [(i, i ^ distance) for i in range(size)])  12.4 us
    ppermute x7, starting transfers between devices, rotated(): return lax.ppermute(block, axis, route)  10.6 us
    all_to_all x1, waiting for transfers between devices, shards(): got = lax.all_to_all(messages, 'seq', 0, 0, tiled=False).astype(jnp.float32)  8.89 us
    dot_general x5, matrix products, contract(): return jnp.einsum(spec, left, right, preferred_element_type=jnp.float32)  6.87 us
    ppermute x2, starting transfers between devices, shifted(): return lax.ppermute(block, axis, route)  5.61 us
    ppermute x7, waiting for transfers between devices, rotated(): return lax.ppermute(block, axis, route)  5.58 us
  transfers between devices with their start and end apart: 15, of which 9 were waited for; matrix products, arithmetic and copies ran while one was open for 14% of the time, Pallas kernels for 0%

profile of v9, /device:TPU:4, one launch (start us, length us, event | category | flops | bytes accessed | tf_op | source)
XLA Modules:
  0.0 144.1 jit_solution(2185793820788929012)
XLA Ops:
  0.7 1.6 %collective-permute-start = (bf16[32,1792]{1,0:T(8,128)(2,1)}, bf16[32,1792]{1,0:T(8,128)(2,1)S(1)}, u32[]{:S(2)}, u32[]{:S(2)}) collective-permute-start(bf16[32,1792]{1,0:T(8,128)(2,1)} %bitcast.303), channel_id=1, source_target_pairs={{0,2},{2,4},{4,6},{6,8},{8,10},{10,12},{12,14},{14,0},{1,3},{3,5},... | collective-permute-start | bytes 344072 | tf_op jit(solution)/shard_map/ppermute | solution.py:18
  2.2 1.6 %collective-permute-start.1 = (bf16[32,1792]{1,0:T(8,128)(2,1)}, bf16[32,1792]{1,0:T(8,128)(2,1)S(1)}, u32[]{:S(2)}, u32[]{:S(2)}) collective-permute-start(bf16[32,1792]{1,0:T(8,128)(2,1)} %bitcast.304), channel_id=1, source_target_pairs={{0,4},{2,6},{4,8},{6,10},{8,12},{10,14},{12,0},{14,2},{1,5},{3,7},... | collective-permute-start | bytes 344072 | tf_op jit(solution)/shard_map/ppermute | solution.py:18
  3.8 2.5 %collective-permute-start.2 = (bf16[32,1792]{1,0:T(8,128)(2,1)}, bf16[32,1792]{1,0:T(8,128)(2,1)S(1)}, u32[]{:S(2)}, u32[]{:S(2)}) collective-permute-start(bf16[32,1792]{1,0:T(8,128)(2,1)} %bitcast.305), channel_id=1, source_target_pairs={{0,6},{2,8},{4,10},{6,12},{8,14},{10,0},{12,2},{14,4},{1,7},{3,9},... | collective-permute-start | bytes 344072 | tf_op jit(solution)/shard_map/ppermute | solution.py:18
  6.7 1.2 slice.123
  7.9 4.3 %collective-permute-start.8 = (s32[1]{0:T(128)}, s32[1]{0:T(128)}, u32[]{:S(2)}, u32[]{:S(2)}) collective-permute-start(s32[1]{0:T(128)} %bitcast.13), channel_id=1, source_target_pairs={{0,2},{2,4},{4,6},{6,8},{8,10},{10,12},{12,14},{1,3},{3,5},{5,7},{... | collective-permute-start | bytes 20 | tf_op jit(solution)/shard_map/ppermute | solution.py:12
  12.2 0.9 constant_dynamic-update-slice_fusion.7
  13.2 0.7 reduce
  14.6 1.3 copy.66
  16.8 1.0 convert.51
  17.9 0.7 broadcast_compare_fusion
  18.6 1.3 collective-permute-start.4
  19.9 1.3 broadcast_compare_fusion.1
  23.4 3.2 %collective-permute-start.5 = (bf16[32,1792]{1,0:T(8,128)(2,1)S(1)}, bf16[32,1792]{1,0:T(8,128)(2,1)S(1)}, u32[]{:S(2)}, u32[]{:S(2)}) collective-permute-start(bf16[32,1792]{1,0:T(8,128)(2,1)S(1)} %bitcast.308), channel_id=1, source_target_pairs={{0,12},{2,14},{4,0},{6,2},{8,4},{10,6},{12,8},{14,10},{1,13},{3,15... | collective-permute-start | bytes 344072 | tf_op jit(solution)/shard_map/ppermute | solution.py:18
  26.7 0.7 collective-permute-done.4
  27.4 1.5 %collective-permute-done.5 = bf16[32,1792]{1,0:T(8,128)(2,1)S(1)} collective-permute-done((bf16[32,1792]{1,0:T(8,128)(2,1)S(1)}, bf16[32,1792]{1,0:T(8,128)(2,1)S(1)}, u32[]{:S(2)}, u32[]{:S(2)}) %collective-permute-start.5) | collective-permute-done | bytes 114720 | tf_op jit(solution)/shard_map/ppermute | solution.py:18
  28.9 3.4 %collective-permute-done.6 = bf16[32,1792]{1,0:T(8,128)(2,1)S(1)} collective-permute-done((bf16[32,1792]{1,0:T(8,128)(2,1)S(1)}, bf16[32,1792]{1,0:T(8,128)(2,1)S(1)}, u32[]{:S(2)}, u32[]{:S(2)}) %collective-permute-start.6) | collective-permute-done | bytes 114720 | tf_op jit(solution)/shard_map/ppermute | solution.py:18
  34.3 0.7 copy.73
  36.5 1.3 copy.71
  37.7 1.6 %reshape.281 = f32[28,4096]{1,0:T(8,128)S(1)} reshape(f32[28,64,64]{2,1,0:T(8,128)} %copy.71) | data formatting | bytes 917504 | tf_op jit(solution)/shard_map/reshape | solution.py:243
  39.4 1.8 %concatenate.41 = bf16[28,8320]{1,0:T(8,128)(2,1)} concatenate(bf16[28,4096]{1,0:T(8,128)(2,1)S(1)} %convert.36, bf16[28,4096]{1,0:T(8,128)(2,1)S(1)} %convert.37, bf16[28,1]{1,0:T(8,128)(2,1)S(1)} %copy.72, bf16[28,1]{1,0:T(8,128)(2,1)} %copy.73, bf16[28,126]{1,0:T(8,128)(2,1)S(1)} %broadcast.164), dimensions={1} | concatenate | bytes 931840 | tf_op jit(solution)/shard_map/concatenate | solution.py:141
  41.2 0.9 multiply_reduce_fusion.3
  42.0 1.2 fusion.96
  43.8 1.9 %fusion.12 = (f32[28,128]{1,0:T(8,128)S(1)}, f32[28,128]{1,0:T(8,128)S(1)}, f32[28,128]{1,0:T(8,128)S(1)}, bf16[128,128]{1,0:T(8,128)(2,1)S(1)}) fusion(f32[28,128]{1,0:T(8,128)S(1)} %fusion.102, f32[128,128]{1,0:T(8,128)S(1)} %fusion.90, f32[128,128]{1,0:T(8,128)S(1)} %copy-done.23, f32[28,128]{1,0:T(8,128)S(1)} %fusion.64, ...), kind=kOutput, calls=%fused_computation.19 | convolution fusion | flops 66033152 | bytes 1628160 | tf_op jit(solution)/shard_map/transpose(jvp(hts,shp->thp))/dot_general | solution.py:33
  46.0 0.9 fusion.110
  46.9 0.8 fusion.94
  49.5 1.8 %fusion.17 = bf16[128,28,64]{0,2,1:T(8,128)(2,1)} fusion(f32[128,28,64]{0,2,1:T(8,128)S(1)} %copy-done.8, f32[28,128]{1,0:T(8,128)S(1)} %fusion.102, f32[128,128]{1,0:T(8,128)S(1)} %fusion.90, f32[128,128]{1,0:T(8,128)S(1)} %copy-done.23, f32[28,128]{1,0:T(8,128)S(1)} %fusion.64, pred[128,128]{1,0:T(8,128)(4,1)S(1)} %copy-done.29, ...), kind=kOutput, calls=%fused_computation.28 | convolution fusion | flops 63078400 | bytes 1574000 | tf_op jit(solution)/shard_map/transpose(jvp(hts,shp->thp))/dot_general | solution.py:33
  51.3 11.5 %collective-permute-done.9 = bf16[28,8320]{1,0:T(8,128)(2,1)S(1)} collective-permute-done((bf16[28,8320]{1,0:T(8,128)(2,1)S(1)}, bf16[28,8320]{1,0:T(8,128)(2,1)S(1)}, u32[]{:S(2)}, u32[]{:S(2)}) %collective-permute-start.9) | collective-permute-done | bytes 465952 | tf_op jit(solution)/shard_map/ppermute | solution.py:148
  64.3 13.7 %collective-permute-done.10 = bf16[28,8320]{1,0:T(8,128)(2,1)} collective-permute-done((bf16[28,8320]{1,0:T(8,128)(2,1)S(1)}, bf16[28,8320]{1,0:T(8,128)(2,1)}, u32[]{:S(2)}, u32[]{:S(2)}) %collective-permute-start.10) | collective-permute-done | bytes 465952 | tf_op jit(solution)/shard_map/ppermute | solution.py:148
  78.1 1.1 convert_element_type.264
  80.0 1.1 select_convert_fusion
  82.0 1.0 bitcast_multiply_fusion
  82.9 12.4 %collective-permute-done.11 = bf16[28,4224]{1,0:T(8,128)(2,1)} collective-permute-done((bf16[28,4224]{1,0:T(8,128)(2,1)S(1)}, bf16[28,4224]{1,0:T(8,128)(2,1)}, u32[]{:S(2)}, u32[]{:S(2)}) %collective-permute-start.11) | collective-permute-done | bytes 236576 | tf_op jit(solution)/shard_map/ppermute | solution.py:155
  95.4 2.7 %multiply_reduce_fusion.4 = (f32[28]{0:T(128)}, f32[28,4096]{1,0:T(8,128)}, bf16[28,4096]{1,0:T(8,128)(2,1)S(1)}) fusion(bf16[28,4224]{1,0:T(8,128)(2,1)} %collective-permute-done.11, f32[28]{0:T(128)S(1)} %copy-done.40, f32[28,8320]{1,0:T(8,128)S(1)} %convert_element_type.264, f32[28]{0:T(128)S(1)} %copy-done.42, f32[28,8320]{1,0:T(8,128)S(1)} %convert_element_type.248, ...), kind=kLoop, calls=%fused_computation.66 | loop fusion | flops 2064356 | bytes 2753075 | tf_op jit(solution)/shard_map/reduce_sum | solution.py:264
  98.1 1.4 reshape.282
  102.1 0.9 multiply_reduce_fusion.6
  103.0 0.8 fusion.116
  103.9 0.8 fusion.117
  105.0 1.0 fusion.22
  106.2 1.2 collective-permute-done.12
  107.8 1.1 pad_maximum_fusion
  109.0 4.5 %all-to-all-start = ((bf16[8,36,1792]{2,1,0:T(8,128)(2,1)}), bf16[8,36,1792]{2,1,0:T(8,128)(2,1)S(1)}, u32[]{:S(2)}, u32[]{:S(2)}) async-start(bf16[8,36,1792]{2,1,0:T(8,128)(2,1)} %pad_maximum_fusion), calls=%async_computation | async-start | bytes 2293760 | tf_op jit(solution)/shard_map/all_to_all | solution.py:308
  113.7 2.5 %fusion.21 = f32[128,28,64]{0,2,1:T(8,128)} fusion(bf16[28,64,64]{2,1,0:T(8,128)(2,1)S(1)} %copy-done.15, bf16[128,28,64]{0,2,1:T(8,128)(2,1)} %fusion.17, f32[28,128]{1,0:T(8,128)S(1)} %copy.82, f32[28,64]{1,0:T(8,128)S(1)} %copy-done.28, f32[28,128]{1,0:T(8,128)S(1)} %copy.77, f32[128,64]{0,1:T(8,128)S(1)} %slice_convert_fusion, f32[128,28]{0,1:T(8,128)S(1)} %copy-done.21), kind=kOutput, calls=%fused_computation.32 | convolution fusion | flops 32112640 | bytes 1688576 | tf_op jit(solution)/shard_map/transpose(jvp(thn,thp->hnp))/dot_general | solution.py:33
  116.2 1.5 %copy.83 = f32[128,1792]{1,0:T(8,128)S(1)} copy(f32[128,1792]{0,1:T(8,128)} %bitcast.294) | data formatting | bytes 1835008 | tf_op jit(solution)/shard_map/reshape | solution.py:278
  118.3 1.3 collective-permute-start.13
  119.6 12.6 %collective-permute-done.13 = bf16[1,128,1792]{2,1,0:T(8,128)(2,1)S(1)} collective-permute-done((bf16[1,128,1792]{2,1,0:T(8,128)(2,1)S(1)}, bf16[1,128,1792]{2,1,0:T(8,128)(2,1)S(1)}, u32[]{:S(2)}, u32[]{:S(2)}) %collective-permute-start.13) | collective-permute-done | bytes 458784 | tf_op jit(solution)/shard_map/ppermute | solution.py:12
  132.2 8.9 %all-to-all-done = bf16[8,36,1792]{2,1,0:T(8,128)(2,1)S(1)} async-done(((bf16[8,36,1792]{2,1,0:T(8,128)(2,1)}), bf16[8,36,1792]{2,1,0:T(8,128)(2,1)S(1)}, u32[]{:S(2)}, u32[]{:S(2)}) %all-to-all-start) | async-done | bytes 1032224 | tf_op jit(solution)/shard_map/all_to_all | solution.py:308
  141.2 0.8 slice_add_fusion
  143.3 0.8 copy.130
  (208 shorter events, 17.3 us)
Async XLA Ops:
  0.6 15.9 %copy-start.45 = (f32[1,28]{1,0:T(1,128)S(1)}, f32[1,28]{1,0:T(1,128)}, u32[]{:S(2)}) copy-start(f32[1,28]{1,0:T(1,128)} %param.15) | copy-start | bytes 340
  0.6 15.9 %copy-start.13 = (bf16[1,128,1792]{2,1,0:T(8,128)(2,1)S(1)}, bf16[1,128,1792]{2,1,0:T(8,128)(2,1)}, u32[]{:S(2)}) copy-start(bf16[1,128,1792]{2,1,0:T(8,128)(2,1)} %param.11) | copy-start | bytes 1376260
  0.7 22.7 %collective-permute-start = (bf16[32,1792]{1,0:T(8,128)(2,1)}, bf16[32,1792]{1,0:T(8,128)(2,1)S(1)}, u32[]{:S(2)}, u32[]{:S(2)}) collective-permute-start(bf16[32,1792]{1,0:T(8,128)(2,1)} %bitcast.303), channel_id=1, source_target_pairs={{0,2},{2,4},{4,6},{6,8},{8,10},{10,12},{12,14},{14,0},{1,3},{3,5},... | collective-permute-start | bytes 344072 | tf_op jit(solution)/shard_map/ppermute | solution.py:18
  2.2 24.3 %collective-permute-start.1 = (bf16[32,1792]{1,0:T(8,128)(2,1)}, bf16[32,1792]{1,0:T(8,128)(2,1)S(1)}, u32[]{:S(2)}, u32[]{:S(2)}) collective-permute-start(bf16[32,1792]{1,0:T(8,128)(2,1)} %bitcast.304), channel_id=1, source_target_pairs={{0,4},{2,6},{4,8},{6,10},{8,12},{10,14},{12,0},{14,2},{1,5},{3,7},... | collective-permute-start | bytes 344072 | tf_op jit(solution)/shard_map/ppermute | solution.py:18
  3.8 22.9 %collective-permute-start.2 = (bf16[32,1792]{1,0:T(8,128)(2,1)}, bf16[32,1792]{1,0:T(8,128)(2,1)S(1)}, u32[]{:S(2)}, u32[]{:S(2)}) collective-permute-start(bf16[32,1792]{1,0:T(8,128)(2,1)} %bitcast.305), channel_id=1, source_target_pairs={{0,6},{2,8},{4,10},{6,12},{8,14},{10,0},{12,2},{14,4},{1,7},{3,9},... | collective-permute-start | bytes 344072 | tf_op jit(solution)/shard_map/ppermute | solution.py:18
  6.3 20.4 %collective-permute-start.3 = (bf16[32,1792]{1,0:T(8,128)(2,1)}, bf16[32,1792]{1,0:T(8,128)(2,1)S(1)}, u32[]{:S(2)}, u32[]{:S(2)}) collective-permute-start(bf16[32,1792]{1,0:T(8,128)(2,1)} %bitcast.306), channel_id=1, source_target_pairs={{0,8},{2,10},{4,12},{6,14},{8,0},{10,2},{12,4},{14,6},{1,9},{3,11}... | collective-permute-start | bytes 344072 | tf_op jit(solution)/shard_map/ppermute | solution.py:18
  7.9 10.7 %collective-permute-start.8 = (s32[1]{0:T(128)}, s32[1]{0:T(128)}, u32[]{:S(2)}, u32[]{:S(2)}) collective-permute-start(s32[1]{0:T(128)} %bitcast.13), channel_id=1, source_target_pairs={{0,2},{2,4},{4,6},{6,8},{8,10},{10,12},{12,14},{1,3},{3,5},{5,7},{... | collective-permute-start | bytes 20 | tf_op jit(solution)/shard_map/ppermute | solution.py:12
  14.6 4.0 %copy-start.17 = (bf16[1,32,1792]{2,1,0:T(8,128)(2,1)S(1)}, bf16[1,32,1792]{2,1,0:T(8,128)(2,1)}, u32[]{:S(2)}) copy-start(bf16[1,32,1792]{2,1,0:T(8,128)(2,1)} %param.12) | copy-start | bytes 344068
  14.6 7.8 %copy-start.30 = (f32[1,28]{1,0:T(1,128)S(1)}, f32[1,28]{1,0:T(1,128)}, u32[]{:S(2)}) copy-start(f32[1,28]{1,0:T(1,128)} %param.14) | copy-start | bytes 340
  15.9 30.9 %copy-start.6 = (bf16[1,128,1792]{1,2,0:T(8,128)(2,1)}, bf16[1,128,1792]{1,2,0:T(8,128)(2,1)S(1)}, u32[]{:S(2)}) copy-start(bf16[1,128,1792]{1,2,0:T(8,128)(2,1)S(1)} %copy.66) | copy-start | bytes 1376260
  16.5 10.2 %copy-start.10 = (f32[28,1,128]{0,2,1:T(8,128)}, f32[28,1,128]{0,2,1:T(8,128)S(1)}, u32[]{:S(2)}) copy-start(f32[28,1,128]{0,2,1:T(8,128)S(1)} %copy.87) | copy-start | bytes 43012
  16.6 6.3 %copy-start.53 = (f32[28]{0:T(128)}, f32[28]{0:T(128)S(1)}, u32[]{:S(2)}) copy-start(f32[28]{0:T(128)S(1)} %negate_bitcast_fusion) | copy-start | bytes 340
  16.8 15.5 %copy-start.4 = (bf16[1,128,1792]{2,1,0:T(8,128)(2,1)S(1)}, bf16[1,128,1792]{2,1,0:T(8,128)(2,1)}, u32[]{:S(2)}) copy-start(bf16[1,128,1792]{2,1,0:T(8,128)(2,1)} %param.9) | copy-start | bytes 1376260
  18.6 8.8 %collective-permute-start.4 = (bf16[32,1792]{1,0:T(8,128)(2,1)S(1)}, bf16[32,1792]{1,0:T(8,128)(2,1)S(1)}, u32[]{:S(2)}, u32[]{:S(2)}) collective-permute-start(bf16[32,1792]{1,0:T(8,128)(2,1)S(1)} %bitcast.307), channel_id=1, source_target_pairs={{0,10},{2,12},{4,14},{6,0},{8,2},{10,4},{12,6},{14,8},{1,11},{3,13... | collective-permute-start | bytes 344072 | tf_op jit(solution)/shard_map/ppermute | solution.py:18
  22.7 9.6 %copy-start.25 = (f32[128,28]{0,1:T(8,128)}, f32[128,28]{0,1:T(8,128)S(1)}, u32[]{:S(2)}) copy-start(f32[128,28]{0,1:T(8,128)S(1)} %get-tuple-element.96) | copy-start | bytes 43012
  22.7 13.1 %copy-start.18 = (f32[128,28]{0,1:T(8,128)}, f32[128,28]{0,1:T(8,128)S(1)}, u32[]{:S(2)}) copy-start(f32[128,28]{0,1:T(8,128)S(1)} %get-tuple-element.95) | copy-start | bytes 43012
  23.4 5.6 %collective-permute-start.5 = (bf16[32,1792]{1,0:T(8,128)(2,1)S(1)}, bf16[32,1792]{1,0:T(8,128)(2,1)S(1)}, u32[]{:S(2)}, u32[]{:S(2)}) collective-permute-start(bf16[32,1792]{1,0:T(8,128)(2,1)S(1)} %bitcast.308), channel_id=1, source_target_pairs={{0,12},{2,14},{4,0},{6,2},{8,4},{10,6},{12,8},{14,10},{1,13},{3,15... | collective-permute-start | bytes 344072 | tf_op jit(solution)/shard_map/ppermute | solution.py:18
  26.6 5.7 %collective-permute-start.6 = (bf16[32,1792]{1,0:T(8,128)(2,1)S(1)}, bf16[32,1792]{1,0:T(8,128)(2,1)S(1)}, u32[]{:S(2)}, u32[]{:S(2)}) collective-permute-start(bf16[32,1792]{1,0:T(8,128)(2,1)S(1)} %bitcast.309), channel_id=1, source_target_pairs={{0,14},{2,0},{4,2},{6,4},{8,6},{10,8},{12,10},{14,12},{1,15},{3,1}... | collective-permute-start | bytes 344072 | tf_op jit(solution)/shard_map/ppermute | solution.py:18
  32.8 2.2 %collective-permute-start.7 = (bf16[128,128]{0,1:T(8,128)(2,1)S(1)}, bf16[128,128]{0,1:T(8,128)(2,1)S(1)}, u32[]{:S(2)}, u32[]{:S(2)}) collective-permute-start(bf16[128,128]{0,1:T(8,128)(2,1)S(1)} %fusion.48), channel_id=1, source_target_pairs={{0,1},{1,0},{2,3},{3,2},{4,5},{5,4},{6,7},{7,6},{8,9},{9,8},{10,11... | collective-permute-start | bytes 98312 | tf_op jit(solution)/shard_map/ppermute | solution.py:29
  37.7 3.4 %copy-start.8 = (f32[128,28,64]{0,2,1:T(8,128)S(1)}, f32[128,28,64]{0,2,1:T(8,128)}, u32[]{:S(2)}) copy-start(f32[128,28,64]{0,2,1:T(8,128)} %convert.51) | copy-start | bytes 2752516
  39.3 24.4 %copy-start = (f32[28,4096]{1,0:T(8,128)}, f32[28,4096]{1,0:T(8,128)S(1)}, u32[]{:S(2)}) copy-start(f32[28,4096]{1,0:T(8,128)S(1)} %reshape.281) | copy-start | bytes 1376260
  43.8 4.5 %copy-start.12 = (bf16[28,8320]{1,0:T(8,128)(2,1)S(1)}, bf16[28,8320]{1,0:T(8,128)(2,1)}, u32[]{:S(2)}) copy-start(bf16[28,8320]{1,0:T(8,128)(2,1)} %concatenate.41) | copy-start | bytes 1397764
  43.8 5.1 %copy-start.50 = (f32[1,28]{1,0:T(1,128)S(1)}, f32[1,28]{1,0:T(1,128)}, u32[]{:S(2)}) copy-start(f32[1,28]{1,0:T(1,128)} %param.16) | copy-start | bytes 340
  43.8 5.7 %copy-start.27 = (f32[28,64]{1,0:T(8,128)S(1)}, f32[28,64]{1,0:T(8,128)}, u32[]{:S(2)}) copy-start(f32[28,64]{1,0:T(8,128)} %reshape_squeeze.7) | copy-start | bytes 21508
  48.3 14.5 %collective-permute-start.9 = (bf16[28,8320]{1,0:T(8,128)(2,1)S(1)}, bf16[28,8320]{1,0:T(8,128)(2,1)S(1)}, u32[]{:S(2)}, u32[]{:S(2)}) collective-permute-start(bf16[28,8320]{1,0:T(8,128)(2,1)S(1)} %copy-done.12), channel_id=1, source_target_pairs={{0,2},{2,0},{4,6},{6,4},{8,10},{10,8},{12,14},{14,12},{1,3},{3,1},... | collective-permute-start | bytes 1397768 | tf_op jit(solution)/shard_map/ppermute | solution.py:148
  49.5 13.4 %copy-start.22 = (f32[28,1]{1,0:T(8,128)S(1)}, f32[28,1]{1,0:T(8,128)}, u32[]{:S(2)}) copy-start(f32[28,1]{1,0:T(8,128)} %copy.74) | copy-start | bytes 340
  49.5 14.2 %copy-start.49 = (f32[28]{0:T(128)S(1)}, f32[28]{0:T(128)}, u32[]{:S(2)}) copy-start(f32[28]{0:T(128)} %exponential_multiply_fusion.1) | copy-start | bytes 340
  64.2 13.9 %collective-permute-start.10 = (bf16[28,8320]{1,0:T(8,128)(2,1)S(1)}, bf16[28,8320]{1,0:T(8,128)(2,1)}, u32[]{:S(2)}, u32[]{:S(2)}) collective-permute-start(bf16[28,8320]{1,0:T(8,128)(2,1)S(1)} %concatenate.42), channel_id=1, source_target_pairs={{0,4},{2,6},{4,0},{6,2},{8,12},{10,14},{12,8},{14,10},{1,5},{3,7},... | collective-permute-start | bytes 1397768 | tf_op jit(solution)/shard_map/ppermute | solution.py:148
  64.3 15.7 %copy-start.1 = (f32[28,4096]{1,0:T(8,128)S(1)}, f32[28,4096]{1,0:T(8,128)}, u32[]{:S(2)}) copy-start(f32[28,4096]{1,0:T(8,128)} %copy-done) | copy-start | bytes 1376260
  81.1 14.2 %copy-start.40 = (f32[28]{0:T(128)S(1)}, f32[28]{0:T(128)}, u32[]{:S(2)}) copy-start(f32[28]{0:T(128)} %get-tuple-element.52) | copy-start | bytes 340
  81.1 14.2 %copy-start.41 = (f32[28]{0:T(128)S(1)}, f32[28]{0:T(128)}, u32[]{:S(2)}) copy-start(f32[28]{0:T(128)} %get-tuple-element.53) | copy-start | bytes 340
  81.1 14.2 %copy-start.42 = (f32[28]{0:T(128)S(1)}, f32[28]{0:T(128)}, u32[]{:S(2)}) copy-start(f32[28]{0:T(128)} %get-tuple-element.54) | copy-start | bytes 340
  81.2 14.2 %copy-start.43 = (f32[28]{0:T(128)S(1)}, f32[28]{0:T(128)}, u32[]{:S(2)}) copy-start(f32[28]{0:T(128)} %get-tuple-element.56) | copy-start | bytes 340
  81.3 14.1 %collective-permute-start.11 = (bf16[28,4224]{1,0:T(8,128)(2,1)S(1)}, bf16[28,4224]{1,0:T(8,128)(2,1)}, u32[]{:S(2)}, u32[]{:S(2)}) collective-permute-start(bf16[28,4224]{1,0:T(8,128)(2,1)S(1)} %concatenate.43), channel_id=1, source_target_pairs={{0,8},{2,10},{4,12},{6,14},{8,0},{10,2},{12,4},{14,6},{1,9},{3,11}... | collective-permute-start | bytes 709640 | tf_op jit(solution)/shard_map/ppermute | solution.py:155
  101.1 3.7 %copy-start.24 = (f32[28,1,64]{2,0,1:T(8,128)S(1)}, f32[28,1,64]{2,0,1:T(8,128)}, u32[]{:S(2)}) copy-start(f32[28,1,64]{2,0,1:T(8,128)} %copy.121) | copy-start | bytes 21508
  101.1 3.7 %copy-start.47 = (f32[1,28]{1,0:T(1,128)S(1)}, f32[1,28]{1,0:T(1,128)}, u32[]{:S(2)}) copy-start(f32[1,28]{1,0:T(1,128)} %param.15) | copy-start | bytes 340
  101.1 3.7 %copy-start.48 = (f32[28]{0:T(128)S(1)}, f32[28]{0:T(128)}, u32[]{:S(2)}) copy-start(f32[28]{0:T(128)} %get-tuple-element.42) | copy-start | bytes 340
  101.2 3.7 %copy-start.52 = (f32[28]{0:T(128)S(1)}, f32[28]{0:T(128)}, u32[]{:S(2)}) copy-start(f32[28]{0:T(128)} %get-tuple-element.41) | copy-start | bytes 340
  101.2 3.8 %copy-start.37 = (f32[28]{0:T(128)S(1)}, f32[28]{0:T(128)}, u32[]{:S(2)}) copy-start(f32[28]{0:T(128)} %multiply_reduce_fusion.3) | copy-start | bytes 340
  101.2 3.9 %copy-start.9 = (f32[1,128,1792]{1,2,0:T(8,128)S(1)}, f32[1,128,1792]{1,2,0:T(8,128)}, u32[]{:S(2)}) copy-start(f32[1,128,1792]{1,2,0:T(8,128)} %bitcast_multiply_fusion) | copy-start | bytes 2752516
  102.0 4.0 %copy-start.16 = (bf16[128,128]{0,1:T(8,128)(2,1)S(1)}, bf16[128,128]{0,1:T(8,128)(2,1)}, u32[]{:S(2)}) copy-start(bf16[128,128]{0,1:T(8,128)(2,1)} %pad_add_fusion) | copy-start | bytes 98308
  103.0 4.4 %copy-start.5 = (bf16[1,128,1792]{2,1,0:T(8,128)(2,1)S(1)}, bf16[1,128,1792]{2,1,0:T(8,128)(2,1)}, u32[]{:S(2)}) copy-start(bf16[1,128,1792]{2,1,0:T(8,128)(2,1)} %param.9) | copy-start | bytes 1376260
  106.1 1.3 collective-permute-start.12
  107.8 5.8 %copy-start.15 = (bf16[28,64,64]{2,1,0:T(8,128)(2,1)S(1)}, bf16[28,64,64]{2,1,0:T(8,128)(2,1)}, u32[]{:S(2)}) copy-start(bf16[28,64,64]{2,1,0:T(8,128)(2,1)} %copy-done.14) | copy-start | bytes 688132
  107.8 5.8 %copy-start.28 = (f32[28,64]{1,0:T(8,128)S(1)}, f32[28,64]{1,0:T(8,128)}, u32[]{:S(2)}) copy-start(f32[28,64]{1,0:T(8,128)} %reshape_squeeze.7) | copy-start | bytes 21508
  109.0 32.1 %all-to-all-start = ((bf16[8,36,1792]{2,1,0:T(8,128)(2,1)}), bf16[8,36,1792]{2,1,0:T(8,128)(2,1)S(1)}, u32[]{:S(2)}, u32[]{:S(2)}) async-start(bf16[8,36,1792]{2,1,0:T(8,128)(2,1)} %pad_maximum_fusion), calls=%async_computation | async-start | bytes 2293760 | tf_op jit(solution)/shard_map/all_to_all | solution.py:308
  113.7 4.3 %copy-start.3 = (bf16[256,1792]{1,0:T(8,128)(2,1)S(1)}, bf16[256,1792]{1,0:T(8,128)(2,1)}, u32[]{:S(2)}) copy-start(bf16[256,1792]{1,0:T(8,128)(2,1)} %copy-done.2) | copy-start | bytes 2752516
  118.3 13.9 %collective-permute-start.13 = (bf16[1,128,1792]{2,1,0:T(8,128)(2,1)S(1)}, bf16[1,128,1792]{2,1,0:T(8,128)(2,1)S(1)}, u32[]{:S(2)}, u32[]{:S(2)}) collective-permute-start(bf16[1,128,1792]{2,1,0:T(8,128)(2,1)S(1)} %fusion.1), channel_id=1, source_target_pairs={{16,0},{17,1},{18,2},{19,3},{20,4},{21,5},{22,6},{23,7},{24,8},{25... | collective-permute-start | bytes 1376264 | tf_op jit(solution)/shard_map/ppermute | solution.py:12
  (21 other events, 36.5 us)

commit v10 on v5

--- a/solution.py
+++ b/solution.py
@@ -118,13 +118,12 @@
     return near_state
 
 
-def both_scans(decay, state, state_grad, axis, filler_fn, filler_args):
+def both_scans(decay, state, state_grad, axis):
     size, mine = (lax.axis_size(axis), lax.axis_index(axis))
     if size & (size - 1):
         return (
             scan_rounds(decay, state, axis, True),
             scan_rounds(decay, state_grad, axis, False),
-            filler_fn(*filler_args),
         )
     width = state.shape[1]
     total_decay = decay
@@ -142,8 +141,6 @@
             [total_fwd, total_bwd, high[:, None], low[:, None], pad], axis=1
         ).astype(jnp.bfloat16)
         upper = (mine // distance) % 2 == 1
-        if distance == 1:
-            payload, filler_args = lax.optimization_barrier((payload, filler_args))
         if distance * 2 < size:
             got = lax.ppermute(payload, axis, [(i, i ^ distance) for i in range(size)])
             got = got.astype(jnp.float32)
@@ -157,8 +154,6 @@
             got_fwd = got[:, :width]
             got_bwd = got_fwd
             got = jnp.concatenate([got[:, :width], got], axis=1)
-        if distance == 1:
-            got, filler = lax.optimization_barrier((got, filler_fn(*filler_args)))
         got_decay = got[:, 2 * width] + got[:, 2 * width + 1]
         before = jnp.where(upper, before + before_decay[:, None] * got_fwd, before)
         before_decay = jnp.where(upper, before_decay * got_decay, before_decay)
@@ -177,7 +172,7 @@
             )
             total_decay = total_decay * got_decay
         distance *= 2
-    return (before, after, filler)
+    return (before, after)
 
 
 def shards(bwd_input, bwd_docs, bwd_grad, proj_weight, step_weight, step_bias, rate_log, skip_gain):
@@ -227,9 +222,9 @@
     def local_bwd(values_in, mixer_in, weight_in, bias_in, rate_in, skip_in):
         return span_local(values_in, mixer_in, weight_in, bias_in, rate_in, skip_in, docs_bwd)
 
-    def local_pull(*primals):
-        return jax.vjp(local_bwd, *primals[:-1])[1](primals[-1])
-
+    local_grads = jax.vjp(
+        local_bwd, bwd_values, mixer_bwd, weight_heads, bias_heads, rate_heads, skip_heads
+    )[1](out_ct)
 
     def carry_bwd(values_in, mixer_in, weight_in, bias_in, rate_in, state_in):
         return span_carry(
@@ -241,14 +236,7 @@
 
     state_grad = jax.vjp(carried_only, jnp.zeros(state_shape, jnp.float32))[1](out_ct)[0]
     state_grad = state_grad.reshape(heads_here, -1)
-    incoming_flat, adjoint_flat, local_grads = both_scans(
-        decay_bwd,
-        state_flat,
-        state_grad,
-        "seq",
-        local_pull,
-        (bwd_values, mixer_bwd, weight_heads, bias_heads, rate_heads, skip_heads, out_ct),
-    )
+    incoming_flat, adjoint_flat = both_scans(decay_bwd, state_flat, state_grad, "seq")
     incoming_bwd = incoming_flat.reshape(state_shape)
     carry_grads = jax.vjp(
         carry_bwd, bwd_values, mixer_bwd, weight_heads, bias_heads, rate_heads, incoming_bwd

time: 145 us -> 146 us (level)
  starting transfers between devices: 36.1 us -> 25.5 us
  other arithmetic: 14 us -> 18.7 us
  waiting for transfers between devices: 57.4 us -> 61.9 us
    ppermute x14, waiting for transfers between devices: 11.7 us -> 27.3 us  [rotated(): return lax.ppermute(block, axis, route)]
    ppermute x14, starting transfers between devices: 29.5 us -> 18.9 us  [rotated(): return lax.ppermute(block, axis, route)]
    ppermute x2, waiting for transfers between devices: 7 us -> 0.01 us  [shifted(): return lax.ppermute(block, axis, route)]
    ppermute x1, waiting for transfers between devices: 12.3 us -> 7.03 us  [both_scans(): got = lax.ppermute(last, axis, [(i, i ^ distance) for i in range(size)])]
    reduce_sum x1 -> x2, other arithmetic: 0.3 us -> 2.94 us  [span_local(): values.astype(jnp.float32) * (1.0 + skip_gain)[None, :, None] + local_part]
    dot_general x5, matrix products: 6.82 us -> 5.16 us  [contract(): return jnp.einsum(spec, left, right, preferred_element_type=jnp.float32)]
    concatenate x2, other arithmetic: 1.6 us -> 0.08 us  [shards(): jnp.concatenate([row_parts[k].astype(jnp.bfloat16), small_coded], axis=0)]
    unnamed x144 -> x154, local copies, waits for them, and re-layouts: 4.32 us -> 5.38 us
  transfers between devices with their start and end apart: 21 -> 21, of which waited for: 11 -> 11; matrix products, arithmetic and copies ran while one was open for 15% -> 17% of each run, Pallas kernels for 0% -> 0%
where the time goes in v10:
time: 146 us; the launch traced here: 144 us
  waiting for transfers between devices  61.9 us (42%)
  starting transfers between devices  25.5 us (17%)
  other arithmetic  18.7 us (13%)
  matrix products  17.9 us (12%)
  local copies, waits for them, and re-layouts  16.9 us (12%)
  between operations  3.36 us (2%)
    ppermute x14, waiting for transfers between devices, rotated(): return lax.ppermute(block, axis, route)  27.3 us
    ppermute x2, waiting for transfers between devices, both_scans(): got = lax.ppermute(payload, axis, [(i, i ^ distance) for i in range(size)])  26.7 us
    ppermute x14, starting transfers between devices, rotated(): return lax.ppermute(block, axis, route)  18.9 us
    ppermute x1, waiting for transfers between devices, both_scans(): got = lax.ppermute(last, axis, [(i, i ^ distance) for i in range(size)])  7.03 us
    ppermute x2, starting transfers between devices, shifted(): return lax.ppermute(block, axis, route)  5.6 us
    unnamed x154, local copies, waits for them, and re-layouts  5.38 us
    dot_general x5, matrix products, contract(): return jnp.einsum(spec, left, right, preferred_element_type=jnp.float32)  5.16 us
    dot_general x4, matrix products, local_setup(): jnp.einsum('thp,hp->th', values.astype(jnp.float32), step_weight, precisi...  2.98 us
  transfers between devices with their start and end apart: 21, of which 11 were waited for; matrix products, arithmetic and copies ran while one was open for 17% of the time, Pallas kernels for 0%

profile of v10, /device:TPU:4, one launch (start us, length us, event | category | flops | bytes accessed | tf_op | source)
XLA Modules:
  0.0 144.3 jit_solution(11751527806089769006)
XLA Ops:
  0.7 1.6 %collective-permute-start = (bf16[32,1792]{1,0:T(8,128)(2,1)}, bf16[32,1792]{1,0:T(8,128)(2,1)S(1)}, u32[]{:S(2)}, u32[]{:S(2)}) collective-permute-start(bf16[32,1792]{1,0:T(8,128)(2,1)} %bitcast.309), channel_id=1, source_target_pairs={{0,2},{2,4},{4,6},{6,8},{8,10},{10,12},{12,14},{14,0},{1,3},{3,5},... | collective-permute-start | bytes 344072 | tf_op jit(solution)/shard_map/ppermute | solution.py:18
  2.2 1.6 %collective-permute-start.1 = (bf16[32,1792]{1,0:T(8,128)(2,1)}, bf16[32,1792]{1,0:T(8,128)(2,1)S(1)}, u32[]{:S(2)}, u32[]{:S(2)}) collective-permute-start(bf16[32,1792]{1,0:T(8,128)(2,1)} %bitcast.310), channel_id=1, source_target_pairs={{0,4},{2,6},{4,8},{6,10},{8,12},{10,14},{12,0},{14,2},{1,5},{3,7},... | collective-permute-start | bytes 344072 | tf_op jit(solution)/shard_map/ppermute | solution.py:18
  3.8 2.5 %collective-permute-start.2 = (bf16[32,1792]{1,0:T(8,128)(2,1)}, bf16[32,1792]{1,0:T(8,128)(2,1)S(1)}, u32[]{:S(2)}, u32[]{:S(2)}) collective-permute-start(bf16[32,1792]{1,0:T(8,128)(2,1)} %bitcast.311), channel_id=1, source_target_pairs={{0,6},{2,8},{4,10},{6,12},{8,14},{10,0},{12,2},{14,4},{1,7},{3,9},... | collective-permute-start | bytes 344072 | tf_op jit(solution)/shard_map/ppermute | solution.py:18
  6.7 1.2 slice.178
  7.9 4.3 %collective-permute-start.8 = (s32[1]{0:T(128)}, s32[1]{0:T(128)}, u32[]{:S(2)}, u32[]{:S(2)}) collective-permute-start(s32[1]{0:T(128)} %bitcast.23), channel_id=1, source_target_pairs={{0,2},{2,4},{4,6},{6,8},{8,10},{10,12},{12,14},{1,3},{3,5},{5,7},{... | collective-permute-start | bytes 20 | tf_op jit(solution)/shard_map/ppermute | solution.py:12
  12.3 0.9 constant_dynamic-update-slice_fusion.7
  13.2 1.3 copy.91
  16.0 1.3 copy.92
  18.0 1.3 collective-permute-start.4
  19.3 1.2 broadcast_compare_fusion.1
  22.3 3.8 %collective-permute-start.5 = (bf16[32,1792]{1,0:T(8,128)(2,1)S(1)}, bf16[32,1792]{1,0:T(8,128)(2,1)S(1)}, u32[]{:S(2)}, u32[]{:S(2)}) collective-permute-start(bf16[32,1792]{1,0:T(8,128)(2,1)S(1)} %bitcast.314), channel_id=1, source_target_pairs={{0,12},{2,14},{4,0},{6,2},{8,4},{10,6},{12,8},{14,10},{1,13},{3,15... | collective-permute-start | bytes 344072 | tf_op jit(solution)/shard_map/ppermute | solution.py:18
  26.9 1.7 %collective-permute-done.5 = bf16[32,1792]{1,0:T(8,128)(2,1)S(1)} collective-permute-done((bf16[32,1792]{1,0:T(8,128)(2,1)S(1)}, bf16[32,1792]{1,0:T(8,128)(2,1)S(1)}, u32[]{:S(2)}, u32[]{:S(2)}) %collective-permute-start.5) | collective-permute-done | bytes 114720 | tf_op jit(solution)/shard_map/ppermute | solution.py:18
  28.6 3.4 %collective-permute-done.6 = bf16[32,1792]{1,0:T(8,128)(2,1)S(1)} collective-permute-done((bf16[32,1792]{1,0:T(8,128)(2,1)S(1)}, bf16[32,1792]{1,0:T(8,128)(2,1)S(1)}, u32[]{:S(2)}, u32[]{:S(2)}) %collective-permute-start.6) | collective-permute-done | bytes 114720 | tf_op jit(solution)/shard_map/ppermute | solution.py:18
  32.9 0.9 collective-permute-done.7
  33.9 1.5 %convolution_bitcast_fusion = f32[28,64,64]{1,2,0:T(8,128)} fusion(bf16[128,28,64]{0,2,1:T(8,128)(2,1)S(1)} %bitcast.282, f32[128,28]{0,1:T(8,128)S(1)} %get-tuple-element.79, bf16[128,128]{0,1:T(8,128)(2,1)S(1)} %fusion.63), kind=kOutput, calls=%fused_computation.22 | convolution fusion | flops 176619520 | bytes 950272 | tf_op jit(solution)/shard_map/transpose(jvp(tn,hnp->thp))/dot_general | solution.py:97
  35.4 1.5 %copy.100 = f32[28,64,64]{2,1,0:T(8,128)S(1)} copy(f32[28,64,64]{1,2,0:T(8,128)} %convolution_bitcast_fusion) | data formatting | bytes 917504 | tf_op jit(solution)/shard_map/transpose(jvp(tn,hnp->thp))/transpose | solution.py:97
  38.7 14.0 %collective-permute-done.9 = bf16[28,8320]{1,0:T(8,128)(2,1)S(1)} collective-permute-done((bf16[28,8320]{1,0:T(8,128)(2,1)S(1)}, bf16[28,8320]{1,0:T(8,128)(2,1)S(1)}, u32[]{:S(2)}, u32[]{:S(2)}) %collective-permute-start.9) | collective-permute-done | bytes 465952 | tf_op jit(solution)/shard_map/ppermute | solution.py:145
  55.0 12.6 %collective-permute-done.10 = bf16[28,8320]{1,0:T(8,128)(2,1)} collective-permute-done((bf16[28,8320]{1,0:T(8,128)(2,1)S(1)}, bf16[28,8320]{1,0:T(8,128)(2,1)}, u32[]{:S(2)}, u32[]{:S(2)}) %collective-permute-start.10) | collective-permute-done | bytes 465952 | tf_op jit(solution)/shard_map/ppermute | solution.py:145
  67.6 1.1 convert_element_type.284
  69.4 1.3 fusion.84
  70.7 1.1 select_convert_fusion
  71.9 0.8 concatenate.73
  73.4 1.2 add_bitcast_fusion
  74.6 1.4 reshape_squeeze.10
  76.0 2.3 %fusion.25 = (f32[1792]{0:T(1024)S(1)}, f32[1,128,1792]{1,2,0:T(8,128)}) fusion(bf16[1,128,1792]{1,2,0:T(8,128)(2,1)} %copy-done, bf16[1,128,1792]{1,2,0:T(8,128)(2,1)} %copy-done.4, f32[128,28]{0,1:T(8,128)} %copy-done.22), kind=kLoop, calls=%fused_computation.43 | loop fusion | flops 1145088 | bytes 1856512 | tf_op jit(solution)/shard_map/transpose(jvp())/reduce_sum | solution.py:88
  79.2 7.0 %collective-permute-done.11 = bf16[28,4224]{1,0:T(8,128)(2,1)S(1)} collective-permute-done((bf16[28,4224]{1,0:T(8,128)(2,1)S(1)}, bf16[28,4224]{1,0:T(8,128)(2,1)S(1)}, u32[]{:S(2)}, u32[]{:S(2)}) %collective-permute-start.11) | collective-permute-done | bytes 236576 | tf_op jit(solution)/shard_map/ppermute | solution.py:152
  86.3 1.8 %multiply_reduce_fusion.2 = (f32[28]{0:T(128)}, bf16[28,4096]{1,0:T(8,128)(2,1)S(1)}, f32[28,4096]{1,0:T(8,128)}) fusion(bf16[28,4224]{1,0:T(8,128)(2,1)S(1)} %collective-permute-done.11, f32[28]{0:T(128)S(1)} %copy-done.52, f32[28,8320]{1,0:T(8,128)S(1)} %convert_element_type.284, f32[28]{0:T(128)S(1)} %copy-done.54, ...), kind=kLoop, calls=%fused_computation.66 | loop fusion | flops 2064356 | bytes 2753075 | tf_op jit(solution)/shard_map/reduce_sum | solution.py:252
  88.6 0.9 multiply_reduce_fusion
  89.7 1.2 fusion.111
  91.1 2.5 %fusion.12 = (f32[28,128]{1,0:T(8,128)}, f32[28,128]{1,0:T(8,128)}, f32[28,128]{1,0:T(8,128)}, bf16[128,128]{1,0:T(8,128)(2,1)S(1)}) fusion(f32[28,128]{1,0:T(8,128)S(1)} %copy.93, f32[128,128]{1,0:T(8,128)S(1)} %fusion.92, f32[128,128]{1,0:T(8,128)S(1)} %copy-done.27, f32[28,128]{1,0:T(8,128)S(1)} %bitcast.316, pred[128,128]{1,0:T(8,128)(4,1)S(1)} %copy-done.37, ...), kind=kOutput, calls=%fused_computation.18 | convolution fusion | flops 66491904 | bytes 1169408 | tf_op jit(solution)/shard_map/transpose(jvp(hts,shp->thp))/dot_general | solution.py:33
  95.5 1.2 copy.104
  96.8 1.8 %fusion.95 = f32[128,1792]{0,1:S(1)} fusion(f32[64,1792]{0,1:T(8,128)} %bitcast.296, bf16[128,128]{0,1:T(8,128)(2,1)S(1)} %fusion.63), kind=kOutput, calls=%fused_computation.222 | convolution fusion | flops 176160768 | bytes 1392640
  99.5 1.0 multiply_reduce_fusion.5
  100.8 1.0 fusion.24
  102.0 0.8 fusion.119
  102.9 0.8 fusion.118
  103.8 0.8 fusion.117
  105.0 0.9 fusion.23
  107.2 1.1 fusion.1
  108.2 1.3 collective-permute-start.13
  110.2 1.0 collective-permute-start.20
  111.3 1.9 %collective-permute-start.19 = (bf16[36,1792]{1,0:T(8,128)(2,1)S(1)}, bf16[36,1792]{1,0:T(8,128)(2,1)S(1)}, u32[]{:S(2)}, u32[]{:S(2)}) collective-permute-start(bf16[36,1792]{1,0:T(8,128)(2,1)S(1)} %get-tuple-element.73), channel_id=1, source_target_pairs={{0,12},{2,14},{4,0},{6,2},{8,4},{10,6},{12,8},{14,10},{1,13},{3,15... | collective-permute-start | bytes 387080 | tf_op jit(solution)/shard_map/ppermute | solution.py:18
  113.2 3.4 %collective-permute-start.17 = (bf16[36,1792]{1,0:T(8,128)(2,1)S(1)}, bf16[36,1792]{1,0:T(8,128)(2,1)S(1)}, u32[]{:S(2)}, u32[]{:S(2)}) collective-permute-start(bf16[36,1792]{1,0:T(8,128)(2,1)S(1)} %get-tuple-element.71), channel_id=1, source_target_pairs={{0,8},{2,10},{4,12},{6,14},{8,0},{10,2},{12,4},{14,6},{1,9},{3,11}... | collective-permute-start | bytes 387080 | tf_op jit(solution)/shard_map/ppermute | solution.py:18
  116.6 1.1 collective-permute-done.20
  117.9 1.3 collective-permute-start.15
  119.3 15.4 %collective-permute-done.18 = bf16[36,1792]{1,0:T(8,128)(2,1)S(1)} collective-permute-done((bf16[36,1792]{1,0:T(8,128)(2,1)S(1)}, bf16[36,1792]{1,0:T(8,128)(2,1)S(1)}, u32[]{:S(2)}, u32[]{:S(2)}) %collective-permute-start.18) | collective-permute-done | bytes 129056 | tf_op jit(solution)/shard_map/ppermute | solution.py:18
  134.8 5.0 %collective-permute-done.14 = bf16[36,1792]{1,0:T(8,128)(2,1)S(1)} collective-permute-done((bf16[36,1792]{1,0:T(8,128)(2,1)S(1)}, bf16[36,1792]{1,0:T(8,128)(2,1)S(1)}, u32[]{:S(2)}, u32[]{:S(2)}) %collective-permute-start.14) | collective-permute-done | bytes 129056 | tf_op jit(solution)/shard_map/ppermute | solution.py:18
  140.6 1.7 %fusion.53 = f32[1,32,1792]{2,1,0:T(8,128)} fusion(f32[256,1792]{1,0:T(8,128)S(1)} %get-tuple-element.82, bf16[36,1792]{1,0:T(8,128)(2,1)S(1)} %collective-permute-done.20, bf16[36,1792]{1,0:T(8,128)(2,1)S(1)} %collective-permute-done.19, bf16[36,1792]{1,0:T(8,128)(2,1)S(1)} %collective-permute-done.18, bf16[36,1792]{1,0:T(8,128)(2,1)S(1)} %collective-permute-done.17, ...), kind=kLoop, calls=%fused_computation.106 | loop fusion | flops 802816 | bytes 1261568 | tf_op jit(solution)/shard_map/broadcast_in_dim | solution.py:312
  (255 shorter events, 19.8 us)
Async XLA Ops:
  0.6 17.3 %copy-start.20 = (bf16[1,32,1792]{2,1,0:T(8,128)(2,1)S(1)}, bf16[1,32,1792]{2,1,0:T(8,128)(2,1)}, u32[]{:S(2)}) copy-start(bf16[1,32,1792]{2,1,0:T(8,128)(2,1)} %param.12) | copy-start | bytes 344068
  0.6 18.7 %copy-start.46 = (s32[1,128]{1,0:T(1,128)S(1)}, s32[1,128]{1,0:T(1,128)}, u32[]{:S(2)}) copy-start(s32[1,128]{1,0:T(1,128)} %param.10) | copy-start | bytes 1540
  0.7 21.1 %copy-start.48 = (f32[1,28]{1,0:T(1,128)S(1)}, f32[1,28]{1,0:T(1,128)}, u32[]{:S(2)}) copy-start(f32[1,28]{1,0:T(1,128)} %param.14) | copy-start | bytes 340
  0.7 21.7 %collective-permute-start = (bf16[32,1792]{1,0:T(8,128)(2,1)}, bf16[32,1792]{1,0:T(8,128)(2,1)S(1)}, u32[]{:S(2)}, u32[]{:S(2)}) collective-permute-start(bf16[32,1792]{1,0:T(8,128)(2,1)} %bitcast.309), channel_id=1, source_target_pairs={{0,2},{2,4},{4,6},{6,8},{8,10},{10,12},{12,14},{14,0},{1,3},{3,5},... | collective-permute-start | bytes 344072 | tf_op jit(solution)/shard_map/ppermute | solution.py:18
  2.2 24.0 %collective-permute-start.1 = (bf16[32,1792]{1,0:T(8,128)(2,1)}, bf16[32,1792]{1,0:T(8,128)(2,1)S(1)}, u32[]{:S(2)}, u32[]{:S(2)}) collective-permute-start(bf16[32,1792]{1,0:T(8,128)(2,1)} %bitcast.310), channel_id=1, source_target_pairs={{0,4},{2,6},{4,8},{6,10},{8,12},{10,14},{12,0},{14,2},{1,5},{3,7},... | collective-permute-start | bytes 344072 | tf_op jit(solution)/shard_map/ppermute | solution.py:18
  3.8 22.5 %collective-permute-start.2 = (bf16[32,1792]{1,0:T(8,128)(2,1)}, bf16[32,1792]{1,0:T(8,128)(2,1)S(1)}, u32[]{:S(2)}, u32[]{:S(2)}) collective-permute-start(bf16[32,1792]{1,0:T(8,128)(2,1)} %bitcast.311), channel_id=1, source_target_pairs={{0,6},{2,8},{4,10},{6,12},{8,14},{10,0},{12,2},{14,4},{1,7},{3,9},... | collective-permute-start | bytes 344072 | tf_op jit(solution)/shard_map/ppermute | solution.py:18
  6.3 20.0 %collective-permute-start.3 = (bf16[32,1792]{1,0:T(8,128)(2,1)}, bf16[32,1792]{1,0:T(8,128)(2,1)S(1)}, u32[]{:S(2)}, u32[]{:S(2)}) collective-permute-start(bf16[32,1792]{1,0:T(8,128)(2,1)} %bitcast.312), channel_id=1, source_target_pairs={{0,8},{2,10},{4,12},{6,14},{8,0},{10,2},{12,4},{14,6},{1,9},{3,11}... | collective-permute-start | bytes 344072 | tf_op jit(solution)/shard_map/ppermute | solution.py:18
  7.9 10.0 %collective-permute-start.8 = (s32[1]{0:T(128)}, s32[1]{0:T(128)}, u32[]{:S(2)}, u32[]{:S(2)}) collective-permute-start(s32[1]{0:T(128)} %bitcast.23), channel_id=1, source_target_pairs={{0,2},{2,4},{4,6},{6,8},{8,10},{10,12},{12,14},{1,3},{3,5},{5,7},{... | collective-permute-start | bytes 20 | tf_op jit(solution)/shard_map/ppermute | solution.py:12
  14.4 19.4 %copy-start = (bf16[1,128,1792]{1,2,0:T(8,128)(2,1)}, bf16[1,128,1792]{1,2,0:T(8,128)(2,1)S(1)}, u32[]{:S(2)}) copy-start(bf16[1,128,1792]{1,2,0:T(8,128)(2,1)S(1)} %copy.91) | copy-start | bytes 1376260
  14.5 17.5 %copy-start.6 = (bf16[1,128,1792]{2,1,0:T(8,128)(2,1)S(1)}, bf16[1,128,1792]{2,1,0:T(8,128)(2,1)}, u32[]{:S(2)}) copy-start(bf16[1,128,1792]{2,1,0:T(8,128)(2,1)} %param.9) | copy-start | bytes 1376260
  15.2 17.2 %copy-start.63 = (f32[28]{0:T(128)}, f32[28]{0:T(128)S(1)}, u32[]{:S(2)}) copy-start(f32[28]{0:T(128)S(1)} %negate_bitcast_fusion) | copy-start | bytes 340
  17.3 19.9 %copy-start.4 = (bf16[1,128,1792]{1,2,0:T(8,128)(2,1)}, bf16[1,128,1792]{1,2,0:T(8,128)(2,1)S(1)}, u32[]{:S(2)}) copy-start(bf16[1,128,1792]{1,2,0:T(8,128)(2,1)S(1)} %copy.92) | copy-start | bytes 1376260
  17.9 14.5 %copy-start.12 = (f32[28,1,128]{0,2,1:T(8,128)}, f32[28,1,128]{0,2,1:T(8,128)S(1)}, u32[]{:S(2)}) copy-start(f32[28,1,128]{0,2,1:T(8,128)S(1)} %copy.119) | copy-start | bytes 43012
  18.0 8.9 %collective-permute-start.4 = (bf16[32,1792]{1,0:T(8,128)(2,1)S(1)}, bf16[32,1792]{1,0:T(8,128)(2,1)S(1)}, u32[]{:S(2)}, u32[]{:S(2)}) collective-permute-start(bf16[32,1792]{1,0:T(8,128)(2,1)S(1)} %bitcast.313), channel_id=1, source_target_pairs={{0,10},{2,12},{4,14},{6,0},{8,2},{10,4},{12,6},{14,8},{1,11},{3,13... | collective-permute-start | bytes 344072 | tf_op jit(solution)/shard_map/ppermute | solution.py:18
  20.5 11.9 %copy-start.42 = (pred[128]{0:T(512)(128)(4,1)}, pred[128]{0:T(512)(128)(4,1)S(1)}, u32[]{:S(2)}) copy-start(pred[128]{0:T(512)(128)(4,1)S(1)} %get-tuple-element.44) | copy-start | bytes 388
  20.6 11.9 %copy-start.44 = (f32[128]{0:T(128)}, f32[128]{0:T(128)S(1)}, u32[]{:S(2)}) copy-start(f32[128]{0:T(128)S(1)} %get-tuple-element.45) | copy-start | bytes 1540
  22.1 10.4 %copy-start.29 = (f32[128,28]{0,1:T(8,128)}, f32[128,28]{0,1:T(8,128)S(1)}, u32[]{:S(2)}) copy-start(f32[128,28]{0,1:T(8,128)S(1)} %get-tuple-element.80) | copy-start | bytes 43012
  22.1 11.8 %copy-start.22 = (f32[128,28]{0,1:T(8,128)}, f32[128,28]{0,1:T(8,128)S(1)}, u32[]{:S(2)}) copy-start(f32[128,28]{0,1:T(8,128)S(1)} %get-tuple-element.79) | copy-start | bytes 43012
  22.2 10.2 %copy-start.50 = (f32[28]{0:T(128)}, f32[28]{0:T(128)S(1)}, u32[]{:S(2)}) copy-start(f32[28]{0:T(128)S(1)} %slice_bitcast_fusion.11) | copy-start | bytes 340
  22.3 6.2 %collective-permute-start.5 = (bf16[32,1792]{1,0:T(8,128)(2,1)S(1)}, bf16[32,1792]{1,0:T(8,128)(2,1)S(1)}, u32[]{:S(2)}, u32[]{:S(2)}) collective-permute-start(bf16[32,1792]{1,0:T(8,128)(2,1)S(1)} %bitcast.314), channel_id=1, source_target_pairs={{0,12},{2,14},{4,0},{6,2},{8,4},{10,6},{12,8},{14,10},{1,13},{3,15... | collective-permute-start | bytes 344072 | tf_op jit(solution)/shard_map/ppermute | solution.py:18
  26.2 5.7 %collective-permute-start.6 = (bf16[32,1792]{1,0:T(8,128)(2,1)S(1)}, bf16[32,1792]{1,0:T(8,128)(2,1)S(1)}, u32[]{:S(2)}, u32[]{:S(2)}) collective-permute-start(bf16[32,1792]{1,0:T(8,128)(2,1)S(1)} %bitcast.315), channel_id=1, source_target_pairs={{0,14},{2,0},{4,2},{6,4},{8,6},{10,8},{12,10},{14,12},{1,15},{3,1}... | collective-permute-start | bytes 344072 | tf_op jit(solution)/shard_map/ppermute | solution.py:18
  32.5 1.3 collective-permute-start.7
  38.0 15.8 %copy-start.19 = (bf16[28,126]{1,0:T(8,128)(2,1)}, bf16[28,126]{1,0:T(8,128)(2,1)S(1)}, u32[]{:S(2)}) copy-start(bf16[28,126]{1,0:T(8,128)(2,1)S(1)} %broadcast.167) | copy-start | bytes 21172
  38.5 14.2 %collective-permute-start.9 = (bf16[28,8320]{1,0:T(8,128)(2,1)S(1)}, bf16[28,8320]{1,0:T(8,128)(2,1)S(1)}, u32[]{:S(2)}, u32[]{:S(2)}) collective-permute-start(bf16[28,8320]{1,0:T(8,128)(2,1)S(1)} %concatenate.71), channel_id=1, source_target_pairs={{0,2},{2,0},{4,6},{6,4},{8,10},{10,8},{12,14},{14,12},{1,3},{3,1},... | collective-permute-start | bytes 1397768 | tf_op jit(solution)/shard_map/ppermute | solution.py:145
  38.7 15.2 %copy-start.61 = (f32[28]{0:T(128)}, f32[28]{0:T(128)S(1)}, u32[]{:S(2)}) copy-start(f32[28]{0:T(128)S(1)} %exponential_multiply_fusion.1) | copy-start | bytes 340
  54.1 13.5 %collective-permute-start.10 = (bf16[28,8320]{1,0:T(8,128)(2,1)S(1)}, bf16[28,8320]{1,0:T(8,128)(2,1)}, u32[]{:S(2)}, u32[]{:S(2)}) collective-permute-start(bf16[28,8320]{1,0:T(8,128)(2,1)S(1)} %concatenate.72), channel_id=1, source_target_pairs={{0,4},{2,6},{4,0},{6,2},{8,12},{10,14},{12,8},{14,10},{1,5},{3,7},... | collective-permute-start | bytes 1397768 | tf_op jit(solution)/shard_map/ppermute | solution.py:145
  71.8 14.4 %copy-start.52 = (f32[28]{0:T(128)S(1)}, f32[28]{0:T(128)}, u32[]{:S(2)}) copy-start(f32[28]{0:T(128)} %get-tuple-element.19) | copy-start | bytes 340
  71.8 14.4 %copy-start.53 = (f32[28]{0:T(128)S(1)}, f32[28]{0:T(128)}, u32[]{:S(2)}) copy-start(f32[28]{0:T(128)} %get-tuple-element.20) | copy-start | bytes 340
  71.8 14.4 %copy-start.54 = (f32[28]{0:T(128)S(1)}, f32[28]{0:T(128)}, u32[]{:S(2)}) copy-start(f32[28]{0:T(128)} %get-tuple-element.21) | copy-start | bytes 340
  71.9 14.4 %copy-start.55 = (f32[28]{0:T(128)S(1)}, f32[28]{0:T(128)}, u32[]{:S(2)}) copy-start(f32[28]{0:T(128)} %get-tuple-element.23) | copy-start | bytes 340
  72.7 13.6 %collective-permute-start.11 = (bf16[28,4224]{1,0:T(8,128)(2,1)S(1)}, bf16[28,4224]{1,0:T(8,128)(2,1)S(1)}, u32[]{:S(2)}, u32[]{:S(2)}) collective-permute-start(bf16[28,4224]{1,0:T(8,128)(2,1)S(1)} %concatenate.73), channel_id=1, source_target_pairs={{0,8},{2,10},{4,12},{6,14},{8,0},{10,2},{12,4},{14,6},{1,9},{3,11}... | collective-permute-start | bytes 709640 | tf_op jit(solution)/shard_map/ppermute | solution.py:152
  79.2 11.8 %copy-start.25 = (f32[128,128]{1,0:T(8,128)}, f32[128,128]{1,0:T(8,128)S(1)}, u32[]{:S(2)}) copy-start(f32[128,128]{1,0:T(8,128)S(1)} %fusion.92) | copy-start | bytes 196612
  100.7 4.2 %copy-start.23 = (f32[28,64]{1,0:T(8,128)S(1)}, f32[28,64]{1,0:T(8,128)}, u32[]{:S(2)}) copy-start(f32[28,64]{1,0:T(8,128)} %reshape_squeeze.10) | copy-start | bytes 21508
  100.7 4.2 %copy-start.26 = (f32[128,128]{1,0:T(8,128)S(1)}, f32[128,128]{1,0:T(8,128)}, u32[]{:S(2)}) copy-start(f32[128,128]{1,0:T(8,128)} %copy-done.25) | copy-start | bytes 196612
  100.8 4.2 %copy-start.28 = (f32[128,128]{1,0:T(8,128)S(1)}, f32[128,128]{1,0:T(8,128)}, u32[]{:S(2)}) copy-start(f32[128,128]{1,0:T(8,128)} %get-tuple-element.78) | copy-start | bytes 196612
  100.8 4.2 %copy-start.31 = (f32[128,28]{0,1:T(8,128)S(1)}, f32[128,28]{0,1:T(8,128)}, u32[]{:S(2)}) copy-start(f32[128,28]{0,1:T(8,128)} %copy-done.29) | copy-start | bytes 43012
  100.8 4.2 %copy-start.35 = (f32[28,128]{1,0:T(8,128)S(1)}, f32[28,128]{1,0:T(8,128)}, u32[]{:S(2)}) copy-start(f32[28,128]{1,0:T(8,128)} %copy-done.34) | copy-start | bytes 43012
  100.8 4.2 %copy-start.38 = (pred[128,128]{1,0:T(8,128)(4,1)S(1)}, pred[128,128]{1,0:T(8,128)(4,1)}, u32[]{:S(2)}) copy-start(pred[128,128]{1,0:T(8,128)(4,1)} %get-tuple-element.77) | copy-start | bytes 49156
  100.8 4.2 %copy-start.64 = (f32[28]{0:T(128)S(1)}, f32[28]{0:T(128)}, u32[]{:S(2)}) copy-start(f32[28]{0:T(128)} %add_bitcast_fusion) | copy-start | bytes 340
  101.8 4.9 %collective-permute-start.12 = (bf16[128,128]{0,1:T(8,128)(2,1)S(1)}, bf16[128,128]{0,1:T(8,128)(2,1)S(1)}, u32[]{:S(2)}, u32[]{:S(2)}) collective-permute-start(bf16[128,128]{0,1:T(8,128)(2,1)S(1)} %add_convert_fusion), channel_id=1, source_target_pairs={{0,1},{1,0},{2,3},{3,2},{4,5},{5,4},{6,7},{7,6},{8,9},{9,8},{10,11... | collective-permute-start | bytes 98312 | tf_op jit(solution)/shard_map/ppermute | solution.py:29
  108.2 35.3 %collective-permute-start.13 = (bf16[1,128,1792]{2,1,0:T(8,128)(2,1)}, bf16[1,128,1792]{2,1,0:T(8,128)(2,1)S(1)}, u32[]{:S(2)}, u32[]{:S(2)}) collective-permute-start(bf16[1,128,1792]{2,1,0:T(8,128)(2,1)} %fusion.1), channel_id=1, source_target_pairs={{16,0},{17,1},{18,2},{19,3},{20,4},{21,5},{22,6},{23,7},{24,8},{25... | collective-permute-start | bytes 1376264 | tf_op jit(solution)/shard_map/ppermute | solution.py:12
  110.2 7.5 %collective-permute-start.20 = (bf16[36,1792]{1,0:T(8,128)(2,1)S(1)}, bf16[36,1792]{1,0:T(8,128)(2,1)S(1)}, u32[]{:S(2)}, u32[]{:S(2)}) collective-permute-start(bf16[36,1792]{1,0:T(8,128)(2,1)S(1)} %pad_maximum_fusion), channel_id=1, source_target_pairs={{0,14},{2,0},{4,2},{6,4},{8,6},{10,8},{12,10},{14,12},{1,15},{3,1}... | collective-permute-start | bytes 387080 | tf_op jit(solution)/shard_map/ppermute | solution.py:18
  111.3 6.6 %collective-permute-start.19 = (bf16[36,1792]{1,0:T(8,128)(2,1)S(1)}, bf16[36,1792]{1,0:T(8,128)(2,1)S(1)}, u32[]{:S(2)}, u32[]{:S(2)}) collective-permute-start(bf16[36,1792]{1,0:T(8,128)(2,1)S(1)} %get-tuple-element.73), channel_id=1, source_target_pairs={{0,12},{2,14},{4,0},{6,2},{8,4},{10,6},{12,8},{14,10},{1,13},{3,15... | collective-permute-start | bytes 387080 | tf_op jit(solution)/shard_map/ppermute | solution.py:18
  113.1 21.6 %collective-permute-start.18 = (bf16[36,1792]{1,0:T(8,128)(2,1)S(1)}, bf16[36,1792]{1,0:T(8,128)(2,1)S(1)}, u32[]{:S(2)}, u32[]{:S(2)}) collective-permute-start(bf16[36,1792]{1,0:T(8,128)(2,1)S(1)} %get-tuple-element.72), channel_id=1, source_target_pairs={{0,10},{2,12},{4,14},{6,0},{8,2},{10,4},{12,6},{14,8},{1,11},{3,13... | collective-permute-start | bytes 387080 | tf_op jit(solution)/shard_map/ppermute | solution.py:18
  113.2 21.5 %collective-permute-start.17 = (bf16[36,1792]{1,0:T(8,128)(2,1)S(1)}, bf16[36,1792]{1,0:T(8,128)(2,1)S(1)}, u32[]{:S(2)}, u32[]{:S(2)}) collective-permute-start(bf16[36,1792]{1,0:T(8,128)(2,1)S(1)} %get-tuple-element.71), channel_id=1, source_target_pairs={{0,8},{2,10},{4,12},{6,14},{8,0},{10,2},{12,4},{14,6},{1,9},{3,11}... | collective-permute-start | bytes 387080 | tf_op jit(solution)/shard_map/ppermute | solution.py:18
  117.7 17.0 %collective-permute-start.16 = (bf16[36,1792]{1,0:T(8,128)(2,1)S(1)}, bf16[36,1792]{1,0:T(8,128)(2,1)S(1)}, u32[]{:S(2)}, u32[]{:S(2)}) collective-permute-start(bf16[36,1792]{1,0:T(8,128)(2,1)S(1)} %get-tuple-element.70), channel_id=1, source_target_pairs={{0,6},{2,8},{4,10},{6,12},{8,14},{10,0},{12,2},{14,4},{1,7},{3,9},... | collective-permute-start | bytes 387080 | tf_op jit(solution)/shard_map/ppermute | solution.py:18
  117.9 16.9 %collective-permute-start.15 = (bf16[36,1792]{1,0:T(8,128)(2,1)S(1)}, bf16[36,1792]{1,0:T(8,128)(2,1)S(1)}, u32[]{:S(2)}, u32[]{:S(2)}) collective-permute-start(bf16[36,1792]{1,0:T(8,128)(2,1)S(1)} %get-tuple-element.69), channel_id=1, source_target_pairs={{0,4},{2,6},{4,8},{6,10},{8,12},{10,14},{12,0},{14,2},{1,5},{3,7},... | collective-permute-start | bytes 387080 | tf_op jit(solution)/shard_map/ppermute | solution.py:18
  134.7 5.1 %collective-permute-start.14 = (bf16[36,1792]{1,0:T(8,128)(2,1)S(1)}, bf16[36,1792]{1,0:T(8,128)(2,1)S(1)}, u32[]{:S(2)}, u32[]{:S(2)}) collective-permute-start(bf16[36,1792]{1,0:T(8,128)(2,1)S(1)} %get-tuple-element.68), channel_id=1, source_target_pairs={{0,2},{2,4},{4,6},{6,8},{8,10},{10,12},{12,14},{14,0},{1,3},{3,5},... | collective-permute-start | bytes 387080 | tf_op jit(solution)/shard_map/ppermute | solution.py:18
  (38 other events, 91.9 us)

commit v11 on v5

--- a/solution.py
+++ b/solution.py
@@ -292,23 +292,25 @@
             out_grads[5],
         ]
     )
-    small_rows = -(-small.shape[0] // channels_here)
-    small = jnp.pad(small, (0, small_rows * channels_here - small.shape[0]))
-    small = small.reshape(small_rows, channels_here)
+    count = small.shape[0]
+    block_rows = row_parts.shape[1]
     small_high = small.astype(jnp.bfloat16)
     small_low = (small - small_high.astype(jnp.float32)).astype(jnp.bfloat16)
-    small_coded = jnp.concatenate([small_high, small_low], axis=0)
-    block_rows = row_parts.shape[1]
+    small_cols = -(-(2 * count) // (block_rows * 128)) * 128
+    small_coded = jnp.concatenate([small_high, small_low])
+    small_coded = jnp.pad(small_coded, (0, block_rows * small_cols - 2 * count))
+    small_coded = small_coded.reshape(block_rows, small_cols)
     grad_rows = row_parts[0]
     small_slots = [small_coded]
     for k in range(1, size):
-        message = jnp.concatenate([row_parts[k].astype(jnp.bfloat16), small_coded], axis=0)
+        message = jnp.concatenate([row_parts[k].astype(jnp.bfloat16), small_coded], axis=1)
         got = rotated(message, "seq", k)
-        grad_rows = grad_rows + got[:block_rows].astype(jnp.float32)
-        small_slots.append(got[block_rows:])
+        grad_rows = grad_rows + got[:, :channels_here].astype(jnp.float32)
+        small_slots.append(got[:, channels_here:])
     small_slots = jnp.stack(small_slots[::-1])
     small_slots = roll_blocks(small_slots, mine + 1, size, 0).astype(jnp.float32)
-    small_parts = small_slots[:, :small_rows] + small_slots[:, small_rows:]
+    small_slots = small_slots.reshape(size, -1)
+    small_parts = small_slots[:, :count] + small_slots[:, count : 2 * count]
     small_total = small_parts[0]
     for j in range(1, size):
         small_total = small_total + small_parts[j]

time: 145 us -> 141 us (0.972)
  starting transfers between devices: 36.1 us -> 26.4 us
  waiting for transfers between devices: 57.4 us -> 64.2 us
    ppermute x14, starting transfers between devices: 29.5 us -> 19.8 us  [rotated(): return lax.ppermute(block, axis, route)]
    ppermute x14, waiting for transfers between devices: 11.7 us -> 17.9 us  [rotated(): return lax.ppermute(block, axis, route)]
    unnamed x144 -> x141, local copies, waits for them, and re-layouts: 4.32 us -> 4.31 us
  transfers between devices with their start and end apart: 21 -> 21, of which waited for: 11 -> 10; matrix products, arithmetic and copies ran while one was open for 15% -> 15% of each run, Pallas kernels for 0% -> 0%
where the time goes in v11:
time: 141 us; the launch traced here: 140 us
  waiting for transfers between devices  64.2 us (46%)
  starting transfers between devices  26.4 us (19%)
  local copies, waits for them, and re-layouts  16.6 us (12%)
  matrix products  16.6 us (12%)
  other arithmetic  13.4 us (10%)
  between operations  3.28 us (2%)
    ppermute x2, waiting for transfers between devices, both_scans(): got = lax.ppermute(payload, axis, [(i, i ^ distance) for i in range(size)])  26.3 us
    ppermute x14, starting transfers between devices, rotated(): return lax.ppermute(block, axis, route)  19.8 us
    ppermute x14, waiting for transfers between devices, rotated(): return lax.ppermute(block, axis, route)  17.9 us
    ppermute x1, waiting for transfers between devices, both_scans(): got = lax.ppermute(last, axis, [(i, i ^ distance) for i in range(size)])  12.3 us
    ppermute x2, waiting for transfers between devices, shifted(): return lax.ppermute(block, axis, route)  7.67 us
    dot_general x5, matrix products, contract(): return jnp.einsum(spec, left, right, preferred_element_type=jnp.float32)  6.83 us
    ppermute x2, starting transfers between devices, shifted(): return lax.ppermute(block, axis, route)  5.6 us
    unnamed x141, local copies, waits for them, and re-layouts  4.31 us
  transfers between devices with their start and end apart: 21, of which 10 were waited for; matrix products, arithmetic and copies ran while one was open for 15% of the time, Pallas kernels for 0%

profile of v11, /device:TPU:4, one launch (start us, length us, event | category | flops | bytes accessed | tf_op | source)
XLA Modules:
  0.0 140.4 jit_solution(6243420667855408329)
XLA Ops:
  0.7 1.6 %collective-permute-start = (bf16[32,1792]{1,0:T(8,128)(2,1)}, bf16[32,1792]{1,0:T(8,128)(2,1)S(1)}, u32[]{:S(2)}, u32[]{:S(2)}) collective-permute-start(bf16[32,1792]{1,0:T(8,128)(2,1)} %bitcast.346), channel_id=1, source_target_pairs={{0,2},{2,4},{4,6},{6,8},{8,10},{10,12},{12,14},{14,0},{1,3},{3,5},... | collective-permute-start | bytes 344072 | tf_op jit(solution)/shard_map/ppermute | solution.py:18
  2.2 1.6 %collective-permute-start.1 = (bf16[32,1792]{1,0:T(8,128)(2,1)}, bf16[32,1792]{1,0:T(8,128)(2,1)S(1)}, u32[]{:S(2)}, u32[]{:S(2)}) collective-permute-start(bf16[32,1792]{1,0:T(8,128)(2,1)} %bitcast.347), channel_id=1, source_target_pairs={{0,4},{2,6},{4,8},{6,10},{8,12},{10,14},{12,0},{14,2},{1,5},{3,7},... | collective-permute-start | bytes 344072 | tf_op jit(solution)/shard_map/ppermute | solution.py:18
  3.8 2.5 %collective-permute-start.2 = (bf16[32,1792]{1,0:T(8,128)(2,1)}, bf16[32,1792]{1,0:T(8,128)(2,1)S(1)}, u32[]{:S(2)}, u32[]{:S(2)}) collective-permute-start(bf16[32,1792]{1,0:T(8,128)(2,1)} %bitcast.348), channel_id=1, source_target_pairs={{0,6},{2,8},{4,10},{6,12},{8,14},{10,0},{12,2},{14,4},{1,7},{3,9},... | collective-permute-start | bytes 344072 | tf_op jit(solution)/shard_map/ppermute | solution.py:18
  6.7 1.2 slice.179
  7.9 4.3 %collective-permute-start.8 = (s32[1]{0:T(128)}, s32[1]{0:T(128)}, u32[]{:S(2)}, u32[]{:S(2)}) collective-permute-start(s32[1]{0:T(128)} %bitcast.13), channel_id=1, source_target_pairs={{0,2},{2,4},{4,6},{6,8},{8,10},{10,12},{12,14},{1,3},{3,5},{5,7},{... | collective-permute-start | bytes 20 | tf_op jit(solution)/shard_map/ppermute | solution.py:12
  12.2 0.9 constant_dynamic-update-slice_fusion.7
  13.2 0.7 reduce
  14.0 0.7 reshape_squeeze.7
  14.6 1.3 copy.66
  16.8 1.1 convert.62
  17.9 0.7 broadcast_compare_fusion
  18.6 1.3 collective-permute-start.4
  19.9 1.3 broadcast_compare_fusion.1
  23.6 3.1 %collective-permute-start.5 = (bf16[32,1792]{1,0:T(8,128)(2,1)S(1)}, bf16[32,1792]{1,0:T(8,128)(2,1)S(1)}, u32[]{:S(2)}, u32[]{:S(2)}) collective-permute-start(bf16[32,1792]{1,0:T(8,128)(2,1)S(1)} %bitcast.351), channel_id=1, source_target_pairs={{0,12},{2,14},{4,0},{6,2},{8,4},{10,6},{12,8},{14,10},{1,13},{3,15... | collective-permute-start | bytes 344072 | tf_op jit(solution)/shard_map/ppermute | solution.py:18
  27.5 1.6 %collective-permute-done.5 = bf16[32,1792]{1,0:T(8,128)(2,1)S(1)} collective-permute-done((bf16[32,1792]{1,0:T(8,128)(2,1)S(1)}, bf16[32,1792]{1,0:T(8,128)(2,1)S(1)}, u32[]{:S(2)}, u32[]{:S(2)}) %collective-permute-start.5) | collective-permute-done | bytes 114720 | tf_op jit(solution)/shard_map/ppermute | solution.py:18
  29.1 3.4 %collective-permute-done.6 = bf16[32,1792]{1,0:T(8,128)(2,1)S(1)} collective-permute-done((bf16[32,1792]{1,0:T(8,128)(2,1)S(1)}, bf16[32,1792]{1,0:T(8,128)(2,1)S(1)}, u32[]{:S(2)}, u32[]{:S(2)}) %collective-permute-start.6) | collective-permute-done | bytes 114720 | tf_op jit(solution)/shard_map/ppermute | solution.py:18
  33.6 0.7 copy.74
  34.4 0.7 copy.72
  35.1 0.7 copy.73
  37.3 1.2 copy.71
  38.5 1.6 %reshape.286 = f32[28,4096]{1,0:T(8,128)S(1)} reshape(f32[28,64,64]{2,1,0:T(8,128)} %copy.71) | data formatting | bytes 917504 | tf_op jit(solution)/shard_map/reshape | solution.py:243
  40.2 1.1 concatenate.64
  42.8 2.8 %fusion.12 = (f32[28,128]{1,0:T(8,128)S(1)}, f32[28,128]{1,0:T(8,128)S(1)}, f32[28,128]{1,0:T(8,128)S(1)}, bf16[128,128]{1,0:T(8,128)(2,1)S(1)}) fusion(f32[28,128]{1,0:T(8,128)S(1)} %fusion.118, f32[128,128]{1,0:T(8,128)S(1)} %fusion.102, f32[128,128]{1,0:T(8,128)} %get-tuple-element.107, f32[28,128]{1,0:T(8,128)S(1)} %fusion.74, ...), kind=kOutput, calls=%fused_computation.18 | convolution fusion | flops 66033152 | bytes 1628160 | tf_op jit(solution)/shard_map/transpose(jvp(hts,shp->thp))/dot_general | solution.py:33
  46.2 0.8 fusion.106
  47.2 1.8 %fusion.17 = bf16[128,28,64]{0,2,1:T(8,128)(2,1)} fusion(f32[128,28,64]{0,2,1:T(8,128)S(1)} %copy-done.8, f32[28,128]{1,0:T(8,128)S(1)} %fusion.118, f32[128,128]{1,0:T(8,128)S(1)} %fusion.102, f32[128,128]{1,0:T(8,128)S(1)} %copy-done.31, f32[28,128]{1,0:T(8,128)S(1)} %fusion.74, pred[128,128]{1,0:T(8,128)(4,1)S(1)} %copy-done.38, ...), kind=kOutput, calls=%fused_computation.27 | convolution fusion | flops 63078400 | bytes 1574000 | tf_op jit(solution)/shard_map/transpose(jvp(hts,shp->thp))/dot_general | solution.py:33
  48.9 12.6 %collective-permute-done.9 = bf16[28,8320]{1,0:T(8,128)(2,1)S(1)} collective-permute-done((bf16[28,8320]{1,0:T(8,128)(2,1)S(1)}, bf16[28,8320]{1,0:T(8,128)(2,1)S(1)}, u32[]{:S(2)}, u32[]{:S(2)}) %collective-permute-start.9) | collective-permute-done | bytes 465952 | tf_op jit(solution)/shard_map/ppermute | solution.py:148
  62.6 13.7 %collective-permute-done.10 = bf16[28,8320]{1,0:T(8,128)(2,1)} collective-permute-done((bf16[28,8320]{1,0:T(8,128)(2,1)S(1)}, bf16[28,8320]{1,0:T(8,128)(2,1)}, u32[]{:S(2)}, u32[]{:S(2)}) %collective-permute-start.10) | collective-permute-done | bytes 465952 | tf_op jit(solution)/shard_map/ppermute | solution.py:148
  76.3 1.1 convert_element_type.287
  78.3 0.7 collective-permute-start.11
  79.0 1.0 bitcast_multiply_fusion
  80.0 12.3 %collective-permute-done.11 = bf16[28,4224]{1,0:T(8,128)(2,1)} collective-permute-done((bf16[28,4224]{1,0:T(8,128)(2,1)S(1)}, bf16[28,4224]{1,0:T(8,128)(2,1)}, u32[]{:S(2)}, u32[]{:S(2)}) %collective-permute-start.11) | collective-permute-done | bytes 236576 | tf_op jit(solution)/shard_map/ppermute | solution.py:155
  92.3 1.4 %multiply_reduce_fusion.4 = (f32[28]{0:T(128)S(1)}, f32[28,4096]{1,0:T(8,128)S(1)}, bf16[28,4096]{1,0:T(8,128)(2,1)S(1)}) fusion(bf16[28,4224]{1,0:T(8,128)(2,1)} %collective-permute-done.11, f32[28]{0:T(128)S(1)} %get-tuple-element.52, f32[28,8320]{1,0:T(8,128)S(1)} %convert_element_type.287, f32[28]{0:T(128)S(1)} %get-tuple-element.54, ...), kind=kLoop, calls=%fused_computation.64 | loop fusion | flops 2064356 | bytes 2753075 | tf_op jit(solution)/shard_map/reduce_sum | solution.py:264
  97.1 0.8 fusion.136
  98.0 0.8 fusion.137
  99.1 1.0 fusion.22
  100.4 1.6 %fusion.21 = f32[128,28,64]{0,2,1:T(8,128)S(1)} fusion(bf16[28,64,64]{2,1,0:T(8,128)(2,1)S(1)} %copy-done.20, bf16[128,28,64]{0,2,1:T(8,128)(2,1)} %fusion.17, f32[28,128]{1,0:T(8,128)S(1)} %copy.82, f32[28,64]{1,0:T(8,128)S(1)} %copy-done.37, f32[28,128]{1,0:T(8,128)S(1)} %copy.77, f32[128,64]{0,1:T(8,128)S(1)} %copy-done.24, f32[128,28]{0,1:T(8,128)S(1)} %copy-done.29), kind=kOutput, calls=%fused_computation.31 | convolution fusion | flops 32112640 | bytes 1688576 | tf_op jit(solution)/shard_map/transpose(jvp(thn,thp->hnp))/dot_general | solution.py:33
  102.3 1.8 %fusion.131 = (bf16[256,1792]{1,0:T(8,128)(2,1)S(1)}, f32[256,1792]{1,0:T(8,128)}) fusion(bf16[1,128,1792]{2,1,0:T(8,128)(2,1)S(1)} %copy-done.7, s32[]{:T(128)S(6)} %select_n.220, bf16[128,256]{0,1:T(8,128)(2,1)S(1)} %maximum_select_fusion), kind=kOutput, calls=%fused_computation.276 | convolution fusion | flops 118030336 | bytes 3276804 | tf_op jit(solution)/shard_map/dot_general | solution.py:284
  104.2 0.7 pad_maximum_fusion.6
  105.0 0.7 collective-permute-start.20
  105.7 1.8 %collective-permute-start.19 = (bf16[32,1920]{1,0:T(8,128)(2,1)S(1)}, bf16[32,1920]{1,0:T(8,128)(2,1)S(1)}, u32[]{:S(2)}, u32[]{:S(2)}) collective-permute-start(bf16[32,1920]{1,0:T(8,128)(2,1)S(1)} %get-tuple-element.99), channel_id=1, source_target_pairs={{0,12},{2,14},{4,0},{6,2},{8,4},{10,6},{12,8},{14,10},{1,13},{3,15... | collective-permute-start | bytes 368648 | tf_op jit(solution)/shard_map/ppermute | solution.py:18
  107.7 3.5 %collective-permute-start.17 = (bf16[32,1920]{1,0:T(8,128)(2,1)S(1)}, bf16[32,1920]{1,0:T(8,128)(2,1)S(1)}, u32[]{:S(2)}, u32[]{:S(2)}) collective-permute-start(bf16[32,1920]{1,0:T(8,128)(2,1)S(1)} %get-tuple-element.97), channel_id=1, source_target_pairs={{0,8},{2,10},{4,12},{6,14},{8,0},{10,2},{12,4},{14,6},{1,9},{3,11}... | collective-permute-start | bytes 368648 | tf_op jit(solution)/shard_map/ppermute | solution.py:18
  112.3 1.0 collective-permute-start.15
  113.3 1.8 %collective-permute-start.14 = (bf16[32,1920]{1,0:T(8,128)(2,1)S(1)}, bf16[32,1920]{1,0:T(8,128)(2,1)S(1)}, u32[]{:S(2)}, u32[]{:S(2)}) collective-permute-start(bf16[32,1920]{1,0:T(8,128)(2,1)S(1)} %get-tuple-element.94), channel_id=1, source_target_pairs={{0,2},{2,4},{4,6},{6,8},{8,10},{10,12},{12,14},{14,0},{1,3},{3,5},... | collective-permute-start | bytes 368648 | tf_op jit(solution)/shard_map/ppermute | solution.py:18
  115.1 11.6 %collective-permute-done.18 = bf16[32,1920]{1,0:T(8,128)(2,1)S(1)} collective-permute-done((bf16[32,1920]{1,0:T(8,128)(2,1)S(1)}, bf16[32,1920]{1,0:T(8,128)(2,1)S(1)}, u32[]{:S(2)}, u32[]{:S(2)}) %collective-permute-start.18) | collective-permute-done | bytes 122912 | tf_op jit(solution)/shard_map/ppermute | solution.py:18
  126.7 1.3 collective-permute-start.13
  130.3 1.7 %fusion.51 = f32[1,32,1792]{2,1,0:T(8,128)} fusion(f32[256,1792]{1,0:T(8,128)} %get-tuple-element.112, bf16[32,1920]{1,0:T(8,128)(2,1)S(1)} %collective-permute-done.20, bf16[32,1920]{1,0:T(8,128)(2,1)S(1)} %collective-permute-done.19, bf16[32,1920]{1,0:T(8,128)(2,1)S(1)} %collective-permute-done.18, bf16[32,1920]{1,0:T(8,128)(2,1)S(1)} %collective-permute-done.17, ...), kind=kLoop, calls=%fused_computation.97 | loop fusion | flops 802816 | bytes 1261568 | tf_op jit(solution)/shard_map/broadcast_in_dim | solution.py:326
  132.0 7.7 %collective-permute-done.13 = bf16[1,128,1792]{2,1,0:T(8,128)(2,1)S(1)} collective-permute-done((bf16[1,128,1792]{2,1,0:T(8,128)(2,1)S(1)}, bf16[1,128,1792]{2,1,0:T(8,128)(2,1)S(1)}, u32[]{:S(2)}, u32[]{:S(2)}) %collective-permute-start.13) | collective-permute-done | bytes 458784 | tf_op jit(solution)/shard_map/ppermute | solution.py:12
  139.7 0.8 copy.148
  (242 shorter events, 16.8 us)
Async XLA Ops:
  0.6 15.9 %copy-start.49 = (f32[1,28]{1,0:T(1,128)S(1)}, f32[1,28]{1,0:T(1,128)}, u32[]{:S(2)}) copy-start(f32[1,28]{1,0:T(1,128)} %param.15) | copy-start | bytes 340
  0.6 15.9 %copy-start.18 = (bf16[1,128,1792]{2,1,0:T(8,128)(2,1)S(1)}, bf16[1,128,1792]{2,1,0:T(8,128)(2,1)}, u32[]{:S(2)}) copy-start(bf16[1,128,1792]{2,1,0:T(8,128)(2,1)} %param.11) | copy-start | bytes 1376260
  0.7 23.0 %collective-permute-start = (bf16[32,1792]{1,0:T(8,128)(2,1)}, bf16[32,1792]{1,0:T(8,128)(2,1)S(1)}, u32[]{:S(2)}, u32[]{:S(2)}) collective-permute-start(bf16[32,1792]{1,0:T(8,128)(2,1)} %bitcast.346), channel_id=1, source_target_pairs={{0,2},{2,4},{4,6},{6,8},{8,10},{10,12},{12,14},{14,0},{1,3},{3,5},... | collective-permute-start | bytes 344072 | tf_op jit(solution)/shard_map/ppermute | solution.py:18
  2.2 24.5 %collective-permute-start.1 = (bf16[32,1792]{1,0:T(8,128)(2,1)}, bf16[32,1792]{1,0:T(8,128)(2,1)S(1)}, u32[]{:S(2)}, u32[]{:S(2)}) collective-permute-start(bf16[32,1792]{1,0:T(8,128)(2,1)} %bitcast.347), channel_id=1, source_target_pairs={{0,4},{2,6},{4,8},{6,10},{8,12},{10,14},{12,0},{14,2},{1,5},{3,7},... | collective-permute-start | bytes 344072 | tf_op jit(solution)/shard_map/ppermute | solution.py:18
  3.8 23.2 %collective-permute-start.2 = (bf16[32,1792]{1,0:T(8,128)(2,1)}, bf16[32,1792]{1,0:T(8,128)(2,1)S(1)}, u32[]{:S(2)}, u32[]{:S(2)}) collective-permute-start(bf16[32,1792]{1,0:T(8,128)(2,1)} %bitcast.348), channel_id=1, source_target_pairs={{0,6},{2,8},{4,10},{6,12},{8,14},{10,0},{12,2},{14,4},{1,7},{3,9},... | collective-permute-start | bytes 344072 | tf_op jit(solution)/shard_map/ppermute | solution.py:18
  6.3 20.7 %collective-permute-start.3 = (bf16[32,1792]{1,0:T(8,128)(2,1)}, bf16[32,1792]{1,0:T(8,128)(2,1)S(1)}, u32[]{:S(2)}, u32[]{:S(2)}) collective-permute-start(bf16[32,1792]{1,0:T(8,128)(2,1)} %bitcast.349), channel_id=1, source_target_pairs={{0,8},{2,10},{4,12},{6,14},{8,0},{10,2},{12,4},{14,6},{1,9},{3,11}... | collective-permute-start | bytes 344072 | tf_op jit(solution)/shard_map/ppermute | solution.py:18
  7.9 10.7 %collective-permute-start.8 = (s32[1]{0:T(128)}, s32[1]{0:T(128)}, u32[]{:S(2)}, u32[]{:S(2)}) collective-permute-start(s32[1]{0:T(128)} %bitcast.13), channel_id=1, source_target_pairs={{0,2},{2,4},{4,6},{6,8},{8,10},{10,12},{12,14},{1,3},{3,5},{5,7},{... | collective-permute-start | bytes 20 | tf_op jit(solution)/shard_map/ppermute | solution.py:12
  14.6 3.3 %copy-start.46 = (s32[1,128]{1,0:T(1,128)S(1)}, s32[1,128]{1,0:T(1,128)}, u32[]{:S(2)}) copy-start(s32[1,128]{1,0:T(1,128)} %param.10) | copy-start | bytes 1540
  14.6 4.0 %copy-start.25 = (bf16[1,32,1792]{2,1,0:T(8,128)(2,1)S(1)}, bf16[1,32,1792]{2,1,0:T(8,128)(2,1)}, u32[]{:S(2)}) copy-start(bf16[1,32,1792]{2,1,0:T(8,128)(2,1)} %param.12) | copy-start | bytes 344068
  14.6 8.0 %copy-start.39 = (f32[1,28]{1,0:T(1,128)S(1)}, f32[1,28]{1,0:T(1,128)}, u32[]{:S(2)}) copy-start(f32[1,28]{1,0:T(1,128)} %param.14) | copy-start | bytes 340
  15.9 30.2 %copy-start.4 = (bf16[1,128,1792]{1,2,0:T(8,128)(2,1)}, bf16[1,128,1792]{1,2,0:T(8,128)(2,1)S(1)}, u32[]{:S(2)}) copy-start(bf16[1,128,1792]{1,2,0:T(8,128)(2,1)S(1)} %copy.66) | copy-start | bytes 1376260
  16.5 10.5 %copy-start.15 = (f32[28,1,128]{0,2,1:T(8,128)}, f32[28,1,128]{0,2,1:T(8,128)S(1)}, u32[]{:S(2)}) copy-start(f32[28,1,128]{0,2,1:T(8,128)S(1)} %copy.87) | copy-start | bytes 43012
  16.6 6.3 %copy-start.56 = (f32[28]{0:T(128)}, f32[28]{0:T(128)S(1)}, u32[]{:S(2)}) copy-start(f32[28]{0:T(128)S(1)} %negate_bitcast_fusion) | copy-start | bytes 340
  16.8 15.7 %copy-start.6 = (bf16[1,128,1792]{2,1,0:T(8,128)(2,1)S(1)}, bf16[1,128,1792]{2,1,0:T(8,128)(2,1)}, u32[]{:S(2)}) copy-start(bf16[1,128,1792]{2,1,0:T(8,128)(2,1)} %param.9) | copy-start | bytes 1376260
  18.6 8.8 %collective-permute-start.4 = (bf16[32,1792]{1,0:T(8,128)(2,1)S(1)}, bf16[32,1792]{1,0:T(8,128)(2,1)S(1)}, u32[]{:S(2)}, u32[]{:S(2)}) collective-permute-start(bf16[32,1792]{1,0:T(8,128)(2,1)S(1)} %bitcast.350), channel_id=1, source_target_pairs={{0,10},{2,12},{4,14},{6,0},{8,2},{10,4},{12,6},{14,8},{1,11},{3,13... | collective-permute-start | bytes 344072 | tf_op jit(solution)/shard_map/ppermute | solution.py:18
  21.3 11.2 %copy-start.42 = (pred[128]{0:T(512)(128)(4,1)}, pred[128]{0:T(512)(128)(4,1)S(1)}, u32[]{:S(2)}) copy-start(pred[128]{0:T(512)(128)(4,1)S(1)} %get-tuple-element.77) | copy-start | bytes 388
  21.3 11.2 %copy-start.44 = (f32[128]{0:T(128)}, f32[128]{0:T(128)S(1)}, u32[]{:S(2)}) copy-start(f32[128]{0:T(128)S(1)} %get-tuple-element.78) | copy-start | bytes 1540
  22.9 13.7 %copy-start.26 = (f32[128,28]{0,1:T(8,128)}, f32[128,28]{0,1:T(8,128)S(1)}, u32[]{:S(2)}) copy-start(f32[128,28]{0,1:T(8,128)S(1)} %get-tuple-element.109) | copy-start | bytes 43012
  23.0 10.1 %copy-start.13 = (f32[128,28]{1,0:T(8,128)}, f32[128,28]{1,0:T(8,128)S(1)}, u32[]{:S(2)}) copy-start(f32[128,28]{1,0:T(8,128)S(1)} %copy.67) | copy-start | bytes 43012
  23.1 9.4 %copy-start.47 = (f32[28]{0:T(128)}, f32[28]{0:T(128)S(1)}, u32[]{:S(2)}) copy-start(f32[28]{0:T(128)S(1)} %slice_bitcast_fusion.7) | copy-start | bytes 340
  23.6 5.4 %collective-permute-start.5 = (bf16[32,1792]{1,0:T(8,128)(2,1)S(1)}, bf16[32,1792]{1,0:T(8,128)(2,1)S(1)}, u32[]{:S(2)}, u32[]{:S(2)}) collective-permute-start(bf16[32,1792]{1,0:T(8,128)(2,1)S(1)} %bitcast.351), channel_id=1, source_target_pairs={{0,12},{2,14},{4,0},{6,2},{8,4},{10,6},{12,8},{14,10},{1,13},{3,15... | collective-permute-start | bytes 344072 | tf_op jit(solution)/shard_map/ppermute | solution.py:18
  26.7 5.7 %collective-permute-start.6 = (bf16[32,1792]{1,0:T(8,128)(2,1)S(1)}, bf16[32,1792]{1,0:T(8,128)(2,1)S(1)}, u32[]{:S(2)}, u32[]{:S(2)}) collective-permute-start(bf16[32,1792]{1,0:T(8,128)(2,1)S(1)} %bitcast.352), channel_id=1, source_target_pairs={{0,14},{2,0},{4,2},{6,4},{8,6},{10,8},{12,10},{14,12},{1,15},{3,1}... | collective-permute-start | bytes 344072 | tf_op jit(solution)/shard_map/ppermute | solution.py:18
  32.5 3.8 %copy-start.2 = (bf16[256,1792]{1,0:T(8,128)(2,1)}, bf16[256,1792]{1,0:T(8,128)(2,1)S(1)}, u32[]{:S(2)}) copy-start(bf16[256,1792]{1,0:T(8,128)(2,1)S(1)} %constant_dynamic-update-slice_fusion) | copy-start | bytes 2752516
  33.0 2.8 %collective-permute-start.7 = (bf16[128,128]{0,1:T(8,128)(2,1)S(1)}, bf16[128,128]{0,1:T(8,128)(2,1)S(1)}, u32[]{:S(2)}, u32[]{:S(2)}) collective-permute-start(bf16[128,128]{0,1:T(8,128)(2,1)S(1)} %fusion.58), channel_id=1, source_target_pairs={{0,1},{1,0},{2,3},{3,2},{4,5},{5,4},{6,7},{7,6},{8,9},{9,8},{10,11... | collective-permute-start | bytes 98312 | tf_op jit(solution)/shard_map/ppermute | solution.py:29
  40.1 21.8 %copy-start = (f32[28,4096]{1,0:T(8,128)}, f32[28,4096]{1,0:T(8,128)S(1)}, u32[]{:S(2)}) copy-start(f32[28,4096]{1,0:T(8,128)S(1)} %reshape.286) | copy-start | bytes 1376260
  40.2 5.4 %copy-start.21 = (bf16[28,126]{1,0:T(8,128)(2,1)}, bf16[28,126]{1,0:T(8,128)(2,1)S(1)}, u32[]{:S(2)}) copy-start(bf16[28,126]{1,0:T(8,128)(2,1)S(1)} %broadcast.164) | copy-start | bytes 21172
  42.7 4.3 %copy-start.17 = (bf16[28,8320]{1,0:T(8,128)(2,1)S(1)}, bf16[28,8320]{1,0:T(8,128)(2,1)}, u32[]{:S(2)}) copy-start(bf16[28,8320]{1,0:T(8,128)(2,1)} %concatenate.64) | copy-start | bytes 1397764
  42.7 4.4 %copy-start.53 = (f32[1,28]{1,0:T(1,128)S(1)}, f32[1,28]{1,0:T(1,128)}, u32[]{:S(2)}) copy-start(f32[1,28]{1,0:T(1,128)} %param.16) | copy-start | bytes 340
  42.7 4.4 %copy-start.31 = (f32[128,128]{1,0:T(8,128)S(1)}, f32[128,128]{1,0:T(8,128)}, u32[]{:S(2)}) copy-start(f32[128,128]{1,0:T(8,128)} %get-tuple-element.107) | copy-start | bytes 196612
  42.7 4.4 %copy-start.37 = (f32[28,64]{1,0:T(8,128)S(1)}, f32[28,64]{1,0:T(8,128)}, u32[]{:S(2)}) copy-start(f32[28,64]{1,0:T(8,128)} %reshape_squeeze.7) | copy-start | bytes 21508
  42.8 4.4 %copy-start.38 = (pred[128,128]{1,0:T(8,128)(4,1)S(1)}, pred[128,128]{1,0:T(8,128)(4,1)}, u32[]{:S(2)}) copy-start(pred[128,128]{1,0:T(8,128)(4,1)} %get-tuple-element.106) | copy-start | bytes 49156
  47.0 14.6 %collective-permute-start.9 = (bf16[28,8320]{1,0:T(8,128)(2,1)S(1)}, bf16[28,8320]{1,0:T(8,128)(2,1)S(1)}, u32[]{:S(2)}, u32[]{:S(2)}) collective-permute-start(bf16[28,8320]{1,0:T(8,128)(2,1)S(1)} %copy-done.17), channel_id=1, source_target_pairs={{0,2},{2,0},{4,6},{6,4},{8,10},{10,8},{12,14},{14,12},{1,3},{3,1},... | collective-permute-start | bytes 1397768 | tf_op jit(solution)/shard_map/ppermute | solution.py:148
  47.1 14.5 %copy-start.30 = (f32[28,1]{1,0:T(8,128)S(1)}, f32[28,1]{1,0:T(8,128)}, u32[]{:S(2)}) copy-start(f32[28,1]{1,0:T(8,128)} %copy.74) | copy-start | bytes 340
  47.1 14.8 %copy-start.52 = (f32[28]{0:T(128)S(1)}, f32[28]{0:T(128)}, u32[]{:S(2)}) copy-start(f32[28]{0:T(128)} %exponential_multiply_fusion.1) | copy-start | bytes 340
  48.9 13.3 %copy-start.22 = (bf16[28,126]{1,0:T(8,128)(2,1)S(1)}, bf16[28,126]{1,0:T(8,128)(2,1)}, u32[]{:S(2)}) copy-start(bf16[28,126]{1,0:T(8,128)(2,1)} %copy-done.21) | copy-start | bytes 21172
  62.5 13.9 %collective-permute-start.10 = (bf16[28,8320]{1,0:T(8,128)(2,1)S(1)}, bf16[28,8320]{1,0:T(8,128)(2,1)}, u32[]{:S(2)}, u32[]{:S(2)}) collective-permute-start(bf16[28,8320]{1,0:T(8,128)(2,1)S(1)} %concatenate.65), channel_id=1, source_target_pairs={{0,4},{2,6},{4,0},{6,2},{8,12},{10,14},{12,8},{14,10},{1,5},{3,7},... | collective-permute-start | bytes 1397768 | tf_op jit(solution)/shard_map/ppermute | solution.py:148
  62.6 15.1 %copy-start.1 = (f32[28,4096]{1,0:T(8,128)S(1)}, f32[28,4096]{1,0:T(8,128)}, u32[]{:S(2)}) copy-start(f32[28,4096]{1,0:T(8,128)} %copy-done) | copy-start | bytes 1376260
  78.3 14.1 %collective-permute-start.11 = (bf16[28,4224]{1,0:T(8,128)(2,1)S(1)}, bf16[28,4224]{1,0:T(8,128)(2,1)}, u32[]{:S(2)}, u32[]{:S(2)}) collective-permute-start(bf16[28,4224]{1,0:T(8,128)(2,1)S(1)} %concatenate.66), channel_id=1, source_target_pairs={{0,8},{2,10},{4,12},{6,14},{8,0},{10,2},{12,4},{14,6},{1,9},{3,11}... | collective-permute-start | bytes 709640 | tf_op jit(solution)/shard_map/ppermute | solution.py:155
  100.1 2.2 %collective-permute-start.12 = (bf16[128,128]{0,1:T(8,128)(2,1)S(1)}, bf16[128,128]{0,1:T(8,128)(2,1)S(1)}, u32[]{:S(2)}, u32[]{:S(2)}) collective-permute-start(bf16[128,128]{0,1:T(8,128)(2,1)S(1)} %add_convert_fusion), channel_id=1, source_target_pairs={{0,1},{1,0},{2,3},{3,2},{4,5},{5,4},{6,7},{7,6},{8,9},{9,8},{10,11... | collective-permute-start | bytes 98312 | tf_op jit(solution)/shard_map/ppermute | solution.py:29
  104.2 7.4 %copy-start.3 = (bf16[256,1792]{1,0:T(8,128)(2,1)S(1)}, bf16[256,1792]{1,0:T(8,128)(2,1)}, u32[]{:S(2)}) copy-start(bf16[256,1792]{1,0:T(8,128)(2,1)} %copy-done.2) | copy-start | bytes 2752516
  105.0 7.3 %collective-permute-start.20 = (bf16[32,1920]{1,0:T(8,128)(2,1)}, bf16[32,1920]{1,0:T(8,128)(2,1)S(1)}, u32[]{:S(2)}, u32[]{:S(2)}) collective-permute-start(bf16[32,1920]{1,0:T(8,128)(2,1)} %get-tuple-element.100), channel_id=1, source_target_pairs={{0,14},{2,0},{4,2},{6,4},{8,6},{10,8},{12,10},{14,12},{1,15},{3,1}... | collective-permute-start | bytes 368648 | tf_op jit(solution)/shard_map/ppermute | solution.py:18
  105.7 7.6 %collective-permute-start.19 = (bf16[32,1920]{1,0:T(8,128)(2,1)S(1)}, bf16[32,1920]{1,0:T(8,128)(2,1)S(1)}, u32[]{:S(2)}, u32[]{:S(2)}) collective-permute-start(bf16[32,1920]{1,0:T(8,128)(2,1)S(1)} %get-tuple-element.99), channel_id=1, source_target_pairs={{0,12},{2,14},{4,0},{6,2},{8,4},{10,6},{12,8},{14,10},{1,13},{3,15... | collective-permute-start | bytes 368648 | tf_op jit(solution)/shard_map/ppermute | solution.py:18
  107.5 19.2 %collective-permute-start.18 = (bf16[32,1920]{1,0:T(8,128)(2,1)S(1)}, bf16[32,1920]{1,0:T(8,128)(2,1)S(1)}, u32[]{:S(2)}, u32[]{:S(2)}) collective-permute-start(bf16[32,1920]{1,0:T(8,128)(2,1)S(1)} %get-tuple-element.98), channel_id=1, source_target_pairs={{0,10},{2,12},{4,14},{6,0},{8,2},{10,4},{12,6},{14,8},{1,11},{3,13... | collective-permute-start | bytes 368648 | tf_op jit(solution)/shard_map/ppermute | solution.py:18
  107.7 20.8 %collective-permute-start.17 = (bf16[32,1920]{1,0:T(8,128)(2,1)S(1)}, bf16[32,1920]{1,0:T(8,128)(2,1)S(1)}, u32[]{:S(2)}, u32[]{:S(2)}) collective-permute-start(bf16[32,1920]{1,0:T(8,128)(2,1)S(1)} %get-tuple-element.97), channel_id=1, source_target_pairs={{0,8},{2,10},{4,12},{6,14},{8,0},{10,2},{12,4},{14,6},{1,9},{3,11}... | collective-permute-start | bytes 368648 | tf_op jit(solution)/shard_map/ppermute | solution.py:18
  111.2 17.4 %collective-permute-start.16 = (bf16[32,1920]{1,0:T(8,128)(2,1)S(1)}, bf16[32,1920]{1,0:T(8,128)(2,1)S(1)}, u32[]{:S(2)}, u32[]{:S(2)}) collective-permute-start(bf16[32,1920]{1,0:T(8,128)(2,1)S(1)} %get-tuple-element.96), channel_id=1, source_target_pairs={{0,6},{2,8},{4,10},{6,12},{8,14},{10,0},{12,2},{14,4},{1,7},{3,9},... | collective-permute-start | bytes 368648 | tf_op jit(solution)/shard_map/ppermute | solution.py:18
  112.3 16.3 %collective-permute-start.15 = (bf16[32,1920]{1,0:T(8,128)(2,1)S(1)}, bf16[32,1920]{1,0:T(8,128)(2,1)S(1)}, u32[]{:S(2)}, u32[]{:S(2)}) collective-permute-start(bf16[32,1920]{1,0:T(8,128)(2,1)S(1)} %get-tuple-element.95), channel_id=1, source_target_pairs={{0,4},{2,6},{4,8},{6,10},{8,12},{10,14},{12,0},{14,2},{1,5},{3,7},... | collective-permute-start | bytes 368648 | tf_op jit(solution)/shard_map/ppermute | solution.py:18
  113.3 15.3 %collective-permute-start.14 = (bf16[32,1920]{1,0:T(8,128)(2,1)S(1)}, bf16[32,1920]{1,0:T(8,128)(2,1)S(1)}, u32[]{:S(2)}, u32[]{:S(2)}) collective-permute-start(bf16[32,1920]{1,0:T(8,128)(2,1)S(1)} %get-tuple-element.94), channel_id=1, source_target_pairs={{0,2},{2,4},{4,6},{6,8},{8,10},{10,12},{12,14},{14,0},{1,3},{3,5},... | collective-permute-start | bytes 368648 | tf_op jit(solution)/shard_map/ppermute | solution.py:18
  126.7 13.0 %collective-permute-start.13 = (bf16[1,128,1792]{2,1,0:T(8,128)(2,1)S(1)}, bf16[1,128,1792]{2,1,0:T(8,128)(2,1)S(1)}, u32[]{:S(2)}, u32[]{:S(2)}) collective-permute-start(bf16[1,128,1792]{2,1,0:T(8,128)(2,1)S(1)} %fusion.1), channel_id=1, source_target_pairs={{16,0},{17,1},{18,2},{19,3},{20,4},{21,5},{22,6},{23,7},{24,8},{25... | collective-permute-start | bytes 1376264 | tf_op jit(solution)/shard_map/ppermute | solution.py:12
  (31 other events, 54.0 us)

commit v12 on v11

--- a/solution.py
+++ b/solution.py
@@ -116,6 +116,14 @@
             far_decay = far_decay * got_decay
         distance *= 2
     return near_state
+
+
+def dense_swap(block, axis, pairs):
+    count = block.size
+    tiles = -(-count // 2048) * 2048
+    flat = jnp.pad(block.reshape(-1), (0, tiles - count)).reshape(-1, 128)
+    got = lax.ppermute(flat, axis, pairs)
+    return got.reshape(-1)[:count].reshape(block.shape)
 
 
 def both_scans(decay, state, state_grad, axis, filler_fn, filler_args):
@@ -145,14 +153,14 @@
         if distance == 1:
             payload, filler_args = lax.optimization_barrier((payload, filler_args))
         if distance * 2 < size:
-            got = lax.ppermute(payload, axis, [(i, i ^ distance) for i in range(size)])
+            got = dense_swap(payload, axis, [(i, i ^ distance) for i in range(size)])
             got = got.astype(jnp.float32)
             got_fwd = got[:, :width]
             got_bwd = got[:, width : 2 * width]
         else:
             last = jnp.where(upper, total_bwd, total_fwd).astype(jnp.bfloat16)
             last = jnp.concatenate([last, payload[:, 2 * width :]], axis=1)
-            got = lax.ppermute(last, axis, [(i, i ^ distance) for i in range(size)])
+            got = dense_swap(last, axis, [(i, i ^ distance) for i in range(size)])
             got = got.astype(jnp.float32)
             got_fwd = got[:, :width]
             got_bwd = got_fwd

time: 141 us -> 145 us (1.028)
  local copies, waits for them, and re-layouts: 16.6 us -> 21.4 us
  waiting for transfers between devices: 64.2 us -> 59.8 us
  other arithmetic: 13.4 us -> 15.6 us
    ppermute x3, waiting for transfers between devices: 38.6 us -> 33.8 us  [dense_swap(): got = lax.ppermute(flat, axis, pairs)]
    convert_element_type x0 -> x4, local copies, waits for them, and re-layouts: none -> 2.58 us  [the longest x3 1.89 us: both_scans(): got = got.astype(jnp.float32)]
    reshape x0 -> x5, local copies, waits for them, and re-layouts: none -> 2.12 us  [dense_swap(): flat = jnp.pad(block.reshape(-1), (0, tiles - count)).reshape(-1, 128)]
    unnamed x141 -> x149, local copies, waits for them, and re-layouts: 4.31 us -> 3.93 us
  transfers between devices with their start and end apart: 21 -> 21, of which waited for: 10 -> 10; matrix products, arithmetic and copies ran while one was open for 15% -> 14% of each run, Pallas kernels for 0% -> 0%
where the time goes in v12:
time: 145 us; the launch traced here: 144 us
  waiting for transfers between devices  59.8 us (41%)
  starting transfers between devices  26.3 us (18%)
  local copies, waits for them, and re-layouts  21.4 us (15%)
  matrix products  18 us (12%)
  other arithmetic  15.6 us (11%)
  between operations  3.22 us (2%)
    ppermute x3, waiting for transfers between devices, dense_swap(): got = lax.ppermute(flat, axis, pairs)  33.8 us
    ppermute x14, starting transfers between devices, rotated(): return lax.ppermute(block, axis, route)  19.8 us
    ppermute x14, waiting for transfers between devices, rotated(): return lax.ppermute(block, axis, route)  18.1 us
    ppermute x2, waiting for transfers between devices, shifted(): return lax.ppermute(block, axis, route)  7.85 us
    dot_general x5, matrix products, contract(): return jnp.einsum(spec, left, right, preferred_element_type=jnp.float32)  7.71 us
    ppermute x2, starting transfers between devices, shifted(): return lax.ppermute(block, axis, route)  5.6 us
    unnamed x149, local copies, waits for them, and re-layouts  3.93 us
    dot_general x5, matrix products, local_setup(): jnp.einsum('thp,hp->th', values.astype(jnp.float32), step_weight, precisi...  3.42 us
  transfers between devices with their start and end apart: 21, of which 10 were waited for; matrix products, arithmetic and copies ran while one was open for 14% of the time, Pallas kernels for 0%

profile of v12, /device:TPU:4, one launch (start us, length us, event | category | flops | bytes accessed | tf_op | source)
XLA Modules:
  0.0 144.4 jit_solution(11653579352083421547)
XLA Ops:
  0.7 1.6 %collective-permute-start = (bf16[32,1792]{1,0:T(8,128)(2,1)}, bf16[32,1792]{1,0:T(8,128)(2,1)S(1)}, u32[]{:S(2)}, u32[]{:S(2)}) collective-permute-start(bf16[32,1792]{1,0:T(8,128)(2,1)} %bitcast.354), channel_id=1, source_target_pairs={{0,2},{2,4},{4,6},{6,8},{8,10},{10,12},{12,14},{14,0},{1,3},{3,5},... | collective-permute-start | bytes 344072 | tf_op jit(solution)/shard_map/ppermute | solution.py:18
  2.2 1.6 %collective-permute-start.1 = (bf16[32,1792]{1,0:T(8,128)(2,1)}, bf16[32,1792]{1,0:T(8,128)(2,1)S(1)}, u32[]{:S(2)}, u32[]{:S(2)}) collective-permute-start(bf16[32,1792]{1,0:T(8,128)(2,1)} %bitcast.355), channel_id=1, source_target_pairs={{0,4},{2,6},{4,8},{6,10},{8,12},{10,14},{12,0},{14,2},{1,5},{3,7},... | collective-permute-start | bytes 344072 | tf_op jit(solution)/shard_map/ppermute | solution.py:18
  3.8 2.5 %collective-permute-start.2 = (bf16[32,1792]{1,0:T(8,128)(2,1)}, bf16[32,1792]{1,0:T(8,128)(2,1)S(1)}, u32[]{:S(2)}, u32[]{:S(2)}) collective-permute-start(bf16[32,1792]{1,0:T(8,128)(2,1)} %bitcast.356), channel_id=1, source_target_pairs={{0,6},{2,8},{4,10},{6,12},{8,14},{10,0},{12,2},{14,4},{1,7},{3,9},... | collective-permute-start | bytes 344072 | tf_op jit(solution)/shard_map/ppermute | solution.py:18
  6.7 1.2 slice.191
  7.9 4.3 %collective-permute-start.8 = (s32[1]{0:T(128)}, s32[1]{0:T(128)}, u32[]{:S(2)}, u32[]{:S(2)}) collective-permute-start(s32[1]{0:T(128)} %bitcast.13), channel_id=1, source_target_pairs={{0,2},{2,4},{4,6},{6,8},{8,10},{10,12},{12,14},{1,3},{3,5},{5,7},{... | collective-permute-start | bytes 20 | tf_op jit(solution)/shard_map/ppermute | solution.py:12
  12.2 0.9 constant_dynamic-update-slice_fusion.7
  14.6 1.3 copy.66
  16.8 1.0 convert.65
  18.6 1.3 collective-permute-start.4
  19.9 1.2 broadcast_compare_fusion.1
  22.9 3.2 %collective-permute-start.5 = (bf16[32,1792]{1,0:T(8,128)(2,1)S(1)}, bf16[32,1792]{1,0:T(8,128)(2,1)S(1)}, u32[]{:S(2)}, u32[]{:S(2)}) collective-permute-start(bf16[32,1792]{1,0:T(8,128)(2,1)S(1)} %bitcast.359), channel_id=1, source_target_pairs={{0,12},{2,14},{4,0},{6,2},{8,4},{10,6},{12,8},{14,10},{1,13},{3,15... | collective-permute-start | bytes 344072 | tf_op jit(solution)/shard_map/ppermute | solution.py:18
  26.3 1.1 collective-permute-done.4
  27.5 1.1 collective-permute-done.5
  28.5 3.4 %collective-permute-done.6 = bf16[32,1792]{1,0:T(8,128)(2,1)S(1)} collective-permute-done((bf16[32,1792]{1,0:T(8,128)(2,1)S(1)}, bf16[32,1792]{1,0:T(8,128)(2,1)S(1)}, u32[]{:S(2)}, u32[]{:S(2)}) %collective-permute-start.6) | collective-permute-done | bytes 114720 | tf_op jit(solution)/shard_map/ppermute | solution.py:18
  34.2 1.3 fusion.33
  35.5 1.5 %reshape.321 = f32[28,4096]{1,0:T(8,128)S(1)} reshape(f32[28,64,64]{2,1,0:T(8,128)} %fusion.33) | data formatting | bytes 917504 | tf_op jit(solution)/shard_map/reshape | solution.py:231
  37.7 1.2 copy.71
  38.9 1.6 %reshape.322 = f32[28,4096]{1,0:T(8,128)S(1)} reshape(f32[28,64,64]{2,1,0:T(8,128)} %copy.71) | data formatting | bytes 917504 | tf_op jit(solution)/shard_map/reshape | solution.py:251
  40.6 0.9 concatenate.64
  41.6 0.9 multiply_reduce_fusion.3
  43.5 2.8 %fusion.12 = (f32[28,128]{1,0:T(8,128)S(1)}, f32[28,128]{1,0:T(8,128)S(1)}, f32[28,128]{1,0:T(8,128)S(1)}, bf16[128,128]{1,0:T(8,128)(2,1)S(1)}) fusion(f32[28,128]{1,0:T(8,128)S(1)} %fusion.118, f32[128,128]{1,0:T(8,128)S(1)} %fusion.102, f32[128,128]{1,0:T(8,128)} %get-tuple-element.107, f32[28,128]{1,0:T(8,128)S(1)} %fusion.74, ...), kind=kOutput, calls=%fused_computation.18 | convolution fusion | flops 66033152 | bytes 1628160 | tf_op jit(solution)/shard_map/transpose(jvp(hts,shp->thp))/dot_general | solution.py:33
  46.6 0.8 fusion.126
  47.4 0.8 fusion.106
  48.8 1.7 %reshape.323 = bf16[232960]{0:T(1024)(128)(2,1)S(1)} reshape(bf16[28,8320]{1,0:T(8,128)(2,1)} %concatenate.64) | data formatting | bytes 931840 | tf_op jit(solution)/shard_map/reshape | solution.py:124
  51.2 1.8 %fusion.17 = bf16[128,28,64]{0,2,1:T(8,128)(2,1)} fusion(f32[128,28,64]{0,2,1:T(8,128)S(1)} %copy-done.7, f32[28,128]{1,0:T(8,128)S(1)} %fusion.118, f32[128,128]{1,0:T(8,128)S(1)} %fusion.102, f32[128,128]{1,0:T(8,128)S(1)} %copy-done.30, f32[28,128]{1,0:T(8,128)S(1)} %fusion.74, pred[128,128]{1,0:T(8,128)(4,1)S(1)} %copy-done.37, ...), kind=kOutput, calls=%fused_computation.27 | convolution fusion | flops 63078400 | bytes 1574000 | tf_op jit(solution)/shard_map/transpose(jvp(hts,shp->thp))/dot_general | solution.py:33
  53.0 10.7 %collective-permute-done.9 = bf16[1824,128]{1,0:T(8,128)(2,1)S(1)} collective-permute-done((bf16[1824,128]{1,0:T(8,128)(2,1)S(1)}, bf16[1824,128]{1,0:T(8,128)(2,1)S(1)}, u32[]{:S(2)}, u32[]{:S(2)}) %collective-permute-start.9) | collective-permute-done | bytes 466976 | tf_op jit(solution)/shard_map/ppermute | solution.py:125
  64.4 0.9 fusion.120
  66.6 12.2 %collective-permute-done.10 = bf16[1824,128]{1,0:T(8,128)(2,1)S(1)} collective-permute-done((bf16[1824,128]{1,0:T(8,128)(2,1)S(1)}, bf16[1824,128]{1,0:T(8,128)(2,1)S(1)}, u32[]{:S(2)}, u32[]{:S(2)}) %collective-permute-start.10) | collective-permute-done | bytes 466976 | tf_op jit(solution)/shard_map/ppermute | solution.py:125
  78.8 1.0 slice_convert_fusion
  79.8 1.4 reshape.341
  81.5 1.5 %select_convert_fusion = bf16[28,4096]{1,0:T(8,128)(2,1)S(1)} fusion(f32[28,8320]{1,0:T(8,128)S(1)} %reshape.341, f32[28]{0:T(128)S(1)} %get-tuple-element.68, f32[28]{0:T(128)S(1)} %get-tuple-element.55, pred[]{:T(512)S(6)} %eq.83, pred[]{:T(512)S(6)} %eq.82, f32[28,4096]{1,0:T(8,128)S(1)} %reshape.321, f32[28]{0:T(128)S(1)} %reduce.3, ...), kind=kLoop, calls=%fused_computation.65 | loop fusion | flops 2523136 | bytes 2982339 | tf_op jit(solution)/shard_map/convert_element_type | solution.py:161
  84.1 1.0 bitcast_multiply_fusion
  85.1 10.9 %collective-permute-done.11 = bf16[928,128]{1,0:T(8,128)(2,1)S(1)} collective-permute-done((bf16[928,128]{1,0:T(8,128)(2,1)S(1)}, bf16[928,128]{1,0:T(8,128)(2,1)S(1)}, u32[]{:S(2)}, u32[]{:S(2)}) %collective-permute-start.11) | collective-permute-done | bytes 237600 | tf_op jit(solution)/shard_map/ppermute | solution.py:125
  96.3 1.2 multiply_reduce_fusion.4
  100.9 0.8 fusion.136
  101.8 0.8 fusion.137
  102.9 1.0 fusion.22
  104.2 1.6 %fusion.21 = f32[128,28,64]{0,2,1:T(8,128)S(1)} fusion(bf16[28,64,64]{2,1,0:T(8,128)(2,1)S(1)} %copy-done.19, bf16[128,28,64]{0,2,1:T(8,128)(2,1)} %fusion.17, f32[28,128]{1,0:T(8,128)S(1)} %copy.82, f32[28,64]{1,0:T(8,128)S(1)} %copy-done.36, f32[28,128]{1,0:T(8,128)S(1)} %copy.77, f32[128,64]{0,1:T(8,128)S(1)} %copy-done.23, f32[128,28]{0,1:T(8,128)S(1)} %copy-done.28), kind=kOutput, calls=%fused_computation.31 | convolution fusion | flops 32112640 | bytes 1688576 | tf_op jit(solution)/shard_map/transpose(jvp(thn,thp->hnp))/dot_general | solution.py:33
  106.2 1.8 %fusion.131 = (bf16[256,1792]{1,0:T(8,128)(2,1)S(1)}, f32[256,1792]{1,0:T(8,128)}) fusion(bf16[1,128,1792]{2,1,0:T(8,128)(2,1)S(1)} %copy-done.6, s32[]{:T(128)S(6)} %select_n.220, bf16[128,256]{0,1:T(8,128)(2,1)S(1)} %maximum_select_fusion), kind=kOutput, calls=%fused_computation.281 | convolution fusion | flops 118030336 | bytes 3276804 | tf_op jit(solution)/shard_map/dot_general | solution.py:292
  109.5 1.8 %collective-permute-start.19 = (bf16[32,1920]{1,0:T(8,128)(2,1)S(1)}, bf16[32,1920]{1,0:T(8,128)(2,1)S(1)}, u32[]{:S(2)}, u32[]{:S(2)}) collective-permute-start(bf16[32,1920]{1,0:T(8,128)(2,1)S(1)} %get-tuple-element.99), channel_id=1, source_target_pairs={{0,12},{2,14},{4,0},{6,2},{8,4},{10,6},{12,8},{14,10},{1,13},{3,15... | collective-permute-start | bytes 368648 | tf_op jit(solution)/shard_map/ppermute | solution.py:18
  111.6 3.4 %collective-permute-start.17 = (bf16[32,1920]{1,0:T(8,128)(2,1)S(1)}, bf16[32,1920]{1,0:T(8,128)(2,1)S(1)}, u32[]{:S(2)}, u32[]{:S(2)}) collective-permute-start(bf16[32,1920]{1,0:T(8,128)(2,1)S(1)} %get-tuple-element.97), channel_id=1, source_target_pairs={{0,8},{2,10},{4,12},{6,14},{8,0},{10,2},{12,4},{14,6},{1,9},{3,11}... | collective-permute-start | bytes 368648 | tf_op jit(solution)/shard_map/ppermute | solution.py:18
  116.0 1.1 collective-permute-start.15
  117.1 1.7 %collective-permute-start.14 = (bf16[32,1920]{1,0:T(8,128)(2,1)S(1)}, bf16[32,1920]{1,0:T(8,128)(2,1)S(1)}, u32[]{:S(2)}, u32[]{:S(2)}) collective-permute-start(bf16[32,1920]{1,0:T(8,128)(2,1)S(1)} %get-tuple-element.94), channel_id=1, source_target_pairs={{0,2},{2,4},{4,6},{6,8},{8,10},{10,12},{12,14},{14,0},{1,3},{3,5},... | collective-permute-start | bytes 368648 | tf_op jit(solution)/shard_map/ppermute | solution.py:18
  118.8 11.7 %collective-permute-done.18 = bf16[32,1920]{1,0:T(8,128)(2,1)S(1)} collective-permute-done((bf16[32,1920]{1,0:T(8,128)(2,1)S(1)}, bf16[32,1920]{1,0:T(8,128)(2,1)S(1)}, u32[]{:S(2)}, u32[]{:S(2)}) %collective-permute-start.18) | collective-permute-done | bytes 122912 | tf_op jit(solution)/shard_map/ppermute | solution.py:18
  130.5 1.3 collective-permute-start.13
  134.0 1.7 %fusion.51 = f32[1,32,1792]{2,1,0:T(8,128)} fusion(f32[256,1792]{1,0:T(8,128)} %get-tuple-element.112, bf16[32,1920]{1,0:T(8,128)(2,1)S(1)} %collective-permute-done.20, bf16[32,1920]{1,0:T(8,128)(2,1)S(1)} %collective-permute-done.19, bf16[32,1920]{1,0:T(8,128)(2,1)S(1)} %collective-permute-done.18, bf16[32,1920]{1,0:T(8,128)(2,1)S(1)} %collective-permute-done.17, ...), kind=kLoop, calls=%fused_computation.102 | loop fusion | flops 802816 | bytes 1261568 | tf_op jit(solution)/shard_map/broadcast_in_dim | solution.py:334
  135.8 7.9 %collective-permute-done.13 = bf16[1,128,1792]{2,1,0:T(8,128)(2,1)S(1)} collective-permute-done((bf16[1,128,1792]{2,1,0:T(8,128)(2,1)S(1)}, bf16[1,128,1792]{2,1,0:T(8,128)(2,1)S(1)}, u32[]{:S(2)}, u32[]{:S(2)}) %collective-permute-start.13) | collective-permute-done | bytes 458784 | tf_op jit(solution)/shard_map/ppermute | solution.py:12
  143.6 0.8 copy.148
  (259 shorter events, 22.0 us)
Async XLA Ops:
  0.6 15.9 %copy-start.50 = (f32[1,28]{1,0:T(1,128)S(1)}, f32[1,28]{1,0:T(1,128)}, u32[]{:S(2)}) copy-start(f32[1,28]{1,0:T(1,128)} %param.15) | copy-start | bytes 340
  0.6 15.9 %copy-start.17 = (bf16[1,128,1792]{2,1,0:T(8,128)(2,1)S(1)}, bf16[1,128,1792]{2,1,0:T(8,128)(2,1)}, u32[]{:S(2)}) copy-start(bf16[1,128,1792]{2,1,0:T(8,128)(2,1)} %param.11) | copy-start | bytes 1376260
  0.7 22.3 %collective-permute-start = (bf16[32,1792]{1,0:T(8,128)(2,1)}, bf16[32,1792]{1,0:T(8,128)(2,1)S(1)}, u32[]{:S(2)}, u32[]{:S(2)}) collective-permute-start(bf16[32,1792]{1,0:T(8,128)(2,1)} %bitcast.354), channel_id=1, source_target_pairs={{0,2},{2,4},{4,6},{6,8},{8,10},{10,12},{12,14},{14,0},{1,3},{3,5},... | collective-permute-start | bytes 344072 | tf_op jit(solution)/shard_map/ppermute | solution.py:18
  2.2 23.9 %collective-permute-start.1 = (bf16[32,1792]{1,0:T(8,128)(2,1)}, bf16[32,1792]{1,0:T(8,128)(2,1)S(1)}, u32[]{:S(2)}, u32[]{:S(2)}) collective-permute-start(bf16[32,1792]{1,0:T(8,128)(2,1)} %bitcast.355), channel_id=1, source_target_pairs={{0,4},{2,6},{4,8},{6,10},{8,12},{10,14},{12,0},{14,2},{1,5},{3,7},... | collective-permute-start | bytes 344072 | tf_op jit(solution)/shard_map/ppermute | solution.py:18
  3.8 22.5 %collective-permute-start.2 = (bf16[32,1792]{1,0:T(8,128)(2,1)}, bf16[32,1792]{1,0:T(8,128)(2,1)S(1)}, u32[]{:S(2)}, u32[]{:S(2)}) collective-permute-start(bf16[32,1792]{1,0:T(8,128)(2,1)} %bitcast.356), channel_id=1, source_target_pairs={{0,6},{2,8},{4,10},{6,12},{8,14},{10,0},{12,2},{14,4},{1,7},{3,9},... | collective-permute-start | bytes 344072 | tf_op jit(solution)/shard_map/ppermute | solution.py:18
  6.3 20.0 %collective-permute-start.3 = (bf16[32,1792]{1,0:T(8,128)(2,1)}, bf16[32,1792]{1,0:T(8,128)(2,1)S(1)}, u32[]{:S(2)}, u32[]{:S(2)}) collective-permute-start(bf16[32,1792]{1,0:T(8,128)(2,1)} %bitcast.357), channel_id=1, source_target_pairs={{0,8},{2,10},{4,12},{6,14},{8,0},{10,2},{12,4},{14,6},{1,9},{3,11}... | collective-permute-start | bytes 344072 | tf_op jit(solution)/shard_map/ppermute | solution.py:18
  7.9 10.7 %collective-permute-start.8 = (s32[1]{0:T(128)}, s32[1]{0:T(128)}, u32[]{:S(2)}, u32[]{:S(2)}) collective-permute-start(s32[1]{0:T(128)} %bitcast.13), channel_id=1, source_target_pairs={{0,2},{2,4},{4,6},{6,8},{8,10},{10,12},{12,14},{1,3},{3,5},{5,7},{... | collective-permute-start | bytes 20 | tf_op jit(solution)/shard_map/ppermute | solution.py:12
  14.6 4.0 %copy-start.24 = (bf16[1,32,1792]{2,1,0:T(8,128)(2,1)S(1)}, bf16[1,32,1792]{2,1,0:T(8,128)(2,1)}, u32[]{:S(2)}) copy-start(bf16[1,32,1792]{2,1,0:T(8,128)(2,1)} %param.12) | copy-start | bytes 344068
  14.6 7.7 %copy-start.38 = (f32[1,28]{1,0:T(1,128)S(1)}, f32[1,28]{1,0:T(1,128)}, u32[]{:S(2)}) copy-start(f32[1,28]{1,0:T(1,128)} %param.14) | copy-start | bytes 340
  15.9 31.4 %copy-start.3 = (bf16[1,128,1792]{1,2,0:T(8,128)(2,1)}, bf16[1,128,1792]{1,2,0:T(8,128)(2,1)S(1)}, u32[]{:S(2)}) copy-start(bf16[1,128,1792]{1,2,0:T(8,128)(2,1)S(1)} %copy.66) | copy-start | bytes 1376260
  16.5 9.8 %copy-start.15 = (f32[28,1,128]{0,2,1:T(8,128)}, f32[28,1,128]{0,2,1:T(8,128)S(1)}, u32[]{:S(2)}) copy-start(f32[28,1,128]{0,2,1:T(8,128)S(1)} %copy.87) | copy-start | bytes 43012
  16.6 6.0 %copy-start.60 = (f32[28]{0:T(128)}, f32[28]{0:T(128)S(1)}, u32[]{:S(2)}) copy-start(f32[28]{0:T(128)S(1)} %negate_bitcast_fusion) | copy-start | bytes 340
  16.8 15.1 %copy-start.5 = (bf16[1,128,1792]{2,1,0:T(8,128)(2,1)S(1)}, bf16[1,128,1792]{2,1,0:T(8,128)(2,1)}, u32[]{:S(2)}) copy-start(bf16[1,128,1792]{2,1,0:T(8,128)(2,1)} %param.9) | copy-start | bytes 1376260
  18.6 8.8 %collective-permute-start.4 = (bf16[32,1792]{1,0:T(8,128)(2,1)S(1)}, bf16[32,1792]{1,0:T(8,128)(2,1)S(1)}, u32[]{:S(2)}, u32[]{:S(2)}) collective-permute-start(bf16[32,1792]{1,0:T(8,128)(2,1)S(1)} %bitcast.358), channel_id=1, source_target_pairs={{0,10},{2,12},{4,14},{6,0},{8,2},{10,4},{12,6},{14,8},{1,11},{3,13... | collective-permute-start | bytes 344072 | tf_op jit(solution)/shard_map/ppermute | solution.py:18
  21.1 10.8 %copy-start.42 = (pred[128]{0:T(512)(128)(4,1)}, pred[128]{0:T(512)(128)(4,1)S(1)}, u32[]{:S(2)}) copy-start(pred[128]{0:T(512)(128)(4,1)S(1)} %get-tuple-element.77) | copy-start | bytes 388
  21.1 10.8 %copy-start.44 = (f32[128]{0:T(128)}, f32[128]{0:T(128)S(1)}, u32[]{:S(2)}) copy-start(f32[128]{0:T(128)S(1)} %get-tuple-element.78) | copy-start | bytes 1540
  22.6 9.3 %copy-start.32 = (f32[128,28]{0,1:T(8,128)}, f32[128,28]{0,1:T(8,128)S(1)}, u32[]{:S(2)}) copy-start(f32[128,28]{0,1:T(8,128)S(1)} %get-tuple-element.110) | copy-start | bytes 43012
  22.6 14.4 %copy-start.25 = (f32[128,28]{0,1:T(8,128)}, f32[128,28]{0,1:T(8,128)S(1)}, u32[]{:S(2)}) copy-start(f32[128,28]{0,1:T(8,128)S(1)} %get-tuple-element.109) | copy-start | bytes 43012
  22.7 9.8 %copy-start.13 = (f32[128,28]{1,0:T(8,128)}, f32[128,28]{1,0:T(8,128)S(1)}, u32[]{:S(2)}) copy-start(f32[128,28]{1,0:T(8,128)S(1)} %copy.67) | copy-start | bytes 43012
  22.8 9.2 %copy-start.48 = (f32[28]{0:T(128)}, f32[28]{0:T(128)S(1)}, u32[]{:S(2)}) copy-start(f32[28]{0:T(128)S(1)} %slice_bitcast_fusion.7) | copy-start | bytes 340
  22.9 5.6 %collective-permute-start.5 = (bf16[32,1792]{1,0:T(8,128)(2,1)S(1)}, bf16[32,1792]{1,0:T(8,128)(2,1)S(1)}, u32[]{:S(2)}, u32[]{:S(2)}) collective-permute-start(bf16[32,1792]{1,0:T(8,128)(2,1)S(1)} %bitcast.359), channel_id=1, source_target_pairs={{0,12},{2,14},{4,0},{6,2},{8,4},{10,6},{12,8},{14,10},{1,13},{3,15... | collective-permute-start | bytes 344072 | tf_op jit(solution)/shard_map/ppermute | solution.py:18
  26.2 5.7 %collective-permute-start.6 = (bf16[32,1792]{1,0:T(8,128)(2,1)S(1)}, bf16[32,1792]{1,0:T(8,128)(2,1)S(1)}, u32[]{:S(2)}, u32[]{:S(2)}) collective-permute-start(bf16[32,1792]{1,0:T(8,128)(2,1)S(1)} %bitcast.360), channel_id=1, source_target_pairs={{0,14},{2,0},{4,2},{6,4},{8,6},{10,8},{12,10},{14,12},{1,15},{3,1}... | collective-permute-start | bytes 344072 | tf_op jit(solution)/shard_map/ppermute | solution.py:18
  32.0 3.5 %copy-start.1 = (bf16[256,1792]{1,0:T(8,128)(2,1)}, bf16[256,1792]{1,0:T(8,128)(2,1)S(1)}, u32[]{:S(2)}) copy-start(bf16[256,1792]{1,0:T(8,128)(2,1)S(1)} %constant_dynamic-update-slice_fusion) | copy-start | bytes 2752516
  32.5 1.6 %collective-permute-start.7 = (bf16[128,128]{0,1:T(8,128)(2,1)S(1)}, bf16[128,128]{0,1:T(8,128)(2,1)S(1)}, u32[]{:S(2)}, u32[]{:S(2)}) collective-permute-start(bf16[128,128]{0,1:T(8,128)(2,1)S(1)} %fusion.58), channel_id=1, source_target_pairs={{0,1},{1,0},{2,3},{3,2},{4,5},{5,4},{6,7},{7,6},{8,9},{9,8},{10,11... | collective-permute-start | bytes 98312 | tf_op jit(solution)/shard_map/ppermute | solution.py:29
  34.2 3.5 %copy-start.22 = (f32[128,64]{0,1:T(8,128)}, f32[128,64]{0,1:T(8,128)S(1)}, u32[]{:S(2)}) copy-start(f32[128,64]{0,1:T(8,128)S(1)} %slice_convert_fusion.2) | copy-start | bytes 98308
  40.5 23.9 %copy-start = (f32[28,4096]{1,0:T(8,128)}, f32[28,4096]{1,0:T(8,128)S(1)}, u32[]{:S(2)}) copy-start(f32[28,4096]{1,0:T(8,128)S(1)} %reshape.322) | copy-start | bytes 1376260
  40.6 5.6 %copy-start.20 = (bf16[28,126]{1,0:T(8,128)(2,1)}, bf16[28,126]{1,0:T(8,128)(2,1)S(1)}, u32[]{:S(2)}) copy-start(bf16[28,126]{1,0:T(8,128)(2,1)S(1)} %broadcast.170) | copy-start | bytes 21172
  46.3 4.4 %copy-start.52 = (f32[1,28]{1,0:T(1,128)S(1)}, f32[1,28]{1,0:T(1,128)}, u32[]{:S(2)}) copy-start(f32[1,28]{1,0:T(1,128)} %param.15) | copy-start | bytes 340
  46.3 4.4 %copy-start.56 = (f32[1,28]{1,0:T(1,128)S(1)}, f32[1,28]{1,0:T(1,128)}, u32[]{:S(2)}) copy-start(f32[1,28]{1,0:T(1,128)} %param.16) | copy-start | bytes 340
  46.3 5.0 %copy-start.30 = (f32[128,128]{1,0:T(8,128)S(1)}, f32[128,128]{1,0:T(8,128)}, u32[]{:S(2)}) copy-start(f32[128,128]{1,0:T(8,128)} %get-tuple-element.107) | copy-start | bytes 196612
  46.3 4.9 %copy-start.35 = (f32[28,64]{1,0:T(8,128)S(1)}, f32[28,64]{1,0:T(8,128)}, u32[]{:S(2)}) copy-start(f32[28,64]{1,0:T(8,128)} %reshape_squeeze.7) | copy-start | bytes 21508
  46.3 4.9 %copy-start.37 = (pred[128,128]{1,0:T(8,128)(4,1)S(1)}, pred[128,128]{1,0:T(8,128)(4,1)}, u32[]{:S(2)}) copy-start(pred[128,128]{1,0:T(8,128)(4,1)} %get-tuple-element.106) | copy-start | bytes 49156
  50.6 13.2 %collective-permute-start.9 = (bf16[1824,128]{1,0:T(8,128)(2,1)S(1)}, bf16[1824,128]{1,0:T(8,128)(2,1)S(1)}, u32[]{:S(2)}, u32[]{:S(2)}) collective-permute-start(bf16[1824,128]{1,0:T(8,128)(2,1)S(1)} %pad_bitcast_fusion.1), channel_id=1, source_target_pairs={{0,2},{2,0},{4,6},{6,4},{8,10},{10,8},{12,14},{14,12},{1,3},{3,1},... | collective-permute-start | bytes 1400840 | tf_op jit(solution)/shard_map/ppermute | solution.py:125
  53.0 11.0 %copy-start.29 = (f32[28,1]{1,0:T(8,128)S(1)}, f32[28,1]{1,0:T(8,128)}, u32[]{:S(2)}) copy-start(f32[28,1]{1,0:T(8,128)} %copy.74) | copy-start | bytes 340
  66.4 15.1 %copy-start.55 = (f32[28]{0:T(128)S(1)}, f32[28]{0:T(128)}, u32[]{:S(2)}) copy-start(f32[28]{0:T(128)} %exponential_multiply_fusion.1) | copy-start | bytes 340
  66.4 12.4 %collective-permute-start.10 = (bf16[1824,128]{1,0:T(8,128)(2,1)S(1)}, bf16[1824,128]{1,0:T(8,128)(2,1)S(1)}, u32[]{:S(2)}, u32[]{:S(2)}) collective-permute-start(bf16[1824,128]{1,0:T(8,128)(2,1)S(1)} %pad_bitcast_fusion), channel_id=1, source_target_pairs={{0,4},{2,6},{4,0},{6,2},{8,12},{10,14},{12,8},{14,10},{1,5},{3,7},... | collective-permute-start | bytes 1400840 | tf_op jit(solution)/shard_map/ppermute | solution.py:125
  83.4 12.6 %collective-permute-start.11 = (bf16[928,128]{1,0:T(8,128)(2,1)S(1)}, bf16[928,128]{1,0:T(8,128)(2,1)S(1)}, u32[]{:S(2)}, u32[]{:S(2)}) collective-permute-start(bf16[928,128]{1,0:T(8,128)(2,1)S(1)} %pad_bitcast_fusion.2), channel_id=1, source_target_pairs={{0,8},{2,10},{4,12},{6,14},{8,0},{10,2},{12,4},{14,6},{1,9},{3,11}... | collective-permute-start | bytes 712712 | tf_op jit(solution)/shard_map/ppermute | solution.py:125
  100.8 3.3 %copy-start.36 = (f32[28,64]{1,0:T(8,128)S(1)}, f32[28,64]{1,0:T(8,128)}, u32[]{:S(2)}) copy-start(f32[28,64]{1,0:T(8,128)} %reshape_squeeze.7) | copy-start | bytes 21508
  103.9 2.2 %collective-permute-start.12 = (bf16[128,128]{0,1:T(8,128)(2,1)S(1)}, bf16[128,128]{0,1:T(8,128)(2,1)S(1)}, u32[]{:S(2)}, u32[]{:S(2)}) collective-permute-start(bf16[128,128]{0,1:T(8,128)(2,1)S(1)} %add_convert_fusion), channel_id=1, source_target_pairs={{0,1},{1,0},{2,3},{3,2},{4,5},{5,4},{6,7},{7,6},{8,9},{9,8},{10,11... | collective-permute-start | bytes 98312 | tf_op jit(solution)/shard_map/ppermute | solution.py:29
  108.0 7.4 %copy-start.2 = (bf16[256,1792]{1,0:T(8,128)(2,1)S(1)}, bf16[256,1792]{1,0:T(8,128)(2,1)}, u32[]{:S(2)}) copy-start(bf16[256,1792]{1,0:T(8,128)(2,1)} %copy-done.1) | copy-start | bytes 2752516
  108.8 7.2 %collective-permute-start.20 = (bf16[32,1920]{1,0:T(8,128)(2,1)}, bf16[32,1920]{1,0:T(8,128)(2,1)S(1)}, u32[]{:S(2)}, u32[]{:S(2)}) collective-permute-start(bf16[32,1920]{1,0:T(8,128)(2,1)} %get-tuple-element.100), channel_id=1, source_target_pairs={{0,14},{2,0},{4,2},{6,4},{8,6},{10,8},{12,10},{14,12},{1,15},{3,1}... | collective-permute-start | bytes 368648 | tf_op jit(solution)/shard_map/ppermute | solution.py:18
  109.5 7.6 %collective-permute-start.19 = (bf16[32,1920]{1,0:T(8,128)(2,1)S(1)}, bf16[32,1920]{1,0:T(8,128)(2,1)S(1)}, u32[]{:S(2)}, u32[]{:S(2)}) collective-permute-start(bf16[32,1920]{1,0:T(8,128)(2,1)S(1)} %get-tuple-element.99), channel_id=1, source_target_pairs={{0,12},{2,14},{4,0},{6,2},{8,4},{10,6},{12,8},{14,10},{1,13},{3,15... | collective-permute-start | bytes 368648 | tf_op jit(solution)/shard_map/ppermute | solution.py:18
  111.3 19.2 %collective-permute-start.18 = (bf16[32,1920]{1,0:T(8,128)(2,1)S(1)}, bf16[32,1920]{1,0:T(8,128)(2,1)S(1)}, u32[]{:S(2)}, u32[]{:S(2)}) collective-permute-start(bf16[32,1920]{1,0:T(8,128)(2,1)S(1)} %get-tuple-element.98), channel_id=1, source_target_pairs={{0,10},{2,12},{4,14},{6,0},{8,2},{10,4},{12,6},{14,8},{1,11},{3,13... | collective-permute-start | bytes 368648 | tf_op jit(solution)/shard_map/ppermute | solution.py:18
  111.6 20.7 %collective-permute-start.17 = (bf16[32,1920]{1,0:T(8,128)(2,1)S(1)}, bf16[32,1920]{1,0:T(8,128)(2,1)S(1)}, u32[]{:S(2)}, u32[]{:S(2)}) collective-permute-start(bf16[32,1920]{1,0:T(8,128)(2,1)S(1)} %get-tuple-element.97), channel_id=1, source_target_pairs={{0,8},{2,10},{4,12},{6,14},{8,0},{10,2},{12,4},{14,6},{1,9},{3,11}... | collective-permute-start | bytes 368648 | tf_op jit(solution)/shard_map/ppermute | solution.py:18
  115.0 17.3 %collective-permute-start.16 = (bf16[32,1920]{1,0:T(8,128)(2,1)S(1)}, bf16[32,1920]{1,0:T(8,128)(2,1)S(1)}, u32[]{:S(2)}, u32[]{:S(2)}) collective-permute-start(bf16[32,1920]{1,0:T(8,128)(2,1)S(1)} %get-tuple-element.96), channel_id=1, source_target_pairs={{0,6},{2,8},{4,10},{6,12},{8,14},{10,0},{12,2},{14,4},{1,7},{3,9},... | collective-permute-start | bytes 368648 | tf_op jit(solution)/shard_map/ppermute | solution.py:18
  116.0 16.3 %collective-permute-start.15 = (bf16[32,1920]{1,0:T(8,128)(2,1)S(1)}, bf16[32,1920]{1,0:T(8,128)(2,1)S(1)}, u32[]{:S(2)}, u32[]{:S(2)}) collective-permute-start(bf16[32,1920]{1,0:T(8,128)(2,1)S(1)} %get-tuple-element.95), channel_id=1, source_target_pairs={{0,4},{2,6},{4,8},{6,10},{8,12},{10,14},{12,0},{14,2},{1,5},{3,7},... | collective-permute-start | bytes 368648 | tf_op jit(solution)/shard_map/ppermute | solution.py:18
  117.1 15.3 %collective-permute-start.14 = (bf16[32,1920]{1,0:T(8,128)(2,1)S(1)}, bf16[32,1920]{1,0:T(8,128)(2,1)S(1)}, u32[]{:S(2)}, u32[]{:S(2)}) collective-permute-start(bf16[32,1920]{1,0:T(8,128)(2,1)S(1)} %get-tuple-element.94), channel_id=1, source_target_pairs={{0,2},{2,4},{4,6},{6,8},{8,10},{10,12},{12,14},{14,0},{1,3},{3,5},... | collective-permute-start | bytes 368648 | tf_op jit(solution)/shard_map/ppermute | solution.py:18
  130.5 13.2 %collective-permute-start.13 = (bf16[1,128,1792]{2,1,0:T(8,128)(2,1)S(1)}, bf16[1,128,1792]{2,1,0:T(8,128)(2,1)S(1)}, u32[]{:S(2)}, u32[]{:S(2)}) collective-permute-start(bf16[1,128,1792]{2,1,0:T(8,128)(2,1)S(1)} %fusion.1), channel_id=1, source_target_pairs={{16,0},{17,1},{18,2},{19,3},{20,4},{21,5},{22,6},{23,7},{24,8},{25... | collective-permute-start | bytes 1376264 | tf_op jit(solution)/shard_map/ppermute | solution.py:12
  (35 other events, 73.9 us)

commit v13 on v11

--- a/solution.py
+++ b/solution.py
@@ -157,7 +157,7 @@
             got_fwd = got[:, :width]
             got_bwd = got_fwd
             got = jnp.concatenate([got[:, :width], got], axis=1)
-        if distance == 1:
+        if distance == min(2, size // 2):
             got, filler = lax.optimization_barrier((got, filler_fn(*filler_args)))
         got_decay = got[:, 2 * width] + got[:, 2 * width + 1]
         before = jnp.where(upper, before + before_decay[:, None] * got_fwd, before)

time: 141 us -> 142 us (level)
  waiting for transfers between devices: 64.2 us -> 61.1 us
  matrix products: 16.6 us -> 19.2 us
    ppermute x2, waiting for transfers between devices: 26.3 us -> 23.1 us  [both_scans(): got = lax.ppermute(payload, axis, [(i, i ^ distance) for i in range(size)])]
    unnamed x141 -> x155, local copies, waits for them, and re-layouts: 4.31 us -> 3.92 us
  transfers between devices with their start and end apart: 21 -> 21, of which waited for: 10 -> 10; matrix products, arithmetic and copies ran while one was open for 15% -> 16% of each run, Pallas kernels for 0% -> 0%
where the time goes in v13:
time: 142 us; the launch traced here: 141 us
  waiting for transfers between devices  61.1 us (43%)
  starting transfers between devices  26.3 us (19%)
  matrix products  19.2 us (14%)
  local copies, waits for them, and re-layouts  17 us (12%)
  other arithmetic  14.7 us (10%)
  between operations  3.15 us (2%)
    ppermute x2, waiting for transfers between devices, both_scans(): got = lax.ppermute(payload, axis, [(i, i ^ distance) for i in range(size)])  23.1 us
    ppermute x14, starting transfers between devices, rotated(): return lax.ppermute(block, axis, route)  19.8 us
    ppermute x14, waiting for transfers between devices, rotated(): return lax.ppermute(block, axis, route)  18.1 us
    ppermute x1, waiting for transfers between devices, both_scans(): got = lax.ppermute(last, axis, [(i, i ^ distance) for i in range(size)])  12.3 us
    dot_general x5, matrix products, contract(): return jnp.einsum(spec, left, right, preferred_element_type=jnp.float32)  8.21 us
    ppermute x2, waiting for transfers between devices, shifted(): return lax.ppermute(block, axis, route)  7.65 us
    ppermute x2, starting transfers between devices, shifted(): return lax.ppermute(block, axis, route)  5.6 us
    dot_general x5, matrix products, local_setup(): jnp.einsum('thp,hp->th', values.astype(jnp.float32), step_weight, precisi...  4.13 us
  transfers between devices with their start and end apart: 21, of which 10 were waited for; matrix products, arithmetic and copies ran while one was open for 16% of the time, Pallas kernels for 0%

profile of v13, /device:TPU:4, one launch (start us, length us, event | category | flops | bytes accessed | tf_op | source)
XLA Modules:
  0.0 141.2 jit_solution(9774909595815145721)
XLA Ops:
  0.7 1.6 %collective-permute-start = (bf16[32,1792]{1,0:T(8,128)(2,1)}, bf16[32,1792]{1,0:T(8,128)(2,1)S(1)}, u32[]{:S(2)}, u32[]{:S(2)}) collective-permute-start(bf16[32,1792]{1,0:T(8,128)(2,1)} %bitcast.346), channel_id=1, source_target_pairs={{0,2},{2,4},{4,6},{6,8},{8,10},{10,12},{12,14},{14,0},{1,3},{3,5},... | collective-permute-start | bytes 344072 | tf_op jit(solution)/shard_map/ppermute | solution.py:18
  2.2 1.6 %collective-permute-start.1 = (bf16[32,1792]{1,0:T(8,128)(2,1)}, bf16[32,1792]{1,0:T(8,128)(2,1)S(1)}, u32[]{:S(2)}, u32[]{:S(2)}) collective-permute-start(bf16[32,1792]{1,0:T(8,128)(2,1)} %bitcast.347), channel_id=1, source_target_pairs={{0,4},{2,6},{4,8},{6,10},{8,12},{10,14},{12,0},{14,2},{1,5},{3,7},... | collective-permute-start | bytes 344072 | tf_op jit(solution)/shard_map/ppermute | solution.py:18
  3.8 2.5 %collective-permute-start.2 = (bf16[32,1792]{1,0:T(8,128)(2,1)}, bf16[32,1792]{1,0:T(8,128)(2,1)S(1)}, u32[]{:S(2)}, u32[]{:S(2)}) collective-permute-start(bf16[32,1792]{1,0:T(8,128)(2,1)} %bitcast.348), channel_id=1, source_target_pairs={{0,6},{2,8},{4,10},{6,12},{8,14},{10,0},{12,2},{14,4},{1,7},{3,9},... | collective-permute-start | bytes 344072 | tf_op jit(solution)/shard_map/ppermute | solution.py:18
  6.7 1.2 slice.179
  7.9 4.3 %collective-permute-start.8 = (s32[1]{0:T(128)}, s32[1]{0:T(128)}, u32[]{:S(2)}, u32[]{:S(2)}) collective-permute-start(s32[1]{0:T(128)} %bitcast.13), channel_id=1, source_target_pairs={{0,2},{2,4},{4,6},{6,8},{8,10},{10,12},{12,14},{1,3},{3,5},{5,7},{... | collective-permute-start | bytes 20 | tf_op jit(solution)/shard_map/ppermute | solution.py:12
  12.2 0.9 constant_dynamic-update-slice_fusion.7
  13.2 0.7 reduce
  14.6 1.3 copy.66
  16.8 1.1 convert.62
  17.9 0.7 broadcast_compare_fusion
  18.6 1.3 collective-permute-start.4
  19.9 1.2 broadcast_compare_fusion.1
  22.9 3.2 %collective-permute-start.5 = (bf16[32,1792]{1,0:T(8,128)(2,1)S(1)}, bf16[32,1792]{1,0:T(8,128)(2,1)S(1)}, u32[]{:S(2)}, u32[]{:S(2)}) collective-permute-start(bf16[32,1792]{1,0:T(8,128)(2,1)S(1)} %bitcast.351), channel_id=1, source_target_pairs={{0,12},{2,14},{4,0},{6,2},{8,4},{10,6},{12,8},{14,10},{1,13},{3,15... | collective-permute-start | bytes 344072 | tf_op jit(solution)/shard_map/ppermute | solution.py:18
  26.4 1.1 collective-permute-done.4
  27.5 1.0 collective-permute-done.5
  28.5 3.4 %collective-permute-done.6 = bf16[32,1792]{1,0:T(8,128)(2,1)S(1)} collective-permute-done((bf16[32,1792]{1,0:T(8,128)(2,1)S(1)}, bf16[32,1792]{1,0:T(8,128)(2,1)S(1)}, u32[]{:S(2)}, u32[]{:S(2)}) %collective-permute-start.6) | collective-permute-done | bytes 114720 | tf_op jit(solution)/shard_map/ppermute | solution.py:18
  35.5 1.2 copy.71
  36.7 1.6 %reshape.286 = f32[28,4096]{1,0:T(8,128)S(1)} reshape(f32[28,64,64]{2,1,0:T(8,128)} %copy.71) | data formatting | bytes 917504 | tf_op jit(solution)/shard_map/reshape | solution.py:243
  38.4 1.1 concatenate.64
  39.5 1.2 fusion.108
  41.3 2.8 %fusion.12 = (f32[28,128]{1,0:T(8,128)S(1)}, f32[28,128]{1,0:T(8,128)S(1)}, f32[28,128]{1,0:T(8,128)S(1)}, bf16[128,128]{1,0:T(8,128)(2,1)S(1)}) fusion(f32[28,128]{1,0:T(8,128)S(1)} %fusion.118, f32[128,128]{1,0:T(8,128)S(1)} %fusion.102, f32[128,128]{1,0:T(8,128)} %get-tuple-element.107, f32[28,128]{1,0:T(8,128)S(1)} %fusion.74, ...), kind=kOutput, calls=%fused_computation.18 | convolution fusion | flops 66033152 | bytes 1628160 | tf_op jit(solution)/shard_map/transpose(jvp(hts,shp->thp))/dot_general | solution.py:33
  44.1 0.8 fusion.126
  44.9 0.8 fusion.106
  47.2 0.9 multiply_reduce_fusion.3
  48.1 12.9 %collective-permute-done.9 = bf16[28,8320]{1,0:T(8,128)(2,1)S(1)} collective-permute-done((bf16[28,8320]{1,0:T(8,128)(2,1)S(1)}, bf16[28,8320]{1,0:T(8,128)(2,1)S(1)}, u32[]{:S(2)}, u32[]{:S(2)}) %collective-permute-start.9) | collective-permute-done | bytes 465952 | tf_op jit(solution)/shard_map/ppermute | solution.py:148
  62.3 0.9 concatenate.65
  63.8 3.2 %fusion.17 = bf16[128,28,64]{0,2,1:T(8,128)(2,1)} fusion(f32[128,28,64]{0,2,1:T(8,128)} %convert.62, f32[28,128]{1,0:T(8,128)S(1)} %copy-done.31, f32[128,128]{1,0:T(8,128)S(1)} %copy-done.23, f32[128,128]{1,0:T(8,128)S(1)} %copy-done.24, f32[28,128]{1,0:T(8,128)S(1)} %copy-done.64, pred[128,128]{1,0:T(8,128)(4,1)S(1)} %copy-done.32, ...), kind=kOutput, calls=%fused_computation.27 | convolution fusion | flops 63078400 | bytes 1574000 | tf_op jit(solution)/shard_map/transpose(jvp(hts,shp->thp))/dot_general | solution.py:33
  67.0 10.2 %collective-permute-done.10 = bf16[28,8320]{1,0:T(8,128)(2,1)S(1)} collective-permute-done((bf16[28,8320]{1,0:T(8,128)(2,1)}, bf16[28,8320]{1,0:T(8,128)(2,1)S(1)}, u32[]{:S(2)}, u32[]{:S(2)}) %collective-permute-start.10) | collective-permute-done | bytes 465952 | tf_op jit(solution)/shard_map/ppermute | solution.py:148
  77.3 1.4 fusion.80
  79.1 0.8 concatenate.66
  80.6 1.0 bitcast_multiply_fusion
  81.7 12.3 %collective-permute-done.11 = bf16[28,4224]{1,0:T(8,128)(2,1)S(1)} collective-permute-done((bf16[28,4224]{1,0:T(8,128)(2,1)S(1)}, bf16[28,4224]{1,0:T(8,128)(2,1)S(1)}, u32[]{:S(2)}, u32[]{:S(2)}) %collective-permute-start.11) | collective-permute-done | bytes 236576 | tf_op jit(solution)/shard_map/ppermute | solution.py:155
  93.9 1.2 multiply_reduce_fusion.4
  98.6 0.8 fusion.136
  99.5 0.8 fusion.137
  100.5 1.0 fusion.22
  101.8 1.6 %fusion.21 = f32[128,28,64]{0,2,1:T(8,128)S(1)} fusion(bf16[28,64,64]{2,1,0:T(8,128)(2,1)S(1)} %reshape.288, bf16[128,28,64]{0,2,1:T(8,128)(2,1)} %fusion.17, f32[28,128]{1,0:T(8,128)S(1)} %copy.82, f32[28,64]{1,0:T(8,128)S(1)} %copy-done.29, f32[28,128]{1,0:T(8,128)S(1)} %copy.77, f32[128,64]{0,1:T(8,128)S(1)} %copy-done.16, f32[128,28]{0,1:T(8,128)S(1)} %copy-done.20), kind=kOutput, calls=%fused_computation.31 | convolution fusion | flops 32112640 | bytes 1688576 | tf_op jit(solution)/shard_map/transpose(jvp(thn,thp->hnp))/dot_general | solution.py:33
  103.8 1.8 %fusion.131 = (bf16[256,1792]{1,0:T(8,128)(2,1)S(1)}, f32[256,1792]{1,0:T(8,128)}) fusion(bf16[1,128,1792]{2,1,0:T(8,128)(2,1)S(1)} %copy-done.7, s32[]{:T(128)S(6)} %select_n.220, bf16[128,256]{0,1:T(8,128)(2,1)S(1)} %maximum_select_fusion), kind=kOutput, calls=%fused_computation.276 | convolution fusion | flops 118030336 | bytes 3276804 | tf_op jit(solution)/shard_map/dot_general | solution.py:284
  105.7 0.8 collective-permute-start.20
  106.5 1.8 %collective-permute-start.19 = (bf16[32,1920]{1,0:T(8,128)(2,1)S(1)}, bf16[32,1920]{1,0:T(8,128)(2,1)S(1)}, u32[]{:S(2)}, u32[]{:S(2)}) collective-permute-start(bf16[32,1920]{1,0:T(8,128)(2,1)S(1)} %get-tuple-element.99), channel_id=1, source_target_pairs={{0,12},{2,14},{4,0},{6,2},{8,4},{10,6},{12,8},{14,10},{1,13},{3,15... | collective-permute-start | bytes 368648 | tf_op jit(solution)/shard_map/ppermute | solution.py:18
  108.6 3.4 %collective-permute-start.17 = (bf16[32,1920]{1,0:T(8,128)(2,1)S(1)}, bf16[32,1920]{1,0:T(8,128)(2,1)S(1)}, u32[]{:S(2)}, u32[]{:S(2)}) collective-permute-start(bf16[32,1920]{1,0:T(8,128)(2,1)S(1)} %get-tuple-element.97), channel_id=1, source_target_pairs={{0,8},{2,10},{4,12},{6,14},{8,0},{10,2},{12,4},{14,6},{1,9},{3,11}... | collective-permute-start | bytes 368648 | tf_op jit(solution)/shard_map/ppermute | solution.py:18
  112.8 1.3 collective-permute-start.15
  114.1 1.5 %collective-permute-start.14 = (bf16[32,1920]{1,0:T(8,128)(2,1)S(1)}, bf16[32,1920]{1,0:T(8,128)(2,1)S(1)}, u32[]{:S(2)}, u32[]{:S(2)}) collective-permute-start(bf16[32,1920]{1,0:T(8,128)(2,1)S(1)} %get-tuple-element.94), channel_id=1, source_target_pairs={{0,2},{2,4},{4,6},{6,8},{8,10},{10,12},{12,14},{14,0},{1,3},{3,5},... | collective-permute-start | bytes 368648 | tf_op jit(solution)/shard_map/ppermute | solution.py:18
  115.6 11.9 %collective-permute-done.18 = bf16[32,1920]{1,0:T(8,128)(2,1)S(1)} collective-permute-done((bf16[32,1920]{1,0:T(8,128)(2,1)S(1)}, bf16[32,1920]{1,0:T(8,128)(2,1)S(1)}, u32[]{:S(2)}, u32[]{:S(2)}) %collective-permute-start.18) | collective-permute-done | bytes 122912 | tf_op jit(solution)/shard_map/ppermute | solution.py:18
  127.5 1.3 collective-permute-start.13
  131.1 1.7 %fusion.51 = f32[1,32,1792]{2,1,0:T(8,128)} fusion(f32[256,1792]{1,0:T(8,128)} %get-tuple-element.112, bf16[32,1920]{1,0:T(8,128)(2,1)S(1)} %collective-permute-done.20, bf16[32,1920]{1,0:T(8,128)(2,1)S(1)} %collective-permute-done.19, bf16[32,1920]{1,0:T(8,128)(2,1)S(1)} %collective-permute-done.18, bf16[32,1920]{1,0:T(8,128)(2,1)S(1)} %collective-permute-done.17, ...), kind=kLoop, calls=%fused_computation.97 | loop fusion | flops 802816 | bytes 1261568 | tf_op jit(solution)/shard_map/broadcast_in_dim | solution.py:326
  132.8 7.7 %collective-permute-done.13 = bf16[1,128,1792]{2,1,0:T(8,128)(2,1)S(1)} collective-permute-done((bf16[1,128,1792]{2,1,0:T(8,128)(2,1)S(1)}, bf16[1,128,1792]{2,1,0:T(8,128)(2,1)S(1)}, u32[]{:S(2)}, u32[]{:S(2)}) %collective-permute-start.13) | collective-permute-done | bytes 458784 | tf_op jit(solution)/shard_map/ppermute | solution.py:12
  140.5 0.8 copy.148
  (256 shorter events, 18.7 us)
Async XLA Ops:
  0.6 15.9 %copy-start.50 = (f32[1,28]{1,0:T(1,128)S(1)}, f32[1,28]{1,0:T(1,128)}, u32[]{:S(2)}) copy-start(f32[1,28]{1,0:T(1,128)} %param.15) | copy-start | bytes 340
  0.6 15.9 %copy-start.14 = (bf16[1,128,1792]{2,1,0:T(8,128)(2,1)S(1)}, bf16[1,128,1792]{2,1,0:T(8,128)(2,1)}, u32[]{:S(2)}) copy-start(bf16[1,128,1792]{2,1,0:T(8,128)(2,1)} %param.11) | copy-start | bytes 1376260
  0.7 22.3 %collective-permute-start = (bf16[32,1792]{1,0:T(8,128)(2,1)}, bf16[32,1792]{1,0:T(8,128)(2,1)S(1)}, u32[]{:S(2)}, u32[]{:S(2)}) collective-permute-start(bf16[32,1792]{1,0:T(8,128)(2,1)} %bitcast.346), channel_id=1, source_target_pairs={{0,2},{2,4},{4,6},{6,8},{8,10},{10,12},{12,14},{14,0},{1,3},{3,5},... | collective-permute-start | bytes 344072 | tf_op jit(solution)/shard_map/ppermute | solution.py:18
  2.2 23.9 %collective-permute-start.1 = (bf16[32,1792]{1,0:T(8,128)(2,1)}, bf16[32,1792]{1,0:T(8,128)(2,1)S(1)}, u32[]{:S(2)}, u32[]{:S(2)}) collective-permute-start(bf16[32,1792]{1,0:T(8,128)(2,1)} %bitcast.347), channel_id=1, source_target_pairs={{0,4},{2,6},{4,8},{6,10},{8,12},{10,14},{12,0},{14,2},{1,5},{3,7},... | collective-permute-start | bytes 344072 | tf_op jit(solution)/shard_map/ppermute | solution.py:18
  3.8 22.5 %collective-permute-start.2 = (bf16[32,1792]{1,0:T(8,128)(2,1)}, bf16[32,1792]{1,0:T(8,128)(2,1)S(1)}, u32[]{:S(2)}, u32[]{:S(2)}) collective-permute-start(bf16[32,1792]{1,0:T(8,128)(2,1)} %bitcast.348), channel_id=1, source_target_pairs={{0,6},{2,8},{4,10},{6,12},{8,14},{10,0},{12,2},{14,4},{1,7},{3,9},... | collective-permute-start | bytes 344072 | tf_op jit(solution)/shard_map/ppermute | solution.py:18
  6.3 20.0 %collective-permute-start.3 = (bf16[32,1792]{1,0:T(8,128)(2,1)}, bf16[32,1792]{1,0:T(8,128)(2,1)S(1)}, u32[]{:S(2)}, u32[]{:S(2)}) collective-permute-start(bf16[32,1792]{1,0:T(8,128)(2,1)} %bitcast.349), channel_id=1, source_target_pairs={{0,8},{2,10},{4,12},{6,14},{8,0},{10,2},{12,4},{14,6},{1,9},{3,11}... | collective-permute-start | bytes 344072 | tf_op jit(solution)/shard_map/ppermute | solution.py:18
  7.9 10.7 %collective-permute-start.8 = (s32[1]{0:T(128)}, s32[1]{0:T(128)}, u32[]{:S(2)}, u32[]{:S(2)}) collective-permute-start(s32[1]{0:T(128)} %bitcast.13), channel_id=1, source_target_pairs={{0,2},{2,4},{4,6},{6,8},{8,10},{10,12},{12,14},{1,3},{3,5},{5,7},{... | collective-permute-start | bytes 20 | tf_op jit(solution)/shard_map/ppermute | solution.py:12
  14.6 4.0 %copy-start.18 = (bf16[1,32,1792]{2,1,0:T(8,128)(2,1)S(1)}, bf16[1,32,1792]{2,1,0:T(8,128)(2,1)}, u32[]{:S(2)}) copy-start(bf16[1,32,1792]{2,1,0:T(8,128)(2,1)} %param.12) | copy-start | bytes 344068
  14.6 7.7 %copy-start.33 = (f32[1,28]{1,0:T(1,128)S(1)}, f32[1,28]{1,0:T(1,128)}, u32[]{:S(2)}) copy-start(f32[1,28]{1,0:T(1,128)} %param.14) | copy-start | bytes 340
  15.9 31.3 %copy-start.4 = (bf16[1,128,1792]{1,2,0:T(8,128)(2,1)}, bf16[1,128,1792]{1,2,0:T(8,128)(2,1)S(1)}, u32[]{:S(2)}) copy-start(bf16[1,128,1792]{1,2,0:T(8,128)(2,1)S(1)} %copy.66) | copy-start | bytes 1376260
  16.5 9.8 %copy-start.11 = (f32[28,1,128]{0,2,1:T(8,128)}, f32[28,1,128]{0,2,1:T(8,128)S(1)}, u32[]{:S(2)}) copy-start(f32[28,1,128]{0,2,1:T(8,128)S(1)} %copy.87) | copy-start | bytes 43012
  16.6 9.8 %copy-start.61 = (f32[28]{0:T(128)}, f32[28]{0:T(128)S(1)}, u32[]{:S(2)}) copy-start(f32[28]{0:T(128)S(1)} %negate_bitcast_fusion) | copy-start | bytes 340
  16.8 15.1 %copy-start.6 = (bf16[1,128,1792]{2,1,0:T(8,128)(2,1)S(1)}, bf16[1,128,1792]{2,1,0:T(8,128)(2,1)}, u32[]{:S(2)}) copy-start(bf16[1,128,1792]{2,1,0:T(8,128)(2,1)} %param.9) | copy-start | bytes 1376260
  18.6 8.8 %collective-permute-start.4 = (bf16[32,1792]{1,0:T(8,128)(2,1)S(1)}, bf16[32,1792]{1,0:T(8,128)(2,1)S(1)}, u32[]{:S(2)}, u32[]{:S(2)}) collective-permute-start(bf16[32,1792]{1,0:T(8,128)(2,1)S(1)} %bitcast.350), channel_id=1, source_target_pairs={{0,10},{2,12},{4,14},{6,0},{8,2},{10,4},{12,6},{14,8},{1,11},{3,13... | collective-permute-start | bytes 344072 | tf_op jit(solution)/shard_map/ppermute | solution.py:18
  21.1 11.2 %copy-start.35 = (pred[128]{0:T(512)(128)(4,1)}, pred[128]{0:T(512)(128)(4,1)S(1)}, u32[]{:S(2)}) copy-start(pred[128]{0:T(512)(128)(4,1)S(1)} %get-tuple-element.77) | copy-start | bytes 388
  21.2 11.2 %copy-start.37 = (f32[128]{0:T(128)}, f32[128]{0:T(128)S(1)}, u32[]{:S(2)}) copy-start(f32[128]{0:T(128)S(1)} %get-tuple-element.78) | copy-start | bytes 1540
  22.6 9.3 %copy-start.26 = (f32[128,28]{0,1:T(8,128)}, f32[128,28]{0,1:T(8,128)S(1)}, u32[]{:S(2)}) copy-start(f32[128,28]{0,1:T(8,128)S(1)} %get-tuple-element.110) | copy-start | bytes 43012
  22.8 9.1 %copy-start.43 = (f32[28]{0:T(128)}, f32[28]{0:T(128)S(1)}, u32[]{:S(2)}) copy-start(f32[28]{0:T(128)S(1)} %slice_bitcast_fusion.7) | copy-start | bytes 340
  22.9 5.6 %collective-permute-start.5 = (bf16[32,1792]{1,0:T(8,128)(2,1)S(1)}, bf16[32,1792]{1,0:T(8,128)(2,1)S(1)}, u32[]{:S(2)}, u32[]{:S(2)}) collective-permute-start(bf16[32,1792]{1,0:T(8,128)(2,1)S(1)} %bitcast.351), channel_id=1, source_target_pairs={{0,12},{2,14},{4,0},{6,2},{8,4},{10,6},{12,8},{14,10},{1,13},{3,15... | collective-permute-start | bytes 344072 | tf_op jit(solution)/shard_map/ppermute | solution.py:18
  26.2 5.7 %collective-permute-start.6 = (bf16[32,1792]{1,0:T(8,128)(2,1)S(1)}, bf16[32,1792]{1,0:T(8,128)(2,1)S(1)}, u32[]{:S(2)}, u32[]{:S(2)}) collective-permute-start(bf16[32,1792]{1,0:T(8,128)(2,1)S(1)} %bitcast.352), channel_id=1, source_target_pairs={{0,14},{2,0},{4,2},{6,4},{8,6},{10,8},{12,10},{14,12},{1,15},{3,1}... | collective-permute-start | bytes 344072 | tf_op jit(solution)/shard_map/ppermute | solution.py:18
  32.5 1.6 %collective-permute-start.7 = (bf16[128,128]{0,1:T(8,128)(2,1)S(1)}, bf16[128,128]{0,1:T(8,128)(2,1)S(1)}, u32[]{:S(2)}, u32[]{:S(2)}) collective-permute-start(bf16[128,128]{0,1:T(8,128)(2,1)S(1)} %fusion.58), channel_id=1, source_target_pairs={{0,1},{1,0},{2,3},{3,2},{4,5},{5,4},{6,7},{7,6},{8,9},{9,8},{10,11... | collective-permute-start | bytes 98312 | tf_op jit(solution)/shard_map/ppermute | solution.py:29
  36.7 4.5 %copy-start.8 = (f32[128,28,64]{0,2,1:T(8,128)S(1)}, f32[128,28,64]{0,2,1:T(8,128)}, u32[]{:S(2)}) copy-start(f32[128,28,64]{0,2,1:T(8,128)} %convert.62) | copy-start | bytes 2752516
  38.3 23.6 %copy-start = (f32[28,4096]{1,0:T(8,128)}, f32[28,4096]{1,0:T(8,128)S(1)}, u32[]{:S(2)}) copy-start(f32[28,4096]{1,0:T(8,128)S(1)} %reshape.286) | copy-start | bytes 1376260
  41.3 5.2 %copy-start.13 = (bf16[28,8320]{1,0:T(8,128)(2,1)S(1)}, bf16[28,8320]{1,0:T(8,128)(2,1)}, u32[]{:S(2)}) copy-start(bf16[28,8320]{1,0:T(8,128)(2,1)} %concatenate.64) | copy-start | bytes 1397764
  44.9 16.2 %copy-start.59 = (f32[128,28]{0,1:T(8,128)}, f32[128,28]{0,1:T(8,128)S(1)}, u32[]{:S(2)}) copy-start(f32[128,28]{0,1:T(8,128)S(1)} %get-tuple-element.72) | copy-start | bytes 43012
  44.9 16.2 %copy-start.21 = (f32[28,1]{1,0:T(8,128)S(1)}, f32[28,1]{1,0:T(8,128)}, u32[]{:S(2)}) copy-start(f32[28,1]{1,0:T(8,128)} %copy.74) | copy-start | bytes 340
  44.9 17.0 %copy-start.53 = (f32[28]{0:T(128)S(1)}, f32[28]{0:T(128)}, u32[]{:S(2)}) copy-start(f32[28]{0:T(128)} %exponential_multiply_fusion.1) | copy-start | bytes 340
  46.4 14.5 %collective-permute-start.9 = (bf16[28,8320]{1,0:T(8,128)(2,1)S(1)}, bf16[28,8320]{1,0:T(8,128)(2,1)S(1)}, u32[]{:S(2)}, u32[]{:S(2)}) collective-permute-start(bf16[28,8320]{1,0:T(8,128)(2,1)S(1)} %copy-done.13), channel_id=1, source_target_pairs={{0,2},{2,0},{4,6},{6,4},{8,10},{10,8},{12,14},{14,12},{1,3},{3,1},... | collective-permute-start | bytes 1397768 | tf_op jit(solution)/shard_map/ppermute | solution.py:148
  63.2 13.9 %collective-permute-start.10 = (bf16[28,8320]{1,0:T(8,128)(2,1)}, bf16[28,8320]{1,0:T(8,128)(2,1)S(1)}, u32[]{:S(2)}, u32[]{:S(2)}) collective-permute-start(bf16[28,8320]{1,0:T(8,128)(2,1)} %concatenate.65), channel_id=1, source_target_pairs={{0,4},{2,6},{4,0},{6,2},{8,12},{10,14},{12,8},{14,10},{1,5},{3,7},... | collective-permute-start | bytes 1397768 | tf_op jit(solution)/shard_map/ppermute | solution.py:148
  63.8 14.9 %copy-start.41 = (f32[28]{0:T(128)S(1)}, f32[28]{0:T(128)}, u32[]{:S(2)}) copy-start(f32[28]{0:T(128)} %copy-done.40) | copy-start | bytes 340
  63.8 14.9 %copy-start.49 = (f32[28]{0:T(128)S(1)}, f32[28]{0:T(128)}, u32[]{:S(2)}) copy-start(f32[28]{0:T(128)} %get-tuple-element.68) | copy-start | bytes 340
  63.8 14.9 %copy-start.54 = (f32[28]{0:T(128)S(1)}, f32[28]{0:T(128)}, u32[]{:S(2)}) copy-start(f32[28]{0:T(128)} %exponential_multiply_fusion.1) | copy-start | bytes 340
  67.0 11.7 %copy-start.1 = (f32[28,4096]{1,0:T(8,128)S(1)}, f32[28,4096]{1,0:T(8,128)}, u32[]{:S(2)}) copy-start(f32[28,4096]{1,0:T(8,128)} %copy-done) | copy-start | bytes 1376260
  79.1 14.8 %copy-start.45 = (f32[28]{0:T(128)S(1)}, f32[28]{0:T(128)}, u32[]{:S(2)}) copy-start(f32[28]{0:T(128)} %get-tuple-element.52) | copy-start | bytes 340
  79.1 14.8 %copy-start.46 = (f32[28]{0:T(128)S(1)}, f32[28]{0:T(128)}, u32[]{:S(2)}) copy-start(f32[28]{0:T(128)} %get-tuple-element.53) | copy-start | bytes 340
  79.1 14.8 %copy-start.47 = (f32[28]{0:T(128)S(1)}, f32[28]{0:T(128)}, u32[]{:S(2)}) copy-start(f32[28]{0:T(128)} %get-tuple-element.54) | copy-start | bytes 340
  79.1 14.8 %copy-start.48 = (f32[28]{0:T(128)S(1)}, f32[28]{0:T(128)}, u32[]{:S(2)}) copy-start(f32[28]{0:T(128)} %get-tuple-element.56) | copy-start | bytes 340
  79.9 14.0 %collective-permute-start.11 = (bf16[28,4224]{1,0:T(8,128)(2,1)S(1)}, bf16[28,4224]{1,0:T(8,128)(2,1)S(1)}, u32[]{:S(2)}, u32[]{:S(2)}) collective-permute-start(bf16[28,4224]{1,0:T(8,128)(2,1)S(1)} %concatenate.66), channel_id=1, source_target_pairs={{0,8},{2,10},{4,12},{6,14},{8,0},{10,2},{12,4},{14,6},{1,9},{3,11}... | collective-permute-start | bytes 709640 | tf_op jit(solution)/shard_map/ppermute | solution.py:155
  101.6 2.2 %collective-permute-start.12 = (bf16[128,128]{0,1:T(8,128)(2,1)S(1)}, bf16[128,128]{0,1:T(8,128)(2,1)S(1)}, u32[]{:S(2)}, u32[]{:S(2)}) collective-permute-start(bf16[128,128]{0,1:T(8,128)(2,1)S(1)} %add_convert_fusion), channel_id=1, source_target_pairs={{0,1},{1,0},{2,3},{3,2},{4,5},{5,4},{6,7},{7,6},{8,9},{9,8},{10,11... | collective-permute-start | bytes 98312 | tf_op jit(solution)/shard_map/ppermute | solution.py:29
  105.6 6.8 %copy-start.3 = (bf16[256,1792]{1,0:T(8,128)(2,1)S(1)}, bf16[256,1792]{1,0:T(8,128)(2,1)}, u32[]{:S(2)}) copy-start(bf16[256,1792]{1,0:T(8,128)(2,1)} %copy-done.2) | copy-start | bytes 2752516
  105.7 7.1 %collective-permute-start.20 = (bf16[32,1920]{1,0:T(8,128)(2,1)S(1)}, bf16[32,1920]{1,0:T(8,128)(2,1)S(1)}, u32[]{:S(2)}, u32[]{:S(2)}) collective-permute-start(bf16[32,1920]{1,0:T(8,128)(2,1)S(1)} %get-tuple-element.100), channel_id=1, source_target_pairs={{0,14},{2,0},{4,2},{6,4},{8,6},{10,8},{12,10},{14,12},{1,15},{3,1}... | collective-permute-start | bytes 368648 | tf_op jit(solution)/shard_map/ppermute | solution.py:18
  106.5 7.6 %collective-permute-start.19 = (bf16[32,1920]{1,0:T(8,128)(2,1)S(1)}, bf16[32,1920]{1,0:T(8,128)(2,1)S(1)}, u32[]{:S(2)}, u32[]{:S(2)}) collective-permute-start(bf16[32,1920]{1,0:T(8,128)(2,1)S(1)} %get-tuple-element.99), channel_id=1, source_target_pairs={{0,12},{2,14},{4,0},{6,2},{8,4},{10,6},{12,8},{14,10},{1,13},{3,15... | collective-permute-start | bytes 368648 | tf_op jit(solution)/shard_map/ppermute | solution.py:18
  108.3 19.1 %collective-permute-start.18 = (bf16[32,1920]{1,0:T(8,128)(2,1)S(1)}, bf16[32,1920]{1,0:T(8,128)(2,1)S(1)}, u32[]{:S(2)}, u32[]{:S(2)}) collective-permute-start(bf16[32,1920]{1,0:T(8,128)(2,1)S(1)} %get-tuple-element.98), channel_id=1, source_target_pairs={{0,10},{2,12},{4,14},{6,0},{8,2},{10,4},{12,6},{14,8},{1,11},{3,13... | collective-permute-start | bytes 368648 | tf_op jit(solution)/shard_map/ppermute | solution.py:18
  108.6 20.7 %collective-permute-start.17 = (bf16[32,1920]{1,0:T(8,128)(2,1)S(1)}, bf16[32,1920]{1,0:T(8,128)(2,1)S(1)}, u32[]{:S(2)}, u32[]{:S(2)}) collective-permute-start(bf16[32,1920]{1,0:T(8,128)(2,1)S(1)} %get-tuple-element.97), channel_id=1, source_target_pairs={{0,8},{2,10},{4,12},{6,14},{8,0},{10,2},{12,4},{14,6},{1,9},{3,11}... | collective-permute-start | bytes 368648 | tf_op jit(solution)/shard_map/ppermute | solution.py:18
  112.0 17.3 %collective-permute-start.16 = (bf16[32,1920]{1,0:T(8,128)(2,1)S(1)}, bf16[32,1920]{1,0:T(8,128)(2,1)S(1)}, u32[]{:S(2)}, u32[]{:S(2)}) collective-permute-start(bf16[32,1920]{1,0:T(8,128)(2,1)S(1)} %get-tuple-element.96), channel_id=1, source_target_pairs={{0,6},{2,8},{4,10},{6,12},{8,14},{10,0},{12,2},{14,4},{1,7},{3,9},... | collective-permute-start | bytes 368648 | tf_op jit(solution)/shard_map/ppermute | solution.py:18
  112.8 16.5 %collective-permute-start.15 = (bf16[32,1920]{1,0:T(8,128)(2,1)S(1)}, bf16[32,1920]{1,0:T(8,128)(2,1)S(1)}, u32[]{:S(2)}, u32[]{:S(2)}) collective-permute-start(bf16[32,1920]{1,0:T(8,128)(2,1)S(1)} %get-tuple-element.95), channel_id=1, source_target_pairs={{0,4},{2,6},{4,8},{6,10},{8,12},{10,14},{12,0},{14,2},{1,5},{3,7},... | collective-permute-start | bytes 368648 | tf_op jit(solution)/shard_map/ppermute | solution.py:18
  114.1 15.3 %collective-permute-start.14 = (bf16[32,1920]{1,0:T(8,128)(2,1)S(1)}, bf16[32,1920]{1,0:T(8,128)(2,1)S(1)}, u32[]{:S(2)}, u32[]{:S(2)}) collective-permute-start(bf16[32,1920]{1,0:T(8,128)(2,1)S(1)} %get-tuple-element.94), channel_id=1, source_target_pairs={{0,2},{2,4},{4,6},{6,8},{8,10},{10,12},{12,14},{14,0},{1,3},{3,5},... | collective-permute-start | bytes 368648 | tf_op jit(solution)/shard_map/ppermute | solution.py:18
  127.5 13.0 %collective-permute-start.13 = (bf16[1,128,1792]{2,1,0:T(8,128)(2,1)S(1)}, bf16[1,128,1792]{2,1,0:T(8,128)(2,1)S(1)}, u32[]{:S(2)}, u32[]{:S(2)}) collective-permute-start(bf16[1,128,1792]{2,1,0:T(8,128)(2,1)S(1)} %fusion.1), channel_id=1, source_target_pairs={{16,0},{17,1},{18,2},{19,3},{20,4},{21,5},{22,6},{23,7},{24,8},{25... | collective-permute-start | bytes 1376264 | tf_op jit(solution)/shard_map/ppermute | solution.py:12
  (38 other events, 78.5 us)

commit v14 on v11

--- a/solution.py
+++ b/solution.py
@@ -146,20 +146,17 @@
             payload, filler_args = lax.optimization_barrier((payload, filler_args))
         if distance * 2 < size:
             got = lax.ppermute(payload, axis, [(i, i ^ distance) for i in range(size)])
-            got = got.astype(jnp.float32)
-            got_fwd = got[:, :width]
-            got_bwd = got[:, width : 2 * width]
+            at = 2 * width
         else:
             last = jnp.where(upper, total_bwd, total_fwd).astype(jnp.bfloat16)
             last = jnp.concatenate([last, payload[:, 2 * width :]], axis=1)
             got = lax.ppermute(last, axis, [(i, i ^ distance) for i in range(size)])
-            got = got.astype(jnp.float32)
-            got_fwd = got[:, :width]
-            got_bwd = got_fwd
-            got = jnp.concatenate([got[:, :width], got], axis=1)
+            at = width
         if distance == 1:
             got, filler = lax.optimization_barrier((got, filler_fn(*filler_args)))
-        got_decay = got[:, 2 * width] + got[:, 2 * width + 1]
+        got_fwd = got[:, :width].astype(jnp.float32)
+        got_bwd = got[:, at - width : at].astype(jnp.float32)
+        got_decay = got[:, at].astype(jnp.float32) + got[:, at + 1].astype(jnp.float32)
         before = jnp.where(upper, before + before_decay[:, None] * got_fwd, before)
         before_decay = jnp.where(upper, before_decay * got_decay, before_decay)
         after = jnp.where(upper, after, after + after_decay[:, None] * got_bwd)

time: 141 us -> 153 us (1.085)
  other arithmetic: 13.4 us -> 19.4 us
  matrix products: 16.6 us -> 20.2 us
  local copies, waits for them, and re-layouts: 16.6 us -> 20.2 us
    another operation x6, other arithmetic: 0.41 us -> 2.73 us
    reduce_sum x1, other arithmetic: 0.3 us -> 2.14 us  [span_local(): values.astype(jnp.float32) * (1.0 + skip_gain)[None, :, None] + local_part]
    convert_element_type x1, other arithmetic: 0.44 us -> 2.25 us  [both_scans(): last = jnp.where(upper, total_bwd, total_fwd).astype(jnp.bfloat16)]
    concatenate x2, local copies, waits for them, and re-layouts: 1.37 us -> 3.01 us  [both_scans(): jnp.concatenate([total_fwd, total_bwd, high[:, None], low[:, None], pad],...]
    unnamed x141 -> x117, local copies, waits for them, and re-layouts: 4.31 us -> 4.39 us
  transfers between devices with their start and end apart: 21 -> 21, of which waited for: 10 -> 10; matrix products, arithmetic and copies ran while one was open for 15% -> 13% of each run, Pallas kernels for 0% -> 0%
where the time goes in v14:
time: 153 us; the launch traced here: 152 us
  waiting for transfers between devices  62.9 us (41%)
  starting transfers between devices  26.5 us (17%)
  local copies, waits for them, and re-layouts  20.2 us (13%)
  matrix products  20.2 us (13%)
  other arithmetic  19.4 us (13%)
  between operations  2.85 us (2%)
    ppermute x2, waiting for transfers between devices, both_scans(): got = lax.ppermute(payload, axis, [(i, i ^ distance) for i in range(size)])  25.1 us
    ppermute x14, starting transfers between devices, rotated(): return lax.ppermute(block, axis, route)  20 us
    ppermute x14, waiting for transfers between devices, rotated(): return lax.ppermute(block, axis, route)  17.9 us
    ppermute x1, waiting for transfers between devices, both_scans(): got = lax.ppermute(last, axis, [(i, i ^ distance) for i in range(size)])  11.9 us
    ppermute x2, waiting for transfers between devices, shifted(): return lax.ppermute(block, axis, route)  7.7 us
    dot_general x5, matrix products, contract(): return jnp.einsum(spec, left, right, preferred_element_type=jnp.float32)  6.89 us
    ppermute x2, starting transfers between devices, shifted(): return lax.ppermute(block, axis, route)  5.6 us
    unnamed x117, local copies, waits for them, and re-layouts  4.39 us
  transfers between devices with their start and end apart: 21, of which 10 were waited for; matrix products, arithmetic and copies ran while one was open for 13% of the time, Pallas kernels for 0%

profile of v14, /device:TPU:4, one launch (start us, length us, event | category | flops | bytes accessed | tf_op | source)
XLA Modules:
  0.0 152.1 jit_solution(15214221387423111491)
XLA Ops:
  0.7 1.6 %collective-permute-start = (bf16[32,1792]{1,0:T(8,128)(2,1)}, bf16[32,1792]{1,0:T(8,128)(2,1)S(1)}, u32[]{:S(2)}, u32[]{:S(2)}) collective-permute-start(bf16[32,1792]{1,0:T(8,128)(2,1)} %bitcast.346), channel_id=1, source_target_pairs={{0,2},{2,4},{4,6},{6,8},{8,10},{10,12},{12,14},{14,0},{1,3},{3,5},... | collective-permute-start | bytes 344072 | tf_op jit(solution)/shard_map/ppermute | solution.py:18
  2.2 1.6 %collective-permute-start.1 = (bf16[32,1792]{1,0:T(8,128)(2,1)}, bf16[32,1792]{1,0:T(8,128)(2,1)S(1)}, u32[]{:S(2)}, u32[]{:S(2)}) collective-permute-start(bf16[32,1792]{1,0:T(8,128)(2,1)} %bitcast.347), channel_id=1, source_target_pairs={{0,4},{2,6},{4,8},{6,10},{8,12},{10,14},{12,0},{14,2},{1,5},{3,7},... | collective-permute-start | bytes 344072 | tf_op jit(solution)/shard_map/ppermute | solution.py:18
  3.8 2.5 %collective-permute-start.2 = (bf16[32,1792]{1,0:T(8,128)(2,1)}, bf16[32,1792]{1,0:T(8,128)(2,1)S(1)}, u32[]{:S(2)}, u32[]{:S(2)}) collective-permute-start(bf16[32,1792]{1,0:T(8,128)(2,1)} %bitcast.348), channel_id=1, source_target_pairs={{0,6},{2,8},{4,10},{6,12},{8,14},{10,0},{12,2},{14,4},{1,7},{3,9},... | collective-permute-start | bytes 344072 | tf_op jit(solution)/shard_map/ppermute | solution.py:18
  6.7 1.2 slice.177
  7.9 4.3 %collective-permute-start.8 = (s32[1]{0:T(128)}, s32[1]{0:T(128)}, u32[]{:S(2)}, u32[]{:S(2)}) collective-permute-start(s32[1]{0:T(128)} %bitcast.13), channel_id=1, source_target_pairs={{0,2},{2,4},{4,6},{6,8},{8,10},{10,12},{12,14},{1,3},{3,5},{5,7},{... | collective-permute-start | bytes 20 | tf_op jit(solution)/shard_map/ppermute | solution.py:12
  12.2 0.9 constant_dynamic-update-slice_fusion.7
  14.6 1.3 copy.66
  16.8 1.0 convert.61
  18.6 1.3 collective-permute-start.4
  19.9 1.2 broadcast_compare_fusion.1
  22.9 3.2 %collective-permute-start.5 = (bf16[32,1792]{1,0:T(8,128)(2,1)S(1)}, bf16[32,1792]{1,0:T(8,128)(2,1)S(1)}, u32[]{:S(2)}, u32[]{:S(2)}) collective-permute-start(bf16[32,1792]{1,0:T(8,128)(2,1)S(1)} %bitcast.351), channel_id=1, source_target_pairs={{0,12},{2,14},{4,0},{6,2},{8,4},{10,6},{12,8},{14,10},{1,13},{3,15... | collective-permute-start | bytes 344072 | tf_op jit(solution)/shard_map/ppermute | solution.py:18
  26.3 1.1 collective-permute-done.4
  27.4 1.1 collective-permute-done.5
  28.5 3.4 %collective-permute-done.6 = bf16[32,1792]{1,0:T(8,128)(2,1)S(1)} collective-permute-done((bf16[32,1792]{1,0:T(8,128)(2,1)S(1)}, bf16[32,1792]{1,0:T(8,128)(2,1)S(1)}, u32[]{:S(2)}, u32[]{:S(2)}) %collective-permute-start.6) | collective-permute-done | bytes 114720 | tf_op jit(solution)/shard_map/ppermute | solution.py:18
  34.4 1.3 copy.71
  35.7 1.5 reshape.286
  37.2 1.4 fusion.33
  38.6 1.5 reshape.285
  40.2 1.1 concatenate.64
  41.4 2.1 %multiply_reduce_fusion.3 = f32[28]{0:T(128)} fusion(f32[128,28,64]{0,2,1:T(8,128)} %convert.61, bf16[128,28,64]{0,2,1:T(8,128)(2,1)S(1)} %bitcast.325), kind=kLoop, calls=%fused_computation.45 | loop fusion | flops 688100 | bytes 1376368 | tf_op jit(solution)/shard_map/transpose(jvp())/reduce_sum | solution.py:88
  44.6 1.9 %fusion.12 = (f32[28,128]{1,0:T(8,128)S(1)}, f32[28,128]{1,0:T(8,128)S(1)}, f32[28,128]{1,0:T(8,128)S(1)}, bf16[128,128]{1,0:T(8,128)(2,1)S(1)}) fusion(f32[28,128]{1,0:T(8,128)S(1)} %fusion.133, f32[128,128]{1,0:T(8,128)S(1)} %fusion.112, f32[128,128]{1,0:T(8,128)S(1)} %copy-done.16, f32[28,128]{1,0:T(8,128)S(1)} %fusion.84, ...), kind=kOutput, calls=%fused_computation.18 | convolution fusion | flops 66033152 | bytes 1628160 | tf_op jit(solution)/shard_map/transpose(jvp(hts,shp->thp))/dot_general | solution.py:33
  50.2 1.7 %fusion.17 = bf16[128,28,64]{0,2,1:T(8,128)(2,1)} fusion(f32[128,28,64]{0,2,1:T(8,128)S(1)} %copy-done.2, f32[28,128]{1,0:T(8,128)S(1)} %fusion.133, f32[128,128]{1,0:T(8,128)S(1)} %fusion.112, f32[128,128]{1,0:T(8,128)S(1)} %copy-done.16, f32[28,128]{1,0:T(8,128)S(1)} %fusion.84, pred[128,128]{1,0:T(8,128)(4,1)S(1)} %copy-done.23, ...), kind=kOutput, calls=%fused_computation.27 | convolution fusion | flops 63078400 | bytes 1574000 | tf_op jit(solution)/shard_map/transpose(jvp(hts,shp->thp))/dot_general | solution.py:33
  51.9 11.4 %collective-permute-done.9 = bf16[28,8320]{1,0:T(8,128)(2,1)S(1)} collective-permute-done((bf16[28,8320]{1,0:T(8,128)(2,1)S(1)}, bf16[28,8320]{1,0:T(8,128)(2,1)S(1)}, u32[]{:S(2)}, u32[]{:S(2)}) %collective-permute-start.9) | collective-permute-done | bytes 465952 | tf_op jit(solution)/shard_map/ppermute | solution.py:148
  64.0 1.1 fusion.134
  65.1 1.9 %concatenate.65 = bf16[28,8320]{1,0:T(8,128)(2,1)} concatenate(bf16[28,4096]{1,0:T(8,128)(2,1)} %get-tuple-element.87, bf16[28,4096]{1,0:T(8,128)(2,1)} %get-tuple-element.86, bf16[28,1]{1,0:T(8,128)(2,1)S(1)} %get-tuple-element.72, bf16[28,1]{1,0:T(8,128)(2,1)S(1)} %get-tuple-element.71, bf16[28,126]{1,0:T(8,128)(2,1)S(1)} %broadcast.164), dimensions={1} | concatenate | bytes 931840 | tf_op jit(solution)/shard_map/concatenate | solution.py:141
  67.0 13.7 %collective-permute-done.10 = bf16[28,8320]{1,0:T(8,128)(2,1)} collective-permute-done((bf16[28,8320]{1,0:T(8,128)(2,1)}, bf16[28,8320]{1,0:T(8,128)(2,1)}, u32[]{:S(2)}, u32[]{:S(2)}) %collective-permute-start.10) | collective-permute-done | bytes 465952 | tf_op jit(solution)/shard_map/ppermute | solution.py:148
  80.7 1.5 %subtract_convert_fusion = (bf16[28,1]{1,0:T(8,128)(2,1)S(1)}, bf16[28,1]{1,0:T(8,128)(2,1)S(1)}, f32[28]{0:T(128)S(1)}, f32[28]{0:T(128)}, f32[28]{0:T(128)}) fusion(f32[28,1]{1,0:T(8,128)S(1)} %get-tuple-element.92, bf16[28,8320]{1,0:T(8,128)(2,1)} %collective-permute-done.10, bf16[28,8320]{1,0:T(8,128)(2,1)S(1)} %collective-permute-done.9, pred[]{:T(512)S(6)} %eq.84, ...), kind=kLoop, calls=%fused_computation.220 | loop fusion | flops 476 | bytes 786 | tf_op jit(solution)/shard_map/convert.14
  82.3 2.3 %fusion.41 = bf16[28,4096]{1,0:T(8,128)(2,1)} fusion(f32[28]{0:T(128)S(1)} %get-tuple-element.91, f32[28]{0:T(128)S(1)} %get-tuple-element.88, pred[]{:T(512)S(6)} %eq.83, pred[]{:T(512)S(6)} %eq.82, bf16[28,8320]{1,0:T(8,128)(2,1)} %collective-permute-done.10, f32[28,4096]{1,0:T(8,128)S(1)} %reshape.286, f32[28]{0:T(128)S(1)} %copy-done.40, ...), kind=kLoop, calls=%fused_computation.83 | loop fusion | flops 2981888 | bytes 2064835 | tf_op jit(solution)/shard_map/convert_element_type | solution.py:151
  84.5 1.0 concatenate.66
  86.3 1.0 bitcast_multiply_fusion
  87.3 11.9 %collective-permute-done.11 = bf16[28,4224]{1,0:T(8,128)(2,1)S(1)} collective-permute-done((bf16[28,4224]{1,0:T(8,128)(2,1)S(1)}, bf16[28,4224]{1,0:T(8,128)(2,1)S(1)}, u32[]{:S(2)}, u32[]{:S(2)}) %collective-permute-start.11) | collective-permute-done | bytes 236576 | tf_op jit(solution)/shard_map/ppermute | solution.py:153
  99.9 2.2 %multiply_reduce_fusion.4 = (f32[28]{0:T(128)}, f32[28,4096]{1,0:T(8,128)S(1)}, bf16[28,4096]{1,0:T(8,128)(2,1)S(1)}) fusion(bf16[28,4224]{1,0:T(8,128)(2,1)} %copy-done.11, f32[28]{0:T(128)} %get-tuple-element.90, bf16[28,8320]{1,0:T(8,128)(2,1)} %collective-permute-done.10, f32[28]{0:T(128)} %get-tuple-element.52, ...), kind=kLoop, calls=%fused_computation.86 | loop fusion | flops 2523108 | bytes 1835571 | tf_op jit(solution)/shard_map/reduce_sum | solution.py:261
  102.4 1.3 copy.75
  103.7 1.7 %fusion.108 = f32[128,1792]{0,1:S(1)} fusion(f32[64,1792]{0,1:T(8,128)} %bitcast.332, bf16[128,128]{0,1:T(8,128)(2,1)S(1)} %copy-done.4), kind=kOutput, calls=%fused_computation.232 | convolution fusion | flops 176160768 | bytes 1392640
  107.1 0.9 multiply_reduce_fusion.6
  109.0 0.8 fusion.154
  110.1 2.2 %fusion.21 = bf16[128,64]{0,1:T(8,128)(2,1)S(1)} fusion(f32[128,28,64]{0,2,1:T(8,128)} %bitcast.333, f32[28,64,64]{2,1,0:T(8,128)S(1)} %reshape.287), kind=kOutput, calls=%fused_computation.32 | convolution fusion | flops 176168960 | bytes 1392640 | tf_op jit(solution)/shard_map/transpose(jvp(tn,hnp->thp))/dot_general | solution.py:97
  112.5 1.6 %fusion.22 = f32[128,28,64]{0,2,1:T(8,128)S(1)} fusion(bf16[128,28,64]{0,2,1:T(8,128)(2,1)} %fusion.17, bf16[28,64,64]{2,1,0:T(8,128)(2,1)S(1)} %reshape.288, f32[28,128]{1,0:T(8,128)S(1)} %copy.82, f32[28,64]{1,0:T(8,128)S(1)} %copy-done.21, f32[28,128]{1,0:T(8,128)S(1)} %copy.77, f32[128,64]{0,1:T(8,128)S(1)} %copy-done.13, f32[128,28]{0,1:T(8,128)S(1)} %copy.69), kind=kOutput, calls=%fused_computation.37 | convolution fusion | flops 32112640 | bytes 1688576 | tf_op jit(solution)/shard_map/transpose(jvp(thn,thp->hnp))/dot_general | solution.py:33
  114.5 1.8 %fusion.148 = (bf16[256,1792]{1,0:T(8,128)(2,1)S(1)}, f32[256,1792]{1,0:T(8,128)}) fusion(bf16[1,128,1792]{2,1,0:T(8,128)(2,1)S(1)} %copy-done.1, s32[]{:T(128)S(6)} %select_n.220, bf16[128,256]{0,1:T(8,128)(2,1)S(1)} %maximum_select_fusion), kind=kOutput, calls=%fused_computation.299 | convolution fusion | flops 118030336 | bytes 3276804 | tf_op jit(solution)/shard_map/dot_general | solution.py:281
  116.5 1.0 collective-permute-start.20
  117.5 1.8 %collective-permute-start.19 = (bf16[32,1920]{1,0:T(8,128)(2,1)S(1)}, bf16[32,1920]{1,0:T(8,128)(2,1)S(1)}, u32[]{:S(2)}, u32[]{:S(2)}) collective-permute-start(bf16[32,1920]{1,0:T(8,128)(2,1)S(1)} %get-tuple-element.103), channel_id=1, source_target_pairs={{0,12},{2,14},{4,0},{6,2},{8,4},{10,6},{12,8},{14,10},{1,13},{3,15... | collective-permute-start | bytes 368648 | tf_op jit(solution)/shard_map/ppermute | solution.py:18
  119.4 3.4 %collective-permute-start.17 = (bf16[32,1920]{1,0:T(8,128)(2,1)S(1)}, bf16[32,1920]{1,0:T(8,128)(2,1)S(1)}, u32[]{:S(2)}, u32[]{:S(2)}) collective-permute-start(bf16[32,1920]{1,0:T(8,128)(2,1)S(1)} %get-tuple-element.101), channel_id=1, source_target_pairs={{0,8},{2,10},{4,12},{6,14},{8,0},{10,2},{12,4},{14,6},{1,9},{3,11}... | collective-permute-start | bytes 368648 | tf_op jit(solution)/shard_map/ppermute | solution.py:18
  123.8 1.1 collective-permute-start.15
  124.9 1.6 %collective-permute-start.14 = (bf16[32,1920]{1,0:T(8,128)(2,1)S(1)}, bf16[32,1920]{1,0:T(8,128)(2,1)S(1)}, u32[]{:S(2)}, u32[]{:S(2)}) collective-permute-start(bf16[32,1920]{1,0:T(8,128)(2,1)S(1)} %get-tuple-element.98), channel_id=1, source_target_pairs={{0,2},{2,4},{4,6},{6,8},{8,10},{10,12},{12,14},{14,0},{1,3},{3,5},... | collective-permute-start | bytes 368648 | tf_op jit(solution)/shard_map/ppermute | solution.py:18
  126.5 11.7 %collective-permute-done.18 = bf16[32,1920]{1,0:T(8,128)(2,1)S(1)} collective-permute-done((bf16[32,1920]{1,0:T(8,128)(2,1)S(1)}, bf16[32,1920]{1,0:T(8,128)(2,1)S(1)}, u32[]{:S(2)}, u32[]{:S(2)}) %collective-permute-start.18) | collective-permute-done | bytes 122912 | tf_op jit(solution)/shard_map/ppermute | solution.py:18
  138.2 1.3 collective-permute-start.13
  141.8 1.7 %fusion.61 = f32[1,32,1792]{2,1,0:T(8,128)} fusion(f32[256,1792]{1,0:T(8,128)} %get-tuple-element.116, bf16[32,1920]{1,0:T(8,128)(2,1)S(1)} %collective-permute-done.20, bf16[32,1920]{1,0:T(8,128)(2,1)S(1)} %collective-permute-done.19, bf16[32,1920]{1,0:T(8,128)(2,1)S(1)} %collective-permute-done.18, bf16[32,1920]{1,0:T(8,128)(2,1)S(1)} %collective-permute-done.17, ...), kind=kLoop, calls=%fused_computation.116 | loop fusion | flops 802816 | bytes 1261568 | tf_op jit(solution)/shard_map/broadcast_in_dim | solution.py:323
  143.6 7.7 %collective-permute-done.13 = bf16[1,128,1792]{2,1,0:T(8,128)(2,1)S(1)} collective-permute-done((bf16[1,128,1792]{2,1,0:T(8,128)(2,1)S(1)}, bf16[1,128,1792]{2,1,0:T(8,128)(2,1)S(1)}, u32[]{:S(2)}, u32[]{:S(2)}) %collective-permute-start.13) | collective-permute-done | bytes 458784 | tf_op jit(solution)/shard_map/ppermute | solution.py:12
  (214 shorter events, 21.1 us)
Async XLA Ops:
  0.6 15.9 %copy-start.35 = (f32[1,28]{1,0:T(1,128)S(1)}, f32[1,28]{1,0:T(1,128)}, u32[]{:S(2)}) copy-start(f32[1,28]{1,0:T(1,128)} %param.15) | copy-start | bytes 340
  0.6 15.9 %copy-start.10 = (bf16[1,128,1792]{2,1,0:T(8,128)(2,1)S(1)}, bf16[1,128,1792]{2,1,0:T(8,128)(2,1)}, u32[]{:S(2)}) copy-start(bf16[1,128,1792]{2,1,0:T(8,128)(2,1)} %param.11) | copy-start | bytes 1376260
  0.7 22.2 %collective-permute-start = (bf16[32,1792]{1,0:T(8,128)(2,1)}, bf16[32,1792]{1,0:T(8,128)(2,1)S(1)}, u32[]{:S(2)}, u32[]{:S(2)}) collective-permute-start(bf16[32,1792]{1,0:T(8,128)(2,1)} %bitcast.346), channel_id=1, source_target_pairs={{0,2},{2,4},{4,6},{6,8},{8,10},{10,12},{12,14},{14,0},{1,3},{3,5},... | collective-permute-start | bytes 344072 | tf_op jit(solution)/shard_map/ppermute | solution.py:18
  2.2 23.9 %collective-permute-start.1 = (bf16[32,1792]{1,0:T(8,128)(2,1)}, bf16[32,1792]{1,0:T(8,128)(2,1)S(1)}, u32[]{:S(2)}, u32[]{:S(2)}) collective-permute-start(bf16[32,1792]{1,0:T(8,128)(2,1)} %bitcast.347), channel_id=1, source_target_pairs={{0,4},{2,6},{4,8},{6,10},{8,12},{10,14},{12,0},{14,2},{1,5},{3,7},... | collective-permute-start | bytes 344072 | tf_op jit(solution)/shard_map/ppermute | solution.py:18
  3.8 22.4 %collective-permute-start.2 = (bf16[32,1792]{1,0:T(8,128)(2,1)}, bf16[32,1792]{1,0:T(8,128)(2,1)S(1)}, u32[]{:S(2)}, u32[]{:S(2)}) collective-permute-start(bf16[32,1792]{1,0:T(8,128)(2,1)} %bitcast.348), channel_id=1, source_target_pairs={{0,6},{2,8},{4,10},{6,12},{8,14},{10,0},{12,2},{14,4},{1,7},{3,9},... | collective-permute-start | bytes 344072 | tf_op jit(solution)/shard_map/ppermute | solution.py:18
  6.3 19.9 %collective-permute-start.3 = (bf16[32,1792]{1,0:T(8,128)(2,1)}, bf16[32,1792]{1,0:T(8,128)(2,1)S(1)}, u32[]{:S(2)}, u32[]{:S(2)}) collective-permute-start(bf16[32,1792]{1,0:T(8,128)(2,1)} %bitcast.349), channel_id=1, source_target_pairs={{0,8},{2,10},{4,12},{6,14},{8,0},{10,2},{12,4},{14,6},{1,9},{3,11}... | collective-permute-start | bytes 344072 | tf_op jit(solution)/shard_map/ppermute | solution.py:18
  7.9 10.7 %collective-permute-start.8 = (s32[1]{0:T(128)}, s32[1]{0:T(128)}, u32[]{:S(2)}, u32[]{:S(2)}) collective-permute-start(s32[1]{0:T(128)} %bitcast.13), channel_id=1, source_target_pairs={{0,2},{2,4},{4,6},{6,8},{8,10},{10,12},{12,14},{1,3},{3,5},{5,7},{... | collective-permute-start | bytes 20 | tf_op jit(solution)/shard_map/ppermute | solution.py:12
  14.6 4.0 %copy-start.15 = (bf16[1,32,1792]{2,1,0:T(8,128)(2,1)S(1)}, bf16[1,32,1792]{2,1,0:T(8,128)(2,1)}, u32[]{:S(2)}) copy-start(bf16[1,32,1792]{2,1,0:T(8,128)(2,1)} %param.12) | copy-start | bytes 344068
  14.6 7.7 %copy-start.24 = (f32[1,28]{1,0:T(1,128)S(1)}, f32[1,28]{1,0:T(1,128)}, u32[]{:S(2)}) copy-start(f32[1,28]{1,0:T(1,128)} %param.14) | copy-start | bytes 340
  16.5 9.8 %copy-start.7 = (f32[28,1,128]{0,2,1:T(8,128)}, f32[28,1,128]{0,2,1:T(8,128)S(1)}, u32[]{:S(2)}) copy-start(f32[28,1,128]{0,2,1:T(8,128)S(1)} %copy.87) | copy-start | bytes 43012
  16.6 6.0 %copy-start.45 = (f32[28]{0:T(128)}, f32[28]{0:T(128)S(1)}, u32[]{:S(2)}) copy-start(f32[28]{0:T(128)S(1)} %negate_bitcast_fusion) | copy-start | bytes 340
  16.8 15.1 %copy-start = (bf16[1,128,1792]{2,1,0:T(8,128)(2,1)S(1)}, bf16[1,128,1792]{2,1,0:T(8,128)(2,1)}, u32[]{:S(2)}) copy-start(bf16[1,128,1792]{2,1,0:T(8,128)(2,1)} %param.9) | copy-start | bytes 1376260
  18.6 8.8 %collective-permute-start.4 = (bf16[32,1792]{1,0:T(8,128)(2,1)S(1)}, bf16[32,1792]{1,0:T(8,128)(2,1)S(1)}, u32[]{:S(2)}, u32[]{:S(2)}) collective-permute-start(bf16[32,1792]{1,0:T(8,128)(2,1)S(1)} %bitcast.350), channel_id=1, source_target_pairs={{0,10},{2,12},{4,14},{6,0},{8,2},{10,4},{12,6},{14,8},{1,11},{3,13... | collective-permute-start | bytes 344072 | tf_op jit(solution)/shard_map/ppermute | solution.py:18
  21.1 10.8 %copy-start.27 = (pred[128]{0:T(512)(128)(4,1)}, pred[128]{0:T(512)(128)(4,1)S(1)}, u32[]{:S(2)}) copy-start(pred[128]{0:T(512)(128)(4,1)S(1)} %get-tuple-element.77) | copy-start | bytes 388
  21.1 10.8 %copy-start.29 = (f32[128]{0:T(128)}, f32[128]{0:T(128)S(1)}, u32[]{:S(2)}) copy-start(f32[128]{0:T(128)S(1)} %get-tuple-element.78) | copy-start | bytes 1540
  22.6 9.3 %copy-start.18 = (f32[128,28]{0,1:T(8,128)}, f32[128,28]{0,1:T(8,128)S(1)}, u32[]{:S(2)}) copy-start(f32[128,28]{0,1:T(8,128)S(1)} %get-tuple-element.114) | copy-start | bytes 43012
  22.7 9.8 %copy-start.5 = (f32[128,28]{1,0:T(8,128)}, f32[128,28]{1,0:T(8,128)S(1)}, u32[]{:S(2)}) copy-start(f32[128,28]{1,0:T(8,128)S(1)} %copy.67) | copy-start | bytes 43012
  22.7 9.2 %copy-start.33 = (f32[28]{0:T(128)}, f32[28]{0:T(128)S(1)}, u32[]{:S(2)}) copy-start(f32[28]{0:T(128)S(1)} %slice_bitcast_fusion.7) | copy-start | bytes 340
  22.9 5.6 %collective-permute-start.5 = (bf16[32,1792]{1,0:T(8,128)(2,1)S(1)}, bf16[32,1792]{1,0:T(8,128)(2,1)S(1)}, u32[]{:S(2)}, u32[]{:S(2)}) collective-permute-start(bf16[32,1792]{1,0:T(8,128)(2,1)S(1)} %bitcast.351), channel_id=1, source_target_pairs={{0,12},{2,14},{4,0},{6,2},{8,4},{10,6},{12,8},{14,10},{1,13},{3,15... | collective-permute-start | bytes 344072 | tf_op jit(solution)/shard_map/ppermute | solution.py:18
  26.2 5.7 %collective-permute-start.6 = (bf16[32,1792]{1,0:T(8,128)(2,1)S(1)}, bf16[32,1792]{1,0:T(8,128)(2,1)S(1)}, u32[]{:S(2)}, u32[]{:S(2)}) collective-permute-start(bf16[32,1792]{1,0:T(8,128)(2,1)S(1)} %bitcast.352), channel_id=1, source_target_pairs={{0,14},{2,0},{4,2},{6,4},{8,6},{10,8},{12,10},{14,12},{1,15},{3,1}... | collective-permute-start | bytes 344072 | tf_op jit(solution)/shard_map/ppermute | solution.py:18
  32.4 1.3 collective-permute-start.7
  33.8 12.9 %copy-start.3 = (bf16[128,128]{0,1:T(8,128)(2,1)}, bf16[128,128]{0,1:T(8,128)(2,1)S(1)}, u32[]{:S(2)}) copy-start(bf16[128,128]{0,1:T(8,128)(2,1)S(1)} %fusion.71) | copy-start | bytes 98308
  40.1 3.8 %copy-start.36 = (f32[1,28]{1,0:T(1,128)S(1)}, f32[1,28]{1,0:T(1,128)}, u32[]{:S(2)}) copy-start(f32[1,28]{1,0:T(1,128)} %param.15) | copy-start | bytes 340
  40.1 3.8 %copy-start.25 = (f32[1,28]{1,0:T(1,128)S(1)}, f32[1,28]{1,0:T(1,128)}, u32[]{:S(2)}) copy-start(f32[1,28]{1,0:T(1,128)} %param.14) | copy-start | bytes 340
  40.2 4.4 %copy-start.22 = (pred[128,128]{1,0:T(8,128)(4,1)S(1)}, pred[128,128]{1,0:T(8,128)(4,1)}, u32[]{:S(2)}) copy-start(pred[128,128]{1,0:T(8,128)(4,1)} %get-tuple-element.110) | copy-start | bytes 49156
  44.5 4.5 %copy-start.9 = (bf16[28,8320]{1,0:T(8,128)(2,1)S(1)}, bf16[28,8320]{1,0:T(8,128)(2,1)}, u32[]{:S(2)}) copy-start(bf16[28,8320]{1,0:T(8,128)(2,1)} %concatenate.64) | copy-start | bytes 1397764
  44.6 5.1 %copy-start.37 = (f32[1,28]{1,0:T(1,128)S(1)}, f32[1,28]{1,0:T(1,128)}, u32[]{:S(2)}) copy-start(f32[1,28]{1,0:T(1,128)} %param.15) | copy-start | bytes 340
  44.6 5.1 %copy-start.42 = (f32[1,28]{1,0:T(1,128)S(1)}, f32[1,28]{1,0:T(1,128)}, u32[]{:S(2)}) copy-start(f32[1,28]{1,0:T(1,128)} %param.16) | copy-start | bytes 340
  44.6 5.6 %copy-start.23 = (pred[128,128]{1,0:T(8,128)(4,1)S(1)}, pred[128,128]{1,0:T(8,128)(4,1)}, u32[]{:S(2)}) copy-start(pred[128,128]{1,0:T(8,128)(4,1)} %get-tuple-element.110) | copy-start | bytes 49156
  49.0 14.2 %collective-permute-start.9 = (bf16[28,8320]{1,0:T(8,128)(2,1)S(1)}, bf16[28,8320]{1,0:T(8,128)(2,1)S(1)}, u32[]{:S(2)}, u32[]{:S(2)}) collective-permute-start(bf16[28,8320]{1,0:T(8,128)(2,1)S(1)} %copy-done.9), channel_id=1, source_target_pairs={{0,2},{2,0},{4,6},{6,4},{8,10},{10,8},{12,14},{14,12},{1,3},{3,1},... | collective-permute-start | bytes 1397768 | tf_op jit(solution)/shard_map/ppermute | solution.py:148
  50.2 13.8 %copy-start.40 = (f32[28]{0:T(128)S(1)}, f32[28]{0:T(128)}, u32[]{:S(2)}) copy-start(f32[28]{0:T(128)} %exponential_multiply_fusion.1) | copy-start | bytes 340
  67.0 13.7 %collective-permute-start.10 = (bf16[28,8320]{1,0:T(8,128)(2,1)}, bf16[28,8320]{1,0:T(8,128)(2,1)}, u32[]{:S(2)}, u32[]{:S(2)}) collective-permute-start(bf16[28,8320]{1,0:T(8,128)(2,1)} %concatenate.65), channel_id=1, source_target_pairs={{0,4},{2,6},{4,0},{6,2},{8,12},{10,14},{12,8},{14,10},{1,5},{3,7},... | collective-permute-start | bytes 1397768 | tf_op jit(solution)/shard_map/ppermute | solution.py:148
  85.6 13.6 %collective-permute-start.11 = (bf16[28,4224]{1,0:T(8,128)(2,1)S(1)}, bf16[28,4224]{1,0:T(8,128)(2,1)S(1)}, u32[]{:S(2)}, u32[]{:S(2)}) collective-permute-start(bf16[28,4224]{1,0:T(8,128)(2,1)S(1)} %concatenate.66), channel_id=1, source_target_pairs={{0,8},{2,10},{4,12},{6,14},{8,0},{10,2},{12,4},{14,6},{1,9},{3,11}... | collective-permute-start | bytes 709640 | tf_op jit(solution)/shard_map/ppermute | solution.py:153
  106.2 3.8 %copy-start.38 = (f32[1,28]{1,0:T(1,128)S(1)}, f32[1,28]{1,0:T(1,128)}, u32[]{:S(2)}) copy-start(f32[1,28]{1,0:T(1,128)} %param.15) | copy-start | bytes 340
  106.2 3.7 %copy-start.39 = (f32[28]{0:T(128)S(1)}, f32[28]{0:T(128)}, u32[]{:S(2)}) copy-start(f32[28]{0:T(128)} %get-tuple-element.42) | copy-start | bytes 340
  106.2 3.7 %copy-start.44 = (f32[28]{0:T(128)S(1)}, f32[28]{0:T(128)}, u32[]{:S(2)}) copy-start(f32[28]{0:T(128)} %get-tuple-element.41) | copy-start | bytes 340
  106.2 3.8 %copy-start.32 = (f32[28]{0:T(128)S(1)}, f32[28]{0:T(128)}, u32[]{:S(2)}) copy-start(f32[28]{0:T(128)} %multiply_reduce_fusion.3) | copy-start | bytes 340
  107.1 5.1 %copy-start.14 = (bf16[128,128]{0,1:T(8,128)(2,1)S(1)}, bf16[128,128]{0,1:T(8,128)(2,1)}, u32[]{:S(2)}) copy-start(bf16[128,128]{0,1:T(8,128)(2,1)} %pad_add_fusion) | copy-start | bytes 98308
  108.0 4.5 %copy-start.21 = (f32[28,64]{1,0:T(8,128)S(1)}, f32[28,64]{1,0:T(8,128)}, u32[]{:S(2)}) copy-start(f32[28,64]{1,0:T(8,128)} %reshape_squeeze.7) | copy-start | bytes 21508
  112.3 2.2 %collective-permute-start.12 = (bf16[128,128]{0,1:T(8,128)(2,1)S(1)}, bf16[128,128]{0,1:T(8,128)(2,1)S(1)}, u32[]{:S(2)}, u32[]{:S(2)}) collective-permute-start(bf16[128,128]{0,1:T(8,128)(2,1)S(1)} %add_convert_fusion), channel_id=1, source_target_pairs={{0,1},{1,0},{2,3},{3,2},{4,5},{5,4},{6,7},{7,6},{8,9},{9,8},{10,11... | collective-permute-start | bytes 98312 | tf_op jit(solution)/shard_map/ppermute | solution.py:29
  116.5 7.2 %collective-permute-start.20 = (bf16[32,1920]{1,0:T(8,128)(2,1)S(1)}, bf16[32,1920]{1,0:T(8,128)(2,1)S(1)}, u32[]{:S(2)}, u32[]{:S(2)}) collective-permute-start(bf16[32,1920]{1,0:T(8,128)(2,1)S(1)} %get-tuple-element.104), channel_id=1, source_target_pairs={{0,14},{2,0},{4,2},{6,4},{8,6},{10,8},{12,10},{14,12},{1,15},{3,1}... | collective-permute-start | bytes 368648 | tf_op jit(solution)/shard_map/ppermute | solution.py:18
  117.5 7.4 %collective-permute-start.19 = (bf16[32,1920]{1,0:T(8,128)(2,1)S(1)}, bf16[32,1920]{1,0:T(8,128)(2,1)S(1)}, u32[]{:S(2)}, u32[]{:S(2)}) collective-permute-start(bf16[32,1920]{1,0:T(8,128)(2,1)S(1)} %get-tuple-element.103), channel_id=1, source_target_pairs={{0,12},{2,14},{4,0},{6,2},{8,4},{10,6},{12,8},{14,10},{1,13},{3,15... | collective-permute-start | bytes 368648 | tf_op jit(solution)/shard_map/ppermute | solution.py:18
  119.4 18.8 %collective-permute-start.18 = (bf16[32,1920]{1,0:T(8,128)(2,1)S(1)}, bf16[32,1920]{1,0:T(8,128)(2,1)S(1)}, u32[]{:S(2)}, u32[]{:S(2)}) collective-permute-start(bf16[32,1920]{1,0:T(8,128)(2,1)S(1)} %get-tuple-element.102), channel_id=1, source_target_pairs={{0,10},{2,12},{4,14},{6,0},{8,2},{10,4},{12,6},{14,8},{1,11},{3,13... | collective-permute-start | bytes 368648 | tf_op jit(solution)/shard_map/ppermute | solution.py:18
  119.4 20.7 %collective-permute-start.17 = (bf16[32,1920]{1,0:T(8,128)(2,1)S(1)}, bf16[32,1920]{1,0:T(8,128)(2,1)S(1)}, u32[]{:S(2)}, u32[]{:S(2)}) collective-permute-start(bf16[32,1920]{1,0:T(8,128)(2,1)S(1)} %get-tuple-element.101), channel_id=1, source_target_pairs={{0,8},{2,10},{4,12},{6,14},{8,0},{10,2},{12,4},{14,6},{1,9},{3,11}... | collective-permute-start | bytes 368648 | tf_op jit(solution)/shard_map/ppermute | solution.py:18
  122.8 17.3 %collective-permute-start.16 = (bf16[32,1920]{1,0:T(8,128)(2,1)S(1)}, bf16[32,1920]{1,0:T(8,128)(2,1)S(1)}, u32[]{:S(2)}, u32[]{:S(2)}) collective-permute-start(bf16[32,1920]{1,0:T(8,128)(2,1)S(1)} %get-tuple-element.100), channel_id=1, source_target_pairs={{0,6},{2,8},{4,10},{6,12},{8,14},{10,0},{12,2},{14,4},{1,7},{3,9},... | collective-permute-start | bytes 368648 | tf_op jit(solution)/shard_map/ppermute | solution.py:18
  123.8 16.4 %collective-permute-start.15 = (bf16[32,1920]{1,0:T(8,128)(2,1)S(1)}, bf16[32,1920]{1,0:T(8,128)(2,1)S(1)}, u32[]{:S(2)}, u32[]{:S(2)}) collective-permute-start(bf16[32,1920]{1,0:T(8,128)(2,1)S(1)} %get-tuple-element.99), channel_id=1, source_target_pairs={{0,4},{2,6},{4,8},{6,10},{8,12},{10,14},{12,0},{14,2},{1,5},{3,7},... | collective-permute-start | bytes 368648 | tf_op jit(solution)/shard_map/ppermute | solution.py:18
  124.9 15.3 %collective-permute-start.14 = (bf16[32,1920]{1,0:T(8,128)(2,1)S(1)}, bf16[32,1920]{1,0:T(8,128)(2,1)S(1)}, u32[]{:S(2)}, u32[]{:S(2)}) collective-permute-start(bf16[32,1920]{1,0:T(8,128)(2,1)S(1)} %get-tuple-element.98), channel_id=1, source_target_pairs={{0,2},{2,4},{4,6},{6,8},{8,10},{10,12},{12,14},{14,0},{1,3},{3,5},... | collective-permute-start | bytes 368648 | tf_op jit(solution)/shard_map/ppermute | solution.py:18
  138.2 13.1 %collective-permute-start.13 = (bf16[1,128,1792]{2,1,0:T(8,128)(2,1)S(1)}, bf16[1,128,1792]{2,1,0:T(8,128)(2,1)S(1)}, u32[]{:S(2)}, u32[]{:S(2)}) collective-permute-start(bf16[1,128,1792]{2,1,0:T(8,128)(2,1)S(1)} %fusion.1), channel_id=1, source_target_pairs={{16,0},{17,1},{18,2},{19,3},{20,4},{21,5},{22,6},{23,7},{24,8},{25... | collective-permute-start | bytes 1376264 | tf_op jit(solution)/shard_map/ppermute | solution.py:12
  (19 other events, 38.1 us)

commit v15 on v11

--- a/solution.py
+++ b/solution.py
@@ -156,10 +156,10 @@
             got = got.astype(jnp.float32)
             got_fwd = got[:, :width]
             got_bwd = got_fwd
-            got = jnp.concatenate([got[:, :width], got], axis=1)
+        at = 2 * width if distance * 2 < size else width
         if distance == 1:
             got, filler = lax.optimization_barrier((got, filler_fn(*filler_args)))
-        got_decay = got[:, 2 * width] + got[:, 2 * width + 1]
+        got_decay = got[:, at] + got[:, at + 1]
         before = jnp.where(upper, before + before_decay[:, None] * got_fwd, before)
         before_decay = jnp.where(upper, before_decay * got_decay, before_decay)
         after = jnp.where(upper, after, after + after_decay[:, None] * got_bwd)

time: 141 us -> 141 us (level)
  no operation moved by 1% of the time
where the time goes in v15:
time: 141 us; the launch traced here: 140 us
  waiting for transfers between devices  64.2 us (46%)
  starting transfers between devices  26.4 us (19%)
  local copies, waits for them, and re-layouts  16.6 us (12%)
  matrix products  16.6 us (12%)
  other arithmetic  13.4 us (10%)
  between operations  3.28 us (2%)
    ppermute x2, waiting for transfers between devices, both_scans(): got = lax.ppermute(payload, axis, [(i, i ^ distance) for i in range(size)])  26.3 us
    ppermute x14, starting transfers between devices, rotated(): return lax.ppermute(block, axis, route)  19.8 us
    ppermute x14, waiting for transfers between devices, rotated(): return lax.ppermute(block, axis, route)  17.9 us
    ppermute x1, waiting for transfers between devices, both_scans(): got = lax.ppermute(last, axis, [(i, i ^ distance) for i in range(size)])  12.3 us
    ppermute x2, waiting for transfers between devices, shifted(): return lax.ppermute(block, axis, route)  7.67 us
    dot_general x5, matrix products, contract(): return jnp.einsum(spec, left, right, preferred_element_type=jnp.float32)  6.83 us
    ppermute x2, starting transfers between devices, shifted(): return lax.ppermute(block, axis, route)  5.6 us
    unnamed x141, local copies, waits for them, and re-layouts  4.31 us
  transfers between devices with their start and end apart: 21, of which 10 were waited for; matrix products, arithmetic and copies ran while one was open for 15% of the time, Pallas kernels for 0%

profile of v15, /device:TPU:4, one launch (start us, length us, event | category | flops | bytes accessed | tf_op | source)
XLA Modules:
  0.0 140.4 jit_solution(6243420667855408329)
XLA Ops:
  0.7 1.6 %collective-permute-start = (bf16[32,1792]{1,0:T(8,128)(2,1)}, bf16[32,1792]{1,0:T(8,128)(2,1)S(1)}, u32[]{:S(2)}, u32[]{:S(2)}) collective-permute-start(bf16[32,1792]{1,0:T(8,128)(2,1)} %bitcast.346), channel_id=1, source_target_pairs={{0,2},{2,4},{4,6},{6,8},{8,10},{10,12},{12,14},{14,0},{1,3},{3,5},... | collective-permute-start | bytes 344072 | tf_op jit(solution)/shard_map/ppermute | solution.py:18
  2.2 1.6 %collective-permute-start.1 = (bf16[32,1792]{1,0:T(8,128)(2,1)}, bf16[32,1792]{1,0:T(8,128)(2,1)S(1)}, u32[]{:S(2)}, u32[]{:S(2)}) collective-permute-start(bf16[32,1792]{1,0:T(8,128)(2,1)} %bitcast.347), channel_id=1, source_target_pairs={{0,4},{2,6},{4,8},{6,10},{8,12},{10,14},{12,0},{14,2},{1,5},{3,7},... | collective-permute-start | bytes 344072 | tf_op jit(solution)/shard_map/ppermute | solution.py:18
  3.8 2.5 %collective-permute-start.2 = (bf16[32,1792]{1,0:T(8,128)(2,1)}, bf16[32,1792]{1,0:T(8,128)(2,1)S(1)}, u32[]{:S(2)}, u32[]{:S(2)}) collective-permute-start(bf16[32,1792]{1,0:T(8,128)(2,1)} %bitcast.348), channel_id=1, source_target_pairs={{0,6},{2,8},{4,10},{6,12},{8,14},{10,0},{12,2},{14,4},{1,7},{3,9},... | collective-permute-start | bytes 344072 | tf_op jit(solution)/shard_map/ppermute | solution.py:18
  6.7 1.2 slice.179
  7.9 4.3 %collective-permute-start.8 = (s32[1]{0:T(128)}, s32[1]{0:T(128)}, u32[]{:S(2)}, u32[]{:S(2)}) collective-permute-start(s32[1]{0:T(128)} %bitcast.13), channel_id=1, source_target_pairs={{0,2},{2,4},{4,6},{6,8},{8,10},{10,12},{12,14},{1,3},{3,5},{5,7},{... | collective-permute-start | bytes 20 | tf_op jit(solution)/shard_map/ppermute | solution.py:12
  12.2 0.9 constant_dynamic-update-slice_fusion.7
  13.2 0.7 reduce
  14.0 0.7 reshape_squeeze.7
  14.6 1.3 copy.66
  16.8 1.1 convert.62
  17.9 0.7 broadcast_compare_fusion
  18.6 1.3 collective-permute-start.4
  19.9 1.3 broadcast_compare_fusion.1
  23.6 3.1 %collective-permute-start.5 = (bf16[32,1792]{1,0:T(8,128)(2,1)S(1)}, bf16[32,1792]{1,0:T(8,128)(2,1)S(1)}, u32[]{:S(2)}, u32[]{:S(2)}) collective-permute-start(bf16[32,1792]{1,0:T(8,128)(2,1)S(1)} %bitcast.351), channel_id=1, source_target_pairs={{0,12},{2,14},{4,0},{6,2},{8,4},{10,6},{12,8},{14,10},{1,13},{3,15... | collective-permute-start | bytes 344072 | tf_op jit(solution)/shard_map/ppermute | solution.py:18
  27.5 1.6 %collective-permute-done.5 = bf16[32,1792]{1,0:T(8,128)(2,1)S(1)} collective-permute-done((bf16[32,1792]{1,0:T(8,128)(2,1)S(1)}, bf16[32,1792]{1,0:T(8,128)(2,1)S(1)}, u32[]{:S(2)}, u32[]{:S(2)}) %collective-permute-start.5) | collective-permute-done | bytes 114720 | tf_op jit(solution)/shard_map/ppermute | solution.py:18
  29.1 3.4 %collective-permute-done.6 = bf16[32,1792]{1,0:T(8,128)(2,1)S(1)} collective-permute-done((bf16[32,1792]{1,0:T(8,128)(2,1)S(1)}, bf16[32,1792]{1,0:T(8,128)(2,1)S(1)}, u32[]{:S(2)}, u32[]{:S(2)}) %collective-permute-start.6) | collective-permute-done | bytes 114720 | tf_op jit(solution)/shard_map/ppermute | solution.py:18
  33.6 0.7 copy.74
  34.4 0.7 copy.72
  35.1 0.7 copy.73
  37.3 1.2 copy.71
  38.5 1.6 %reshape.286 = f32[28,4096]{1,0:T(8,128)S(1)} reshape(f32[28,64,64]{2,1,0:T(8,128)} %copy.71) | data formatting | bytes 917504 | tf_op jit(solution)/shard_map/reshape | solution.py:243
  40.2 1.1 concatenate.64
  42.8 2.8 %fusion.12 = (f32[28,128]{1,0:T(8,128)S(1)}, f32[28,128]{1,0:T(8,128)S(1)}, f32[28,128]{1,0:T(8,128)S(1)}, bf16[128,128]{1,0:T(8,128)(2,1)S(1)}) fusion(f32[28,128]{1,0:T(8,128)S(1)} %fusion.118, f32[128,128]{1,0:T(8,128)S(1)} %fusion.102, f32[128,128]{1,0:T(8,128)} %get-tuple-element.107, f32[28,128]{1,0:T(8,128)S(1)} %fusion.74, ...), kind=kOutput, calls=%fused_computation.18 | convolution fusion | flops 66033152 | bytes 1628160 | tf_op jit(solution)/shard_map/transpose(jvp(hts,shp->thp))/dot_general | solution.py:33
  46.2 0.8 fusion.106
  47.2 1.8 %fusion.17 = bf16[128,28,64]{0,2,1:T(8,128)(2,1)} fusion(f32[128,28,64]{0,2,1:T(8,128)S(1)} %copy-done.8, f32[28,128]{1,0:T(8,128)S(1)} %fusion.118, f32[128,128]{1,0:T(8,128)S(1)} %fusion.102, f32[128,128]{1,0:T(8,128)S(1)} %copy-done.31, f32[28,128]{1,0:T(8,128)S(1)} %fusion.74, pred[128,128]{1,0:T(8,128)(4,1)S(1)} %copy-done.38, ...), kind=kOutput, calls=%fused_computation.27 | convolution fusion | flops 63078400 | bytes 1574000 | tf_op jit(solution)/shard_map/transpose(jvp(hts,shp->thp))/dot_general | solution.py:33
  48.9 12.6 %collective-permute-done.9 = bf16[28,8320]{1,0:T(8,128)(2,1)S(1)} collective-permute-done((bf16[28,8320]{1,0:T(8,128)(2,1)S(1)}, bf16[28,8320]{1,0:T(8,128)(2,1)S(1)}, u32[]{:S(2)}, u32[]{:S(2)}) %collective-permute-start.9) | collective-permute-done | bytes 465952 | tf_op jit(solution)/shard_map/ppermute | solution.py:148
  62.6 13.7 %collective-permute-done.10 = bf16[28,8320]{1,0:T(8,128)(2,1)} collective-permute-done((bf16[28,8320]{1,0:T(8,128)(2,1)S(1)}, bf16[28,8320]{1,0:T(8,128)(2,1)}, u32[]{:S(2)}, u32[]{:S(2)}) %collective-permute-start.10) | collective-permute-done | bytes 465952 | tf_op jit(solution)/shard_map/ppermute | solution.py:148
  76.3 1.1 convert_element_type.287
  78.3 0.7 collective-permute-start.11
  79.0 1.0 bitcast_multiply_fusion
  80.0 12.3 %collective-permute-done.11 = bf16[28,4224]{1,0:T(8,128)(2,1)} collective-permute-done((bf16[28,4224]{1,0:T(8,128)(2,1)S(1)}, bf16[28,4224]{1,0:T(8,128)(2,1)}, u32[]{:S(2)}, u32[]{:S(2)}) %collective-permute-start.11) | collective-permute-done | bytes 236576 | tf_op jit(solution)/shard_map/ppermute | solution.py:155
  92.3 1.4 %multiply_reduce_fusion.4 = (f32[28]{0:T(128)S(1)}, f32[28,4096]{1,0:T(8,128)S(1)}, bf16[28,4096]{1,0:T(8,128)(2,1)S(1)}) fusion(bf16[28,4224]{1,0:T(8,128)(2,1)} %collective-permute-done.11, f32[28]{0:T(128)S(1)} %get-tuple-element.52, f32[28,8320]{1,0:T(8,128)S(1)} %convert_element_type.287, f32[28]{0:T(128)S(1)} %get-tuple-element.54, ...), kind=kLoop, calls=%fused_computation.64 | loop fusion | flops 2064356 | bytes 2753075 | tf_op jit(solution)/shard_map/reduce_sum | solution.py:264
  97.1 0.8 fusion.136
  98.0 0.8 fusion.137
  99.1 1.0 fusion.22
  100.4 1.6 %fusion.21 = f32[128,28,64]{0,2,1:T(8,128)S(1)} fusion(bf16[28,64,64]{2,1,0:T(8,128)(2,1)S(1)} %copy-done.20, bf16[128,28,64]{0,2,1:T(8,128)(2,1)} %fusion.17, f32[28,128]{1,0:T(8,128)S(1)} %copy.82, f32[28,64]{1,0:T(8,128)S(1)} %copy-done.37, f32[28,128]{1,0:T(8,128)S(1)} %copy.77, f32[128,64]{0,1:T(8,128)S(1)} %copy-done.24, f32[128,28]{0,1:T(8,128)S(1)} %copy-done.29), kind=kOutput, calls=%fused_computation.31 | convolution fusion | flops 32112640 | bytes 1688576 | tf_op jit(solution)/shard_map/transpose(jvp(thn,thp->hnp))/dot_general | solution.py:33
  102.3 1.8 %fusion.131 = (bf16[256,1792]{1,0:T(8,128)(2,1)S(1)}, f32[256,1792]{1,0:T(8,128)}) fusion(bf16[1,128,1792]{2,1,0:T(8,128)(2,1)S(1)} %copy-done.7, s32[]{:T(128)S(6)} %select_n.220, bf16[128,256]{0,1:T(8,128)(2,1)S(1)} %maximum_select_fusion), kind=kOutput, calls=%fused_computation.276 | convolution fusion | flops 118030336 | bytes 3276804 | tf_op jit(solution)/shard_map/dot_general | solution.py:284
  104.2 0.7 pad_maximum_fusion.6
  105.0 0.7 collective-permute-start.20
  105.7 1.8 %collective-permute-start.19 = (bf16[32,1920]{1,0:T(8,128)(2,1)S(1)}, bf16[32,1920]{1,0:T(8,128)(2,1)S(1)}, u32[]{:S(2)}, u32[]{:S(2)}) collective-permute-start(bf16[32,1920]{1,0:T(8,128)(2,1)S(1)} %get-tuple-element.99), channel_id=1, source_target_pairs={{0,12},{2,14},{4,0},{6,2},{8,4},{10,6},{12,8},{14,10},{1,13},{3,15... | collective-permute-start | bytes 368648 | tf_op jit(solution)/shard_map/ppermute | solution.py:18
  107.7 3.5 %collective-permute-start.17 = (bf16[32,1920]{1,0:T(8,128)(2,1)S(1)}, bf16[32,1920]{1,0:T(8,128)(2,1)S(1)}, u32[]{:S(2)}, u32[]{:S(2)}) collective-permute-start(bf16[32,1920]{1,0:T(8,128)(2,1)S(1)} %get-tuple-element.97), channel_id=1, source_target_pairs={{0,8},{2,10},{4,12},{6,14},{8,0},{10,2},{12,4},{14,6},{1,9},{3,11}... | collective-permute-start | bytes 368648 | tf_op jit(solution)/shard_map/ppermute | solution.py:18
  112.3 1.0 collective-permute-start.15
  113.3 1.8 %collective-permute-start.14 = (bf16[32,1920]{1,0:T(8,128)(2,1)S(1)}, bf16[32,1920]{1,0:T(8,128)(2,1)S(1)}, u32[]{:S(2)}, u32[]{:S(2)}) collective-permute-start(bf16[32,1920]{1,0:T(8,128)(2,1)S(1)} %get-tuple-element.94), channel_id=1, source_target_pairs={{0,2},{2,4},{4,6},{6,8},{8,10},{10,12},{12,14},{14,0},{1,3},{3,5},... | collective-permute-start | bytes 368648 | tf_op jit(solution)/shard_map/ppermute | solution.py:18
  115.1 11.6 %collective-permute-done.18 = bf16[32,1920]{1,0:T(8,128)(2,1)S(1)} collective-permute-done((bf16[32,1920]{1,0:T(8,128)(2,1)S(1)}, bf16[32,1920]{1,0:T(8,128)(2,1)S(1)}, u32[]{:S(2)}, u32[]{:S(2)}) %collective-permute-start.18) | collective-permute-done | bytes 122912 | tf_op jit(solution)/shard_map/ppermute | solution.py:18
  126.7 1.3 collective-permute-start.13
  130.3 1.7 %fusion.51 = f32[1,32,1792]{2,1,0:T(8,128)} fusion(f32[256,1792]{1,0:T(8,128)} %get-tuple-element.112, bf16[32,1920]{1,0:T(8,128)(2,1)S(1)} %collective-permute-done.20, bf16[32,1920]{1,0:T(8,128)(2,1)S(1)} %collective-permute-done.19, bf16[32,1920]{1,0:T(8,128)(2,1)S(1)} %collective-permute-done.18, bf16[32,1920]{1,0:T(8,128)(2,1)S(1)} %collective-permute-done.17, ...), kind=kLoop, calls=%fused_computation.97 | loop fusion | flops 802816 | bytes 1261568 | tf_op jit(solution)/shard_map/broadcast_in_dim | solution.py:326
  132.0 7.7 %collective-permute-done.13 = bf16[1,128,1792]{2,1,0:T(8,128)(2,1)S(1)} collective-permute-done((bf16[1,128,1792]{2,1,0:T(8,128)(2,1)S(1)}, bf16[1,128,1792]{2,1,0:T(8,128)(2,1)S(1)}, u32[]{:S(2)}, u32[]{:S(2)}) %collective-permute-start.13) | collective-permute-done | bytes 458784 | tf_op jit(solution)/shard_map/ppermute | solution.py:12
  139.7 0.8 copy.148
  (242 shorter events, 16.8 us)
Async XLA Ops:
  0.6 15.9 %copy-start.49 = (f32[1,28]{1,0:T(1,128)S(1)}, f32[1,28]{1,0:T(1,128)}, u32[]{:S(2)}) copy-start(f32[1,28]{1,0:T(1,128)} %param.15) | copy-start | bytes 340
  0.6 15.9 %copy-start.18 = (bf16[1,128,1792]{2,1,0:T(8,128)(2,1)S(1)}, bf16[1,128,1792]{2,1,0:T(8,128)(2,1)}, u32[]{:S(2)}) copy-start(bf16[1,128,1792]{2,1,0:T(8,128)(2,1)} %param.11) | copy-start | bytes 1376260
  0.7 23.0 %collective-permute-start = (bf16[32,1792]{1,0:T(8,128)(2,1)}, bf16[32,1792]{1,0:T(8,128)(2,1)S(1)}, u32[]{:S(2)}, u32[]{:S(2)}) collective-permute-start(bf16[32,1792]{1,0:T(8,128)(2,1)} %bitcast.346), channel_id=1, source_target_pairs={{0,2},{2,4},{4,6},{6,8},{8,10},{10,12},{12,14},{14,0},{1,3},{3,5},... | collective-permute-start | bytes 344072 | tf_op jit(solution)/shard_map/ppermute | solution.py:18
  2.2 24.5 %collective-permute-start.1 = (bf16[32,1792]{1,0:T(8,128)(2,1)}, bf16[32,1792]{1,0:T(8,128)(2,1)S(1)}, u32[]{:S(2)}, u32[]{:S(2)}) collective-permute-start(bf16[32,1792]{1,0:T(8,128)(2,1)} %bitcast.347), channel_id=1, source_target_pairs={{0,4},{2,6},{4,8},{6,10},{8,12},{10,14},{12,0},{14,2},{1,5},{3,7},... | collective-permute-start | bytes 344072 | tf_op jit(solution)/shard_map/ppermute | solution.py:18
  3.8 23.2 %collective-permute-start.2 = (bf16[32,1792]{1,0:T(8,128)(2,1)}, bf16[32,1792]{1,0:T(8,128)(2,1)S(1)}, u32[]{:S(2)}, u32[]{:S(2)}) collective-permute-start(bf16[32,1792]{1,0:T(8,128)(2,1)} %bitcast.348), channel_id=1, source_target_pairs={{0,6},{2,8},{4,10},{6,12},{8,14},{10,0},{12,2},{14,4},{1,7},{3,9},... | collective-permute-start | bytes 344072 | tf_op jit(solution)/shard_map/ppermute | solution.py:18
  6.3 20.7 %collective-permute-start.3 = (bf16[32,1792]{1,0:T(8,128)(2,1)}, bf16[32,1792]{1,0:T(8,128)(2,1)S(1)}, u32[]{:S(2)}, u32[]{:S(2)}) collective-permute-start(bf16[32,1792]{1,0:T(8,128)(2,1)} %bitcast.349), channel_id=1, source_target_pairs={{0,8},{2,10},{4,12},{6,14},{8,0},{10,2},{12,4},{14,6},{1,9},{3,11}... | collective-permute-start | bytes 344072 | tf_op jit(solution)/shard_map/ppermute | solution.py:18
  7.9 10.7 %collective-permute-start.8 = (s32[1]{0:T(128)}, s32[1]{0:T(128)}, u32[]{:S(2)}, u32[]{:S(2)}) collective-permute-start(s32[1]{0:T(128)} %bitcast.13), channel_id=1, source_target_pairs={{0,2},{2,4},{4,6},{6,8},{8,10},{10,12},{12,14},{1,3},{3,5},{5,7},{... | collective-permute-start | bytes 20 | tf_op jit(solution)/shard_map/ppermute | solution.py:12
  14.6 3.3 %copy-start.46 = (s32[1,128]{1,0:T(1,128)S(1)}, s32[1,128]{1,0:T(1,128)}, u32[]{:S(2)}) copy-start(s32[1,128]{1,0:T(1,128)} %param.10) | copy-start | bytes 1540
  14.6 4.0 %copy-start.25 = (bf16[1,32,1792]{2,1,0:T(8,128)(2,1)S(1)}, bf16[1,32,1792]{2,1,0:T(8,128)(2,1)}, u32[]{:S(2)}) copy-start(bf16[1,32,1792]{2,1,0:T(8,128)(2,1)} %param.12) | copy-start | bytes 344068
  14.6 8.0 %copy-start.39 = (f32[1,28]{1,0:T(1,128)S(1)}, f32[1,28]{1,0:T(1,128)}, u32[]{:S(2)}) copy-start(f32[1,28]{1,0:T(1,128)} %param.14) | copy-start | bytes 340
  15.9 30.2 %copy-start.4 = (bf16[1,128,1792]{1,2,0:T(8,128)(2,1)}, bf16[1,128,1792]{1,2,0:T(8,128)(2,1)S(1)}, u32[]{:S(2)}) copy-start(bf16[1,128,1792]{1,2,0:T(8,128)(2,1)S(1)} %copy.66) | copy-start | bytes 1376260
  16.5 10.5 %copy-start.15 = (f32[28,1,128]{0,2,1:T(8,128)}, f32[28,1,128]{0,2,1:T(8,128)S(1)}, u32[]{:S(2)}) copy-start(f32[28,1,128]{0,2,1:T(8,128)S(1)} %copy.87) | copy-start | bytes 43012
  16.6 6.3 %copy-start.56 = (f32[28]{0:T(128)}, f32[28]{0:T(128)S(1)}, u32[]{:S(2)}) copy-start(f32[28]{0:T(128)S(1)} %negate_bitcast_fusion) | copy-start | bytes 340
  16.8 15.7 %copy-start.6 = (bf16[1,128,1792]{2,1,0:T(8,128)(2,1)S(1)}, bf16[1,128,1792]{2,1,0:T(8,128)(2,1)}, u32[]{:S(2)}) copy-start(bf16[1,128,1792]{2,1,0:T(8,128)(2,1)} %param.9) | copy-start | bytes 1376260
  18.6 8.8 %collective-permute-start.4 = (bf16[32,1792]{1,0:T(8,128)(2,1)S(1)}, bf16[32,1792]{1,0:T(8,128)(2,1)S(1)}, u32[]{:S(2)}, u32[]{:S(2)}) collective-permute-start(bf16[32,1792]{1,0:T(8,128)(2,1)S(1)} %bitcast.350), channel_id=1, source_target_pairs={{0,10},{2,12},{4,14},{6,0},{8,2},{10,4},{12,6},{14,8},{1,11},{3,13... | collective-permute-start | bytes 344072 | tf_op jit(solution)/shard_map/ppermute | solution.py:18
  21.3 11.2 %copy-start.42 = (pred[128]{0:T(512)(128)(4,1)}, pred[128]{0:T(512)(128)(4,1)S(1)}, u32[]{:S(2)}) copy-start(pred[128]{0:T(512)(128)(4,1)S(1)} %get-tuple-element.77) | copy-start | bytes 388
  21.3 11.2 %copy-start.44 = (f32[128]{0:T(128)}, f32[128]{0:T(128)S(1)}, u32[]{:S(2)}) copy-start(f32[128]{0:T(128)S(1)} %get-tuple-element.78) | copy-start | bytes 1540
  22.9 13.7 %copy-start.26 = (f32[128,28]{0,1:T(8,128)}, f32[128,28]{0,1:T(8,128)S(1)}, u32[]{:S(2)}) copy-start(f32[128,28]{0,1:T(8,128)S(1)} %get-tuple-element.109) | copy-start | bytes 43012
  23.0 10.1 %copy-start.13 = (f32[128,28]{1,0:T(8,128)}, f32[128,28]{1,0:T(8,128)S(1)}, u32[]{:S(2)}) copy-start(f32[128,28]{1,0:T(8,128)S(1)} %copy.67) | copy-start | bytes 43012
  23.1 9.4 %copy-start.47 = (f32[28]{0:T(128)}, f32[28]{0:T(128)S(1)}, u32[]{:S(2)}) copy-start(f32[28]{0:T(128)S(1)} %slice_bitcast_fusion.7) | copy-start | bytes 340
  23.6 5.4 %collective-permute-start.5 = (bf16[32,1792]{1,0:T(8,128)(2,1)S(1)}, bf16[32,1792]{1,0:T(8,128)(2,1)S(1)}, u32[]{:S(2)}, u32[]{:S(2)}) collective-permute-start(bf16[32,1792]{1,0:T(8,128)(2,1)S(1)} %bitcast.351), channel_id=1, source_target_pairs={{0,12},{2,14},{4,0},{6,2},{8,4},{10,6},{12,8},{14,10},{1,13},{3,15... | collective-permute-start | bytes 344072 | tf_op jit(solution)/shard_map/ppermute | solution.py:18
  26.7 5.7 %collective-permute-start.6 = (bf16[32,1792]{1,0:T(8,128)(2,1)S(1)}, bf16[32,1792]{1,0:T(8,128)(2,1)S(1)}, u32[]{:S(2)}, u32[]{:S(2)}) collective-permute-start(bf16[32,1792]{1,0:T(8,128)(2,1)S(1)} %bitcast.352), channel_id=1, source_target_pairs={{0,14},{2,0},{4,2},{6,4},{8,6},{10,8},{12,10},{14,12},{1,15},{3,1}... | collective-permute-start | bytes 344072 | tf_op jit(solution)/shard_map/ppermute | solution.py:18
  32.5 3.8 %copy-start.2 = (bf16[256,1792]{1,0:T(8,128)(2,1)}, bf16[256,1792]{1,0:T(8,128)(2,1)S(1)}, u32[]{:S(2)}) copy-start(bf16[256,1792]{1,0:T(8,128)(2,1)S(1)} %constant_dynamic-update-slice_fusion) | copy-start | bytes 2752516
  33.0 2.8 %collective-permute-start.7 = (bf16[128,128]{0,1:T(8,128)(2,1)S(1)}, bf16[128,128]{0,1:T(8,128)(2,1)S(1)}, u32[]{:S(2)}, u32[]{:S(2)}) collective-permute-start(bf16[128,128]{0,1:T(8,128)(2,1)S(1)} %fusion.58), channel_id=1, source_target_pairs={{0,1},{1,0},{2,3},{3,2},{4,5},{5,4},{6,7},{7,6},{8,9},{9,8},{10,11... | collective-permute-start | bytes 98312 | tf_op jit(solution)/shard_map/ppermute | solution.py:29
  40.1 21.8 %copy-start = (f32[28,4096]{1,0:T(8,128)}, f32[28,4096]{1,0:T(8,128)S(1)}, u32[]{:S(2)}) copy-start(f32[28,4096]{1,0:T(8,128)S(1)} %reshape.286) | copy-start | bytes 1376260
  40.2 5.4 %copy-start.21 = (bf16[28,126]{1,0:T(8,128)(2,1)}, bf16[28,126]{1,0:T(8,128)(2,1)S(1)}, u32[]{:S(2)}) copy-start(bf16[28,126]{1,0:T(8,128)(2,1)S(1)} %broadcast.164) | copy-start | bytes 21172
  42.7 4.3 %copy-start.17 = (bf16[28,8320]{1,0:T(8,128)(2,1)S(1)}, bf16[28,8320]{1,0:T(8,128)(2,1)}, u32[]{:S(2)}) copy-start(bf16[28,8320]{1,0:T(8,128)(2,1)} %concatenate.64) | copy-start | bytes 1397764
  42.7 4.4 %copy-start.53 = (f32[1,28]{1,0:T(1,128)S(1)}, f32[1,28]{1,0:T(1,128)}, u32[]{:S(2)}) copy-start(f32[1,28]{1,0:T(1,128)} %param.16) | copy-start | bytes 340
  42.7 4.4 %copy-start.31 = (f32[128,128]{1,0:T(8,128)S(1)}, f32[128,128]{1,0:T(8,128)}, u32[]{:S(2)}) copy-start(f32[128,128]{1,0:T(8,128)} %get-tuple-element.107) | copy-start | bytes 196612
  42.7 4.4 %copy-start.37 = (f32[28,64]{1,0:T(8,128)S(1)}, f32[28,64]{1,0:T(8,128)}, u32[]{:S(2)}) copy-start(f32[28,64]{1,0:T(8,128)} %reshape_squeeze.7) | copy-start | bytes 21508
  42.8 4.4 %copy-start.38 = (pred[128,128]{1,0:T(8,128)(4,1)S(1)}, pred[128,128]{1,0:T(8,128)(4,1)}, u32[]{:S(2)}) copy-start(pred[128,128]{1,0:T(8,128)(4,1)} %get-tuple-element.106) | copy-start | bytes 49156
  47.0 14.6 %collective-permute-start.9 = (bf16[28,8320]{1,0:T(8,128)(2,1)S(1)}, bf16[28,8320]{1,0:T(8,128)(2,1)S(1)}, u32[]{:S(2)}, u32[]{:S(2)}) collective-permute-start(bf16[28,8320]{1,0:T(8,128)(2,1)S(1)} %copy-done.17), channel_id=1, source_target_pairs={{0,2},{2,0},{4,6},{6,4},{8,10},{10,8},{12,14},{14,12},{1,3},{3,1},... | collective-permute-start | bytes 1397768 | tf_op jit(solution)/shard_map/ppermute | solution.py:148
  47.1 14.5 %copy-start.30 = (f32[28,1]{1,0:T(8,128)S(1)}, f32[28,1]{1,0:T(8,128)}, u32[]{:S(2)}) copy-start(f32[28,1]{1,0:T(8,128)} %copy.74) | copy-start | bytes 340
  47.1 14.8 %copy-start.52 = (f32[28]{0:T(128)S(1)}, f32[28]{0:T(128)}, u32[]{:S(2)}) copy-start(f32[28]{0:T(128)} %exponential_multiply_fusion.1) | copy-start | bytes 340
  48.9 13.3 %copy-start.22 = (bf16[28,126]{1,0:T(8,128)(2,1)S(1)}, bf16[28,126]{1,0:T(8,128)(2,1)}, u32[]{:S(2)}) copy-start(bf16[28,126]{1,0:T(8,128)(2,1)} %copy-done.21) | copy-start | bytes 21172
  62.5 13.9 %collective-permute-start.10 = (bf16[28,8320]{1,0:T(8,128)(2,1)S(1)}, bf16[28,8320]{1,0:T(8,128)(2,1)}, u32[]{:S(2)}, u32[]{:S(2)}) collective-permute-start(bf16[28,8320]{1,0:T(8,128)(2,1)S(1)} %concatenate.65), channel_id=1, source_target_pairs={{0,4},{2,6},{4,0},{6,2},{8,12},{10,14},{12,8},{14,10},{1,5},{3,7},... | collective-permute-start | bytes 1397768 | tf_op jit(solution)/shard_map/ppermute | solution.py:148
  62.6 15.1 %copy-start.1 = (f32[28,4096]{1,0:T(8,128)S(1)}, f32[28,4096]{1,0:T(8,128)}, u32[]{:S(2)}) copy-start(f32[28,4096]{1,0:T(8,128)} %copy-done) | copy-start | bytes 1376260
  78.3 14.1 %collective-permute-start.11 = (bf16[28,4224]{1,0:T(8,128)(2,1)S(1)}, bf16[28,4224]{1,0:T(8,128)(2,1)}, u32[]{:S(2)}, u32[]{:S(2)}) collective-permute-start(bf16[28,4224]{1,0:T(8,128)(2,1)S(1)} %concatenate.66), channel_id=1, source_target_pairs={{0,8},{2,10},{4,12},{6,14},{8,0},{10,2},{12,4},{14,6},{1,9},{3,11}... | collective-permute-start | bytes 709640 | tf_op jit(solution)/shard_map/ppermute | solution.py:155
  100.1 2.2 %collective-permute-start.12 = (bf16[128,128]{0,1:T(8,128)(2,1)S(1)}, bf16[128,128]{0,1:T(8,128)(2,1)S(1)}, u32[]{:S(2)}, u32[]{:S(2)}) collective-permute-start(bf16[128,128]{0,1:T(8,128)(2,1)S(1)} %add_convert_fusion), channel_id=1, source_target_pairs={{0,1},{1,0},{2,3},{3,2},{4,5},{5,4},{6,7},{7,6},{8,9},{9,8},{10,11... | collective-permute-start | bytes 98312 | tf_op jit(solution)/shard_map/ppermute | solution.py:29
  104.2 7.4 %copy-start.3 = (bf16[256,1792]{1,0:T(8,128)(2,1)S(1)}, bf16[256,1792]{1,0:T(8,128)(2,1)}, u32[]{:S(2)}) copy-start(bf16[256,1792]{1,0:T(8,128)(2,1)} %copy-done.2) | copy-start | bytes 2752516
  105.0 7.3 %collective-permute-start.20 = (bf16[32,1920]{1,0:T(8,128)(2,1)}, bf16[32,1920]{1,0:T(8,128)(2,1)S(1)}, u32[]{:S(2)}, u32[]{:S(2)}) collective-permute-start(bf16[32,1920]{1,0:T(8,128)(2,1)} %get-tuple-element.100), channel_id=1, source_target_pairs={{0,14},{2,0},{4,2},{6,4},{8,6},{10,8},{12,10},{14,12},{1,15},{3,1}... | collective-permute-start | bytes 368648 | tf_op jit(solution)/shard_map/ppermute | solution.py:18
  105.7 7.6 %collective-permute-start.19 = (bf16[32,1920]{1,0:T(8,128)(2,1)S(1)}, bf16[32,1920]{1,0:T(8,128)(2,1)S(1)}, u32[]{:S(2)}, u32[]{:S(2)}) collective-permute-start(bf16[32,1920]{1,0:T(8,128)(2,1)S(1)} %get-tuple-element.99), channel_id=1, source_target_pairs={{0,12},{2,14},{4,0},{6,2},{8,4},{10,6},{12,8},{14,10},{1,13},{3,15... | collective-permute-start | bytes 368648 | tf_op jit(solution)/shard_map/ppermute | solution.py:18
  107.5 19.2 %collective-permute-start.18 = (bf16[32,1920]{1,0:T(8,128)(2,1)S(1)}, bf16[32,1920]{1,0:T(8,128)(2,1)S(1)}, u32[]{:S(2)}, u32[]{:S(2)}) collective-permute-start(bf16[32,1920]{1,0:T(8,128)(2,1)S(1)} %get-tuple-element.98), channel_id=1, source_target_pairs={{0,10},{2,12},{4,14},{6,0},{8,2},{10,4},{12,6},{14,8},{1,11},{3,13... | collective-permute-start | bytes 368648 | tf_op jit(solution)/shard_map/ppermute | solution.py:18
  107.7 20.8 %collective-permute-start.17 = (bf16[32,1920]{1,0:T(8,128)(2,1)S(1)}, bf16[32,1920]{1,0:T(8,128)(2,1)S(1)}, u32[]{:S(2)}, u32[]{:S(2)}) collective-permute-start(bf16[32,1920]{1,0:T(8,128)(2,1)S(1)} %get-tuple-element.97), channel_id=1, source_target_pairs={{0,8},{2,10},{4,12},{6,14},{8,0},{10,2},{12,4},{14,6},{1,9},{3,11}... | collective-permute-start | bytes 368648 | tf_op jit(solution)/shard_map/ppermute | solution.py:18
  111.2 17.4 %collective-permute-start.16 = (bf16[32,1920]{1,0:T(8,128)(2,1)S(1)}, bf16[32,1920]{1,0:T(8,128)(2,1)S(1)}, u32[]{:S(2)}, u32[]{:S(2)}) collective-permute-start(bf16[32,1920]{1,0:T(8,128)(2,1)S(1)} %get-tuple-element.96), channel_id=1, source_target_pairs={{0,6},{2,8},{4,10},{6,12},{8,14},{10,0},{12,2},{14,4},{1,7},{3,9},... | collective-permute-start | bytes 368648 | tf_op jit(solution)/shard_map/ppermute | solution.py:18
  112.3 16.3 %collective-permute-start.15 = (bf16[32,1920]{1,0:T(8,128)(2,1)S(1)}, bf16[32,1920]{1,0:T(8,128)(2,1)S(1)}, u32[]{:S(2)}, u32[]{:S(2)}) collective-permute-start(bf16[32,1920]{1,0:T(8,128)(2,1)S(1)} %get-tuple-element.95), channel_id=1, source_target_pairs={{0,4},{2,6},{4,8},{6,10},{8,12},{10,14},{12,0},{14,2},{1,5},{3,7},... | collective-permute-start | bytes 368648 | tf_op jit(solution)/shard_map/ppermute | solution.py:18
  113.3 15.3 %collective-permute-start.14 = (bf16[32,1920]{1,0:T(8,128)(2,1)S(1)}, bf16[32,1920]{1,0:T(8,128)(2,1)S(1)}, u32[]{:S(2)}, u32[]{:S(2)}) collective-permute-start(bf16[32,1920]{1,0:T(8,128)(2,1)S(1)} %get-tuple-element.94), channel_id=1, source_target_pairs={{0,2},{2,4},{4,6},{6,8},{8,10},{10,12},{12,14},{14,0},{1,3},{3,5},... | collective-permute-start | bytes 368648 | tf_op jit(solution)/shard_map/ppermute | solution.py:18
  126.7 13.0 %collective-permute-start.13 = (bf16[1,128,1792]{2,1,0:T(8,128)(2,1)S(1)}, bf16[1,128,1792]{2,1,0:T(8,128)(2,1)S(1)}, u32[]{:S(2)}, u32[]{:S(2)}) collective-permute-start(bf16[1,128,1792]{2,1,0:T(8,128)(2,1)S(1)} %fusion.1), channel_id=1, source_target_pairs={{16,0},{17,1},{18,2},{19,3},{20,4},{21,5},{22,6},{23,7},{24,8},{25... | collective-permute-start | bytes 1376264 | tf_op jit(solution)/shard_map/ppermute | solution.py:12
  (31 other events, 54.0 us)

commit v16 on v11

--- a/solution.py
+++ b/solution.py
@@ -94,7 +94,9 @@
     readers = mixer[:, half_width:]
     unbroken = (docs == doc_before).astype(jnp.float32)
     carry_scale = jnp.exp(cumulative) * unbroken[:, None]
-    carried = jnp.einsum("tn,hnp->thp", readers.astype(jnp.float32), incoming, precision=EXACT)
+    carried = jnp.einsum(
+        "tn,hnp->thp", readers, incoming.astype(jnp.bfloat16), preferred_element_type=jnp.float32
+    )
     return carry_scale[:, :, None] * carried
 
 

time: 141 us -> 143 us (1.014); the launches traced: 140 us -> 140 us
  other arithmetic: 13.4 us -> 20.3 us
  waiting for transfers between devices: 64.2 us -> 59.7 us
  starting transfers between devices: 26.4 us -> 24.4 us
    ppermute x2, waiting for transfers between devices: 7.67 us -> 0.01 us  [shifted(): return lax.ppermute(block, axis, route)]
    ppermute x14, waiting for transfers between devices: 17.9 us -> 24.6 us  [rotated(): return lax.ppermute(block, axis, route)]
    ppermute x2, waiting for transfers between devices: 26.3 us -> 22.4 us  [both_scans(): got = lax.ppermute(payload, axis, [(i, i ^ distance) for i in range(size)])]
    ppermute x14, starting transfers between devices: 19.8 us -> 17.9 us  [rotated(): return lax.ppermute(block, axis, route)]
    unnamed x141 -> x143, local copies, waits for them, and re-layouts: 4.31 us -> 6.17 us
    select_n x1, other arithmetic: 0.19 us -> 1.98 us  [both_scans(): before_decay = jnp.where(upper, before_decay * got_decay, before_decay)]
    convert_element_type x0 -> x1, other arithmetic: none -> 1.59 us  [span_carry(): incoming.astype(jnp.bfloat16)]
  transfers between devices with their start and end apart: 21 -> 21, of which waited for: 10 -> 10; matrix products, arithmetic and copies ran while one was open for 15% -> 17% of each run, Pallas kernels for 0% -> 0%
where the time goes in v16:
time: 143 us; the launch traced here: 140 us
  waiting for transfers between devices  59.7 us (42%)
  starting transfers between devices  24.4 us (17%)
  other arithmetic  20.3 us (14%)
  local copies, waits for them, and re-layouts  17.4 us (12%)
  matrix products  15.4 us (11%)
  between operations  3.1 us (2%)
    ppermute x14, waiting for transfers between devices, rotated(): return lax.ppermute(block, axis, route)  24.6 us
    ppermute x2, waiting for transfers between devices, both_scans(): got = lax.ppermute(payload, axis, [(i, i ^ distance) for i in range(size)])  22.4 us
    ppermute x14, starting transfers between devices, rotated(): return lax.ppermute(block, axis, route)  17.9 us
    ppermute x1, waiting for transfers between devices, both_scans(): got = lax.ppermute(last, axis, [(i, i ^ distance) for i in range(size)])  12 us
    dot_general x5, matrix products, contract(): return jnp.einsum(spec, left, right, preferred_element_type=jnp.float32)  7.69 us
    unnamed x143, local copies, waits for them, and re-layouts  6.17 us
    ppermute x2, starting transfers between devices, shifted(): return lax.ppermute(block, axis, route)  5.61 us
    dot_general x5, matrix products, local_setup(): jnp.einsum('thp,hp->th', values.astype(jnp.float32), step_weight, precisi...  3.41 us
  transfers between devices with their start and end apart: 21, of which 10 were waited for; matrix products, arithmetic and copies ran while one was open for 17% of the time, Pallas kernels for 0%

profile of v16, /device:TPU:4, one launch (start us, length us, event | category | flops | bytes accessed | tf_op | source)
XLA Modules:
  0.0 140.3 jit_solution(3593049265662101512)
XLA Ops:
  0.6 1.6 %collective-permute-start = (bf16[32,1792]{1,0:T(8,128)(2,1)}, bf16[32,1792]{1,0:T(8,128)(2,1)}, u32[]{:S(2)}, u32[]{:S(2)}) collective-permute-start(bf16[32,1792]{1,0:T(8,128)(2,1)} %bitcast.346), channel_id=1, source_target_pairs={{0,2},{2,4},{4,6},{6,8},{8,10},{10,12},{12,14},{14,0},{1,3},{3,5},... | collective-permute-start | bytes 344072 | tf_op jit(solution)/shard_map/ppermute | solution.py:18
  2.2 1.6 %collective-permute-start.1 = (bf16[32,1792]{1,0:T(8,128)(2,1)}, bf16[32,1792]{1,0:T(8,128)(2,1)S(1)}, u32[]{:S(2)}, u32[]{:S(2)}) collective-permute-start(bf16[32,1792]{1,0:T(8,128)(2,1)} %bitcast.347), channel_id=1, source_target_pairs={{0,4},{2,6},{4,8},{6,10},{8,12},{10,14},{12,0},{14,2},{1,5},{3,7},... | collective-permute-start | bytes 344072 | tf_op jit(solution)/shard_map/ppermute | solution.py:18
  3.8 2.5 %collective-permute-start.2 = (bf16[32,1792]{1,0:T(8,128)(2,1)}, bf16[32,1792]{1,0:T(8,128)(2,1)S(1)}, u32[]{:S(2)}, u32[]{:S(2)}) collective-permute-start(bf16[32,1792]{1,0:T(8,128)(2,1)} %bitcast.348), channel_id=1, source_target_pairs={{0,6},{2,8},{4,10},{6,12},{8,14},{10,0},{12,2},{14,4},{1,7},{3,9},... | collective-permute-start | bytes 344072 | tf_op jit(solution)/shard_map/ppermute | solution.py:18
  6.7 1.2 slice.179
  7.9 4.3 %collective-permute-start.8 = (s32[1]{0:T(128)}, s32[1]{0:T(128)}, u32[]{:S(2)}, u32[]{:S(2)}) collective-permute-start(s32[1]{0:T(128)} %bitcast.13), channel_id=1, source_target_pairs={{0,2},{2,4},{4,6},{6,8},{8,10},{10,12},{12,14},{1,3},{3,5},{5,7},{... | collective-permute-start | bytes 20 | tf_op jit(solution)/shard_map/ppermute | solution.py:12
  12.2 0.9 constant_dynamic-update-slice_fusion.7
  13.1 0.7 reduce
  14.7 1.3 copy.66
  16.9 1.0 convert.61
  17.9 0.7 broadcast_compare_fusion
  18.7 1.3 collective-permute-start.4
  21.2 1.3 broadcast_compare_fusion.1
  23.4 3.2 %collective-permute-start.5 = (bf16[32,1792]{1,0:T(8,128)(2,1)S(1)}, bf16[32,1792]{1,0:T(8,128)(2,1)S(1)}, u32[]{:S(2)}, u32[]{:S(2)}) collective-permute-start(bf16[32,1792]{1,0:T(8,128)(2,1)S(1)} %bitcast.351), channel_id=1, source_target_pairs={{0,12},{2,14},{4,0},{6,2},{8,4},{10,6},{12,8},{14,10},{1,13},{3,15... | collective-permute-start | bytes 344072 | tf_op jit(solution)/shard_map/ppermute | solution.py:18
  26.5 0.9 constant_dynamic-update-slice_fusion.6
  27.7 1.2 collective-permute-done.5
  28.9 4.3 %collective-permute-done.6 = bf16[32,1792]{1,0:T(8,128)(2,1)S(1)} collective-permute-done((bf16[32,1792]{1,0:T(8,128)(2,1)S(1)}, bf16[32,1792]{1,0:T(8,128)(2,1)S(1)}, u32[]{:S(2)}, u32[]{:S(2)}) %collective-permute-start.6) | collective-permute-done | bytes 114720 | tf_op jit(solution)/shard_map/ppermute | solution.py:18
  34.2 0.8 collective-permute-done.7
  36.0 1.3 fusion.34
  37.4 1.6 %reshape.288 = f32[28,4096]{1,0:T(8,128)S(1)} reshape(f32[28,64,64]{2,1,0:T(8,128)} %fusion.34) | data formatting | bytes 917504 | tf_op jit(solution)/shard_map/reshape | solution.py:225
  39.0 1.1 concatenate.64
  41.2 2.8 %fusion.12 = (f32[28,128]{1,0:T(8,128)S(1)}, f32[28,128]{1,0:T(8,128)S(1)}, f32[28,128]{1,0:T(8,128)S(1)}, bf16[128,128]{1,0:T(8,128)(2,1)S(1)}) fusion(f32[28,128]{1,0:T(8,128)S(1)} %fusion.121, f32[128,128]{1,0:T(8,128)S(1)} %fusion.105, f32[128,128]{1,0:T(8,128)} %get-tuple-element.108, f32[28,128]{1,0:T(8,128)S(1)} %fusion.77, ...), kind=kOutput, calls=%fused_computation.18 | convolution fusion | flops 66033152 | bytes 1628160 | tf_op jit(solution)/shard_map/transpose(jvp(hts,shp->thp))/dot_general | solution.py:33
  44.3 0.9 multiply_reduce_fusion.3
  45.1 0.8 fusion.130
  45.9 0.8 fusion.109
  48.5 1.7 %fusion.17 = bf16[128,28,64]{0,2,1:T(8,128)(2,1)} fusion(f32[128,28,64]{0,2,1:T(8,128)S(1)} %copy-done.6, f32[28,128]{1,0:T(8,128)S(1)} %fusion.121, f32[128,128]{1,0:T(8,128)S(1)} %fusion.105, f32[128,128]{1,0:T(8,128)S(1)} %copy-done.23, f32[28,128]{1,0:T(8,128)S(1)} %fusion.77, pred[128,128]{1,0:T(8,128)(4,1)S(1)} %copy-done.29, ...), kind=kOutput, calls=%fused_computation.27 | convolution fusion | flops 63078400 | bytes 1574000 | tf_op jit(solution)/shard_map/transpose(jvp(hts,shp->thp))/dot_general | solution.py:33
  50.2 9.1 %collective-permute-done.9 = bf16[28,8320]{1,0:T(8,128)(2,1)S(1)} collective-permute-done((bf16[28,8320]{1,0:T(8,128)(2,1)S(1)}, bf16[28,8320]{1,0:T(8,128)(2,1)S(1)}, u32[]{:S(2)}, u32[]{:S(2)}) %collective-permute-start.9) | collective-permute-done | bytes 465952 | tf_op jit(solution)/shard_map/ppermute | solution.py:150
  61.6 0.9 concatenate.65
  62.6 13.4 %collective-permute-done.10 = bf16[28,8320]{1,0:T(8,128)(2,1)} collective-permute-done((bf16[28,8320]{1,0:T(8,128)(2,1)S(1)}, bf16[28,8320]{1,0:T(8,128)(2,1)}, u32[]{:S(2)}, u32[]{:S(2)}) %collective-permute-start.10) | collective-permute-done | bytes 465952 | tf_op jit(solution)/shard_map/ppermute | solution.py:150
  76.0 1.1 convert_element_type.302
  77.7 2.0 %fusion.83 = (f32[28]{0:T(128)}, f32[28]{0:T(128)}, f32[28]{0:T(128)}, f32[28]{0:T(128)S(1)}, f32[28]{0:T(128)}, /*index=5*/bf16[28,1]{1,0:T(8,128)(2,1)}) fusion(f32[28,1]{1,0:T(8,128)S(1)} %get-tuple-element.68, f32[28,1]{1,0:T(8,128)} %copy-done.12, pred[]{:T(512)S(6)} %eq.83, pred[]{:T(512)S(6)} %eq.84, f32[28,1]{1,0:T(8,128)S(1)} %get-tuple-element.70), kind=kLoop, calls=%fused_computation.182 | loop fusion | flops 224 | bytes 954 | tf_op jit(solution)/shard_map/jit(_where)/select_n | solution.py:166
  79.7 1.8 %select_convert_fusion = bf16[28,4096]{1,0:T(8,128)(2,1)} fusion(f32[28,8320]{1,0:T(8,128)S(1)} %convert_element_type.302, f32[28]{0:T(128)} %get-tuple-element.69, f32[28]{0:T(128)S(1)} %get-tuple-element.55, pred[]{:T(512)S(6)} %eq.83, pred[]{:T(512)S(6)} %eq.82, f32[28]{0:T(128)} %copy-done.52, bf16[28,4096]{1,0:T(8,128)(2,1)S(1)} %reshape.289, ...), kind=kLoop, calls=%fused_computation.70 | loop fusion | flops 2637824 | bytes 2752963 | tf_op jit(solution)/shard_map/convert_element_type | solution.py:155
  81.6 1.1 concatenate.66
  83.3 0.9 bitcast_multiply_fusion
  84.2 12.0 %collective-permute-done.11 = bf16[28,4224]{1,0:T(8,128)(2,1)S(1)} collective-permute-done((bf16[28,4224]{1,0:T(8,128)(2,1)S(1)}, bf16[28,4224]{1,0:T(8,128)(2,1)S(1)}, u32[]{:S(2)}, u32[]{:S(2)}) %collective-permute-start.11) | collective-permute-done | bytes 236576 | tf_op jit(solution)/shard_map/ppermute | solution.py:157
  96.9 1.6 %fusion.127 = (bf16[28,4096]{1,0:T(8,128)(2,1)}, f32[28,4096]{1,0:T(8,128)S(1)}) fusion(bf16[28,4224]{1,0:T(8,128)(2,1)S(1)} %collective-permute-done.11, f32[28]{0:T(128)} %get-tuple-element.52, f32[28,8320]{1,0:T(8,128)S(1)} %convert_element_type.302, f32[28]{0:T(128)} %get-tuple-element.54, f32[28,8320]{1,0:T(8,128)S(1)} %convert_element_type.286, ...), kind=kLoop, calls=%fused_computation.274 | loop fusion | flops 1032192 | bytes 1835235 | tf_op jit(solution)/shard_map/jvp()/convert_element_type | solution.py:98
  98.5 1.9 %multiply_reduce_fusion.4 = (f32[28]{0:T(128)}, bf16[28,4096]{1,0:T(8,128)(2,1)S(1)}) fusion(f32[28,4096]{1,0:T(8,128)S(1)} %get-tuple-element.62, bf16[28,4224]{1,0:T(8,128)(2,1)} %copy-done.9, f32[28]{0:T(128)S(1)} %copy-done.46, f32[28,8320]{1,0:T(8,128)S(1)} %convert_element_type.302, f32[28]{0:T(128)S(1)} %copy-done.47, ...), kind=kLoop, calls=%fused_computation.69 | loop fusion | flops 1261540 | bytes 1835347 | tf_op jit(solution)/shard_map/reduce_sum | solution.py:266
  104.0 0.8 fusion.141
  104.9 0.8 fusion.140
  106.0 1.6 %fusion.21 = f32[128,28,64]{0,2,1:T(8,128)S(1)} fusion(bf16[28,64,64]{2,1,0:T(8,128)(2,1)S(1)} %reshape.291, bf16[128,28,64]{0,2,1:T(8,128)(2,1)} %fusion.17, f32[28,128]{1,0:T(8,128)S(1)} %copy.82, f32[28,64]{1,0:T(8,128)S(1)} %copy-done.28, f32[28,128]{1,0:T(8,128)S(1)} %copy.77, f32[128,64]{0,1:T(8,128)S(1)} %copy-done.16, f32[128,28]{0,1:T(8,128)S(1)} %copy-done.20), kind=kOutput, calls=%fused_computation.31 | convolution fusion | flops 32112640 | bytes 1688576 | tf_op jit(solution)/shard_map/transpose(jvp(thn,thp->hnp))/dot_general | solution.py:33
  109.0 1.0 collective-permute-start.20
  110.3 1.3 collective-permute-start.13
  111.6 1.9 %collective-permute-start.19 = (bf16[32,1920]{1,0:T(8,128)(2,1)S(1)}, bf16[32,1920]{1,0:T(8,128)(2,1)S(1)}, u32[]{:S(2)}, u32[]{:S(2)}) collective-permute-start(bf16[32,1920]{1,0:T(8,128)(2,1)S(1)} %get-tuple-element.100), channel_id=1, source_target_pairs={{0,12},{2,14},{4,0},{6,2},{8,4},{10,6},{12,8},{14,10},{1,13},{3,15... | collective-permute-start | bytes 368648 | tf_op jit(solution)/shard_map/ppermute | solution.py:18
  114.0 3.0 %collective-permute-start.17 = (bf16[32,1920]{1,0:T(8,128)(2,1)S(1)}, bf16[32,1920]{1,0:T(8,128)(2,1)S(1)}, u32[]{:S(2)}, u32[]{:S(2)}) collective-permute-start(bf16[32,1920]{1,0:T(8,128)(2,1)S(1)} %get-tuple-element.98), channel_id=1, source_target_pairs={{0,8},{2,10},{4,12},{6,14},{8,0},{10,2},{12,4},{14,6},{1,9},{3,11}... | collective-permute-start | bytes 368648 | tf_op jit(solution)/shard_map/ppermute | solution.py:18
  118.4 13.8 %collective-permute-done.18 = bf16[32,1920]{1,0:T(8,128)(2,1)S(1)} collective-permute-done((bf16[32,1920]{1,0:T(8,128)(2,1)S(1)}, bf16[32,1920]{1,0:T(8,128)(2,1)S(1)}, u32[]{:S(2)}, u32[]{:S(2)}) %collective-permute-start.18) | collective-permute-done | bytes 122912 | tf_op jit(solution)/shard_map/ppermute | solution.py:18
  132.2 0.8 collective-permute-done.17
  133.0 4.1 %collective-permute-done.14 = bf16[32,1920]{1,0:T(8,128)(2,1)S(1)} collective-permute-done((bf16[32,1920]{1,0:T(8,128)(2,1)S(1)}, bf16[32,1920]{1,0:T(8,128)(2,1)S(1)}, u32[]{:S(2)}, u32[]{:S(2)}) %collective-permute-start.14) | collective-permute-done | bytes 122912 | tf_op jit(solution)/shard_map/ppermute | solution.py:18
  138.7 0.8 fusion.54
  139.5 0.8 copy.148
  (244 shorter events, 21.3 us)
Async XLA Ops:
  0.6 16.0 %copy-start.11 = (bf16[1,128,1792]{2,1,0:T(8,128)(2,1)S(1)}, bf16[1,128,1792]{2,1,0:T(8,128)(2,1)}, u32[]{:S(2)}) copy-start(bf16[1,128,1792]{2,1,0:T(8,128)(2,1)} %param.11) | copy-start | bytes 1376260
  0.6 22.7 %collective-permute-start = (bf16[32,1792]{1,0:T(8,128)(2,1)}, bf16[32,1792]{1,0:T(8,128)(2,1)}, u32[]{:S(2)}, u32[]{:S(2)}) collective-permute-start(bf16[32,1792]{1,0:T(8,128)(2,1)} %bitcast.346), channel_id=1, source_target_pairs={{0,2},{2,4},{4,6},{6,8},{8,10},{10,12},{12,14},{14,0},{1,3},{3,5},... | collective-permute-start | bytes 344072 | tf_op jit(solution)/shard_map/ppermute | solution.py:18
  2.2 25.2 %collective-permute-start.1 = (bf16[32,1792]{1,0:T(8,128)(2,1)}, bf16[32,1792]{1,0:T(8,128)(2,1)S(1)}, u32[]{:S(2)}, u32[]{:S(2)}) collective-permute-start(bf16[32,1792]{1,0:T(8,128)(2,1)} %bitcast.347), channel_id=1, source_target_pairs={{0,4},{2,6},{4,8},{6,10},{8,12},{10,14},{12,0},{14,2},{1,5},{3,7},... | collective-permute-start | bytes 344072 | tf_op jit(solution)/shard_map/ppermute | solution.py:18
  3.8 23.8 %collective-permute-start.2 = (bf16[32,1792]{1,0:T(8,128)(2,1)}, bf16[32,1792]{1,0:T(8,128)(2,1)S(1)}, u32[]{:S(2)}, u32[]{:S(2)}) collective-permute-start(bf16[32,1792]{1,0:T(8,128)(2,1)} %bitcast.348), channel_id=1, source_target_pairs={{0,6},{2,8},{4,10},{6,12},{8,14},{10,0},{12,2},{14,4},{1,7},{3,9},... | collective-permute-start | bytes 344072 | tf_op jit(solution)/shard_map/ppermute | solution.py:18
  6.3 21.3 %collective-permute-start.3 = (bf16[32,1792]{1,0:T(8,128)(2,1)}, bf16[32,1792]{1,0:T(8,128)(2,1)S(1)}, u32[]{:S(2)}, u32[]{:S(2)}) collective-permute-start(bf16[32,1792]{1,0:T(8,128)(2,1)} %bitcast.349), channel_id=1, source_target_pairs={{0,8},{2,10},{4,12},{6,14},{8,0},{10,2},{12,4},{14,6},{1,9},{3,11}... | collective-permute-start | bytes 344072 | tf_op jit(solution)/shard_map/ppermute | solution.py:18
  7.9 10.8 %collective-permute-start.8 = (s32[1]{0:T(128)}, s32[1]{0:T(128)}, u32[]{:S(2)}, u32[]{:S(2)}) collective-permute-start(s32[1]{0:T(128)} %bitcast.13), channel_id=1, source_target_pairs={{0,2},{2,4},{4,6},{6,8},{8,10},{10,12},{12,14},{1,3},{3,5},{5,7},{... | collective-permute-start | bytes 20 | tf_op jit(solution)/shard_map/ppermute | solution.py:12
  14.0 34.5 %copy-start.27 = (f32[28,64]{1,0:T(8,128)}, f32[28,64]{1,0:T(8,128)S(1)}, u32[]{:S(2)}) copy-start(f32[28,64]{1,0:T(8,128)S(1)} %reshape_squeeze.7) | copy-start | bytes 21508
  14.7 7.8 %copy-start.57 = (f32[28]{0:T(128)}, f32[28]{0:T(128)S(1)}, u32[]{:S(2)}) copy-start(f32[28]{0:T(128)S(1)} %negate_bitcast_fusion) | copy-start | bytes 340
  14.7 3.3 %copy-start.40 = (s32[1,128]{1,0:T(1,128)S(1)}, s32[1,128]{1,0:T(1,128)}, u32[]{:S(2)}) copy-start(s32[1,128]{1,0:T(1,128)} %param.10) | copy-start | bytes 1540
  14.7 4.0 %copy-start.18 = (bf16[1,32,1792]{2,1,0:T(8,128)(2,1)S(1)}, bf16[1,32,1792]{2,1,0:T(8,128)(2,1)}, u32[]{:S(2)}) copy-start(bf16[1,32,1792]{2,1,0:T(8,128)(2,1)} %param.12) | copy-start | bytes 344068
  14.7 7.9 %copy-start.30 = (f32[1,28]{1,0:T(1,128)S(1)}, f32[1,28]{1,0:T(1,128)}, u32[]{:S(2)}) copy-start(f32[1,28]{1,0:T(1,128)} %param.14) | copy-start | bytes 340
  16.0 29.9 %copy-start.2 = (bf16[1,128,1792]{1,2,0:T(8,128)(2,1)}, bf16[1,128,1792]{1,2,0:T(8,128)(2,1)S(1)}, u32[]{:S(2)}) copy-start(bf16[1,128,1792]{1,2,0:T(8,128)(2,1)S(1)} %copy.66) | copy-start | bytes 1376260
  16.9 16.3 %copy-start.4 = (bf16[1,128,1792]{2,1,0:T(8,128)(2,1)S(1)}, bf16[1,128,1792]{2,1,0:T(8,128)(2,1)}, u32[]{:S(2)}) copy-start(bf16[1,128,1792]{2,1,0:T(8,128)(2,1)} %param.9) | copy-start | bytes 1376260
  18.7 9.0 %collective-permute-start.4 = (bf16[32,1792]{1,0:T(8,128)(2,1)S(1)}, bf16[32,1792]{1,0:T(8,128)(2,1)S(1)}, u32[]{:S(2)}, u32[]{:S(2)}) collective-permute-start(bf16[32,1792]{1,0:T(8,128)(2,1)S(1)} %bitcast.350), channel_id=1, source_target_pairs={{0,10},{2,12},{4,14},{6,0},{8,2},{10,4},{12,6},{14,8},{1,11},{3,13... | collective-permute-start | bytes 344072 | tf_op jit(solution)/shard_map/ppermute | solution.py:18
  22.5 10.7 %copy-start.34 = (pred[128]{0:T(512)(128)(4,1)}, pred[128]{0:T(512)(128)(4,1)S(1)}, u32[]{:S(2)}) copy-start(pred[128]{0:T(512)(128)(4,1)S(1)} %get-tuple-element.78) | copy-start | bytes 388
  22.5 10.7 %copy-start.37 = (f32[128]{0:T(128)}, f32[128]{0:T(128)S(1)}, u32[]{:S(2)}) copy-start(f32[128]{0:T(128)S(1)} %get-tuple-element.79) | copy-start | bytes 1540
  23.1 10.6 %copy-start.25 = (f32[128,28]{0,1:T(8,128)}, f32[128,28]{0,1:T(8,128)S(1)}, u32[]{:S(2)}) copy-start(f32[128,28]{0,1:T(8,128)S(1)} %get-tuple-element.111) | copy-start | bytes 43012
  23.1 12.0 %copy-start.21 = (f32[128,28]{0,1:T(8,128)}, f32[128,28]{0,1:T(8,128)S(1)}, u32[]{:S(2)}) copy-start(f32[128,28]{0,1:T(8,128)S(1)} %get-tuple-element.110) | copy-start | bytes 43012
  23.2 10.0 %copy-start.43 = (f32[28]{0:T(128)}, f32[28]{0:T(128)S(1)}, u32[]{:S(2)}) copy-start(f32[28]{0:T(128)S(1)} %slice_bitcast_fusion.7) | copy-start | bytes 340
  23.4 5.5 %collective-permute-start.5 = (bf16[32,1792]{1,0:T(8,128)(2,1)S(1)}, bf16[32,1792]{1,0:T(8,128)(2,1)S(1)}, u32[]{:S(2)}, u32[]{:S(2)}) collective-permute-start(bf16[32,1792]{1,0:T(8,128)(2,1)S(1)} %bitcast.351), channel_id=1, source_target_pairs={{0,12},{2,14},{4,0},{6,2},{8,4},{10,6},{12,8},{14,10},{1,13},{3,15... | collective-permute-start | bytes 344072 | tf_op jit(solution)/shard_map/ppermute | solution.py:18
  27.4 5.7 %collective-permute-start.6 = (bf16[32,1792]{1,0:T(8,128)(2,1)S(1)}, bf16[32,1792]{1,0:T(8,128)(2,1)S(1)}, u32[]{:S(2)}, u32[]{:S(2)}) collective-permute-start(bf16[32,1792]{1,0:T(8,128)(2,1)S(1)} %bitcast.352), channel_id=1, source_target_pairs={{0,14},{2,0},{4,2},{6,4},{8,6},{10,8},{12,10},{14,12},{1,15},{3,1}... | collective-permute-start | bytes 344072 | tf_op jit(solution)/shard_map/ppermute | solution.py:18
  33.7 1.3 collective-permute-start.7
  33.8 27.5 %copy-start.52 = (f32[28]{0:T(128)}, f32[28]{0:T(128)S(1)}, u32[]{:S(2)}) copy-start(f32[28]{0:T(128)S(1)} %exponential_multiply_fusion.1) | copy-start | bytes 340
  34.0 3.3 %copy-start.19 = (f32[128,28]{0,1:T(8,128)}, f32[128,28]{0,1:T(8,128)S(1)}, u32[]{:S(2)}) copy-start(f32[128,28]{0,1:T(8,128)S(1)} %copy.69) | copy-start | bytes 43012
  37.3 3.5 %copy-start.31 = (f32[1,28]{1,0:T(1,128)S(1)}, f32[1,28]{1,0:T(1,128)}, u32[]{:S(2)}) copy-start(f32[1,28]{1,0:T(1,128)} %param.14) | copy-start | bytes 340
  37.3 3.8 %copy-start.6 = (f32[128,28,64]{0,2,1:T(8,128)S(1)}, f32[128,28,64]{0,2,1:T(8,128)}, u32[]{:S(2)}) copy-start(f32[128,28,64]{0,2,1:T(8,128)} %convert.61) | copy-start | bytes 2752516
  37.4 3.8 %copy-start.29 = (pred[128,128]{1,0:T(8,128)(4,1)S(1)}, pred[128,128]{1,0:T(8,128)(4,1)}, u32[]{:S(2)}) copy-start(pred[128,128]{1,0:T(8,128)(4,1)} %get-tuple-element.107) | copy-start | bytes 49156
  39.0 22.6 %copy-start.13 = (bf16[28,126]{1,0:T(8,128)(2,1)}, bf16[28,126]{1,0:T(8,128)(2,1)S(1)}, u32[]{:S(2)}) copy-start(bf16[28,126]{1,0:T(8,128)(2,1)S(1)} %broadcast.164) | copy-start | bytes 21172
  41.2 3.9 %copy-start.10 = (bf16[28,8320]{1,0:T(8,128)(2,1)S(1)}, bf16[28,8320]{1,0:T(8,128)(2,1)}, u32[]{:S(2)}) copy-start(bf16[28,8320]{1,0:T(8,128)(2,1)} %concatenate.64) | copy-start | bytes 1397764
  44.0 4.0 %copy-start.53 = (f32[1,28]{1,0:T(1,128)S(1)}, f32[1,28]{1,0:T(1,128)}, u32[]{:S(2)}) copy-start(f32[1,28]{1,0:T(1,128)} %param.16) | copy-start | bytes 340
  44.0 4.5 %copy-start.23 = (f32[128,128]{1,0:T(8,128)S(1)}, f32[128,128]{1,0:T(8,128)}, u32[]{:S(2)}) copy-start(f32[128,128]{1,0:T(8,128)} %get-tuple-element.108) | copy-start | bytes 196612
  45.1 14.2 %collective-permute-start.9 = (bf16[28,8320]{1,0:T(8,128)(2,1)S(1)}, bf16[28,8320]{1,0:T(8,128)(2,1)S(1)}, u32[]{:S(2)}, u32[]{:S(2)}) collective-permute-start(bf16[28,8320]{1,0:T(8,128)(2,1)S(1)} %copy-done.10), channel_id=1, source_target_pairs={{0,2},{2,0},{4,6},{6,4},{8,10},{10,8},{12,14},{14,12},{1,3},{3,1},... | collective-permute-start | bytes 1397768 | tf_op jit(solution)/shard_map/ppermute | solution.py:150
  62.5 13.5 %collective-permute-start.10 = (bf16[28,8320]{1,0:T(8,128)(2,1)S(1)}, bf16[28,8320]{1,0:T(8,128)(2,1)}, u32[]{:S(2)}, u32[]{:S(2)}) collective-permute-start(bf16[28,8320]{1,0:T(8,128)(2,1)S(1)} %concatenate.65), channel_id=1, source_target_pairs={{0,4},{2,6},{4,0},{6,2},{8,12},{10,14},{12,8},{14,10},{1,5},{3,7},... | collective-permute-start | bytes 1397768 | tf_op jit(solution)/shard_map/ppermute | solution.py:150
  79.7 3.6 %copy-start.22 = (f32[128,28]{0,1:T(8,128)S(1)}, f32[128,28]{0,1:T(8,128)}, u32[]{:S(2)}) copy-start(f32[128,28]{0,1:T(8,128)} %copy-done.21) | copy-start | bytes 43012
  81.5 16.9 %copy-start.46 = (f32[28]{0:T(128)S(1)}, f32[28]{0:T(128)}, u32[]{:S(2)}) copy-start(f32[28]{0:T(128)} %get-tuple-element.53) | copy-start | bytes 340
  81.6 16.9 %copy-start.47 = (f32[28]{0:T(128)S(1)}, f32[28]{0:T(128)}, u32[]{:S(2)}) copy-start(f32[28]{0:T(128)} %get-tuple-element.56) | copy-start | bytes 340
  82.6 13.6 %collective-permute-start.11 = (bf16[28,4224]{1,0:T(8,128)(2,1)S(1)}, bf16[28,4224]{1,0:T(8,128)(2,1)S(1)}, u32[]{:S(2)}, u32[]{:S(2)}) collective-permute-start(bf16[28,4224]{1,0:T(8,128)(2,1)S(1)} %concatenate.66), channel_id=1, source_target_pairs={{0,8},{2,10},{4,12},{6,14},{8,0},{10,2},{12,4},{14,6},{1,9},{3,11}... | collective-permute-start | bytes 709640 | tf_op jit(solution)/shard_map/ppermute | solution.py:157
  102.8 3.2 %copy-start.16 = (f32[128,64]{0,1:T(8,128)S(1)}, f32[128,64]{0,1:T(8,128)}, u32[]{:S(2)}) copy-start(f32[128,64]{0,1:T(8,128)} %copy-done.14) | copy-start | bytes 98308
  102.8 3.2 %copy-start.28 = (f32[28,64]{1,0:T(8,128)S(1)}, f32[28,64]{1,0:T(8,128)}, u32[]{:S(2)}) copy-start(f32[28,64]{1,0:T(8,128)} %copy-done.27) | copy-start | bytes 21508
  103.9 4.1 %collective-permute-start.12 = (bf16[128,128]{0,1:T(8,128)(2,1)S(1)}, bf16[128,128]{0,1:T(8,128)(2,1)S(1)}, u32[]{:S(2)}, u32[]{:S(2)}) collective-permute-start(bf16[128,128]{0,1:T(8,128)(2,1)S(1)} %add_convert_fusion), channel_id=1, source_target_pairs={{0,1},{1,0},{2,3},{3,2},{4,5},{5,4},{6,7},{7,6},{8,9},{9,8},{10,11... | collective-permute-start | bytes 98312 | tf_op jit(solution)/shard_map/ppermute | solution.py:29
  109.0 7.9 %collective-permute-start.20 = (bf16[32,1920]{1,0:T(8,128)(2,1)S(1)}, bf16[32,1920]{1,0:T(8,128)(2,1)S(1)}, u32[]{:S(2)}, u32[]{:S(2)}) collective-permute-start(bf16[32,1920]{1,0:T(8,128)(2,1)S(1)} %get-tuple-element.101), channel_id=1, source_target_pairs={{0,14},{2,0},{4,2},{6,4},{8,6},{10,8},{12,10},{14,12},{1,15},{3,1}... | collective-permute-start | bytes 368648 | tf_op jit(solution)/shard_map/ppermute | solution.py:18
  110.3 29.2 %collective-permute-start.13 = (bf16[1,128,1792]{2,1,0:T(8,128)(2,1)S(1)}, bf16[1,128,1792]{2,1,0:T(8,128)(2,1)S(1)}, u32[]{:S(2)}, u32[]{:S(2)}) collective-permute-start(bf16[1,128,1792]{2,1,0:T(8,128)(2,1)S(1)} %fusion.1), channel_id=1, source_target_pairs={{16,0},{17,1},{18,2},{19,3},{20,4},{21,5},{22,6},{23,7},{24,8},{25... | collective-permute-start | bytes 1376264 | tf_op jit(solution)/shard_map/ppermute | solution.py:12
  111.6 6.2 %collective-permute-start.19 = (bf16[32,1920]{1,0:T(8,128)(2,1)S(1)}, bf16[32,1920]{1,0:T(8,128)(2,1)S(1)}, u32[]{:S(2)}, u32[]{:S(2)}) collective-permute-start(bf16[32,1920]{1,0:T(8,128)(2,1)S(1)} %get-tuple-element.100), channel_id=1, source_target_pairs={{0,12},{2,14},{4,0},{6,2},{8,4},{10,6},{12,8},{14,10},{1,13},{3,15... | collective-permute-start | bytes 368648 | tf_op jit(solution)/shard_map/ppermute | solution.py:18
  113.5 18.7 %collective-permute-start.18 = (bf16[32,1920]{1,0:T(8,128)(2,1)S(1)}, bf16[32,1920]{1,0:T(8,128)(2,1)S(1)}, u32[]{:S(2)}, u32[]{:S(2)}) collective-permute-start(bf16[32,1920]{1,0:T(8,128)(2,1)S(1)} %get-tuple-element.99), channel_id=1, source_target_pairs={{0,10},{2,12},{4,14},{6,0},{8,2},{10,4},{12,6},{14,8},{1,11},{3,13... | collective-permute-start | bytes 368648 | tf_op jit(solution)/shard_map/ppermute | solution.py:18
  114.0 19.0 %collective-permute-start.17 = (bf16[32,1920]{1,0:T(8,128)(2,1)S(1)}, bf16[32,1920]{1,0:T(8,128)(2,1)S(1)}, u32[]{:S(2)}, u32[]{:S(2)}) collective-permute-start(bf16[32,1920]{1,0:T(8,128)(2,1)S(1)} %get-tuple-element.98), channel_id=1, source_target_pairs={{0,8},{2,10},{4,12},{6,14},{8,0},{10,2},{12,4},{14,6},{1,9},{3,11}... | collective-permute-start | bytes 368648 | tf_op jit(solution)/shard_map/ppermute | solution.py:18
  116.9 16.0 %collective-permute-start.16 = (bf16[32,1920]{1,0:T(8,128)(2,1)S(1)}, bf16[32,1920]{1,0:T(8,128)(2,1)S(1)}, u32[]{:S(2)}, u32[]{:S(2)}) collective-permute-start(bf16[32,1920]{1,0:T(8,128)(2,1)S(1)} %get-tuple-element.97), channel_id=1, source_target_pairs={{0,6},{2,8},{4,10},{6,12},{8,14},{10,0},{12,2},{14,4},{1,7},{3,9},... | collective-permute-start | bytes 368648 | tf_op jit(solution)/shard_map/ppermute | solution.py:18
  117.8 15.2 %collective-permute-start.15 = (bf16[32,1920]{1,0:T(8,128)(2,1)S(1)}, bf16[32,1920]{1,0:T(8,128)(2,1)S(1)}, u32[]{:S(2)}, u32[]{:S(2)}) collective-permute-start(bf16[32,1920]{1,0:T(8,128)(2,1)S(1)} %get-tuple-element.96), channel_id=1, source_target_pairs={{0,4},{2,6},{4,8},{6,10},{8,12},{10,14},{12,0},{14,2},{1,5},{3,7},... | collective-permute-start | bytes 368648 | tf_op jit(solution)/shard_map/ppermute | solution.py:18
  132.2 4.9 %collective-permute-start.14 = (bf16[32,1920]{1,0:T(8,128)(2,1)S(1)}, bf16[32,1920]{1,0:T(8,128)(2,1)S(1)}, u32[]{:S(2)}, u32[]{:S(2)}) collective-permute-start(bf16[32,1920]{1,0:T(8,128)(2,1)S(1)} %get-tuple-element.95), channel_id=1, source_target_pairs={{0,2},{2,4},{4,6},{6,8},{8,10},{10,12},{12,14},{14,0},{1,3},{3,5},... | collective-permute-start | bytes 368648 | tf_op jit(solution)/shard_map/ppermute | solution.py:18
  (32 other events, 60.7 us)

commit v17 on v11

--- a/solution.py
+++ b/solution.py
@@ -142,8 +142,6 @@
             [total_fwd, total_bwd, high[:, None], low[:, None], pad], axis=1
         ).astype(jnp.bfloat16)
         upper = (mine // distance) % 2 == 1
-        if distance == 1:
-            payload, filler_args = lax.optimization_barrier((payload, filler_args))
         if distance * 2 < size:
             got = lax.ppermute(payload, axis, [(i, i ^ distance) for i in range(size)])
             got = got.astype(jnp.float32)
@@ -158,6 +156,8 @@
             got_bwd = got_fwd
             got = jnp.concatenate([got[:, :width], got], axis=1)
         if distance == 1:
+            got, filler_args = lax.optimization_barrier((got, filler_args))
+        if distance * 2 >= size:
             got, filler = lax.optimization_barrier((got, filler_fn(*filler_args)))
         got_decay = got[:, 2 * width] + got[:, 2 * width + 1]
         before = jnp.where(upper, before + before_decay[:, None] * got_fwd, before)

time: 141 us -> 147 us (1.043)
  waiting for transfers between devices: 64.2 us -> 54.7 us
  matrix products: 16.6 us -> 22.8 us
  other arithmetic: 13.4 us -> 18.7 us
  starting transfers between devices: 26.4 us -> 29.4 us
    ppermute x2, waiting for transfers between devices: 26.3 us -> 18.7 us  [both_scans(): got = lax.ppermute(payload, axis, [(i, i ^ distance) for i in range(size)])]
    ppermute x14, starting transfers between devices: 19.8 us -> 22.9 us  [rotated(): return lax.ppermute(block, axis, route)]
    ppermute x1, waiting for transfers between devices: 12.3 us -> 9.61 us  [both_scans(): got = lax.ppermute(last, axis, [(i, i ^ distance) for i in range(size)])]
    dot_general x5, matrix products: 6.83 us -> 8.94 us  [contract(): return jnp.einsum(spec, left, right, preferred_element_type=jnp.float32)]
    another operation x6, other arithmetic: 0.41 us -> 2.37 us
    dot_general x5, matrix products: 1.23 us -> 3.17 us  [local_setup(): cumulative = jnp.dot(triangle, decay_log, precision=EXACT)]
    reduce_sum x1, other arithmetic: 0.3 us -> 2.02 us  [span_local(): values.astype(jnp.float32) * (1.0 + skip_gain)[None, :, None] + local_part]
    unnamed x141 -> x157, local copies, waits for them, and re-layouts: 4.31 us -> 4.94 us
  transfers between devices with their start and end apart: 21 -> 21, of which waited for: 10 -> 9; matrix products, arithmetic and copies ran while one was open for 15% -> 18% of each run, Pallas kernels for 0% -> 0%
where the time goes in v17:
time: 147 us; the launch traced here: 146 us
  waiting for transfers between devices  54.7 us (37%)
  starting transfers between devices  29.4 us (20%)
  matrix products  22.8 us (16%)
  other arithmetic  18.7 us (13%)
  local copies, waits for them, and re-layouts  17.1 us (12%)
  between operations  3.07 us (2%)
    ppermute x14, starting transfers between devices, rotated(): return lax.ppermute(block, axis, route)  22.9 us
    ppermute x2, waiting for transfers between devices, both_scans(): got = lax.ppermute(payload, axis, [(i, i ^ distance) for i in range(size)])  18.7 us
    ppermute x14, waiting for transfers between devices, rotated(): return lax.ppermute(block, axis, route)  17.9 us
    ppermute x1, waiting for transfers between devices, both_scans(): got = lax.ppermute(last, axis, [(i, i ^ distance) for i in range(size)])  9.61 us
    dot_general x5, matrix products, contract(): return jnp.einsum(spec, left, right, preferred_element_type=jnp.float32)  8.94 us
    ppermute x2, waiting for transfers between devices, shifted(): return lax.ppermute(block, axis, route)  7.66 us
    ppermute x2, starting transfers between devices, shifted(): return lax.ppermute(block, axis, route)  5.6 us
    unnamed x157, local copies, waits for them, and re-layouts  4.94 us
  transfers between devices with their start and end apart: 21, of which 9 were waited for; matrix products, arithmetic and copies ran while one was open for 18% of the time, Pallas kernels for 0%

profile of v17, /device:TPU:4, one launch (start us, length us, event | category | flops | bytes accessed | tf_op | source)
XLA Modules:
  0.0 145.9 jit_solution(11209306184834239477)
XLA Ops:
  0.7 1.6 %collective-permute-start = (bf16[32,1792]{1,0:T(8,128)(2,1)}, bf16[32,1792]{1,0:T(8,128)(2,1)}, u32[]{:S(2)}, u32[]{:S(2)}) collective-permute-start(bf16[32,1792]{1,0:T(8,128)(2,1)} %bitcast.346), channel_id=1, source_target_pairs={{0,2},{2,4},{4,6},{6,8},{8,10},{10,12},{12,14},{14,0},{1,3},{3,5},... | collective-permute-start | bytes 344072 | tf_op jit(solution)/shard_map/ppermute | solution.py:18
  2.2 1.6 %collective-permute-start.1 = (bf16[32,1792]{1,0:T(8,128)(2,1)}, bf16[32,1792]{1,0:T(8,128)(2,1)S(1)}, u32[]{:S(2)}, u32[]{:S(2)}) collective-permute-start(bf16[32,1792]{1,0:T(8,128)(2,1)} %bitcast.347), channel_id=1, source_target_pairs={{0,4},{2,6},{4,8},{6,10},{8,12},{10,14},{12,0},{14,2},{1,5},{3,7},... | collective-permute-start | bytes 344072 | tf_op jit(solution)/shard_map/ppermute | solution.py:18
  3.8 2.5 %collective-permute-start.2 = (bf16[32,1792]{1,0:T(8,128)(2,1)}, bf16[32,1792]{1,0:T(8,128)(2,1)S(1)}, u32[]{:S(2)}, u32[]{:S(2)}) collective-permute-start(bf16[32,1792]{1,0:T(8,128)(2,1)} %bitcast.348), channel_id=1, source_target_pairs={{0,6},{2,8},{4,10},{6,12},{8,14},{10,0},{12,2},{14,4},{1,7},{3,9},... | collective-permute-start | bytes 344072 | tf_op jit(solution)/shard_map/ppermute | solution.py:18
  6.7 1.2 slice.180
  7.9 4.3 %collective-permute-start.8 = (s32[1]{0:T(128)}, s32[1]{0:T(128)}, u32[]{:S(2)}, u32[]{:S(2)}) collective-permute-start(s32[1]{0:T(128)} %bitcast.13), channel_id=1, source_target_pairs={{0,2},{2,4},{4,6},{6,8},{8,10},{10,12},{12,14},{1,3},{3,5},{5,7},{... | collective-permute-start | bytes 20 | tf_op jit(solution)/shard_map/ppermute | solution.py:12
  12.3 0.9 constant_dynamic-update-slice_fusion.7
  13.2 1.3 copy.66
  16.9 1.3 collective-permute-start.4
  18.2 1.2 broadcast_compare_fusion.1
  21.2 6.2 %collective-permute-start.5 = (bf16[32,1792]{1,0:T(8,128)(2,1)S(1)}, bf16[32,1792]{1,0:T(8,128)(2,1)S(1)}, u32[]{:S(2)}, u32[]{:S(2)}) collective-permute-start(bf16[32,1792]{1,0:T(8,128)(2,1)S(1)} %bitcast.351), channel_id=1, source_target_pairs={{0,12},{2,14},{4,0},{6,2},{8,4},{10,6},{12,8},{14,10},{1,13},{3,15... | collective-permute-start | bytes 344072 | tf_op jit(solution)/shard_map/ppermute | solution.py:18
  27.4 0.9 constant_dynamic-update-slice_fusion.6
  28.4 1.3 collective-permute-done.5
  29.7 4.3 %collective-permute-done.6 = bf16[32,1792]{1,0:T(8,128)(2,1)S(1)} collective-permute-done((bf16[32,1792]{1,0:T(8,128)(2,1)S(1)}, bf16[32,1792]{1,0:T(8,128)(2,1)S(1)}, u32[]{:S(2)}, u32[]{:S(2)}) %collective-permute-start.6) | collective-permute-done | bytes 114720 | tf_op jit(solution)/shard_map/ppermute | solution.py:18
  35.0 0.9 collective-permute-done.7
  35.9 1.3 fusion.33
  37.3 1.5 %reshape.285 = f32[28,4096]{1,0:T(8,128)S(1)} reshape(f32[28,64,64]{2,1,0:T(8,128)} %fusion.33) | data formatting | bytes 917504 | tf_op jit(solution)/shard_map/reshape | solution.py:223
  38.8 1.5 %convolution_bitcast_fusion = f32[28,64,64]{1,2,0:T(8,128)} fusion(f32[128,28]{0,1:T(8,128)S(1)} %get-tuple-element.107, bf16[128,128]{0,1:T(8,128)(2,1)S(1)} %fusion.61, bf16[128,28,64]{0,2,1:T(8,128)(2,1)S(1)} %bitcast.320), kind=kOutput, calls=%fused_computation.19 | convolution fusion | flops 176619520 | bytes 950272 | tf_op jit(solution)/shard_map/transpose(jvp(tn,hnp->thp))/dot_general | solution.py:97
  40.3 1.5 %copy.71 = f32[28,64,64]{2,1,0:T(8,128)S(1)} copy(f32[28,64,64]{1,2,0:T(8,128)} %convolution_bitcast_fusion) | data formatting | bytes 917504 | tf_op jit(solution)/shard_map/transpose(jvp(tn,hnp->thp))/transpose | solution.py:97
  42.7 1.0 convert.62
  44.1 1.0 bitcast_multiply_fusion
  45.6 11.3 %collective-permute-done.9 = bf16[28,8320]{1,0:T(8,128)(2,1)} collective-permute-done((bf16[28,8320]{1,0:T(8,128)(2,1)S(1)}, bf16[28,8320]{1,0:T(8,128)(2,1)}, u32[]{:S(2)}, u32[]{:S(2)}) %collective-permute-start.9) | collective-permute-done | bytes 465952 | tf_op jit(solution)/shard_map/ppermute | solution.py:146
  57.0 1.1 convert_element_type.271
  59.2 2.5 %fusion.12 = (f32[28,128]{1,0:T(8,128)}, f32[28,128]{1,0:T(8,128)}, f32[28,128]{1,0:T(8,128)}, bf16[128,128]{1,0:T(8,128)(2,1)S(1)}) fusion(f32[28,128]{1,0:T(8,128)S(1)} %fusion.118, f32[128,128]{1,0:T(8,128)S(1)} %fusion.102, f32[128,128]{1,0:T(8,128)S(1)} %get-tuple-element.105, f32[28,128]{1,0:T(8,128)S(1)} %fusion.74, ...), kind=kOutput, calls=%fused_computation.18 | convolution fusion | flops 66033152 | bytes 1628160 | tf_op jit(solution)/shard_map/transpose(jvp(hts,shp->thp))/dot_general | solution.py:33
  64.1 1.6 %fusion.120 = (bf16[28,4096]{1,0:T(8,128)(2,1)S(1)}, bf16[28,4096]{1,0:T(8,128)(2,1)}) fusion(f32[28,4096]{1,0:T(8,128)S(1)} %reshape.286, f32[28]{0:T(128)} %exponential_multiply_fusion.1, f32[28]{0:T(128)S(1)} %reduce.3, f32[28,8320]{1,0:T(8,128)S(1)} %convert_element_type.271, pred[]{:T(512)S(6)} %eq.84, f32[28,4096]{1,0:T(8,128)S(1)} %reshape.285), kind=kLoop, calls=%fused_computation.267 | loop fusion | flops 1376256 | bytes 2293985 | tf_op jit(solution)/shard_map/convert.18
  65.7 1.8 %concatenate.66 = bf16[28,8320]{1,0:T(8,128)(2,1)} concatenate(bf16[28,4096]{1,0:T(8,128)(2,1)} %get-tuple-element.78, bf16[28,4096]{1,0:T(8,128)(2,1)S(1)} %get-tuple-element.77, bf16[28,1]{1,0:T(8,128)(2,1)S(1)} %get-tuple-element.72, bf16[28,1]{1,0:T(8,128)(2,1)S(1)} %get-tuple-element.71, bf16[28,126]{1,0:T(8,128)(2,1)S(1)} %broadcast.164), dimensions={1} | concatenate | bytes 931840 | tf_op jit(solution)/shard_map/concatenate | solution.py:141
  67.6 1.6 %fusion.125 = (f32[28]{0:T(128)}, f32[128,28]{0,1:T(8,128)S(1)}, f32[28]{0:T(128)S(1)}) fusion(f32[28]{0:T(128)S(1)} %bitcast.359, f32[28,1,128]{2,1,0:T(1,128)} %copy-done.33, f32[28]{0:T(128)} %copy-done.64, f32[28,128]{1,0:T(8,128)} %get-tuple-element.44, f32[28,128]{1,0:T(8,128)} %get-tuple-element.43, f32[28,128]{1,0:T(8,128)} %get-tuple-element.42), kind=kOutput, calls=%fused_computation.271 | convolution fusion | flops 5593032 | bytes 72128 | tf_op jit(solution)/shard_map/transpose(jvp())/dot_general | solution.py:47
  69.2 0.8 fusion.106
  71.2 2.0 %multiply_reduce_fusion.3 = f32[28]{0:T(128)} fusion(f32[128,28,64]{0,2,1:T(8,128)} %convert.62, bf16[128,28,64]{0,2,1:T(8,128)(2,1)S(1)} %bitcast.328), kind=kLoop, calls=%fused_computation.45 | loop fusion | flops 688100 | bytes 1376368 | tf_op jit(solution)/shard_map/transpose(jvp())/reduce_sum | solution.py:88
  73.8 7.3 %collective-permute-done.10 = bf16[28,8320]{1,0:T(8,128)(2,1)S(1)} collective-permute-done((bf16[28,8320]{1,0:T(8,128)(2,1)}, bf16[28,8320]{1,0:T(8,128)(2,1)S(1)}, u32[]{:S(2)}, u32[]{:S(2)}) %collective-permute-start.10) | collective-permute-done | bytes 465952 | tf_op jit(solution)/shard_map/ppermute | solution.py:146
  81.8 1.3 fusion.80
  85.4 3.2 %fusion.17 = bf16[128,28,64]{0,2,1:T(8,128)(2,1)} fusion(f32[128,28,64]{0,2,1:T(8,128)} %convert.62, f32[28,128]{1,0:T(8,128)} %copy-done.31, f32[128,128]{1,0:T(8,128)} %copy-done.20, f32[128,128]{1,0:T(8,128)} %copy-done.21, f32[28,128]{1,0:T(8,128)} %copy-done.65, pred[128,128]{1,0:T(8,128)(4,1)} %copy-done.32, f32[28,64]{1,0:T(8,128)} %copy-done.29, ...), kind=kOutput, calls=%fused_computation.27 | convolution fusion | flops 63078400 | bytes 1574000 | tf_op jit(solution)/shard_map/transpose(jvp(hts,shp->thp))/dot_general | solution.py:33
  88.6 9.6 %collective-permute-done.11 = bf16[28,4224]{1,0:T(8,128)(2,1)S(1)} collective-permute-done((bf16[28,4224]{1,0:T(8,128)(2,1)S(1)}, bf16[28,4224]{1,0:T(8,128)(2,1)S(1)}, u32[]{:S(2)}, u32[]{:S(2)}) %collective-permute-start.11) | collective-permute-done | bytes 236576 | tf_op jit(solution)/shard_map/ppermute | solution.py:153
  98.2 1.0 multiply_reduce_fusion.4
  102.1 0.9 multiply_reduce_fusion.6
  103.1 0.8 fusion.136
  104.1 0.8 fusion.137
  105.1 1.0 fusion.22
  106.4 1.6 %fusion.21 = f32[128,28,64]{0,2,1:T(8,128)S(1)} fusion(bf16[28,64,64]{2,1,0:T(8,128)(2,1)S(1)} %reshape.288, bf16[128,28,64]{0,2,1:T(8,128)(2,1)} %fusion.17, f32[28,128]{1,0:T(8,128)S(1)} %copy.82, f32[28,64]{1,0:T(8,128)S(1)} %copy-done.30, f32[28,128]{1,0:T(8,128)S(1)} %copy.77, f32[128,64]{0,1:T(8,128)S(1)} %copy-done.15, f32[128,28]{0,1:T(8,128)S(1)} %copy-done.19), kind=kOutput, calls=%fused_computation.31 | convolution fusion | flops 32112640 | bytes 1688576 | tf_op jit(solution)/shard_map/transpose(jvp(thn,thp->hnp))/dot_general | solution.py:33
  108.4 1.8 %fusion.131 = (bf16[256,1792]{1,0:T(8,128)(2,1)S(1)}, f32[256,1792]{1,0:T(8,128)}) fusion(bf16[1,128,1792]{2,1,0:T(8,128)(2,1)S(1)} %copy-done.7, s32[]{:T(128)S(6)} %select_n.220, bf16[128,256]{0,1:T(8,128)(2,1)S(1)} %maximum_select_fusion), kind=kOutput, calls=%fused_computation.276 | convolution fusion | flops 118030336 | bytes 3276804 | tf_op jit(solution)/shard_map/dot_general | solution.py:284
  110.4 1.0 collective-permute-start.20
  111.4 1.8 %collective-permute-start.19 = (bf16[32,1920]{1,0:T(8,128)(2,1)S(1)}, bf16[32,1920]{1,0:T(8,128)(2,1)S(1)}, u32[]{:S(2)}, u32[]{:S(2)}) collective-permute-start(bf16[32,1920]{1,0:T(8,128)(2,1)S(1)} %get-tuple-element.97), channel_id=1, source_target_pairs={{0,12},{2,14},{4,0},{6,2},{8,4},{10,6},{12,8},{14,10},{1,13},{3,15... | collective-permute-start | bytes 368648 | tf_op jit(solution)/shard_map/ppermute | solution.py:18
  113.2 3.4 %collective-permute-start.17 = (bf16[32,1920]{1,0:T(8,128)(2,1)S(1)}, bf16[32,1920]{1,0:T(8,128)(2,1)S(1)}, u32[]{:S(2)}, u32[]{:S(2)}) collective-permute-start(bf16[32,1920]{1,0:T(8,128)(2,1)S(1)} %get-tuple-element.95), channel_id=1, source_target_pairs={{0,8},{2,10},{4,12},{6,14},{8,0},{10,2},{12,4},{14,6},{1,9},{3,11}... | collective-permute-start | bytes 368648 | tf_op jit(solution)/shard_map/ppermute | solution.py:18
  117.6 1.1 collective-permute-start.15
  118.7 1.6 %collective-permute-start.14 = (bf16[32,1920]{1,0:T(8,128)(2,1)S(1)}, bf16[32,1920]{1,0:T(8,128)(2,1)S(1)}, u32[]{:S(2)}, u32[]{:S(2)}) collective-permute-start(bf16[32,1920]{1,0:T(8,128)(2,1)S(1)} %get-tuple-element.92), channel_id=1, source_target_pairs={{0,2},{2,4},{4,6},{6,8},{8,10},{10,12},{12,14},{14,0},{1,3},{3,5},... | collective-permute-start | bytes 368648 | tf_op jit(solution)/shard_map/ppermute | solution.py:18
  120.3 11.8 %collective-permute-done.18 = bf16[32,1920]{1,0:T(8,128)(2,1)S(1)} collective-permute-done((bf16[32,1920]{1,0:T(8,128)(2,1)S(1)}, bf16[32,1920]{1,0:T(8,128)(2,1)S(1)}, u32[]{:S(2)}, u32[]{:S(2)}) %collective-permute-start.18) | collective-permute-done | bytes 122912 | tf_op jit(solution)/shard_map/ppermute | solution.py:18
  132.1 1.3 collective-permute-start.13
  135.7 1.7 %fusion.51 = f32[1,32,1792]{2,1,0:T(8,128)} fusion(f32[256,1792]{1,0:T(8,128)} %get-tuple-element.110, bf16[32,1920]{1,0:T(8,128)(2,1)S(1)} %collective-permute-done.20, bf16[32,1920]{1,0:T(8,128)(2,1)S(1)} %collective-permute-done.19, bf16[32,1920]{1,0:T(8,128)(2,1)S(1)} %collective-permute-done.18, bf16[32,1920]{1,0:T(8,128)(2,1)S(1)} %collective-permute-done.17, ...), kind=kLoop, calls=%fused_computation.97 | loop fusion | flops 802816 | bytes 1261568 | tf_op jit(solution)/shard_map/broadcast_in_dim | solution.py:326
  137.4 7.7 %collective-permute-done.13 = bf16[1,128,1792]{2,1,0:T(8,128)(2,1)S(1)} collective-permute-done((bf16[1,128,1792]{2,1,0:T(8,128)(2,1)S(1)}, bf16[1,128,1792]{2,1,0:T(8,128)(2,1)S(1)}, u32[]{:S(2)}, u32[]{:S(2)}) %collective-permute-start.13) | collective-permute-done | bytes 458784 | tf_op jit(solution)/shard_map/ppermute | solution.py:12
  (258 shorter events, 21.8 us)
Async XLA Ops:
  0.6 16.2 %copy-start.17 = (bf16[1,32,1792]{2,1,0:T(8,128)(2,1)S(1)}, bf16[1,32,1792]{2,1,0:T(8,128)(2,1)}, u32[]{:S(2)}) copy-start(bf16[1,32,1792]{2,1,0:T(8,128)(2,1)} %param.12) | copy-start | bytes 344068
  0.6 17.6 %copy-start.41 = (s32[1,128]{1,0:T(1,128)S(1)}, s32[1,128]{1,0:T(1,128)}, u32[]{:S(2)}) copy-start(s32[1,128]{1,0:T(1,128)} %param.10) | copy-start | bytes 1540
  0.7 15.9 %copy-start.10 = (bf16[1,128,1792]{2,1,0:T(8,128)(2,1)S(1)}, bf16[1,128,1792]{2,1,0:T(8,128)(2,1)}, u32[]{:S(2)}) copy-start(bf16[1,128,1792]{2,1,0:T(8,128)(2,1)} %param.11) | copy-start | bytes 1376260
  0.7 20.0 %copy-start.34 = (f32[1,28]{1,0:T(1,128)S(1)}, f32[1,28]{1,0:T(1,128)}, u32[]{:S(2)}) copy-start(f32[1,28]{1,0:T(1,128)} %param.14) | copy-start | bytes 340
  0.7 20.5 %collective-permute-start = (bf16[32,1792]{1,0:T(8,128)(2,1)}, bf16[32,1792]{1,0:T(8,128)(2,1)}, u32[]{:S(2)}, u32[]{:S(2)}) collective-permute-start(bf16[32,1792]{1,0:T(8,128)(2,1)} %bitcast.346), channel_id=1, source_target_pairs={{0,2},{2,4},{4,6},{6,8},{8,10},{10,12},{12,14},{14,0},{1,3},{3,5},... | collective-permute-start | bytes 344072 | tf_op jit(solution)/shard_map/ppermute | solution.py:18
  2.2 26.0 %collective-permute-start.1 = (bf16[32,1792]{1,0:T(8,128)(2,1)}, bf16[32,1792]{1,0:T(8,128)(2,1)S(1)}, u32[]{:S(2)}, u32[]{:S(2)}) collective-permute-start(bf16[32,1792]{1,0:T(8,128)(2,1)} %bitcast.347), channel_id=1, source_target_pairs={{0,4},{2,6},{4,8},{6,10},{8,12},{10,14},{12,0},{14,2},{1,5},{3,7},... | collective-permute-start | bytes 344072 | tf_op jit(solution)/shard_map/ppermute | solution.py:18
  3.8 24.5 %collective-permute-start.2 = (bf16[32,1792]{1,0:T(8,128)(2,1)}, bf16[32,1792]{1,0:T(8,128)(2,1)S(1)}, u32[]{:S(2)}, u32[]{:S(2)}) collective-permute-start(bf16[32,1792]{1,0:T(8,128)(2,1)} %bitcast.348), channel_id=1, source_target_pairs={{0,6},{2,8},{4,10},{6,12},{8,14},{10,0},{12,2},{14,4},{1,7},{3,9},... | collective-permute-start | bytes 344072 | tf_op jit(solution)/shard_map/ppermute | solution.py:18
  6.4 22.0 %collective-permute-start.3 = (bf16[32,1792]{1,0:T(8,128)(2,1)}, bf16[32,1792]{1,0:T(8,128)(2,1)S(1)}, u32[]{:S(2)}, u32[]{:S(2)}) collective-permute-start(bf16[32,1792]{1,0:T(8,128)(2,1)} %bitcast.349), channel_id=1, source_target_pairs={{0,8},{2,10},{4,12},{6,14},{8,0},{10,2},{12,4},{14,6},{1,9},{3,11}... | collective-permute-start | bytes 344072 | tf_op jit(solution)/shard_map/ppermute | solution.py:18
  7.9 8.9 %collective-permute-start.8 = (s32[1]{0:T(128)}, s32[1]{0:T(128)}, u32[]{:S(2)}, u32[]{:S(2)}) collective-permute-start(s32[1]{0:T(128)} %bitcast.13), channel_id=1, source_target_pairs={{0,2},{2,4},{4,6},{6,8},{8,10},{10,12},{12,14},{1,3},{3,5},{5,7},{... | collective-permute-start | bytes 20 | tf_op jit(solution)/shard_map/ppermute | solution.py:12
  14.5 56.7 %copy-start.4 = (bf16[1,128,1792]{1,2,0:T(8,128)(2,1)}, bf16[1,128,1792]{1,2,0:T(8,128)(2,1)S(1)}, u32[]{:S(2)}) copy-start(bf16[1,128,1792]{1,2,0:T(8,128)(2,1)S(1)} %copy.66) | copy-start | bytes 1376260
  14.5 19.6 %copy-start.6 = (bf16[1,128,1792]{2,1,0:T(8,128)(2,1)S(1)}, bf16[1,128,1792]{2,1,0:T(8,128)(2,1)}, u32[]{:S(2)}) copy-start(bf16[1,128,1792]{2,1,0:T(8,128)(2,1)} %param.9) | copy-start | bytes 1376260
  16.9 11.5 %collective-permute-start.4 = (bf16[32,1792]{1,0:T(8,128)(2,1)S(1)}, bf16[32,1792]{1,0:T(8,128)(2,1)S(1)}, u32[]{:S(2)}, u32[]{:S(2)}) collective-permute-start(bf16[32,1792]{1,0:T(8,128)(2,1)S(1)} %bitcast.350), channel_id=1, source_target_pairs={{0,10},{2,12},{4,14},{6,0},{8,2},{10,4},{12,6},{14,8},{1,11},{3,13... | collective-permute-start | bytes 344072 | tf_op jit(solution)/shard_map/ppermute | solution.py:18
  19.4 15.0 %copy-start.37 = (pred[128]{0:T(512)(128)(4,1)}, pred[128]{0:T(512)(128)(4,1)S(1)}, u32[]{:S(2)}) copy-start(pred[128]{0:T(512)(128)(4,1)S(1)} %get-tuple-element.75) | copy-start | bytes 388
  19.5 15.0 %copy-start.39 = (f32[128]{0:T(128)}, f32[128]{0:T(128)S(1)}, u32[]{:S(2)}) copy-start(f32[128]{0:T(128)S(1)} %get-tuple-element.76) | copy-start | bytes 1540
  20.9 13.5 %copy-start.27 = (f32[128,28]{0,1:T(8,128)}, f32[128,28]{0,1:T(8,128)S(1)}, u32[]{:S(2)}) copy-start(f32[128,28]{0,1:T(8,128)S(1)} %get-tuple-element.108) | copy-start | bytes 43012
  21.1 13.5 %copy-start.46 = (f32[28]{0:T(128)}, f32[28]{0:T(128)S(1)}, u32[]{:S(2)}) copy-start(f32[28]{0:T(128)S(1)} %slice_bitcast_fusion.7) | copy-start | bytes 340
  21.2 8.5 %collective-permute-start.5 = (bf16[32,1792]{1,0:T(8,128)(2,1)S(1)}, bf16[32,1792]{1,0:T(8,128)(2,1)S(1)}, u32[]{:S(2)}, u32[]{:S(2)}) collective-permute-start(bf16[32,1792]{1,0:T(8,128)(2,1)S(1)} %bitcast.351), channel_id=1, source_target_pairs={{0,12},{2,14},{4,0},{6,2},{8,4},{10,6},{12,8},{14,10},{1,13},{3,15... | collective-permute-start | bytes 344072 | tf_op jit(solution)/shard_map/ppermute | solution.py:18
  28.3 5.7 %collective-permute-start.6 = (bf16[32,1792]{1,0:T(8,128)(2,1)S(1)}, bf16[32,1792]{1,0:T(8,128)(2,1)S(1)}, u32[]{:S(2)}, u32[]{:S(2)}) collective-permute-start(bf16[32,1792]{1,0:T(8,128)(2,1)S(1)} %bitcast.352), channel_id=1, source_target_pairs={{0,14},{2,0},{4,2},{6,4},{8,6},{10,8},{12,10},{14,12},{1,15},{3,1}... | collective-permute-start | bytes 344072 | tf_op jit(solution)/shard_map/ppermute | solution.py:18
  34.6 1.3 collective-permute-start.7
  42.1 21.9 %copy-start = (f32[28,4096]{1,0:T(8,128)}, f32[28,4096]{1,0:T(8,128)S(1)}, u32[]{:S(2)}) copy-start(f32[28,4096]{1,0:T(8,128)S(1)} %reshape.286) | copy-start | bytes 1376260
  42.2 23.5 %copy-start.13 = (bf16[28,126]{1,0:T(8,128)(2,1)}, bf16[28,126]{1,0:T(8,128)(2,1)S(1)}, u32[]{:S(2)}) copy-start(bf16[28,126]{1,0:T(8,128)(2,1)S(1)} %broadcast.164) | copy-start | bytes 21172
  42.6 14.3 %collective-permute-start.9 = (bf16[28,8320]{1,0:T(8,128)(2,1)S(1)}, bf16[28,8320]{1,0:T(8,128)(2,1)}, u32[]{:S(2)}, u32[]{:S(2)}) collective-permute-start(bf16[28,8320]{1,0:T(8,128)(2,1)S(1)} %concatenate.65), channel_id=1, source_target_pairs={{0,2},{2,0},{4,6},{6,4},{8,10},{10,8},{12,14},{14,12},{1,3},{3,1},... | collective-permute-start | bytes 1397768 | tf_op jit(solution)/shard_map/ppermute | solution.py:146
  43.7 14.3 %copy-start.54 = (f32[1,28]{1,0:T(1,128)S(1)}, f32[1,28]{1,0:T(1,128)}, u32[]{:S(2)}) copy-start(f32[1,28]{1,0:T(1,128)} %param.15) | copy-start | bytes 340
  43.8 14.8 %copy-start.29 = (f32[28,64]{1,0:T(8,128)}, f32[28,64]{1,0:T(8,128)S(1)}, u32[]{:S(2)}) copy-start(f32[28,64]{1,0:T(8,128)S(1)} %reshape_squeeze.7) | copy-start | bytes 21508
  43.8 14.8 %copy-start.35 = (f32[1,28]{1,0:T(1,128)S(1)}, f32[1,28]{1,0:T(1,128)}, u32[]{:S(2)}) copy-start(f32[1,28]{1,0:T(1,128)} %param.14) | copy-start | bytes 340
  44.0 15.2 %copy-start.21 = (f32[128,128]{1,0:T(8,128)}, f32[128,128]{1,0:T(8,128)S(1)}, u32[]{:S(2)}) copy-start(f32[128,128]{1,0:T(8,128)S(1)} %get-tuple-element.105) | copy-start | bytes 196612
  44.0 15.2 %copy-start.32 = (pred[128,128]{1,0:T(8,128)(4,1)}, pred[128,128]{1,0:T(8,128)(4,1)S(1)}, u32[]{:S(2)}) copy-start(pred[128,128]{1,0:T(8,128)(4,1)S(1)} %get-tuple-element.104) | copy-start | bytes 49156
  44.1 15.1 %copy-start.8 = (f32[128,28,64]{0,2,1:T(8,128)S(1)}, f32[128,28,64]{0,2,1:T(8,128)}, u32[]{:S(2)}) copy-start(f32[128,28,64]{0,2,1:T(8,128)} %convert.62) | copy-start | bytes 2752516
  67.5 13.6 %collective-permute-start.10 = (bf16[28,8320]{1,0:T(8,128)(2,1)}, bf16[28,8320]{1,0:T(8,128)(2,1)S(1)}, u32[]{:S(2)}, u32[]{:S(2)}) collective-permute-start(bf16[28,8320]{1,0:T(8,128)(2,1)} %concatenate.66), channel_id=1, source_target_pairs={{0,4},{2,6},{4,0},{6,2},{8,12},{10,14},{12,8},{14,10},{1,5},{3,7},... | collective-permute-start | bytes 1397768 | tf_op jit(solution)/shard_map/ppermute | solution.py:146
  69.1 12.7 %copy-start.12 = (f32[28,1]{1,0:T(8,128)S(1)}, f32[28,1]{1,0:T(8,128)}, u32[]{:S(2)}) copy-start(f32[28,1]{1,0:T(8,128)} %copy-done.11) | copy-start | bytes 340
  69.1 14.0 %copy-start.1 = (f32[28,4096]{1,0:T(8,128)S(1)}, f32[28,4096]{1,0:T(8,128)}, u32[]{:S(2)}) copy-start(f32[28,4096]{1,0:T(8,128)} %copy-done) | copy-start | bytes 1376260
  69.1 14.0 %copy-start.44 = (f32[28]{0:T(128)S(1)}, f32[28]{0:T(128)}, u32[]{:S(2)}) copy-start(f32[28]{0:T(128)} %copy-done.43) | copy-start | bytes 340
  69.1 14.0 %copy-start.48 = (f32[28]{0:T(128)S(1)}, f32[28]{0:T(128)}, u32[]{:S(2)}) copy-start(f32[28]{0:T(128)} %get-tuple-element.68) | copy-start | bytes 340
  69.1 14.0 %copy-start.58 = (f32[28]{0:T(128)S(1)}, f32[28]{0:T(128)}, u32[]{:S(2)}) copy-start(f32[28]{0:T(128)} %exponential_multiply_fusion.1) | copy-start | bytes 340
  84.7 13.5 %collective-permute-start.11 = (bf16[28,4224]{1,0:T(8,128)(2,1)S(1)}, bf16[28,4224]{1,0:T(8,128)(2,1)S(1)}, u32[]{:S(2)}, u32[]{:S(2)}) collective-permute-start(bf16[28,4224]{1,0:T(8,128)(2,1)S(1)} %concatenate.67), channel_id=1, source_target_pairs={{0,8},{2,10},{4,12},{6,14},{8,0},{10,2},{12,4},{14,6},{1,9},{3,11}... | collective-permute-start | bytes 709640 | tf_op jit(solution)/shard_map/ppermute | solution.py:153
  85.4 12.9 %copy-start.49 = (f32[28]{0:T(128)S(1)}, f32[28]{0:T(128)}, u32[]{:S(2)}) copy-start(f32[28]{0:T(128)} %get-tuple-element.50) | copy-start | bytes 340
  85.4 12.9 %copy-start.50 = (f32[28]{0:T(128)S(1)}, f32[28]{0:T(128)}, u32[]{:S(2)}) copy-start(f32[28]{0:T(128)} %get-tuple-element.51) | copy-start | bytes 340
  85.4 12.9 %copy-start.51 = (f32[28]{0:T(128)S(1)}, f32[28]{0:T(128)}, u32[]{:S(2)}) copy-start(f32[28]{0:T(128)} %get-tuple-element.52) | copy-start | bytes 340
  85.4 12.9 %copy-start.52 = (f32[28]{0:T(128)S(1)}, f32[28]{0:T(128)}, u32[]{:S(2)}) copy-start(f32[28]{0:T(128)} %get-tuple-element.54) | copy-start | bytes 340
  106.2 2.2 %collective-permute-start.12 = (bf16[128,128]{0,1:T(8,128)(2,1)S(1)}, bf16[128,128]{0,1:T(8,128)(2,1)S(1)}, u32[]{:S(2)}, u32[]{:S(2)}) collective-permute-start(bf16[128,128]{0,1:T(8,128)(2,1)S(1)} %add_convert_fusion), channel_id=1, source_target_pairs={{0,1},{1,0},{2,3},{3,2},{4,5},{5,4},{6,7},{7,6},{8,9},{9,8},{10,11... | collective-permute-start | bytes 98312 | tf_op jit(solution)/shard_map/ppermute | solution.py:29
  110.4 7.2 %collective-permute-start.20 = (bf16[32,1920]{1,0:T(8,128)(2,1)S(1)}, bf16[32,1920]{1,0:T(8,128)(2,1)S(1)}, u32[]{:S(2)}, u32[]{:S(2)}) collective-permute-start(bf16[32,1920]{1,0:T(8,128)(2,1)S(1)} %get-tuple-element.98), channel_id=1, source_target_pairs={{0,14},{2,0},{4,2},{6,4},{8,6},{10,8},{12,10},{14,12},{1,15},{3,1}... | collective-permute-start | bytes 368648 | tf_op jit(solution)/shard_map/ppermute | solution.py:18
  111.4 7.4 %collective-permute-start.19 = (bf16[32,1920]{1,0:T(8,128)(2,1)S(1)}, bf16[32,1920]{1,0:T(8,128)(2,1)S(1)}, u32[]{:S(2)}, u32[]{:S(2)}) collective-permute-start(bf16[32,1920]{1,0:T(8,128)(2,1)S(1)} %get-tuple-element.97), channel_id=1, source_target_pairs={{0,12},{2,14},{4,0},{6,2},{8,4},{10,6},{12,8},{14,10},{1,13},{3,15... | collective-permute-start | bytes 368648 | tf_op jit(solution)/shard_map/ppermute | solution.py:18
  113.2 18.9 %collective-permute-start.18 = (bf16[32,1920]{1,0:T(8,128)(2,1)S(1)}, bf16[32,1920]{1,0:T(8,128)(2,1)S(1)}, u32[]{:S(2)}, u32[]{:S(2)}) collective-permute-start(bf16[32,1920]{1,0:T(8,128)(2,1)S(1)} %get-tuple-element.96), channel_id=1, source_target_pairs={{0,10},{2,12},{4,14},{6,0},{8,2},{10,4},{12,6},{14,8},{1,11},{3,13... | collective-permute-start | bytes 368648 | tf_op jit(solution)/shard_map/ppermute | solution.py:18
  113.2 20.7 %collective-permute-start.17 = (bf16[32,1920]{1,0:T(8,128)(2,1)S(1)}, bf16[32,1920]{1,0:T(8,128)(2,1)S(1)}, u32[]{:S(2)}, u32[]{:S(2)}) collective-permute-start(bf16[32,1920]{1,0:T(8,128)(2,1)S(1)} %get-tuple-element.95), channel_id=1, source_target_pairs={{0,8},{2,10},{4,12},{6,14},{8,0},{10,2},{12,4},{14,6},{1,9},{3,11}... | collective-permute-start | bytes 368648 | tf_op jit(solution)/shard_map/ppermute | solution.py:18
  116.6 17.3 %collective-permute-start.16 = (bf16[32,1920]{1,0:T(8,128)(2,1)S(1)}, bf16[32,1920]{1,0:T(8,128)(2,1)S(1)}, u32[]{:S(2)}, u32[]{:S(2)}) collective-permute-start(bf16[32,1920]{1,0:T(8,128)(2,1)S(1)} %get-tuple-element.94), channel_id=1, source_target_pairs={{0,6},{2,8},{4,10},{6,12},{8,14},{10,0},{12,2},{14,4},{1,7},{3,9},... | collective-permute-start | bytes 368648 | tf_op jit(solution)/shard_map/ppermute | solution.py:18
  117.6 16.4 %collective-permute-start.15 = (bf16[32,1920]{1,0:T(8,128)(2,1)S(1)}, bf16[32,1920]{1,0:T(8,128)(2,1)S(1)}, u32[]{:S(2)}, u32[]{:S(2)}) collective-permute-start(bf16[32,1920]{1,0:T(8,128)(2,1)S(1)} %get-tuple-element.93), channel_id=1, source_target_pairs={{0,4},{2,6},{4,8},{6,10},{8,12},{10,14},{12,0},{14,2},{1,5},{3,7},... | collective-permute-start | bytes 368648 | tf_op jit(solution)/shard_map/ppermute | solution.py:18
  118.7 15.3 %collective-permute-start.14 = (bf16[32,1920]{1,0:T(8,128)(2,1)S(1)}, bf16[32,1920]{1,0:T(8,128)(2,1)S(1)}, u32[]{:S(2)}, u32[]{:S(2)}) collective-permute-start(bf16[32,1920]{1,0:T(8,128)(2,1)S(1)} %get-tuple-element.92), channel_id=1, source_target_pairs={{0,2},{2,4},{4,6},{6,8},{8,10},{10,12},{12,14},{14,0},{1,3},{3,5},... | collective-permute-start | bytes 368648 | tf_op jit(solution)/shard_map/ppermute | solution.py:18
  132.1 13.0 %collective-permute-start.13 = (bf16[1,128,1792]{2,1,0:T(8,128)(2,1)S(1)}, bf16[1,128,1792]{2,1,0:T(8,128)(2,1)S(1)}, u32[]{:S(2)}, u32[]{:S(2)}) collective-permute-start(bf16[1,128,1792]{2,1,0:T(8,128)(2,1)S(1)} %fusion.1), channel_id=1, source_target_pairs={{16,0},{17,1},{18,2},{19,3},{20,4},{21,5},{22,6},{23,7},{24,8},{25... | collective-permute-start | bytes 1376264 | tf_op jit(solution)/shard_map/ppermute | solution.py:12
  (39 other events, 123.9 us)

commit v18 on v11

--- a/solution.py
+++ b/solution.py
@@ -302,12 +302,12 @@
     small_coded = small_coded.reshape(block_rows, small_cols)
     grad_rows = row_parts[0]
     small_slots = [small_coded]
-    for k in range(1, size):
+    for k in range(size - 1, 0, -1):
         message = jnp.concatenate([row_parts[k].astype(jnp.bfloat16), small_coded], axis=1)
         got = rotated(message, "seq", k)
         grad_rows = grad_rows + got[:, :channels_here].astype(jnp.float32)
         small_slots.append(got[:, channels_here:])
-    small_slots = jnp.stack(small_slots[::-1])
+    small_slots = jnp.stack([small_slots[0]] + small_slots[1:][::-1])[::-1]
     small_slots = roll_blocks(small_slots, mine + 1, size, 0).astype(jnp.float32)
     small_slots = small_slots.reshape(size, -1)
     small_parts = small_slots[:, :count] + small_slots[:, count : 2 * count]

time: 141 us -> 141 us (level)
  the two profiles are of different devices: /device:TPU:4 before, /device:TPU:0 now
where the time goes in v18:
time: 141 us
  waiting for transfers between devices  57.8 us (41%)
  starting transfers between devices  33.5 us (24%)
  matrix products  16.6 us (12%)
  local copies, waits for them, and re-layouts  16.5 us (12%)
  other arithmetic  13.3 us (9%)
  between operations  3.21 us (2%)
    ppermute x14, starting transfers between devices, rotated(): return lax.ppermute(block, axis, route)  25.4 us
    ppermute x2, waiting for transfers between devices, both_scans(): got = lax.ppermute(payload, axis, [(i, i ^ distance) for i in range(size)])  24.8 us
    ppermute x1, waiting for transfers between devices, both_scans(): got = lax.ppermute(last, axis, [(i, i ^ distance) for i in range(size)])  12.6 us
    ppermute x14, waiting for transfers between devices, rotated(): return lax.ppermute(block, axis, route)  10.8 us
    ppermute x2, waiting for transfers between devices, shifted(): return lax.ppermute(block, axis, route)  9.64 us
    dot_general x5, matrix products, contract(): return jnp.einsum(spec, left, right, preferred_element_type=jnp.float32)  6.81 us
    ppermute x2, starting transfers between devices, shifted(): return lax.ppermute(block, axis, route)  4.34 us
    unnamed x135, local copies, waits for them, and re-layouts  4.25 us
  transfers between devices with their start and end apart: 21, of which 8 were waited for; matrix products, arithmetic and copies ran while one was open for 15% of the time, Pallas kernels for 0%

profile of v18, /device:TPU:0, one launch (start us, length us, event | category | flops | bytes accessed | tf_op | source)
XLA Modules:
  0.0 141.0 jit_solution(18123922138174473061)
XLA Ops:
  0.7 3.0 %collective-permute-start = (bf16[32,1792]{1,0:T(8,128)(2,1)}, bf16[32,1792]{1,0:T(8,128)(2,1)S(1)}, u32[]{:S(2)}, u32[]{:S(2)}) collective-permute-start(bf16[32,1792]{1,0:T(8,128)(2,1)} %bitcast.331), channel_id=1, source_target_pairs={{0,2},{2,4},{4,6},{6,8},{8,10},{10,12},{12,14},{14,0},{1,3},{3,5},... | collective-permute-start | bytes 344072 | tf_op jit(solution)/shard_map/ppermute | solution.py:18
  3.7 1.6 %collective-permute-start.1 = (bf16[32,1792]{1,0:T(8,128)(2,1)}, bf16[32,1792]{1,0:T(8,128)(2,1)S(1)}, u32[]{:S(2)}, u32[]{:S(2)}) collective-permute-start(bf16[32,1792]{1,0:T(8,128)(2,1)} %bitcast.332), channel_id=1, source_target_pairs={{0,4},{2,6},{4,8},{6,10},{8,12},{10,14},{12,0},{14,2},{1,5},{3,7},... | collective-permute-start | bytes 344072 | tf_op jit(solution)/shard_map/ppermute | solution.py:18
  5.2 2.5 %collective-permute-start.2 = (bf16[32,1792]{1,0:T(8,128)(2,1)}, bf16[32,1792]{1,0:T(8,128)(2,1)S(1)}, u32[]{:S(2)}, u32[]{:S(2)}) collective-permute-start(bf16[32,1792]{1,0:T(8,128)(2,1)} %bitcast.333), channel_id=1, source_target_pairs={{0,6},{2,8},{4,10},{6,12},{8,14},{10,0},{12,2},{14,4},{1,7},{3,9},... | collective-permute-start | bytes 344072 | tf_op jit(solution)/shard_map/ppermute | solution.py:18
  7.8 1.2 collective-permute-start.3
  9.0 1.2 slice.179
  10.3 3.1 %collective-permute-start.8 = (s32[1]{0:T(128)}, s32[1]{0:T(128)}, u32[]{:S(2)}, u32[]{:S(2)}) collective-permute-start(s32[1]{0:T(128)} %bitcast.13), channel_id=1, source_target_pairs={{0,2},{2,4},{4,6},{6,8},{8,10},{10,12},{12,14},{1,3},{3,5},{5,7},{... | collective-permute-start | bytes 20 | tf_op jit(solution)/shard_map/ppermute | solution.py:12
  13.3 0.9 constant_dynamic-update-slice_fusion.7
  14.2 0.7 reduce
  15.7 1.3 copy.66
  17.9 1.0 convert.62
  19.7 1.6 %collective-permute-start.4 = (bf16[32,1792]{1,0:T(8,128)(2,1)S(1)}, bf16[32,1792]{1,0:T(8,128)(2,1)S(1)}, u32[]{:S(2)}, u32[]{:S(2)}) collective-permute-start(bf16[32,1792]{1,0:T(8,128)(2,1)S(1)} %bitcast.335), channel_id=1, source_target_pairs={{0,10},{2,12},{4,14},{6,0},{8,2},{10,4},{12,6},{14,8},{1,11},{3,13... | collective-permute-start | bytes 344072 | tf_op jit(solution)/shard_map/ppermute | solution.py:18
  21.2 1.3 broadcast_compare_fusion.1
  24.8 2.9 %collective-permute-start.5 = (bf16[32,1792]{1,0:T(8,128)(2,1)S(1)}, bf16[32,1792]{1,0:T(8,128)(2,1)S(1)}, u32[]{:S(2)}, u32[]{:S(2)}) collective-permute-start(bf16[32,1792]{1,0:T(8,128)(2,1)S(1)} %bitcast.336), channel_id=1, source_target_pairs={{0,12},{2,14},{4,0},{6,2},{8,4},{10,6},{12,8},{14,10},{1,13},{3,15... | collective-permute-start | bytes 344072 | tf_op jit(solution)/shard_map/ppermute | solution.py:18
  27.7 1.4 collective-permute-start.6
  29.2 1.0 collective-permute-done.5
  30.2 2.4 %collective-permute-done.6 = bf16[32,1792]{1,0:T(8,128)(2,1)S(1)} collective-permute-done((bf16[32,1792]{1,0:T(8,128)(2,1)S(1)}, bf16[32,1792]{1,0:T(8,128)(2,1)S(1)}, u32[]{:S(2)}, u32[]{:S(2)}) %collective-permute-start.6) | collective-permute-done | bytes 114720 | tf_op jit(solution)/shard_map/ppermute | solution.py:18
  34.5 0.7 copy.72
  37.4 1.2 copy.71
  38.6 1.6 %reshape.286 = f32[28,4096]{1,0:T(8,128)S(1)} reshape(f32[28,64,64]{2,1,0:T(8,128)} %copy.71) | data formatting | bytes 917504 | tf_op jit(solution)/shard_map/reshape | solution.py:243
  40.3 1.1 concatenate.63
  42.8 2.8 %fusion.12 = (f32[28,128]{1,0:T(8,128)S(1)}, f32[28,128]{1,0:T(8,128)S(1)}, f32[28,128]{1,0:T(8,128)S(1)}, bf16[128,128]{1,0:T(8,128)(2,1)S(1)}) fusion(f32[28,128]{1,0:T(8,128)S(1)} %fusion.119, f32[128,128]{1,0:T(8,128)S(1)} %fusion.103, f32[128,128]{1,0:T(8,128)} %get-tuple-element.107, f32[28,128]{1,0:T(8,128)S(1)} %fusion.75, ...), kind=kOutput, calls=%fused_computation.18 | convolution fusion | flops 66033152 | bytes 1628160 | tf_op jit(solution)/shard_map/transpose(jvp(hts,shp->thp))/dot_general | solution.py:33
  46.2 0.8 fusion.107
  47.0 2.8 %collective-permute-start.9 = (bf16[28,8320]{1,0:T(8,128)(2,1)S(1)}, bf16[28,8320]{1,0:T(8,128)(2,1)S(1)}, u32[]{:S(2)}, u32[]{:S(2)}) collective-permute-start(bf16[28,8320]{1,0:T(8,128)(2,1)S(1)} %copy-done.17), channel_id=1, source_target_pairs={{0,2},{2,0},{4,6},{6,4},{8,10},{10,8},{12,14},{14,12},{1,3},{3,1},... | collective-permute-start | bytes 1397768 | tf_op jit(solution)/shard_map/ppermute | solution.py:148
  49.9 1.8 %fusion.17 = bf16[128,28,64]{0,2,1:T(8,128)(2,1)} fusion(f32[128,28,64]{0,2,1:T(8,128)S(1)} %copy-done.8, f32[28,128]{1,0:T(8,128)S(1)} %fusion.119, f32[128,128]{1,0:T(8,128)S(1)} %fusion.103, f32[128,128]{1,0:T(8,128)S(1)} %copy-done.31, f32[28,128]{1,0:T(8,128)S(1)} %fusion.75, pred[128,128]{1,0:T(8,128)(4,1)S(1)} %copy-done.39, ...), kind=kOutput, calls=%fused_computation.27 | convolution fusion | flops 63078400 | bytes 1574000 | tf_op jit(solution)/shard_map/transpose(jvp(hts,shp->thp))/dot_general | solution.py:33
  51.7 10.9 %collective-permute-done.9 = bf16[28,8320]{1,0:T(8,128)(2,1)S(1)} collective-permute-done((bf16[28,8320]{1,0:T(8,128)(2,1)S(1)}, bf16[28,8320]{1,0:T(8,128)(2,1)S(1)}, u32[]{:S(2)}, u32[]{:S(2)}) %collective-permute-start.9) | collective-permute-done | bytes 465952 | tf_op jit(solution)/shard_map/ppermute | solution.py:148
  63.7 13.9 %collective-permute-done.10 = bf16[28,8320]{1,0:T(8,128)(2,1)} collective-permute-done((bf16[28,8320]{1,0:T(8,128)(2,1)S(1)}, bf16[28,8320]{1,0:T(8,128)(2,1)}, u32[]{:S(2)}, u32[]{:S(2)}) %collective-permute-start.10) | collective-permute-done | bytes 465952 | tf_op jit(solution)/shard_map/ppermute | solution.py:148
  77.6 1.1 convert_element_type.287
  79.5 0.7 collective-permute-start.11
  80.3 1.0 bitcast_multiply_fusion
  81.3 12.6 %collective-permute-done.11 = bf16[28,4224]{1,0:T(8,128)(2,1)} collective-permute-done((bf16[28,4224]{1,0:T(8,128)(2,1)S(1)}, bf16[28,4224]{1,0:T(8,128)(2,1)}, u32[]{:S(2)}, u32[]{:S(2)}) %collective-permute-start.11) | collective-permute-done | bytes 236576 | tf_op jit(solution)/shard_map/ppermute | solution.py:155
  93.8 1.4 %multiply_reduce_fusion.4 = (f32[28]{0:T(128)S(1)}, f32[28,4096]{1,0:T(8,128)S(1)}, bf16[28,4096]{1,0:T(8,128)(2,1)S(1)}) fusion(bf16[28,4224]{1,0:T(8,128)(2,1)} %collective-permute-done.11, f32[28]{0:T(128)S(1)} %get-tuple-element.52, f32[28,8320]{1,0:T(8,128)S(1)} %convert_element_type.287, f32[28]{0:T(128)S(1)} %get-tuple-element.54, ...), kind=kLoop, calls=%fused_computation.64 | loop fusion | flops 2064356 | bytes 2753075 | tf_op jit(solution)/shard_map/reduce_sum | solution.py:264
  98.6 0.8 fusion.137
  99.5 0.8 fusion.138
  100.6 1.0 fusion.22
  101.9 1.6 %fusion.21 = f32[128,28,64]{0,2,1:T(8,128)S(1)} fusion(bf16[28,64,64]{2,1,0:T(8,128)(2,1)S(1)} %copy-done.20, bf16[128,28,64]{0,2,1:T(8,128)(2,1)} %fusion.17, f32[28,128]{1,0:T(8,128)S(1)} %copy.82, f32[28,64]{1,0:T(8,128)S(1)} %copy-done.38, f32[28,128]{1,0:T(8,128)S(1)} %copy.77, f32[128,64]{0,1:T(8,128)S(1)} %copy-done.24, f32[128,28]{0,1:T(8,128)S(1)} %copy-done.29), kind=kOutput, calls=%fused_computation.31 | convolution fusion | flops 32112640 | bytes 1688576 | tf_op jit(solution)/shard_map/transpose(jvp(thn,thp->hnp))/dot_general | solution.py:33
  103.9 1.8 %fusion.132 = (bf16[256,1792]{1,0:T(8,128)(2,1)S(1)}, f32[256,1792]{1,0:T(8,128)}) fusion(bf16[1,128,1792]{2,1,0:T(8,128)(2,1)S(1)} %copy-done.7, s32[]{:T(128)S(6)} %select_n.220, bf16[128,256]{0,1:T(8,128)(2,1)S(1)} %maximum_select_fusion), kind=kOutput, calls=%fused_computation.271 | convolution fusion | flops 118030336 | bytes 3276804 | tf_op jit(solution)/shard_map/dot_general | solution.py:284
  105.8 0.8 pad_maximum_fusion.6
  106.6 1.3 collective-permute-start.20
  107.9 2.6 %collective-permute-start.18 = (bf16[32,1920]{1,0:T(8,128)(2,1)}, bf16[32,1920]{1,0:T(8,128)(2,1)S(1)}, u32[]{:S(2)}, u32[]{:S(2)}) collective-permute-start(bf16[32,1920]{1,0:T(8,128)(2,1)} %get-tuple-element.98), channel_id=1, source_target_pairs={{0,6},{2,8},{4,10},{6,12},{8,14},{10,0},{12,2},{14,4},{1,7},{3,9},... | collective-permute-start | bytes 368648 | tf_op jit(solution)/shard_map/ppermute | solution.py:18
  110.5 1.4 %collective-permute-start.17 = (bf16[32,1920]{1,0:T(8,128)(2,1)}, bf16[32,1920]{1,0:T(8,128)(2,1)S(1)}, u32[]{:S(2)}, u32[]{:S(2)}) collective-permute-start(bf16[32,1920]{1,0:T(8,128)(2,1)} %get-tuple-element.97), channel_id=1, source_target_pairs={{0,8},{2,10},{4,12},{6,14},{8,0},{10,2},{12,4},{14,6},{1,9},{3,11}... | collective-permute-start | bytes 368648 | tf_op jit(solution)/shard_map/ppermute | solution.py:18
  111.9 2.3 %collective-permute-start.16 = (bf16[32,1920]{1,0:T(8,128)(2,1)}, bf16[32,1920]{1,0:T(8,128)(2,1)S(1)}, u32[]{:S(2)}, u32[]{:S(2)}) collective-permute-start(bf16[32,1920]{1,0:T(8,128)(2,1)} %get-tuple-element.96), channel_id=1, source_target_pairs={{0,10},{2,12},{4,14},{6,0},{8,2},{10,4},{12,6},{14,8},{1,11},{3,13... | collective-permute-start | bytes 368648 | tf_op jit(solution)/shard_map/ppermute | solution.py:18
  114.8 1.0 collective-permute-done.20
  116.2 3.3 %collective-permute-start.14 = (bf16[32,1920]{1,0:T(8,128)(2,1)S(1)}, bf16[32,1920]{1,0:T(8,128)(2,1)S(1)}, u32[]{:S(2)}, u32[]{:S(2)}) collective-permute-start(bf16[32,1920]{1,0:T(8,128)(2,1)S(1)} %get-tuple-element.94), channel_id=1, source_target_pairs={{0,14},{2,0},{4,2},{6,4},{8,6},{10,8},{12,10},{14,12},{1,15},{3,1}... | collective-permute-start | bytes 368648 | tf_op jit(solution)/shard_map/ppermute | solution.py:18
  119.5 6.4 %collective-permute-done.18 = bf16[32,1920]{1,0:T(8,128)(2,1)S(1)} collective-permute-done((bf16[32,1920]{1,0:T(8,128)(2,1)}, bf16[32,1920]{1,0:T(8,128)(2,1)S(1)}, u32[]{:S(2)}, u32[]{:S(2)}) %collective-permute-start.18) | collective-permute-done | bytes 122912 | tf_op jit(solution)/shard_map/ppermute | solution.py:18
  125.9 1.3 collective-permute-start.13
  128.8 1.7 %fusion.51 = f32[1,32,1792]{2,1,0:T(8,128)} fusion(f32[256,1792]{1,0:T(8,128)} %get-tuple-element.112, bf16[32,1920]{1,0:T(8,128)(2,1)S(1)} %collective-permute-done.20, bf16[32,1920]{1,0:T(8,128)(2,1)S(1)} %collective-permute-done.19, bf16[32,1920]{1,0:T(8,128)(2,1)S(1)} %collective-permute-done.18, bf16[32,1920]{1,0:T(8,128)(2,1)S(1)} %collective-permute-done.17, ...), kind=kLoop, calls=%fused_computation.97 | loop fusion | flops 802816 | bytes 1261568 | tf_op jit(solution)/shard_map/broadcast_in_dim | solution.py:326
  130.6 9.6 %collective-permute-done.13 = bf16[1,128,1792]{2,1,0:T(8,128)(2,1)S(1)} collective-permute-done((bf16[1,128,1792]{2,1,0:T(8,128)(2,1)S(1)}, bf16[1,128,1792]{2,1,0:T(8,128)(2,1)S(1)}, u32[]{:S(2)}, u32[]{:S(2)}) %collective-permute-start.13) | collective-permute-done | bytes 458784 | tf_op jit(solution)/shard_map/ppermute | solution.py:12
  140.2 0.8 copy.140
  (237 shorter events, 17.6 us)
Async XLA Ops:
  0.6 17.0 %copy-start.50 = (f32[1,28]{1,0:T(1,128)S(1)}, f32[1,28]{1,0:T(1,128)}, u32[]{:S(2)}) copy-start(f32[1,28]{1,0:T(1,128)} %param.15) | copy-start | bytes 340
  0.6 17.0 %copy-start.18 = (bf16[1,128,1792]{2,1,0:T(8,128)(2,1)S(1)}, bf16[1,128,1792]{2,1,0:T(8,128)(2,1)}, u32[]{:S(2)}) copy-start(bf16[1,128,1792]{2,1,0:T(8,128)(2,1)} %param.11) | copy-start | bytes 1376260
  0.7 24.2 %collective-permute-start = (bf16[32,1792]{1,0:T(8,128)(2,1)}, bf16[32,1792]{1,0:T(8,128)(2,1)S(1)}, u32[]{:S(2)}, u32[]{:S(2)}) collective-permute-start(bf16[32,1792]{1,0:T(8,128)(2,1)} %bitcast.331), channel_id=1, source_target_pairs={{0,2},{2,4},{4,6},{6,8},{8,10},{10,12},{12,14},{14,0},{1,3},{3,5},... | collective-permute-start | bytes 344072 | tf_op jit(solution)/shard_map/ppermute | solution.py:18
  3.7 24.0 %collective-permute-start.1 = (bf16[32,1792]{1,0:T(8,128)(2,1)}, bf16[32,1792]{1,0:T(8,128)(2,1)S(1)}, u32[]{:S(2)}, u32[]{:S(2)}) collective-permute-start(bf16[32,1792]{1,0:T(8,128)(2,1)} %bitcast.332), channel_id=1, source_target_pairs={{0,4},{2,6},{4,8},{6,10},{8,12},{10,14},{12,0},{14,2},{1,5},{3,7},... | collective-permute-start | bytes 344072 | tf_op jit(solution)/shard_map/ppermute | solution.py:18
  5.2 23.8 %collective-permute-start.2 = (bf16[32,1792]{1,0:T(8,128)(2,1)}, bf16[32,1792]{1,0:T(8,128)(2,1)S(1)}, u32[]{:S(2)}, u32[]{:S(2)}) collective-permute-start(bf16[32,1792]{1,0:T(8,128)(2,1)} %bitcast.333), channel_id=1, source_target_pairs={{0,6},{2,8},{4,10},{6,12},{8,14},{10,0},{12,2},{14,4},{1,7},{3,9},... | collective-permute-start | bytes 344072 | tf_op jit(solution)/shard_map/ppermute | solution.py:18
  7.8 21.3 %collective-permute-start.3 = (bf16[32,1792]{1,0:T(8,128)(2,1)}, bf16[32,1792]{1,0:T(8,128)(2,1)S(1)}, u32[]{:S(2)}, u32[]{:S(2)}) collective-permute-start(bf16[32,1792]{1,0:T(8,128)(2,1)} %bitcast.334), channel_id=1, source_target_pairs={{0,8},{2,10},{4,12},{6,14},{8,0},{10,2},{12,4},{14,6},{1,9},{3,11}... | collective-permute-start | bytes 344072 | tf_op jit(solution)/shard_map/ppermute | solution.py:18
  10.3 9.4 %collective-permute-start.8 = (s32[1]{0:T(128)}, s32[1]{0:T(128)}, u32[]{:S(2)}, u32[]{:S(2)}) collective-permute-start(s32[1]{0:T(128)} %bitcast.13), channel_id=1, source_target_pairs={{0,2},{2,4},{4,6},{6,8},{8,10},{10,12},{12,14},{1,3},{3,5},{5,7},{... | collective-permute-start | bytes 20 | tf_op jit(solution)/shard_map/ppermute | solution.py:12
  15.7 4.0 %copy-start.25 = (bf16[1,32,1792]{2,1,0:T(8,128)(2,1)S(1)}, bf16[1,32,1792]{2,1,0:T(8,128)(2,1)}, u32[]{:S(2)}) copy-start(bf16[1,32,1792]{2,1,0:T(8,128)(2,1)} %param.12) | copy-start | bytes 344068
  15.7 8.1 %copy-start.40 = (f32[1,28]{1,0:T(1,128)S(1)}, f32[1,28]{1,0:T(1,128)}, u32[]{:S(2)}) copy-start(f32[1,28]{1,0:T(1,128)} %param.14) | copy-start | bytes 340
  17.0 29.2 %copy-start.4 = (bf16[1,128,1792]{1,2,0:T(8,128)(2,1)}, bf16[1,128,1792]{1,2,0:T(8,128)(2,1)S(1)}, u32[]{:S(2)}) copy-start(bf16[1,128,1792]{1,2,0:T(8,128)(2,1)S(1)} %copy.66) | copy-start | bytes 1376260
  17.6 11.5 %copy-start.15 = (f32[28,1,128]{0,2,1:T(8,128)}, f32[28,1,128]{0,2,1:T(8,128)S(1)}, u32[]{:S(2)}) copy-start(f32[28,1,128]{0,2,1:T(8,128)S(1)} %copy.87) | copy-start | bytes 43012
  17.6 6.4 %copy-start.57 = (f32[28]{0:T(128)}, f32[28]{0:T(128)S(1)}, u32[]{:S(2)}) copy-start(f32[28]{0:T(128)S(1)} %negate_bitcast_fusion) | copy-start | bytes 340
  17.9 14.7 %copy-start.6 = (bf16[1,128,1792]{2,1,0:T(8,128)(2,1)S(1)}, bf16[1,128,1792]{2,1,0:T(8,128)(2,1)}, u32[]{:S(2)}) copy-start(bf16[1,128,1792]{2,1,0:T(8,128)(2,1)} %param.9) | copy-start | bytes 1376260
  19.7 9.5 %collective-permute-start.4 = (bf16[32,1792]{1,0:T(8,128)(2,1)S(1)}, bf16[32,1792]{1,0:T(8,128)(2,1)S(1)}, u32[]{:S(2)}, u32[]{:S(2)}) collective-permute-start(bf16[32,1792]{1,0:T(8,128)(2,1)S(1)} %bitcast.335), channel_id=1, source_target_pairs={{0,10},{2,12},{4,14},{6,0},{8,2},{10,4},{12,6},{14,8},{1,11},{3,13... | collective-permute-start | bytes 344072 | tf_op jit(solution)/shard_map/ppermute | solution.py:18
  22.5 10.0 %copy-start.43 = (pred[128]{0:T(512)(128)(4,1)}, pred[128]{0:T(512)(128)(4,1)S(1)}, u32[]{:S(2)}) copy-start(pred[128]{0:T(512)(128)(4,1)S(1)} %get-tuple-element.77) | copy-start | bytes 388
  22.5 10.0 %copy-start.45 = (f32[128]{0:T(128)}, f32[128]{0:T(128)S(1)}, u32[]{:S(2)}) copy-start(f32[128]{0:T(128)S(1)} %get-tuple-element.78) | copy-start | bytes 1540
  24.1 12.6 %copy-start.26 = (f32[128,28]{0,1:T(8,128)}, f32[128,28]{0,1:T(8,128)S(1)}, u32[]{:S(2)}) copy-start(f32[128,28]{0,1:T(8,128)S(1)} %get-tuple-element.109) | copy-start | bytes 43012
  24.2 8.9 %copy-start.13 = (f32[128,28]{1,0:T(8,128)}, f32[128,28]{1,0:T(8,128)S(1)}, u32[]{:S(2)}) copy-start(f32[128,28]{1,0:T(8,128)S(1)} %copy.67) | copy-start | bytes 43012
  24.2 8.3 %copy-start.48 = (f32[28]{0:T(128)}, f32[28]{0:T(128)S(1)}, u32[]{:S(2)}) copy-start(f32[28]{0:T(128)S(1)} %slice_bitcast_fusion.7) | copy-start | bytes 340
  24.8 5.3 %collective-permute-start.5 = (bf16[32,1792]{1,0:T(8,128)(2,1)S(1)}, bf16[32,1792]{1,0:T(8,128)(2,1)S(1)}, u32[]{:S(2)}, u32[]{:S(2)}) collective-permute-start(bf16[32,1792]{1,0:T(8,128)(2,1)S(1)} %bitcast.336), channel_id=1, source_target_pairs={{0,12},{2,14},{4,0},{6,2},{8,4},{10,6},{12,8},{14,10},{1,13},{3,15... | collective-permute-start | bytes 344072 | tf_op jit(solution)/shard_map/ppermute | solution.py:18
  27.7 4.8 %collective-permute-start.6 = (bf16[32,1792]{1,0:T(8,128)(2,1)S(1)}, bf16[32,1792]{1,0:T(8,128)(2,1)S(1)}, u32[]{:S(2)}, u32[]{:S(2)}) collective-permute-start(bf16[32,1792]{1,0:T(8,128)(2,1)S(1)} %bitcast.337), channel_id=1, source_target_pairs={{0,14},{2,0},{4,2},{6,4},{8,6},{10,8},{12,10},{14,12},{1,15},{3,1}... | collective-permute-start | bytes 344072 | tf_op jit(solution)/shard_map/ppermute | solution.py:18
  32.6 3.8 %copy-start.2 = (bf16[256,1792]{1,0:T(8,128)(2,1)}, bf16[256,1792]{1,0:T(8,128)(2,1)S(1)}, u32[]{:S(2)}) copy-start(bf16[256,1792]{1,0:T(8,128)(2,1)S(1)} %constant_dynamic-update-slice_fusion) | copy-start | bytes 2752516
  33.1 2.8 %collective-permute-start.7 = (bf16[128,128]{0,1:T(8,128)(2,1)S(1)}, bf16[128,128]{0,1:T(8,128)(2,1)S(1)}, u32[]{:S(2)}, u32[]{:S(2)}) collective-permute-start(bf16[128,128]{0,1:T(8,128)(2,1)S(1)} %fusion.59), channel_id=1, source_target_pairs={{0,1},{1,0},{2,3},{3,2},{4,5},{5,4},{6,7},{7,6},{8,9},{9,8},{10,11... | collective-permute-start | bytes 98312 | tf_op jit(solution)/shard_map/ppermute | solution.py:29
  40.2 22.8 %copy-start = (f32[28,4096]{1,0:T(8,128)}, f32[28,4096]{1,0:T(8,128)S(1)}, u32[]{:S(2)}) copy-start(f32[28,4096]{1,0:T(8,128)S(1)} %reshape.286) | copy-start | bytes 1376260
  40.3 5.3 %copy-start.21 = (bf16[28,126]{1,0:T(8,128)(2,1)}, bf16[28,126]{1,0:T(8,128)(2,1)S(1)}, u32[]{:S(2)}) copy-start(bf16[28,126]{1,0:T(8,128)(2,1)S(1)} %broadcast.164) | copy-start | bytes 21172
  42.8 4.3 %copy-start.17 = (bf16[28,8320]{1,0:T(8,128)(2,1)S(1)}, bf16[28,8320]{1,0:T(8,128)(2,1)}, u32[]{:S(2)}) copy-start(bf16[28,8320]{1,0:T(8,128)(2,1)} %concatenate.63) | copy-start | bytes 1397764
  42.8 7.1 %copy-start.54 = (f32[1,28]{1,0:T(1,128)S(1)}, f32[1,28]{1,0:T(1,128)}, u32[]{:S(2)}) copy-start(f32[1,28]{1,0:T(1,128)} %param.16) | copy-start | bytes 340
  42.8 7.1 %copy-start.31 = (f32[128,128]{1,0:T(8,128)S(1)}, f32[128,128]{1,0:T(8,128)}, u32[]{:S(2)}) copy-start(f32[128,128]{1,0:T(8,128)} %get-tuple-element.107) | copy-start | bytes 196612
  42.8 7.1 %copy-start.37 = (f32[28,64]{1,0:T(8,128)S(1)}, f32[28,64]{1,0:T(8,128)}, u32[]{:S(2)}) copy-start(f32[28,64]{1,0:T(8,128)} %reshape_squeeze.7) | copy-start | bytes 21508
  42.8 7.1 %copy-start.39 = (pred[128,128]{1,0:T(8,128)(4,1)S(1)}, pred[128,128]{1,0:T(8,128)(4,1)}, u32[]{:S(2)}) copy-start(pred[128,128]{1,0:T(8,128)(4,1)} %get-tuple-element.106) | copy-start | bytes 49156
  47.0 15.6 %collective-permute-start.9 = (bf16[28,8320]{1,0:T(8,128)(2,1)S(1)}, bf16[28,8320]{1,0:T(8,128)(2,1)S(1)}, u32[]{:S(2)}, u32[]{:S(2)}) collective-permute-start(bf16[28,8320]{1,0:T(8,128)(2,1)S(1)} %copy-done.17), channel_id=1, source_target_pairs={{0,2},{2,0},{4,6},{6,4},{8,10},{10,8},{12,14},{14,12},{1,3},{3,1},... | collective-permute-start | bytes 1397768 | tf_op jit(solution)/shard_map/ppermute | solution.py:148
  49.9 12.8 %copy-start.30 = (f32[28,1]{1,0:T(8,128)S(1)}, f32[28,1]{1,0:T(8,128)}, u32[]{:S(2)}) copy-start(f32[28,1]{1,0:T(8,128)} %copy.74) | copy-start | bytes 340
  49.9 13.1 %copy-start.53 = (f32[28]{0:T(128)S(1)}, f32[28]{0:T(128)}, u32[]{:S(2)}) copy-start(f32[28]{0:T(128)} %exponential_multiply_fusion.1) | copy-start | bytes 340
  51.7 11.6 %copy-start.22 = (bf16[28,126]{1,0:T(8,128)(2,1)S(1)}, bf16[28,126]{1,0:T(8,128)(2,1)}, u32[]{:S(2)}) copy-start(bf16[28,126]{1,0:T(8,128)(2,1)} %copy-done.21) | copy-start | bytes 21172
  63.5 14.1 %collective-permute-start.10 = (bf16[28,8320]{1,0:T(8,128)(2,1)S(1)}, bf16[28,8320]{1,0:T(8,128)(2,1)}, u32[]{:S(2)}, u32[]{:S(2)}) collective-permute-start(bf16[28,8320]{1,0:T(8,128)(2,1)S(1)} %concatenate.64), channel_id=1, source_target_pairs={{0,4},{2,6},{4,0},{6,2},{8,12},{10,14},{12,8},{14,10},{1,5},{3,7},... | collective-permute-start | bytes 1397768 | tf_op jit(solution)/shard_map/ppermute | solution.py:148
  63.6 15.3 %copy-start.1 = (f32[28,4096]{1,0:T(8,128)S(1)}, f32[28,4096]{1,0:T(8,128)}, u32[]{:S(2)}) copy-start(f32[28,4096]{1,0:T(8,128)} %copy-done) | copy-start | bytes 1376260
  79.5 14.3 %collective-permute-start.11 = (bf16[28,4224]{1,0:T(8,128)(2,1)S(1)}, bf16[28,4224]{1,0:T(8,128)(2,1)}, u32[]{:S(2)}, u32[]{:S(2)}) collective-permute-start(bf16[28,4224]{1,0:T(8,128)(2,1)S(1)} %concatenate.65), channel_id=1, source_target_pairs={{0,8},{2,10},{4,12},{6,14},{8,0},{10,2},{12,4},{14,6},{1,9},{3,11}... | collective-permute-start | bytes 709640 | tf_op jit(solution)/shard_map/ppermute | solution.py:155
  98.5 3.4 %copy-start.38 = (f32[28,64]{1,0:T(8,128)S(1)}, f32[28,64]{1,0:T(8,128)}, u32[]{:S(2)}) copy-start(f32[28,64]{1,0:T(8,128)} %reshape_squeeze.7) | copy-start | bytes 21508
  101.6 2.3 %collective-permute-start.12 = (bf16[128,128]{0,1:T(8,128)(2,1)S(1)}, bf16[128,128]{0,1:T(8,128)(2,1)S(1)}, u32[]{:S(2)}, u32[]{:S(2)}) collective-permute-start(bf16[128,128]{0,1:T(8,128)(2,1)S(1)} %add_convert_fusion), channel_id=1, source_target_pairs={{0,1},{1,0},{2,3},{3,2},{4,5},{5,4},{6,7},{7,6},{8,9},{9,8},{10,11... | collective-permute-start | bytes 98312 | tf_op jit(solution)/shard_map/ppermute | solution.py:29
  105.8 8.7 %copy-start.3 = (bf16[256,1792]{1,0:T(8,128)(2,1)S(1)}, bf16[256,1792]{1,0:T(8,128)(2,1)}, u32[]{:S(2)}) copy-start(bf16[256,1792]{1,0:T(8,128)(2,1)} %copy-done.2) | copy-start | bytes 2752516
  106.6 9.2 %collective-permute-start.20 = (bf16[32,1920]{1,0:T(8,128)(2,1)}, bf16[32,1920]{1,0:T(8,128)(2,1)S(1)}, u32[]{:S(2)}, u32[]{:S(2)}) collective-permute-start(bf16[32,1920]{1,0:T(8,128)(2,1)} %get-tuple-element.100), channel_id=1, source_target_pairs={{0,2},{2,4},{4,6},{6,8},{8,10},{10,12},{12,14},{14,0},{1,3},{3,5},... | collective-permute-start | bytes 368648 | tf_op jit(solution)/shard_map/ppermute | solution.py:18
  107.9 8.3 %collective-permute-start.19 = (bf16[32,1920]{1,0:T(8,128)(2,1)}, bf16[32,1920]{1,0:T(8,128)(2,1)S(1)}, u32[]{:S(2)}, u32[]{:S(2)}) collective-permute-start(bf16[32,1920]{1,0:T(8,128)(2,1)} %get-tuple-element.99), channel_id=1, source_target_pairs={{0,4},{2,6},{4,8},{6,10},{8,12},{10,14},{12,0},{14,2},{1,5},{3,7},... | collective-permute-start | bytes 368648 | tf_op jit(solution)/shard_map/ppermute | solution.py:18
  107.9 18.0 %collective-permute-start.18 = (bf16[32,1920]{1,0:T(8,128)(2,1)}, bf16[32,1920]{1,0:T(8,128)(2,1)S(1)}, u32[]{:S(2)}, u32[]{:S(2)}) collective-permute-start(bf16[32,1920]{1,0:T(8,128)(2,1)} %get-tuple-element.98), channel_id=1, source_target_pairs={{0,6},{2,8},{4,10},{6,12},{8,14},{10,0},{12,2},{14,4},{1,7},{3,9},... | collective-permute-start | bytes 368648 | tf_op jit(solution)/shard_map/ppermute | solution.py:18
  110.5 16.7 %collective-permute-start.17 = (bf16[32,1920]{1,0:T(8,128)(2,1)}, bf16[32,1920]{1,0:T(8,128)(2,1)S(1)}, u32[]{:S(2)}, u32[]{:S(2)}) collective-permute-start(bf16[32,1920]{1,0:T(8,128)(2,1)} %get-tuple-element.97), channel_id=1, source_target_pairs={{0,8},{2,10},{4,12},{6,14},{8,0},{10,2},{12,4},{14,6},{1,9},{3,11}... | collective-permute-start | bytes 368648 | tf_op jit(solution)/shard_map/ppermute | solution.py:18
  111.9 15.3 %collective-permute-start.16 = (bf16[32,1920]{1,0:T(8,128)(2,1)}, bf16[32,1920]{1,0:T(8,128)(2,1)S(1)}, u32[]{:S(2)}, u32[]{:S(2)}) collective-permute-start(bf16[32,1920]{1,0:T(8,128)(2,1)} %get-tuple-element.96), channel_id=1, source_target_pairs={{0,10},{2,12},{4,14},{6,0},{8,2},{10,4},{12,6},{14,8},{1,11},{3,13... | collective-permute-start | bytes 368648 | tf_op jit(solution)/shard_map/ppermute | solution.py:18
  115.8 11.4 %collective-permute-start.15 = (bf16[32,1920]{1,0:T(8,128)(2,1)S(1)}, bf16[32,1920]{1,0:T(8,128)(2,1)S(1)}, u32[]{:S(2)}, u32[]{:S(2)}) collective-permute-start(bf16[32,1920]{1,0:T(8,128)(2,1)S(1)} %get-tuple-element.95), channel_id=1, source_target_pairs={{0,12},{2,14},{4,0},{6,2},{8,4},{10,6},{12,8},{14,10},{1,13},{3,15... | collective-permute-start | bytes 368648 | tf_op jit(solution)/shard_map/ppermute | solution.py:18
  116.2 11.0 %collective-permute-start.14 = (bf16[32,1920]{1,0:T(8,128)(2,1)S(1)}, bf16[32,1920]{1,0:T(8,128)(2,1)S(1)}, u32[]{:S(2)}, u32[]{:S(2)}) collective-permute-start(bf16[32,1920]{1,0:T(8,128)(2,1)S(1)} %get-tuple-element.94), channel_id=1, source_target_pairs={{0,14},{2,0},{4,2},{6,4},{8,6},{10,8},{12,10},{14,12},{1,15},{3,1}... | collective-permute-start | bytes 368648 | tf_op jit(solution)/shard_map/ppermute | solution.py:18
  125.9 14.3 %collective-permute-start.13 = (bf16[1,128,1792]{2,1,0:T(8,128)(2,1)S(1)}, bf16[1,128,1792]{2,1,0:T(8,128)(2,1)S(1)}, u32[]{:S(2)}, u32[]{:S(2)}) collective-permute-start(bf16[1,128,1792]{2,1,0:T(8,128)(2,1)S(1)} %fusion.1), channel_id=1, source_target_pairs={{16,0},{17,1},{18,2},{19,3},{20,4},{21,5},{22,6},{23,7},{24,8},{25... | collective-permute-start | bytes 1376264 | tf_op jit(solution)/shard_map/ppermute | solution.py:12
  (32 other events, 57.3 us)

commit v19 on v11

--- a/solution.py
+++ b/solution.py
@@ -302,9 +302,15 @@
     small_coded = small_coded.reshape(block_rows, small_cols)
     grad_rows = row_parts[0]
     small_slots = [small_coded]
+    messages = jnp.concatenate(
+        [
+            row_parts.astype(jnp.bfloat16),
+            jnp.broadcast_to(small_coded[None], (size,) + small_coded.shape),
+        ],
+        axis=2,
+    )
     for k in range(1, size):
-        message = jnp.concatenate([row_parts[k].astype(jnp.bfloat16), small_coded], axis=1)
-        got = rotated(message, "seq", k)
+        got = rotated(messages[k], "seq", k)
         grad_rows = grad_rows + got[:, :channels_here].astype(jnp.float32)
         small_slots.append(got[:, channels_here:])
     small_slots = jnp.stack(small_slots[::-1])

time: 141 us -> 140 us (level)
  transfers between devices with their start and end apart: 21 -> 21, of which waited for: 10 -> 9; matrix products, arithmetic and copies ran while one was open for 15% -> 15% of each run, Pallas kernels for 0% -> 0%
where the time goes in v19:
time: 140 us
  waiting for transfers between devices  64.2 us (46%)
  starting transfers between devices  26.5 us (19%)
  matrix products  16.6 us (12%)
  local copies, waits for them, and re-layouts  16.5 us (12%)
  other arithmetic  12.6 us (9%)
  between operations  3.22 us (2%)
    ppermute x2, waiting for transfers between devices, both_scans(): got = lax.ppermute(payload, axis, [(i, i ^ distance) for i in range(size)])  26.3 us
    ppermute x14, starting transfers between devices, rotated(): return lax.ppermute(block, axis, route)  19.9 us
    ppermute x14, waiting for transfers between devices, rotated(): return lax.ppermute(block, axis, route)  17.9 us
    ppermute x1, waiting for transfers between devices, both_scans(): got = lax.ppermute(last, axis, [(i, i ^ distance) for i in range(size)])  12.3 us
    ppermute x2, waiting for transfers between devices, shifted(): return lax.ppermute(block, axis, route)  7.62 us
    dot_general x5, matrix products, contract(): return jnp.einsum(spec, left, right, preferred_element_type=jnp.float32)  6.82 us
    ppermute x2, starting transfers between devices, shifted(): return lax.ppermute(block, axis, route)  5.6 us
    unnamed x141, local copies, waits for them, and re-layouts  4.31 us
  transfers between devices with their start and end apart: 21, of which 9 were waited for; matrix products, arithmetic and copies ran while one was open for 15% of the time, Pallas kernels for 0%

profile of v19, /device:TPU:4, one launch (start us, length us, event | category | flops | bytes accessed | tf_op | source)
XLA Modules:
  0.0 139.7 jit_solution(7715351170217858818)
XLA Ops:
  0.7 1.6 %collective-permute-start = (bf16[32,1792]{1,0:T(8,128)(2,1)}, bf16[32,1792]{1,0:T(8,128)(2,1)S(1)}, u32[]{:S(2)}, u32[]{:S(2)}) collective-permute-start(bf16[32,1792]{1,0:T(8,128)(2,1)} %bitcast.362), channel_id=1, source_target_pairs={{0,2},{2,4},{4,6},{6,8},{8,10},{10,12},{12,14},{14,0},{1,3},{3,5},... | collective-permute-start | bytes 344072 | tf_op jit(solution)/shard_map/ppermute | solution.py:18
  2.2 1.6 %collective-permute-start.1 = (bf16[32,1792]{1,0:T(8,128)(2,1)}, bf16[32,1792]{1,0:T(8,128)(2,1)S(1)}, u32[]{:S(2)}, u32[]{:S(2)}) collective-permute-start(bf16[32,1792]{1,0:T(8,128)(2,1)} %bitcast.363), channel_id=1, source_target_pairs={{0,4},{2,6},{4,8},{6,10},{8,12},{10,14},{12,0},{14,2},{1,5},{3,7},... | collective-permute-start | bytes 344072 | tf_op jit(solution)/shard_map/ppermute | solution.py:18
  3.8 2.5 %collective-permute-start.2 = (bf16[32,1792]{1,0:T(8,128)(2,1)}, bf16[32,1792]{1,0:T(8,128)(2,1)S(1)}, u32[]{:S(2)}, u32[]{:S(2)}) collective-permute-start(bf16[32,1792]{1,0:T(8,128)(2,1)} %bitcast.364), channel_id=1, source_target_pairs={{0,6},{2,8},{4,10},{6,12},{8,14},{10,0},{12,2},{14,4},{1,7},{3,9},... | collective-permute-start | bytes 344072 | tf_op jit(solution)/shard_map/ppermute | solution.py:18
  6.7 1.2 slice.165
  7.9 4.3 %collective-permute-start.8 = (s32[1]{0:T(128)}, s32[1]{0:T(128)}, u32[]{:S(2)}, u32[]{:S(2)}) collective-permute-start(s32[1]{0:T(128)} %bitcast.13), channel_id=1, source_target_pairs={{0,2},{2,4},{4,6},{6,8},{8,10},{10,12},{12,14},{1,3},{3,5},{5,7},{... | collective-permute-start | bytes 20 | tf_op jit(solution)/shard_map/ppermute | solution.py:12
  12.2 0.9 constant_dynamic-update-slice_fusion.7
  13.2 0.7 reduce
  14.0 0.7 reshape_squeeze.7
  14.6 1.3 copy.66
  16.8 1.0 convert.52
  17.9 0.7 broadcast_compare_fusion
  18.6 1.3 collective-permute-start.4
  19.9 1.3 broadcast_compare_fusion.1
  23.5 3.1 %collective-permute-start.5 = (bf16[32,1792]{1,0:T(8,128)(2,1)S(1)}, bf16[32,1792]{1,0:T(8,128)(2,1)S(1)}, u32[]{:S(2)}, u32[]{:S(2)}) collective-permute-start(bf16[32,1792]{1,0:T(8,128)(2,1)S(1)} %bitcast.367), channel_id=1, source_target_pairs={{0,12},{2,14},{4,0},{6,2},{8,4},{10,6},{12,8},{14,10},{1,13},{3,15... | collective-permute-start | bytes 344072 | tf_op jit(solution)/shard_map/ppermute | solution.py:18
  27.5 1.5 %collective-permute-done.5 = bf16[32,1792]{1,0:T(8,128)(2,1)S(1)} collective-permute-done((bf16[32,1792]{1,0:T(8,128)(2,1)S(1)}, bf16[32,1792]{1,0:T(8,128)(2,1)S(1)}, u32[]{:S(2)}, u32[]{:S(2)}) %collective-permute-start.5) | collective-permute-done | bytes 114720 | tf_op jit(solution)/shard_map/ppermute | solution.py:18
  29.0 3.4 %collective-permute-done.6 = bf16[32,1792]{1,0:T(8,128)(2,1)S(1)} collective-permute-done((bf16[32,1792]{1,0:T(8,128)(2,1)S(1)}, bf16[32,1792]{1,0:T(8,128)(2,1)S(1)}, u32[]{:S(2)}, u32[]{:S(2)}) %collective-permute-start.6) | collective-permute-done | bytes 114720 | tf_op jit(solution)/shard_map/ppermute | solution.py:18
  33.5 0.7 copy.74
  34.3 0.7 copy.72
  35.0 0.7 copy.73
  37.2 1.3 copy.71
  38.4 1.6 %reshape.271 = f32[28,4096]{1,0:T(8,128)S(1)} reshape(f32[28,64,64]{2,1,0:T(8,128)} %copy.71) | data formatting | bytes 917504 | tf_op jit(solution)/shard_map/reshape | solution.py:243
  40.1 1.1 concatenate.46
  42.7 2.8 %fusion.12 = (f32[28,128]{1,0:T(8,128)S(1)}, f32[28,128]{1,0:T(8,128)S(1)}, f32[28,128]{1,0:T(8,128)S(1)}, bf16[128,128]{1,0:T(8,128)(2,1)S(1)}) fusion(f32[28,128]{1,0:T(8,128)S(1)} %fusion.119, f32[128,128]{1,0:T(8,128)S(1)} %fusion.103, f32[128,128]{1,0:T(8,128)} %get-tuple-element.100, f32[28,128]{1,0:T(8,128)S(1)} %fusion.75, ...), kind=kOutput, calls=%fused_computation.18 | convolution fusion | flops 66033152 | bytes 1628160 | tf_op jit(solution)/shard_map/transpose(jvp(hts,shp->thp))/dot_general | solution.py:33
  46.1 0.8 fusion.107
  47.1 1.8 %fusion.17 = bf16[128,28,64]{0,2,1:T(8,128)(2,1)} fusion(f32[128,28,64]{0,2,1:T(8,128)S(1)} %copy-done.8, f32[28,128]{1,0:T(8,128)S(1)} %fusion.119, f32[128,128]{1,0:T(8,128)S(1)} %fusion.103, f32[128,128]{1,0:T(8,128)S(1)} %copy-done.31, f32[28,128]{1,0:T(8,128)S(1)} %fusion.75, pred[128,128]{1,0:T(8,128)(4,1)S(1)} %copy-done.38, ...), kind=kOutput, calls=%fused_computation.27 | convolution fusion | flops 63078400 | bytes 1574000 | tf_op jit(solution)/shard_map/transpose(jvp(hts,shp->thp))/dot_general | solution.py:33
  48.8 12.6 %collective-permute-done.9 = bf16[28,8320]{1,0:T(8,128)(2,1)S(1)} collective-permute-done((bf16[28,8320]{1,0:T(8,128)(2,1)S(1)}, bf16[28,8320]{1,0:T(8,128)(2,1)S(1)}, u32[]{:S(2)}, u32[]{:S(2)}) %collective-permute-start.9) | collective-permute-done | bytes 465952 | tf_op jit(solution)/shard_map/ppermute | solution.py:148
  62.5 13.7 %collective-permute-done.10 = bf16[28,8320]{1,0:T(8,128)(2,1)} collective-permute-done((bf16[28,8320]{1,0:T(8,128)(2,1)S(1)}, bf16[28,8320]{1,0:T(8,128)(2,1)}, u32[]{:S(2)}, u32[]{:S(2)}) %collective-permute-start.10) | collective-permute-done | bytes 465952 | tf_op jit(solution)/shard_map/ppermute | solution.py:148
  76.2 1.1 convert_element_type.286
  78.2 0.7 collective-permute-start.11
  78.9 1.0 bitcast_multiply_fusion
  79.9 12.3 %collective-permute-done.11 = bf16[28,4224]{1,0:T(8,128)(2,1)} collective-permute-done((bf16[28,4224]{1,0:T(8,128)(2,1)S(1)}, bf16[28,4224]{1,0:T(8,128)(2,1)}, u32[]{:S(2)}, u32[]{:S(2)}) %collective-permute-start.11) | collective-permute-done | bytes 236576 | tf_op jit(solution)/shard_map/ppermute | solution.py:155
  92.3 1.4 %multiply_reduce_fusion.4 = (f32[28]{0:T(128)S(1)}, f32[28,4096]{1,0:T(8,128)S(1)}, bf16[28,4096]{1,0:T(8,128)(2,1)S(1)}) fusion(bf16[28,4224]{1,0:T(8,128)(2,1)} %collective-permute-done.11, f32[28]{0:T(128)S(1)} %get-tuple-element.52, f32[28,8320]{1,0:T(8,128)S(1)} %convert_element_type.286, f32[28]{0:T(128)S(1)} %get-tuple-element.54, ...), kind=kLoop, calls=%fused_computation.64 | loop fusion | flops 2064356 | bytes 2753075 | tf_op jit(solution)/shard_map/reduce_sum | solution.py:264
  97.0 0.8 fusion.136
  97.9 0.8 fusion.137
  99.0 1.0 fusion.22
  100.3 1.6 %fusion.21 = f32[128,28,64]{0,2,1:T(8,128)S(1)} fusion(bf16[28,64,64]{2,1,0:T(8,128)(2,1)S(1)} %copy-done.20, bf16[128,28,64]{0,2,1:T(8,128)(2,1)} %fusion.17, f32[28,128]{1,0:T(8,128)S(1)} %copy.82, f32[28,64]{1,0:T(8,128)S(1)} %copy-done.37, f32[28,128]{1,0:T(8,128)S(1)} %copy.77, f32[128,64]{0,1:T(8,128)S(1)} %copy-done.24, f32[128,28]{0,1:T(8,128)S(1)} %copy-done.29), kind=kOutput, calls=%fused_computation.31 | convolution fusion | flops 32112640 | bytes 1688576 | tf_op jit(solution)/shard_map/transpose(jvp(thn,thp->hnp))/dot_general | solution.py:33
  102.3 1.8 %fusion.131 = (bf16[256,1792]{1,0:T(8,128)(2,1)S(1)}, f32[256,1792]{1,0:T(8,128)}) fusion(bf16[1,128,1792]{2,1,0:T(8,128)(2,1)S(1)} %copy-done.7, s32[]{:T(128)S(6)} %select_n.220, bf16[128,256]{0,1:T(8,128)(2,1)S(1)} %maximum_select_fusion), kind=kOutput, calls=%fused_computation.276 | convolution fusion | flops 118030336 | bytes 3276804 | tf_op jit(solution)/shard_map/dot_general | solution.py:284
  104.2 0.8 collective-permute-start.20
  104.9 1.8 %collective-permute-start.19 = (bf16[32,1920]{1,0:T(8,128)(2,1)S(1)}, bf16[32,1920]{1,0:T(8,128)(2,1)S(1)}, u32[]{:S(2)}, u32[]{:S(2)}) collective-permute-start(bf16[32,1920]{1,0:T(8,128)(2,1)S(1)} %get-tuple-element.82), channel_id=1, source_target_pairs={{0,12},{2,14},{4,0},{6,2},{8,4},{10,6},{12,8},{14,10},{1,13},{3,15... | collective-permute-start | bytes 368648 | tf_op jit(solution)/shard_map/ppermute | solution.py:18
  107.0 3.5 %collective-permute-start.17 = (bf16[32,1920]{1,0:T(8,128)(2,1)S(1)}, bf16[32,1920]{1,0:T(8,128)(2,1)S(1)}, u32[]{:S(2)}, u32[]{:S(2)}) collective-permute-start(bf16[32,1920]{1,0:T(8,128)(2,1)S(1)} %get-tuple-element.84), channel_id=1, source_target_pairs={{0,8},{2,10},{4,12},{6,14},{8,0},{10,2},{12,4},{14,6},{1,9},{3,11}... | collective-permute-start | bytes 368648 | tf_op jit(solution)/shard_map/ppermute | solution.py:18
  111.2 1.3 collective-permute-start.15
  112.6 1.5 %collective-permute-start.14 = (bf16[32,1920]{1,0:T(8,128)(2,1)S(1)}, bf16[32,1920]{1,0:T(8,128)(2,1)S(1)}, u32[]{:S(2)}, u32[]{:S(2)}) collective-permute-start(bf16[32,1920]{1,0:T(8,128)(2,1)S(1)} %get-tuple-element.81), channel_id=1, source_target_pairs={{0,2},{2,4},{4,6},{6,8},{8,10},{10,12},{12,14},{14,0},{1,3},{3,5},... | collective-permute-start | bytes 368648 | tf_op jit(solution)/shard_map/ppermute | solution.py:18
  114.0 11.9 %collective-permute-done.18 = bf16[32,1920]{1,0:T(8,128)(2,1)S(1)} collective-permute-done((bf16[32,1920]{1,0:T(8,128)(2,1)S(1)}, bf16[32,1920]{1,0:T(8,128)(2,1)S(1)}, u32[]{:S(2)}, u32[]{:S(2)}) %collective-permute-start.18) | collective-permute-done | bytes 122912 | tf_op jit(solution)/shard_map/ppermute | solution.py:18
  125.9 1.3 collective-permute-start.13
  128.3 0.6 slice.257
  129.5 1.7 %fusion.51 = f32[1,32,1792]{2,1,0:T(8,128)} fusion(f32[256,1792]{1,0:T(8,128)} %get-tuple-element.105, bf16[32,1920]{1,0:T(8,128)(2,1)S(1)} %collective-permute-done.20, bf16[32,1920]{1,0:T(8,128)(2,1)S(1)} %collective-permute-done.19, bf16[32,1920]{1,0:T(8,128)(2,1)S(1)} %collective-permute-done.18, bf16[32,1920]{1,0:T(8,128)(2,1)S(1)} %collective-permute-done.17, ...), kind=kLoop, calls=%fused_computation.90 | loop fusion | flops 802816 | bytes 1261568 | tf_op jit(solution)/shard_map/broadcast_in_dim | solution.py:332
  131.3 7.6 %collective-permute-done.13 = bf16[1,128,1792]{2,1,0:T(8,128)(2,1)S(1)} collective-permute-done((bf16[1,128,1792]{2,1,0:T(8,128)(2,1)S(1)}, bf16[1,128,1792]{2,1,0:T(8,128)(2,1)S(1)}, u32[]{:S(2)}, u32[]{:S(2)}) %collective-permute-start.13) | collective-permute-done | bytes 458784 | tf_op jit(solution)/shard_map/ppermute | solution.py:12
  138.9 0.8 copy.148
  (242 shorter events, 16.1 us)
Async XLA Ops:
  0.6 15.9 %copy-start.49 = (f32[1,28]{1,0:T(1,128)S(1)}, f32[1,28]{1,0:T(1,128)}, u32[]{:S(2)}) copy-start(f32[1,28]{1,0:T(1,128)} %param.15) | copy-start | bytes 340
  0.6 15.9 %copy-start.18 = (bf16[1,128,1792]{2,1,0:T(8,128)(2,1)S(1)}, bf16[1,128,1792]{2,1,0:T(8,128)(2,1)}, u32[]{:S(2)}) copy-start(bf16[1,128,1792]{2,1,0:T(8,128)(2,1)} %param.11) | copy-start | bytes 1376260
  0.7 22.8 %collective-permute-start = (bf16[32,1792]{1,0:T(8,128)(2,1)}, bf16[32,1792]{1,0:T(8,128)(2,1)S(1)}, u32[]{:S(2)}, u32[]{:S(2)}) collective-permute-start(bf16[32,1792]{1,0:T(8,128)(2,1)} %bitcast.362), channel_id=1, source_target_pairs={{0,2},{2,4},{4,6},{6,8},{8,10},{10,12},{12,14},{14,0},{1,3},{3,5},... | collective-permute-start | bytes 344072 | tf_op jit(solution)/shard_map/ppermute | solution.py:18
  2.2 24.4 %collective-permute-start.1 = (bf16[32,1792]{1,0:T(8,128)(2,1)}, bf16[32,1792]{1,0:T(8,128)(2,1)S(1)}, u32[]{:S(2)}, u32[]{:S(2)}) collective-permute-start(bf16[32,1792]{1,0:T(8,128)(2,1)} %bitcast.363), channel_id=1, source_target_pairs={{0,4},{2,6},{4,8},{6,10},{8,12},{10,14},{12,0},{14,2},{1,5},{3,7},... | collective-permute-start | bytes 344072 | tf_op jit(solution)/shard_map/ppermute | solution.py:18
  3.8 23.1 %collective-permute-start.2 = (bf16[32,1792]{1,0:T(8,128)(2,1)}, bf16[32,1792]{1,0:T(8,128)(2,1)S(1)}, u32[]{:S(2)}, u32[]{:S(2)}) collective-permute-start(bf16[32,1792]{1,0:T(8,128)(2,1)} %bitcast.364), channel_id=1, source_target_pairs={{0,6},{2,8},{4,10},{6,12},{8,14},{10,0},{12,2},{14,4},{1,7},{3,9},... | collective-permute-start | bytes 344072 | tf_op jit(solution)/shard_map/ppermute | solution.py:18
  6.3 20.5 %collective-permute-start.3 = (bf16[32,1792]{1,0:T(8,128)(2,1)}, bf16[32,1792]{1,0:T(8,128)(2,1)S(1)}, u32[]{:S(2)}, u32[]{:S(2)}) collective-permute-start(bf16[32,1792]{1,0:T(8,128)(2,1)} %bitcast.365), channel_id=1, source_target_pairs={{0,8},{2,10},{4,12},{6,14},{8,0},{10,2},{12,4},{14,6},{1,9},{3,11}... | collective-permute-start | bytes 344072 | tf_op jit(solution)/shard_map/ppermute | solution.py:18
  7.9 10.7 %collective-permute-start.8 = (s32[1]{0:T(128)}, s32[1]{0:T(128)}, u32[]{:S(2)}, u32[]{:S(2)}) collective-permute-start(s32[1]{0:T(128)} %bitcast.13), channel_id=1, source_target_pairs={{0,2},{2,4},{4,6},{6,8},{8,10},{10,12},{12,14},{1,3},{3,5},{5,7},{... | collective-permute-start | bytes 20 | tf_op jit(solution)/shard_map/ppermute | solution.py:12
  14.6 3.3 %copy-start.46 = (s32[1,128]{1,0:T(1,128)S(1)}, s32[1,128]{1,0:T(1,128)}, u32[]{:S(2)}) copy-start(s32[1,128]{1,0:T(1,128)} %param.10) | copy-start | bytes 1540
  14.6 4.0 %copy-start.25 = (bf16[1,32,1792]{2,1,0:T(8,128)(2,1)S(1)}, bf16[1,32,1792]{2,1,0:T(8,128)(2,1)}, u32[]{:S(2)}) copy-start(bf16[1,32,1792]{2,1,0:T(8,128)(2,1)} %param.12) | copy-start | bytes 344068
  14.6 7.9 %copy-start.39 = (f32[1,28]{1,0:T(1,128)S(1)}, f32[1,28]{1,0:T(1,128)}, u32[]{:S(2)}) copy-start(f32[1,28]{1,0:T(1,128)} %param.14) | copy-start | bytes 340
  15.9 30.1 %copy-start.4 = (bf16[1,128,1792]{1,2,0:T(8,128)(2,1)}, bf16[1,128,1792]{1,2,0:T(8,128)(2,1)S(1)}, u32[]{:S(2)}) copy-start(bf16[1,128,1792]{1,2,0:T(8,128)(2,1)S(1)} %copy.66) | copy-start | bytes 1376260
  16.5 10.4 %copy-start.15 = (f32[28,1,128]{0,2,1:T(8,128)}, f32[28,1,128]{0,2,1:T(8,128)S(1)}, u32[]{:S(2)}) copy-start(f32[28,1,128]{0,2,1:T(8,128)S(1)} %copy.87) | copy-start | bytes 43012
  16.6 6.2 %copy-start.56 = (f32[28]{0:T(128)}, f32[28]{0:T(128)S(1)}, u32[]{:S(2)}) copy-start(f32[28]{0:T(128)S(1)} %negate_bitcast_fusion) | copy-start | bytes 340
  16.8 15.5 %copy-start.6 = (bf16[1,128,1792]{2,1,0:T(8,128)(2,1)S(1)}, bf16[1,128,1792]{2,1,0:T(8,128)(2,1)}, u32[]{:S(2)}) copy-start(bf16[1,128,1792]{2,1,0:T(8,128)(2,1)} %param.9) | copy-start | bytes 1376260
  18.6 8.8 %collective-permute-start.4 = (bf16[32,1792]{1,0:T(8,128)(2,1)S(1)}, bf16[32,1792]{1,0:T(8,128)(2,1)S(1)}, u32[]{:S(2)}, u32[]{:S(2)}) collective-permute-start(bf16[32,1792]{1,0:T(8,128)(2,1)S(1)} %bitcast.366), channel_id=1, source_target_pairs={{0,10},{2,12},{4,14},{6,0},{8,2},{10,4},{12,6},{14,8},{1,11},{3,13... | collective-permute-start | bytes 344072 | tf_op jit(solution)/shard_map/ppermute | solution.py:18
  21.2 11.2 %copy-start.42 = (pred[128]{0:T(512)(128)(4,1)}, pred[128]{0:T(512)(128)(4,1)S(1)}, u32[]{:S(2)}) copy-start(pred[128]{0:T(512)(128)(4,1)S(1)} %get-tuple-element.77) | copy-start | bytes 388
  21.2 11.1 %copy-start.44 = (f32[128]{0:T(128)}, f32[128]{0:T(128)S(1)}, u32[]{:S(2)}) copy-start(f32[128]{0:T(128)S(1)} %get-tuple-element.78) | copy-start | bytes 1540
  22.8 13.8 %copy-start.26 = (f32[128,28]{0,1:T(8,128)}, f32[128,28]{0,1:T(8,128)S(1)}, u32[]{:S(2)}) copy-start(f32[128,28]{0,1:T(8,128)S(1)} %get-tuple-element.102) | copy-start | bytes 43012
  22.9 10.1 %copy-start.13 = (f32[128,28]{1,0:T(8,128)}, f32[128,28]{1,0:T(8,128)S(1)}, u32[]{:S(2)}) copy-start(f32[128,28]{1,0:T(8,128)S(1)} %copy.67) | copy-start | bytes 43012
  22.9 9.4 %copy-start.47 = (f32[28]{0:T(128)}, f32[28]{0:T(128)S(1)}, u32[]{:S(2)}) copy-start(f32[28]{0:T(128)S(1)} %slice_bitcast_fusion.7) | copy-start | bytes 340
  23.5 5.4 %collective-permute-start.5 = (bf16[32,1792]{1,0:T(8,128)(2,1)S(1)}, bf16[32,1792]{1,0:T(8,128)(2,1)S(1)}, u32[]{:S(2)}, u32[]{:S(2)}) collective-permute-start(bf16[32,1792]{1,0:T(8,128)(2,1)S(1)} %bitcast.367), channel_id=1, source_target_pairs={{0,12},{2,14},{4,0},{6,2},{8,4},{10,6},{12,8},{14,10},{1,13},{3,15... | collective-permute-start | bytes 344072 | tf_op jit(solution)/shard_map/ppermute | solution.py:18
  26.6 5.7 %collective-permute-start.6 = (bf16[32,1792]{1,0:T(8,128)(2,1)S(1)}, bf16[32,1792]{1,0:T(8,128)(2,1)S(1)}, u32[]{:S(2)}, u32[]{:S(2)}) collective-permute-start(bf16[32,1792]{1,0:T(8,128)(2,1)S(1)} %bitcast.368), channel_id=1, source_target_pairs={{0,14},{2,0},{4,2},{6,4},{8,6},{10,8},{12,10},{14,12},{1,15},{3,1}... | collective-permute-start | bytes 344072 | tf_op jit(solution)/shard_map/ppermute | solution.py:18
  32.4 3.8 %copy-start.2 = (bf16[256,1792]{1,0:T(8,128)(2,1)}, bf16[256,1792]{1,0:T(8,128)(2,1)S(1)}, u32[]{:S(2)}) copy-start(bf16[256,1792]{1,0:T(8,128)(2,1)S(1)} %constant_dynamic-update-slice_fusion) | copy-start | bytes 2752516
  32.9 2.8 %collective-permute-start.7 = (bf16[128,128]{0,1:T(8,128)(2,1)S(1)}, bf16[128,128]{0,1:T(8,128)(2,1)S(1)}, u32[]{:S(2)}, u32[]{:S(2)}) collective-permute-start(bf16[128,128]{0,1:T(8,128)(2,1)S(1)} %fusion.59), channel_id=1, source_target_pairs={{0,1},{1,0},{2,3},{3,2},{4,5},{5,4},{6,7},{7,6},{8,9},{9,8},{10,11... | collective-permute-start | bytes 98312 | tf_op jit(solution)/shard_map/ppermute | solution.py:29
  40.0 21.8 %copy-start = (f32[28,4096]{1,0:T(8,128)}, f32[28,4096]{1,0:T(8,128)S(1)}, u32[]{:S(2)}) copy-start(f32[28,4096]{1,0:T(8,128)S(1)} %reshape.271) | copy-start | bytes 1376260
  40.1 5.4 %copy-start.21 = (bf16[28,126]{1,0:T(8,128)(2,1)}, bf16[28,126]{1,0:T(8,128)(2,1)S(1)}, u32[]{:S(2)}) copy-start(bf16[28,126]{1,0:T(8,128)(2,1)S(1)} %broadcast.164) | copy-start | bytes 21172
  42.6 4.3 %copy-start.17 = (bf16[28,8320]{1,0:T(8,128)(2,1)S(1)}, bf16[28,8320]{1,0:T(8,128)(2,1)}, u32[]{:S(2)}) copy-start(bf16[28,8320]{1,0:T(8,128)(2,1)} %concatenate.46) | copy-start | bytes 1397764
  42.6 4.4 %copy-start.53 = (f32[1,28]{1,0:T(1,128)S(1)}, f32[1,28]{1,0:T(1,128)}, u32[]{:S(2)}) copy-start(f32[1,28]{1,0:T(1,128)} %param.16) | copy-start | bytes 340
  42.6 4.4 %copy-start.31 = (f32[128,128]{1,0:T(8,128)S(1)}, f32[128,128]{1,0:T(8,128)}, u32[]{:S(2)}) copy-start(f32[128,128]{1,0:T(8,128)} %get-tuple-element.100) | copy-start | bytes 196612
  42.6 4.4 %copy-start.37 = (f32[28,64]{1,0:T(8,128)S(1)}, f32[28,64]{1,0:T(8,128)}, u32[]{:S(2)}) copy-start(f32[28,64]{1,0:T(8,128)} %reshape_squeeze.7) | copy-start | bytes 21508
  42.7 4.4 %copy-start.38 = (pred[128,128]{1,0:T(8,128)(4,1)S(1)}, pred[128,128]{1,0:T(8,128)(4,1)}, u32[]{:S(2)}) copy-start(pred[128,128]{1,0:T(8,128)(4,1)} %get-tuple-element.99) | copy-start | bytes 49156
  46.9 14.6 %collective-permute-start.9 = (bf16[28,8320]{1,0:T(8,128)(2,1)S(1)}, bf16[28,8320]{1,0:T(8,128)(2,1)S(1)}, u32[]{:S(2)}, u32[]{:S(2)}) collective-permute-start(bf16[28,8320]{1,0:T(8,128)(2,1)S(1)} %copy-done.17), channel_id=1, source_target_pairs={{0,2},{2,0},{4,6},{6,4},{8,10},{10,8},{12,14},{14,12},{1,3},{3,1},... | collective-permute-start | bytes 1397768 | tf_op jit(solution)/shard_map/ppermute | solution.py:148
  47.0 14.5 %copy-start.30 = (f32[28,1]{1,0:T(8,128)S(1)}, f32[28,1]{1,0:T(8,128)}, u32[]{:S(2)}) copy-start(f32[28,1]{1,0:T(8,128)} %copy.74) | copy-start | bytes 340
  47.0 14.8 %copy-start.52 = (f32[28]{0:T(128)S(1)}, f32[28]{0:T(128)}, u32[]{:S(2)}) copy-start(f32[28]{0:T(128)} %exponential_multiply_fusion.1) | copy-start | bytes 340
  48.8 13.3 %copy-start.22 = (bf16[28,126]{1,0:T(8,128)(2,1)S(1)}, bf16[28,126]{1,0:T(8,128)(2,1)}, u32[]{:S(2)}) copy-start(bf16[28,126]{1,0:T(8,128)(2,1)} %copy-done.21) | copy-start | bytes 21172
  62.4 13.9 %collective-permute-start.10 = (bf16[28,8320]{1,0:T(8,128)(2,1)S(1)}, bf16[28,8320]{1,0:T(8,128)(2,1)}, u32[]{:S(2)}, u32[]{:S(2)}) collective-permute-start(bf16[28,8320]{1,0:T(8,128)(2,1)S(1)} %concatenate.47), channel_id=1, source_target_pairs={{0,4},{2,6},{4,0},{6,2},{8,12},{10,14},{12,8},{14,10},{1,5},{3,7},... | collective-permute-start | bytes 1397768 | tf_op jit(solution)/shard_map/ppermute | solution.py:148
  62.5 15.1 %copy-start.1 = (f32[28,4096]{1,0:T(8,128)S(1)}, f32[28,4096]{1,0:T(8,128)}, u32[]{:S(2)}) copy-start(f32[28,4096]{1,0:T(8,128)} %copy-done) | copy-start | bytes 1376260
  78.2 14.1 %collective-permute-start.11 = (bf16[28,4224]{1,0:T(8,128)(2,1)S(1)}, bf16[28,4224]{1,0:T(8,128)(2,1)}, u32[]{:S(2)}, u32[]{:S(2)}) collective-permute-start(bf16[28,4224]{1,0:T(8,128)(2,1)S(1)} %concatenate.48), channel_id=1, source_target_pairs={{0,8},{2,10},{4,12},{6,14},{8,0},{10,2},{12,4},{14,6},{1,9},{3,11}... | collective-permute-start | bytes 709640 | tf_op jit(solution)/shard_map/ppermute | solution.py:155
  100.0 2.2 %collective-permute-start.12 = (bf16[128,128]{0,1:T(8,128)(2,1)S(1)}, bf16[128,128]{0,1:T(8,128)(2,1)S(1)}, u32[]{:S(2)}, u32[]{:S(2)}) collective-permute-start(bf16[128,128]{0,1:T(8,128)(2,1)S(1)} %add_convert_fusion), channel_id=1, source_target_pairs={{0,1},{1,0},{2,3},{3,2},{4,5},{5,4},{6,7},{7,6},{8,9},{9,8},{10,11... | collective-permute-start | bytes 98312 | tf_op jit(solution)/shard_map/ppermute | solution.py:29
  104.1 6.8 %copy-start.3 = (bf16[256,1792]{1,0:T(8,128)(2,1)S(1)}, bf16[256,1792]{1,0:T(8,128)(2,1)}, u32[]{:S(2)}) copy-start(bf16[256,1792]{1,0:T(8,128)(2,1)} %copy-done.2) | copy-start | bytes 2752516
  104.2 7.1 %collective-permute-start.20 = (bf16[32,1920]{1,0:T(8,128)(2,1)S(1)}, bf16[32,1920]{1,0:T(8,128)(2,1)S(1)}, u32[]{:S(2)}, u32[]{:S(2)}) collective-permute-start(bf16[32,1920]{1,0:T(8,128)(2,1)S(1)} %get-tuple-element.87), channel_id=1, source_target_pairs={{0,14},{2,0},{4,2},{6,4},{8,6},{10,8},{12,10},{14,12},{1,15},{3,1}... | collective-permute-start | bytes 368648 | tf_op jit(solution)/shard_map/ppermute | solution.py:18
  104.9 7.6 %collective-permute-start.19 = (bf16[32,1920]{1,0:T(8,128)(2,1)S(1)}, bf16[32,1920]{1,0:T(8,128)(2,1)S(1)}, u32[]{:S(2)}, u32[]{:S(2)}) collective-permute-start(bf16[32,1920]{1,0:T(8,128)(2,1)S(1)} %get-tuple-element.82), channel_id=1, source_target_pairs={{0,12},{2,14},{4,0},{6,2},{8,4},{10,6},{12,8},{14,10},{1,13},{3,15... | collective-permute-start | bytes 368648 | tf_op jit(solution)/shard_map/ppermute | solution.py:18
  106.8 19.1 %collective-permute-start.18 = (bf16[32,1920]{1,0:T(8,128)(2,1)S(1)}, bf16[32,1920]{1,0:T(8,128)(2,1)S(1)}, u32[]{:S(2)}, u32[]{:S(2)}) collective-permute-start(bf16[32,1920]{1,0:T(8,128)(2,1)S(1)} %get-tuple-element.83), channel_id=1, source_target_pairs={{0,10},{2,12},{4,14},{6,0},{8,2},{10,4},{12,6},{14,8},{1,11},{3,13... | collective-permute-start | bytes 368648 | tf_op jit(solution)/shard_map/ppermute | solution.py:18
  107.0 20.8 %collective-permute-start.17 = (bf16[32,1920]{1,0:T(8,128)(2,1)S(1)}, bf16[32,1920]{1,0:T(8,128)(2,1)S(1)}, u32[]{:S(2)}, u32[]{:S(2)}) collective-permute-start(bf16[32,1920]{1,0:T(8,128)(2,1)S(1)} %get-tuple-element.84), channel_id=1, source_target_pairs={{0,8},{2,10},{4,12},{6,14},{8,0},{10,2},{12,4},{14,6},{1,9},{3,11}... | collective-permute-start | bytes 368648 | tf_op jit(solution)/shard_map/ppermute | solution.py:18
  110.5 17.3 %collective-permute-start.16 = (bf16[32,1920]{1,0:T(8,128)(2,1)S(1)}, bf16[32,1920]{1,0:T(8,128)(2,1)S(1)}, u32[]{:S(2)}, u32[]{:S(2)}) collective-permute-start(bf16[32,1920]{1,0:T(8,128)(2,1)S(1)} %get-tuple-element.85), channel_id=1, source_target_pairs={{0,6},{2,8},{4,10},{6,12},{8,14},{10,0},{12,2},{14,4},{1,7},{3,9},... | collective-permute-start | bytes 368648 | tf_op jit(solution)/shard_map/ppermute | solution.py:18
  111.2 16.6 %collective-permute-start.15 = (bf16[32,1920]{1,0:T(8,128)(2,1)S(1)}, bf16[32,1920]{1,0:T(8,128)(2,1)S(1)}, u32[]{:S(2)}, u32[]{:S(2)}) collective-permute-start(bf16[32,1920]{1,0:T(8,128)(2,1)S(1)} %get-tuple-element.86), channel_id=1, source_target_pairs={{0,4},{2,6},{4,8},{6,10},{8,12},{10,14},{12,0},{14,2},{1,5},{3,7},... | collective-permute-start | bytes 368648 | tf_op jit(solution)/shard_map/ppermute | solution.py:18
  112.6 15.3 %collective-permute-start.14 = (bf16[32,1920]{1,0:T(8,128)(2,1)S(1)}, bf16[32,1920]{1,0:T(8,128)(2,1)S(1)}, u32[]{:S(2)}, u32[]{:S(2)}) collective-permute-start(bf16[32,1920]{1,0:T(8,128)(2,1)S(1)} %get-tuple-element.81), channel_id=1, source_target_pairs={{0,2},{2,4},{4,6},{6,8},{8,10},{10,12},{12,14},{14,0},{1,3},{3,5},... | collective-permute-start | bytes 368648 | tf_op jit(solution)/shard_map/ppermute | solution.py:18
  125.9 13.0 %collective-permute-start.13 = (bf16[1,128,1792]{2,1,0:T(8,128)(2,1)S(1)}, bf16[1,128,1792]{2,1,0:T(8,128)(2,1)S(1)}, u32[]{:S(2)}, u32[]{:S(2)}) collective-permute-start(bf16[1,128,1792]{2,1,0:T(8,128)(2,1)S(1)} %fusion.1), channel_id=1, source_target_pairs={{16,0},{17,1},{18,2},{19,3},{20,4},{21,5},{22,6},{23,7},{24,8},{25... | collective-permute-start | bytes 1376264 | tf_op jit(solution)/shard_map/ppermute | solution.py:12
  (31 other events, 54.1 us)
